TPU v7x, 32 devices: a whole 2x2x4 slice. The times are simulated.
32 devices in a mesh: req: 2 (over x), ctx: 8 (over z, core), exp: 2 (over y).
Axes of the slice: x: 2, y: 2, z: 4, core: 2. Of those that a mesh axis runs over, the one named last changes fastest.
Arguments:
- query_states: bfloat16 [2, 512, 1024], P('req', 'ctx', 'exp'), may hold values from -6 to 6
- key_states: bfloat16 [2, 512, 1024], P('req', 'ctx', 'exp'), may hold values from -6 to 6
- value_states: bfloat16 [2, 512, 1024], P('req', 'ctx', 'exp'), may hold values from -6 to 6
- residual: bfloat16 [2, 512, 2048], P('req', ('ctx', 'exp')), may hold values from -6 to 6
- out_weight: bfloat16 [2048, 1024], P('ctx', 'exp'), may hold values from -0.1875 to 0.1875
- norm_gain: float32 [2048], replicated, may hold values from 0.1 to 1.9
- gate_weight: bfloat16 [8, 2048, 704], P('ctx', None, 'exp'), may hold values from -0.125 to 0.125
- up_weight: bfloat16 [8, 2048, 704], P('ctx', None, 'exp'), may hold values from -0.125 to 0.125
- down_weight: bfloat16 [8, 704, 2048], P('ctx', 'exp'), may hold values from -0.21875 to 0.21875
- routes: int32 [2, 512, 4], P('req', 'ctx'), may hold values from 0 to 7, all different within a row; in each aligned block of 64 rows (0 to 63, 64 to 127, ..., all dimensions but the last counted through in order) at most 48 rows name the same one
- route_weights: float32 [2, 512, 4], P('req', 'ctx'), may hold values from 0.1 to 1
- prompt_lengths: int32 [2], P('req'), may hold values from 128 to 512, as said below
Outputs:
- layer_out: bfloat16 [2, 512, 2048], P('req', ('ctx', 'exp'))
- cache_keys: bfloat16 [2, 512, 1024], P('req', 'ctx', 'exp')
- cache_values: bfloat16 [2, 512, 1024], P('req', 'ctx', 'exp')
Inputs may be any that keep to these rules, and one draw needn't show every extreme that they name: `routes`: each row names 4 different experts; in each aligned block of 64 rows of a request no expert is named by more than 48 rows, a bound that some block reaches. `prompt_lengths`: one request has exactly 512 tokens.
All inputs are finite; a program needn't handle non-finite values.
Results may differ from a plain program's by a relative error of at most 0.019.
Values may be sent and summed in bfloat16 or wider, within the bound.
No kernel may reach another device: no remote copies, remote signals or barrier semaphores. Data moves between devices by JAX's collectives and lax.ppermute only.
A program may use at most 64 MiB of HBM per device.

v0:
```python
import jax
import jax.numpy as jnp
from jax import lax
from jax.sharding import PartitionSpec as P

D = 2048
HD = 128
TOP = 4


EPS = 1e-06
NEG = -1e30


def row_positions(row_ids, half_block, n_groups):
    block_ids = row_ids // half_block
    device = block_ids // 2
    target = jnp.where(block_ids % 2 == 0, device, 2 * n_groups - 1 - device)
    return target * half_block + row_ids % half_block


def slot_tables(route_block, weight_block, experts, capacity):
    tok_here, top_here = route_block.shape
    flat_ids = route_block.reshape(tok_here * top_here)
    hit_table = (flat_ids[:, None] == jnp.arange(experts, dtype=jnp.int32)[None, :]).astype(
        jnp.int32
    )
    before = jnp.cumsum(hit_table, axis=0) - hit_table
    slot_rank = jnp.sum(before * hit_table, axis=1)
    slot_index = flat_ids * capacity + slot_rank
    slot_match = (
        jnp.arange(experts * capacity, dtype=jnp.int32)[:, None] == slot_index[None, :]
    ).astype(jnp.float32)
    slot_match = slot_match.reshape(experts * capacity, tok_here, top_here)
    dispatch = jnp.sum(slot_match, axis=2)
    combine = jnp.transpose(jnp.sum(slot_match * weight_block[None, :, :], axis=2))
    return (dispatch, combine)


def expert_ffn(token_rows, gate_matrix, up_matrix, down_matrix):
    gate_act = jnp.dot(token_rows, gate_matrix, preferred_element_type=jnp.float32)
    up_act = jnp.dot(token_rows, up_matrix, preferred_element_type=jnp.float32)
    hidden = (jax.nn.silu(gate_act) * up_act).astype(jnp.bfloat16)
    return jnp.dot(hidden, down_matrix, preferred_element_type=jnp.float32)


def local(
    query_states,
    key_states,
    value_states,
    residual,
    out_weight,
    norm_gain,
    gate_weight,
    up_weight,
    down_weight,
    routes,
    route_weights,
    prompt_lengths,
):
    n_ctx = lax.axis_size("ctx")
    my_ctx = lax.axis_index("ctx")
    tok_here = query_states.shape[1]
    feat_width = query_states.shape[2]
    heads_dev = feat_width // HD
    half_block = tok_here // 2
    score_scale = HD ** (-0.5)
    length = prompt_lengths[0]
    local_ids = jnp.arange(tok_here, dtype=jnp.int32)
    query_pos = row_positions(my_ctx * tok_here + local_ids, half_block, n_ctx)
    decode_pos = my_ctx * tok_here + local_ids
    query_three = query_states[0].reshape(tok_here, heads_dev, HD)
    run_max = jnp.full((heads_dev, tok_here), NEG, jnp.float32)
    key_two = lax.all_gather(key_states, "ctx", axis=1, tiled=True)[0]
    value_two = lax.all_gather(value_states, "ctx", axis=1, tiled=True)[0]
    row_count = key_two.shape[0]
    key_pos = row_positions(jnp.arange(row_count, dtype=jnp.int32), half_block, n_ctx)
    pick_rows = (decode_pos[:, None] == key_pos[None, :]).astype(jnp.bfloat16)
    kept_keys = jnp.dot(pick_rows, key_two, preferred_element_type=jnp.float32)
    kept_values = jnp.dot(pick_rows, value_two, preferred_element_type=jnp.float32)
    old_max = run_max
    key_heads = key_two.reshape(row_count, heads_dev, HD)
    value_heads = value_two.reshape(row_count, heads_dev, HD)
    logits = (
        jnp.einsum("qhd,khd->hqk", query_three, key_heads, preferred_element_type=jnp.float32)
        * score_scale
    )
    visible = (key_pos[None, :] <= query_pos[:, None]) & (key_pos[None, :] < length)
    logits = jnp.where(visible[None], logits, NEG)
    new_max = jnp.maximum(old_max, jnp.max(logits, axis=2))
    weights = jnp.where(visible[None], jnp.exp(logits - new_max[:, :, None]), 0.0)
    new_sum = jnp.sum(weights, axis=2)
    gained = jnp.einsum(
        "hqk,khd->hqd",
        weights.astype(jnp.bfloat16),
        value_heads,
        preferred_element_type=jnp.float32,
    )
    inner_state = (new_max, new_sum, gained)
    run_max, run_sum, run_out, kept_keys, kept_values = inner_state + (kept_keys, kept_values)
    mixed = (run_out / run_sum[:, :, None]).astype(jnp.bfloat16)
    mixed = jnp.transpose(mixed, (1, 0, 2)).reshape(tok_here, feat_width)
    out_parts = jnp.einsum(
        "tc,oc->to",
        mixed,
        lax.all_gather(out_weight, "ctx", axis=0, tiled=True),
        preferred_element_type=jnp.float32,
    )
    head_total = lax.psum_scatter(
        out_parts.astype(jnp.bfloat16), "exp", scatter_dimension=0, tiled=True
    ).astype(jnp.float32)
    stream = (residual[0].astype(jnp.float32) + head_total).astype(jnp.bfloat16)
    stream_f = stream.astype(jnp.float32)
    mean_sq = jnp.mean(stream_f * stream_f, axis=1, keepdims=True)
    normed = (stream_f * lax.rsqrt(mean_sq + EPS) * norm_gain).astype(jnp.bfloat16)
    all_normed = lax.all_gather(normed, "exp", axis=0, tiled=True)
    capacity = min(tok_here, 2 * max(1, 3 * tok_here * TOP // (4 * n_ctx)))
    dispatch, combine = slot_tables(routes[0], route_weights[0], n_ctx, capacity)
    send_rows = jnp.dot(
        dispatch.astype(jnp.bfloat16), all_normed, preferred_element_type=jnp.float32
    ).astype(jnp.bfloat16)
    send_rows = send_rows.reshape(n_ctx, capacity, D)
    arrived = lax.all_to_all(send_rows, "ctx", split_axis=0, concat_axis=0, tiled=True)
    slot_count = arrived.shape[1]
    flat_rows = arrived.reshape(n_ctx * slot_count, D)
    produced = expert_ffn(flat_rows, gate_weight[0], up_weight[0], down_weight[0]).reshape(
        n_ctx, slot_count, D
    )
    served = lax.all_to_all(
        produced.astype(jnp.bfloat16), "ctx", split_axis=0, concat_axis=0, tiled=True
    ).astype(produced.dtype)
    results = served.reshape(n_ctx * capacity, D)
    moe_part = jnp.dot(
        combine, results, precision=lax.Precision.HIGHEST, preferred_element_type=jnp.float32
    )
    moe_rows = lax.psum_scatter(
        moe_part.astype(jnp.bfloat16), "exp", scatter_dimension=0, tiled=True
    ).astype(jnp.float32)
    layer_out = (stream.astype(jnp.float32) + moe_rows).astype(jnp.bfloat16)
    return (
        layer_out[None],
        kept_keys.astype(jnp.bfloat16)[None],
        kept_values.astype(jnp.bfloat16)[None],
    )


def solution(mesh):
    return jax.shard_map(
        local,
        mesh=mesh,
        in_specs=(
            P("req", "ctx", "exp"),
            P("req", "ctx", "exp"),
            P("req", "ctx", "exp"),
            P("req", ("ctx", "exp"), None),
            P("ctx", "exp"),
            P(),
            P("ctx", None, "exp"),
            P("ctx", None, "exp"),
            P("ctx", "exp", None),
            P("req", "ctx", None),
            P("req", "ctx", None),
            P("req"),
        ),
        out_specs=(P("req", ("ctx", "exp"), None), P("req", "ctx", "exp"), P("req", "ctx", "exp")),
        check_vma=False,
    )
```

profile of v0, /device:TPU:0, one launch (start us, length us, event | category | flops | bytes accessed | tf_op | source)
XLA Modules:
  0.0 179.1 jit_solution(11814725338556139426)
XLA Ops:
  7.2 0.7 all-gather.2.cloned.1.call-update
  8.0 0.8 copy.47
  9.6 0.9 reshape_squeeze.10
  10.5 17.5 %all_gather.12 = bf16[1,512,512]{2,1,0:T(8,128)(2,1)S(1)} all-gather(bf16[1,64,512]{2,1,0:T(8,128)(2,1)} %param.13), channel_id=1, replica_groups=mesh['req'=2,'ctx'=8,'exp'=2] {'ctx'}, dimensions={1}, use_global_device_ids=true | all-gather | bytes 589824 | tf_op jit(solution)/shard_map/all_gather | solution.py:74
  28.0 0.2 copy.41
  28.2 18.0 %all_gather.13 = bf16[1,512,512]{2,1,0:T(8,128)(2,1)S(1)} all-gather(bf16[1,64,512]{2,1,0:T(8,128)(2,1)S(1)} %copy-done.4), channel_id=1, replica_groups=mesh['req'=2,'ctx'=8,'exp'=2] {'ctx'}, dimensions={1}, use_global_device_ids=true | all-gather | bytes 589824 | tf_op jit(solution)/shard_map/all_gather | solution.py:75
  46.2 1.0 copy.44
  47.2 0.6 reduce-window.6
  47.9 0.3 fusion.61
  48.2 0.2 fusion.19
  48.5 0.3 copy-done.3
  48.8 0.3 fusion.14
  49.2 3.1 %convolution_convert_fusion.3 = bf16[64,2048]{1,0:T(8,128)(2,1)} fusion(bf16[2048,512]{1,0:T(8,128)(2,1)} %all-gather.2.cloned.1.call-done, bf16[4,8,8,128]{3,2,1,0:T(8,128)(2,1)S(1)} %fusion.14), kind=kOutput, calls=%fused_computation.3 | convolution fusion | flops 134348800 | bytes 2424832 | tf_op jit(solution)/shard_map/tc,oc->to/dot_general | solution.py:103
  52.4 0.2 slice_reduce_fusion
  52.9 0.1 convert_reduce_fusion
  53.1 11.8 %reduce-scatter.3.cloned.1.call-done = bf16[32,2048]{1,0:T(8,128)(2,1)} async-done(((bf16[64,2048]{1,0:T(8,128)(2,1)}), bf16[32,2048]{1,0:T(8,128)(2,1)}) %reduce-scatter.3.cloned.1.call-update) | async-done | bytes 131088 | tf_op jit(solution)/shard_map/reduce_scatter | solution.py:109
  64.9 1.1 fusion.21
  65.9 1.0 fusion.23
  66.9 5.9 %all_gather.15 = bf16[64,2048]{1,0:T(8,128)(2,1)S(1)} all-gather(bf16[32,2048]{1,0:T(8,128)(2,1)S(1)} %fusion.23), channel_id=1, replica_groups=mesh['req'=2,'ctx'=8,'exp'=2] {'exp'}, dimensions={0}, use_global_device_ids=true | all-gather | bytes 393216 | tf_op jit(solution)/shard_map/all_gather | solution.py:116
  72.9 0.6 convolution_convert_fusion.1
  73.5 42.4 %all_to_all.10 = bf16[8,48,2048]{2,1,0:T(8,128)(2,1)S(1)} all-to-all(bf16[8,48,2048]{2,1,0:T(8,128)(2,1)S(1)} %bitcast.78), channel_id=1, replica_groups=mesh['req'=2,'ctx'=8,'exp'=2] {'ctx'}, dimensions={0} | all-to-all | bytes 3145728 | tf_op jit(solution)/shard_map/all_to_all | solution.py:123
  115.8 0.9 fusion.3
  116.8 0.4 copy-done.8
  117.2 0.9 fusion.9
  118.1 0.2 copy.51
  118.4 1.0 convolution_convert_fusion
  119.3 40.3 %all_to_all.11 = bf16[8,48,2048]{2,1,0:T(8,128)(2,1)S(1)} all-to-all(bf16[8,48,2048]{2,1,0:T(8,128)(2,1)S(1)} %convolution_convert_fusion), channel_id=1, replica_groups=mesh['req'=2,'ctx'=8,'exp'=2] {'ctx'}, dimensions={0} | all-to-all | bytes 3145728 | tf_op jit(solution)/shard_map/all_to_all | solution.py:129
  159.6 1.6 convolution_convert_fusion.2
  161.2 0.9 fusion.15
  162.1 0.9 fusion.16
  163.0 8.0 %reduce-scatter.5.cloned.1.call-done = bf16[32,2048]{1,0:T(8,128)(2,1)} async-done(((bf16[64,2048]{1,0:T(8,128)(2,1)}), bf16[32,2048]{1,0:T(8,128)(2,1)}) %reduce-scatter.5.cloned.1.call-update) | async-done | bytes 131088 | tf_op jit(solution)/shard_map/reduce_scatter | solution.py:136
  170.9 1.6 fusion.32
  (38 shorter events, 0.9 us)
Async XLA Ops:
  7.2 111.2 %copy-start = (bf16[1,352,2048]{2,1,0:T(8,128)(2,1)S(1)}, bf16[1,352,2048]{2,1,0:T(8,128)(2,1)}, u32[]{:S(2)}) copy-start(bf16[1,352,2048]{2,1,0:T(8,128)(2,1)} %param.20) | copy-start | bytes 4325380
  7.2 21.0 %copy-start.4 = (bf16[1,64,512]{2,1,0:T(8,128)(2,1)S(1)}, bf16[1,64,512]{2,1,0:T(8,128)(2,1)}, u32[]{:S(2)}) copy-start(bf16[1,64,512]{2,1,0:T(8,128)(2,1)} %param.14) | copy-start | bytes 196612
  7.2 42.0 %all-gather.2.cloned.1.call-start = ((), (), s32[]{:S(2)}) async-start(), calls=%async_computation.4 | async-start | bytes 2359296 | tf_op jit(solution)/shard_map/all_gather | solution.py:106
  7.9 56.9 %reduce-scatter.3.cloned.1.call-start = ((), (), s32[]{:S(2)}) async-start(), calls=%async_computation.5 | async-start | bytes 393216 | tf_op jit(solution)/shard_map/reduce_scatter | solution.py:109
  47.8 1.0 copy-start.3
  49.1 3.8 %copy-start.6 = (f32[1,64,4]{1,2,0:T(4,128)S(1)}, f32[1,64,4]{1,2,0:T(4,128)}, u32[]{:S(2)}) copy-start(f32[1,64,4]{1,2,0:T(4,128)} %param.22) | copy-start | bytes 3076
  49.2 15.7 %copy-start.1 = (bf16[1,32,2048]{2,1,0:T(8,128)(2,1)S(1)}, bf16[1,32,2048]{2,1,0:T(8,128)(2,1)}, u32[]{:S(2)}) copy-start(bf16[1,32,2048]{2,1,0:T(8,128)(2,1)} %param.15) | copy-start | bytes 393220
  49.2 16.7 %copy-start.5 = (f32[2048]{0:T(1024)S(1)}, f32[2048]{0:T(1024)}, u32[]{:S(2)}) copy-start(f32[2048]{0:T(1024)} %param.17) | copy-start | bytes 24580
  52.3 118.6 %reduce-scatter.5.cloned.1.call-start = ((), (), s32[]{:S(2)}) async-start(), calls=%async_computation.6 | async-start | bytes 393216 | tf_op jit(solution)/shard_map/reduce_scatter | solution.py:136
  73.4 42.4 %copy-start.7 = (bf16[1,2048,352]{1,2,0:T(8,128)(2,1)S(1)}, bf16[1,2048,352]{1,2,0:T(8,128)(2,1)}, u32[]{:S(2)}) copy-start(bf16[1,2048,352]{1,2,0:T(8,128)(2,1)} %param.18) | copy-start | bytes 4325380
  115.8 1.4 copy-start.8
  159.6 11.3 %copy-start.2 = (bf16[32,2048]{1,0:T(8,128)(2,1)S(1)}, bf16[32,2048]{1,0:T(8,128)(2,1)}, u32[]{:S(2)}) copy-start(bf16[32,2048]{1,0:T(8,128)(2,1)} %reduce-scatter.3.cloned.1.call-done) | copy-start | bytes 393220
Sparse Core Ops, SparseCore 0:
  9.6 37.8 all-gather.1
  52.5 12.3 reduce-scatter.2
  161.3 9.5 reduce-scatter.4
where the time goes:
time: 180 us; the launch traced here: 179 us
  blocking collectives  124 us (69%)
  waiting for transfers between devices  20.5 us (11%)
  between operations  14.6 us (8%)
  matrix products  10.5 us (6%)
  other arithmetic  4.92 us (3%)
  local copies, waits for them, and re-layouts  4.48 us (2%)
    all_to_all x1, blocking collectives, local(): lax.all_to_all(send_rows, 'ctx', split_axis=0, concat_axis=0, tiled=True)  42.4 us
    all_to_all x1, blocking collectives, local(): lax.all_to_all(produced.astype(jnp.bfloat16), 'ctx', split_axis=0, concat...  40.3 us
    all_gather x1, blocking collectives, local(): value_two = lax.all_gather(value_states, 'ctx', axis=1, tiled=True)[0]  18 us
    all_gather x1, blocking collectives, local(): key_two = lax.all_gather(key_states, 'ctx', axis=1, tiled=True)[0]  17.5 us
    reduce_scatter x1, waiting for transfers between devices, local(): lax.psum_scatter(out_parts.astype(jnp.bfloat16), 'exp', scatter_dimension...  11.8 us
    reduce_scatter x1, waiting for transfers between devices, local(): lax.psum_scatter(moe_part.astype(jnp.bfloat16), 'exp', scatter_dimension=...  7.99 us
    all_gather x1, blocking collectives, local(): all_normed = lax.all_gather(normed, 'exp', axis=0, tiled=True)  5.92 us
  transfers between devices with their start and end apart: 3, of which 2 were waited for; matrix products, arithmetic and copies ran while one was open for 4% of the time, Pallas kernels for 0%

commit v1 on v0

--- a/solution.py
+++ b/solution.py
@@ -44,6 +44,35 @@
     return jnp.dot(hidden, down_matrix, preferred_element_type=jnp.float32)
 
 
+def exp_swap(x):
+    return lax.ppermute(x, "exp", perm=[(0, 1), (1, 0)])
+
+
+def exp_reduce_rows(parts):
+    if lax.axis_size("exp") != 2:
+        return lax.psum_scatter(
+            parts.astype(jnp.bfloat16), "exp", scatter_dimension=0, tiled=True
+        ).astype(jnp.float32)
+    half = parts.shape[0] // 2
+    first = lax.axis_index("exp") == 0
+    lower = parts[:half]
+    upper = parts[half:]
+    mine = jnp.where(first, lower, upper)
+    theirs = jnp.where(first, upper, lower)
+    got = exp_swap(theirs.astype(jnp.bfloat16))
+    return mine + got.astype(jnp.float32)
+
+
+def exp_gather_rows(rows):
+    if lax.axis_size("exp") != 2:
+        return lax.all_gather(rows, "exp", axis=0, tiled=True)
+    got = exp_swap(rows)
+    first = lax.axis_index("exp") == 0
+    return jnp.where(
+        first, jnp.concatenate([rows, got], axis=0), jnp.concatenate([got, rows], axis=0)
+    )
+
+
 def local(
     query_states,
     key_states,
@@ -71,8 +100,10 @@
     decode_pos = my_ctx * tok_here + local_ids
     query_three = query_states[0].reshape(tok_here, heads_dev, HD)
     run_max = jnp.full((heads_dev, tok_here), NEG, jnp.float32)
-    key_two = lax.all_gather(key_states, "ctx", axis=1, tiled=True)[0]
-    value_two = lax.all_gather(value_states, "ctx", axis=1, tiled=True)[0]
+    kv_here = jnp.concatenate([key_states[0], value_states[0]], axis=1)
+    kv_all = lax.all_gather(kv_here, "ctx", axis=0, tiled=True)
+    key_two = kv_all[:, :feat_width]
+    value_two = kv_all[:, feat_width:]
     row_count = key_two.shape[0]
     key_pos = row_positions(jnp.arange(row_count, dtype=jnp.int32), half_block, n_ctx)
     pick_rows = (decode_pos[:, None] == key_pos[None, :]).astype(jnp.bfloat16)
@@ -106,14 +137,12 @@
         lax.all_gather(out_weight, "ctx", axis=0, tiled=True),
         preferred_element_type=jnp.float32,
     )
-    head_total = lax.psum_scatter(
-        out_parts.astype(jnp.bfloat16), "exp", scatter_dimension=0, tiled=True
-    ).astype(jnp.float32)
+    head_total = exp_reduce_rows(out_parts)
     stream = (residual[0].astype(jnp.float32) + head_total).astype(jnp.bfloat16)
     stream_f = stream.astype(jnp.float32)
     mean_sq = jnp.mean(stream_f * stream_f, axis=1, keepdims=True)
     normed = (stream_f * lax.rsqrt(mean_sq + EPS) * norm_gain).astype(jnp.bfloat16)
-    all_normed = lax.all_gather(normed, "exp", axis=0, tiled=True)
+    all_normed = exp_gather_rows(normed)
     capacity = min(tok_here, 2 * max(1, 3 * tok_here * TOP // (4 * n_ctx)))
     dispatch, combine = slot_tables(routes[0], route_weights[0], n_ctx, capacity)
     send_rows = jnp.dot(
@@ -133,9 +162,7 @@
     moe_part = jnp.dot(
         combine, results, precision=lax.Precision.HIGHEST, preferred_element_type=jnp.float32
     )
-    moe_rows = lax.psum_scatter(
-        moe_part.astype(jnp.bfloat16), "exp", scatter_dimension=0, tiled=True
-    ).astype(jnp.float32)
+    moe_rows = exp_reduce_rows(moe_part)
     layer_out = (stream.astype(jnp.float32) + moe_rows).astype(jnp.bfloat16)
     return (
         layer_out[None],

time: 180 us -> 180 us (level)
  blocking collectives: 124 us -> 41 us
  waiting for transfers between devices: 20.5 us -> 96.1 us
  starting transfers between devices: 0.12 us -> 8.24 us
    all_gather x3 -> x0, blocking collectives: 41.4 us -> none  [the longest x1 18 us: local(): value_two = lax.all_gather(value_states, 'ctx', axis=1, tiled=True)[0]]
    all_to_all x1 -> x0, blocking collectives: 40.3 us -> none  [local(): lax.all_to_all(produced.astype(jnp.bfloat16), 'ctx', split_axis=0, concat...]
    all_to_all x0 -> x1, waiting for transfers between devices: none -> 35.8 us  [local(): lax.all_to_all(produced.astype(jnp.bfloat16), 'ctx', split_axis=0, concat...]
    all_gather x1, waiting for transfers between devices: 0.02 us -> 27.7 us  [local(): lax.all_gather(out_weight, 'ctx', axis=0, tiled=True)]
    all_gather x0 -> x1, waiting for transfers between devices: none -> 22.2 us  [local(): kv_all = lax.all_gather(kv_here, 'ctx', axis=0, tiled=True)]
    reduce_scatter x2 -> x0, waiting for transfers between devices: 19.7 us -> none  [the longest x1 11.8 us: local(): lax.psum_scatter(out_parts.astype(jnp.bfloat16), 'exp', scatter_dimension...]
    ppermute x0 -> x3, waiting for transfers between devices: none -> 9.58 us  [exp_swap(): return lax.ppermute(x, 'exp', perm=[(0, 1), (1, 0)])]
    ppermute x0 -> x3, starting transfers between devices: none -> 4.58 us  [exp_swap(): return lax.ppermute(x, 'exp', perm=[(0, 1), (1, 0)])]
  transfers between devices with their start and end apart: 3 -> 6, of which waited for: 2 -> 6; matrix products, arithmetic and copies ran while one was open for 4% -> 5% of each run, Pallas kernels for 0% -> 0%
where the time goes in v1:
time: 180 us
  waiting for transfers between devices  96.1 us (53%)
  blocking collectives  41 us (23%)
  between operations  14.9 us (8%)
  matrix products  11.2 us (6%)
  starting transfers between devices  8.24 us (5%)
  local copies, waits for them, and re-layouts  4.62 us (3%)
  other arithmetic  3.95 us (2%)
    all_to_all x1, blocking collectives, local(): lax.all_to_all(send_rows, 'ctx', split_axis=0, concat_axis=0, tiled=True)  41 us
    all_to_all x1, waiting for transfers between devices, local(): lax.all_to_all(produced.astype(jnp.bfloat16), 'ctx', split_axis=0, concat...  35.8 us
    all_gather x1, waiting for transfers between devices, local(): lax.all_gather(out_weight, 'ctx', axis=0, tiled=True)  27.7 us
    all_gather x1, waiting for transfers between devices, local(): kv_all = lax.all_gather(kv_here, 'ctx', axis=0, tiled=True)  22.2 us
    ppermute x3, waiting for transfers between devices, exp_swap(): return lax.ppermute(x, 'exp', perm=[(0, 1), (1, 0)])  9.58 us
    ppermute x3, starting transfers between devices, exp_swap(): return lax.ppermute(x, 'exp', perm=[(0, 1), (1, 0)])  4.58 us
  transfers between devices with their start and end apart: 6, of which 6 were waited for; matrix products, arithmetic and copies ran while one was open for 5% of the time, Pallas kernels for 0%

profile of v1, /device:TPU:0, one launch (start us, length us, event | category | flops | bytes accessed | tf_op | source)
XLA Modules:
  0.0 180.0 jit_solution(15707757264715683724)
XLA Ops:
  7.2 1.6 pad_maximum_fusion
  8.9 0.7 all-gather.5.cloned.1.call-update
  10.3 0.8 copy.47
  11.2 0.6 reduce-window.6
  11.8 0.9 reshape_squeeze.4
  12.8 22.2 %all-gather.3.cloned.1.call-done = bf16[512,1024]{1,0:T(8,128)(2,1)} async-done(((bf16[64,1024]{1,0:T(8,128)(2,1)}), bf16[512,1024]{1,0:T(8,128)(2,1)}) %all-gather.3.cloned.1.call-update) | async-done | bytes 1048592 | tf_op jit(solution)/shard_map/all_gather | solution.py:104
  35.0 1.3 fusion.71
  36.3 0.2 copy.54
  36.7 0.3 fusion.72
  37.1 0.2 fusion.18
  37.3 0.3 fusion.15
  37.7 27.7 %all-gather.5.cloned.1.call-done = bf16[2048,512]{1,0:T(8,128)(2,1)} async-done(((bf16[256,512]{1,0:T(8,128)(2,1)}), bf16[2048,512]{1,0:T(8,128)(2,1)}) %all-gather.5.cloned.1.call-update) | async-done | bytes 2097168 | tf_op jit(solution)/shard_map/all_gather | solution.py:137
  65.4 2.3 %fusion.38 = f32[64,2048]{1,0:T(8,128)S(1)} fusion(bf16[2048,512]{1,0:T(8,128)(2,1)} %all-gather.5.cloned.1.call-done, bf16[4,8,8,128]{3,2,1,0:T(8,128)(2,1)S(1)} %fusion.15), kind=kOutput, calls=%fused_computation.52 | convolution fusion | flops 134217728 | bytes 2686976 | tf_op jit(solution)/shard_map/tc,oc->to/dot_general | solution.py:134
  67.8 1.5 collective-permute-start
  69.9 3.6 %collective-permute-done = bf16[32,2048]{1,0:T(8,128)(2,1)S(1)} collective-permute-done((bf16[32,2048]{1,0:T(8,128)(2,1)S(1)}, bf16[32,2048]{1,0:T(8,128)(2,1)S(1)}, u32[]{:S(2)}, u32[]{:S(2)}) %collective-permute-start) | collective-permute-done | bytes 131104 | tf_op jit(solution)/shard_map/ppermute | solution.py:48
  73.8 1.5 collective-permute-start.1
  75.6 3.3 %collective-permute-done.1 = bf16[32,2048]{1,0:T(8,128)(2,1)S(1)} collective-permute-done((bf16[32,2048]{1,0:T(8,128)(2,1)S(1)}, bf16[32,2048]{1,0:T(8,128)(2,1)S(1)}, u32[]{:S(2)}, u32[]{:S(2)}) %collective-permute-start.1) | collective-permute-done | bytes 131104 | tf_op jit(solution)/shard_map/ppermute | solution.py:48
  78.8 0.6 convolution_convert_fusion.1
  79.4 41.0 %all_to_all.10 = bf16[8,48,2048]{2,1,0:T(8,128)(2,1)S(1)} all-to-all(bf16[8,48,2048]{2,1,0:T(8,128)(2,1)S(1)} %bitcast.73), channel_id=1, replica_groups=mesh['req'=2,'ctx'=8,'exp'=2] {'ctx'}, dimensions={0} | all-to-all | bytes 3145728 | tf_op jit(solution)/shard_map/all_to_all | solution.py:152
  120.4 0.9 fusion.3
  121.3 0.4 copy-done.6
  121.8 0.9 fusion.10
  122.7 0.2 copy.51
  122.9 2.1 %convolution_convert_fusion = bf16[8,48,2048]{2,1,0:T(8,128)(2,1)} fusion(bf16[8,48,352]{2,1,0:T(8,128)(2,1)S(1)} %bitcast.77, bf16[1,352,2048]{2,1,0:T(8,128)(2,1)S(1)} %copy-done), kind=kOutput, calls=%fused_computation | convolution fusion | flops 554434560 | bytes 3284992 | tf_op jit(solution)/shard_map/dot_general | solution.py:44
  125.1 3.6 %all-to-all-start.1 = ((bf16[8,48,2048]{2,1,0:T(8,128)(2,1)}), bf16[8,48,2048]{2,1,0:T(8,128)(2,1)S(1)}, u32[]{:S(2)}, u32[]{:S(2)}) async-start(bf16[8,48,2048]{2,1,0:T(8,128)(2,1)} %convolution_convert_fusion), calls=%async_computation.1 | async-start | bytes 3145728 | tf_op jit(solution)/shard_map/all_to_all | solution.py:158
  128.7 1.9 %fusion.17 = bf16[1,64,512]{2,1,0:T(8,128)(2,1)} fusion(s32[512]{0:T(512)S(1)} %fusion.56, s32[64]{0:T(128)S(1)} %iota_add_fusion, bf16[512,1024]{1,0:T(8,128)(2,1)} %all-gather.3.cloned.1.call-done), kind=kOutput, calls=%fused_computation.19 | convolution fusion | flops 33619968 | bytes 592128 | tf_op jit(solution)/shard_map/dot_general | solution.py:111
  130.6 35.8 %all-to-all-done.1 = bf16[8,48,2048]{2,1,0:T(8,128)(2,1)S(1)} async-done(((bf16[8,48,2048]{2,1,0:T(8,128)(2,1)}), bf16[8,48,2048]{2,1,0:T(8,128)(2,1)S(1)}, u32[]{:S(2)}, u32[]{:S(2)}) %all-to-all-start.1) | async-done | bytes 1572896 | tf_op jit(solution)/shard_map/all_to_all | solution.py:158
  166.4 0.9 fusion.73
  167.3 1.5 collective-permute-start.2
  168.8 0.9 fusion.16
  169.7 2.7 %collective-permute-done.2 = bf16[32,2048]{1,0:T(8,128)(2,1)S(1)} collective-permute-done((bf16[32,2048]{1,0:T(8,128)(2,1)S(1)}, bf16[32,2048]{1,0:T(8,128)(2,1)S(1)}, u32[]{:S(2)}, u32[]{:S(2)}) %collective-permute-start.2) | collective-permute-done | bytes 131104 | tf_op jit(solution)/shard_map/ppermute | solution.py:48
  172.4 0.7 fusion.37
  (39 shorter events, 1.7 us)
Async XLA Ops:
  7.2 115.8 %copy-start = (bf16[1,352,2048]{2,1,0:T(8,128)(2,1)S(1)}, bf16[1,352,2048]{2,1,0:T(8,128)(2,1)}, u32[]{:S(2)}) copy-start(bf16[1,352,2048]{2,1,0:T(8,128)(2,1)} %param.20) | copy-start | bytes 4325380
  7.2 27.9 %all-gather.3.cloned.1.call-start = ((), (), s32[]{:S(2)}) async-start(), calls=%async_computation.2 | async-start | bytes 1179648 | tf_op jit(solution)/shard_map/all_gather | solution.py:104
  8.9 56.5 %all-gather.5.cloned.1.call-start = ((), (), s32[]{:S(2)}) async-start(), calls=%async_computation.3 | async-start | bytes 2359296 | tf_op jit(solution)/shard_map/all_gather | solution.py:137
  37.7 35.8 %copy-start.2 = (bf16[1,32,2048]{2,1,0:T(8,128)(2,1)S(1)}, bf16[1,32,2048]{2,1,0:T(8,128)(2,1)}, u32[]{:S(2)}) copy-start(bf16[1,32,2048]{2,1,0:T(8,128)(2,1)} %param.15) | copy-start | bytes 393220
  37.7 36.0 %copy-start.3 = (f32[2048]{0:T(1024)S(1)}, f32[2048]{0:T(1024)}, u32[]{:S(2)}) copy-start(f32[2048]{0:T(1024)} %param.17) | copy-start | bytes 24580
  67.7 7.7 %copy-start.4 = (f32[1,64,4]{1,2,0:T(4,128)S(1)}, f32[1,64,4]{1,2,0:T(4,128)}, u32[]{:S(2)}) copy-start(f32[1,64,4]{1,2,0:T(4,128)} %param.22) | copy-start | bytes 3076
  67.8 5.7 %collective-permute-start = (bf16[32,2048]{1,0:T(8,128)(2,1)S(1)}, bf16[32,2048]{1,0:T(8,128)(2,1)S(1)}, u32[]{:S(2)}, u32[]{:S(2)}) collective-permute-start(bf16[32,2048]{1,0:T(8,128)(2,1)S(1)} %select_convert_fusion.1), channel_id=1, source_target_pairs={{0,1},{1,0},{2,3},{3,2},{4,5},{5,4},{6,7},{7,6},{8,9},{9,8},{10,11... | collective-permute-start | bytes 393224 | tf_op jit(solution)/shard_map/ppermute | solution.py:48
  73.8 5.0 %collective-permute-start.1 = (bf16[32,2048]{1,0:T(8,128)(2,1)S(1)}, bf16[32,2048]{1,0:T(8,128)(2,1)S(1)}, u32[]{:S(2)}, u32[]{:S(2)}) collective-permute-start(bf16[32,2048]{1,0:T(8,128)(2,1)S(1)} %fusion.22), channel_id=1, source_target_pairs={{0,1},{1,0},{2,3},{3,2},{4,5},{5,4},{6,7},{7,6},{8,9},{9,8},{10,11... | collective-permute-start | bytes 393224 | tf_op jit(solution)/shard_map/ppermute | solution.py:48
  79.4 41.0 %copy-start.5 = (bf16[1,2048,352]{1,2,0:T(8,128)(2,1)S(1)}, bf16[1,2048,352]{1,2,0:T(8,128)(2,1)}, u32[]{:S(2)}) copy-start(bf16[1,2048,352]{1,2,0:T(8,128)(2,1)} %param.18) | copy-start | bytes 4325380
  120.4 1.4 copy-start.6
  125.1 41.3 %all-to-all-start.1 = ((bf16[8,48,2048]{2,1,0:T(8,128)(2,1)}), bf16[8,48,2048]{2,1,0:T(8,128)(2,1)S(1)}, u32[]{:S(2)}, u32[]{:S(2)}) async-start(bf16[8,48,2048]{2,1,0:T(8,128)(2,1)} %convolution_convert_fusion), calls=%async_computation.1 | async-start | bytes 3145728 | tf_op jit(solution)/shard_map/all_to_all | solution.py:158
  166.4 2.4 %copy-start.1 = (bf16[512,1024]{1,0:T(8,128)(2,1)S(1)}, bf16[512,1024]{1,0:T(8,128)(2,1)}, u32[]{:S(2)}) copy-start(bf16[512,1024]{1,0:T(8,128)(2,1)} %all-gather.3.cloned.1.call-done) | copy-start | bytes 3145732
  167.3 5.1 %collective-permute-start.2 = (bf16[32,2048]{1,0:T(8,128)(2,1)S(1)}, bf16[32,2048]{1,0:T(8,128)(2,1)S(1)}, u32[]{:S(2)}, u32[]{:S(2)}) collective-permute-start(bf16[32,2048]{1,0:T(8,128)(2,1)S(1)} %select_convert_fusion), channel_id=1, source_target_pairs={{0,1},{1,0},{2,3},{3,2},{4,5},{5,4},{6,7},{7,6},{8,9},{9,8},{10,11... | collective-permute-start | bytes 393224 | tf_op jit(solution)/shard_map/ppermute | solution.py:48
Sparse Core Ops, SparseCore 0:
  10.2 24.8 all-gather.2
  36.6 28.7 all-gather.4

commit v2 on v1

--- a/solution.py
+++ b/solution.py
@@ -100,10 +100,8 @@
     decode_pos = my_ctx * tok_here + local_ids
     query_three = query_states[0].reshape(tok_here, heads_dev, HD)
     run_max = jnp.full((heads_dev, tok_here), NEG, jnp.float32)
-    kv_here = jnp.concatenate([key_states[0], value_states[0]], axis=1)
-    kv_all = lax.all_gather(kv_here, "ctx", axis=0, tiled=True)
-    key_two = kv_all[:, :feat_width]
-    value_two = kv_all[:, feat_width:]
+    key_two = lax.all_gather(key_states, "ctx", axis=1, tiled=True)[0]
+    value_two = lax.all_gather(value_states, "ctx", axis=1, tiled=True)[0]
     row_count = key_two.shape[0]
     key_pos = row_positions(jnp.arange(row_count, dtype=jnp.int32), half_block, n_ctx)
     pick_rows = (decode_pos[:, None] == key_pos[None, :]).astype(jnp.bfloat16)

time: 180 us -> 167 us (0.928)
  waiting for transfers between devices: 96.1 us -> 45.4 us
  blocking collectives: 41 us -> 77.5 us
    all_gather x0 -> x2, blocking collectives: none -> 35.5 us  [the longest x1 17.9 us: local(): key_two = lax.all_gather(key_states, 'ctx', axis=1, tiled=True)[0]]
    all_gather x1, waiting for transfers between devices: 27.7 us -> 0.02 us  [local(): lax.all_gather(out_weight, 'ctx', axis=0, tiled=True)]
    all_gather x1 -> x0, waiting for transfers between devices: 22.2 us -> none  [local(): kv_all = lax.all_gather(kv_here, 'ctx', axis=0, tiled=True)]
  transfers between devices with their start and end apart: 6 -> 5, of which waited for: 6 -> 4; matrix products, arithmetic and copies ran while one was open for 5% -> 5% of each run, Pallas kernels for 0% -> 0%
where the time goes in v2:
time: 167 us; the launch traced here: 166 us
  blocking collectives  77.5 us (46%)
  waiting for transfers between devices  45.4 us (27%)
  between operations  14.9 us (9%)
  matrix products  12.2 us (7%)
  starting transfers between devices  8.39 us (5%)
  local copies, waits for them, and re-layouts  4.79 us (3%)
  other arithmetic  2.92 us (2%)
    all_to_all x1, blocking collectives, local(): lax.all_to_all(send_rows, 'ctx', split_axis=0, concat_axis=0, tiled=True)  42.1 us
    all_to_all x1, waiting for transfers between devices, local(): lax.all_to_all(produced.astype(jnp.bfloat16), 'ctx', split_axis=0, concat...  35.8 us
    all_gather x1, blocking collectives, local(): key_two = lax.all_gather(key_states, 'ctx', axis=1, tiled=True)[0]  17.9 us
    all_gather x1, blocking collectives, local(): value_two = lax.all_gather(value_states, 'ctx', axis=1, tiled=True)[0]  17.5 us
    ppermute x3, waiting for transfers between devices, exp_swap(): return lax.ppermute(x, 'exp', perm=[(0, 1), (1, 0)])  8.88 us
    ppermute x3, starting transfers between devices, exp_swap(): return lax.ppermute(x, 'exp', perm=[(0, 1), (1, 0)])  4.77 us
    all_to_all x1, starting transfers between devices, local(): lax.all_to_all(produced.astype(jnp.bfloat16), 'ctx', split_axis=0, concat...  3.58 us
  transfers between devices with their start and end apart: 5, of which 4 were waited for; matrix products, arithmetic and copies ran while one was open for 5% of the time, Pallas kernels for 0%

profile of v2, /device:TPU:0, one launch (start us, length us, event | category | flops | bytes accessed | tf_op | source)
XLA Modules:
  0.0 166.1 jit_solution(13683940806211899243)
XLA Ops:
  7.2 0.7 all-gather.2.cloned.1.call-update
  8.6 0.8 copy.47
  9.5 0.6 reduce-window.6
  10.1 0.9 reshape_squeeze.10
  10.9 17.9 %all_gather.9 = bf16[1,512,512]{2,1,0:T(8,128)(2,1)S(1)} all-gather(bf16[1,64,512]{2,1,0:T(8,128)(2,1)} %param.13), channel_id=1, replica_groups=mesh['req'=2,'ctx'=8,'exp'=2] {'ctx'}, dimensions={1}, use_global_device_ids=true | all-gather | bytes 589824 | tf_op jit(solution)/shard_map/all_gather | solution.py:103
  28.9 0.8 copy-done.1
  29.9 17.5 %all_gather.10 = bf16[1,512,512]{2,1,0:T(8,128)(2,1)S(1)} all-gather(bf16[1,64,512]{2,1,0:T(8,128)(2,1)S(1)} %copy-done.5), channel_id=1, replica_groups=mesh['req'=2,'ctx'=8,'exp'=2] {'ctx'}, dimensions={1}, use_global_device_ids=true | all-gather | bytes 589824 | tf_op jit(solution)/shard_map/all_gather | solution.py:104
  47.8 0.3 fusion.70
  48.1 0.2 fusion.19
  48.4 0.3 fusion.14
  48.8 2.4 %fusion.39 = f32[64,2048]{1,0:T(8,128)S(1)} fusion(bf16[2048,512]{1,0:T(8,128)(2,1)} %all-gather.2.cloned.1.call-done, bf16[4,8,8,128]{3,2,1,0:T(8,128)(2,1)S(1)} %fusion.14), kind=kOutput, calls=%fused_computation.52 | convolution fusion | flops 134217728 | bytes 2686976 | tf_op jit(solution)/shard_map/tc,oc->to/dot_general | solution.py:132
  51.2 1.6 collective-permute-start
  53.3 3.6 %collective-permute-done = bf16[32,2048]{1,0:T(8,128)(2,1)S(1)} collective-permute-done((bf16[32,2048]{1,0:T(8,128)(2,1)S(1)}, bf16[32,2048]{1,0:T(8,128)(2,1)S(1)}, u32[]{:S(2)}, u32[]{:S(2)}) %collective-permute-start) | collective-permute-done | bytes 131104 | tf_op jit(solution)/shard_map/ppermute | solution.py:48
  57.2 0.6 copy-done.2
  57.9 1.6 collective-permute-start.1
  59.6 0.8 convert_reduce_fusion
  60.4 2.6 %collective-permute-done.1 = bf16[32,2048]{1,0:T(8,128)(2,1)S(1)} collective-permute-done((bf16[32,2048]{1,0:T(8,128)(2,1)S(1)}, bf16[32,2048]{1,0:T(8,128)(2,1)S(1)}, u32[]{:S(2)}, u32[]{:S(2)}) %collective-permute-start.1) | collective-permute-done | bytes 131104 | tf_op jit(solution)/shard_map/ppermute | solution.py:48
  63.0 0.6 convolution_convert_fusion.1
  63.6 42.1 %all_to_all.10 = bf16[8,48,2048]{2,1,0:T(8,128)(2,1)S(1)} all-to-all(bf16[8,48,2048]{2,1,0:T(8,128)(2,1)S(1)} %bitcast.73), channel_id=1, replica_groups=mesh['req'=2,'ctx'=8,'exp'=2] {'ctx'}, dimensions={0} | all-to-all | bytes 3145728 | tf_op jit(solution)/shard_map/all_to_all | solution.py:150
  105.6 0.9 fusion.3
  106.5 0.4 copy-done.9
  107.0 0.9 fusion.9
  107.9 0.2 copy.51
  108.2 2.1 %convolution_convert_fusion = bf16[8,48,2048]{2,1,0:T(8,128)(2,1)} fusion(bf16[8,48,352]{2,1,0:T(8,128)(2,1)S(1)} %bitcast.77, bf16[1,352,2048]{2,1,0:T(8,128)(2,1)S(1)} %copy-done), kind=kOutput, calls=%fused_computation | convolution fusion | flops 554434560 | bytes 3284992 | tf_op jit(solution)/shard_map/dot_general | solution.py:44
  110.3 3.6 %all-to-all-start.1 = ((bf16[8,48,2048]{2,1,0:T(8,128)(2,1)}), bf16[8,48,2048]{2,1,0:T(8,128)(2,1)S(1)}, u32[]{:S(2)}, u32[]{:S(2)}) async-start(bf16[8,48,2048]{2,1,0:T(8,128)(2,1)} %convolution_convert_fusion), calls=%async_computation.1 | async-start | bytes 3145728 | tf_op jit(solution)/shard_map/all_to_all | solution.py:156
  113.9 1.9 %fusion.15 = bf16[1,64,512]{2,1,0:T(8,128)(2,1)} fusion(bf16[1,512,512]{2,1,0:T(8,128)(2,1)} %copy-done.1, s32[512]{0:T(512)S(1)} %fusion.57, s32[64]{0:T(128)S(1)} %iota_add_fusion), kind=kOutput, calls=%fused_computation.17 | convolution fusion | flops 33619968 | bytes 592128 | tf_op jit(solution)/shard_map/dot_general | solution.py:108
  115.8 35.8 %all-to-all-done.1 = bf16[8,48,2048]{2,1,0:T(8,128)(2,1)S(1)} async-done(((bf16[8,48,2048]{2,1,0:T(8,128)(2,1)}), bf16[8,48,2048]{2,1,0:T(8,128)(2,1)S(1)}, u32[]{:S(2)}, u32[]{:S(2)}) %all-to-all-start.1) | async-done | bytes 1572896 | tf_op jit(solution)/shard_map/all_to_all | solution.py:156
  151.6 1.8 %fusion.71 = f32[64,2048]{1,0:T(8,128)S(1)} fusion(f32[384,64]{0,1:T(8,128)} %get-tuple-element.4, bf16[384,2048]{1,0:T(8,128)(2,1)S(1)} %bitcast.72), kind=kOutput, calls=%fused_computation.113 | convolution fusion | flops 603979776 | bytes 2195456 | tf_op jit(solution)/shard_map/dot_general | solution.py:160
  153.5 1.6 collective-permute-start.2
  155.1 0.9 fusion.16
  155.9 2.6 %collective-permute-done.2 = bf16[32,2048]{1,0:T(8,128)(2,1)S(1)} collective-permute-done((bf16[32,2048]{1,0:T(8,128)(2,1)S(1)}, bf16[32,2048]{1,0:T(8,128)(2,1)S(1)}, u32[]{:S(2)}, u32[]{:S(2)}) %collective-permute-start.2) | collective-permute-done | bytes 131104 | tf_op jit(solution)/shard_map/ppermute | solution.py:48
  158.6 0.7 fusion.38
  (42 shorter events, 1.8 us)
Async XLA Ops:
  7.2 101.0 %copy-start = (bf16[1,352,2048]{2,1,0:T(8,128)(2,1)S(1)}, bf16[1,352,2048]{2,1,0:T(8,128)(2,1)}, u32[]{:S(2)}) copy-start(bf16[1,352,2048]{2,1,0:T(8,128)(2,1)} %param.20) | copy-start | bytes 4325380
  7.2 22.7 %copy-start.5 = (bf16[1,64,512]{2,1,0:T(8,128)(2,1)S(1)}, bf16[1,64,512]{2,1,0:T(8,128)(2,1)}, u32[]{:S(2)}) copy-start(bf16[1,64,512]{2,1,0:T(8,128)(2,1)} %param.14) | copy-start | bytes 196612
  7.2 41.6 %all-gather.2.cloned.1.call-start = ((), (), s32[]{:S(2)}) async-start(), calls=%async_computation.2 | async-start | bytes 2359296 | tf_op jit(solution)/shard_map/all_gather | solution.py:135
  28.9 0.8 copy-start.1
  48.7 8.3 %copy-start.4 = (bf16[1,32,2048]{2,1,0:T(8,128)(2,1)S(1)}, bf16[1,32,2048]{2,1,0:T(8,128)(2,1)}, u32[]{:S(2)}) copy-start(bf16[1,32,2048]{2,1,0:T(8,128)(2,1)} %param.15) | copy-start | bytes 393220
  48.7 9.1 %copy-start.6 = (f32[2048]{0:T(1024)S(1)}, f32[2048]{0:T(1024)}, u32[]{:S(2)}) copy-start(f32[2048]{0:T(1024)} %param.17) | copy-start | bytes 24580
  51.1 8.5 %copy-start.7 = (f32[1,64,4]{1,2,0:T(4,128)S(1)}, f32[1,64,4]{1,2,0:T(4,128)}, u32[]{:S(2)}) copy-start(f32[1,64,4]{1,2,0:T(4,128)} %param.22) | copy-start | bytes 3076
  51.2 5.8 %collective-permute-start = (bf16[32,2048]{1,0:T(8,128)(2,1)S(1)}, bf16[32,2048]{1,0:T(8,128)(2,1)S(1)}, u32[]{:S(2)}, u32[]{:S(2)}) collective-permute-start(bf16[32,2048]{1,0:T(8,128)(2,1)S(1)} %select_convert_fusion.1), channel_id=1, source_target_pairs={{0,1},{1,0},{2,3},{3,2},{4,5},{5,4},{6,7},{7,6},{8,9},{9,8},{10,11... | collective-permute-start | bytes 393224 | tf_op jit(solution)/shard_map/ppermute | solution.py:48
  57.2 0.7 copy-start.2
  57.9 5.0 %collective-permute-start.1 = (bf16[32,2048]{1,0:T(8,128)(2,1)S(1)}, bf16[32,2048]{1,0:T(8,128)(2,1)S(1)}, u32[]{:S(2)}, u32[]{:S(2)}) collective-permute-start(bf16[32,2048]{1,0:T(8,128)(2,1)S(1)} %fusion.23), channel_id=1, source_target_pairs={{0,1},{1,0},{2,3},{3,2},{4,5},{5,4},{6,7},{7,6},{8,9},{9,8},{10,11... | collective-permute-start | bytes 393224 | tf_op jit(solution)/shard_map/ppermute | solution.py:48
  63.6 42.1 %copy-start.8 = (bf16[1,2048,352]{1,2,0:T(8,128)(2,1)S(1)}, bf16[1,2048,352]{1,2,0:T(8,128)(2,1)}, u32[]{:S(2)}) copy-start(bf16[1,2048,352]{1,2,0:T(8,128)(2,1)} %param.18) | copy-start | bytes 4325380
  105.6 1.4 copy-start.9
  110.3 41.3 %all-to-all-start.1 = ((bf16[8,48,2048]{2,1,0:T(8,128)(2,1)}), bf16[8,48,2048]{2,1,0:T(8,128)(2,1)S(1)}, u32[]{:S(2)}, u32[]{:S(2)}) async-start(bf16[8,48,2048]{2,1,0:T(8,128)(2,1)} %convolution_convert_fusion), calls=%async_computation.1 | async-start | bytes 3145728 | tf_op jit(solution)/shard_map/all_to_all | solution.py:156
  151.6 6.9 %copy-start.3 = (bf16[32,2048]{1,0:T(8,128)(2,1)S(1)}, bf16[32,2048]{1,0:T(8,128)(2,1)}, u32[]{:S(2)}) copy-start(bf16[32,2048]{1,0:T(8,128)(2,1)} %copy-done.2) | copy-start | bytes 393220
  153.5 5.1 %collective-permute-start.2 = (bf16[32,2048]{1,0:T(8,128)(2,1)S(1)}, bf16[32,2048]{1,0:T(8,128)(2,1)S(1)}, u32[]{:S(2)}, u32[]{:S(2)}) collective-permute-start(bf16[32,2048]{1,0:T(8,128)(2,1)S(1)} %select_convert_fusion), channel_id=1, source_target_pairs={{0,1},{1,0},{2,3},{3,2},{4,5},{5,4},{6,7},{7,6},{8,9},{9,8},{10,11... | collective-permute-start | bytes 393224 | tf_op jit(solution)/shard_map/ppermute | solution.py:48
Sparse Core Ops, SparseCore 0:
  9.6 36.9 all-gather.1

commit v3 on v2

--- a/solution.py
+++ b/solution.py
@@ -71,6 +71,90 @@
     return jnp.where(
         first, jnp.concatenate([rows, got], axis=0), jnp.concatenate([got, rows], axis=0)
     )
+
+
+def moe_whole_rows(normed, dispatch, combine, gate_matrix, up_matrix, down_matrix, n_ctx, capacity):
+    all_normed = lax.all_gather(normed, "exp", axis=0, tiled=True)
+    send_rows = jnp.dot(
+        dispatch.astype(jnp.bfloat16), all_normed, preferred_element_type=jnp.float32
+    ).astype(jnp.bfloat16)
+    send_rows = send_rows.reshape(n_ctx, capacity, D)
+    arrived = lax.all_to_all(send_rows, "ctx", split_axis=0, concat_axis=0, tiled=True)
+    flat_rows = arrived.reshape(n_ctx * capacity, D)
+    produced = expert_ffn(flat_rows, gate_matrix, up_matrix, down_matrix).reshape(
+        n_ctx, capacity, D
+    )
+    served = lax.all_to_all(
+        produced.astype(jnp.bfloat16), "ctx", split_axis=0, concat_axis=0, tiled=True
+    )
+    results = served.reshape(n_ctx * capacity, D).astype(jnp.float32)
+    moe_part = jnp.dot(
+        combine, results, precision=lax.Precision.HIGHEST, preferred_element_type=jnp.float32
+    )
+    return lax.psum_scatter(
+        moe_part.astype(jnp.bfloat16), "exp", scatter_dimension=0, tiled=True
+    ).astype(jnp.float32)
+
+
+def halves(x, first, axis):
+    size = x.shape[axis] // 2
+    lower = lax.slice_in_dim(x, 0, size, axis=axis)
+    upper = lax.slice_in_dim(x, size, 2 * size, axis=axis)
+    return jnp.where(first, lower, upper), jnp.where(first, upper, lower)
+
+
+def join(mine, theirs, first, axis):
+    return jnp.where(
+        first,
+        jnp.concatenate([mine, theirs], axis=axis),
+        jnp.concatenate([theirs, mine], axis=axis),
+    )
+
+
+def moe_column_halves(normed, dispatch, combine, gate_matrix, up_matrix, down_matrix, n_ctx, capacity):
+    my_exp = lax.axis_index("exp")
+    first = my_exp == 0
+    half_d = normed.shape[1] // 2
+    my_cols, other_cols = halves(normed, first, 1)
+    tokens_cols = join(my_cols, exp_swap(other_cols), first, 0)
+    send_rows = jnp.dot(
+        dispatch.astype(jnp.bfloat16), tokens_cols, preferred_element_type=jnp.float32
+    ).astype(jnp.bfloat16)
+    arrived = lax.all_to_all(
+        send_rows.reshape(n_ctx, capacity, half_d), "ctx", split_axis=0, concat_axis=0, tiled=True
+    ).reshape(n_ctx * capacity, half_d)
+    partner_cols = exp_swap(arrived)
+    my_start = my_exp * half_d
+    other_start = (1 - my_exp) * half_d
+    gate_mine = lax.dynamic_slice_in_dim(gate_matrix, my_start, half_d, axis=0)
+    gate_other = lax.dynamic_slice_in_dim(gate_matrix, other_start, half_d, axis=0)
+    up_mine = lax.dynamic_slice_in_dim(up_matrix, my_start, half_d, axis=0)
+    up_other = lax.dynamic_slice_in_dim(up_matrix, other_start, half_d, axis=0)
+    gate_act = jnp.dot(arrived, gate_mine, preferred_element_type=jnp.float32) + jnp.dot(
+        partner_cols, gate_other, preferred_element_type=jnp.float32
+    )
+    up_act = jnp.dot(arrived, up_mine, preferred_element_type=jnp.float32) + jnp.dot(
+        partner_cols, up_other, preferred_element_type=jnp.float32
+    )
+    hidden = (jax.nn.silu(gate_act) * up_act).astype(jnp.bfloat16)
+    down_other = lax.dynamic_slice_in_dim(down_matrix, other_start, half_d, axis=1)
+    down_mine = lax.dynamic_slice_in_dim(down_matrix, my_start, half_d, axis=1)
+    out_other = jnp.dot(hidden, down_other, preferred_element_type=jnp.float32)
+    got_other = exp_swap(out_other.astype(jnp.bfloat16))
+    out_mine = jnp.dot(hidden, down_mine, preferred_element_type=jnp.float32)
+    summed = (out_mine + got_other.astype(jnp.float32)).astype(jnp.bfloat16)
+    served = lax.all_to_all(
+        summed.reshape(n_ctx, capacity, half_d), "ctx", split_axis=0, concat_axis=0, tiled=True
+    ).reshape(n_ctx * capacity, half_d)
+    moe_half = jnp.dot(
+        combine,
+        served.astype(jnp.float32),
+        precision=lax.Precision.HIGHEST,
+        preferred_element_type=jnp.float32,
+    )
+    my_tok, other_tok = halves(moe_half, first, 0)
+    got_tok = exp_swap(other_tok.astype(jnp.bfloat16)).astype(jnp.float32)
+    return join(my_tok, got_tok, first, 1)
 
 
 def local(
@@ -140,27 +224,16 @@
     stream_f = stream.astype(jnp.float32)
     mean_sq = jnp.mean(stream_f * stream_f, axis=1, keepdims=True)
     normed = (stream_f * lax.rsqrt(mean_sq + EPS) * norm_gain).astype(jnp.bfloat16)
-    all_normed = exp_gather_rows(normed)
     capacity = min(tok_here, 2 * max(1, 3 * tok_here * TOP // (4 * n_ctx)))
     dispatch, combine = slot_tables(routes[0], route_weights[0], n_ctx, capacity)
-    send_rows = jnp.dot(
-        dispatch.astype(jnp.bfloat16), all_normed, preferred_element_type=jnp.float32
-    ).astype(jnp.bfloat16)
-    send_rows = send_rows.reshape(n_ctx, capacity, D)
-    arrived = lax.all_to_all(send_rows, "ctx", split_axis=0, concat_axis=0, tiled=True)
-    slot_count = arrived.shape[1]
-    flat_rows = arrived.reshape(n_ctx * slot_count, D)
-    produced = expert_ffn(flat_rows, gate_weight[0], up_weight[0], down_weight[0]).reshape(
-        n_ctx, slot_count, D
-    )
-    served = lax.all_to_all(
-        produced.astype(jnp.bfloat16), "ctx", split_axis=0, concat_axis=0, tiled=True
-    ).astype(produced.dtype)
-    results = served.reshape(n_ctx * capacity, D)
-    moe_part = jnp.dot(
-        combine, results, precision=lax.Precision.HIGHEST, preferred_element_type=jnp.float32
-    )
-    moe_rows = exp_reduce_rows(moe_part)
+    if lax.axis_size("exp") == 2:
+        moe_rows = moe_column_halves(
+            normed, dispatch, combine, gate_weight[0], up_weight[0], down_weight[0], n_ctx, capacity
+        )
+    else:
+        moe_rows = moe_whole_rows(
+            normed, dispatch, combine, gate_weight[0], up_weight[0], down_weight[0], n_ctx, capacity
+        )
     layer_out = (stream.astype(jnp.float32) + moe_rows).astype(jnp.bfloat16)
     return (
         layer_out[None],

time: 167 us -> 168 us (level)
  blocking collectives: 77.5 us -> 60.6 us
  waiting for transfers between devices: 45.4 us -> 61.3 us
  starting transfers between devices: 8.39 us -> 11.6 us
  local copies, waits for them, and re-layouts: 4.79 us -> 2.98 us
    ppermute x3 -> x5, waiting for transfers between devices: 8.88 us -> 41.3 us  [exp_swap(): return lax.ppermute(x, 'exp', perm=[(0, 1), (1, 0)])]
    all_to_all x1, blocking collectives: 42.1 us -> 25.1 us  [moe_column_halves(): lax.all_to_all(send_rows.reshape(n_ctx, capacity, half_d), 'ctx', split_a...]
    all_to_all x1, waiting for transfers between devices: 35.8 us -> 19.2 us  [moe_column_halves(): lax.all_to_all(summed.reshape(n_ctx, capacity, half_d), 'ctx', split_axis...]
    ppermute x3 -> x5, starting transfers between devices: 4.77 us -> 7.72 us  [exp_swap(): return lax.ppermute(x, 'exp', perm=[(0, 1), (1, 0)])]
    dot_general x5 -> x8, matrix products: 6.39 us -> 8.67 us  [the longest x1 1.77 us: moe_column_halves(): jnp.dot(arrived, gate_mine, preferred_element_type=jnp.float32)]
  transfers between devices with their start and end apart: 5 -> 7, of which waited for: 4 -> 6; matrix products, arithmetic and copies ran while one was open for 5% -> 5% of each run, Pallas kernels for 0% -> 0%
where the time goes in v3:
time: 168 us
  waiting for transfers between devices  61.3 us (36%)
  blocking collectives  60.6 us (36%)
  between operations  15 us (9%)
  matrix products  13.4 us (8%)
  starting transfers between devices  11.6 us (7%)
  other arithmetic  3.2 us (2%)
  local copies, waits for them, and re-layouts  2.98 us (2%)
    ppermute x5, waiting for transfers between devices, exp_swap(): return lax.ppermute(x, 'exp', perm=[(0, 1), (1, 0)])  41.3 us
    all_to_all x1, blocking collectives, moe_column_halves(): lax.all_to_all(send_rows.reshape(n_ctx, capacity, half_d), 'ctx', split_a...  25.1 us
    all_to_all x1, waiting for transfers between devices, moe_column_halves(): lax.all_to_all(summed.reshape(n_ctx, capacity, half_d), 'ctx', split_axis...  19.2 us
    all_gather x1, blocking collectives, local(): value_two = lax.all_gather(value_states, 'ctx', axis=1, tiled=True)[0]  17.9 us
    all_gather x1, blocking collectives, local(): key_two = lax.all_gather(key_states, 'ctx', axis=1, tiled=True)[0]  17.7 us
    ppermute x5, starting transfers between devices, exp_swap(): return lax.ppermute(x, 'exp', perm=[(0, 1), (1, 0)])  7.72 us
    all_to_all x1, starting transfers between devices, moe_column_halves(): lax.all_to_all(summed.reshape(n_ctx, capacity, half_d), 'ctx', split_axis...  3.81 us
  transfers between devices with their start and end apart: 7, of which 6 were waited for; matrix products, arithmetic and copies ran while one was open for 5% of the time, Pallas kernels for 0%

profile of v3, /device:TPU:0, one launch (start us, length us, event | category | flops | bytes accessed | tf_op | source)
XLA Modules:
  0.0 168.0 jit_solution(271821892838166667)
XLA Ops:
  7.2 0.7 all-gather.2.cloned.1.call-update
  7.9 0.8 copy.44
  9.6 17.7 %all_gather.9 = bf16[1,512,512]{2,1,0:T(8,128)(2,1)S(1)} all-gather(bf16[1,64,512]{2,1,0:T(8,128)(2,1)} %param.13), channel_id=1, replica_groups=mesh['req'=2,'ctx'=8,'exp'=2] {'ctx'}, dimensions={1}, use_global_device_ids=true | all-gather | bytes 589824 | tf_op jit(solution)/shard_map/all_gather | solution.py:187
  27.5 17.9 %all_gather.10 = bf16[1,512,512]{2,1,0:T(8,128)(2,1)S(1)} all-gather(bf16[1,64,512]{2,1,0:T(8,128)(2,1)S(1)} %copy-done.5), channel_id=1, replica_groups=mesh['req'=2,'ctx'=8,'exp'=2] {'ctx'}, dimensions={1}, use_global_device_ids=true | all-gather | bytes 589824 | tf_op jit(solution)/shard_map/all_gather | solution.py:188
  45.4 1.0 copy.41
  46.4 0.6 reduce-window.6
  48.9 2.4 %fusion.45 = f32[64,2048]{1,0:T(8,128)S(1)} fusion(bf16[2048,512]{1,0:T(8,128)(2,1)} %all-gather.2.cloned.1.call-done, bf16[4,8,8,128]{3,2,1,0:T(8,128)(2,1)S(1)} %fusion.3), kind=kOutput, calls=%fused_computation.66 | convolution fusion | flops 134217728 | bytes 2686976 | tf_op jit(solution)/shard_map/tc,oc->to/dot_general | solution.py:216
  51.3 1.6 collective-permute-start
  52.9 4.3 %collective-permute-done = bf16[32,2048]{1,0:T(8,128)(2,1)} collective-permute-done((bf16[32,2048]{1,0:T(8,128)(2,1)S(1)}, bf16[32,2048]{1,0:T(8,128)(2,1)}, u32[]{:S(2)}, u32[]{:S(2)}) %collective-permute-start) | collective-permute-done | bytes 131104 | tf_op jit(solution)/shard_map/ppermute | solution.py:48
  57.2 1.1 fusion.27
  58.4 1.6 collective-permute-start.1
  60.2 2.6 %collective-permute-done.1 = bf16[32,1024]{1,0:T(8,128)(2,1)S(1)} collective-permute-done((bf16[32,1024]{1,0:T(8,128)(2,1)S(1)}, bf16[32,1024]{1,0:T(8,128)(2,1)S(1)}, u32[]{:S(2)}, u32[]{:S(2)}) %collective-permute-start.1) | collective-permute-done | bytes 65568 | tf_op jit(solution)/shard_map/ppermute | solution.py:48
  62.8 0.4 convolution_convert_fusion
  63.2 25.1 %all_to_all.10 = bf16[8,48,1024]{2,1,0:T(8,128)(2,1)S(1)} all-to-all(bf16[8,48,1024]{2,1,0:T(8,128)(2,1)S(1)} %bitcast.87), channel_id=1, replica_groups=mesh['req'=2,'ctx'=8,'exp'=2] {'ctx'}, dimensions={0} | all-to-all | bytes 1572864 | tf_op jit(solution)/shard_map/all_to_all | solution.py:123
  88.2 1.5 collective-permute-start.2
  89.7 1.8 %fusion.15 = f32[384,352]{0,1:T(8,128)S(1)} fusion(bf16[384,1024]{1,0:T(8,128)(2,1)S(1)} %bitcast.84, bf16[1,2048,352]{1,2,0:T(8,128)(2,1)} %param.18, s32[]{:T(128)S(6)} %select_n.201), kind=kOutput, calls=%fused_computation.22 | convolution fusion | flops 276824064 | bytes 2048004 | tf_op jit(solution)/shard_map/dot_general | solution.py:133
  91.5 0.6 fusion.12
  92.1 15.2 %collective-permute-done.2 = bf16[384,1024]{1,0:T(8,128)(2,1)} collective-permute-done((bf16[384,1024]{1,0:T(8,128)(2,1)S(1)}, bf16[384,1024]{1,0:T(8,128)(2,1)}, u32[]{:S(2)}, u32[]{:S(2)}) %collective-permute-start.2) | collective-permute-done | bytes 786464 | tf_op jit(solution)/shard_map/ppermute | solution.py:48
  107.3 1.7 %convolution_add_fusion.1 = f32[384,352]{0,1:T(8,128)S(1)} fusion(f32[384,352]{0,1:T(8,128)S(1)} %fusion.15, bf16[384,1024]{1,0:T(8,128)(2,1)} %collective-permute-done.2, bf16[1,2048,352]{1,2,0:T(8,128)(2,1)S(1)} %copy-done.1, s32[]{:T(128)S(6)} %select_n.202), kind=kOutput, calls=%fused_computation.4 | convolution fusion | flops 276959232 | bytes 2588676 | tf_op jit(solution)/shard_map/dot_general | solution.py:133
  109.0 1.7 %multiply_convert_fusion = bf16[384,352]{0,1:T(8,128)(2,1)S(1)} fusion(f32[384,352]{0,1:T(8,128)S(1)} %convolution_add_fusion.1, f32[384,352]{0,1:T(8,128)S(1)} %fusion.12, bf16[384,1024]{1,0:T(8,128)(2,1)} %collective-permute-done.2, bf16[1,2048,352]{1,2,0:T(8,128)(2,1)S(1)} %copy-done.3, s32[]{:T(128)S(6)} %select_n.202), kind=kOutput, calls=%fused_computation.30 | convolution fusion | flops 277770240 | bytes 2859012 | tf_op jit(solution)/shard_map/dot_general | solution.py:136
  110.7 0.6 convolution_convert_fusion.1
  111.3 1.6 collective-permute-start.3
  112.8 16.5 %collective-permute-done.3 = bf16[384,1024]{1,0:T(8,128)(2,1)S(1)} collective-permute-done((bf16[384,1024]{1,0:T(8,128)(2,1)S(1)}, bf16[384,1024]{1,0:T(8,128)(2,1)S(1)}, u32[]{:S(2)}, u32[]{:S(2)}) %collective-permute-start.3) | collective-permute-done | bytes 786464 | tf_op jit(solution)/shard_map/ppermute | solution.py:48
  129.3 1.5 add_convert_fusion
  130.8 3.8 %all-to-all-start.1 = ((bf16[8,48,1024]{2,1,0:T(8,128)(2,1)}), bf16[8,48,1024]{2,1,0:T(8,128)(2,1)S(1)}, u32[]{:S(2)}, u32[]{:S(2)}) async-start(bf16[8,48,1024]{2,1,0:T(8,128)(2,1)} %bitcast.88), calls=%async_computation.1 | async-start | bytes 1572864 | tf_op jit(solution)/shard_map/all_to_all | solution.py:146
  134.6 0.9 fusion.4
  135.5 0.9 fusion.5
  136.4 19.2 %all-to-all-done.1 = bf16[8,48,1024]{2,1,0:T(8,128)(2,1)S(1)} async-done(((bf16[8,48,1024]{2,1,0:T(8,128)(2,1)}), bf16[8,48,1024]{2,1,0:T(8,128)(2,1)S(1)}, u32[]{:S(2)}, u32[]{:S(2)}) %all-to-all-start.1) | async-done | bytes 786464 | tf_op jit(solution)/shard_map/all_to_all | solution.py:146
  155.6 0.5 fusion.85
  156.1 1.6 collective-permute-start.4
  157.7 2.8 %collective-permute-done.4 = bf16[32,1024]{1,0:T(8,128)(2,1)S(1)} collective-permute-done((bf16[32,1024]{1,0:T(8,128)(2,1)S(1)}, bf16[32,1024]{1,0:T(8,128)(2,1)S(1)}, u32[]{:S(2)}, u32[]{:S(2)}) %collective-permute-start.4) | collective-permute-done | bytes 65568 | tf_op jit(solution)/shard_map/ppermute | solution.py:48
  160.5 0.7 fusion.38
  (49 shorter events, 2.8 us)
Async XLA Ops:
  7.2 103.5 %copy-start = (bf16[1,352,2048]{2,1,0:T(8,128)(2,1)S(1)}, bf16[1,352,2048]{2,1,0:T(8,128)(2,1)}, u32[]{:S(2)}) copy-start(bf16[1,352,2048]{2,1,0:T(8,128)(2,1)} %param.20) | copy-start | bytes 4325380
  7.2 20.3 %copy-start.6 = (bf16[1,64,512]{2,1,0:T(8,128)(2,1)S(1)}, bf16[1,64,512]{2,1,0:T(8,128)(2,1)}, u32[]{:S(2)}) copy-start(bf16[1,64,512]{2,1,0:T(8,128)(2,1)} %param.12) | copy-start | bytes 196612
  7.2 20.3 %copy-start.5 = (bf16[1,64,512]{2,1,0:T(8,128)(2,1)S(1)}, bf16[1,64,512]{2,1,0:T(8,128)(2,1)}, u32[]{:S(2)}) copy-start(bf16[1,64,512]{2,1,0:T(8,128)(2,1)} %param.14) | copy-start | bytes 196612
  7.2 41.7 %all-gather.2.cloned.1.call-start = ((), (), s32[]{:S(2)}) async-start(), calls=%async_computation.2 | async-start | bytes 2359296 | tf_op jit(solution)/shard_map/all_gather | solution.py:219
  47.4 1.0 copy-start.2
  48.8 8.4 %copy-start.4 = (bf16[1,32,2048]{2,1,0:T(8,128)(2,1)S(1)}, bf16[1,32,2048]{2,1,0:T(8,128)(2,1)}, u32[]{:S(2)}) copy-start(bf16[1,32,2048]{2,1,0:T(8,128)(2,1)} %param.15) | copy-start | bytes 393220
  48.8 9.5 %copy-start.7 = (f32[2048]{0:T(1024)S(1)}, f32[2048]{0:T(1024)}, u32[]{:S(2)}) copy-start(f32[2048]{0:T(1024)} %param.17) | copy-start | bytes 24580
  51.2 8.8 %copy-start.8 = (f32[1,64,4]{1,2,0:T(4,128)S(1)}, f32[1,64,4]{1,2,0:T(4,128)}, u32[]{:S(2)}) copy-start(f32[1,64,4]{1,2,0:T(4,128)} %param.22) | copy-start | bytes 3076
  51.3 5.9 %collective-permute-start = (bf16[32,2048]{1,0:T(8,128)(2,1)S(1)}, bf16[32,2048]{1,0:T(8,128)(2,1)}, u32[]{:S(2)}, u32[]{:S(2)}) collective-permute-start(bf16[32,2048]{1,0:T(8,128)(2,1)S(1)} %select_convert_fusion), channel_id=1, source_target_pairs={{0,1},{1,0},{2,3},{3,2},{4,5},{5,4},{6,7},{7,6},{8,9},{9,8},{10,11... | collective-permute-start | bytes 393224 | tf_op jit(solution)/shard_map/ppermute | solution.py:48
  58.4 4.3 %collective-permute-start.1 = (bf16[32,1024]{1,0:T(8,128)(2,1)S(1)}, bf16[32,1024]{1,0:T(8,128)(2,1)S(1)}, u32[]{:S(2)}, u32[]{:S(2)}) collective-permute-start(bf16[32,1024]{1,0:T(8,128)(2,1)S(1)} %get-tuple-element.8), channel_id=1, source_target_pairs={{0,1},{1,0},{2,3},{3,2},{4,5},{5,4},{6,7},{7,6},{8,9},{9,8},{10,11... | collective-permute-start | bytes 196616 | tf_op jit(solution)/shard_map/ppermute | solution.py:48
  88.2 19.0 %collective-permute-start.2 = (bf16[384,1024]{1,0:T(8,128)(2,1)S(1)}, bf16[384,1024]{1,0:T(8,128)(2,1)}, u32[]{:S(2)}, u32[]{:S(2)}) collective-permute-start(bf16[384,1024]{1,0:T(8,128)(2,1)S(1)} %bitcast.83), channel_id=1, source_target_pairs={{0,1},{1,0},{2,3},{3,2},{4,5},{5,4},{6,7},{7,6},{8,9},{9,8},{10,11... | collective-permute-start | bytes 2359304 | tf_op jit(solution)/shard_map/ppermute | solution.py:48
  89.7 1.8 %copy-start.3 = (bf16[1,2048,352]{1,2,0:T(8,128)(2,1)S(1)}, bf16[1,2048,352]{1,2,0:T(8,128)(2,1)}, u32[]{:S(2)}) copy-start(bf16[1,2048,352]{1,2,0:T(8,128)(2,1)} %param.19) | copy-start | bytes 4325380
  91.5 15.7 %copy-start.1 = (bf16[1,2048,352]{1,2,0:T(8,128)(2,1)S(1)}, bf16[1,2048,352]{1,2,0:T(8,128)(2,1)}, u32[]{:S(2)}) copy-start(bf16[1,2048,352]{1,2,0:T(8,128)(2,1)} %param.18) | copy-start | bytes 4325380
  111.3 18.1 %collective-permute-start.3 = (bf16[384,1024]{1,0:T(8,128)(2,1)S(1)}, bf16[384,1024]{1,0:T(8,128)(2,1)S(1)}, u32[]{:S(2)}, u32[]{:S(2)}) collective-permute-start(bf16[384,1024]{1,0:T(8,128)(2,1)S(1)} %convolution_convert_fusion.1), channel_id=1, source_target_pairs={{0,1},{1,0},{2,3},{3,2},{4,5},{5,4},{6,7},{7,6},{8,9},{9,8},{10,11... | collective-permute-start | bytes 2359304 | tf_op jit(solution)/shard_map/ppermute | solution.py:48
  130.8 24.8 %all-to-all-start.1 = ((bf16[8,48,1024]{2,1,0:T(8,128)(2,1)}), bf16[8,48,1024]{2,1,0:T(8,128)(2,1)S(1)}, u32[]{:S(2)}, u32[]{:S(2)}) async-start(bf16[8,48,1024]{2,1,0:T(8,128)(2,1)} %bitcast.88), calls=%async_computation.1 | async-start | bytes 1572864 | tf_op jit(solution)/shard_map/all_to_all | solution.py:146
  156.1 4.3 %collective-permute-start.4 = (bf16[32,1024]{1,0:T(8,128)(2,1)S(1)}, bf16[32,1024]{1,0:T(8,128)(2,1)S(1)}, u32[]{:S(2)}, u32[]{:S(2)}) collective-permute-start(bf16[32,1024]{1,0:T(8,128)(2,1)S(1)} %select_convert_fusion.1), channel_id=1, source_target_pairs={{0,1},{1,0},{2,3},{3,2},{4,5},{5,4},{6,7},{7,6},{8,9},{9,8},{10,11... | collective-permute-start | bytes 196616 | tf_op jit(solution)/shard_map/ppermute | solution.py:48
Sparse Core Ops, SparseCore 0:
  9.6 37.3 all-gather.1

commit v4 on v3

--- a/solution.py
+++ b/solution.py
@@ -120,38 +120,47 @@
     send_rows = jnp.dot(
         dispatch.astype(jnp.bfloat16), tokens_cols, preferred_element_type=jnp.float32
     ).astype(jnp.bfloat16)
-    arrived = lax.all_to_all(
-        send_rows.reshape(n_ctx, capacity, half_d), "ctx", split_axis=0, concat_axis=0, tiled=True
-    ).reshape(n_ctx * capacity, half_d)
-    partner_cols = exp_swap(arrived)
+    send_rows = send_rows.reshape(n_ctx, capacity, half_d)
     my_start = my_exp * half_d
     other_start = (1 - my_exp) * half_d
     gate_mine = lax.dynamic_slice_in_dim(gate_matrix, my_start, half_d, axis=0)
     gate_other = lax.dynamic_slice_in_dim(gate_matrix, other_start, half_d, axis=0)
     up_mine = lax.dynamic_slice_in_dim(up_matrix, my_start, half_d, axis=0)
     up_other = lax.dynamic_slice_in_dim(up_matrix, other_start, half_d, axis=0)
-    gate_act = jnp.dot(arrived, gate_mine, preferred_element_type=jnp.float32) + jnp.dot(
-        partner_cols, gate_other, preferred_element_type=jnp.float32
-    )
-    up_act = jnp.dot(arrived, up_mine, preferred_element_type=jnp.float32) + jnp.dot(
-        partner_cols, up_other, preferred_element_type=jnp.float32
-    )
-    hidden = (jax.nn.silu(gate_act) * up_act).astype(jnp.bfloat16)
     down_other = lax.dynamic_slice_in_dim(down_matrix, other_start, half_d, axis=1)
     down_mine = lax.dynamic_slice_in_dim(down_matrix, my_start, half_d, axis=1)
-    out_other = jnp.dot(hidden, down_other, preferred_element_type=jnp.float32)
-    got_other = exp_swap(out_other.astype(jnp.bfloat16))
-    out_mine = jnp.dot(hidden, down_mine, preferred_element_type=jnp.float32)
-    summed = (out_mine + got_other.astype(jnp.float32)).astype(jnp.bfloat16)
-    served = lax.all_to_all(
-        summed.reshape(n_ctx, capacity, half_d), "ctx", split_axis=0, concat_axis=0, tiled=True
-    ).reshape(n_ctx * capacity, half_d)
-    moe_half = jnp.dot(
-        combine,
-        served.astype(jnp.float32),
-        precision=lax.Precision.HIGHEST,
-        preferred_element_type=jnp.float32,
-    )
+    n_chunks = 2 if capacity % 2 == 0 else 1
+    chunk = capacity // n_chunks
+    combine_slots = combine.reshape(combine.shape[0], n_ctx, capacity)
+    moe_half = None
+    for k in range(n_chunks):
+        part = send_rows[:, k * chunk : (k + 1) * chunk]
+        arrived = lax.all_to_all(part, "ctx", split_axis=0, concat_axis=0, tiled=True).reshape(
+            n_ctx * chunk, half_d
+        )
+        partner_cols = exp_swap(arrived)
+        gate_act = jnp.dot(arrived, gate_mine, preferred_element_type=jnp.float32) + jnp.dot(
+            partner_cols, gate_other, preferred_element_type=jnp.float32
+        )
+        up_act = jnp.dot(arrived, up_mine, preferred_element_type=jnp.float32) + jnp.dot(
+            partner_cols, up_other, preferred_element_type=jnp.float32
+        )
+        hidden = (jax.nn.silu(gate_act) * up_act).astype(jnp.bfloat16)
+        out_other = jnp.dot(hidden, down_other, preferred_element_type=jnp.float32)
+        got_other = exp_swap(out_other.astype(jnp.bfloat16))
+        out_mine = jnp.dot(hidden, down_mine, preferred_element_type=jnp.float32)
+        summed = (out_mine + got_other.astype(jnp.float32)).astype(jnp.bfloat16)
+        served = lax.all_to_all(
+            summed.reshape(n_ctx, chunk, half_d), "ctx", split_axis=0, concat_axis=0, tiled=True
+        ).reshape(n_ctx * chunk, half_d)
+        weights_k = combine_slots[:, :, k * chunk : (k + 1) * chunk].reshape(-1, n_ctx * chunk)
+        term = jnp.dot(
+            weights_k,
+            served.astype(jnp.float32),
+            precision=lax.Precision.HIGHEST,
+            preferred_element_type=jnp.float32,
+        )
+        moe_half = term if moe_half is None else moe_half + term
     my_tok, other_tok = halves(moe_half, first, 0)
     got_tok = exp_swap(other_tok.astype(jnp.bfloat16)).astype(jnp.float32)
     return join(my_tok, got_tok, first, 1)

time: 168 us -> 167 us (level)
  waiting for transfers between devices: 61.3 us -> 49.3 us
  starting transfers between devices: 11.6 us -> 23.1 us
  blocking collectives: 60.6 us -> 52.3 us
  matrix products: 13.4 us -> 19.2 us
    ppermute x5 -> x7, waiting for transfers between devices: 41.3 us -> 28.9 us  [exp_swap(): return lax.ppermute(x, 'exp', perm=[(0, 1), (1, 0)])]
    all_to_all x1 -> x3, starting transfers between devices: 3.81 us -> 12.3 us  [the longest x2 8.19 us: moe_column_halves(): lax.all_to_all(summed.reshape(n_ctx, chunk, half_d), 'ctx', split_axis=0,...]
    all_to_all x1, blocking collectives: 25.1 us -> 16.8 us  [moe_column_halves(): lax.all_to_all(part, 'ctx', split_axis=0, concat_axis=0, tiled=True)]
    ppermute x5 -> x7, starting transfers between devices: 7.72 us -> 10.8 us  [exp_swap(): return lax.ppermute(x, 'exp', perm=[(0, 1), (1, 0)])]
    dot_general x1 -> x2, matrix products: 0.5 us -> 2.54 us  [moe_column_halves(): jnp.dot(weights_k, served.astype(jnp.float32), precision=lax.Precision.HI...]
    all_to_all x1 -> x3, waiting for transfers between devices: 19.2 us -> 19.7 us  [the longest x1 11 us: moe_column_halves(): lax.all_to_all(part, 'ctx', split_axis=0, concat_axis=0, tiled=True)]
  transfers between devices with their start and end apart: 7 -> 11, of which waited for: 6 -> 8; matrix products, arithmetic and copies ran while one was open for 5% -> 12% of each run, Pallas kernels for 0% -> 0%
where the time goes in v4:
time: 167 us
  blocking collectives  52.3 us (31%)
  waiting for transfers between devices  49.3 us (30%)
  starting transfers between devices  23.1 us (14%)
  matrix products  19.2 us (11%)
  between operations  15.1 us (9%)
  local copies, waits for them, and re-layouts  4.63 us (3%)
  other arithmetic  2.93 us (2%)
    ppermute x7, waiting for transfers between devices, exp_swap(): return lax.ppermute(x, 'exp', perm=[(0, 1), (1, 0)])  28.9 us
    all_gather x1, blocking collectives, local(): value_two = lax.all_gather(value_states, 'ctx', axis=1, tiled=True)[0]  17.9 us
    all_gather x1, blocking collectives, local(): key_two = lax.all_gather(key_states, 'ctx', axis=1, tiled=True)[0]  17.7 us
    all_to_all x1, blocking collectives, moe_column_halves(): lax.all_to_all(part, 'ctx', split_axis=0, concat_axis=0, tiled=True)  16.8 us
    all_to_all x1, waiting for transfers between devices, moe_column_halves(): lax.all_to_all(part, 'ctx', split_axis=0, concat_axis=0, tiled=True)  11 us
    ppermute x7, starting transfers between devices, exp_swap(): return lax.ppermute(x, 'exp', perm=[(0, 1), (1, 0)])  10.8 us
    all_to_all x2, waiting for transfers between devices, moe_column_halves(): lax.all_to_all(summed.reshape(n_ctx, chunk, half_d), 'ctx', split_axis=0,...  8.71 us
    all_to_all x2, starting transfers between devices, moe_column_halves(): lax.all_to_all(summed.reshape(n_ctx, chunk, half_d), 'ctx', split_axis=0,...  8.19 us
  transfers between devices with their start and end apart: 11, of which 8 were waited for; matrix products, arithmetic and copies ran while one was open for 12% of the time, Pallas kernels for 0%

profile of v4, /device:TPU:0, one launch (start us, length us, event | category | flops | bytes accessed | tf_op | source)
XLA Modules:
  0.0 166.5 jit_solution(17132931957670180003)
XLA Ops:
  9.6 17.7 %all_gather.9 = bf16[1,512,512]{2,1,0:T(8,128)(2,1)S(1)} all-gather(bf16[1,64,512]{2,1,0:T(8,128)(2,1)} %param.13), channel_id=1, replica_groups=mesh['req'=2,'ctx'=8,'exp'=2] {'ctx'}, dimensions={1}, use_global_device_ids=true | all-gather | bytes 589824 | tf_op jit(solution)/shard_map/all_gather | solution.py:196
  27.5 17.9 %all_gather.10 = bf16[1,512,512]{2,1,0:T(8,128)(2,1)S(1)} all-gather(bf16[1,64,512]{2,1,0:T(8,128)(2,1)S(1)} %copy-done.9), channel_id=1, replica_groups=mesh['req'=2,'ctx'=8,'exp'=2] {'ctx'}, dimensions={1}, use_global_device_ids=true | all-gather | bytes 589824 | tf_op jit(solution)/shard_map/all_gather | solution.py:197
  45.4 1.0 copy.41
  48.9 2.4 %fusion.69 = f32[64,2048]{1,0:T(8,128)S(1)} fusion(bf16[2048,512]{1,0:T(8,128)(2,1)} %all-gather.2.cloned.1.call-done, bf16[4,8,8,128]{3,2,1,0:T(8,128)(2,1)S(1)} %fusion.8), kind=kOutput, calls=%fused_computation.93 | convolution fusion | flops 134217728 | bytes 2686976 | tf_op jit(solution)/shard_map/tc,oc->to/dot_general | solution.py:225
  51.3 1.6 collective-permute-start
  52.9 4.2 %collective-permute-done = bf16[32,2048]{1,0:T(8,128)(2,1)S(1)} collective-permute-done((bf16[32,2048]{1,0:T(8,128)(2,1)S(1)}, bf16[32,2048]{1,0:T(8,128)(2,1)S(1)}, u32[]{:S(2)}, u32[]{:S(2)}) %collective-permute-start) | collective-permute-done | bytes 131104 | tf_op jit(solution)/shard_map/ppermute | solution.py:48
  57.4 1.6 collective-permute-start.1
  59.8 2.0 %collective-permute-done.1 = bf16[32,1024]{1,0:T(8,128)(2,1)S(1)} collective-permute-done((bf16[32,1024]{1,0:T(8,128)(2,1)S(1)}, bf16[32,1024]{1,0:T(8,128)(2,1)S(1)}, u32[]{:S(2)}, u32[]{:S(2)}) %collective-permute-start.1) | collective-permute-done | bytes 65568 | tf_op jit(solution)/shard_map/ppermute | solution.py:48
  63.0 16.8 %all_to_all.20 = bf16[8,24,1024]{2,1,0:T(8,128)(2,1)} all-to-all(bf16[8,24,1024]{2,1,0:T(8,128)(2,1)S(1)} %get-tuple-element.7), channel_id=1, replica_groups=mesh['req'=2,'ctx'=8,'exp'=2] {'ctx'}, dimensions={0} | all-to-all | bytes 786432 | tf_op jit(solution)/shard_map/all_to_all | solution.py:138
  79.7 4.1 %all-to-all-start = ((bf16[8,24,1024]{2,1,0:T(8,128)(2,1)}), bf16[8,24,1024]{2,1,0:T(8,128)(2,1)}, u32[]{:S(2)}, u32[]{:S(2)}) async-start(bf16[8,24,1024]{2,1,0:T(8,128)(2,1)} %get-tuple-element.8), calls=%async_computation | async-start | bytes 786432 | tf_op jit(solution)/shard_map/all_to_all | solution.py:138
  83.8 1.6 collective-permute-start.4
  85.4 11.0 %all-to-all-done = bf16[8,24,1024]{2,1,0:T(8,128)(2,1)} async-done(((bf16[8,24,1024]{2,1,0:T(8,128)(2,1)}), bf16[8,24,1024]{2,1,0:T(8,128)(2,1)}, u32[]{:S(2)}, u32[]{:S(2)}) %all-to-all-start) | async-done | bytes 393248 | tf_op jit(solution)/shard_map/all_to_all | solution.py:138
  96.4 1.5 collective-permute-start.2
  97.9 1.4 fusion.29
  99.3 1.4 fusion.31
  101.2 1.4 fusion.25
  102.6 4.6 %collective-permute-done.2 = bf16[192,1024]{1,0:T(8,128)(2,1)S(1)} collective-permute-done((bf16[192,1024]{1,0:T(8,128)(2,1)}, bf16[192,1024]{1,0:T(8,128)(2,1)S(1)}, u32[]{:S(2)}, u32[]{:S(2)}) %collective-permute-start.2) | collective-permute-done | bytes 393248 | tf_op jit(solution)/shard_map/ppermute | solution.py:48
  108.5 1.6 collective-permute-start.3
  110.1 1.4 convolution_add_fusion.1
  111.5 1.4 fusion.5
  113.0 5.4 %collective-permute-done.3 = bf16[192,1024]{1,0:T(8,128)(2,1)S(1)} collective-permute-done((bf16[192,1024]{1,0:T(8,128)(2,1)S(1)}, bf16[192,1024]{1,0:T(8,128)(2,1)S(1)}, u32[]{:S(2)}, u32[]{:S(2)}) %collective-permute-start.3) | collective-permute-done | bytes 393248 | tf_op jit(solution)/shard_map/ppermute | solution.py:48
  118.4 1.1 add_convert_fusion.1
  119.5 3.5 %all-to-all-start.1 = ((bf16[8,24,1024]{2,1,0:T(8,128)(2,1)}), bf16[8,24,1024]{2,1,0:T(8,128)(2,1)S(1)}, u32[]{:S(2)}, u32[]{:S(2)}) async-start(bf16[8,24,1024]{2,1,0:T(8,128)(2,1)} %bitcast.20), calls=%async_computation.1 | async-start | bytes 786432 | tf_op jit(solution)/shard_map/all_to_all | solution.py:153
  123.4 1.6 collective-permute-start.5
  124.9 10.0 %collective-permute-done.5 = bf16[192,1024]{1,0:T(8,128)(2,1)S(1)} collective-permute-done((bf16[192,1024]{1,0:T(8,128)(2,1)S(1)}, bf16[192,1024]{1,0:T(8,128)(2,1)S(1)}, u32[]{:S(2)}, u32[]{:S(2)}) %collective-permute-start.5) | collective-permute-done | bytes 393248 | tf_op jit(solution)/shard_map/ppermute | solution.py:48
  134.9 1.1 add_convert_fusion
  136.1 4.7 %all-to-all-start.3 = ((bf16[8,24,1024]{2,1,0:T(8,128)(2,1)}), bf16[8,24,1024]{2,1,0:T(8,128)(2,1)S(1)}, u32[]{:S(2)}, u32[]{:S(2)}) async-start(bf16[8,24,1024]{2,1,0:T(8,128)(2,1)} %bitcast.23), calls=%async_computation.3 | async-start | bytes 786432 | tf_op jit(solution)/shard_map/all_to_all | solution.py:153
  143.4 1.3 convolution_bitcast_fusion.1
  144.7 8.7 %all-to-all-done.3 = bf16[8,24,1024]{2,1,0:T(8,128)(2,1)S(1)} async-done(((bf16[8,24,1024]{2,1,0:T(8,128)(2,1)}), bf16[8,24,1024]{2,1,0:T(8,128)(2,1)S(1)}, u32[]{:S(2)}, u32[]{:S(2)}) %all-to-all-start.3) | async-done | bytes 393248 | tf_op jit(solution)/shard_map/all_to_all | solution.py:153
  153.4 1.3 fusion.3
  154.7 1.6 collective-permute-start.6
  156.2 2.8 %collective-permute-done.6 = bf16[32,1024]{1,0:T(8,128)(2,1)S(1)} collective-permute-done((bf16[32,1024]{1,0:T(8,128)(2,1)S(1)}, bf16[32,1024]{1,0:T(8,128)(2,1)S(1)}, u32[]{:S(2)}, u32[]{:S(2)}) %collective-permute-start.6) | collective-permute-done | bytes 65568 | tf_op jit(solution)/shard_map/ppermute | solution.py:48
  (74 shorter events, 12.2 us)
Async XLA Ops:
  7.2 101.0 %copy-start = (bf16[1,352,2048]{2,1,0:T(8,128)(2,1)S(1)}, bf16[1,352,2048]{2,1,0:T(8,128)(2,1)}, u32[]{:S(2)}) copy-start(bf16[1,352,2048]{2,1,0:T(8,128)(2,1)} %param.20) | copy-start | bytes 4325380
  7.2 20.3 %copy-start.10 = (bf16[1,64,512]{2,1,0:T(8,128)(2,1)S(1)}, bf16[1,64,512]{2,1,0:T(8,128)(2,1)}, u32[]{:S(2)}) copy-start(bf16[1,64,512]{2,1,0:T(8,128)(2,1)} %param.12) | copy-start | bytes 196612
  7.2 20.3 %copy-start.9 = (bf16[1,64,512]{2,1,0:T(8,128)(2,1)S(1)}, bf16[1,64,512]{2,1,0:T(8,128)(2,1)}, u32[]{:S(2)}) copy-start(bf16[1,64,512]{2,1,0:T(8,128)(2,1)} %param.14) | copy-start | bytes 196612
  7.2 41.7 %all-gather.2.cloned.1.call-start = ((), (), s32[]{:S(2)}) async-start(), calls=%async_computation.4 | async-start | bytes 2359296 | tf_op jit(solution)/shard_map/all_gather | solution.py:228
  45.4 2.8 %copy-start.2 = (bf16[1,512,512]{2,1,0:T(8,128)(2,1)}, bf16[1,512,512]{2,1,0:T(8,128)(2,1)S(1)}, u32[]{:S(2)}) copy-start(bf16[1,512,512]{2,1,0:T(8,128)(2,1)S(1)} %all_gather.10) | copy-start | bytes 1572868
  47.4 1.0 copy-start.6
  48.8 8.3 %copy-start.8 = (bf16[1,32,2048]{2,1,0:T(8,128)(2,1)S(1)}, bf16[1,32,2048]{2,1,0:T(8,128)(2,1)}, u32[]{:S(2)}) copy-start(bf16[1,32,2048]{2,1,0:T(8,128)(2,1)} %param.15) | copy-start | bytes 393220
  48.8 8.5 %copy-start.11 = (f32[2048]{0:T(1024)S(1)}, f32[2048]{0:T(1024)}, u32[]{:S(2)}) copy-start(f32[2048]{0:T(1024)} %param.17) | copy-start | bytes 24580
  51.3 7.7 %copy-start.12 = (f32[1,64,4]{1,2,0:T(4,128)S(1)}, f32[1,64,4]{1,2,0:T(4,128)}, u32[]{:S(2)}) copy-start(f32[1,64,4]{1,2,0:T(4,128)} %param.22) | copy-start | bytes 3076
  51.3 5.8 %collective-permute-start = (bf16[32,2048]{1,0:T(8,128)(2,1)S(1)}, bf16[32,2048]{1,0:T(8,128)(2,1)S(1)}, u32[]{:S(2)}, u32[]{:S(2)}) collective-permute-start(bf16[32,2048]{1,0:T(8,128)(2,1)S(1)} %select_convert_fusion), channel_id=1, source_target_pairs={{0,1},{1,0},{2,3},{3,2},{4,5},{5,4},{6,7},{7,6},{8,9},{9,8},{10,11... | collective-permute-start | bytes 393224 | tf_op jit(solution)/shard_map/ppermute | solution.py:48
  57.4 4.3 %collective-permute-start.1 = (bf16[32,1024]{1,0:T(8,128)(2,1)S(1)}, bf16[32,1024]{1,0:T(8,128)(2,1)S(1)}, u32[]{:S(2)}, u32[]{:S(2)}) collective-permute-start(bf16[32,1024]{1,0:T(8,128)(2,1)S(1)} %get-tuple-element.10), channel_id=1, source_target_pairs={{0,1},{1,0},{2,3},{3,2},{4,5},{5,4},{6,7},{7,6},{8,9},{9,8},{10,11... | collective-permute-start | bytes 196616 | tf_op jit(solution)/shard_map/ppermute | solution.py:48
  62.2 35.7 %copy-start.1 = (bf16[1,2048,352]{1,2,0:T(8,128)(2,1)S(1)}, bf16[1,2048,352]{1,2,0:T(8,128)(2,1)}, u32[]{:S(2)}) copy-start(bf16[1,2048,352]{1,2,0:T(8,128)(2,1)} %param.18) | copy-start | bytes 4325380
  79.7 16.6 %all-to-all-start = ((bf16[8,24,1024]{2,1,0:T(8,128)(2,1)}), bf16[8,24,1024]{2,1,0:T(8,128)(2,1)}, u32[]{:S(2)}, u32[]{:S(2)}) async-start(bf16[8,24,1024]{2,1,0:T(8,128)(2,1)} %get-tuple-element.8), calls=%async_computation | async-start | bytes 786432 | tf_op jit(solution)/shard_map/all_to_all | solution.py:138
  83.8 26.3 %collective-permute-start.4 = (bf16[192,1024]{1,0:T(8,128)(2,1)}, bf16[192,1024]{1,0:T(8,128)(2,1)}, u32[]{:S(2)}, u32[]{:S(2)}) collective-permute-start(bf16[192,1024]{1,0:T(8,128)(2,1)} %bitcast.110), channel_id=1, source_target_pairs={{0,1},{1,0},{2,3},{3,2},{4,5},{5,4},{6,7},{7,6},{8,9},{9,8},{10,11... | collective-permute-start | bytes 1179656 | tf_op jit(solution)/shard_map/ppermute | solution.py:48
  96.4 4.4 %copy-start.4 = (bf16[8,24,1024]{2,1,0:T(8,128)(2,1)S(1)}, bf16[8,24,1024]{2,1,0:T(8,128)(2,1)}, u32[]{:S(2)}) copy-start(bf16[8,24,1024]{2,1,0:T(8,128)(2,1)} %all_to_all.20) | copy-start | bytes 1179652
  96.4 4.4 %copy-start.5 = (bf16[1,2048,352]{1,2,0:T(8,128)(2,1)S(1)}, bf16[1,2048,352]{1,2,0:T(8,128)(2,1)}, u32[]{:S(2)}) copy-start(bf16[1,2048,352]{1,2,0:T(8,128)(2,1)} %param.19) | copy-start | bytes 4325380
  96.4 10.9 %collective-permute-start.2 = (bf16[192,1024]{1,0:T(8,128)(2,1)}, bf16[192,1024]{1,0:T(8,128)(2,1)S(1)}, u32[]{:S(2)}, u32[]{:S(2)}) collective-permute-start(bf16[192,1024]{1,0:T(8,128)(2,1)} %bitcast.13), channel_id=1, source_target_pairs={{0,1},{1,0},{2,3},{3,2},{4,5},{5,4},{6,7},{7,6},{8,9},{9,8},{10,11... | collective-permute-start | bytes 1179656 | tf_op jit(solution)/shard_map/ppermute | solution.py:48
  108.5 9.8 %collective-permute-start.3 = (bf16[192,1024]{1,0:T(8,128)(2,1)S(1)}, bf16[192,1024]{1,0:T(8,128)(2,1)S(1)}, u32[]{:S(2)}, u32[]{:S(2)}) collective-permute-start(bf16[192,1024]{1,0:T(8,128)(2,1)S(1)} %convolution_convert_fusion.2), channel_id=1, source_target_pairs={{0,1},{1,0},{2,3},{3,2},{4,5},{5,4},{6,7},{7,6},{8,9},{9,8},{10,11... | collective-permute-start | bytes 1179656 | tf_op jit(solution)/shard_map/ppermute | solution.py:48
  119.5 16.6 %all-to-all-start.1 = ((bf16[8,24,1024]{2,1,0:T(8,128)(2,1)}), bf16[8,24,1024]{2,1,0:T(8,128)(2,1)S(1)}, u32[]{:S(2)}, u32[]{:S(2)}) async-start(bf16[8,24,1024]{2,1,0:T(8,128)(2,1)} %bitcast.20), calls=%async_computation.1 | async-start | bytes 786432 | tf_op jit(solution)/shard_map/all_to_all | solution.py:153
  123.4 17.4 %copy-start.7 = (f32[384,64]{0,1:T(8,128)S(1)}, f32[384,64]{0,1:T(8,128)}, u32[]{:S(2)}) copy-start(f32[384,64]{0,1:T(8,128)} %get-tuple-element.3) | copy-start | bytes 294916
  123.4 18.3 %copy-start.3 = (bf16[1,512,512]{2,1,0:T(8,128)(2,1)S(1)}, bf16[1,512,512]{2,1,0:T(8,128)(2,1)}, u32[]{:S(2)}) copy-start(bf16[1,512,512]{2,1,0:T(8,128)(2,1)} %copy-done.2) | copy-start | bytes 1572868
  123.4 11.6 %collective-permute-start.5 = (bf16[192,1024]{1,0:T(8,128)(2,1)S(1)}, bf16[192,1024]{1,0:T(8,128)(2,1)S(1)}, u32[]{:S(2)}, u32[]{:S(2)}) collective-permute-start(bf16[192,1024]{1,0:T(8,128)(2,1)S(1)} %convolution_convert_fusion.1), channel_id=1, source_target_pairs={{0,1},{1,0},{2,3},{3,2},{4,5},{5,4},{6,7},{7,6},{8,9},{9,8},{10,11... | collective-permute-start | bytes 1179656 | tf_op jit(solution)/shard_map/ppermute | solution.py:48
  136.1 17.3 %all-to-all-start.3 = ((bf16[8,24,1024]{2,1,0:T(8,128)(2,1)}), bf16[8,24,1024]{2,1,0:T(8,128)(2,1)S(1)}, u32[]{:S(2)}, u32[]{:S(2)}) async-start(bf16[8,24,1024]{2,1,0:T(8,128)(2,1)} %bitcast.23), calls=%async_computation.3 | async-start | bytes 786432 | tf_op jit(solution)/shard_map/all_to_all | solution.py:153
  154.7 4.3 %collective-permute-start.6 = (bf16[32,1024]{1,0:T(8,128)(2,1)S(1)}, bf16[32,1024]{1,0:T(8,128)(2,1)S(1)}, u32[]{:S(2)}, u32[]{:S(2)}) collective-permute-start(bf16[32,1024]{1,0:T(8,128)(2,1)S(1)} %select_convert_fusion.1), channel_id=1, source_target_pairs={{0,1},{1,0},{2,3},{3,2},{4,5},{5,4},{6,7},{7,6},{8,9},{9,8},{10,11... | collective-permute-start | bytes 196616 | tf_op jit(solution)/shard_map/ppermute | solution.py:48
Sparse Core Ops, SparseCore 0:
  9.6 37.3 all-gather.1

commit v5 on v4

--- a/solution.py
+++ b/solution.py
@@ -164,6 +164,22 @@
     my_tok, other_tok = halves(moe_half, first, 0)
     got_tok = exp_swap(other_tok.astype(jnp.bfloat16)).astype(jnp.float32)
     return join(my_tok, got_tok, first, 1)
+
+
+def ctx_gather_blocks(rows, n_ctx, my_ctx):
+    n_chip = n_ctx // 2
+    my_chip = my_ctx // 2
+    my_core = my_ctx % 2
+    stack = [rows]
+    for shift in range(1, n_chip):
+        perm = [(i, ((i // 2 + shift) % n_chip) * 2 + i % 2) for i in range(n_ctx)]
+        stack.append(lax.ppermute(rows, "ctx", perm=perm))
+    own = jnp.stack(stack)
+    partner = lax.ppermute(own, "ctx", perm=[(i, i ^ 1) for i in range(n_ctx)])
+    shifts = jnp.arange(n_chip, dtype=jnp.int32)
+    chips = (my_chip - shifts) % n_chip
+    src_ctx = jnp.concatenate([chips * 2 + my_core, chips * 2 + (1 - my_core)])
+    return jnp.concatenate([own, partner]), src_ctx
 
 
 def local(
@@ -193,10 +209,14 @@
     decode_pos = my_ctx * tok_here + local_ids
     query_three = query_states[0].reshape(tok_here, heads_dev, HD)
     run_max = jnp.full((heads_dev, tok_here), NEG, jnp.float32)
-    key_two = lax.all_gather(key_states, "ctx", axis=1, tiled=True)[0]
-    value_two = lax.all_gather(value_states, "ctx", axis=1, tiled=True)[0]
+    kv_here = jnp.concatenate([key_states[0], value_states[0]], axis=1)
+    kv_blocks, src_ctx = ctx_gather_blocks(kv_here, n_ctx, my_ctx)
+    kv_all = kv_blocks.reshape(n_ctx * tok_here, 2 * feat_width)
+    key_two = kv_all[:, :feat_width]
+    value_two = kv_all[:, feat_width:]
     row_count = key_two.shape[0]
-    key_pos = row_positions(jnp.arange(row_count, dtype=jnp.int32), half_block, n_ctx)
+    row_ids = (src_ctx[:, None] * tok_here + local_ids[None, :]).reshape(row_count)
+    key_pos = row_positions(row_ids, half_block, n_ctx)
     pick_rows = (decode_pos[:, None] == key_pos[None, :]).astype(jnp.bfloat16)
     kept_keys = jnp.dot(pick_rows, key_two, preferred_element_type=jnp.float32)
     kept_values = jnp.dot(pick_rows, value_two, preferred_element_type=jnp.float32)

time: 167 us -> 161 us (0.964)
  blocking collectives: 52.3 us -> 15.2 us
  waiting for transfers between devices: 49.3 us -> 71.5 us
  starting transfers between devices: 23.1 us -> 30.4 us
    all_gather x2 -> x0, blocking collectives: 35.5 us -> none  [the longest x1 17.9 us: local(): value_two = lax.all_gather(value_states, 'ctx', axis=1, tiled=True)[0]]
    all_gather x1, waiting for transfers between devices: 0.02 us -> 16.7 us  [local(): lax.all_gather(out_weight, 'ctx', axis=0, tiled=True)]
    ppermute x0 -> x4, starting transfers between devices: none -> 7.1 us  [the longest x3 7.03 us: ctx_gather_blocks(): stack.append(lax.ppermute(rows, 'ctx', perm=perm))]
    ppermute x0 -> x4, waiting for transfers between devices: none -> 4.18 us  [the longest x3 2.34 us: ctx_gather_blocks(): stack.append(lax.ppermute(rows, 'ctx', perm=perm))]
  transfers between devices with their start and end apart: 11 -> 15, of which waited for: 8 -> 11; matrix products, arithmetic and copies ran while one was open for 12% -> 13% of each run, Pallas kernels for 0% -> 0%
where the time goes in v5:
time: 161 us; the launch traced here: 160 us
  waiting for transfers between devices  71.5 us (44%)
  starting transfers between devices  30.4 us (19%)
  matrix products  18.1 us (11%)
  blocking collectives  15.2 us (9%)
  between operations  15.1 us (9%)
  local copies, waits for them, and re-layouts  5.43 us (3%)
  other arithmetic  4.38 us (3%)
    ppermute x7, waiting for transfers between devices, exp_swap(): return lax.ppermute(x, 'exp', perm=[(0, 1), (1, 0)])  30.3 us
    all_gather x1, waiting for transfers between devices, local(): lax.all_gather(out_weight, 'ctx', axis=0, tiled=True)  16.7 us
    all_to_all x1, blocking collectives, moe_column_halves(): lax.all_to_all(part, 'ctx', split_axis=0, concat_axis=0, tiled=True)  15.2 us
    ppermute x7, starting transfers between devices, exp_swap(): return lax.ppermute(x, 'exp', perm=[(0, 1), (1, 0)])  11 us
    all_to_all x1, waiting for transfers between devices, moe_column_halves(): lax.all_to_all(part, 'ctx', split_axis=0, concat_axis=0, tiled=True)  11 us
    all_to_all x2, waiting for transfers between devices, moe_column_halves(): lax.all_to_all(summed.reshape(n_ctx, chunk, half_d), 'ctx', split_axis=0,...  8.71 us
    all_to_all x2, starting transfers between devices, moe_column_halves(): lax.all_to_all(summed.reshape(n_ctx, chunk, half_d), 'ctx', split_axis=0,...  8.19 us
    ppermute x3, starting transfers between devices, ctx_gather_blocks(): stack.append(lax.ppermute(rows, 'ctx', perm=perm))  7.03 us
  transfers between devices with their start and end apart: 15, of which 11 were waited for; matrix products, arithmetic and copies ran while one was open for 13% of the time, Pallas kernels for 0%

profile of v5, /device:TPU:0, one launch (start us, length us, event | category | flops | bytes accessed | tf_op | source)
XLA Modules:
  0.0 160.2 jit_solution(8037675091161416962)
XLA Ops:
  8.8 3.1 %collective-permute-start = (bf16[64,1024]{1,0:T(8,128)(2,1)S(1)}, bf16[64,1024]{1,0:T(8,128)(2,1)S(1)}, u32[]{:S(2)}, u32[]{:S(2)}) collective-permute-start(bf16[64,1024]{1,0:T(8,128)(2,1)S(1)} %get-tuple-element.16), channel_id=1, source_target_pairs={{0,4},{2,6},{4,8},{6,10},{8,12},{10,14},{12,0},{14,2},{1,5},{3,7},... | collective-permute-start | bytes 393224 | tf_op jit(solution)/shard_map/ppermute | solution.py:176
  11.9 2.6 %collective-permute-start.1 = (bf16[64,1024]{1,0:T(8,128)(2,1)S(1)}, bf16[64,1024]{1,0:T(8,128)(2,1)S(1)}, u32[]{:S(2)}, u32[]{:S(2)}) collective-permute-start(bf16[64,1024]{1,0:T(8,128)(2,1)S(1)} %get-tuple-element.16), channel_id=1, source_target_pairs={{0,8},{2,10},{4,12},{6,14},{8,0},{10,2},{12,4},{14,6},{1,9},{3,11}... | collective-permute-start | bytes 393224 | tf_op jit(solution)/shard_map/ppermute | solution.py:176
  14.5 1.4 collective-permute-start.2
  20.8 2.3 %collective-permute-done.1 = bf16[64,1024]{1,0:T(8,128)(2,1)S(1)} collective-permute-done((bf16[64,1024]{1,0:T(8,128)(2,1)S(1)}, bf16[64,1024]{1,0:T(8,128)(2,1)S(1)}, u32[]{:S(2)}, u32[]{:S(2)}) %collective-permute-start.1) | collective-permute-done | bytes 131104 | tf_op jit(solution)/shard_map/ppermute | solution.py:176
  23.3 1.8 %collective-permute-done.3 = bf16[4,64,1024]{2,1,0:T(8,128)(2,1)S(1)} collective-permute-done((bf16[4,64,1024]{2,1,0:T(8,128)(2,1)S(1)}, bf16[4,64,1024]{2,1,0:T(8,128)(2,1)S(1)}, u32[]{:S(2)}, u32[]{:S(2)}) %collective-permute-start.3) | collective-permute-done | bytes 524320 | tf_op jit(solution)/shard_map/ppermute | solution.py:178
  27.6 16.7 %all-gather.2.cloned.1.call-done = bf16[2048,512]{1,0:T(8,128)(2,1)} async-done(((bf16[256,512]{1,0:T(8,128)(2,1)}), bf16[2048,512]{1,0:T(8,128)(2,1)}) %all-gather.2.cloned.1.call-update) | async-done | bytes 2097168 | tf_op jit(solution)/shard_map/all_gather | solution.py:248
  44.2 2.3 %fusion.68 = f32[64,2048]{1,0:T(8,128)S(1)} fusion(bf16[2048,512]{1,0:T(8,128)(2,1)} %all-gather.2.cloned.1.call-done, bf16[4,8,8,128]{3,2,1,0:T(8,128)(2,1)S(1)} %fusion.9), kind=kOutput, calls=%fused_computation.94 | convolution fusion | flops 134217728 | bytes 2686976 | tf_op jit(solution)/shard_map/tc,oc->to/dot_general | solution.py:245
  46.6 1.6 collective-permute-start.4
  48.3 4.0 %collective-permute-done.4 = bf16[32,2048]{1,0:T(8,128)(2,1)S(1)} collective-permute-done((bf16[32,2048]{1,0:T(8,128)(2,1)S(1)}, bf16[32,2048]{1,0:T(8,128)(2,1)S(1)}, u32[]{:S(2)}, u32[]{:S(2)}) %collective-permute-start.4) | collective-permute-done | bytes 131104 | tf_op jit(solution)/shard_map/ppermute | solution.py:48
  52.6 1.6 collective-permute-start.5
  54.4 2.6 %collective-permute-done.5 = bf16[32,1024]{1,0:T(8,128)(2,1)S(1)} collective-permute-done((bf16[32,1024]{1,0:T(8,128)(2,1)S(1)}, bf16[32,1024]{1,0:T(8,128)(2,1)S(1)}, u32[]{:S(2)}, u32[]{:S(2)}) %collective-permute-start.5) | collective-permute-done | bytes 65568 | tf_op jit(solution)/shard_map/ppermute | solution.py:48
  58.2 15.2 %all_to_all.20 = bf16[8,24,1024]{2,1,0:T(8,128)(2,1)S(1)} all-to-all(bf16[8,24,1024]{2,1,0:T(8,128)(2,1)S(1)} %get-tuple-element.11), channel_id=1, replica_groups=mesh['req'=2,'ctx'=8,'exp'=2] {'ctx'}, dimensions={0} | all-to-all | bytes 786432 | tf_op jit(solution)/shard_map/all_to_all | solution.py:138
  73.4 4.1 %all-to-all-start = ((bf16[8,24,1024]{2,1,0:T(8,128)(2,1)}), bf16[8,24,1024]{2,1,0:T(8,128)(2,1)}, u32[]{:S(2)}, u32[]{:S(2)}) async-start(bf16[8,24,1024]{2,1,0:T(8,128)(2,1)} %get-tuple-element.12), calls=%async_computation | async-start | bytes 786432 | tf_op jit(solution)/shard_map/all_to_all | solution.py:138
  77.5 1.6 collective-permute-start.8
  79.1 11.0 %all-to-all-done = bf16[8,24,1024]{2,1,0:T(8,128)(2,1)} async-done(((bf16[8,24,1024]{2,1,0:T(8,128)(2,1)}), bf16[8,24,1024]{2,1,0:T(8,128)(2,1)}, u32[]{:S(2)}, u32[]{:S(2)}) %all-to-all-start) | async-done | bytes 393248 | tf_op jit(solution)/shard_map/all_to_all | solution.py:138
  90.1 1.5 collective-permute-start.6
  92.0 1.4 fusion.32
  93.9 1.4 fusion.26
  95.3 5.6 %collective-permute-done.6 = bf16[192,1024]{1,0:T(8,128)(2,1)S(1)} collective-permute-done((bf16[192,1024]{1,0:T(8,128)(2,1)}, bf16[192,1024]{1,0:T(8,128)(2,1)S(1)}, u32[]{:S(2)}, u32[]{:S(2)}) %collective-permute-start.6) | collective-permute-done | bytes 393248 | tf_op jit(solution)/shard_map/ppermute | solution.py:48
  102.2 1.6 collective-permute-start.7
  103.8 1.4 convolution_add_fusion.1
  105.2 1.4 fusion.6
  106.7 5.4 %collective-permute-done.7 = bf16[192,1024]{1,0:T(8,128)(2,1)S(1)} collective-permute-done((bf16[192,1024]{1,0:T(8,128)(2,1)S(1)}, bf16[192,1024]{1,0:T(8,128)(2,1)S(1)}, u32[]{:S(2)}, u32[]{:S(2)}) %collective-permute-start.7) | collective-permute-done | bytes 393248 | tf_op jit(solution)/shard_map/ppermute | solution.py:48
  113.2 3.5 %all-to-all-start.1 = ((bf16[8,24,1024]{2,1,0:T(8,128)(2,1)}), bf16[8,24,1024]{2,1,0:T(8,128)(2,1)S(1)}, u32[]{:S(2)}, u32[]{:S(2)}) async-start(bf16[8,24,1024]{2,1,0:T(8,128)(2,1)} %bitcast.28), calls=%async_computation.1 | async-start | bytes 786432 | tf_op jit(solution)/shard_map/all_to_all | solution.py:153
  117.0 1.6 collective-permute-start.9
  118.6 10.0 %collective-permute-done.9 = bf16[192,1024]{1,0:T(8,128)(2,1)S(1)} collective-permute-done((bf16[192,1024]{1,0:T(8,128)(2,1)S(1)}, bf16[192,1024]{1,0:T(8,128)(2,1)S(1)}, u32[]{:S(2)}, u32[]{:S(2)}) %collective-permute-start.9) | collective-permute-done | bytes 393248 | tf_op jit(solution)/shard_map/ppermute | solution.py:48
  129.7 4.7 %all-to-all-start.3 = ((bf16[8,24,1024]{2,1,0:T(8,128)(2,1)}), bf16[8,24,1024]{2,1,0:T(8,128)(2,1)S(1)}, u32[]{:S(2)}, u32[]{:S(2)}) async-start(bf16[8,24,1024]{2,1,0:T(8,128)(2,1)} %bitcast.31), calls=%async_computation.3 | async-start | bytes 786432 | tf_op jit(solution)/shard_map/all_to_all | solution.py:153
  137.0 1.3 convolution_bitcast_fusion.1
  138.3 8.7 %all-to-all-done.3 = bf16[8,24,1024]{2,1,0:T(8,128)(2,1)S(1)} async-done(((bf16[8,24,1024]{2,1,0:T(8,128)(2,1)}), bf16[8,24,1024]{2,1,0:T(8,128)(2,1)S(1)}, u32[]{:S(2)}, u32[]{:S(2)}) %all-to-all-start.3) | async-done | bytes 393248 | tf_op jit(solution)/shard_map/all_to_all | solution.py:153
  147.0 1.3 fusion.4
  148.3 1.6 collective-permute-start.10
  149.9 2.7 %collective-permute-done.10 = bf16[32,1024]{1,0:T(8,128)(2,1)S(1)} collective-permute-done((bf16[32,1024]{1,0:T(8,128)(2,1)S(1)}, bf16[32,1024]{1,0:T(8,128)(2,1)S(1)}, u32[]{:S(2)}, u32[]{:S(2)}) %collective-permute-start.10) | collective-permute-done | bytes 65568 | tf_op jit(solution)/shard_map/ppermute | solution.py:48
  (81 shorter events, 18.1 us)
Async XLA Ops:
  7.2 94.7 %copy-start = (bf16[1,352,2048]{2,1,0:T(8,128)(2,1)S(1)}, bf16[1,352,2048]{2,1,0:T(8,128)(2,1)}, u32[]{:S(2)}) copy-start(bf16[1,352,2048]{2,1,0:T(8,128)(2,1)} %param.20) | copy-start | bytes 4325380
  7.2 37.1 %all-gather.2.cloned.1.call-start = ((), (), s32[]{:S(2)}) async-start(), calls=%async_computation.4 | async-start | bytes 2359296 | tf_op jit(solution)/shard_map/all_gather | solution.py:248
  8.8 12.0 %collective-permute-start = (bf16[64,1024]{1,0:T(8,128)(2,1)S(1)}, bf16[64,1024]{1,0:T(8,128)(2,1)S(1)}, u32[]{:S(2)}, u32[]{:S(2)}) collective-permute-start(bf16[64,1024]{1,0:T(8,128)(2,1)S(1)} %get-tuple-element.16), channel_id=1, source_target_pairs={{0,4},{2,6},{4,8},{6,10},{8,12},{10,14},{12,0},{14,2},{1,5},{3,7},... | collective-permute-start | bytes 393224 | tf_op jit(solution)/shard_map/ppermute | solution.py:176
  11.9 11.2 %collective-permute-start.1 = (bf16[64,1024]{1,0:T(8,128)(2,1)S(1)}, bf16[64,1024]{1,0:T(8,128)(2,1)S(1)}, u32[]{:S(2)}, u32[]{:S(2)}) collective-permute-start(bf16[64,1024]{1,0:T(8,128)(2,1)S(1)} %get-tuple-element.16), channel_id=1, source_target_pairs={{0,8},{2,10},{4,12},{6,14},{8,0},{10,2},{12,4},{14,6},{1,9},{3,11}... | collective-permute-start | bytes 393224 | tf_op jit(solution)/shard_map/ppermute | solution.py:176
  14.5 8.6 %collective-permute-start.2 = (bf16[64,1024]{1,0:T(8,128)(2,1)S(1)}, bf16[64,1024]{1,0:T(8,128)(2,1)S(1)}, u32[]{:S(2)}, u32[]{:S(2)}) collective-permute-start(bf16[64,1024]{1,0:T(8,128)(2,1)S(1)} %get-tuple-element.16), channel_id=1, source_target_pairs={{0,12},{2,14},{4,0},{6,2},{8,4},{10,6},{12,8},{14,10},{1,13},{3,15... | collective-permute-start | bytes 393224 | tf_op jit(solution)/shard_map/ppermute | solution.py:176
  23.2 2.0 %collective-permute-start.3 = (bf16[4,64,1024]{2,1,0:T(8,128)(2,1)S(1)}, bf16[4,64,1024]{2,1,0:T(8,128)(2,1)S(1)}, u32[]{:S(2)}, u32[]{:S(2)}) collective-permute-start(bf16[4,64,1024]{2,1,0:T(8,128)(2,1)S(1)} %pad_maximum_fusion), channel_id=1, source_target_pairs={{0,2},{2,0},{4,6},{6,4},{8,10},{10,8},{12,14},{14,12},{1,3},{3,1},... | collective-permute-start | bytes 1572872 | tf_op jit(solution)/shard_map/ppermute | solution.py:178
  25.2 1.0 copy-start.3
  27.5 24.8 %copy-start.5 = (bf16[1,32,2048]{2,1,0:T(8,128)(2,1)S(1)}, bf16[1,32,2048]{2,1,0:T(8,128)(2,1)}, u32[]{:S(2)}) copy-start(bf16[1,32,2048]{2,1,0:T(8,128)(2,1)} %param.15) | copy-start | bytes 393220
  27.6 25.0 %copy-start.6 = (f32[2048]{0:T(1024)S(1)}, f32[2048]{0:T(1024)}, u32[]{:S(2)}) copy-start(f32[2048]{0:T(1024)} %param.17) | copy-start | bytes 24580
  46.6 7.7 %copy-start.7 = (f32[1,64,4]{1,2,0:T(4,128)S(1)}, f32[1,64,4]{1,2,0:T(4,128)}, u32[]{:S(2)}) copy-start(f32[1,64,4]{1,2,0:T(4,128)} %param.22) | copy-start | bytes 3076
  46.6 5.7 %collective-permute-start.4 = (bf16[32,2048]{1,0:T(8,128)(2,1)S(1)}, bf16[32,2048]{1,0:T(8,128)(2,1)S(1)}, u32[]{:S(2)}, u32[]{:S(2)}) collective-permute-start(bf16[32,2048]{1,0:T(8,128)(2,1)S(1)} %select_convert_fusion), channel_id=1, source_target_pairs={{0,1},{1,0},{2,3},{3,2},{4,5},{5,4},{6,7},{7,6},{8,9},{9,8},{10,11... | collective-permute-start | bytes 393224 | tf_op jit(solution)/shard_map/ppermute | solution.py:48
  52.6 4.3 %collective-permute-start.5 = (bf16[32,1024]{1,0:T(8,128)(2,1)S(1)}, bf16[32,1024]{1,0:T(8,128)(2,1)S(1)}, u32[]{:S(2)}, u32[]{:S(2)}) collective-permute-start(bf16[32,1024]{1,0:T(8,128)(2,1)S(1)} %get-tuple-element.14), channel_id=1, source_target_pairs={{0,1},{1,0},{2,3},{3,2},{4,5},{5,4},{6,7},{7,6},{8,9},{9,8},{10,11... | collective-permute-start | bytes 196616 | tf_op jit(solution)/shard_map/ppermute | solution.py:48
  57.4 34.2 %copy-start.1 = (bf16[1,2048,352]{1,2,0:T(8,128)(2,1)S(1)}, bf16[1,2048,352]{1,2,0:T(8,128)(2,1)}, u32[]{:S(2)}) copy-start(bf16[1,2048,352]{1,2,0:T(8,128)(2,1)} %param.18) | copy-start | bytes 4325380
  73.4 16.7 %all-to-all-start = ((bf16[8,24,1024]{2,1,0:T(8,128)(2,1)}), bf16[8,24,1024]{2,1,0:T(8,128)(2,1)}, u32[]{:S(2)}, u32[]{:S(2)}) async-start(bf16[8,24,1024]{2,1,0:T(8,128)(2,1)} %get-tuple-element.12), calls=%async_computation | async-start | bytes 786432 | tf_op jit(solution)/shard_map/all_to_all | solution.py:138
  77.5 26.3 %collective-permute-start.8 = (bf16[192,1024]{1,0:T(8,128)(2,1)S(1)}, bf16[192,1024]{1,0:T(8,128)(2,1)}, u32[]{:S(2)}, u32[]{:S(2)}) collective-permute-start(bf16[192,1024]{1,0:T(8,128)(2,1)S(1)} %bitcast.120), channel_id=1, source_target_pairs={{0,1},{1,0},{2,3},{3,2},{4,5},{5,4},{6,7},{7,6},{8,9},{9,8},{10,11... | collective-permute-start | bytes 1179656 | tf_op jit(solution)/shard_map/ppermute | solution.py:48
  90.1 3.4 %copy-start.2 = (bf16[1,2048,352]{1,2,0:T(8,128)(2,1)S(1)}, bf16[1,2048,352]{1,2,0:T(8,128)(2,1)}, u32[]{:S(2)}) copy-start(bf16[1,2048,352]{1,2,0:T(8,128)(2,1)} %param.19) | copy-start | bytes 4325380
  90.1 10.9 %collective-permute-start.6 = (bf16[192,1024]{1,0:T(8,128)(2,1)}, bf16[192,1024]{1,0:T(8,128)(2,1)S(1)}, u32[]{:S(2)}, u32[]{:S(2)}) collective-permute-start(bf16[192,1024]{1,0:T(8,128)(2,1)} %bitcast.21), channel_id=1, source_target_pairs={{0,1},{1,0},{2,3},{3,2},{4,5},{5,4},{6,7},{7,6},{8,9},{9,8},{10,11... | collective-permute-start | bytes 1179656 | tf_op jit(solution)/shard_map/ppermute | solution.py:48
  102.2 9.8 %collective-permute-start.7 = (bf16[192,1024]{1,0:T(8,128)(2,1)S(1)}, bf16[192,1024]{1,0:T(8,128)(2,1)S(1)}, u32[]{:S(2)}, u32[]{:S(2)}) collective-permute-start(bf16[192,1024]{1,0:T(8,128)(2,1)S(1)} %convolution_convert_fusion.2), channel_id=1, source_target_pairs={{0,1},{1,0},{2,3},{3,2},{4,5},{5,4},{6,7},{7,6},{8,9},{9,8},{10,11... | collective-permute-start | bytes 1179656 | tf_op jit(solution)/shard_map/ppermute | solution.py:48
  113.2 16.5 %all-to-all-start.1 = ((bf16[8,24,1024]{2,1,0:T(8,128)(2,1)}), bf16[8,24,1024]{2,1,0:T(8,128)(2,1)S(1)}, u32[]{:S(2)}, u32[]{:S(2)}) async-start(bf16[8,24,1024]{2,1,0:T(8,128)(2,1)} %bitcast.28), calls=%async_computation.1 | async-start | bytes 786432 | tf_op jit(solution)/shard_map/all_to_all | solution.py:153
  117.0 18.3 %copy-start.4 = (bf16[8,64,1024]{2,1,0:T(8,128)(2,1)S(1)}, bf16[8,64,1024]{2,1,0:T(8,128)(2,1)}, u32[]{:S(2)}) copy-start(bf16[8,64,1024]{2,1,0:T(8,128)(2,1)} %copy-done.3) | copy-start | bytes 3145732
  117.0 11.6 %collective-permute-start.9 = (bf16[192,1024]{1,0:T(8,128)(2,1)S(1)}, bf16[192,1024]{1,0:T(8,128)(2,1)S(1)}, u32[]{:S(2)}, u32[]{:S(2)}) collective-permute-start(bf16[192,1024]{1,0:T(8,128)(2,1)S(1)} %convolution_convert_fusion.1), channel_id=1, source_target_pairs={{0,1},{1,0},{2,3},{3,2},{4,5},{5,4},{6,7},{7,6},{8,9},{9,8},{10,11... | collective-permute-start | bytes 1179656 | tf_op jit(solution)/shard_map/ppermute | solution.py:48
  129.7 17.3 %all-to-all-start.3 = ((bf16[8,24,1024]{2,1,0:T(8,128)(2,1)}), bf16[8,24,1024]{2,1,0:T(8,128)(2,1)S(1)}, u32[]{:S(2)}, u32[]{:S(2)}) async-start(bf16[8,24,1024]{2,1,0:T(8,128)(2,1)} %bitcast.31), calls=%async_computation.3 | async-start | bytes 786432 | tf_op jit(solution)/shard_map/all_to_all | solution.py:153
  148.3 4.3 %collective-permute-start.10 = (bf16[32,1024]{1,0:T(8,128)(2,1)S(1)}, bf16[32,1024]{1,0:T(8,128)(2,1)S(1)}, u32[]{:S(2)}, u32[]{:S(2)}) collective-permute-start(bf16[32,1024]{1,0:T(8,128)(2,1)S(1)} %select_convert_fusion.1), channel_id=1, source_target_pairs={{0,1},{1,0},{2,3},{3,2},{4,5},{5,4},{6,7},{7,6},{8,9},{9,8},{10,11... | collective-permute-start | bytes 196616 | tf_op jit(solution)/shard_map/ppermute | solution.py:48
Sparse Core Ops, SparseCore 0:
  9.6 34.5 all-gather.1

commit v6 on v5

--- a/solution.py
+++ b/solution.py
@@ -180,6 +180,20 @@
     chips = (my_chip - shifts) % n_chip
     src_ctx = jnp.concatenate([chips * 2 + my_core, chips * 2 + (1 - my_core)])
     return jnp.concatenate([own, partner]), src_ctx
+
+
+def gather_out_weight(weight_rows, n_ctx, my_ctx):
+    rows_dev, width = weight_rows.shape
+    split = rows_dev // 2
+    if n_ctx % 2 or split % 8:
+        return lax.all_gather(weight_rows, "ctx", axis=0, tiled=True)
+    front = lax.all_gather(weight_rows[:split], "ctx", axis=0, tiled=False)
+    back_blocks, src_ctx = ctx_gather_blocks(weight_rows[split:], n_ctx, my_ctx)
+    n_chip = n_ctx // 2
+    ctx_ids = jnp.arange(n_ctx, dtype=jnp.int32)
+    block_of = (ctx_ids % 2 != my_ctx % 2) * n_chip + (my_ctx // 2 - ctx_ids // 2) % n_chip
+    back = jnp.take(back_blocks, block_of, axis=0)
+    return jnp.concatenate([front, back], axis=1).reshape(n_ctx * rows_dev, width)
 
 
 def local(
@@ -245,7 +259,7 @@
     out_parts = jnp.einsum(
         "tc,oc->to",
         mixed,
-        lax.all_gather(out_weight, "ctx", axis=0, tiled=True),
+        gather_out_weight(out_weight, n_ctx, my_ctx),
         preferred_element_type=jnp.float32,
     )
     head_total = exp_reduce_rows(out_parts)

time: 161 us -> 177 us (1.099)
  local copies, waits for them, and re-layouts: 5.43 us -> 21.4 us
  waiting for transfers between devices: 71.5 us -> 57.1 us
  other arithmetic: 4.38 us -> 13.5 us
  blocking collectives: 15.2 us -> 17.2 us
    all_gather x1, waiting for transfers between devices: 16.7 us -> 0.02 us  [gather_out_weight(): front = lax.all_gather(weight_rows[:split], 'ctx', axis=0, tiled=False)]
    unnamed x20 -> x42, local copies, waits for them, and re-layouts: 1.74 us -> 7.35 us
    ppermute x3 -> x6, waiting for transfers between devices: 2.34 us -> 7.93 us  [ctx_gather_blocks(): stack.append(lax.ppermute(rows, 'ctx', perm=perm))]
    ppermute x3 -> x6, starting transfers between devices: 7.03 us -> 10.8 us  [ctx_gather_blocks(): stack.append(lax.ppermute(rows, 'ctx', perm=perm))]
    another operation x2 -> x3, other arithmetic: 0.96 us -> 4.74 us  [ctx_gather_blocks(): own = jnp.stack(stack)]
    all_to_all x1, waiting for transfers between devices: 11 us -> 8.46 us  [moe_column_halves(): lax.all_to_all(part, 'ctx', split_axis=0, concat_axis=0, tiled=True)]
    dot_general x2, matrix products: 1.87 us -> 3.99 us  [moe_column_halves(): jnp.dot(arrived, up_mine, preferred_element_type=jnp.float32)]
    eq x2, local copies, waits for them, and re-layouts: 0.21 us -> 2.29 us  [slot_tables(): flat_ids[:, None] == jnp.arange(experts, dtype=jnp.int32)[None, :]]
  transfers between devices with their start and end apart: 15 -> 19, of which waited for: 11 -> 10; matrix products, arithmetic and copies ran while one was open for 13% -> 26% of each run, Pallas kernels for 0% -> 0%
where the time goes in v6:
time: 177 us; the launch traced here: 176 us
  waiting for transfers between devices  57.1 us (32%)
  starting transfers between devices  32.1 us (18%)
  local copies, waits for them, and re-layouts  21.4 us (12%)
  matrix products  19.2 us (11%)
  blocking collectives  17.2 us (10%)
  between operations  15.2 us (9%)
  other arithmetic  13.5 us (8%)
    ppermute x7, waiting for transfers between devices, exp_swap(): return lax.ppermute(x, 'exp', perm=[(0, 1), (1, 0)])  32 us
    all_to_all x1, blocking collectives, moe_column_halves(): lax.all_to_all(part, 'ctx', split_axis=0, concat_axis=0, tiled=True)  17.2 us
    ppermute x6, starting transfers between devices, ctx_gather_blocks(): stack.append(lax.ppermute(rows, 'ctx', perm=perm))  10.8 us
    ppermute x7, starting transfers between devices, exp_swap(): return lax.ppermute(x, 'exp', perm=[(0, 1), (1, 0)])  9.46 us
    all_to_all x2, waiting for transfers between devices, moe_column_halves(): lax.all_to_all(summed.reshape(n_ctx, chunk, half_d), 'ctx', split_axis=0,...  8.72 us
    all_to_all x1, waiting for transfers between devices, moe_column_halves(): lax.all_to_all(part, 'ctx', split_axis=0, concat_axis=0, tiled=True)  8.46 us
    all_to_all x2, starting transfers between devices, moe_column_halves(): lax.all_to_all(summed.reshape(n_ctx, chunk, half_d), 'ctx', split_axis=0,...  8.23 us
    ppermute x6, waiting for transfers between devices, ctx_gather_blocks(): stack.append(lax.ppermute(rows, 'ctx', perm=perm))  7.93 us
  transfers between devices with their start and end apart: 19, of which 10 were waited for; matrix products, arithmetic and copies ran while one was open for 26% of the time, Pallas kernels for 0%

profile of v6, /device:TPU:0, one launch (start us, length us, event | category | flops | bytes accessed | tf_op | source)
XLA Modules:
  0.0 175.8 jit_solution(11005411641629003573)
XLA Ops:
  7.2 1.8 %fusion.117 = (bf16[128,512]{1,0:T(8,128)(2,1)}, bf16[1,128,512]{2,1,0:T(8,128)(2,1)}, bf16[128,512]{1,0:T(8,128)(2,1)}) fusion(bf16[256,512]{1,0:T(8,128)(2,1)} %param.16), kind=kLoop, calls=%fused_computation.218 | loop fusion | bytes 655360 | tf_op jit(solution)/shard_map/slice | solution.py:190
  9.1 3.0 %collective-permute-start.4 = (bf16[128,512]{1,0:T(8,128)(2,1)}, bf16[128,512]{1,0:T(8,128)(2,1)}, u32[]{:S(2)}, u32[]{:S(2)}) collective-permute-start(bf16[128,512]{1,0:T(8,128)(2,1)} %get-tuple-element.15), channel_id=1, source_target_pairs={{0,4},{2,6},{4,8},{6,10},{8,12},{10,14},{12,0},{14,2},{1,5},{3,7},... | collective-permute-start | bytes 393224 | tf_op jit(solution)/shard_map/ppermute | solution.py:176
  12.1 2.6 %collective-permute-start.5 = (bf16[128,512]{1,0:T(8,128)(2,1)}, bf16[128,512]{1,0:T(8,128)(2,1)}, u32[]{:S(2)}, u32[]{:S(2)}) collective-permute-start(bf16[128,512]{1,0:T(8,128)(2,1)} %get-tuple-element.15), channel_id=1, source_target_pairs={{0,8},{2,10},{4,12},{6,14},{8,0},{10,2},{12,4},{14,6},{1,9},{3,11}... | collective-permute-start | bytes 393224 | tf_op jit(solution)/shard_map/ppermute | solution.py:176
  16.0 1.6 fusion.112
  22.1 1.4 eq.91
  29.2 2.9 %collective-permute-start.2 = (bf16[64,1024]{1,0:T(8,128)(2,1)}, bf16[64,1024]{1,0:T(8,128)(2,1)}, u32[]{:S(2)}, u32[]{:S(2)}) collective-permute-start(bf16[64,1024]{1,0:T(8,128)(2,1)} %get-tuple-element.19), channel_id=1, source_target_pairs={{0,12},{2,14},{4,0},{6,2},{8,4},{10,6},{12,8},{14,10},{1,13},{3,15... | collective-permute-start | bytes 393224 | tf_op jit(solution)/shard_map/ppermute | solution.py:176
  32.1 1.5 reshape_squeeze.4
  34.3 2.0 %pad_maximum_fusion.2 = bf16[4,128,512]{2,1,0:T(8,128)(2,1)} fusion(bf16[1,128,512]{2,1,0:T(8,128)(2,1)} %bitcast.18, bf16[1,128,512]{2,1,0:T(8,128)(2,1)} %bitcast.17, bf16[1,128,512]{2,1,0:T(8,128)(2,1)} %bitcast.16, bf16[1,128,512]{2,1,0:T(8,128)(2,1)} %get-tuple-element.14), kind=kLoop, calls=%fused_computation.61 | loop fusion | flops 786432 | bytes 1048576 | tf_op jit(solution)/shard_map/stack | solution.py:177
  36.3 4.7 %collective-permute-done.1 = bf16[64,1024]{1,0:T(8,128)(2,1)} collective-permute-done((bf16[64,1024]{1,0:T(8,128)(2,1)}, bf16[64,1024]{1,0:T(8,128)(2,1)}, u32[]{:S(2)}, u32[]{:S(2)}) %collective-permute-start.1) | collective-permute-done | bytes 131104 | tf_op jit(solution)/shard_map/ppermute | solution.py:176
  40.9 3.3 %collective-permute-done.2 = bf16[64,1024]{1,0:T(8,128)(2,1)} collective-permute-done((bf16[64,1024]{1,0:T(8,128)(2,1)}, bf16[64,1024]{1,0:T(8,128)(2,1)}, u32[]{:S(2)}, u32[]{:S(2)}) %collective-permute-start.2) | collective-permute-done | bytes 131104 | tf_op jit(solution)/shard_map/ppermute | solution.py:176
  52.6 1.9 %constant_dynamic-update-slice_fusion.5 = bf16[8,128,512]{2,1,0:T(8,128)(2,1)} fusion(bf16[8,128,512]{2,1,0:T(8,128)(2,1)} %copy-done.4, bf16[4,128,512]{2,1,0:T(8,128)(2,1)} %collective-permute-done.7), kind=kLoop, calls=%fused_computation.115 | loop fusion | bytes 1048576 | tf_op jit(solution)/shard_map/concatenate | solution.py:182
  54.5 1.9 %gather_fusion = bf16[8,128,512]{2,1,0:T(8,128)(2,1)S(1)} fusion(bf16[8,128,512]{2,1,0:T(8,128)(2,1)} %constant_dynamic-update-slice_fusion.5, s32[1024]{0:T(1024)S(1)} %pad_clamp_fusion), kind=kCustom, calls=%fused_computation | custom fusion | bytes 2097184 | tf_op jit(solution)/shard_map/jit(_take)/gather | solution.py:195
  63.3 4.6 %collective-permute-done.8 = bf16[32,2048]{1,0:T(8,128)(2,1)S(1)} collective-permute-done((bf16[32,2048]{1,0:T(8,128)(2,1)S(1)}, bf16[32,2048]{1,0:T(8,128)(2,1)S(1)}, u32[]{:S(2)}, u32[]{:S(2)}) %collective-permute-start.8) | collective-permute-done | bytes 131104 | tf_op jit(solution)/shard_map/ppermute | solution.py:48
  69.7 3.0 %collective-permute-done.9 = bf16[32,1024]{1,0:T(8,128)(2,1)S(1)} collective-permute-done((bf16[32,1024]{1,0:T(8,128)(2,1)S(1)}, bf16[32,1024]{1,0:T(8,128)(2,1)S(1)}, u32[]{:S(2)}, u32[]{:S(2)}) %collective-permute-start.9) | collective-permute-done | bytes 65568 | tf_op jit(solution)/shard_map/ppermute | solution.py:48
  73.8 17.2 %all_to_all.20 = bf16[8,24,1024]{2,1,0:T(8,128)(2,1)} all-to-all(bf16[8,24,1024]{2,1,0:T(8,128)(2,1)S(1)} %get-tuple-element.12), channel_id=1, replica_groups=mesh['req'=2,'ctx'=8,'exp'=2] {'ctx'}, dimensions={0} | all-to-all | bytes 786432 | tf_op jit(solution)/shard_map/all_to_all | solution.py:138
  91.0 3.5 %all-to-all-start.2 = ((bf16[8,24,1024]{2,1,0:T(8,128)(2,1)}), bf16[8,24,1024]{2,1,0:T(8,128)(2,1)S(1)}, u32[]{:S(2)}, u32[]{:S(2)}) async-start(bf16[8,24,1024]{2,1,0:T(8,128)(2,1)} %get-tuple-element.11), calls=%async_computation.2 | async-start | bytes 786432 | tf_op jit(solution)/shard_map/all_to_all | solution.py:138
  94.5 1.6 collective-permute-start.10
  96.1 2.4 %fusion.26 = f32[192,352]{1,0:T(8,128)} fusion(bf16[192,1024]{1,0:T(8,128)(2,1)} %bitcast.138, bf16[1,2048,352]{1,2,0:T(8,128)(2,1)} %param.19, s32[]{:T(128)S(6)} %select_n.283), kind=kOutput, calls=%fused_computation.40 | convolution fusion | flops 138412032 | bytes 1384452 | tf_op jit(solution)/shard_map/dot_general | solution.py:145
  98.5 8.5 %all-to-all-done.2 = bf16[8,24,1024]{2,1,0:T(8,128)(2,1)S(1)} async-done(((bf16[8,24,1024]{2,1,0:T(8,128)(2,1)}), bf16[8,24,1024]{2,1,0:T(8,128)(2,1)S(1)}, u32[]{:S(2)}, u32[]{:S(2)}) %all-to-all-start.2) | async-done | bytes 393248 | tf_op jit(solution)/shard_map/all_to_all | solution.py:138
  106.9 1.6 fusion.24
  108.5 1.6 collective-permute-start.12
  111.0 1.5 convolution_add_fusion.3
  112.5 1.4 fusion.5
  114.9 5.7 %collective-permute-done.12 = bf16[192,1024]{1,0:T(8,128)(2,1)S(1)} collective-permute-done((bf16[192,1024]{1,0:T(8,128)(2,1)S(1)}, bf16[192,1024]{1,0:T(8,128)(2,1)S(1)}, u32[]{:S(2)}, u32[]{:S(2)}) %collective-permute-start.12) | collective-permute-done | bytes 393248 | tf_op jit(solution)/shard_map/ppermute | solution.py:48
  121.5 6.1 %collective-permute-done.11 = bf16[192,1024]{1,0:T(8,128)(2,1)S(1)} collective-permute-done((bf16[192,1024]{1,0:T(8,128)(2,1)S(1)}, bf16[192,1024]{1,0:T(8,128)(2,1)S(1)}, u32[]{:S(2)}, u32[]{:S(2)}) %collective-permute-start.11) | collective-permute-done | bytes 393248 | tf_op jit(solution)/shard_map/ppermute | solution.py:48
  128.8 3.5 %all-to-all-start.1 = ((bf16[8,24,1024]{2,1,0:T(8,128)(2,1)}), bf16[8,24,1024]{2,1,0:T(8,128)(2,1)S(1)}, u32[]{:S(2)}, u32[]{:S(2)}) async-start(bf16[8,24,1024]{2,1,0:T(8,128)(2,1)} %bitcast.35), calls=%async_computation.1 | async-start | bytes 786432 | tf_op jit(solution)/shard_map/all_to_all | solution.py:153
  132.6 1.6 collective-permute-start.13
  134.3 9.8 %collective-permute-done.13 = bf16[192,1024]{1,0:T(8,128)(2,1)S(1)} collective-permute-done((bf16[192,1024]{1,0:T(8,128)(2,1)S(1)}, bf16[192,1024]{1,0:T(8,128)(2,1)S(1)}, u32[]{:S(2)}, u32[]{:S(2)}) %collective-permute-start.13) | collective-permute-done | bytes 393248 | tf_op jit(solution)/shard_map/ppermute | solution.py:48
  145.2 4.8 %all-to-all-start.3 = ((bf16[8,24,1024]{2,1,0:T(8,128)(2,1)}), bf16[8,24,1024]{2,1,0:T(8,128)(2,1)S(1)}, u32[]{:S(2)}, u32[]{:S(2)}) async-start(bf16[8,24,1024]{2,1,0:T(8,128)(2,1)} %bitcast.38), calls=%async_computation.3 | async-start | bytes 786432 | tf_op jit(solution)/shard_map/all_to_all | solution.py:153
  153.9 8.7 %all-to-all-done.3 = bf16[8,24,1024]{2,1,0:T(8,128)(2,1)S(1)} async-done(((bf16[8,24,1024]{2,1,0:T(8,128)(2,1)}), bf16[8,24,1024]{2,1,0:T(8,128)(2,1)S(1)}, u32[]{:S(2)}, u32[]{:S(2)}) %all-to-all-start.3) | async-done | bytes 393248 | tf_op jit(solution)/shard_map/all_to_all | solution.py:153
  163.9 1.6 collective-permute-start.14
  165.5 2.7 %collective-permute-done.14 = bf16[32,1024]{1,0:T(8,128)(2,1)S(1)} collective-permute-done((bf16[32,1024]{1,0:T(8,128)(2,1)S(1)}, bf16[32,1024]{1,0:T(8,128)(2,1)S(1)}, u32[]{:S(2)}, u32[]{:S(2)}) %collective-permute-start.14) | collective-permute-done | bytes 65568 | tf_op jit(solution)/shard_map/ppermute | solution.py:48
  (120 shorter events, 40.7 us)
Async XLA Ops:
  7.2 106.8 %copy-start = (bf16[1,352,2048]{2,1,0:T(8,128)(2,1)S(1)}, bf16[1,352,2048]{2,1,0:T(8,128)(2,1)}, u32[]{:S(2)}) copy-start(bf16[1,352,2048]{2,1,0:T(8,128)(2,1)} %param.20) | copy-start | bytes 4325380
  7.2 13.3 %copy-start.16 = (s32[1,64,4]{1,2,0:T(4,128)S(1)}, s32[1,64,4]{1,2,0:T(4,128)}, u32[]{:S(2)}) copy-start(s32[1,64,4]{1,2,0:T(4,128)} %param.21) | copy-start | bytes 3076
  7.2 52.5 %all-gather.3.cloned.1.call-start = ((), (), s32[]{:S(2)}) async-start(), calls=%async_computation.4 | async-start | bytes 1179648 | tf_op jit(solution)/shard_map/all_gather | solution.py:190
  9.1 20.1 %collective-permute-start.4 = (bf16[128,512]{1,0:T(8,128)(2,1)}, bf16[128,512]{1,0:T(8,128)(2,1)}, u32[]{:S(2)}, u32[]{:S(2)}) collective-permute-start(bf16[128,512]{1,0:T(8,128)(2,1)} %get-tuple-element.15), channel_id=1, source_target_pairs={{0,4},{2,6},{4,8},{6,10},{8,12},{10,14},{12,0},{14,2},{1,5},{3,7},... | collective-permute-start | bytes 393224 | tf_op jit(solution)/shard_map/ppermute | solution.py:176
  12.1 22.2 %collective-permute-start.5 = (bf16[128,512]{1,0:T(8,128)(2,1)}, bf16[128,512]{1,0:T(8,128)(2,1)}, u32[]{:S(2)}, u32[]{:S(2)}) collective-permute-start(bf16[128,512]{1,0:T(8,128)(2,1)} %get-tuple-element.15), channel_id=1, source_target_pairs={{0,8},{2,10},{4,12},{6,14},{8,0},{10,2},{12,4},{14,6},{1,9},{3,11}... | collective-permute-start | bytes 393224 | tf_op jit(solution)/shard_map/ppermute | solution.py:176
  14.7 19.6 %collective-permute-start.6 = (bf16[128,512]{1,0:T(8,128)(2,1)}, bf16[128,512]{1,0:T(8,128)(2,1)}, u32[]{:S(2)}, u32[]{:S(2)}) collective-permute-start(bf16[128,512]{1,0:T(8,128)(2,1)} %get-tuple-element.15), channel_id=1, source_target_pairs={{0,12},{2,14},{4,0},{6,2},{8,4},{10,6},{12,8},{14,10},{1,13},{3,15... | collective-permute-start | bytes 393224 | tf_op jit(solution)/shard_map/ppermute | solution.py:176
  17.6 18.6 %collective-permute-start = (bf16[64,1024]{1,0:T(8,128)(2,1)}, bf16[64,1024]{1,0:T(8,128)(2,1)}, u32[]{:S(2)}, u32[]{:S(2)}) collective-permute-start(bf16[64,1024]{1,0:T(8,128)(2,1)} %get-tuple-element.19), channel_id=1, source_target_pairs={{0,4},{2,6},{4,8},{6,10},{8,12},{10,14},{12,0},{14,2},{1,5},{3,7},... | collective-permute-start | bytes 393224 | tf_op jit(solution)/shard_map/ppermute | solution.py:176
  18.3 22.6 %collective-permute-start.1 = (bf16[64,1024]{1,0:T(8,128)(2,1)}, bf16[64,1024]{1,0:T(8,128)(2,1)}, u32[]{:S(2)}, u32[]{:S(2)}) collective-permute-start(bf16[64,1024]{1,0:T(8,128)(2,1)} %get-tuple-element.19), channel_id=1, source_target_pairs={{0,8},{2,10},{4,12},{6,14},{8,0},{10,2},{12,4},{14,6},{1,9},{3,11}... | collective-permute-start | bytes 393224 | tf_op jit(solution)/shard_map/ppermute | solution.py:176
  29.2 15.0 %collective-permute-start.2 = (bf16[64,1024]{1,0:T(8,128)(2,1)}, bf16[64,1024]{1,0:T(8,128)(2,1)}, u32[]{:S(2)}, u32[]{:S(2)}) collective-permute-start(bf16[64,1024]{1,0:T(8,128)(2,1)} %get-tuple-element.19), channel_id=1, source_target_pairs={{0,12},{2,14},{4,0},{6,2},{8,4},{10,6},{12,8},{14,10},{1,13},{3,15... | collective-permute-start | bytes 393224 | tf_op jit(solution)/shard_map/ppermute | solution.py:176
  36.3 16.3 %collective-permute-start.7 = (bf16[4,128,512]{2,1,0:T(8,128)(2,1)}, bf16[4,128,512]{2,1,0:T(8,128)(2,1)}, u32[]{:S(2)}, u32[]{:S(2)}) collective-permute-start(bf16[4,128,512]{2,1,0:T(8,128)(2,1)} %pad_maximum_fusion.2), channel_id=1, source_target_pairs={{0,2},{2,0},{4,6},{6,4},{8,10},{10,8},{12,14},{14,12},{1,3},{3,1},... | collective-permute-start | bytes 1572872 | tf_op jit(solution)/shard_map/ppermute | solution.py:178
  45.4 5.7 %collective-permute-start.3 = (bf16[4,64,1024]{2,1,0:T(8,128)(2,1)S(1)}, bf16[4,64,1024]{2,1,0:T(8,128)(2,1)S(1)}, u32[]{:S(2)}, u32[]{:S(2)}) collective-permute-start(bf16[4,64,1024]{2,1,0:T(8,128)(2,1)S(1)} %pad_maximum_fusion.1), channel_id=1, source_target_pairs={{0,2},{2,0},{4,6},{6,4},{8,10},{10,8},{12,14},{14,12},{1,3},{3,1},... | collective-permute-start | bytes 1572872 | tf_op jit(solution)/shard_map/ppermute | solution.py:178
  48.2 3.0 %copy-start.4 = (bf16[8,128,512]{2,1,0:T(8,128)(2,1)}, bf16[8,128,512]{2,1,0:T(8,128)(2,1)S(1)}, u32[]{:S(2)}) copy-start(bf16[8,128,512]{2,1,0:T(8,128)(2,1)S(1)} %constant_dynamic-update-slice_fusion.6) | copy-start | bytes 3145732
  54.5 4.1 %copy-start.8 = (bf16[512,512]{0,1:T(8,128)(2,1)S(1)}, bf16[512,512]{0,1:T(8,128)(2,1)}, u32[]{:S(2)}) copy-start(bf16[512,512]{0,1:T(8,128)(2,1)} %copy.40) | copy-start | bytes 1572868
  56.4 2.2 %copy-start.10 = (pred[64,512]{1,0:T(8,128)(4,1)S(1)}, pred[64,512]{1,0:T(8,128)(4,1)}, u32[]{:S(2)}) copy-start(pred[64,512]{1,0:T(8,128)(4,1)} %compare_and_fusion) | copy-start | bytes 98308
  61.1 2.1 %copy-start.7 = (s32[1,64,4]{2,1,0:T(8,128)S(1)}, s32[1,64,4]{2,1,0:T(8,128)}, u32[]{:S(2)}) copy-start(s32[1,64,4]{2,1,0:T(8,128)} %copy.43) | copy-start | bytes 3076
  61.2 2.1 %copy-start.11 = (s32[64,4]{1,0:T(8,128)S(1)}, s32[64,4]{1,0:T(8,128)}, u32[]{:S(2)}) copy-start(s32[64,4]{1,0:T(8,128)} %reduce_sum.49) | copy-start | bytes 3076
  61.2 6.8 %copy-start.12 = (bf16[1,32,2048]{2,1,0:T(8,128)(2,1)S(1)}, bf16[1,32,2048]{2,1,0:T(8,128)(2,1)}, u32[]{:S(2)}) copy-start(bf16[1,32,2048]{2,1,0:T(8,128)(2,1)} %param.15) | copy-start | bytes 393220
  61.2 7.0 %copy-start.14 = (f32[2048]{0:T(1024)S(1)}, f32[2048]{0:T(1024)}, u32[]{:S(2)}) copy-start(f32[2048]{0:T(1024)} %param.17) | copy-start | bytes 24580
  61.9 7.6 %copy-start.15 = (f32[1,64,4]{1,2,0:T(4,128)S(1)}, f32[1,64,4]{1,2,0:T(4,128)}, u32[]{:S(2)}) copy-start(f32[1,64,4]{1,2,0:T(4,128)} %param.22) | copy-start | bytes 3076
  62.0 6.0 %collective-permute-start.8 = (bf16[32,2048]{1,0:T(8,128)(2,1)S(1)}, bf16[32,2048]{1,0:T(8,128)(2,1)S(1)}, u32[]{:S(2)}, u32[]{:S(2)}) collective-permute-start(bf16[32,2048]{1,0:T(8,128)(2,1)S(1)} %select_convert_fusion), channel_id=1, source_target_pairs={{0,1},{1,0},{2,3},{3,2},{4,5},{5,4},{6,7},{7,6},{8,9},{9,8},{10,11... | collective-permute-start | bytes 393224 | tf_op jit(solution)/shard_map/ppermute | solution.py:48
  68.3 4.3 %collective-permute-start.9 = (bf16[32,1024]{1,0:T(8,128)(2,1)S(1)}, bf16[32,1024]{1,0:T(8,128)(2,1)S(1)}, u32[]{:S(2)}, u32[]{:S(2)}) collective-permute-start(bf16[32,1024]{1,0:T(8,128)(2,1)S(1)} %get-tuple-element.17), channel_id=1, source_target_pairs={{0,1},{1,0},{2,3},{3,2},{4,5},{5,4},{6,7},{7,6},{8,9},{9,8},{10,11... | collective-permute-start | bytes 196616 | tf_op jit(solution)/shard_map/ppermute | solution.py:48
  91.0 15.9 %all-to-all-start.2 = ((bf16[8,24,1024]{2,1,0:T(8,128)(2,1)}), bf16[8,24,1024]{2,1,0:T(8,128)(2,1)S(1)}, u32[]{:S(2)}, u32[]{:S(2)}) async-start(bf16[8,24,1024]{2,1,0:T(8,128)(2,1)} %get-tuple-element.11), calls=%async_computation.2 | async-start | bytes 786432 | tf_op jit(solution)/shard_map/all_to_all | solution.py:138
  94.5 15.7 %copy-start.1 = (bf16[1,2048,352]{1,2,0:T(8,128)(2,1)S(1)}, bf16[1,2048,352]{1,2,0:T(8,128)(2,1)}, u32[]{:S(2)}) copy-start(bf16[1,2048,352]{1,2,0:T(8,128)(2,1)} %param.18) | copy-start | bytes 4325380
  94.5 16.6 %collective-permute-start.10 = (bf16[192,1024]{1,0:T(8,128)(2,1)}, bf16[192,1024]{1,0:T(8,128)(2,1)}, u32[]{:S(2)}, u32[]{:S(2)}) collective-permute-start(bf16[192,1024]{1,0:T(8,128)(2,1)} %bitcast.137), channel_id=1, source_target_pairs={{0,1},{1,0},{2,3},{3,2},{4,5},{5,4},{6,7},{7,6},{8,9},{9,8},{10,11... | collective-permute-start | bytes 1179656 | tf_op jit(solution)/shard_map/ppermute | solution.py:48
  106.9 3.2 %copy-start.2 = (bf16[8,24,1024]{2,1,0:T(8,128)(2,1)S(1)}, bf16[8,24,1024]{2,1,0:T(8,128)(2,1)}, u32[]{:S(2)}) copy-start(bf16[8,24,1024]{2,1,0:T(8,128)(2,1)} %all_to_all.20) | copy-start | bytes 1179652
  108.5 12.1 %collective-permute-start.12 = (bf16[192,1024]{1,0:T(8,128)(2,1)S(1)}, bf16[192,1024]{1,0:T(8,128)(2,1)S(1)}, u32[]{:S(2)}, u32[]{:S(2)}) collective-permute-start(bf16[192,1024]{1,0:T(8,128)(2,1)S(1)} %bitcast.135), channel_id=1, source_target_pairs={{0,1},{1,0},{2,3},{3,2},{4,5},{5,4},{6,7},{7,6},{8,9},{9,8},{10,11... | collective-permute-start | bytes 1179656 | tf_op jit(solution)/shard_map/ppermute | solution.py:48
  114.4 13.3 %collective-permute-start.11 = (bf16[192,1024]{1,0:T(8,128)(2,1)S(1)}, bf16[192,1024]{1,0:T(8,128)(2,1)S(1)}, u32[]{:S(2)}, u32[]{:S(2)}) collective-permute-start(bf16[192,1024]{1,0:T(8,128)(2,1)S(1)} %convolution_convert_fusion.2), channel_id=1, source_target_pairs={{0,1},{1,0},{2,3},{3,2},{4,5},{5,4},{6,7},{7,6},{8,9},{9,8},{10,11... | collective-permute-start | bytes 1179656 | tf_op jit(solution)/shard_map/ppermute | solution.py:48
  128.8 16.5 %all-to-all-start.1 = ((bf16[8,24,1024]{2,1,0:T(8,128)(2,1)}), bf16[8,24,1024]{2,1,0:T(8,128)(2,1)S(1)}, u32[]{:S(2)}, u32[]{:S(2)}) async-start(bf16[8,24,1024]{2,1,0:T(8,128)(2,1)} %bitcast.35), calls=%async_computation.1 | async-start | bytes 786432 | tf_op jit(solution)/shard_map/all_to_all | solution.py:153
  132.6 18.2 %copy-start.6 = (bf16[8,64,1024]{2,1,0:T(8,128)(2,1)S(1)}, bf16[8,64,1024]{2,1,0:T(8,128)(2,1)}, u32[]{:S(2)}) copy-start(bf16[8,64,1024]{2,1,0:T(8,128)(2,1)} %copy-done.5) | copy-start | bytes 3145732
  132.6 11.5 %collective-permute-start.13 = (bf16[192,1024]{1,0:T(8,128)(2,1)S(1)}, bf16[192,1024]{1,0:T(8,128)(2,1)S(1)}, u32[]{:S(2)}, u32[]{:S(2)}) collective-permute-start(bf16[192,1024]{1,0:T(8,128)(2,1)S(1)} %convolution_convert_fusion.1), channel_id=1, source_target_pairs={{0,1},{1,0},{2,3},{3,2},{4,5},{5,4},{6,7},{7,6},{8,9},{9,8},{10,11... | collective-permute-start | bytes 1179656 | tf_op jit(solution)/shard_map/ppermute | solution.py:48
  145.2 17.3 %all-to-all-start.3 = ((bf16[8,24,1024]{2,1,0:T(8,128)(2,1)}), bf16[8,24,1024]{2,1,0:T(8,128)(2,1)S(1)}, u32[]{:S(2)}, u32[]{:S(2)}) async-start(bf16[8,24,1024]{2,1,0:T(8,128)(2,1)} %bitcast.38), calls=%async_computation.3 | async-start | bytes 786432 | tf_op jit(solution)/shard_map/all_to_all | solution.py:153
  163.9 4.3 %collective-permute-start.14 = (bf16[32,1024]{1,0:T(8,128)(2,1)S(1)}, bf16[32,1024]{1,0:T(8,128)(2,1)S(1)}, u32[]{:S(2)}, u32[]{:S(2)}) collective-permute-start(bf16[32,1024]{1,0:T(8,128)(2,1)S(1)} %select_convert_fusion.1), channel_id=1, source_target_pairs={{0,1},{1,0},{2,3},{3,2},{4,5},{5,4},{6,7},{7,6},{8,9},{9,8},{10,11... | collective-permute-start | bytes 196616 | tf_op jit(solution)/shard_map/ppermute | solution.py:48
  (4 other events, 6.5 us)
Sparse Core Ops, SparseCore 0:
  18.8 28.4 all-gather.2

commit v7 on v5

--- a/solution.py
+++ b/solution.py
@@ -117,10 +117,19 @@
     half_d = normed.shape[1] // 2
     my_cols, other_cols = halves(normed, first, 1)
     tokens_cols = join(my_cols, exp_swap(other_cols), first, 0)
+    tok_count = tokens_cols.shape[0]
+    my_ctx = lax.axis_index("ctx")
+    dispatch_rot = jnp.roll(dispatch.reshape(n_ctx, capacity, tok_count), -my_ctx, axis=0)
     send_rows = jnp.dot(
-        dispatch.astype(jnp.bfloat16), tokens_cols, preferred_element_type=jnp.float32
+        dispatch_rot.reshape(n_ctx * capacity, tok_count).astype(jnp.bfloat16),
+        tokens_cols,
+        preferred_element_type=jnp.float32,
     ).astype(jnp.bfloat16)
     send_rows = send_rows.reshape(n_ctx, capacity, half_d)
+    arrived = [send_rows[0]]
+    for shift in range(1, n_ctx):
+        perm = [(i, (i + shift) % n_ctx) for i in range(n_ctx)]
+        arrived.append(lax.ppermute(send_rows[shift], "ctx", perm=perm))
     my_start = my_exp * half_d
     other_start = (1 - my_exp) * half_d
     gate_mine = lax.dynamic_slice_in_dim(gate_matrix, my_start, half_d, axis=0)
@@ -129,20 +138,17 @@
     up_other = lax.dynamic_slice_in_dim(up_matrix, other_start, half_d, axis=0)
     down_other = lax.dynamic_slice_in_dim(down_matrix, other_start, half_d, axis=1)
     down_mine = lax.dynamic_slice_in_dim(down_matrix, my_start, half_d, axis=1)
-    n_chunks = 2 if capacity % 2 == 0 else 1
-    chunk = capacity // n_chunks
-    combine_slots = combine.reshape(combine.shape[0], n_ctx, capacity)
-    moe_half = None
-    for k in range(n_chunks):
-        part = send_rows[:, k * chunk : (k + 1) * chunk]
-        arrived = lax.all_to_all(part, "ctx", split_axis=0, concat_axis=0, tiled=True).reshape(
-            n_ctx * chunk, half_d
-        )
-        partner_cols = exp_swap(arrived)
-        gate_act = jnp.dot(arrived, gate_mine, preferred_element_type=jnp.float32) + jnp.dot(
+    n_groups = 2 if n_ctx % 2 == 0 else 1
+    per_group = n_ctx // n_groups
+    returned = [None] * n_ctx
+    for group in range(n_groups):
+        shifts = range(group * per_group, (group + 1) * per_group)
+        block = jnp.concatenate([arrived[k] for k in shifts], axis=0)
+        partner_cols = exp_swap(block)
+        gate_act = jnp.dot(block, gate_mine, preferred_element_type=jnp.float32) + jnp.dot(
             partner_cols, gate_other, preferred_element_type=jnp.float32
         )
-        up_act = jnp.dot(arrived, up_mine, preferred_element_type=jnp.float32) + jnp.dot(
+        up_act = jnp.dot(block, up_mine, preferred_element_type=jnp.float32) + jnp.dot(
             partner_cols, up_other, preferred_element_type=jnp.float32
         )
         hidden = (jax.nn.silu(gate_act) * up_act).astype(jnp.bfloat16)
@@ -150,17 +156,21 @@
         got_other = exp_swap(out_other.astype(jnp.bfloat16))
         out_mine = jnp.dot(hidden, down_mine, preferred_element_type=jnp.float32)
         summed = (out_mine + got_other.astype(jnp.float32)).astype(jnp.bfloat16)
-        served = lax.all_to_all(
-            summed.reshape(n_ctx, chunk, half_d), "ctx", split_axis=0, concat_axis=0, tiled=True
-        ).reshape(n_ctx * chunk, half_d)
-        weights_k = combine_slots[:, :, k * chunk : (k + 1) * chunk].reshape(-1, n_ctx * chunk)
-        term = jnp.dot(
-            weights_k,
-            served.astype(jnp.float32),
-            precision=lax.Precision.HIGHEST,
-            preferred_element_type=jnp.float32,
-        )
-        moe_half = term if moe_half is None else moe_half + term
+        summed = summed.reshape(per_group, capacity, half_d)
+        for idx, shift in enumerate(shifts):
+            if shift == 0:
+                returned[shift] = summed[idx]
+            else:
+                perm = [(i, (i - shift) % n_ctx) for i in range(n_ctx)]
+                returned[shift] = lax.ppermute(summed[idx], "ctx", perm=perm)
+    served = jnp.stack(returned).reshape(n_ctx * capacity, half_d)
+    combine_rot = jnp.roll(combine.reshape(tok_count, n_ctx, capacity), -my_ctx, axis=1)
+    moe_half = jnp.dot(
+        combine_rot.reshape(tok_count, n_ctx * capacity),
+        served.astype(jnp.float32),
+        precision=lax.Precision.HIGHEST,
+        preferred_element_type=jnp.float32,
+    )
     my_tok, other_tok = halves(moe_half, first, 0)
     got_tok = exp_swap(other_tok.astype(jnp.bfloat16)).astype(jnp.float32)
     return join(my_tok, got_tok, first, 1)

time: 161 us -> 141 us (0.88)
  blocking collectives: 15.2 us -> 0 us
  matrix products: 18.1 us -> 10.8 us
  waiting for transfers between devices: 71.5 us -> 74.7 us
    ppermute x0 -> x14, waiting for transfers between devices: none -> 24.5 us  [the longest x7 14.7 us: moe_column_halves(): returned[shift] = lax.ppermute(summed[idx], 'ctx', perm=perm)]
    all_to_all x3 -> x0, waiting for transfers between devices: 19.7 us -> none  [the longest x1 11 us: moe_column_halves(): lax.all_to_all(part, 'ctx', split_axis=0, concat_axis=0, tiled=True)]
    ppermute x0 -> x14, starting transfers between devices: none -> 15.6 us  [the longest x7 10.4 us: moe_column_halves(): arrived.append(lax.ppermute(send_rows[shift], 'ctx', perm=perm))]
    all_to_all x1 -> x0, blocking collectives: 15.2 us -> none  [moe_column_halves(): lax.all_to_all(part, 'ctx', split_axis=0, concat_axis=0, tiled=True)]
    all_to_all x3 -> x0, starting transfers between devices: 12.3 us -> none  [the longest x2 8.19 us: moe_column_halves(): lax.all_to_all(summed.reshape(n_ctx, chunk, half_d), 'ctx', split_axis=0,...]
    dot_general x7 -> x6, matrix products: 6.66 us -> 2.79 us  [the longest x2 0.91 us: moe_column_halves(): jnp.dot(block, up_mine, preferred_element_type=jnp.float32)]
    ppermute x7, starting transfers between devices: 11 us -> 8.09 us  [exp_swap(): return lax.ppermute(x, 'exp', perm=[(0, 1), (1, 0)])]
    ppermute x7, waiting for transfers between devices: 30.3 us -> 28.6 us  [exp_swap(): return lax.ppermute(x, 'exp', perm=[(0, 1), (1, 0)])]
  transfers between devices with their start and end apart: 15 -> 26, of which waited for: 11 -> 16; matrix products, arithmetic and copies ran while one was open for 13% -> 10% of each run, Pallas kernels for 0% -> 0%
where the time goes in v7:
time: 141 us; the launch traced here: 140 us
  waiting for transfers between devices  74.7 us (53%)
  starting transfers between devices  30.8 us (22%)
  between operations  15.3 us (11%)
  matrix products  10.8 us (8%)
  other arithmetic  4.55 us (3%)
  local copies, waits for them, and re-layouts  4.43 us (3%)
    ppermute x7, waiting for transfers between devices, exp_swap(): return lax.ppermute(x, 'exp', perm=[(0, 1), (1, 0)])  28.6 us
    all_gather x1, waiting for transfers between devices, local(): lax.all_gather(out_weight, 'ctx', axis=0, tiled=True)  16.7 us
    ppermute x7, waiting for transfers between devices, moe_column_halves(): returned[shift] = lax.ppermute(summed[idx], 'ctx', perm=perm)  14.7 us
    ppermute x7, starting transfers between devices, moe_column_halves(): arrived.append(lax.ppermute(send_rows[shift], 'ctx', perm=perm))  10.4 us
    ppermute x7, waiting for transfers between devices, moe_column_halves(): arrived.append(lax.ppermute(send_rows[shift], 'ctx', perm=perm))  9.8 us
    ppermute x7, starting transfers between devices, exp_swap(): return lax.ppermute(x, 'exp', perm=[(0, 1), (1, 0)])  8.09 us
    ppermute x3, starting transfers between devices, ctx_gather_blocks(): stack.append(lax.ppermute(rows, 'ctx', perm=perm))  7.03 us
    ppermute x7, starting transfers between devices, moe_column_halves(): returned[shift] = lax.ppermute(summed[idx], 'ctx', perm=perm)  5.16 us
  transfers between devices with their start and end apart: 26, of which 16 were waited for; matrix products, arithmetic and copies ran while one was open for 10% of the time, Pallas kernels for 0%

profile of v7, /device:TPU:0, one launch (start us, length us, event | category | flops | bytes accessed | tf_op | source)
XLA Modules:
  0.0 140.4 jit_solution(393216315396057780)
XLA Ops:
  8.8 3.1 %collective-permute-start = (bf16[64,1024]{1,0:T(8,128)(2,1)S(1)}, bf16[64,1024]{1,0:T(8,128)(2,1)S(1)}, u32[]{:S(2)}, u32[]{:S(2)}) collective-permute-start(bf16[64,1024]{1,0:T(8,128)(2,1)S(1)} %get-tuple-element.29), channel_id=1, source_target_pairs={{0,4},{2,6},{4,8},{6,10},{8,12},{10,14},{12,0},{14,2},{1,5},{3,7},... | collective-permute-start | bytes 393224 | tf_op jit(solution)/shard_map/ppermute | solution.py:186
  11.9 2.6 %collective-permute-start.1 = (bf16[64,1024]{1,0:T(8,128)(2,1)S(1)}, bf16[64,1024]{1,0:T(8,128)(2,1)S(1)}, u32[]{:S(2)}, u32[]{:S(2)}) collective-permute-start(bf16[64,1024]{1,0:T(8,128)(2,1)S(1)} %get-tuple-element.29), channel_id=1, source_target_pairs={{0,8},{2,10},{4,12},{6,14},{8,0},{10,2},{12,4},{14,6},{1,9},{3,11}... | collective-permute-start | bytes 393224 | tf_op jit(solution)/shard_map/ppermute | solution.py:186
  14.5 1.4 collective-permute-start.2
  19.8 0.9 constant_dynamic-update-slice_fusion.4
  20.8 2.3 %collective-permute-done.1 = bf16[64,1024]{1,0:T(8,128)(2,1)S(1)} collective-permute-done((bf16[64,1024]{1,0:T(8,128)(2,1)S(1)}, bf16[64,1024]{1,0:T(8,128)(2,1)S(1)}, u32[]{:S(2)}, u32[]{:S(2)}) %collective-permute-start.1) | collective-permute-done | bytes 131104 | tf_op jit(solution)/shard_map/ppermute | solution.py:186
  23.3 1.8 %collective-permute-done.3 = bf16[4,64,1024]{2,1,0:T(8,128)(2,1)S(1)} collective-permute-done((bf16[4,64,1024]{2,1,0:T(8,128)(2,1)S(1)}, bf16[4,64,1024]{2,1,0:T(8,128)(2,1)S(1)}, u32[]{:S(2)}, u32[]{:S(2)}) %collective-permute-start.3) | collective-permute-done | bytes 524320 | tf_op jit(solution)/shard_map/ppermute | solution.py:188
  27.6 16.7 %all-gather.2.cloned.1.call-done = bf16[2048,512]{1,0:T(8,128)(2,1)} async-done(((bf16[256,512]{1,0:T(8,128)(2,1)}), bf16[2048,512]{1,0:T(8,128)(2,1)}) %all-gather.2.cloned.1.call-update) | async-done | bytes 2097168 | tf_op jit(solution)/shard_map/all_gather | solution.py:258
  44.2 2.3 %fusion.66 = f32[64,2048]{1,0:T(8,128)S(1)} fusion(bf16[2048,512]{1,0:T(8,128)(2,1)} %all-gather.2.cloned.1.call-done, bf16[4,8,8,128]{3,2,1,0:T(8,128)(2,1)S(1)} %fusion.4), kind=kOutput, calls=%fused_computation.105 | convolution fusion | flops 134217728 | bytes 2686976 | tf_op jit(solution)/shard_map/tc,oc->to/dot_general | solution.py:255
  46.6 1.6 %collective-permute-start.4 = (bf16[32,2048]{1,0:T(8,128)(2,1)S(1)}, bf16[32,2048]{1,0:T(8,128)(2,1)S(1)}, u32[]{:S(2)}, u32[]{:S(2)}) collective-permute-start(bf16[32,2048]{1,0:T(8,128)(2,1)S(1)} %select_convert_fusion), channel_id=1, source_target_pairs={{0,1},{1,0},{2,3},{3,2},{4,5},{5,4},{6,7},{7,6},{8,9},{9,8},{10,11... | collective-permute-start | bytes 393224 | tf_op jit(solution)/shard_map/ppermute | solution.py:48
  48.6 3.7 %collective-permute-done.4 = bf16[32,2048]{1,0:T(8,128)(2,1)S(1)} collective-permute-done((bf16[32,2048]{1,0:T(8,128)(2,1)S(1)}, bf16[32,2048]{1,0:T(8,128)(2,1)S(1)}, u32[]{:S(2)}, u32[]{:S(2)}) %collective-permute-start.4) | collective-permute-done | bytes 131104 | tf_op jit(solution)/shard_map/ppermute | solution.py:48
  52.6 1.6 %collective-permute-start.5 = (bf16[32,1024]{1,0:T(8,128)(2,1)S(1)}, bf16[32,1024]{1,0:T(8,128)(2,1)S(1)}, u32[]{:S(2)}, u32[]{:S(2)}) collective-permute-start(bf16[32,1024]{1,0:T(8,128)(2,1)S(1)} %get-tuple-element.27), channel_id=1, source_target_pairs={{0,1},{1,0},{2,3},{3,2},{4,5},{5,4},{6,7},{7,6},{8,9},{9,8},{10,11... | collective-permute-start | bytes 196616 | tf_op jit(solution)/shard_map/ppermute | solution.py:48
  54.6 2.3 %collective-permute-done.5 = bf16[32,1024]{1,0:T(8,128)(2,1)S(1)} collective-permute-done((bf16[32,1024]{1,0:T(8,128)(2,1)S(1)}, bf16[32,1024]{1,0:T(8,128)(2,1)S(1)}, u32[]{:S(2)}, u32[]{:S(2)}) %collective-permute-start.5) | collective-permute-done | bytes 65568 | tf_op jit(solution)/shard_map/ppermute | solution.py:48
  58.1 1.8 %collective-permute-start.16 = (bf16[48,1024]{1,0:T(8,128)(2,1)S(1)}, bf16[48,1024]{1,0:T(8,128)(2,1)S(1)}, u32[]{:S(2)}, u32[]{:S(2)}) collective-permute-start(bf16[48,1024]{1,0:T(8,128)(2,1)S(1)} %get-tuple-element.12), channel_id=1, source_target_pairs={{0,12},{2,14},{4,0},{6,2},{8,4},{10,6},{12,8},{14,10},{1,13},{3,15... | collective-permute-start | bytes 294920 | tf_op jit(solution)/shard_map/ppermute | solution.py:132
  59.9 2.2 %collective-permute-start.17 = (bf16[48,1024]{1,0:T(8,128)(2,1)S(1)}, bf16[48,1024]{1,0:T(8,128)(2,1)S(1)}, u32[]{:S(2)}, u32[]{:S(2)}) collective-permute-start(bf16[48,1024]{1,0:T(8,128)(2,1)S(1)} %get-tuple-element.11), channel_id=1, source_target_pairs={{0,14},{2,0},{4,2},{6,4},{8,6},{10,8},{12,10},{14,12},{1,15},{3,1}... | collective-permute-start | bytes 294920 | tf_op jit(solution)/shard_map/ppermute | solution.py:132
  62.1 3.5 %collective-permute-done.14 = bf16[48,1024]{1,0:T(8,128)(2,1)S(1)} collective-permute-done((bf16[48,1024]{1,0:T(8,128)(2,1)S(1)}, bf16[48,1024]{1,0:T(8,128)(2,1)S(1)}, u32[]{:S(2)}, u32[]{:S(2)}) %collective-permute-start.14) | collective-permute-done | bytes 98336 | tf_op jit(solution)/shard_map/ppermute | solution.py:132
  65.7 1.6 %collective-permute-start.18 = (bf16[192,1024]{1,0:T(8,128)(2,1)S(1)}, bf16[192,1024]{1,0:T(8,128)(2,1)S(1)}, u32[]{:S(2)}, u32[]{:S(2)}) collective-permute-start(bf16[192,1024]{1,0:T(8,128)(2,1)S(1)} %constant_dynamic-update-slice_fusion.5), channel_id=1, source_target_pairs={{0,1},{1,0},{2,3},{3,2},{4,5},{5,4},{6,7},{7,6},{8,9},{9,8},{10,11... | collective-permute-start | bytes 1179656 | tf_op jit(solution)/shard_map/ppermute | solution.py:48
  68.1 1.6 %collective-permute-start.6 = (bf16[48,1024]{1,0:T(8,128)(2,1)S(1)}, bf16[48,1024]{1,0:T(8,128)(2,1)S(1)}, u32[]{:S(2)}, u32[]{:S(2)}) collective-permute-start(bf16[48,1024]{1,0:T(8,128)(2,1)S(1)} %get-tuple-element.17), channel_id=1, source_target_pairs={{0,2},{2,4},{4,6},{6,8},{8,10},{10,12},{12,14},{14,0},{1,3},{3,5},... | collective-permute-start | bytes 294920 | tf_op jit(solution)/shard_map/ppermute | solution.py:132
  69.7 2.6 %collective-permute-start.7 = (bf16[48,1024]{1,0:T(8,128)(2,1)S(1)}, bf16[48,1024]{1,0:T(8,128)(2,1)S(1)}, u32[]{:S(2)}, u32[]{:S(2)}) collective-permute-start(bf16[48,1024]{1,0:T(8,128)(2,1)S(1)} %get-tuple-element.16), channel_id=1, source_target_pairs={{0,4},{2,6},{4,8},{6,10},{8,12},{10,14},{12,0},{14,2},{1,5},{3,7},... | collective-permute-start | bytes 294920 | tf_op jit(solution)/shard_map/ppermute | solution.py:132
  72.4 1.6 %collective-permute-start.8 = (bf16[48,1024]{1,0:T(8,128)(2,1)S(1)}, bf16[48,1024]{1,0:T(8,128)(2,1)S(1)}, u32[]{:S(2)}, u32[]{:S(2)}) collective-permute-start(bf16[48,1024]{1,0:T(8,128)(2,1)S(1)} %get-tuple-element.15), channel_id=1, source_target_pairs={{0,6},{2,8},{4,10},{6,12},{8,14},{10,0},{12,2},{14,4},{1,7},{3,9},... | collective-permute-start | bytes 294920 | tf_op jit(solution)/shard_map/ppermute | solution.py:132
  74.8 1.4 %collective-permute-done.6 = bf16[48,1024]{1,0:T(8,128)(2,1)S(1)} collective-permute-done((bf16[48,1024]{1,0:T(8,128)(2,1)S(1)}, bf16[48,1024]{1,0:T(8,128)(2,1)S(1)}, u32[]{:S(2)}, u32[]{:S(2)}) %collective-permute-start.6) | collective-permute-done | bytes 98336 | tf_op jit(solution)/shard_map/ppermute | solution.py:132
  76.2 1.3 collective-permute-done.7
  77.6 3.5 %collective-permute-done.8 = bf16[48,1024]{1,0:T(8,128)(2,1)S(1)} collective-permute-done((bf16[48,1024]{1,0:T(8,128)(2,1)S(1)}, bf16[48,1024]{1,0:T(8,128)(2,1)S(1)}, u32[]{:S(2)}, u32[]{:S(2)}) %collective-permute-start.8) | collective-permute-done | bytes 98336 | tf_op jit(solution)/shard_map/ppermute | solution.py:132
  83.9 1.6 %collective-permute-start.19 = (bf16[192,1024]{1,0:T(8,128)(2,1)S(1)}, bf16[192,1024]{1,0:T(8,128)(2,1)S(1)}, u32[]{:S(2)}, u32[]{:S(2)}) collective-permute-start(bf16[192,1024]{1,0:T(8,128)(2,1)S(1)} %convolution_convert_fusion.1), channel_id=1, source_target_pairs={{0,1},{1,0},{2,3},{3,2},{4,5},{5,4},{6,7},{7,6},{8,9},{9,8},{10,11... | collective-permute-start | bytes 1179656 | tf_op jit(solution)/shard_map/ppermute | solution.py:48
  85.5 7.8 %collective-permute-done.9 = bf16[192,1024]{1,0:T(8,128)(2,1)S(1)} collective-permute-done((bf16[192,1024]{1,0:T(8,128)(2,1)S(1)}, bf16[192,1024]{1,0:T(8,128)(2,1)S(1)}, u32[]{:S(2)}, u32[]{:S(2)}) %collective-permute-start.9) | collective-permute-done | bytes 393248 | tf_op jit(solution)/shard_map/ppermute | solution.py:48
  96.0 5.7 %collective-permute-done.19 = bf16[192,1024]{1,0:T(8,128)(2,1)S(1)} collective-permute-done((bf16[192,1024]{1,0:T(8,128)(2,1)S(1)}, bf16[192,1024]{1,0:T(8,128)(2,1)S(1)}, u32[]{:S(2)}, u32[]{:S(2)}) %collective-permute-start.19) | collective-permute-done | bytes 393248 | tf_op jit(solution)/shard_map/ppermute | solution.py:48
  102.1 5.4 %collective-permute-done.10 = bf16[192,1024]{1,0:T(8,128)(2,1)S(1)} collective-permute-done((bf16[192,1024]{1,0:T(8,128)(2,1)S(1)}, bf16[192,1024]{1,0:T(8,128)(2,1)S(1)}, u32[]{:S(2)}, u32[]{:S(2)}) %collective-permute-start.10) | collective-permute-done | bytes 393248 | tf_op jit(solution)/shard_map/ppermute | solution.py:48
  108.0 1.3 collective-permute-start.20
  109.3 1.8 %collective-permute-start.12 = (bf16[48,1024]{1,0:T(8,128)(2,1)S(1)}, bf16[48,1024]{1,0:T(8,128)(2,1)S(1)}, u32[]{:S(2)}, u32[]{:S(2)}) collective-permute-start(bf16[48,1024]{1,0:T(8,128)(2,1)S(1)} %get-tuple-element.24), channel_id=1, source_target_pairs={{0,12},{2,14},{4,0},{6,2},{8,4},{10,6},{12,8},{14,10},{1,13},{3,15... | collective-permute-start | bytes 294920 | tf_op jit(solution)/shard_map/ppermute | solution.py:165
  111.3 1.5 %collective-permute-start.21 = (bf16[48,1024]{1,0:T(8,128)(2,1)S(1)}, bf16[48,1024]{1,0:T(8,128)(2,1)S(1)}, u32[]{:S(2)}, u32[]{:S(2)}) collective-permute-start(bf16[48,1024]{1,0:T(8,128)(2,1)S(1)} %get-tuple-element.21), channel_id=1, source_target_pairs={{0,6},{2,8},{4,10},{6,12},{8,14},{10,0},{12,2},{14,4},{1,7},{3,9},... | collective-permute-start | bytes 294920 | tf_op jit(solution)/shard_map/ppermute | solution.py:165
  113.1 3.4 %collective-permute-done.12 = bf16[48,1024]{1,0:T(8,128)(2,1)S(1)} collective-permute-done((bf16[48,1024]{1,0:T(8,128)(2,1)S(1)}, bf16[48,1024]{1,0:T(8,128)(2,1)S(1)}, u32[]{:S(2)}, u32[]{:S(2)}) %collective-permute-start.12) | collective-permute-done | bytes 98336 | tf_op jit(solution)/shard_map/ppermute | solution.py:165
  117.3 10.5 %collective-permute-done.21 = bf16[48,1024]{1,0:T(8,128)(2,1)S(1)} collective-permute-done((bf16[48,1024]{1,0:T(8,128)(2,1)S(1)}, bf16[48,1024]{1,0:T(8,128)(2,1)S(1)}, u32[]{:S(2)}, u32[]{:S(2)}) %collective-permute-start.21) | collective-permute-done | bytes 98336 | tf_op jit(solution)/shard_map/ppermute | solution.py:165
  129.1 3.7 %collective-permute-done.24 = bf16[32,1024]{1,0:T(8,128)(2,1)S(1)} collective-permute-done((bf16[32,1024]{1,0:T(8,128)(2,1)S(1)}, bf16[32,1024]{1,0:T(8,128)(2,1)S(1)}, u32[]{:S(2)}, u32[]{:S(2)}) %collective-permute-start.24) | collective-permute-done | bytes 65568 | tf_op jit(solution)/shard_map/ppermute | solution.py:48
  (119 shorter events, 20.9 us)
Async XLA Ops:
  7.2 76.4 %copy-start = (bf16[1,352,2048]{2,1,0:T(8,128)(2,1)S(1)}, bf16[1,352,2048]{2,1,0:T(8,128)(2,1)}, u32[]{:S(2)}) copy-start(bf16[1,352,2048]{2,1,0:T(8,128)(2,1)} %param.20) | copy-start | bytes 4325380
  7.2 37.1 %all-gather.2.cloned.1.call-start = ((), (), s32[]{:S(2)}) async-start(), calls=%async_computation | async-start | bytes 2359296 | tf_op jit(solution)/shard_map/all_gather | solution.py:258
  8.8 12.0 %collective-permute-start = (bf16[64,1024]{1,0:T(8,128)(2,1)S(1)}, bf16[64,1024]{1,0:T(8,128)(2,1)S(1)}, u32[]{:S(2)}, u32[]{:S(2)}) collective-permute-start(bf16[64,1024]{1,0:T(8,128)(2,1)S(1)} %get-tuple-element.29), channel_id=1, source_target_pairs={{0,4},{2,6},{4,8},{6,10},{8,12},{10,14},{12,0},{14,2},{1,5},{3,7},... | collective-permute-start | bytes 393224 | tf_op jit(solution)/shard_map/ppermute | solution.py:186
  11.9 11.2 %collective-permute-start.1 = (bf16[64,1024]{1,0:T(8,128)(2,1)S(1)}, bf16[64,1024]{1,0:T(8,128)(2,1)S(1)}, u32[]{:S(2)}, u32[]{:S(2)}) collective-permute-start(bf16[64,1024]{1,0:T(8,128)(2,1)S(1)} %get-tuple-element.29), channel_id=1, source_target_pairs={{0,8},{2,10},{4,12},{6,14},{8,0},{10,2},{12,4},{14,6},{1,9},{3,11}... | collective-permute-start | bytes 393224 | tf_op jit(solution)/shard_map/ppermute | solution.py:186
  14.5 8.6 %collective-permute-start.2 = (bf16[64,1024]{1,0:T(8,128)(2,1)S(1)}, bf16[64,1024]{1,0:T(8,128)(2,1)S(1)}, u32[]{:S(2)}, u32[]{:S(2)}) collective-permute-start(bf16[64,1024]{1,0:T(8,128)(2,1)S(1)} %get-tuple-element.29), channel_id=1, source_target_pairs={{0,12},{2,14},{4,0},{6,2},{8,4},{10,6},{12,8},{14,10},{1,13},{3,15... | collective-permute-start | bytes 393224 | tf_op jit(solution)/shard_map/ppermute | solution.py:186
  23.2 2.0 %collective-permute-start.3 = (bf16[4,64,1024]{2,1,0:T(8,128)(2,1)S(1)}, bf16[4,64,1024]{2,1,0:T(8,128)(2,1)S(1)}, u32[]{:S(2)}, u32[]{:S(2)}) collective-permute-start(bf16[4,64,1024]{2,1,0:T(8,128)(2,1)S(1)} %pad_maximum_fusion), channel_id=1, source_target_pairs={{0,2},{2,0},{4,6},{6,4},{8,10},{10,8},{12,14},{14,12},{1,3},{3,1},... | collective-permute-start | bytes 1572872 | tf_op jit(solution)/shard_map/ppermute | solution.py:188
  27.5 20.8 %copy-start.7 = (f32[1,64,4]{1,2,0:T(4,128)S(1)}, f32[1,64,4]{1,2,0:T(4,128)}, u32[]{:S(2)}) copy-start(f32[1,64,4]{1,2,0:T(4,128)} %param.22) | copy-start | bytes 3076
  27.5 24.8 %copy-start.5 = (bf16[1,32,2048]{2,1,0:T(8,128)(2,1)S(1)}, bf16[1,32,2048]{2,1,0:T(8,128)(2,1)}, u32[]{:S(2)}) copy-start(bf16[1,32,2048]{2,1,0:T(8,128)(2,1)} %param.15) | copy-start | bytes 393220
  46.6 5.9 %copy-start.6 = (f32[2048]{0:T(1024)S(1)}, f32[2048]{0:T(1024)}, u32[]{:S(2)}) copy-start(f32[2048]{0:T(1024)} %param.17) | copy-start | bytes 24580
  46.6 5.7 %collective-permute-start.4 = (bf16[32,2048]{1,0:T(8,128)(2,1)S(1)}, bf16[32,2048]{1,0:T(8,128)(2,1)S(1)}, u32[]{:S(2)}, u32[]{:S(2)}) collective-permute-start(bf16[32,2048]{1,0:T(8,128)(2,1)S(1)} %select_convert_fusion), channel_id=1, source_target_pairs={{0,1},{1,0},{2,3},{3,2},{4,5},{5,4},{6,7},{7,6},{8,9},{9,8},{10,11... | collective-permute-start | bytes 393224 | tf_op jit(solution)/shard_map/ppermute | solution.py:48
  52.6 4.3 %collective-permute-start.5 = (bf16[32,1024]{1,0:T(8,128)(2,1)S(1)}, bf16[32,1024]{1,0:T(8,128)(2,1)S(1)}, u32[]{:S(2)}, u32[]{:S(2)}) collective-permute-start(bf16[32,1024]{1,0:T(8,128)(2,1)S(1)} %get-tuple-element.27), channel_id=1, source_target_pairs={{0,1},{1,0},{2,3},{3,2},{4,5},{5,4},{6,7},{7,6},{8,9},{9,8},{10,11... | collective-permute-start | bytes 196616 | tf_op jit(solution)/shard_map/ppermute | solution.py:48
  57.0 10.3 %copy-start.4 = (bf16[8,64,1024]{2,1,0:T(8,128)(2,1)S(1)}, bf16[8,64,1024]{2,1,0:T(8,128)(2,1)}, u32[]{:S(2)}) copy-start(bf16[8,64,1024]{2,1,0:T(8,128)(2,1)} %copy-done.3) | copy-start | bytes 3145732
  57.4 24.3 %copy-start.1 = (bf16[1,2048,352]{1,2,0:T(8,128)(2,1)S(1)}, bf16[1,2048,352]{1,2,0:T(8,128)(2,1)}, u32[]{:S(2)}) copy-start(bf16[1,2048,352]{1,2,0:T(8,128)(2,1)} %param.18) | copy-start | bytes 4325380
  57.4 8.1 %collective-permute-start.14 = (bf16[48,1024]{1,0:T(8,128)(2,1)S(1)}, bf16[48,1024]{1,0:T(8,128)(2,1)S(1)}, u32[]{:S(2)}, u32[]{:S(2)}) collective-permute-start(bf16[48,1024]{1,0:T(8,128)(2,1)S(1)} %get-tuple-element.14), channel_id=1, source_target_pairs={{0,8},{2,10},{4,12},{6,14},{8,0},{10,2},{12,4},{14,6},{1,9},{3,11}... | collective-permute-start | bytes 294920 | tf_op jit(solution)/shard_map/ppermute | solution.py:132
  58.1 7.5 %collective-permute-start.15 = (bf16[48,1024]{1,0:T(8,128)(2,1)S(1)}, bf16[48,1024]{1,0:T(8,128)(2,1)S(1)}, u32[]{:S(2)}, u32[]{:S(2)}) collective-permute-start(bf16[48,1024]{1,0:T(8,128)(2,1)S(1)} %get-tuple-element.13), channel_id=1, source_target_pairs={{0,10},{2,12},{4,14},{6,0},{8,2},{10,4},{12,6},{14,8},{1,11},{3,13... | collective-permute-start | bytes 294920 | tf_op jit(solution)/shard_map/ppermute | solution.py:132
  58.1 7.5 %collective-permute-start.16 = (bf16[48,1024]{1,0:T(8,128)(2,1)S(1)}, bf16[48,1024]{1,0:T(8,128)(2,1)S(1)}, u32[]{:S(2)}, u32[]{:S(2)}) collective-permute-start(bf16[48,1024]{1,0:T(8,128)(2,1)S(1)} %get-tuple-element.12), channel_id=1, source_target_pairs={{0,12},{2,14},{4,0},{6,2},{8,4},{10,6},{12,8},{14,10},{1,13},{3,15... | collective-permute-start | bytes 294920 | tf_op jit(solution)/shard_map/ppermute | solution.py:132
  59.9 5.8 %collective-permute-start.17 = (bf16[48,1024]{1,0:T(8,128)(2,1)S(1)}, bf16[48,1024]{1,0:T(8,128)(2,1)S(1)}, u32[]{:S(2)}, u32[]{:S(2)}) collective-permute-start(bf16[48,1024]{1,0:T(8,128)(2,1)S(1)} %get-tuple-element.11), channel_id=1, source_target_pairs={{0,14},{2,0},{4,2},{6,4},{8,6},{10,8},{12,10},{14,12},{1,15},{3,1}... | collective-permute-start | bytes 294920 | tf_op jit(solution)/shard_map/ppermute | solution.py:132
  65.7 16.1 %collective-permute-start.18 = (bf16[192,1024]{1,0:T(8,128)(2,1)S(1)}, bf16[192,1024]{1,0:T(8,128)(2,1)S(1)}, u32[]{:S(2)}, u32[]{:S(2)}) collective-permute-start(bf16[192,1024]{1,0:T(8,128)(2,1)S(1)} %constant_dynamic-update-slice_fusion.5), channel_id=1, source_target_pairs={{0,1},{1,0},{2,3},{3,2},{4,5},{5,4},{6,7},{7,6},{8,9},{9,8},{10,11... | collective-permute-start | bytes 1179656 | tf_op jit(solution)/shard_map/ppermute | solution.py:48
  68.1 8.1 %collective-permute-start.6 = (bf16[48,1024]{1,0:T(8,128)(2,1)S(1)}, bf16[48,1024]{1,0:T(8,128)(2,1)S(1)}, u32[]{:S(2)}, u32[]{:S(2)}) collective-permute-start(bf16[48,1024]{1,0:T(8,128)(2,1)S(1)} %get-tuple-element.17), channel_id=1, source_target_pairs={{0,2},{2,4},{4,6},{6,8},{8,10},{10,12},{12,14},{14,0},{1,3},{3,5},... | collective-permute-start | bytes 294920 | tf_op jit(solution)/shard_map/ppermute | solution.py:132
  69.7 7.8 %collective-permute-start.7 = (bf16[48,1024]{1,0:T(8,128)(2,1)S(1)}, bf16[48,1024]{1,0:T(8,128)(2,1)S(1)}, u32[]{:S(2)}, u32[]{:S(2)}) collective-permute-start(bf16[48,1024]{1,0:T(8,128)(2,1)S(1)} %get-tuple-element.16), channel_id=1, source_target_pairs={{0,4},{2,6},{4,8},{6,10},{8,12},{10,14},{12,0},{14,2},{1,5},{3,7},... | collective-permute-start | bytes 294920 | tf_op jit(solution)/shard_map/ppermute | solution.py:132
  72.4 8.7 %collective-permute-start.8 = (bf16[48,1024]{1,0:T(8,128)(2,1)S(1)}, bf16[48,1024]{1,0:T(8,128)(2,1)S(1)}, u32[]{:S(2)}, u32[]{:S(2)}) collective-permute-start(bf16[48,1024]{1,0:T(8,128)(2,1)S(1)} %get-tuple-element.15), channel_id=1, source_target_pairs={{0,6},{2,8},{4,10},{6,12},{8,14},{10,0},{12,2},{14,4},{1,7},{3,9},... | collective-permute-start | bytes 294920 | tf_op jit(solution)/shard_map/ppermute | solution.py:132
  81.1 12.1 %collective-permute-start.9 = (bf16[192,1024]{1,0:T(8,128)(2,1)S(1)}, bf16[192,1024]{1,0:T(8,128)(2,1)S(1)}, u32[]{:S(2)}, u32[]{:S(2)}) collective-permute-start(bf16[192,1024]{1,0:T(8,128)(2,1)S(1)} %pad_maximum_fusion.1), channel_id=1, source_target_pairs={{0,1},{1,0},{2,3},{3,2},{4,5},{5,4},{6,7},{7,6},{8,9},{9,8},{10,11... | collective-permute-start | bytes 1179656 | tf_op jit(solution)/shard_map/ppermute | solution.py:48
  83.9 17.8 %collective-permute-start.19 = (bf16[192,1024]{1,0:T(8,128)(2,1)S(1)}, bf16[192,1024]{1,0:T(8,128)(2,1)S(1)}, u32[]{:S(2)}, u32[]{:S(2)}) collective-permute-start(bf16[192,1024]{1,0:T(8,128)(2,1)S(1)} %convolution_convert_fusion.1), channel_id=1, source_target_pairs={{0,1},{1,0},{2,3},{3,2},{4,5},{5,4},{6,7},{7,6},{8,9},{9,8},{10,11... | collective-permute-start | bytes 1179656 | tf_op jit(solution)/shard_map/ppermute | solution.py:48
  95.4 12.1 %collective-permute-start.10 = (bf16[192,1024]{1,0:T(8,128)(2,1)S(1)}, bf16[192,1024]{1,0:T(8,128)(2,1)S(1)}, u32[]{:S(2)}, u32[]{:S(2)}) collective-permute-start(bf16[192,1024]{1,0:T(8,128)(2,1)S(1)} %convolution_convert_fusion.2), channel_id=1, source_target_pairs={{0,1},{1,0},{2,3},{3,2},{4,5},{5,4},{6,7},{7,6},{8,9},{9,8},{10,11... | collective-permute-start | bytes 1179656 | tf_op jit(solution)/shard_map/ppermute | solution.py:48
  107.9 4.9 %collective-permute-start.11 = (bf16[48,1024]{1,0:T(8,128)(2,1)S(1)}, bf16[48,1024]{1,0:T(8,128)(2,1)S(1)}, u32[]{:S(2)}, u32[]{:S(2)}) collective-permute-start(bf16[48,1024]{1,0:T(8,128)(2,1)S(1)} %get-tuple-element.25), channel_id=1, source_target_pairs={{0,14},{2,0},{4,2},{6,4},{8,6},{10,8},{12,10},{14,12},{1,15},{3,1}... | collective-permute-start | bytes 294920 | tf_op jit(solution)/shard_map/ppermute | solution.py:165
  108.0 9.3 %collective-permute-start.20 = (bf16[48,1024]{1,0:T(8,128)(2,1)S(1)}, bf16[48,1024]{1,0:T(8,128)(2,1)S(1)}, u32[]{:S(2)}, u32[]{:S(2)}) collective-permute-start(bf16[48,1024]{1,0:T(8,128)(2,1)S(1)} %get-tuple-element.22), channel_id=1, source_target_pairs={{0,8},{2,10},{4,12},{6,14},{8,0},{10,2},{12,4},{14,6},{1,9},{3,11}... | collective-permute-start | bytes 294920 | tf_op jit(solution)/shard_map/ppermute | solution.py:165
  109.3 7.2 %collective-permute-start.12 = (bf16[48,1024]{1,0:T(8,128)(2,1)S(1)}, bf16[48,1024]{1,0:T(8,128)(2,1)S(1)}, u32[]{:S(2)}, u32[]{:S(2)}) collective-permute-start(bf16[48,1024]{1,0:T(8,128)(2,1)S(1)} %get-tuple-element.24), channel_id=1, source_target_pairs={{0,12},{2,14},{4,0},{6,2},{8,4},{10,6},{12,8},{14,10},{1,13},{3,15... | collective-permute-start | bytes 294920 | tf_op jit(solution)/shard_map/ppermute | solution.py:165
  111.1 6.2 %collective-permute-start.13 = (bf16[48,1024]{1,0:T(8,128)(2,1)S(1)}, bf16[48,1024]{1,0:T(8,128)(2,1)S(1)}, u32[]{:S(2)}, u32[]{:S(2)}) collective-permute-start(bf16[48,1024]{1,0:T(8,128)(2,1)S(1)} %get-tuple-element.23), channel_id=1, source_target_pairs={{0,10},{2,12},{4,14},{6,0},{8,2},{10,4},{12,6},{14,8},{1,11},{3,13... | collective-permute-start | bytes 294920 | tf_op jit(solution)/shard_map/ppermute | solution.py:165
  111.3 16.6 %collective-permute-start.21 = (bf16[48,1024]{1,0:T(8,128)(2,1)S(1)}, bf16[48,1024]{1,0:T(8,128)(2,1)S(1)}, u32[]{:S(2)}, u32[]{:S(2)}) collective-permute-start(bf16[48,1024]{1,0:T(8,128)(2,1)S(1)} %get-tuple-element.21), channel_id=1, source_target_pairs={{0,6},{2,8},{4,10},{6,12},{8,14},{10,0},{12,2},{14,4},{1,7},{3,9},... | collective-permute-start | bytes 294920 | tf_op jit(solution)/shard_map/ppermute | solution.py:165
  112.8 15.0 %collective-permute-start.22 = (bf16[48,1024]{1,0:T(8,128)(2,1)S(1)}, bf16[48,1024]{1,0:T(8,128)(2,1)S(1)}, u32[]{:S(2)}, u32[]{:S(2)}) collective-permute-start(bf16[48,1024]{1,0:T(8,128)(2,1)S(1)} %get-tuple-element.20), channel_id=1, source_target_pairs={{0,4},{2,6},{4,8},{6,10},{8,12},{10,14},{12,0},{14,2},{1,5},{3,7},... | collective-permute-start | bytes 294920 | tf_op jit(solution)/shard_map/ppermute | solution.py:165
  116.5 11.4 %collective-permute-start.23 = (bf16[48,1024]{1,0:T(8,128)(2,1)S(1)}, bf16[48,1024]{1,0:T(8,128)(2,1)S(1)}, u32[]{:S(2)}, u32[]{:S(2)}) collective-permute-start(bf16[48,1024]{1,0:T(8,128)(2,1)S(1)} %get-tuple-element.19), channel_id=1, source_target_pairs={{0,2},{2,4},{4,6},{6,8},{8,10},{10,12},{12,14},{14,0},{1,3},{3,5},... | collective-permute-start | bytes 294920 | tf_op jit(solution)/shard_map/ppermute | solution.py:165
  128.5 4.3 %collective-permute-start.24 = (bf16[32,1024]{1,0:T(8,128)(2,1)S(1)}, bf16[32,1024]{1,0:T(8,128)(2,1)S(1)}, u32[]{:S(2)}, u32[]{:S(2)}) collective-permute-start(bf16[32,1024]{1,0:T(8,128)(2,1)S(1)} %select_convert_fusion.1), channel_id=1, source_target_pairs={{0,1},{1,0},{2,3},{3,2},{4,5},{5,4},{6,7},{7,6},{8,9},{9,8},{10,11... | collective-permute-start | bytes 196616 | tf_op jit(solution)/shard_map/ppermute | solution.py:48
  (2 other events, 2.5 us)
Sparse Core Ops, SparseCore 0:
  9.6 34.5 all-gather.1

commit v8 on v7

--- a/solution.py
+++ b/solution.py
@@ -119,17 +119,25 @@
     tokens_cols = join(my_cols, exp_swap(other_cols), first, 0)
     tok_count = tokens_cols.shape[0]
     my_ctx = lax.axis_index("ctx")
-    dispatch_rot = jnp.roll(dispatch.reshape(n_ctx, capacity, tok_count), -my_ctx, axis=0)
+    n_chip = n_ctx // 2
+    my_chip = my_ctx // 2
+    my_core = my_ctx % 2
+    chips = (my_chip + jnp.arange(n_chip, dtype=jnp.int32)) % n_chip
+    expert_ids = jnp.concatenate([chips * 2 + my_core, chips * 2 + (1 - my_core)])
+    dispatch_ord = jnp.take(dispatch.reshape(n_ctx, capacity, tok_count), expert_ids, axis=0)
     send_rows = jnp.dot(
-        dispatch_rot.reshape(n_ctx * capacity, tok_count).astype(jnp.bfloat16),
+        dispatch_ord.reshape(n_ctx * capacity, tok_count).astype(jnp.bfloat16),
         tokens_cols,
         preferred_element_type=jnp.float32,
     ).astype(jnp.bfloat16)
-    send_rows = send_rows.reshape(n_ctx, capacity, half_d)
-    arrived = [send_rows[0]]
-    for shift in range(1, n_ctx):
-        perm = [(i, (i + shift) % n_ctx) for i in range(n_ctx)]
-        arrived.append(lax.ppermute(send_rows[shift], "ctx", perm=perm))
+    send_rows = send_rows.reshape(2, n_chip, capacity, half_d)
+    core_swap = [(i, i ^ 1) for i in range(n_ctx)]
+    from_partner = lax.ppermute(send_rows[1], "ctx", perm=core_swap)
+    pairs = jnp.stack([send_rows[0], from_partner], axis=1)
+    arrived = [pairs[0]]
+    for shift in range(1, n_chip):
+        perm = [(i, ((i // 2 + shift) % n_chip) * 2 + i % 2) for i in range(n_ctx)]
+        arrived.append(lax.ppermute(pairs[shift], "ctx", perm=perm))
     my_start = my_exp * half_d
     other_start = (1 - my_exp) * half_d
     gate_mine = lax.dynamic_slice_in_dim(gate_matrix, my_start, half_d, axis=0)
@@ -138,12 +146,12 @@
     up_other = lax.dynamic_slice_in_dim(up_matrix, other_start, half_d, axis=0)
     down_other = lax.dynamic_slice_in_dim(down_matrix, other_start, half_d, axis=1)
     down_mine = lax.dynamic_slice_in_dim(down_matrix, my_start, half_d, axis=1)
-    n_groups = 2 if n_ctx % 2 == 0 else 1
-    per_group = n_ctx // n_groups
-    returned = [None] * n_ctx
+    n_groups = 2 if n_chip % 2 == 0 else 1
+    per_group = n_chip // n_groups
+    returned = [None] * n_chip
     for group in range(n_groups):
         shifts = range(group * per_group, (group + 1) * per_group)
-        block = jnp.concatenate([arrived[k] for k in shifts], axis=0)
+        block = jnp.concatenate([arrived[k] for k in shifts], axis=0).reshape(-1, half_d)
         partner_cols = exp_swap(block)
         gate_act = jnp.dot(block, gate_mine, preferred_element_type=jnp.float32) + jnp.dot(
             partner_cols, gate_other, preferred_element_type=jnp.float32
@@ -156,17 +164,19 @@
         got_other = exp_swap(out_other.astype(jnp.bfloat16))
         out_mine = jnp.dot(hidden, down_mine, preferred_element_type=jnp.float32)
         summed = (out_mine + got_other.astype(jnp.float32)).astype(jnp.bfloat16)
-        summed = summed.reshape(per_group, capacity, half_d)
+        summed = summed.reshape(per_group, 2, capacity, half_d)
         for idx, shift in enumerate(shifts):
             if shift == 0:
                 returned[shift] = summed[idx]
             else:
-                perm = [(i, (i - shift) % n_ctx) for i in range(n_ctx)]
+                perm = [(i, ((i // 2 - shift) % n_chip) * 2 + i % 2) for i in range(n_ctx)]
                 returned[shift] = lax.ppermute(summed[idx], "ctx", perm=perm)
-    served = jnp.stack(returned).reshape(n_ctx * capacity, half_d)
-    combine_rot = jnp.roll(combine.reshape(tok_count, n_ctx, capacity), -my_ctx, axis=1)
+    back = jnp.stack(returned)
+    partner_res = lax.ppermute(back[:, 1], "ctx", perm=core_swap)
+    served = jnp.stack([back[:, 0], partner_res]).reshape(n_ctx * capacity, half_d)
+    combine_ord = jnp.take(combine.reshape(tok_count, n_ctx, capacity), expert_ids, axis=1)
     moe_half = jnp.dot(
-        combine_rot.reshape(tok_count, n_ctx * capacity),
+        combine_ord.reshape(tok_count, n_ctx * capacity),
         served.astype(jnp.float32),
         precision=lax.Precision.HIGHEST,
         preferred_element_type=jnp.float32,

time: 141 us -> 141 us (level)
  waiting for transfers between devices: 74.7 us -> 67.5 us
  local copies, waits for them, and re-layouts: 4.43 us -> 10.2 us
  starting transfers between devices: 30.8 us -> 27.8 us
  other arithmetic: 4.55 us -> 6.78 us
  matrix products: 10.8 us -> 12.7 us
    ppermute x7 -> x5, starting transfers between devices: 10.4 us -> 2.14 us  [the longest x3 2 us: moe_column_halves(): arrived.append(lax.ppermute(pairs[shift], 'ctx', perm=perm))]
    ppermute x7, waiting for transfers between devices: 28.6 us -> 21.7 us  [exp_swap(): return lax.ppermute(x, 'exp', perm=[(0, 1), (1, 0)])]
    ppermute x7 -> x5, waiting for transfers between devices: 9.8 us -> 15.8 us  [the longest x3 14.1 us: moe_column_halves(): arrived.append(lax.ppermute(pairs[shift], 'ctx', perm=perm))]
    ppermute x7 -> x3, starting transfers between devices: 5.16 us -> 10.3 us  [moe_column_halves(): returned[shift] = lax.ppermute(summed[idx], 'ctx', perm=perm)]
    ppermute x7 -> x3, waiting for transfers between devices: 14.7 us -> 10.7 us  [moe_column_halves(): returned[shift] = lax.ppermute(summed[idx], 'ctx', perm=perm)]
    gather x0 -> x3, local copies, waits for them, and re-layouts: none -> 2.83 us  [the longest x1 2.17 us: moe_column_halves(): jnp.take(combine.reshape(tok_count, n_ctx, capacity), expert_ids, axis=1)]
  transfers between devices with their start and end apart: 26 -> 20, of which waited for: 16 -> 14; matrix products, arithmetic and copies ran while one was open for 10% -> 15% of each run, Pallas kernels for 0% -> 0%
where the time goes in v8:
time: 141 us; the launch traced here: 140 us
  waiting for transfers between devices  67.5 us (48%)
  starting transfers between devices  27.8 us (20%)
  between operations  15.2 us (11%)
  matrix products  12.7 us (9%)
  local copies, waits for them, and re-layouts  10.2 us (7%)
  other arithmetic  6.78 us (5%)
    ppermute x7, waiting for transfers between devices, exp_swap(): return lax.ppermute(x, 'exp', perm=[(0, 1), (1, 0)])  21.7 us
    all_gather x1, waiting for transfers between devices, local(): lax.all_gather(out_weight, 'ctx', axis=0, tiled=True)  15.4 us
    ppermute x3, waiting for transfers between devices, moe_column_halves(): arrived.append(lax.ppermute(pairs[shift], 'ctx', perm=perm))  14.1 us
    ppermute x3, waiting for transfers between devices, moe_column_halves(): returned[shift] = lax.ppermute(summed[idx], 'ctx', perm=perm)  10.7 us
    ppermute x3, starting transfers between devices, moe_column_halves(): returned[shift] = lax.ppermute(summed[idx], 'ctx', perm=perm)  10.3 us
    ppermute x7, starting transfers between devices, exp_swap(): return lax.ppermute(x, 'exp', perm=[(0, 1), (1, 0)])  8.18 us
    ppermute x3, starting transfers between devices, ctx_gather_blocks(): stack.append(lax.ppermute(rows, 'ctx', perm=perm))  7.01 us
  transfers between devices with their start and end apart: 20, of which 14 were waited for; matrix products, arithmetic and copies ran while one was open for 15% of the time, Pallas kernels for 0%

profile of v8, /device:TPU:0, one launch (start us, length us, event | category | flops | bytes accessed | tf_op | source)
XLA Modules:
  0.0 140.1 jit_solution(1646546266768289769)
XLA Ops:
  7.2 1.0 fusion.114
  8.2 3.1 %collective-permute-start = (bf16[64,1024]{1,0:T(8,128)(2,1)S(1)}, bf16[64,1024]{1,0:T(8,128)(2,1)S(1)}, u32[]{:S(2)}, u32[]{:S(2)}) collective-permute-start(bf16[64,1024]{1,0:T(8,128)(2,1)S(1)} %get-tuple-element.26), channel_id=1, source_target_pairs={{0,4},{2,6},{4,8},{6,10},{8,12},{10,14},{12,0},{14,2},{1,5},{3,7},... | collective-permute-start | bytes 393224 | tf_op jit(solution)/shard_map/ppermute | solution.py:196
  11.3 2.6 %collective-permute-start.1 = (bf16[64,1024]{1,0:T(8,128)(2,1)S(1)}, bf16[64,1024]{1,0:T(8,128)(2,1)S(1)}, u32[]{:S(2)}, u32[]{:S(2)}) collective-permute-start(bf16[64,1024]{1,0:T(8,128)(2,1)S(1)} %get-tuple-element.26), channel_id=1, source_target_pairs={{0,8},{2,10},{4,12},{6,14},{8,0},{10,2},{12,4},{14,6},{1,9},{3,11}... | collective-permute-start | bytes 393224 | tf_op jit(solution)/shard_map/ppermute | solution.py:196
  13.9 1.3 collective-permute-start.2
  20.5 2.1 %collective-permute-done.1 = bf16[64,1024]{1,0:T(8,128)(2,1)S(1)} collective-permute-done((bf16[64,1024]{1,0:T(8,128)(2,1)S(1)}, bf16[64,1024]{1,0:T(8,128)(2,1)S(1)}, u32[]{:S(2)}, u32[]{:S(2)}) %collective-permute-start.1) | collective-permute-done | bytes 131104 | tf_op jit(solution)/shard_map/ppermute | solution.py:196
  22.8 1.8 %collective-permute-done.3 = bf16[4,64,1024]{2,1,0:T(8,128)(2,1)S(1)} collective-permute-done((bf16[4,64,1024]{2,1,0:T(8,128)(2,1)S(1)}, bf16[4,64,1024]{2,1,0:T(8,128)(2,1)S(1)}, u32[]{:S(2)}, u32[]{:S(2)}) %collective-permute-start.3) | collective-permute-done | bytes 524320 | tf_op jit(solution)/shard_map/ppermute | solution.py:198
  24.6 1.0 copy-done.3
  25.6 1.3 fusion.117
  28.2 15.4 %all-gather.2.cloned.1.call-done = bf16[2048,512]{1,0:T(8,128)(2,1)} async-done(((bf16[256,512]{1,0:T(8,128)(2,1)}), bf16[2048,512]{1,0:T(8,128)(2,1)}) %all-gather.2.cloned.1.call-update) | async-done | bytes 2097168 | tf_op jit(solution)/shard_map/all_gather | solution.py:268
  43.6 2.3 %fusion.72 = f32[64,2048]{1,0:T(8,128)S(1)} fusion(bf16[2048,512]{1,0:T(8,128)(2,1)} %all-gather.2.cloned.1.call-done, bf16[4,8,8,128]{3,2,1,0:T(8,128)(2,1)S(1)} %fusion.8), kind=kOutput, calls=%fused_computation.113 | convolution fusion | flops 134217728 | bytes 2686976 | tf_op jit(solution)/shard_map/tc,oc->to/dot_general | solution.py:265
  46.0 1.6 %collective-permute-start.4 = (bf16[32,2048]{1,0:T(8,128)(2,1)S(1)}, bf16[32,2048]{1,0:T(8,128)(2,1)S(1)}, u32[]{:S(2)}, u32[]{:S(2)}) collective-permute-start(bf16[32,2048]{1,0:T(8,128)(2,1)S(1)} %select_convert_fusion), channel_id=1, source_target_pairs={{0,1},{1,0},{2,3},{3,2},{4,5},{5,4},{6,7},{7,6},{8,9},{9,8},{10,11... | collective-permute-start | bytes 393224 | tf_op jit(solution)/shard_map/ppermute | solution.py:48
  48.5 3.2 %collective-permute-done.4 = bf16[32,2048]{1,0:T(8,128)(2,1)S(1)} collective-permute-done((bf16[32,2048]{1,0:T(8,128)(2,1)S(1)}, bf16[32,2048]{1,0:T(8,128)(2,1)S(1)}, u32[]{:S(2)}, u32[]{:S(2)}) %collective-permute-start.4) | collective-permute-done | bytes 131104 | tf_op jit(solution)/shard_map/ppermute | solution.py:48
  52.0 1.6 %collective-permute-start.5 = (bf16[32,1024]{1,0:T(8,128)(2,1)S(1)}, bf16[32,1024]{1,0:T(8,128)(2,1)S(1)}, u32[]{:S(2)}, u32[]{:S(2)}) collective-permute-start(bf16[32,1024]{1,0:T(8,128)(2,1)S(1)} %get-tuple-element.24), channel_id=1, source_target_pairs={{0,1},{1,0},{2,3},{3,2},{4,5},{5,4},{6,7},{7,6},{8,9},{9,8},{10,11... | collective-permute-start | bytes 196616 | tf_op jit(solution)/shard_map/ppermute | solution.py:48
  53.9 2.5 %collective-permute-done.5 = bf16[32,1024]{1,0:T(8,128)(2,1)S(1)} collective-permute-done((bf16[32,1024]{1,0:T(8,128)(2,1)S(1)}, bf16[32,1024]{1,0:T(8,128)(2,1)S(1)}, u32[]{:S(2)}, u32[]{:S(2)}) %collective-permute-start.5) | collective-permute-done | bytes 65568 | tf_op jit(solution)/shard_map/ppermute | solution.py:48
  56.9 1.7 %collective-permute-done.6 = bf16[4,48,1024]{2,1,0:T(8,128)(2,1)S(1)} collective-permute-done((bf16[4,48,1024]{2,1,0:T(8,128)(2,1)S(1)}, bf16[4,48,1024]{2,1,0:T(8,128)(2,1)S(1)}, u32[]{:S(2)}, u32[]{:S(2)}) %collective-permute-start.6) | collective-permute-done | bytes 393248 | tf_op jit(solution)/shard_map/ppermute | solution.py:135
  60.1 8.0 %collective-permute-done.7 = bf16[2,48,1024]{2,1,0:T(8,128)(2,1)S(1)} collective-permute-done((bf16[2,48,1024]{2,1,0:T(8,128)(2,1)S(1)}, bf16[2,48,1024]{2,1,0:T(8,128)(2,1)S(1)}, u32[]{:S(2)}, u32[]{:S(2)}) %collective-permute-start.7) | collective-permute-done | bytes 196640 | tf_op jit(solution)/shard_map/ppermute | solution.py:140
  68.2 1.6 %collective-permute-start.8 = (bf16[192,1024]{1,0:T(8,128)(2,1)S(1)}, bf16[192,1024]{1,0:T(8,128)(2,1)}, u32[]{:S(2)}, u32[]{:S(2)}) collective-permute-start(bf16[192,1024]{1,0:T(8,128)(2,1)S(1)} %bitcast.151), channel_id=1, source_target_pairs={{0,1},{1,0},{2,3},{3,2},{4,5},{5,4},{6,7},{7,6},{8,9},{9,8},{10,11... | collective-permute-start | bytes 1179656 | tf_op jit(solution)/shard_map/ppermute | solution.py:48
  69.8 1.2 collective-permute-start.12
  71.8 2.2 %gather_fusion = f32[8,64,48]{1,2,0:T(8,128)} fusion(f32[64,8,48]{0,2,1:T(8,128)} %bitcast.161, s32[1024]{0:T(1024)S(1)} %pad_clamp_fusion), kind=kCustom, calls=%fused_computation | custom fusion | bytes 196640 | tf_op jit(solution)/shard_map/jit(_take)/gather | solution.py:177
  74.0 5.8 %collective-permute-done.11 = bf16[2,48,1024]{2,1,0:T(8,128)(2,1)} collective-permute-done((bf16[2,48,1024]{2,1,0:T(8,128)(2,1)}, bf16[2,48,1024]{2,1,0:T(8,128)(2,1)}, u32[]{:S(2)}, u32[]{:S(2)}) %collective-permute-start.11) | collective-permute-done | bytes 196640 | tf_op jit(solution)/shard_map/ppermute | solution.py:140
  80.2 1.1 pad_maximum_fusion.4
  81.8 1.4 %fusion.29 = f32[192,352]{1,0:T(8,128)S(1)} fusion(bf16[192,1024]{1,0:T(8,128)(2,1)} %collective-permute-done.8, bf16[1,2048,352]{1,2,0:T(8,128)(2,1)S(1)} %copy-done.1, s32[]{:T(128)S(6)} %select_n.279), kind=kOutput, calls=%fused_computation.48 | convolution fusion | flops 138412032 | bytes 1384452 | tf_op jit(solution)/shard_map/dot_general | solution.py:156
  83.7 1.4 %fusion.23 = f32[192,352]{1,0:T(8,128)S(1)} fusion(bf16[192,1024]{1,0:T(8,128)(2,1)} %collective-permute-done.8, bf16[1,2048,352]{1,2,0:T(8,128)(2,1)S(1)} %copy-done.2, s32[]{:T(128)S(6)} %select_n.279), kind=kOutput, calls=%fused_computation.42 | convolution fusion | flops 138412032 | bytes 1384452 | tf_op jit(solution)/shard_map/dot_general | solution.py:159
  85.9 1.6 %collective-permute-start.9 = (bf16[192,1024]{1,0:T(8,128)(2,1)S(1)}, bf16[192,1024]{1,0:T(8,128)(2,1)S(1)}, u32[]{:S(2)}, u32[]{:S(2)}) collective-permute-start(bf16[192,1024]{1,0:T(8,128)(2,1)S(1)} %convolution_convert_fusion.2), channel_id=1, source_target_pairs={{0,1},{1,0},{2,3},{3,2},{4,5},{5,4},{6,7},{7,6},{8,9},{9,8},{10,11... | collective-permute-start | bytes 1179656 | tf_op jit(solution)/shard_map/ppermute | solution.py:48
  87.6 5.8 %collective-permute-done.13 = bf16[192,1024]{1,0:T(8,128)(2,1)S(1)} collective-permute-done((bf16[192,1024]{1,0:T(8,128)(2,1)S(1)}, bf16[192,1024]{1,0:T(8,128)(2,1)S(1)}, u32[]{:S(2)}, u32[]{:S(2)}) %collective-permute-start.13) | collective-permute-done | bytes 393248 | tf_op jit(solution)/shard_map/ppermute | solution.py:48
  96.1 5.7 %collective-permute-done.9 = bf16[192,1024]{1,0:T(8,128)(2,1)S(1)} collective-permute-done((bf16[192,1024]{1,0:T(8,128)(2,1)S(1)}, bf16[192,1024]{1,0:T(8,128)(2,1)S(1)}, u32[]{:S(2)}, u32[]{:S(2)}) %collective-permute-start.9) | collective-permute-done | bytes 393248 | tf_op jit(solution)/shard_map/ppermute | solution.py:48
  102.2 5.0 %collective-permute-start.10 = (bf16[2,48,1024]{2,1,0:T(8,128)(2,1)S(1)}, bf16[2,48,1024]{2,1,0:T(8,128)(2,1)S(1)}, u32[]{:S(2)}, u32[]{:S(2)}) collective-permute-start(bf16[2,48,1024]{2,1,0:T(8,128)(2,1)S(1)} %bitcast.181), channel_id=1, source_target_pairs={{0,12},{2,14},{4,0},{6,2},{8,4},{10,6},{12,8},{14,10},{1,13},{3,15... | collective-permute-start | bytes 589832 | tf_op jit(solution)/shard_map/ppermute | solution.py:173
  108.5 3.8 %collective-permute-start.15 = (bf16[2,48,1024]{2,1,0:T(8,128)(2,1)S(1)}, bf16[2,48,1024]{2,1,0:T(8,128)(2,1)S(1)}, u32[]{:S(2)}, u32[]{:S(2)}) collective-permute-start(bf16[2,48,1024]{2,1,0:T(8,128)(2,1)S(1)} %bitcast.183), channel_id=1, source_target_pairs={{0,8},{2,10},{4,12},{6,14},{8,0},{10,2},{12,4},{14,6},{1,9},{3,11}... | collective-permute-start | bytes 589832 | tf_op jit(solution)/shard_map/ppermute | solution.py:173
  112.3 1.5 %collective-permute-start.16 = (bf16[2,48,1024]{2,1,0:T(8,128)(2,1)S(1)}, bf16[2,48,1024]{2,1,0:T(8,128)(2,1)S(1)}, u32[]{:S(2)}, u32[]{:S(2)}) collective-permute-start(bf16[2,48,1024]{2,1,0:T(8,128)(2,1)S(1)} %bitcast.182), channel_id=1, source_target_pairs={{0,4},{2,6},{4,8},{6,10},{8,12},{10,14},{12,0},{14,2},{1,5},{3,7},... | collective-permute-start | bytes 589832 | tf_op jit(solution)/shard_map/ppermute | solution.py:173
  113.9 10.7 %collective-permute-done.15 = bf16[2,48,1024]{2,1,0:T(8,128)(2,1)S(1)} collective-permute-done((bf16[2,48,1024]{2,1,0:T(8,128)(2,1)S(1)}, bf16[2,48,1024]{2,1,0:T(8,128)(2,1)S(1)}, u32[]{:S(2)}, u32[]{:S(2)}) %collective-permute-start.15) | collective-permute-done | bytes 196640 | tf_op jit(solution)/shard_map/ppermute | solution.py:173
  124.9 1.0 copy-done.4
  128.9 3.7 %collective-permute-done.18 = bf16[32,1024]{1,0:T(8,128)(2,1)S(1)} collective-permute-done((bf16[32,1024]{1,0:T(8,128)(2,1)S(1)}, bf16[32,1024]{1,0:T(8,128)(2,1)S(1)}, u32[]{:S(2)}, u32[]{:S(2)}) %collective-permute-start.18) | collective-permute-done | bytes 65568 | tf_op jit(solution)/shard_map/ppermute | solution.py:48
  (110 shorter events, 20.9 us)
Async XLA Ops:
  7.2 78.4 %copy-start = (bf16[1,352,2048]{2,1,0:T(8,128)(2,1)S(1)}, bf16[1,352,2048]{2,1,0:T(8,128)(2,1)}, u32[]{:S(2)}) copy-start(bf16[1,352,2048]{2,1,0:T(8,128)(2,1)} %param.20) | copy-start | bytes 4325380
  7.2 13.1 %copy-start.8 = (f32[1,64,4]{1,2,0:T(4,128)S(1)}, f32[1,64,4]{1,2,0:T(4,128)}, u32[]{:S(2)}) copy-start(f32[1,64,4]{1,2,0:T(4,128)} %param.22) | copy-start | bytes 3076
  7.2 36.4 %all-gather.2.cloned.1.call-start = ((), (), s32[]{:S(2)}) async-start(), calls=%async_computation | async-start | bytes 2359296 | tf_op jit(solution)/shard_map/all_gather | solution.py:268
  8.2 12.2 %collective-permute-start = (bf16[64,1024]{1,0:T(8,128)(2,1)S(1)}, bf16[64,1024]{1,0:T(8,128)(2,1)S(1)}, u32[]{:S(2)}, u32[]{:S(2)}) collective-permute-start(bf16[64,1024]{1,0:T(8,128)(2,1)S(1)} %get-tuple-element.26), channel_id=1, source_target_pairs={{0,4},{2,6},{4,8},{6,10},{8,12},{10,14},{12,0},{14,2},{1,5},{3,7},... | collective-permute-start | bytes 393224 | tf_op jit(solution)/shard_map/ppermute | solution.py:196
  11.3 11.2 %collective-permute-start.1 = (bf16[64,1024]{1,0:T(8,128)(2,1)S(1)}, bf16[64,1024]{1,0:T(8,128)(2,1)S(1)}, u32[]{:S(2)}, u32[]{:S(2)}) collective-permute-start(bf16[64,1024]{1,0:T(8,128)(2,1)S(1)} %get-tuple-element.26), channel_id=1, source_target_pairs={{0,8},{2,10},{4,12},{6,14},{8,0},{10,2},{12,4},{14,6},{1,9},{3,11}... | collective-permute-start | bytes 393224 | tf_op jit(solution)/shard_map/ppermute | solution.py:196
  13.9 8.6 %collective-permute-start.2 = (bf16[64,1024]{1,0:T(8,128)(2,1)S(1)}, bf16[64,1024]{1,0:T(8,128)(2,1)S(1)}, u32[]{:S(2)}, u32[]{:S(2)}) collective-permute-start(bf16[64,1024]{1,0:T(8,128)(2,1)S(1)} %get-tuple-element.26), channel_id=1, source_target_pairs={{0,12},{2,14},{4,0},{6,2},{8,4},{10,6},{12,8},{14,10},{1,13},{3,15... | collective-permute-start | bytes 393224 | tf_op jit(solution)/shard_map/ppermute | solution.py:196
  22.6 2.0 %collective-permute-start.3 = (bf16[4,64,1024]{2,1,0:T(8,128)(2,1)S(1)}, bf16[4,64,1024]{2,1,0:T(8,128)(2,1)S(1)}, u32[]{:S(2)}, u32[]{:S(2)}) collective-permute-start(bf16[4,64,1024]{2,1,0:T(8,128)(2,1)S(1)} %pad_maximum_fusion.2), channel_id=1, source_target_pairs={{0,2},{2,0},{4,6},{6,4},{8,10},{10,8},{12,14},{14,12},{1,3},{3,1},... | collective-permute-start | bytes 1572872 | tf_op jit(solution)/shard_map/ppermute | solution.py:198
  24.6 1.0 copy-start.3
  28.2 23.5 %copy-start.6 = (bf16[1,32,2048]{2,1,0:T(8,128)(2,1)S(1)}, bf16[1,32,2048]{2,1,0:T(8,128)(2,1)}, u32[]{:S(2)}) copy-start(bf16[1,32,2048]{2,1,0:T(8,128)(2,1)} %param.15) | copy-start | bytes 393220
  45.9 5.9 %copy-start.7 = (f32[2048]{0:T(1024)S(1)}, f32[2048]{0:T(1024)}, u32[]{:S(2)}) copy-start(f32[2048]{0:T(1024)} %param.17) | copy-start | bytes 24580
  46.0 5.7 %collective-permute-start.4 = (bf16[32,2048]{1,0:T(8,128)(2,1)S(1)}, bf16[32,2048]{1,0:T(8,128)(2,1)S(1)}, u32[]{:S(2)}, u32[]{:S(2)}) collective-permute-start(bf16[32,2048]{1,0:T(8,128)(2,1)S(1)} %select_convert_fusion), channel_id=1, source_target_pairs={{0,1},{1,0},{2,3},{3,2},{4,5},{5,4},{6,7},{7,6},{8,9},{9,8},{10,11... | collective-permute-start | bytes 393224 | tf_op jit(solution)/shard_map/ppermute | solution.py:48
  52.0 4.3 %collective-permute-start.5 = (bf16[32,1024]{1,0:T(8,128)(2,1)S(1)}, bf16[32,1024]{1,0:T(8,128)(2,1)S(1)}, u32[]{:S(2)}, u32[]{:S(2)}) collective-permute-start(bf16[32,1024]{1,0:T(8,128)(2,1)S(1)} %get-tuple-element.24), channel_id=1, source_target_pairs={{0,1},{1,0},{2,3},{3,2},{4,5},{5,4},{6,7},{7,6},{8,9},{9,8},{10,11... | collective-permute-start | bytes 196616 | tf_op jit(solution)/shard_map/ppermute | solution.py:48
  56.8 1.8 %collective-permute-start.6 = (bf16[4,48,1024]{2,1,0:T(8,128)(2,1)S(1)}, bf16[4,48,1024]{2,1,0:T(8,128)(2,1)S(1)}, u32[]{:S(2)}, u32[]{:S(2)}) collective-permute-start(bf16[4,48,1024]{2,1,0:T(8,128)(2,1)S(1)} %bitcast.173), channel_id=1, source_target_pairs={{0,2},{2,0},{4,6},{6,4},{8,10},{10,8},{12,14},{14,12},{1,3},{3,1},... | collective-permute-start | bytes 1179656 | tf_op jit(solution)/shard_map/ppermute | solution.py:135
  59.4 22.4 %copy-start.1 = (bf16[1,2048,352]{1,2,0:T(8,128)(2,1)S(1)}, bf16[1,2048,352]{1,2,0:T(8,128)(2,1)}, u32[]{:S(2)}) copy-start(bf16[1,2048,352]{1,2,0:T(8,128)(2,1)} %param.18) | copy-start | bytes 4325380
  59.4 8.7 %collective-permute-start.7 = (bf16[2,48,1024]{2,1,0:T(8,128)(2,1)S(1)}, bf16[2,48,1024]{2,1,0:T(8,128)(2,1)S(1)}, u32[]{:S(2)}, u32[]{:S(2)}) collective-permute-start(bf16[2,48,1024]{2,1,0:T(8,128)(2,1)S(1)} %get-tuple-element.14), channel_id=1, source_target_pairs={{0,4},{2,6},{4,8},{6,10},{8,12},{10,14},{12,0},{14,2},{1,5},{3,7},... | collective-permute-start | bytes 589832 | tf_op jit(solution)/shard_map/ppermute | solution.py:140
  68.2 13.6 %collective-permute-start.8 = (bf16[192,1024]{1,0:T(8,128)(2,1)S(1)}, bf16[192,1024]{1,0:T(8,128)(2,1)}, u32[]{:S(2)}, u32[]{:S(2)}) collective-permute-start(bf16[192,1024]{1,0:T(8,128)(2,1)S(1)} %bitcast.151), channel_id=1, source_target_pairs={{0,1},{1,0},{2,3},{3,2},{4,5},{5,4},{6,7},{7,6},{8,9},{9,8},{10,11... | collective-permute-start | bytes 1179656 | tf_op jit(solution)/shard_map/ppermute | solution.py:48
  69.8 10.1 %collective-permute-start.11 = (bf16[2,48,1024]{2,1,0:T(8,128)(2,1)}, bf16[2,48,1024]{2,1,0:T(8,128)(2,1)}, u32[]{:S(2)}, u32[]{:S(2)}) collective-permute-start(bf16[2,48,1024]{2,1,0:T(8,128)(2,1)} %get-tuple-element.16), channel_id=1, source_target_pairs={{0,8},{2,10},{4,12},{6,14},{8,0},{10,2},{12,4},{14,6},{1,9},{3,11}... | collective-permute-start | bytes 589832 | tf_op jit(solution)/shard_map/ppermute | solution.py:140
  69.8 10.4 %collective-permute-start.12 = (bf16[2,48,1024]{2,1,0:T(8,128)(2,1)}, bf16[2,48,1024]{2,1,0:T(8,128)(2,1)}, u32[]{:S(2)}, u32[]{:S(2)}) collective-permute-start(bf16[2,48,1024]{2,1,0:T(8,128)(2,1)} %get-tuple-element.15), channel_id=1, source_target_pairs={{0,12},{2,14},{4,0},{6,2},{8,4},{10,6},{12,8},{14,10},{1,13},{3,15... | collective-permute-start | bytes 589832 | tf_op jit(solution)/shard_map/ppermute | solution.py:140
  81.2 2.4 %copy-start.2 = (bf16[1,2048,352]{1,2,0:T(8,128)(2,1)S(1)}, bf16[1,2048,352]{1,2,0:T(8,128)(2,1)}, u32[]{:S(2)}) copy-start(bf16[1,2048,352]{1,2,0:T(8,128)(2,1)} %param.19) | copy-start | bytes 4325380
  81.2 12.1 %collective-permute-start.13 = (bf16[192,1024]{1,0:T(8,128)(2,1)S(1)}, bf16[192,1024]{1,0:T(8,128)(2,1)S(1)}, u32[]{:S(2)}, u32[]{:S(2)}) collective-permute-start(bf16[192,1024]{1,0:T(8,128)(2,1)S(1)} %bitcast.154), channel_id=1, source_target_pairs={{0,1},{1,0},{2,3},{3,2},{4,5},{5,4},{6,7},{7,6},{8,9},{9,8},{10,11... | collective-permute-start | bytes 1179656 | tf_op jit(solution)/shard_map/ppermute | solution.py:48
  85.9 15.8 %collective-permute-start.9 = (bf16[192,1024]{1,0:T(8,128)(2,1)S(1)}, bf16[192,1024]{1,0:T(8,128)(2,1)S(1)}, u32[]{:S(2)}, u32[]{:S(2)}) collective-permute-start(bf16[192,1024]{1,0:T(8,128)(2,1)S(1)} %convolution_convert_fusion.2), channel_id=1, source_target_pairs={{0,1},{1,0},{2,3},{3,2},{4,5},{5,4},{6,7},{7,6},{8,9},{9,8},{10,11... | collective-permute-start | bytes 1179656 | tf_op jit(solution)/shard_map/ppermute | solution.py:48
  95.5 12.6 %collective-permute-start.14 = (bf16[192,1024]{1,0:T(8,128)(2,1)S(1)}, bf16[192,1024]{1,0:T(8,128)(2,1)S(1)}, u32[]{:S(2)}, u32[]{:S(2)}) collective-permute-start(bf16[192,1024]{1,0:T(8,128)(2,1)S(1)} %convolution_convert_fusion.1), channel_id=1, source_target_pairs={{0,1},{1,0},{2,3},{3,2},{4,5},{5,4},{6,7},{7,6},{8,9},{9,8},{10,11... | collective-permute-start | bytes 1179656 | tf_op jit(solution)/shard_map/ppermute | solution.py:48
  102.2 11.7 %copy-start.5 = (f32[8,64,48]{1,2,0:T(8,128)S(1)}, f32[8,64,48]{1,2,0:T(8,128)}, u32[]{:S(2)}) copy-start(f32[8,64,48]{1,2,0:T(8,128)} %gather_fusion) | copy-start | bytes 294916
  102.2 11.7 %collective-permute-start.10 = (bf16[2,48,1024]{2,1,0:T(8,128)(2,1)S(1)}, bf16[2,48,1024]{2,1,0:T(8,128)(2,1)S(1)}, u32[]{:S(2)}, u32[]{:S(2)}) collective-permute-start(bf16[2,48,1024]{2,1,0:T(8,128)(2,1)S(1)} %bitcast.181), channel_id=1, source_target_pairs={{0,12},{2,14},{4,0},{6,2},{8,4},{10,6},{12,8},{14,10},{1,13},{3,15... | collective-permute-start | bytes 589832 | tf_op jit(solution)/shard_map/ppermute | solution.py:173
  108.5 16.1 %collective-permute-start.15 = (bf16[2,48,1024]{2,1,0:T(8,128)(2,1)S(1)}, bf16[2,48,1024]{2,1,0:T(8,128)(2,1)S(1)}, u32[]{:S(2)}, u32[]{:S(2)}) collective-permute-start(bf16[2,48,1024]{2,1,0:T(8,128)(2,1)S(1)} %bitcast.183), channel_id=1, source_target_pairs={{0,8},{2,10},{4,12},{6,14},{8,0},{10,2},{12,4},{14,6},{1,9},{3,11}... | collective-permute-start | bytes 589832 | tf_op jit(solution)/shard_map/ppermute | solution.py:173
  112.3 12.3 %collective-permute-start.16 = (bf16[2,48,1024]{2,1,0:T(8,128)(2,1)S(1)}, bf16[2,48,1024]{2,1,0:T(8,128)(2,1)S(1)}, u32[]{:S(2)}, u32[]{:S(2)}) collective-permute-start(bf16[2,48,1024]{2,1,0:T(8,128)(2,1)S(1)} %bitcast.182), channel_id=1, source_target_pairs={{0,4},{2,6},{4,8},{6,10},{8,12},{10,14},{12,0},{14,2},{1,5},{3,7},... | collective-permute-start | bytes 589832 | tf_op jit(solution)/shard_map/ppermute | solution.py:173
  124.6 1.2 copy-start.4
  124.8 2.8 %collective-permute-start.17 = (bf16[4,48,1024]{2,1,0:T(8,128)(2,1)S(1)}, bf16[4,48,1024]{2,1,0:T(8,128)(2,1)S(1)}, u32[]{:S(2)}, u32[]{:S(2)}) collective-permute-start(bf16[4,48,1024]{2,1,0:T(8,128)(2,1)S(1)} %get-tuple-element.12), channel_id=1, source_target_pairs={{0,2},{2,0},{4,6},{6,4},{8,10},{10,8},{12,14},{14,12},{1,3},{3,1},... | collective-permute-start | bytes 1179656 | tf_op jit(solution)/shard_map/ppermute | solution.py:175
  128.3 4.3 %collective-permute-start.18 = (bf16[32,1024]{1,0:T(8,128)(2,1)S(1)}, bf16[32,1024]{1,0:T(8,128)(2,1)S(1)}, u32[]{:S(2)}, u32[]{:S(2)}) collective-permute-start(bf16[32,1024]{1,0:T(8,128)(2,1)S(1)} %select_convert_fusion.1), channel_id=1, source_target_pairs={{0,1},{1,0},{2,3},{3,2},{4,5},{5,4},{6,7},{7,6},{8,9},{9,8},{10,11... | collective-permute-start | bytes 196616 | tf_op jit(solution)/shard_map/ppermute | solution.py:48
Sparse Core Ops, SparseCore 0:
  15.4 28.1 all-gather.1

commit v9 on v8

--- a/solution.py
+++ b/solution.py
@@ -146,8 +146,8 @@
     up_other = lax.dynamic_slice_in_dim(up_matrix, other_start, half_d, axis=0)
     down_other = lax.dynamic_slice_in_dim(down_matrix, other_start, half_d, axis=1)
     down_mine = lax.dynamic_slice_in_dim(down_matrix, my_start, half_d, axis=1)
-    n_groups = 2 if n_chip % 2 == 0 else 1
-    per_group = n_chip // n_groups
+    per_group = 1 if n_chip <= 4 else n_chip // 2
+    n_groups = n_chip // per_group
     returned = [None] * n_chip
     for group in range(n_groups):
         shifts = range(group * per_group, (group + 1) * per_group)

time: 141 us -> 134 us (0.950)
  waiting for transfers between devices: 67.5 us -> 55.1 us
  starting transfers between devices: 27.8 us -> 31.4 us
    ppermute x7 -> x11, waiting for transfers between devices: 21.7 us -> 16.6 us  [exp_swap(): return lax.ppermute(x, 'exp', perm=[(0, 1), (1, 0)])]
    ppermute x3, waiting for transfers between devices: 14.1 us -> 9.49 us  [moe_column_halves(): arrived.append(lax.ppermute(pairs[shift], 'ctx', perm=perm))]
    ppermute x7 -> x11, starting transfers between devices: 8.18 us -> 11.3 us  [exp_swap(): return lax.ppermute(x, 'exp', perm=[(0, 1), (1, 0)])]
    ppermute x3, starting transfers between devices: 2 us -> 4.02 us  [moe_column_halves(): arrived.append(lax.ppermute(pairs[shift], 'ctx', perm=perm))]
    ppermute x1, waiting for transfers between devices: 1.71 us -> 0.01 us  [moe_column_halves(): from_partner = lax.ppermute(send_rows[1], 'ctx', perm=core_swap)]
    ppermute x3, starting transfers between devices: 10.3 us -> 8.86 us  [moe_column_halves(): returned[shift] = lax.ppermute(summed[idx], 'ctx', perm=perm)]
  transfers between devices with their start and end apart: 20 -> 24, of which waited for: 14 -> 12; matrix products, arithmetic and copies ran while one was open for 15% -> 17% of each run, Pallas kernels for 0% -> 0%
where the time goes in v9:
time: 134 us; the launch traced here: 133 us
  waiting for transfers between devices  55.1 us (41%)
  starting transfers between devices  31.4 us (23%)
  between operations  15.3 us (11%)
  matrix products  13.8 us (10%)
  local copies, waits for them, and re-layouts  10.8 us (8%)
  other arithmetic  7.01 us (5%)
    ppermute x11, waiting for transfers between devices, exp_swap(): return lax.ppermute(x, 'exp', perm=[(0, 1), (1, 0)])  16.6 us
    all_gather x1, waiting for transfers between devices, local(): lax.all_gather(out_weight, 'ctx', axis=0, tiled=True)  15.4 us
    ppermute x11, starting transfers between devices, exp_swap(): return lax.ppermute(x, 'exp', perm=[(0, 1), (1, 0)])  11.3 us
    ppermute x3, waiting for transfers between devices, moe_column_halves(): returned[shift] = lax.ppermute(summed[idx], 'ctx', perm=perm)  9.78 us
    ppermute x3, waiting for transfers between devices, moe_column_halves(): arrived.append(lax.ppermute(pairs[shift], 'ctx', perm=perm))  9.49 us
    ppermute x3, starting transfers between devices, moe_column_halves(): returned[shift] = lax.ppermute(summed[idx], 'ctx', perm=perm)  8.86 us
    ppermute x3, starting transfers between devices, ctx_gather_blocks(): stack.append(lax.ppermute(rows, 'ctx', perm=perm))  7.01 us
    ppermute x3, starting transfers between devices, moe_column_halves(): arrived.append(lax.ppermute(pairs[shift], 'ctx', perm=perm))  4.02 us
  transfers between devices with their start and end apart: 24, of which 12 were waited for; matrix products, arithmetic and copies ran while one was open for 17% of the time, Pallas kernels for 0%

profile of v9, /device:TPU:0, one launch (start us, length us, event | category | flops | bytes accessed | tf_op | source)
XLA Modules:
  0.0 133.4 jit_solution(11741958289810069249)
XLA Ops:
  7.2 1.0 fusion.163
  8.2 3.1 %collective-permute-start = (bf16[64,1024]{1,0:T(8,128)(2,1)S(1)}, bf16[64,1024]{1,0:T(8,128)(2,1)S(1)}, u32[]{:S(2)}, u32[]{:S(2)}) collective-permute-start(bf16[64,1024]{1,0:T(8,128)(2,1)S(1)} %get-tuple-element.22), channel_id=1, source_target_pairs={{0,4},{2,6},{4,8},{6,10},{8,12},{10,14},{12,0},{14,2},{1,5},{3,7},... | collective-permute-start | bytes 393224 | tf_op jit(solution)/shard_map/ppermute | solution.py:196
  11.3 2.6 %collective-permute-start.1 = (bf16[64,1024]{1,0:T(8,128)(2,1)S(1)}, bf16[64,1024]{1,0:T(8,128)(2,1)S(1)}, u32[]{:S(2)}, u32[]{:S(2)}) collective-permute-start(bf16[64,1024]{1,0:T(8,128)(2,1)S(1)} %get-tuple-element.22), channel_id=1, source_target_pairs={{0,8},{2,10},{4,12},{6,14},{8,0},{10,2},{12,4},{14,6},{1,9},{3,11}... | collective-permute-start | bytes 393224 | tf_op jit(solution)/shard_map/ppermute | solution.py:196
  13.9 1.3 %collective-permute-start.2 = (bf16[64,1024]{1,0:T(8,128)(2,1)S(1)}, bf16[64,1024]{1,0:T(8,128)(2,1)S(1)}, u32[]{:S(2)}, u32[]{:S(2)}) collective-permute-start(bf16[64,1024]{1,0:T(8,128)(2,1)S(1)} %get-tuple-element.22), channel_id=1, source_target_pairs={{0,12},{2,14},{4,0},{6,2},{8,4},{10,6},{12,8},{14,10},{1,13},{3,15... | collective-permute-start | bytes 393224 | tf_op jit(solution)/shard_map/ppermute | solution.py:196
  20.5 2.1 %collective-permute-done.1 = bf16[64,1024]{1,0:T(8,128)(2,1)S(1)} collective-permute-done((bf16[64,1024]{1,0:T(8,128)(2,1)S(1)}, bf16[64,1024]{1,0:T(8,128)(2,1)S(1)}, u32[]{:S(2)}, u32[]{:S(2)}) %collective-permute-start.1) | collective-permute-done | bytes 131104 | tf_op jit(solution)/shard_map/ppermute | solution.py:196
  22.8 1.8 %collective-permute-done.3 = bf16[4,64,1024]{2,1,0:T(8,128)(2,1)S(1)} collective-permute-done((bf16[4,64,1024]{2,1,0:T(8,128)(2,1)S(1)}, bf16[4,64,1024]{2,1,0:T(8,128)(2,1)S(1)}, u32[]{:S(2)}, u32[]{:S(2)}) %collective-permute-start.3) | collective-permute-done | bytes 524320 | tf_op jit(solution)/shard_map/ppermute | solution.py:198
  24.6 1.0 copy-done.3
  25.6 1.3 fusion.166
  28.2 15.4 %all-gather.2.cloned.1.call-done = bf16[2048,512]{1,0:T(8,128)(2,1)} async-done(((bf16[256,512]{1,0:T(8,128)(2,1)}), bf16[2048,512]{1,0:T(8,128)(2,1)}) %all-gather.2.cloned.1.call-update) | async-done | bytes 2097168 | tf_op jit(solution)/shard_map/all_gather | solution.py:268
  43.6 2.3 %fusion.93 = f32[64,2048]{1,0:T(8,128)S(1)} fusion(bf16[2048,512]{1,0:T(8,128)(2,1)} %all-gather.2.cloned.1.call-done, bf16[4,8,8,128]{3,2,1,0:T(8,128)(2,1)S(1)} %fusion.4), kind=kOutput, calls=%fused_computation.148 | convolution fusion | flops 134217728 | bytes 2686976 | tf_op jit(solution)/shard_map/tc,oc->to/dot_general | solution.py:265
  46.0 1.6 %collective-permute-start.4 = (bf16[32,2048]{1,0:T(8,128)(2,1)S(1)}, bf16[32,2048]{1,0:T(8,128)(2,1)S(1)}, u32[]{:S(2)}, u32[]{:S(2)}) collective-permute-start(bf16[32,2048]{1,0:T(8,128)(2,1)S(1)} %select_convert_fusion), channel_id=1, source_target_pairs={{0,1},{1,0},{2,3},{3,2},{4,5},{5,4},{6,7},{7,6},{8,9},{9,8},{10,11... | collective-permute-start | bytes 393224 | tf_op jit(solution)/shard_map/ppermute | solution.py:48
  48.5 3.2 %collective-permute-done.4 = bf16[32,2048]{1,0:T(8,128)(2,1)S(1)} collective-permute-done((bf16[32,2048]{1,0:T(8,128)(2,1)S(1)}, bf16[32,2048]{1,0:T(8,128)(2,1)S(1)}, u32[]{:S(2)}, u32[]{:S(2)}) %collective-permute-start.4) | collective-permute-done | bytes 131104 | tf_op jit(solution)/shard_map/ppermute | solution.py:48
  52.0 1.6 %collective-permute-start.5 = (bf16[32,1024]{1,0:T(8,128)(2,1)S(1)}, bf16[32,1024]{1,0:T(8,128)(2,1)S(1)}, u32[]{:S(2)}, u32[]{:S(2)}) collective-permute-start(bf16[32,1024]{1,0:T(8,128)(2,1)S(1)} %get-tuple-element.20), channel_id=1, source_target_pairs={{0,1},{1,0},{2,3},{3,2},{4,5},{5,4},{6,7},{7,6},{8,9},{9,8},{10,11... | collective-permute-start | bytes 196616 | tf_op jit(solution)/shard_map/ppermute | solution.py:48
  53.9 2.5 %collective-permute-done.5 = bf16[32,1024]{1,0:T(8,128)(2,1)S(1)} collective-permute-done((bf16[32,1024]{1,0:T(8,128)(2,1)S(1)}, bf16[32,1024]{1,0:T(8,128)(2,1)S(1)}, u32[]{:S(2)}, u32[]{:S(2)}) %collective-permute-start.5) | collective-permute-done | bytes 65568 | tf_op jit(solution)/shard_map/ppermute | solution.py:48
  58.3 2.2 %gather_fusion = f32[8,64,48]{1,2,0:T(8,128)} fusion(f32[64,8,48]{0,2,1:T(8,128)} %bitcast.202, s32[1024]{0:T(1024)S(1)} %pad_clamp_fusion), kind=kCustom, calls=%fused_computation | custom fusion | bytes 196640 | tf_op jit(solution)/shard_map/jit(_take)/gather | solution.py:177
  60.5 1.1 broadcast_select_fusion
  61.6 1.1 fusion.80
  62.7 1.6 %collective-permute-start.7 = (bf16[96,1024]{1,0:T(8,128)(2,1)S(1)}, bf16[96,1024]{1,0:T(8,128)(2,1)S(1)}, u32[]{:S(2)}, u32[]{:S(2)}) collective-permute-start(bf16[96,1024]{1,0:T(8,128)(2,1)S(1)} %bitcast.195), channel_id=1, source_target_pairs={{0,1},{1,0},{2,3},{3,2},{4,5},{5,4},{6,7},{7,6},{8,9},{9,8},{10,11... | collective-permute-start | bytes 589832 | tf_op jit(solution)/shard_map/ppermute | solution.py:48
  65.0 1.6 %collective-permute-start.13 = (bf16[2,48,1024]{2,1,0:T(8,128)(2,1)S(1)}, bf16[2,48,1024]{2,1,0:T(8,128)(2,1)S(1)}, u32[]{:S(2)}, u32[]{:S(2)}) collective-permute-start(bf16[2,48,1024]{2,1,0:T(8,128)(2,1)S(1)} %get-tuple-element.16), channel_id=1, source_target_pairs={{0,8},{2,10},{4,12},{6,14},{8,0},{10,2},{12,4},{14,6},{1,9},{3,11}... | collective-permute-start | bytes 589832 | tf_op jit(solution)/shard_map/ppermute | solution.py:140
  66.6 1.8 %collective-permute-start.17 = (bf16[2,48,1024]{2,1,0:T(8,128)(2,1)S(1)}, bf16[2,48,1024]{2,1,0:T(8,128)(2,1)S(1)}, u32[]{:S(2)}, u32[]{:S(2)}) collective-permute-start(bf16[2,48,1024]{2,1,0:T(8,128)(2,1)S(1)} %get-tuple-element.15), channel_id=1, source_target_pairs={{0,12},{2,14},{4,0},{6,2},{8,4},{10,6},{12,8},{14,10},{1,13},{3,15... | collective-permute-start | bytes 589832 | tf_op jit(solution)/shard_map/ppermute | solution.py:140
  69.1 4.9 %collective-permute-done.9 = bf16[2,48,1024]{2,1,0:T(8,128)(2,1)S(1)} collective-permute-done((bf16[2,48,1024]{2,1,0:T(8,128)(2,1)S(1)}, bf16[2,48,1024]{2,1,0:T(8,128)(2,1)S(1)}, u32[]{:S(2)}, u32[]{:S(2)}) %collective-permute-start.9) | collective-permute-done | bytes 196640 | tf_op jit(solution)/shard_map/ppermute | solution.py:140
  75.6 1.6 %collective-permute-start.8 = (bf16[96,1024]{1,0:T(8,128)(2,1)S(1)}, bf16[96,1024]{1,0:T(8,128)(2,1)S(1)}, u32[]{:S(2)}, u32[]{:S(2)}) collective-permute-start(bf16[96,1024]{1,0:T(8,128)(2,1)S(1)} %convolution_convert_fusion.4), channel_id=1, source_target_pairs={{0,1},{1,0},{2,3},{3,2},{4,5},{5,4},{6,7},{7,6},{8,9},{9,8},{10,11... | collective-permute-start | bytes 589832 | tf_op jit(solution)/shard_map/ppermute | solution.py:48
  77.2 4.6 %collective-permute-done.13 = bf16[2,48,1024]{2,1,0:T(8,128)(2,1)S(1)} collective-permute-done((bf16[2,48,1024]{2,1,0:T(8,128)(2,1)S(1)}, bf16[2,48,1024]{2,1,0:T(8,128)(2,1)S(1)}, u32[]{:S(2)}, u32[]{:S(2)}) %collective-permute-start.13) | collective-permute-done | bytes 196640 | tf_op jit(solution)/shard_map/ppermute | solution.py:140
  82.2 1.6 %collective-permute-start.18 = (bf16[96,1024]{1,0:T(8,128)(2,1)S(1)}, bf16[96,1024]{1,0:T(8,128)(2,1)S(1)}, u32[]{:S(2)}, u32[]{:S(2)}) collective-permute-start(bf16[96,1024]{1,0:T(8,128)(2,1)S(1)} %bitcast.220), channel_id=1, source_target_pairs={{0,1},{1,0},{2,3},{3,2},{4,5},{5,4},{6,7},{7,6},{8,9},{9,8},{10,11... | collective-permute-start | bytes 589832 | tf_op jit(solution)/shard_map/ppermute | solution.py:48
  86.1 3.5 %collective-permute-done.14 = bf16[96,1024]{1,0:T(8,128)(2,1)S(1)} collective-permute-done((bf16[96,1024]{1,0:T(8,128)(2,1)S(1)}, bf16[96,1024]{1,0:T(8,128)(2,1)S(1)}, u32[]{:S(2)}, u32[]{:S(2)}) %collective-permute-start.14) | collective-permute-done | bytes 196640 | tf_op jit(solution)/shard_map/ppermute | solution.py:48
  91.9 1.9 %collective-permute-done.18 = bf16[96,1024]{1,0:T(8,128)(2,1)S(1)} collective-permute-done((bf16[96,1024]{1,0:T(8,128)(2,1)S(1)}, bf16[96,1024]{1,0:T(8,128)(2,1)S(1)}, u32[]{:S(2)}, u32[]{:S(2)}) %collective-permute-start.18) | collective-permute-done | bytes 196640 | tf_op jit(solution)/shard_map/ppermute | solution.py:48
  96.1 1.9 %collective-permute-done.11 = bf16[96,1024]{1,0:T(8,128)(2,1)S(1)} collective-permute-done((bf16[96,1024]{1,0:T(8,128)(2,1)S(1)}, bf16[96,1024]{1,0:T(8,128)(2,1)S(1)}, u32[]{:S(2)}, u32[]{:S(2)}) %collective-permute-start.11) | collective-permute-done | bytes 196640 | tf_op jit(solution)/shard_map/ppermute | solution.py:48
  98.3 4.3 %collective-permute-start.12 = (bf16[2,48,1024]{2,1,0:T(8,128)(2,1)S(1)}, bf16[2,48,1024]{2,1,0:T(8,128)(2,1)S(1)}, u32[]{:S(2)}, u32[]{:S(2)}) collective-permute-start(bf16[2,48,1024]{2,1,0:T(8,128)(2,1)S(1)} %bitcast.229), channel_id=1, source_target_pairs={{0,12},{2,14},{4,0},{6,2},{8,4},{10,6},{12,8},{14,10},{1,13},{3,15... | collective-permute-start | bytes 589832 | tf_op jit(solution)/shard_map/ppermute | solution.py:173
  103.0 3.7 %collective-permute-start.16 = (bf16[2,48,1024]{2,1,0:T(8,128)(2,1)S(1)}, bf16[2,48,1024]{2,1,0:T(8,128)(2,1)S(1)}, u32[]{:S(2)}, u32[]{:S(2)}) collective-permute-start(bf16[2,48,1024]{2,1,0:T(8,128)(2,1)S(1)} %bitcast.230), channel_id=1, source_target_pairs={{0,8},{2,10},{4,12},{6,14},{8,0},{10,2},{12,4},{14,6},{1,9},{3,11}... | collective-permute-start | bytes 589832 | tf_op jit(solution)/shard_map/ppermute | solution.py:173
  108.1 9.8 %collective-permute-done.16 = bf16[2,48,1024]{2,1,0:T(8,128)(2,1)S(1)} collective-permute-done((bf16[2,48,1024]{2,1,0:T(8,128)(2,1)S(1)}, bf16[2,48,1024]{2,1,0:T(8,128)(2,1)S(1)}, u32[]{:S(2)}, u32[]{:S(2)}) %collective-permute-start.16) | collective-permute-done | bytes 196640 | tf_op jit(solution)/shard_map/ppermute | solution.py:173
  118.2 1.0 copy-done.4
  122.3 3.6 %collective-permute-done.22 = bf16[32,1024]{1,0:T(8,128)(2,1)S(1)} collective-permute-done((bf16[32,1024]{1,0:T(8,128)(2,1)S(1)}, bf16[32,1024]{1,0:T(8,128)(2,1)S(1)}, u32[]{:S(2)}, u32[]{:S(2)}) %collective-permute-start.22) | collective-permute-done | bytes 65568 | tf_op jit(solution)/shard_map/ppermute | solution.py:48
  (124 shorter events, 25.7 us)
Async XLA Ops:
  7.2 68.1 %copy-start = (bf16[1,352,2048]{2,1,0:T(8,128)(2,1)S(1)}, bf16[1,352,2048]{2,1,0:T(8,128)(2,1)}, u32[]{:S(2)}) copy-start(bf16[1,352,2048]{2,1,0:T(8,128)(2,1)} %param.20) | copy-start | bytes 4325380
  7.2 13.1 %copy-start.7 = (f32[1,64,4]{1,2,0:T(4,128)S(1)}, f32[1,64,4]{1,2,0:T(4,128)}, u32[]{:S(2)}) copy-start(f32[1,64,4]{1,2,0:T(4,128)} %param.22) | copy-start | bytes 3076
  7.2 36.4 %all-gather.2.cloned.1.call-start = ((), (), s32[]{:S(2)}) async-start(), calls=%async_computation | async-start | bytes 2359296 | tf_op jit(solution)/shard_map/all_gather | solution.py:268
  8.2 12.2 %collective-permute-start = (bf16[64,1024]{1,0:T(8,128)(2,1)S(1)}, bf16[64,1024]{1,0:T(8,128)(2,1)S(1)}, u32[]{:S(2)}, u32[]{:S(2)}) collective-permute-start(bf16[64,1024]{1,0:T(8,128)(2,1)S(1)} %get-tuple-element.22), channel_id=1, source_target_pairs={{0,4},{2,6},{4,8},{6,10},{8,12},{10,14},{12,0},{14,2},{1,5},{3,7},... | collective-permute-start | bytes 393224 | tf_op jit(solution)/shard_map/ppermute | solution.py:196
  11.3 11.2 %collective-permute-start.1 = (bf16[64,1024]{1,0:T(8,128)(2,1)S(1)}, bf16[64,1024]{1,0:T(8,128)(2,1)S(1)}, u32[]{:S(2)}, u32[]{:S(2)}) collective-permute-start(bf16[64,1024]{1,0:T(8,128)(2,1)S(1)} %get-tuple-element.22), channel_id=1, source_target_pairs={{0,8},{2,10},{4,12},{6,14},{8,0},{10,2},{12,4},{14,6},{1,9},{3,11}... | collective-permute-start | bytes 393224 | tf_op jit(solution)/shard_map/ppermute | solution.py:196
  13.9 8.6 %collective-permute-start.2 = (bf16[64,1024]{1,0:T(8,128)(2,1)S(1)}, bf16[64,1024]{1,0:T(8,128)(2,1)S(1)}, u32[]{:S(2)}, u32[]{:S(2)}) collective-permute-start(bf16[64,1024]{1,0:T(8,128)(2,1)S(1)} %get-tuple-element.22), channel_id=1, source_target_pairs={{0,12},{2,14},{4,0},{6,2},{8,4},{10,6},{12,8},{14,10},{1,13},{3,15... | collective-permute-start | bytes 393224 | tf_op jit(solution)/shard_map/ppermute | solution.py:196
  22.6 2.0 %collective-permute-start.3 = (bf16[4,64,1024]{2,1,0:T(8,128)(2,1)S(1)}, bf16[4,64,1024]{2,1,0:T(8,128)(2,1)S(1)}, u32[]{:S(2)}, u32[]{:S(2)}) collective-permute-start(bf16[4,64,1024]{2,1,0:T(8,128)(2,1)S(1)} %pad_maximum_fusion.2), channel_id=1, source_target_pairs={{0,2},{2,0},{4,6},{6,4},{8,10},{10,8},{12,14},{14,12},{1,3},{3,1},... | collective-permute-start | bytes 1572872 | tf_op jit(solution)/shard_map/ppermute | solution.py:198
  24.6 1.0 copy-start.3
  28.2 23.5 %copy-start.5 = (bf16[1,32,2048]{2,1,0:T(8,128)(2,1)S(1)}, bf16[1,32,2048]{2,1,0:T(8,128)(2,1)}, u32[]{:S(2)}) copy-start(bf16[1,32,2048]{2,1,0:T(8,128)(2,1)} %param.15) | copy-start | bytes 393220
  45.9 5.9 %copy-start.6 = (f32[2048]{0:T(1024)S(1)}, f32[2048]{0:T(1024)}, u32[]{:S(2)}) copy-start(f32[2048]{0:T(1024)} %param.17) | copy-start | bytes 24580
  46.0 5.7 %collective-permute-start.4 = (bf16[32,2048]{1,0:T(8,128)(2,1)S(1)}, bf16[32,2048]{1,0:T(8,128)(2,1)S(1)}, u32[]{:S(2)}, u32[]{:S(2)}) collective-permute-start(bf16[32,2048]{1,0:T(8,128)(2,1)S(1)} %select_convert_fusion), channel_id=1, source_target_pairs={{0,1},{1,0},{2,3},{3,2},{4,5},{5,4},{6,7},{7,6},{8,9},{9,8},{10,11... | collective-permute-start | bytes 393224 | tf_op jit(solution)/shard_map/ppermute | solution.py:48
  52.0 4.3 %collective-permute-start.5 = (bf16[32,1024]{1,0:T(8,128)(2,1)S(1)}, bf16[32,1024]{1,0:T(8,128)(2,1)S(1)}, u32[]{:S(2)}, u32[]{:S(2)}) collective-permute-start(bf16[32,1024]{1,0:T(8,128)(2,1)S(1)} %get-tuple-element.20), channel_id=1, source_target_pairs={{0,1},{1,0},{2,3},{3,2},{4,5},{5,4},{6,7},{7,6},{8,9},{9,8},{10,11... | collective-permute-start | bytes 196616 | tf_op jit(solution)/shard_map/ppermute | solution.py:48
  57.5 10.9 %copy-start.1 = (bf16[1,2048,352]{1,2,0:T(8,128)(2,1)S(1)}, bf16[1,2048,352]{1,2,0:T(8,128)(2,1)}, u32[]{:S(2)}) copy-start(bf16[1,2048,352]{1,2,0:T(8,128)(2,1)} %param.18) | copy-start | bytes 4325380
  57.5 4.1 %collective-permute-start.6 = (bf16[4,48,1024]{2,1,0:T(8,128)(2,1)}, bf16[4,48,1024]{2,1,0:T(8,128)(2,1)}, u32[]{:S(2)}, u32[]{:S(2)}) collective-permute-start(bf16[4,48,1024]{2,1,0:T(8,128)(2,1)} %bitcast.28), channel_id=1, source_target_pairs={{0,2},{2,0},{4,6},{6,4},{8,10},{10,8},{12,14},{14,12},{1,3},{3,1},... | collective-permute-start | bytes 1179656 | tf_op jit(solution)/shard_map/ppermute | solution.py:135
  60.5 8.3 %copy-start.2 = (bf16[1,2048,352]{1,2,0:T(8,128)(2,1)S(1)}, bf16[1,2048,352]{1,2,0:T(8,128)(2,1)}, u32[]{:S(2)}) copy-start(bf16[1,2048,352]{1,2,0:T(8,128)(2,1)} %param.19) | copy-start | bytes 4325380
  62.7 11.8 %collective-permute-start.7 = (bf16[96,1024]{1,0:T(8,128)(2,1)S(1)}, bf16[96,1024]{1,0:T(8,128)(2,1)S(1)}, u32[]{:S(2)}, u32[]{:S(2)}) collective-permute-start(bf16[96,1024]{1,0:T(8,128)(2,1)S(1)} %bitcast.195), channel_id=1, source_target_pairs={{0,1},{1,0},{2,3},{3,2},{4,5},{5,4},{6,7},{7,6},{8,9},{9,8},{10,11... | collective-permute-start | bytes 589832 | tf_op jit(solution)/shard_map/ppermute | solution.py:48
  64.4 9.7 %collective-permute-start.9 = (bf16[2,48,1024]{2,1,0:T(8,128)(2,1)S(1)}, bf16[2,48,1024]{2,1,0:T(8,128)(2,1)S(1)}, u32[]{:S(2)}, u32[]{:S(2)}) collective-permute-start(bf16[2,48,1024]{2,1,0:T(8,128)(2,1)S(1)} %get-tuple-element.14), channel_id=1, source_target_pairs={{0,4},{2,6},{4,8},{6,10},{8,12},{10,14},{12,0},{14,2},{1,5},{3,7},... | collective-permute-start | bytes 589832 | tf_op jit(solution)/shard_map/ppermute | solution.py:140
  65.0 16.7 %collective-permute-start.13 = (bf16[2,48,1024]{2,1,0:T(8,128)(2,1)S(1)}, bf16[2,48,1024]{2,1,0:T(8,128)(2,1)S(1)}, u32[]{:S(2)}, u32[]{:S(2)}) collective-permute-start(bf16[2,48,1024]{2,1,0:T(8,128)(2,1)S(1)} %get-tuple-element.16), channel_id=1, source_target_pairs={{0,8},{2,10},{4,12},{6,14},{8,0},{10,2},{12,4},{14,6},{1,9},{3,11}... | collective-permute-start | bytes 589832 | tf_op jit(solution)/shard_map/ppermute | solution.py:140
  66.6 15.6 %collective-permute-start.17 = (bf16[2,48,1024]{2,1,0:T(8,128)(2,1)S(1)}, bf16[2,48,1024]{2,1,0:T(8,128)(2,1)S(1)}, u32[]{:S(2)}, u32[]{:S(2)}) collective-permute-start(bf16[2,48,1024]{2,1,0:T(8,128)(2,1)S(1)} %get-tuple-element.15), channel_id=1, source_target_pairs={{0,12},{2,14},{4,0},{6,2},{8,4},{10,6},{12,8},{14,10},{1,13},{3,15... | collective-permute-start | bytes 589832 | tf_op jit(solution)/shard_map/ppermute | solution.py:140
  74.1 9.8 %collective-permute-start.10 = (bf16[96,1024]{1,0:T(8,128)(2,1)S(1)}, bf16[96,1024]{1,0:T(8,128)(2,1)S(1)}, u32[]{:S(2)}, u32[]{:S(2)}) collective-permute-start(bf16[96,1024]{1,0:T(8,128)(2,1)S(1)} %bitcast.226), channel_id=1, source_target_pairs={{0,1},{1,0},{2,3},{3,2},{4,5},{5,4},{6,7},{7,6},{8,9},{9,8},{10,11... | collective-permute-start | bytes 589832 | tf_op jit(solution)/shard_map/ppermute | solution.py:48
  75.6 32.2 %collective-permute-start.8 = (bf16[96,1024]{1,0:T(8,128)(2,1)S(1)}, bf16[96,1024]{1,0:T(8,128)(2,1)S(1)}, u32[]{:S(2)}, u32[]{:S(2)}) collective-permute-start(bf16[96,1024]{1,0:T(8,128)(2,1)S(1)} %convolution_convert_fusion.4), channel_id=1, source_target_pairs={{0,1},{1,0},{2,3},{3,2},{4,5},{5,4},{6,7},{7,6},{8,9},{9,8},{10,11... | collective-permute-start | bytes 589832 | tf_op jit(solution)/shard_map/ppermute | solution.py:48
  81.8 7.8 %collective-permute-start.14 = (bf16[96,1024]{1,0:T(8,128)(2,1)S(1)}, bf16[96,1024]{1,0:T(8,128)(2,1)S(1)}, u32[]{:S(2)}, u32[]{:S(2)}) collective-permute-start(bf16[96,1024]{1,0:T(8,128)(2,1)S(1)} %bitcast.223), channel_id=1, source_target_pairs={{0,1},{1,0},{2,3},{3,2},{4,5},{5,4},{6,7},{7,6},{8,9},{9,8},{10,11... | collective-permute-start | bytes 589832 | tf_op jit(solution)/shard_map/ppermute | solution.py:48
  82.2 11.6 %collective-permute-start.18 = (bf16[96,1024]{1,0:T(8,128)(2,1)S(1)}, bf16[96,1024]{1,0:T(8,128)(2,1)S(1)}, u32[]{:S(2)}, u32[]{:S(2)}) collective-permute-start(bf16[96,1024]{1,0:T(8,128)(2,1)S(1)} %bitcast.220), channel_id=1, source_target_pairs={{0,1},{1,0},{2,3},{3,2},{4,5},{5,4},{6,7},{7,6},{8,9},{9,8},{10,11... | collective-permute-start | bytes 589832 | tf_op jit(solution)/shard_map/ppermute | solution.py:48
  85.6 12.5 %collective-permute-start.11 = (bf16[96,1024]{1,0:T(8,128)(2,1)S(1)}, bf16[96,1024]{1,0:T(8,128)(2,1)S(1)}, u32[]{:S(2)}, u32[]{:S(2)}) collective-permute-start(bf16[96,1024]{1,0:T(8,128)(2,1)S(1)} %convolution_convert_fusion.3), channel_id=1, source_target_pairs={{0,1},{1,0},{2,3},{3,2},{4,5},{5,4},{6,7},{7,6},{8,9},{9,8},{10,11... | collective-permute-start | bytes 589832 | tf_op jit(solution)/shard_map/ppermute | solution.py:48
  91.4 11.3 %collective-permute-start.15 = (bf16[96,1024]{1,0:T(8,128)(2,1)S(1)}, bf16[96,1024]{1,0:T(8,128)(2,1)S(1)}, u32[]{:S(2)}, u32[]{:S(2)}) collective-permute-start(bf16[96,1024]{1,0:T(8,128)(2,1)S(1)} %convolution_convert_fusion.2), channel_id=1, source_target_pairs={{0,1},{1,0},{2,3},{3,2},{4,5},{5,4},{6,7},{7,6},{8,9},{9,8},{10,11... | collective-permute-start | bytes 589832 | tf_op jit(solution)/shard_map/ppermute | solution.py:48
  95.6 11.0 %collective-permute-start.19 = (bf16[96,1024]{1,0:T(8,128)(2,1)S(1)}, bf16[96,1024]{1,0:T(8,128)(2,1)S(1)}, u32[]{:S(2)}, u32[]{:S(2)}) collective-permute-start(bf16[96,1024]{1,0:T(8,128)(2,1)S(1)} %convolution_convert_fusion.1), channel_id=1, source_target_pairs={{0,1},{1,0},{2,3},{3,2},{4,5},{5,4},{6,7},{7,6},{8,9},{9,8},{10,11... | collective-permute-start | bytes 589832 | tf_op jit(solution)/shard_map/ppermute | solution.py:48
  98.3 9.8 %collective-permute-start.12 = (bf16[2,48,1024]{2,1,0:T(8,128)(2,1)S(1)}, bf16[2,48,1024]{2,1,0:T(8,128)(2,1)S(1)}, u32[]{:S(2)}, u32[]{:S(2)}) collective-permute-start(bf16[2,48,1024]{2,1,0:T(8,128)(2,1)S(1)} %bitcast.229), channel_id=1, source_target_pairs={{0,12},{2,14},{4,0},{6,2},{8,4},{10,6},{12,8},{14,10},{1,13},{3,15... | collective-permute-start | bytes 589832 | tf_op jit(solution)/shard_map/ppermute | solution.py:173
  103.0 14.9 %collective-permute-start.16 = (bf16[2,48,1024]{2,1,0:T(8,128)(2,1)S(1)}, bf16[2,48,1024]{2,1,0:T(8,128)(2,1)S(1)}, u32[]{:S(2)}, u32[]{:S(2)}) collective-permute-start(bf16[2,48,1024]{2,1,0:T(8,128)(2,1)S(1)} %bitcast.230), channel_id=1, source_target_pairs={{0,8},{2,10},{4,12},{6,14},{8,0},{10,2},{12,4},{14,6},{1,9},{3,11}... | collective-permute-start | bytes 589832 | tf_op jit(solution)/shard_map/ppermute | solution.py:173
  106.9 11.0 %collective-permute-start.20 = (bf16[2,48,1024]{2,1,0:T(8,128)(2,1)S(1)}, bf16[2,48,1024]{2,1,0:T(8,128)(2,1)S(1)}, u32[]{:S(2)}, u32[]{:S(2)}) collective-permute-start(bf16[2,48,1024]{2,1,0:T(8,128)(2,1)S(1)} %bitcast.231), channel_id=1, source_target_pairs={{0,4},{2,6},{4,8},{6,10},{8,12},{10,14},{12,0},{14,2},{1,5},{3,7},... | collective-permute-start | bytes 589832 | tf_op jit(solution)/shard_map/ppermute | solution.py:173
  117.9 1.2 copy-start.4
  118.1 2.8 %collective-permute-start.21 = (bf16[4,48,1024]{2,1,0:T(8,128)(2,1)S(1)}, bf16[4,48,1024]{2,1,0:T(8,128)(2,1)S(1)}, u32[]{:S(2)}, u32[]{:S(2)}) collective-permute-start(bf16[4,48,1024]{2,1,0:T(8,128)(2,1)S(1)} %get-tuple-element.12), channel_id=1, source_target_pairs={{0,2},{2,0},{4,6},{6,4},{8,10},{10,8},{12,14},{14,12},{1,3},{3,1},... | collective-permute-start | bytes 1179656 | tf_op jit(solution)/shard_map/ppermute | solution.py:175
  121.6 4.3 %collective-permute-start.22 = (bf16[32,1024]{1,0:T(8,128)(2,1)S(1)}, bf16[32,1024]{1,0:T(8,128)(2,1)S(1)}, u32[]{:S(2)}, u32[]{:S(2)}) collective-permute-start(bf16[32,1024]{1,0:T(8,128)(2,1)S(1)} %select_convert_fusion.1), channel_id=1, source_target_pairs={{0,1},{1,0},{2,3},{3,2},{4,5},{5,4},{6,7},{7,6},{8,9},{9,8},{10,11... | collective-permute-start | bytes 196616 | tf_op jit(solution)/shard_map/ppermute | solution.py:48
Sparse Core Ops, SparseCore 0:
  15.4 28.1 all-gather.1

commit v10 on v9

--- a/solution.py
+++ b/solution.py
@@ -19,7 +19,7 @@
     return target * half_block + row_ids % half_block
 
 
-def slot_tables(route_block, weight_block, experts, capacity):
+def slot_tables(route_block, weight_block, experts, capacity, block_of=None):
     tok_here, top_here = route_block.shape
     flat_ids = route_block.reshape(tok_here * top_here)
     hit_table = (flat_ids[:, None] == jnp.arange(experts, dtype=jnp.int32)[None, :]).astype(
@@ -27,7 +27,8 @@
     )
     before = jnp.cumsum(hit_table, axis=0) - hit_table
     slot_rank = jnp.sum(before * hit_table, axis=1)
-    slot_index = flat_ids * capacity + slot_rank
+    blocks = flat_ids if block_of is None else block_of(flat_ids)
+    slot_index = blocks * capacity + slot_rank
     slot_match = (
         jnp.arange(experts * capacity, dtype=jnp.int32)[:, None] == slot_index[None, :]
     ).astype(jnp.float32)
@@ -122,11 +123,8 @@
     n_chip = n_ctx // 2
     my_chip = my_ctx // 2
     my_core = my_ctx % 2
-    chips = (my_chip + jnp.arange(n_chip, dtype=jnp.int32)) % n_chip
-    expert_ids = jnp.concatenate([chips * 2 + my_core, chips * 2 + (1 - my_core)])
-    dispatch_ord = jnp.take(dispatch.reshape(n_ctx, capacity, tok_count), expert_ids, axis=0)
     send_rows = jnp.dot(
-        dispatch_ord.reshape(n_ctx * capacity, tok_count).astype(jnp.bfloat16),
+        dispatch.astype(jnp.bfloat16),
         tokens_cols,
         preferred_element_type=jnp.float32,
     ).astype(jnp.bfloat16)
@@ -174,9 +172,8 @@
     back = jnp.stack(returned)
     partner_res = lax.ppermute(back[:, 1], "ctx", perm=core_swap)
     served = jnp.stack([back[:, 0], partner_res]).reshape(n_ctx * capacity, half_d)
-    combine_ord = jnp.take(combine.reshape(tok_count, n_ctx, capacity), expert_ids, axis=1)
     moe_half = jnp.dot(
-        combine_ord.reshape(tok_count, n_ctx * capacity),
+        combine,
         served.astype(jnp.float32),
         precision=lax.Precision.HIGHEST,
         preferred_element_type=jnp.float32,
@@ -274,12 +271,19 @@
     mean_sq = jnp.mean(stream_f * stream_f, axis=1, keepdims=True)
     normed = (stream_f * lax.rsqrt(mean_sq + EPS) * norm_gain).astype(jnp.bfloat16)
     capacity = min(tok_here, 2 * max(1, 3 * tok_here * TOP // (4 * n_ctx)))
-    dispatch, combine = slot_tables(routes[0], route_weights[0], n_ctx, capacity)
     if lax.axis_size("exp") == 2:
+        n_chip = n_ctx // 2
+
+        def block_of(expert):
+            other_core = (expert % 2 != my_ctx % 2).astype(jnp.int32)
+            return other_core * n_chip + (expert // 2 - my_ctx // 2) % n_chip
+
+        dispatch, combine = slot_tables(routes[0], route_weights[0], n_ctx, capacity, block_of)
         moe_rows = moe_column_halves(
             normed, dispatch, combine, gate_weight[0], up_weight[0], down_weight[0], n_ctx, capacity
         )
     else:
+        dispatch, combine = slot_tables(routes[0], route_weights[0], n_ctx, capacity)
         moe_rows = moe_whole_rows(
             normed, dispatch, combine, gate_weight[0], up_weight[0], down_weight[0], n_ctx, capacity
         )

time: 134 us -> 131 us (0.978)
  local copies, waits for them, and re-layouts: 10.8 us -> 5.63 us
  waiting for transfers between devices: 55.1 us -> 58.7 us
    gather x3 -> x0, local copies, waits for them, and re-layouts: 2.83 us -> none  [the longest x1 2.16 us: moe_column_halves(): jnp.take(combine.reshape(tok_count, n_ctx, capacity), expert_ids, axis=1)]
    ppermute x1, waiting for transfers between devices: 0.01 us -> 2.06 us  [moe_column_halves(): from_partner = lax.ppermute(send_rows[1], 'ctx', perm=core_swap)]
    ppermute x3, waiting for transfers between devices: 9.78 us -> 8.24 us  [moe_column_halves(): returned[shift] = lax.ppermute(summed[idx], 'ctx', perm=perm)]
  transfers between devices with their start and end apart: 24 -> 24, of which waited for: 12 -> 14; matrix products, arithmetic and copies ran while one was open for 17% -> 13% of each run, Pallas kernels for 0% -> 0%
where the time goes in v10:
time: 131 us
  waiting for transfers between devices  58.7 us (45%)
  starting transfers between devices  31.9 us (24%)
  between operations  15.2 us (12%)
  matrix products  13.7 us (10%)
  other arithmetic  5.71 us (4%)
  local copies, waits for them, and re-layouts  5.63 us (4%)
    ppermute x11, waiting for transfers between devices, exp_swap(): return lax.ppermute(x, 'exp', perm=[(0, 1), (1, 0)])  17.5 us
    all_gather x1, waiting for transfers between devices, local(): lax.all_gather(out_weight, 'ctx', axis=0, tiled=True)  16.7 us
    ppermute x11, starting transfers between devices, exp_swap(): return lax.ppermute(x, 'exp', perm=[(0, 1), (1, 0)])  11.4 us
    ppermute x3, starting transfers between devices, moe_column_halves(): returned[shift] = lax.ppermute(summed[idx], 'ctx', perm=perm)  9.49 us
    ppermute x3, waiting for transfers between devices, moe_column_halves(): arrived.append(lax.ppermute(pairs[shift], 'ctx', perm=perm))  9.32 us
    ppermute x3, waiting for transfers between devices, moe_column_halves(): returned[shift] = lax.ppermute(summed[idx], 'ctx', perm=perm)  8.24 us
    ppermute x3, starting transfers between devices, ctx_gather_blocks(): stack.append(lax.ppermute(rows, 'ctx', perm=perm))  7.03 us
    ppermute x3, starting transfers between devices, moe_column_halves(): arrived.append(lax.ppermute(pairs[shift], 'ctx', perm=perm))  3.83 us
  transfers between devices with their start and end apart: 24, of which 14 were waited for; matrix products, arithmetic and copies ran while one was open for 13% of the time, Pallas kernels for 0%

profile of v10, /device:TPU:0, one launch (start us, length us, event | category | flops | bytes accessed | tf_op | source)
XLA Modules:
  0.0 130.8 jit_solution(12973115086316184693)
XLA Ops:
  7.9 0.9 fusion.167
  8.8 3.1 %collective-permute-start = (bf16[64,1024]{1,0:T(8,128)(2,1)S(1)}, bf16[64,1024]{1,0:T(8,128)(2,1)S(1)}, u32[]{:S(2)}, u32[]{:S(2)}) collective-permute-start(bf16[64,1024]{1,0:T(8,128)(2,1)S(1)} %get-tuple-element.22), channel_id=1, source_target_pairs={{0,4},{2,6},{4,8},{6,10},{8,12},{10,14},{12,0},{14,2},{1,5},{3,7},... | collective-permute-start | bytes 393224 | tf_op jit(solution)/shard_map/ppermute | solution.py:193
  11.9 2.6 %collective-permute-start.1 = (bf16[64,1024]{1,0:T(8,128)(2,1)S(1)}, bf16[64,1024]{1,0:T(8,128)(2,1)S(1)}, u32[]{:S(2)}, u32[]{:S(2)}) collective-permute-start(bf16[64,1024]{1,0:T(8,128)(2,1)S(1)} %get-tuple-element.22), channel_id=1, source_target_pairs={{0,8},{2,10},{4,12},{6,14},{8,0},{10,2},{12,4},{14,6},{1,9},{3,11}... | collective-permute-start | bytes 393224 | tf_op jit(solution)/shard_map/ppermute | solution.py:193
  14.5 1.4 %collective-permute-start.2 = (bf16[64,1024]{1,0:T(8,128)(2,1)S(1)}, bf16[64,1024]{1,0:T(8,128)(2,1)S(1)}, u32[]{:S(2)}, u32[]{:S(2)}) collective-permute-start(bf16[64,1024]{1,0:T(8,128)(2,1)S(1)} %get-tuple-element.22), channel_id=1, source_target_pairs={{0,12},{2,14},{4,0},{6,2},{8,4},{10,6},{12,8},{14,10},{1,13},{3,15... | collective-permute-start | bytes 393224 | tf_op jit(solution)/shard_map/ppermute | solution.py:193
  19.8 0.9 constant_dynamic-update-slice_fusion.4
  20.8 2.3 %collective-permute-done.1 = bf16[64,1024]{1,0:T(8,128)(2,1)S(1)} collective-permute-done((bf16[64,1024]{1,0:T(8,128)(2,1)S(1)}, bf16[64,1024]{1,0:T(8,128)(2,1)S(1)}, u32[]{:S(2)}, u32[]{:S(2)}) %collective-permute-start.1) | collective-permute-done | bytes 131104 | tf_op jit(solution)/shard_map/ppermute | solution.py:193
  23.3 1.8 %collective-permute-done.3 = bf16[4,64,1024]{2,1,0:T(8,128)(2,1)S(1)} collective-permute-done((bf16[4,64,1024]{2,1,0:T(8,128)(2,1)S(1)}, bf16[4,64,1024]{2,1,0:T(8,128)(2,1)S(1)}, u32[]{:S(2)}, u32[]{:S(2)}) %collective-permute-start.3) | collective-permute-done | bytes 524320 | tf_op jit(solution)/shard_map/ppermute | solution.py:195
  25.3 0.9 copy-done.3
  27.5 16.7 %all-gather.2.cloned.1.call-done = bf16[2048,512]{1,0:T(8,128)(2,1)} async-done(((bf16[256,512]{1,0:T(8,128)(2,1)}), bf16[2048,512]{1,0:T(8,128)(2,1)}) %all-gather.2.cloned.1.call-update) | async-done | bytes 2097168 | tf_op jit(solution)/shard_map/all_gather | solution.py:265
  44.2 2.3 %fusion.93 = f32[64,2048]{1,0:T(8,128)S(1)} fusion(bf16[2048,512]{1,0:T(8,128)(2,1)} %all-gather.2.cloned.1.call-done, bf16[4,8,8,128]{3,2,1,0:T(8,128)(2,1)S(1)} %fusion.4), kind=kOutput, calls=%fused_computation.144 | convolution fusion | flops 134217728 | bytes 2686976 | tf_op jit(solution)/shard_map/tc,oc->to/dot_general | solution.py:262
  46.6 1.6 %collective-permute-start.4 = (bf16[32,2048]{1,0:T(8,128)(2,1)S(1)}, bf16[32,2048]{1,0:T(8,128)(2,1)S(1)}, u32[]{:S(2)}, u32[]{:S(2)}) collective-permute-start(bf16[32,2048]{1,0:T(8,128)(2,1)S(1)} %select_convert_fusion), channel_id=1, source_target_pairs={{0,1},{1,0},{2,3},{3,2},{4,5},{5,4},{6,7},{7,6},{8,9},{9,8},{10,11... | collective-permute-start | bytes 393224 | tf_op jit(solution)/shard_map/ppermute | solution.py:49
  48.3 4.0 %collective-permute-done.4 = bf16[32,2048]{1,0:T(8,128)(2,1)S(1)} collective-permute-done((bf16[32,2048]{1,0:T(8,128)(2,1)S(1)}, bf16[32,2048]{1,0:T(8,128)(2,1)S(1)}, u32[]{:S(2)}, u32[]{:S(2)}) %collective-permute-start.4) | collective-permute-done | bytes 131104 | tf_op jit(solution)/shard_map/ppermute | solution.py:49
  52.6 1.6 %collective-permute-start.5 = (bf16[32,1024]{1,0:T(8,128)(2,1)S(1)}, bf16[32,1024]{1,0:T(8,128)(2,1)S(1)}, u32[]{:S(2)}, u32[]{:S(2)}) collective-permute-start(bf16[32,1024]{1,0:T(8,128)(2,1)S(1)} %get-tuple-element.20), channel_id=1, source_target_pairs={{0,1},{1,0},{2,3},{3,2},{4,5},{5,4},{6,7},{7,6},{8,9},{9,8},{10,11... | collective-permute-start | bytes 196616 | tf_op jit(solution)/shard_map/ppermute | solution.py:49
  54.4 2.6 %collective-permute-done.5 = bf16[32,1024]{1,0:T(8,128)(2,1)S(1)} collective-permute-done((bf16[32,1024]{1,0:T(8,128)(2,1)S(1)}, bf16[32,1024]{1,0:T(8,128)(2,1)S(1)}, u32[]{:S(2)}, u32[]{:S(2)}) %collective-permute-start.5) | collective-permute-done | bytes 65568 | tf_op jit(solution)/shard_map/ppermute | solution.py:49
  58.2 2.1 %collective-permute-done.6 = bf16[4,48,1024]{2,1,0:T(8,128)(2,1)} collective-permute-done((bf16[4,48,1024]{2,1,0:T(8,128)(2,1)}, bf16[4,48,1024]{2,1,0:T(8,128)(2,1)}, u32[]{:S(2)}, u32[]{:S(2)}) %collective-permute-start.6) | collective-permute-done | bytes 393248 | tf_op jit(solution)/shard_map/ppermute | solution.py:133
  60.2 1.1 fusion.80
  61.4 1.6 %collective-permute-start.7 = (bf16[96,1024]{1,0:T(8,128)(2,1)S(1)}, bf16[96,1024]{1,0:T(8,128)(2,1)S(1)}, u32[]{:S(2)}, u32[]{:S(2)}) collective-permute-start(bf16[96,1024]{1,0:T(8,128)(2,1)S(1)} %bitcast.201), channel_id=1, source_target_pairs={{0,1},{1,0},{2,3},{3,2},{4,5},{5,4},{6,7},{7,6},{8,9},{9,8},{10,11... | collective-permute-start | bytes 589832 | tf_op jit(solution)/shard_map/ppermute | solution.py:49
  62.9 2.2 %collective-permute-start.13 = (bf16[2,48,1024]{2,1,0:T(8,128)(2,1)S(1)}, bf16[2,48,1024]{2,1,0:T(8,128)(2,1)S(1)}, u32[]{:S(2)}, u32[]{:S(2)}) collective-permute-start(bf16[2,48,1024]{2,1,0:T(8,128)(2,1)S(1)} %get-tuple-element.16), channel_id=1, source_target_pairs={{0,8},{2,10},{4,12},{6,14},{8,0},{10,2},{12,4},{14,6},{1,9},{3,11}... | collective-permute-start | bytes 589832 | tf_op jit(solution)/shard_map/ppermute | solution.py:138
  65.1 1.6 %collective-permute-start.17 = (bf16[2,48,1024]{2,1,0:T(8,128)(2,1)S(1)}, bf16[2,48,1024]{2,1,0:T(8,128)(2,1)S(1)}, u32[]{:S(2)}, u32[]{:S(2)}) collective-permute-start(bf16[2,48,1024]{2,1,0:T(8,128)(2,1)S(1)} %get-tuple-element.15), channel_id=1, source_target_pairs={{0,12},{2,14},{4,0},{6,2},{8,4},{10,6},{12,8},{14,10},{1,13},{3,15... | collective-permute-start | bytes 589832 | tf_op jit(solution)/shard_map/ppermute | solution.py:138
  67.5 5.1 %collective-permute-done.9 = bf16[2,48,1024]{2,1,0:T(8,128)(2,1)S(1)} collective-permute-done((bf16[2,48,1024]{2,1,0:T(8,128)(2,1)S(1)}, bf16[2,48,1024]{2,1,0:T(8,128)(2,1)S(1)}, u32[]{:S(2)}, u32[]{:S(2)}) %collective-permute-start.9) | collective-permute-done | bytes 196640 | tf_op jit(solution)/shard_map/ppermute | solution.py:138
  74.2 1.6 %collective-permute-start.8 = (bf16[96,1024]{1,0:T(8,128)(2,1)S(1)}, bf16[96,1024]{1,0:T(8,128)(2,1)S(1)}, u32[]{:S(2)}, u32[]{:S(2)}) collective-permute-start(bf16[96,1024]{1,0:T(8,128)(2,1)S(1)} %convolution_convert_fusion.4), channel_id=1, source_target_pairs={{0,1},{1,0},{2,3},{3,2},{4,5},{5,4},{6,7},{7,6},{8,9},{9,8},{10,11... | collective-permute-start | bytes 589832 | tf_op jit(solution)/shard_map/ppermute | solution.py:49
  75.8 4.2 %collective-permute-done.13 = bf16[2,48,1024]{2,1,0:T(8,128)(2,1)S(1)} collective-permute-done((bf16[2,48,1024]{2,1,0:T(8,128)(2,1)S(1)}, bf16[2,48,1024]{2,1,0:T(8,128)(2,1)S(1)}, u32[]{:S(2)}, u32[]{:S(2)}) %collective-permute-start.13) | collective-permute-done | bytes 196640 | tf_op jit(solution)/shard_map/ppermute | solution.py:138
  80.5 1.5 %collective-permute-start.18 = (bf16[96,1024]{1,0:T(8,128)(2,1)S(1)}, bf16[96,1024]{1,0:T(8,128)(2,1)S(1)}, u32[]{:S(2)}, u32[]{:S(2)}) collective-permute-start(bf16[96,1024]{1,0:T(8,128)(2,1)S(1)} %bitcast.221), channel_id=1, source_target_pairs={{0,1},{1,0},{2,3},{3,2},{4,5},{5,4},{6,7},{7,6},{8,9},{9,8},{10,11... | collective-permute-start | bytes 589832 | tf_op jit(solution)/shard_map/ppermute | solution.py:49
  84.4 3.5 %collective-permute-done.14 = bf16[96,1024]{1,0:T(8,128)(2,1)S(1)} collective-permute-done((bf16[96,1024]{1,0:T(8,128)(2,1)S(1)}, bf16[96,1024]{1,0:T(8,128)(2,1)S(1)}, u32[]{:S(2)}, u32[]{:S(2)}) %collective-permute-start.14) | collective-permute-done | bytes 196640 | tf_op jit(solution)/shard_map/ppermute | solution.py:49
  90.2 1.9 %collective-permute-done.18 = bf16[96,1024]{1,0:T(8,128)(2,1)S(1)} collective-permute-done((bf16[96,1024]{1,0:T(8,128)(2,1)S(1)}, bf16[96,1024]{1,0:T(8,128)(2,1)S(1)}, u32[]{:S(2)}, u32[]{:S(2)}) %collective-permute-start.18) | collective-permute-done | bytes 196640 | tf_op jit(solution)/shard_map/ppermute | solution.py:49
  94.4 1.9 %collective-permute-done.11 = bf16[96,1024]{1,0:T(8,128)(2,1)S(1)} collective-permute-done((bf16[96,1024]{1,0:T(8,128)(2,1)S(1)}, bf16[96,1024]{1,0:T(8,128)(2,1)S(1)}, u32[]{:S(2)}, u32[]{:S(2)}) %collective-permute-start.11) | collective-permute-done | bytes 196640 | tf_op jit(solution)/shard_map/ppermute | solution.py:49
  96.5 3.7 %collective-permute-start.12 = (bf16[2,48,1024]{2,1,0:T(8,128)(2,1)S(1)}, bf16[2,48,1024]{2,1,0:T(8,128)(2,1)S(1)}, u32[]{:S(2)}, u32[]{:S(2)}) collective-permute-start(bf16[2,48,1024]{2,1,0:T(8,128)(2,1)S(1)} %bitcast.230), channel_id=1, source_target_pairs={{0,12},{2,14},{4,0},{6,2},{8,4},{10,6},{12,8},{14,10},{1,13},{3,15... | collective-permute-start | bytes 589832 | tf_op jit(solution)/shard_map/ppermute | solution.py:171
  100.8 3.9 %collective-permute-start.16 = (bf16[2,48,1024]{2,1,0:T(8,128)(2,1)S(1)}, bf16[2,48,1024]{2,1,0:T(8,128)(2,1)S(1)}, u32[]{:S(2)}, u32[]{:S(2)}) collective-permute-start(bf16[2,48,1024]{2,1,0:T(8,128)(2,1)S(1)} %bitcast.231), channel_id=1, source_target_pairs={{0,8},{2,10},{4,12},{6,14},{8,0},{10,2},{12,4},{14,6},{1,9},{3,11}... | collective-permute-start | bytes 589832 | tf_op jit(solution)/shard_map/ppermute | solution.py:171
  105.0 1.8 %collective-permute-start.20 = (bf16[2,48,1024]{2,1,0:T(8,128)(2,1)S(1)}, bf16[2,48,1024]{2,1,0:T(8,128)(2,1)S(1)}, u32[]{:S(2)}, u32[]{:S(2)}) collective-permute-start(bf16[2,48,1024]{2,1,0:T(8,128)(2,1)S(1)} %bitcast.232), channel_id=1, source_target_pairs={{0,4},{2,6},{4,8},{6,10},{8,12},{10,14},{12,0},{14,2},{1,5},{3,7},... | collective-permute-start | bytes 589832 | tf_op jit(solution)/shard_map/ppermute | solution.py:171
  107.1 8.2 %collective-permute-done.16 = bf16[2,48,1024]{2,1,0:T(8,128)(2,1)S(1)} collective-permute-done((bf16[2,48,1024]{2,1,0:T(8,128)(2,1)S(1)}, bf16[2,48,1024]{2,1,0:T(8,128)(2,1)S(1)}, u32[]{:S(2)}, u32[]{:S(2)}) %collective-permute-start.16) | collective-permute-done | bytes 196640 | tf_op jit(solution)/shard_map/ppermute | solution.py:171
  115.6 1.0 copy-done.4
  119.7 3.5 %collective-permute-done.22 = bf16[32,1024]{1,0:T(8,128)(2,1)S(1)} collective-permute-done((bf16[32,1024]{1,0:T(8,128)(2,1)S(1)}, bf16[32,1024]{1,0:T(8,128)(2,1)S(1)}, u32[]{:S(2)}, u32[]{:S(2)}) %collective-permute-start.22) | collective-permute-done | bytes 65568 | tf_op jit(solution)/shard_map/ppermute | solution.py:49
  (112 shorter events, 22.5 us)
Async XLA Ops:
  7.2 66.7 %copy-start = (bf16[1,352,2048]{2,1,0:T(8,128)(2,1)S(1)}, bf16[1,352,2048]{2,1,0:T(8,128)(2,1)}, u32[]{:S(2)}) copy-start(bf16[1,352,2048]{2,1,0:T(8,128)(2,1)} %param.20) | copy-start | bytes 4325380
  7.2 37.1 %all-gather.2.cloned.1.call-start = ((), (), s32[]{:S(2)}) async-start(), calls=%async_computation | async-start | bytes 2359296 | tf_op jit(solution)/shard_map/all_gather | solution.py:265
  8.8 12.0 %collective-permute-start = (bf16[64,1024]{1,0:T(8,128)(2,1)S(1)}, bf16[64,1024]{1,0:T(8,128)(2,1)S(1)}, u32[]{:S(2)}, u32[]{:S(2)}) collective-permute-start(bf16[64,1024]{1,0:T(8,128)(2,1)S(1)} %get-tuple-element.22), channel_id=1, source_target_pairs={{0,4},{2,6},{4,8},{6,10},{8,12},{10,14},{12,0},{14,2},{1,5},{3,7},... | collective-permute-start | bytes 393224 | tf_op jit(solution)/shard_map/ppermute | solution.py:193
  11.9 11.2 %collective-permute-start.1 = (bf16[64,1024]{1,0:T(8,128)(2,1)S(1)}, bf16[64,1024]{1,0:T(8,128)(2,1)S(1)}, u32[]{:S(2)}, u32[]{:S(2)}) collective-permute-start(bf16[64,1024]{1,0:T(8,128)(2,1)S(1)} %get-tuple-element.22), channel_id=1, source_target_pairs={{0,8},{2,10},{4,12},{6,14},{8,0},{10,2},{12,4},{14,6},{1,9},{3,11}... | collective-permute-start | bytes 393224 | tf_op jit(solution)/shard_map/ppermute | solution.py:193
  14.5 8.6 %collective-permute-start.2 = (bf16[64,1024]{1,0:T(8,128)(2,1)S(1)}, bf16[64,1024]{1,0:T(8,128)(2,1)S(1)}, u32[]{:S(2)}, u32[]{:S(2)}) collective-permute-start(bf16[64,1024]{1,0:T(8,128)(2,1)S(1)} %get-tuple-element.22), channel_id=1, source_target_pairs={{0,12},{2,14},{4,0},{6,2},{8,4},{10,6},{12,8},{14,10},{1,13},{3,15... | collective-permute-start | bytes 393224 | tf_op jit(solution)/shard_map/ppermute | solution.py:193
  23.2 2.0 %collective-permute-start.3 = (bf16[4,64,1024]{2,1,0:T(8,128)(2,1)S(1)}, bf16[4,64,1024]{2,1,0:T(8,128)(2,1)S(1)}, u32[]{:S(2)}, u32[]{:S(2)}) collective-permute-start(bf16[4,64,1024]{2,1,0:T(8,128)(2,1)S(1)} %pad_maximum_fusion.2), channel_id=1, source_target_pairs={{0,2},{2,0},{4,6},{6,4},{8,10},{10,8},{12,14},{14,12},{1,3},{3,1},... | collective-permute-start | bytes 1572872 | tf_op jit(solution)/shard_map/ppermute | solution.py:195
  25.2 1.0 copy-start.3
  27.5 24.8 %copy-start.5 = (bf16[1,32,2048]{2,1,0:T(8,128)(2,1)S(1)}, bf16[1,32,2048]{2,1,0:T(8,128)(2,1)}, u32[]{:S(2)}) copy-start(bf16[1,32,2048]{2,1,0:T(8,128)(2,1)} %param.15) | copy-start | bytes 393220
  27.5 25.0 %copy-start.6 = (f32[2048]{0:T(1024)S(1)}, f32[2048]{0:T(1024)}, u32[]{:S(2)}) copy-start(f32[2048]{0:T(1024)} %param.17) | copy-start | bytes 24580
  46.6 7.7 %copy-start.7 = (f32[1,64,4]{1,2,0:T(4,128)S(1)}, f32[1,64,4]{1,2,0:T(4,128)}, u32[]{:S(2)}) copy-start(f32[1,64,4]{1,2,0:T(4,128)} %param.22) | copy-start | bytes 3076
  46.6 5.7 %collective-permute-start.4 = (bf16[32,2048]{1,0:T(8,128)(2,1)S(1)}, bf16[32,2048]{1,0:T(8,128)(2,1)S(1)}, u32[]{:S(2)}, u32[]{:S(2)}) collective-permute-start(bf16[32,2048]{1,0:T(8,128)(2,1)S(1)} %select_convert_fusion), channel_id=1, source_target_pairs={{0,1},{1,0},{2,3},{3,2},{4,5},{5,4},{6,7},{7,6},{8,9},{9,8},{10,11... | collective-permute-start | bytes 393224 | tf_op jit(solution)/shard_map/ppermute | solution.py:49
  52.6 4.3 %collective-permute-start.5 = (bf16[32,1024]{1,0:T(8,128)(2,1)S(1)}, bf16[32,1024]{1,0:T(8,128)(2,1)S(1)}, u32[]{:S(2)}, u32[]{:S(2)}) collective-permute-start(bf16[32,1024]{1,0:T(8,128)(2,1)S(1)} %get-tuple-element.20), channel_id=1, source_target_pairs={{0,1},{1,0},{2,3},{3,2},{4,5},{5,4},{6,7},{7,6},{8,9},{9,8},{10,11... | collective-permute-start | bytes 196616 | tf_op jit(solution)/shard_map/ppermute | solution.py:49
  57.4 9.4 %copy-start.1 = (bf16[1,2048,352]{1,2,0:T(8,128)(2,1)S(1)}, bf16[1,2048,352]{1,2,0:T(8,128)(2,1)}, u32[]{:S(2)}) copy-start(bf16[1,2048,352]{1,2,0:T(8,128)(2,1)} %param.18) | copy-start | bytes 4325380
  58.2 2.1 %collective-permute-start.6 = (bf16[4,48,1024]{2,1,0:T(8,128)(2,1)}, bf16[4,48,1024]{2,1,0:T(8,128)(2,1)}, u32[]{:S(2)}, u32[]{:S(2)}) collective-permute-start(bf16[4,48,1024]{2,1,0:T(8,128)(2,1)} %bitcast.19), channel_id=1, source_target_pairs={{0,2},{2,0},{4,6},{6,4},{8,10},{10,8},{12,14},{14,12},{1,3},{3,1},... | collective-permute-start | bytes 1179656 | tf_op jit(solution)/shard_map/ppermute | solution.py:133
  58.2 8.9 %copy-start.2 = (bf16[1,2048,352]{1,2,0:T(8,128)(2,1)S(1)}, bf16[1,2048,352]{1,2,0:T(8,128)(2,1)}, u32[]{:S(2)}) copy-start(bf16[1,2048,352]{1,2,0:T(8,128)(2,1)} %param.19) | copy-start | bytes 4325380
  61.4 11.8 %collective-permute-start.7 = (bf16[96,1024]{1,0:T(8,128)(2,1)S(1)}, bf16[96,1024]{1,0:T(8,128)(2,1)S(1)}, u32[]{:S(2)}, u32[]{:S(2)}) collective-permute-start(bf16[96,1024]{1,0:T(8,128)(2,1)S(1)} %bitcast.201), channel_id=1, source_target_pairs={{0,1},{1,0},{2,3},{3,2},{4,5},{5,4},{6,7},{7,6},{8,9},{9,8},{10,11... | collective-permute-start | bytes 589832 | tf_op jit(solution)/shard_map/ppermute | solution.py:49
  62.9 9.7 %collective-permute-start.9 = (bf16[2,48,1024]{2,1,0:T(8,128)(2,1)S(1)}, bf16[2,48,1024]{2,1,0:T(8,128)(2,1)S(1)}, u32[]{:S(2)}, u32[]{:S(2)}) collective-permute-start(bf16[2,48,1024]{2,1,0:T(8,128)(2,1)S(1)} %get-tuple-element.14), channel_id=1, source_target_pairs={{0,4},{2,6},{4,8},{6,10},{8,12},{10,14},{12,0},{14,2},{1,5},{3,7},... | collective-permute-start | bytes 589832 | tf_op jit(solution)/shard_map/ppermute | solution.py:138
  62.9 17.0 %collective-permute-start.13 = (bf16[2,48,1024]{2,1,0:T(8,128)(2,1)S(1)}, bf16[2,48,1024]{2,1,0:T(8,128)(2,1)S(1)}, u32[]{:S(2)}, u32[]{:S(2)}) collective-permute-start(bf16[2,48,1024]{2,1,0:T(8,128)(2,1)S(1)} %get-tuple-element.16), channel_id=1, source_target_pairs={{0,8},{2,10},{4,12},{6,14},{8,0},{10,2},{12,4},{14,6},{1,9},{3,11}... | collective-permute-start | bytes 589832 | tf_op jit(solution)/shard_map/ppermute | solution.py:138
  65.1 15.4 %collective-permute-start.17 = (bf16[2,48,1024]{2,1,0:T(8,128)(2,1)S(1)}, bf16[2,48,1024]{2,1,0:T(8,128)(2,1)S(1)}, u32[]{:S(2)}, u32[]{:S(2)}) collective-permute-start(bf16[2,48,1024]{2,1,0:T(8,128)(2,1)S(1)} %get-tuple-element.15), channel_id=1, source_target_pairs={{0,12},{2,14},{4,0},{6,2},{8,4},{10,6},{12,8},{14,10},{1,13},{3,15... | collective-permute-start | bytes 589832 | tf_op jit(solution)/shard_map/ppermute | solution.py:138
  72.6 9.4 %collective-permute-start.10 = (bf16[96,1024]{1,0:T(8,128)(2,1)S(1)}, bf16[96,1024]{1,0:T(8,128)(2,1)S(1)}, u32[]{:S(2)}, u32[]{:S(2)}) collective-permute-start(bf16[96,1024]{1,0:T(8,128)(2,1)S(1)} %bitcast.227), channel_id=1, source_target_pairs={{0,1},{1,0},{2,3},{3,2},{4,5},{5,4},{6,7},{7,6},{8,9},{9,8},{10,11... | collective-permute-start | bytes 589832 | tf_op jit(solution)/shard_map/ppermute | solution.py:49
  74.2 32.6 %collective-permute-start.8 = (bf16[96,1024]{1,0:T(8,128)(2,1)S(1)}, bf16[96,1024]{1,0:T(8,128)(2,1)S(1)}, u32[]{:S(2)}, u32[]{:S(2)}) collective-permute-start(bf16[96,1024]{1,0:T(8,128)(2,1)S(1)} %convolution_convert_fusion.4), channel_id=1, source_target_pairs={{0,1},{1,0},{2,3},{3,2},{4,5},{5,4},{6,7},{7,6},{8,9},{9,8},{10,11... | collective-permute-start | bytes 589832 | tf_op jit(solution)/shard_map/ppermute | solution.py:49
  80.0 7.8 %collective-permute-start.14 = (bf16[96,1024]{1,0:T(8,128)(2,1)S(1)}, bf16[96,1024]{1,0:T(8,128)(2,1)S(1)}, u32[]{:S(2)}, u32[]{:S(2)}) collective-permute-start(bf16[96,1024]{1,0:T(8,128)(2,1)S(1)} %bitcast.224), channel_id=1, source_target_pairs={{0,1},{1,0},{2,3},{3,2},{4,5},{5,4},{6,7},{7,6},{8,9},{9,8},{10,11... | collective-permute-start | bytes 589832 | tf_op jit(solution)/shard_map/ppermute | solution.py:49
  80.5 11.5 %collective-permute-start.18 = (bf16[96,1024]{1,0:T(8,128)(2,1)S(1)}, bf16[96,1024]{1,0:T(8,128)(2,1)S(1)}, u32[]{:S(2)}, u32[]{:S(2)}) collective-permute-start(bf16[96,1024]{1,0:T(8,128)(2,1)S(1)} %bitcast.221), channel_id=1, source_target_pairs={{0,1},{1,0},{2,3},{3,2},{4,5},{5,4},{6,7},{7,6},{8,9},{9,8},{10,11... | collective-permute-start | bytes 589832 | tf_op jit(solution)/shard_map/ppermute | solution.py:49
  83.8 12.5 %collective-permute-start.11 = (bf16[96,1024]{1,0:T(8,128)(2,1)S(1)}, bf16[96,1024]{1,0:T(8,128)(2,1)S(1)}, u32[]{:S(2)}, u32[]{:S(2)}) collective-permute-start(bf16[96,1024]{1,0:T(8,128)(2,1)S(1)} %convolution_convert_fusion.3), channel_id=1, source_target_pairs={{0,1},{1,0},{2,3},{3,2},{4,5},{5,4},{6,7},{7,6},{8,9},{9,8},{10,11... | collective-permute-start | bytes 589832 | tf_op jit(solution)/shard_map/ppermute | solution.py:49
  89.6 10.9 %collective-permute-start.15 = (bf16[96,1024]{1,0:T(8,128)(2,1)S(1)}, bf16[96,1024]{1,0:T(8,128)(2,1)S(1)}, u32[]{:S(2)}, u32[]{:S(2)}) collective-permute-start(bf16[96,1024]{1,0:T(8,128)(2,1)S(1)} %convolution_convert_fusion.2), channel_id=1, source_target_pairs={{0,1},{1,0},{2,3},{3,2},{4,5},{5,4},{6,7},{7,6},{8,9},{9,8},{10,11... | collective-permute-start | bytes 589832 | tf_op jit(solution)/shard_map/ppermute | solution.py:49
  93.8 10.9 %collective-permute-start.19 = (bf16[96,1024]{1,0:T(8,128)(2,1)S(1)}, bf16[96,1024]{1,0:T(8,128)(2,1)S(1)}, u32[]{:S(2)}, u32[]{:S(2)}) collective-permute-start(bf16[96,1024]{1,0:T(8,128)(2,1)S(1)} %convolution_convert_fusion.1), channel_id=1, source_target_pairs={{0,1},{1,0},{2,3},{3,2},{4,5},{5,4},{6,7},{7,6},{8,9},{9,8},{10,11... | collective-permute-start | bytes 589832 | tf_op jit(solution)/shard_map/ppermute | solution.py:49
  96.5 10.6 %collective-permute-start.12 = (bf16[2,48,1024]{2,1,0:T(8,128)(2,1)S(1)}, bf16[2,48,1024]{2,1,0:T(8,128)(2,1)S(1)}, u32[]{:S(2)}, u32[]{:S(2)}) collective-permute-start(bf16[2,48,1024]{2,1,0:T(8,128)(2,1)S(1)} %bitcast.230), channel_id=1, source_target_pairs={{0,12},{2,14},{4,0},{6,2},{8,4},{10,6},{12,8},{14,10},{1,13},{3,15... | collective-permute-start | bytes 589832 | tf_op jit(solution)/shard_map/ppermute | solution.py:171
  100.8 14.6 %collective-permute-start.16 = (bf16[2,48,1024]{2,1,0:T(8,128)(2,1)S(1)}, bf16[2,48,1024]{2,1,0:T(8,128)(2,1)S(1)}, u32[]{:S(2)}, u32[]{:S(2)}) collective-permute-start(bf16[2,48,1024]{2,1,0:T(8,128)(2,1)S(1)} %bitcast.231), channel_id=1, source_target_pairs={{0,8},{2,10},{4,12},{6,14},{8,0},{10,2},{12,4},{14,6},{1,9},{3,11}... | collective-permute-start | bytes 589832 | tf_op jit(solution)/shard_map/ppermute | solution.py:171
  105.0 10.4 %collective-permute-start.20 = (bf16[2,48,1024]{2,1,0:T(8,128)(2,1)S(1)}, bf16[2,48,1024]{2,1,0:T(8,128)(2,1)S(1)}, u32[]{:S(2)}, u32[]{:S(2)}) collective-permute-start(bf16[2,48,1024]{2,1,0:T(8,128)(2,1)S(1)} %bitcast.232), channel_id=1, source_target_pairs={{0,4},{2,6},{4,8},{6,10},{8,12},{10,14},{12,0},{14,2},{1,5},{3,7},... | collective-permute-start | bytes 589832 | tf_op jit(solution)/shard_map/ppermute | solution.py:171
  115.4 1.2 copy-start.4
  115.5 2.8 %collective-permute-start.21 = (bf16[4,48,1024]{2,1,0:T(8,128)(2,1)S(1)}, bf16[4,48,1024]{2,1,0:T(8,128)(2,1)S(1)}, u32[]{:S(2)}, u32[]{:S(2)}) collective-permute-start(bf16[4,48,1024]{2,1,0:T(8,128)(2,1)S(1)} %get-tuple-element.12), channel_id=1, source_target_pairs={{0,2},{2,0},{4,6},{6,4},{8,10},{10,8},{12,14},{14,12},{1,3},{3,1},... | collective-permute-start | bytes 1179656 | tf_op jit(solution)/shard_map/ppermute | solution.py:173
  119.0 4.3 %collective-permute-start.22 = (bf16[32,1024]{1,0:T(8,128)(2,1)S(1)}, bf16[32,1024]{1,0:T(8,128)(2,1)S(1)}, u32[]{:S(2)}, u32[]{:S(2)}) collective-permute-start(bf16[32,1024]{1,0:T(8,128)(2,1)S(1)} %select_convert_fusion.1), channel_id=1, source_target_pairs={{0,1},{1,0},{2,3},{3,2},{4,5},{5,4},{6,7},{7,6},{8,9},{9,8},{10,11... | collective-permute-start | bytes 196616 | tf_op jit(solution)/shard_map/ppermute | solution.py:49
Sparse Core Ops, SparseCore 0:
  9.6 34.5 all-gather.1

commit v11 on v10

--- a/solution.py
+++ b/solution.py
@@ -199,6 +199,17 @@
     return jnp.concatenate([own, partner]), src_ctx
 
 
+def gather_out_weight(weight_rows, n_ctx, my_ctx):
+    if n_ctx % 2:
+        return lax.all_gather(weight_rows, "ctx", axis=0, tiled=True)
+    blocks, _ = ctx_gather_blocks(weight_rows, n_ctx, my_ctx)
+    n_chip = n_ctx // 2
+    ctx_ids = jnp.arange(n_ctx, dtype=jnp.int32)
+    other_core = (ctx_ids % 2 != my_ctx % 2).astype(jnp.int32)
+    block_of = other_core * n_chip + (my_ctx // 2 - ctx_ids // 2) % n_chip
+    return jnp.take(blocks, block_of, axis=0).reshape(n_ctx * weight_rows.shape[0], -1)
+
+
 def local(
     query_states,
     key_states,
@@ -262,7 +273,7 @@
     out_parts = jnp.einsum(
         "tc,oc->to",
         mixed,
-        lax.all_gather(out_weight, "ctx", axis=0, tiled=True),
+        gather_out_weight(out_weight, n_ctx, my_ctx),
         preferred_element_type=jnp.float32,
     )
     head_total = exp_reduce_rows(out_parts)

time: 131 us -> 139 us (1.061)
  between operations: 15.2 us -> 1.9 us
  local copies, waits for them, and re-layouts: 5.63 us -> 15.5 us
  waiting for transfers between devices: 58.7 us -> 67.9 us
  other arithmetic: 5.71 us -> 8.39 us
    ppermute x3 -> x6, waiting for transfers between devices: 2.34 us -> 22.1 us  [ctx_gather_blocks(): stack.append(lax.ppermute(rows, 'ctx', perm=perm))]
    all_gather x1 -> x0, waiting for transfers between devices: 16.7 us -> none  [local(): lax.all_gather(out_weight, 'ctx', axis=0, tiled=True)]
    ppermute x3, starting transfers between devices: 9.49 us -> 0.19 us  [moe_column_halves(): returned[shift] = lax.ppermute(summed[idx], 'ctx', perm=perm)]
    ppermute x11, waiting for transfers between devices: 17.5 us -> 22.6 us  [exp_swap(): return lax.ppermute(x, 'exp', perm=[(0, 1), (1, 0)])]
    unnamed x20 -> x38, local copies, waits for them, and re-layouts: 2.69 us -> 7.17 us
    ppermute x11, starting transfers between devices: 11.4 us -> 15.1 us  [exp_swap(): return lax.ppermute(x, 'exp', perm=[(0, 1), (1, 0)])]
    ppermute x3, waiting for transfers between devices: 9.32 us -> 12 us  [moe_column_halves(): arrived.append(lax.ppermute(pairs[shift], 'ctx', perm=perm))]
    ppermute x3 -> x6, starting transfers between devices: 7.03 us -> 9.55 us  [ctx_gather_blocks(): stack.append(lax.ppermute(rows, 'ctx', perm=perm))]
  transfers between devices with their start and end apart: 24 -> 27, of which waited for: 14 -> 16; matrix products, arithmetic and copies ran while one was open for 13% -> 19% of each run, Pallas kernels for 0% -> 0%
where the time goes in v11:
time: 139 us; the launch traced here: 138 us
  waiting for transfers between devices  67.9 us (49%)
  starting transfers between devices  31.1 us (22%)
  local copies, waits for them, and re-layouts  15.5 us (11%)
  matrix products  13.7 us (10%)
  other arithmetic  8.39 us (6%)
  between operations  1.9 us (1%)
    ppermute x11, waiting for transfers between devices, exp_swap(): return lax.ppermute(x, 'exp', perm=[(0, 1), (1, 0)])  22.6 us
    ppermute x6, waiting for transfers between devices, ctx_gather_blocks(): stack.append(lax.ppermute(rows, 'ctx', perm=perm))  22.1 us
    ppermute x11, starting transfers between devices, exp_swap(): return lax.ppermute(x, 'exp', perm=[(0, 1), (1, 0)])  15.1 us
    ppermute x3, waiting for transfers between devices, moe_column_halves(): arrived.append(lax.ppermute(pairs[shift], 'ctx', perm=perm))  12 us
    ppermute x6, starting transfers between devices, ctx_gather_blocks(): stack.append(lax.ppermute(rows, 'ctx', perm=perm))  9.55 us
    ppermute x3, waiting for transfers between devices, moe_column_halves(): returned[shift] = lax.ppermute(summed[idx], 'ctx', perm=perm)  9.11 us
    unnamed x38, local copies, waits for them, and re-layouts  7.17 us
    ppermute x3, starting transfers between devices, moe_column_halves(): arrived.append(lax.ppermute(pairs[shift], 'ctx', perm=perm))  6.03 us
  transfers between devices with their start and end apart: 27, of which 16 were waited for; matrix products, arithmetic and copies ran while one was open for 19% of the time, Pallas kernels for 0%

profile of v11, /device:TPU:0, one launch (start us, length us, event | category | flops | bytes accessed | tf_op | source)
XLA Modules:
  0.0 138.4 jit_solution(16145827468425138213)
XLA Ops:
  0.7 3.1 %collective-permute-start.4 = (bf16[256,512]{1,0:T(8,128)(2,1)}, bf16[256,512]{1,0:T(8,128)(2,1)S(1)}, u32[]{:S(2)}, u32[]{:S(2)}) collective-permute-start(bf16[256,512]{1,0:T(8,128)(2,1)} %param.16), channel_id=1, source_target_pairs={{0,4},{2,6},{4,8},{6,10},{8,12},{10,14},{12,0},{14,2},{1,5},{3,7},... | collective-permute-start | bytes 786440 | tf_op jit(solution)/shard_map/ppermute | solution.py:193
  3.7 2.6 %collective-permute-start.5 = (bf16[256,512]{1,0:T(8,128)(2,1)}, bf16[256,512]{1,0:T(8,128)(2,1)S(1)}, u32[]{:S(2)}, u32[]{:S(2)}) collective-permute-start(bf16[256,512]{1,0:T(8,128)(2,1)} %param.16), channel_id=1, source_target_pairs={{0,8},{2,10},{4,12},{6,14},{8,0},{10,2},{12,4},{14,6},{1,9},{3,11}... | collective-permute-start | bytes 786440 | tf_op jit(solution)/shard_map/ppermute | solution.py:193
  7.4 1.8 %collective-permute-start.1 = (bf16[64,1024]{1,0:T(8,128)(2,1)S(1)}, bf16[64,1024]{1,0:T(8,128)(2,1)S(1)}, u32[]{:S(2)}, u32[]{:S(2)}) collective-permute-start(bf16[64,1024]{1,0:T(8,128)(2,1)S(1)} %get-tuple-element.22), channel_id=1, source_target_pairs={{0,8},{2,10},{4,12},{6,14},{8,0},{10,2},{12,4},{14,6},{1,9},{3,11}... | collective-permute-start | bytes 393224 | tf_op jit(solution)/shard_map/ppermute | solution.py:193
  9.2 1.9 %collective-permute-start.2 = (bf16[64,1024]{1,0:T(8,128)(2,1)S(1)}, bf16[64,1024]{1,0:T(8,128)(2,1)S(1)}, u32[]{:S(2)}, u32[]{:S(2)}) collective-permute-start(bf16[64,1024]{1,0:T(8,128)(2,1)S(1)} %get-tuple-element.22), channel_id=1, source_target_pairs={{0,12},{2,14},{4,0},{6,2},{8,4},{10,6},{12,8},{14,10},{1,13},{3,15... | collective-permute-start | bytes 393224 | tf_op jit(solution)/shard_map/ppermute | solution.py:193
  12.1 1.7 %constant_dynamic-update-slice_fusion.9 = bf16[8,256,512]{2,1,0:T(8,128)(2,1)} fusion(bf16[256,512]{1,0:T(8,128)(2,1)} %param.16), kind=kLoop, calls=%fused_computation.186 | loop fusion | bytes 524288
  17.1 1.5 %reshape_squeeze.9 = bf16[64,4,128]{2,1,0:T(4,128)(2,1)} reshape(bf16[1,64,512]{2,1,0:T(8,128)(2,1)} %param.12) | data formatting | bytes 131072 | tf_op jit(solution)/shard_map/reshape;squeeze | solution.py:238
  19.5 2.1 %collective-permute-done = bf16[64,1024]{1,0:T(8,128)(2,1)S(1)} collective-permute-done((bf16[64,1024]{1,0:T(8,128)(2,1)S(1)}, bf16[64,1024]{1,0:T(8,128)(2,1)S(1)}, u32[]{:S(2)}, u32[]{:S(2)}) %collective-permute-start) | collective-permute-done | bytes 131104 | tf_op jit(solution)/shard_map/ppermute | solution.py:193
  21.6 10.4 %collective-permute-done.1 = bf16[64,1024]{1,0:T(8,128)(2,1)S(1)} collective-permute-done((bf16[64,1024]{1,0:T(8,128)(2,1)S(1)}, bf16[64,1024]{1,0:T(8,128)(2,1)S(1)}, u32[]{:S(2)}, u32[]{:S(2)}) %collective-permute-start.1) | collective-permute-done | bytes 131104 | tf_op jit(solution)/shard_map/ppermute | solution.py:193
  32.3 9.6 %collective-permute-done.6 = bf16[256,512]{1,0:T(8,128)(2,1)S(1)} collective-permute-done((bf16[256,512]{1,0:T(8,128)(2,1)S(1)}, bf16[256,512]{1,0:T(8,128)(2,1)S(1)}, u32[]{:S(2)}, u32[]{:S(2)}) %collective-permute-start.6) | collective-permute-done | bytes 262176 | tf_op jit(solution)/shard_map/ppermute | solution.py:193
  51.7 2.3 %gather_fusion = bf16[8,256,512]{2,1,0:T(8,128)(2,1)S(1)} fusion(bf16[8,256,512]{2,1,0:T(8,128)(2,1)} %constant_dynamic-update-slice_fusion.5, s32[1024]{0:T(1024)S(1)} %pad_clamp_fusion), kind=kCustom, calls=%fused_computation | custom fusion | bytes 4194336 | tf_op jit(solution)/shard_map/jit(_take)/gather | solution.py:210
  55.6 1.6 %collective-permute-start.8 = (bf16[32,2048]{1,0:T(8,128)(2,1)S(1)}, bf16[32,2048]{1,0:T(8,128)(2,1)S(1)}, u32[]{:S(2)}, u32[]{:S(2)}) collective-permute-start(bf16[32,2048]{1,0:T(8,128)(2,1)S(1)} %select_convert_fusion), channel_id=1, source_target_pairs={{0,1},{1,0},{2,3},{3,2},{4,5},{5,4},{6,7},{7,6},{8,9},{9,8},{10,11... | collective-permute-start | bytes 393224 | tf_op jit(solution)/shard_map/ppermute | solution.py:49
  57.4 4.3 %collective-permute-done.8 = bf16[32,2048]{1,0:T(8,128)(2,1)S(1)} collective-permute-done((bf16[32,2048]{1,0:T(8,128)(2,1)S(1)}, bf16[32,2048]{1,0:T(8,128)(2,1)S(1)}, u32[]{:S(2)}, u32[]{:S(2)}) %collective-permute-start.8) | collective-permute-done | bytes 131104 | tf_op jit(solution)/shard_map/ppermute | solution.py:49
  61.9 1.6 %collective-permute-start.9 = (bf16[32,1024]{1,0:T(8,128)(2,1)S(1)}, bf16[32,1024]{1,0:T(8,128)(2,1)S(1)}, u32[]{:S(2)}, u32[]{:S(2)}) collective-permute-start(bf16[32,1024]{1,0:T(8,128)(2,1)S(1)} %get-tuple-element.20), channel_id=1, source_target_pairs={{0,1},{1,0},{2,3},{3,2},{4,5},{5,4},{6,7},{7,6},{8,9},{9,8},{10,11... | collective-permute-start | bytes 196616 | tf_op jit(solution)/shard_map/ppermute | solution.py:49
  63.7 2.6 %collective-permute-done.9 = bf16[32,1024]{1,0:T(8,128)(2,1)S(1)} collective-permute-done((bf16[32,1024]{1,0:T(8,128)(2,1)S(1)}, bf16[32,1024]{1,0:T(8,128)(2,1)S(1)}, u32[]{:S(2)}, u32[]{:S(2)}) %collective-permute-start.9) | collective-permute-done | bytes 65568 | tf_op jit(solution)/shard_map/ppermute | solution.py:49
  67.5 2.1 %collective-permute-done.10 = bf16[4,48,1024]{2,1,0:T(8,128)(2,1)} collective-permute-done((bf16[4,48,1024]{2,1,0:T(8,128)(2,1)}, bf16[4,48,1024]{2,1,0:T(8,128)(2,1)}, u32[]{:S(2)}, u32[]{:S(2)}) %collective-permute-start.10) | collective-permute-done | bytes 393248 | tf_op jit(solution)/shard_map/ppermute | solution.py:133
  70.6 3.0 %collective-permute-start.21 = (bf16[2,48,1024]{2,1,0:T(8,128)(2,1)S(1)}, bf16[2,48,1024]{2,1,0:T(8,128)(2,1)S(1)}, u32[]{:S(2)}, u32[]{:S(2)}) collective-permute-start(bf16[2,48,1024]{2,1,0:T(8,128)(2,1)S(1)} %get-tuple-element.15), channel_id=1, source_target_pairs={{0,12},{2,14},{4,0},{6,2},{8,4},{10,6},{12,8},{14,10},{1,13},{3,15... | collective-permute-start | bytes 589832 | tf_op jit(solution)/shard_map/ppermute | solution.py:138
  74.7 1.9 %collective-permute-start.13 = (bf16[2,48,1024]{2,1,0:T(8,128)(2,1)S(1)}, bf16[2,48,1024]{2,1,0:T(8,128)(2,1)S(1)}, u32[]{:S(2)}, u32[]{:S(2)}) collective-permute-start(bf16[2,48,1024]{2,1,0:T(8,128)(2,1)S(1)} %get-tuple-element.14), channel_id=1, source_target_pairs={{0,4},{2,6},{4,8},{6,10},{8,12},{10,14},{12,0},{14,2},{1,5},{3,7},... | collective-permute-start | bytes 589832 | tf_op jit(solution)/shard_map/ppermute | solution.py:138
  76.7 1.5 %collective-permute-start.11 = (bf16[96,1024]{1,0:T(8,128)(2,1)S(1)}, bf16[96,1024]{1,0:T(8,128)(2,1)S(1)}, u32[]{:S(2)}, u32[]{:S(2)}) collective-permute-start(bf16[96,1024]{1,0:T(8,128)(2,1)S(1)} %bitcast.213), channel_id=1, source_target_pairs={{0,1},{1,0},{2,3},{3,2},{4,5},{5,4},{6,7},{7,6},{8,9},{9,8},{10,11... | collective-permute-start | bytes 589832 | tf_op jit(solution)/shard_map/ppermute | solution.py:49
  79.0 1.5 %collective-permute-start.22 = (bf16[96,1024]{1,0:T(8,128)(2,1)S(1)}, bf16[96,1024]{1,0:T(8,128)(2,1)S(1)}, u32[]{:S(2)}, u32[]{:S(2)}) collective-permute-start(bf16[96,1024]{1,0:T(8,128)(2,1)S(1)} %bitcast.243), channel_id=1, source_target_pairs={{0,1},{1,0},{2,3},{3,2},{4,5},{5,4},{6,7},{7,6},{8,9},{9,8},{10,11... | collective-permute-start | bytes 589832 | tf_op jit(solution)/shard_map/ppermute | solution.py:49
  80.5 12.0 %collective-permute-done.17 = bf16[2,48,1024]{2,1,0:T(8,128)(2,1)S(1)} collective-permute-done((bf16[2,48,1024]{2,1,0:T(8,128)(2,1)S(1)}, bf16[2,48,1024]{2,1,0:T(8,128)(2,1)S(1)}, u32[]{:S(2)}, u32[]{:S(2)}) %collective-permute-start.17) | collective-permute-done | bytes 196640 | tf_op jit(solution)/shard_map/ppermute | solution.py:138
  92.5 1.5 %collective-permute-start.18 = (bf16[96,1024]{1,0:T(8,128)(2,1)S(1)}, bf16[96,1024]{1,0:T(8,128)(2,1)S(1)}, u32[]{:S(2)}, u32[]{:S(2)}) collective-permute-start(bf16[96,1024]{1,0:T(8,128)(2,1)S(1)} %bitcast.240), channel_id=1, source_target_pairs={{0,1},{1,0},{2,3},{3,2},{4,5},{5,4},{6,7},{7,6},{8,9},{9,8},{10,11... | collective-permute-start | bytes 589832 | tf_op jit(solution)/shard_map/ppermute | solution.py:49
  95.6 1.6 %collective-permute-start.12 = (bf16[96,1024]{1,0:T(8,128)(2,1)S(1)}, bf16[96,1024]{1,0:T(8,128)(2,1)S(1)}, u32[]{:S(2)}, u32[]{:S(2)}) collective-permute-start(bf16[96,1024]{1,0:T(8,128)(2,1)S(1)} %convolution_convert_fusion.4), channel_id=1, source_target_pairs={{0,1},{1,0},{2,3},{3,2},{4,5},{5,4},{6,7},{7,6},{8,9},{9,8},{10,11... | collective-permute-start | bytes 589832 | tf_op jit(solution)/shard_map/ppermute | solution.py:49
  102.1 1.6 %collective-permute-start.19 = (bf16[96,1024]{1,0:T(8,128)(2,1)S(1)}, bf16[96,1024]{1,0:T(8,128)(2,1)S(1)}, u32[]{:S(2)}, u32[]{:S(2)}) collective-permute-start(bf16[96,1024]{1,0:T(8,128)(2,1)S(1)} %convolution_convert_fusion.2), channel_id=1, source_target_pairs={{0,1},{1,0},{2,3},{3,2},{4,5},{5,4},{6,7},{7,6},{8,9},{9,8},{10,11... | collective-permute-start | bytes 589832 | tf_op jit(solution)/shard_map/ppermute | solution.py:49
  106.3 1.6 %collective-permute-start.15 = (bf16[96,1024]{1,0:T(8,128)(2,1)S(1)}, bf16[96,1024]{1,0:T(8,128)(2,1)S(1)}, u32[]{:S(2)}, u32[]{:S(2)}) collective-permute-start(bf16[96,1024]{1,0:T(8,128)(2,1)S(1)} %convolution_convert_fusion.3), channel_id=1, source_target_pairs={{0,1},{1,0},{2,3},{3,2},{4,5},{5,4},{6,7},{7,6},{8,9},{9,8},{10,11... | collective-permute-start | bytes 589832 | tf_op jit(solution)/shard_map/ppermute | solution.py:49
  107.9 5.1 %collective-permute-done.23 = bf16[96,1024]{1,0:T(8,128)(2,1)S(1)} collective-permute-done((bf16[96,1024]{1,0:T(8,128)(2,1)S(1)}, bf16[96,1024]{1,0:T(8,128)(2,1)S(1)}, u32[]{:S(2)}, u32[]{:S(2)}) %collective-permute-start.23) | collective-permute-done | bytes 196640 | tf_op jit(solution)/shard_map/ppermute | solution.py:49
  113.3 3.8 %collective-permute-done.19 = bf16[96,1024]{1,0:T(8,128)(2,1)S(1)} collective-permute-done((bf16[96,1024]{1,0:T(8,128)(2,1)S(1)}, bf16[96,1024]{1,0:T(8,128)(2,1)S(1)}, u32[]{:S(2)}, u32[]{:S(2)}) %collective-permute-start.19) | collective-permute-done | bytes 196640 | tf_op jit(solution)/shard_map/ppermute | solution.py:49
  117.5 2.5 %collective-permute-done.15 = bf16[96,1024]{1,0:T(8,128)(2,1)S(1)} collective-permute-done((bf16[96,1024]{1,0:T(8,128)(2,1)S(1)}, bf16[96,1024]{1,0:T(8,128)(2,1)S(1)}, u32[]{:S(2)}, u32[]{:S(2)}) %collective-permute-start.15) | collective-permute-done | bytes 196640 | tf_op jit(solution)/shard_map/ppermute | solution.py:49
  120.7 1.4 %collective-permute-done.24 = bf16[2,48,1024]{2,1,0:T(8,128)(2,1)S(1)} collective-permute-done((bf16[2,48,1024]{2,1,0:T(8,128)(2,1)S(1)}, bf16[2,48,1024]{2,1,0:T(8,128)(2,1)S(1)}, u32[]{:S(2)}, u32[]{:S(2)}) %collective-permute-start.24) | collective-permute-done | bytes 196640 | tf_op jit(solution)/shard_map/ppermute | solution.py:171
  122.1 6.3 %collective-permute-done.20 = bf16[2,48,1024]{2,1,0:T(8,128)(2,1)S(1)} collective-permute-done((bf16[2,48,1024]{2,1,0:T(8,128)(2,1)S(1)}, bf16[2,48,1024]{2,1,0:T(8,128)(2,1)S(1)}, u32[]{:S(2)}, u32[]{:S(2)}) %collective-permute-start.20) | collective-permute-done | bytes 196640 | tf_op jit(solution)/shard_map/ppermute | solution.py:171
  128.4 1.3 collective-permute-done.16
  133.4 1.6 %collective-permute-start.26 = (bf16[32,1024]{1,0:T(8,128)(2,1)S(1)}, bf16[32,1024]{1,0:T(8,128)(2,1)S(1)}, u32[]{:S(2)}, u32[]{:S(2)}) collective-permute-start(bf16[32,1024]{1,0:T(8,128)(2,1)S(1)} %select_convert_fusion.1), channel_id=1, source_target_pairs={{0,1},{1,0},{2,3},{3,2},{4,5},{5,4},{6,7},{7,6},{8,9},{9,8},{10,11... | collective-permute-start | bytes 196616 | tf_op jit(solution)/shard_map/ppermute | solution.py:49
  135.0 2.7 %collective-permute-done.26 = bf16[32,1024]{1,0:T(8,128)(2,1)S(1)} collective-permute-done((bf16[32,1024]{1,0:T(8,128)(2,1)S(1)}, bf16[32,1024]{1,0:T(8,128)(2,1)S(1)}, u32[]{:S(2)}, u32[]{:S(2)}) %collective-permute-start.26) | collective-permute-done | bytes 65568 | tf_op jit(solution)/shard_map/ppermute | solution.py:49
  (142 shorter events, 36.5 us)
Async XLA Ops:
  0.6 94.6 %copy-start = (bf16[1,352,2048]{2,1,0:T(8,128)(2,1)S(1)}, bf16[1,352,2048]{2,1,0:T(8,128)(2,1)}, u32[]{:S(2)}) copy-start(bf16[1,352,2048]{2,1,0:T(8,128)(2,1)} %param.20) | copy-start | bytes 4325380
  0.6 21.0 %copy-start.5 = (bf16[256,512]{1,0:T(8,128)(2,1)S(1)}, bf16[256,512]{1,0:T(8,128)(2,1)}, u32[]{:S(2)}) copy-start(bf16[256,512]{1,0:T(8,128)(2,1)} %param.16) | copy-start | bytes 786436
  0.7 31.6 %collective-permute-start.4 = (bf16[256,512]{1,0:T(8,128)(2,1)}, bf16[256,512]{1,0:T(8,128)(2,1)S(1)}, u32[]{:S(2)}, u32[]{:S(2)}) collective-permute-start(bf16[256,512]{1,0:T(8,128)(2,1)} %param.16), channel_id=1, source_target_pairs={{0,4},{2,6},{4,8},{6,10},{8,12},{10,14},{12,0},{14,2},{1,5},{3,7},... | collective-permute-start | bytes 786440 | tf_op jit(solution)/shard_map/ppermute | solution.py:193
  3.7 28.5 %collective-permute-start.5 = (bf16[256,512]{1,0:T(8,128)(2,1)}, bf16[256,512]{1,0:T(8,128)(2,1)S(1)}, u32[]{:S(2)}, u32[]{:S(2)}) collective-permute-start(bf16[256,512]{1,0:T(8,128)(2,1)} %param.16), channel_id=1, source_target_pairs={{0,8},{2,10},{4,12},{6,14},{8,0},{10,2},{12,4},{14,6},{1,9},{3,11}... | collective-permute-start | bytes 786440 | tf_op jit(solution)/shard_map/ppermute | solution.py:193
  7.2 14.4 %collective-permute-start = (bf16[64,1024]{1,0:T(8,128)(2,1)S(1)}, bf16[64,1024]{1,0:T(8,128)(2,1)S(1)}, u32[]{:S(2)}, u32[]{:S(2)}) collective-permute-start(bf16[64,1024]{1,0:T(8,128)(2,1)S(1)} %get-tuple-element.22), channel_id=1, source_target_pairs={{0,4},{2,6},{4,8},{6,10},{8,12},{10,14},{12,0},{14,2},{1,5},{3,7},... | collective-permute-start | bytes 393224 | tf_op jit(solution)/shard_map/ppermute | solution.py:193
  7.4 24.7 %collective-permute-start.1 = (bf16[64,1024]{1,0:T(8,128)(2,1)S(1)}, bf16[64,1024]{1,0:T(8,128)(2,1)S(1)}, u32[]{:S(2)}, u32[]{:S(2)}) collective-permute-start(bf16[64,1024]{1,0:T(8,128)(2,1)S(1)} %get-tuple-element.22), channel_id=1, source_target_pairs={{0,8},{2,10},{4,12},{6,14},{8,0},{10,2},{12,4},{14,6},{1,9},{3,11}... | collective-permute-start | bytes 393224 | tf_op jit(solution)/shard_map/ppermute | solution.py:193
  9.2 22.9 %collective-permute-start.2 = (bf16[64,1024]{1,0:T(8,128)(2,1)S(1)}, bf16[64,1024]{1,0:T(8,128)(2,1)S(1)}, u32[]{:S(2)}, u32[]{:S(2)}) collective-permute-start(bf16[64,1024]{1,0:T(8,128)(2,1)S(1)} %get-tuple-element.22), channel_id=1, source_target_pairs={{0,12},{2,14},{4,0},{6,2},{8,4},{10,6},{12,8},{14,10},{1,13},{3,15... | collective-permute-start | bytes 393224 | tf_op jit(solution)/shard_map/ppermute | solution.py:193
  21.6 20.2 %collective-permute-start.6 = (bf16[256,512]{1,0:T(8,128)(2,1)S(1)}, bf16[256,512]{1,0:T(8,128)(2,1)S(1)}, u32[]{:S(2)}, u32[]{:S(2)}) collective-permute-start(bf16[256,512]{1,0:T(8,128)(2,1)S(1)} %copy-done.5), channel_id=1, source_target_pairs={{0,12},{2,14},{4,0},{6,2},{8,4},{10,6},{12,8},{14,10},{1,13},{3,15... | collective-permute-start | bytes 786440 | tf_op jit(solution)/shard_map/ppermute | solution.py:193
  32.1 13.0 %collective-permute-start.3 = (bf16[4,64,1024]{2,1,0:T(8,128)(2,1)S(1)}, bf16[4,64,1024]{2,1,0:T(8,128)(2,1)S(1)}, u32[]{:S(2)}, u32[]{:S(2)}) collective-permute-start(bf16[4,64,1024]{2,1,0:T(8,128)(2,1)S(1)} %pad_maximum_fusion.3), channel_id=1, source_target_pairs={{0,2},{2,0},{4,6},{6,4},{8,10},{10,8},{12,14},{14,12},{1,3},{3,1},... | collective-permute-start | bytes 1572872 | tf_op jit(solution)/shard_map/ppermute | solution.py:195
  43.0 7.7 %collective-permute-start.7 = (bf16[4,256,512]{2,1,0:T(8,128)(2,1)}, bf16[4,256,512]{2,1,0:T(8,128)(2,1)S(1)}, u32[]{:S(2)}, u32[]{:S(2)}) collective-permute-start(bf16[4,256,512]{2,1,0:T(8,128)(2,1)} %pad_maximum_fusion), channel_id=1, source_target_pairs={{0,2},{2,0},{4,6},{6,4},{8,10},{10,8},{12,14},{14,12},{1,3},{3,1},... | collective-permute-start | bytes 3145736 | tf_op jit(solution)/shard_map/ppermute | solution.py:195
  55.6 7.9 %copy-start.14 = (f32[1,64,4]{1,2,0:T(4,128)S(1)}, f32[1,64,4]{1,2,0:T(4,128)}, u32[]{:S(2)}) copy-start(f32[1,64,4]{1,2,0:T(4,128)} %param.22) | copy-start | bytes 3076
  55.6 6.0 %collective-permute-start.8 = (bf16[32,2048]{1,0:T(8,128)(2,1)S(1)}, bf16[32,2048]{1,0:T(8,128)(2,1)S(1)}, u32[]{:S(2)}, u32[]{:S(2)}) collective-permute-start(bf16[32,2048]{1,0:T(8,128)(2,1)S(1)} %select_convert_fusion), channel_id=1, source_target_pairs={{0,1},{1,0},{2,3},{3,2},{4,5},{5,4},{6,7},{7,6},{8,9},{9,8},{10,11... | collective-permute-start | bytes 393224 | tf_op jit(solution)/shard_map/ppermute | solution.py:49
  61.9 4.3 %collective-permute-start.9 = (bf16[32,1024]{1,0:T(8,128)(2,1)S(1)}, bf16[32,1024]{1,0:T(8,128)(2,1)S(1)}, u32[]{:S(2)}, u32[]{:S(2)}) collective-permute-start(bf16[32,1024]{1,0:T(8,128)(2,1)S(1)} %get-tuple-element.20), channel_id=1, source_target_pairs={{0,1},{1,0},{2,3},{3,2},{4,5},{5,4},{6,7},{7,6},{8,9},{9,8},{10,11... | collective-permute-start | bytes 196616 | tf_op jit(solution)/shard_map/ppermute | solution.py:49
  66.7 11.5 %copy-start.1 = (bf16[1,2048,352]{1,2,0:T(8,128)(2,1)S(1)}, bf16[1,2048,352]{1,2,0:T(8,128)(2,1)}, u32[]{:S(2)}) copy-start(bf16[1,2048,352]{1,2,0:T(8,128)(2,1)} %param.18) | copy-start | bytes 4325380
  67.5 2.1 %collective-permute-start.10 = (bf16[4,48,1024]{2,1,0:T(8,128)(2,1)}, bf16[4,48,1024]{2,1,0:T(8,128)(2,1)}, u32[]{:S(2)}, u32[]{:S(2)}) collective-permute-start(bf16[4,48,1024]{2,1,0:T(8,128)(2,1)} %bitcast.25), channel_id=1, source_target_pairs={{0,2},{2,0},{4,6},{6,4},{8,10},{10,8},{12,14},{14,12},{1,3},{3,1},... | collective-permute-start | bytes 1179656 | tf_op jit(solution)/shard_map/ppermute | solution.py:133
  67.5 11.1 %copy-start.2 = (bf16[1,2048,352]{1,2,0:T(8,128)(2,1)S(1)}, bf16[1,2048,352]{1,2,0:T(8,128)(2,1)}, u32[]{:S(2)}) copy-start(bf16[1,2048,352]{1,2,0:T(8,128)(2,1)} %param.19) | copy-start | bytes 4325380
  70.6 8.3 %collective-permute-start.21 = (bf16[2,48,1024]{2,1,0:T(8,128)(2,1)S(1)}, bf16[2,48,1024]{2,1,0:T(8,128)(2,1)S(1)}, u32[]{:S(2)}, u32[]{:S(2)}) collective-permute-start(bf16[2,48,1024]{2,1,0:T(8,128)(2,1)S(1)} %get-tuple-element.15), channel_id=1, source_target_pairs={{0,12},{2,14},{4,0},{6,2},{8,4},{10,6},{12,8},{14,10},{1,13},{3,15... | collective-permute-start | bytes 589832 | tf_op jit(solution)/shard_map/ppermute | solution.py:138
  73.6 18.9 %collective-permute-start.17 = (bf16[2,48,1024]{2,1,0:T(8,128)(2,1)S(1)}, bf16[2,48,1024]{2,1,0:T(8,128)(2,1)S(1)}, u32[]{:S(2)}, u32[]{:S(2)}) collective-permute-start(bf16[2,48,1024]{2,1,0:T(8,128)(2,1)S(1)} %get-tuple-element.16), channel_id=1, source_target_pairs={{0,8},{2,10},{4,12},{6,14},{8,0},{10,2},{12,4},{14,6},{1,9},{3,11}... | collective-permute-start | bytes 589832 | tf_op jit(solution)/shard_map/ppermute | solution.py:138
  74.7 19.3 %collective-permute-start.13 = (bf16[2,48,1024]{2,1,0:T(8,128)(2,1)S(1)}, bf16[2,48,1024]{2,1,0:T(8,128)(2,1)S(1)}, u32[]{:S(2)}, u32[]{:S(2)}) collective-permute-start(bf16[2,48,1024]{2,1,0:T(8,128)(2,1)S(1)} %get-tuple-element.14), channel_id=1, source_target_pairs={{0,4},{2,6},{4,8},{6,10},{8,12},{10,14},{12,0},{14,2},{1,5},{3,7},... | collective-permute-start | bytes 589832 | tf_op jit(solution)/shard_map/ppermute | solution.py:138
  76.7 17.8 %collective-permute-start.11 = (bf16[96,1024]{1,0:T(8,128)(2,1)S(1)}, bf16[96,1024]{1,0:T(8,128)(2,1)S(1)}, u32[]{:S(2)}, u32[]{:S(2)}) collective-permute-start(bf16[96,1024]{1,0:T(8,128)(2,1)S(1)} %bitcast.213), channel_id=1, source_target_pairs={{0,1},{1,0},{2,3},{3,2},{4,5},{5,4},{6,7},{7,6},{8,9},{9,8},{10,11... | collective-permute-start | bytes 589832 | tf_op jit(solution)/shard_map/ppermute | solution.py:49
  79.0 18.2 %collective-permute-start.22 = (bf16[96,1024]{1,0:T(8,128)(2,1)S(1)}, bf16[96,1024]{1,0:T(8,128)(2,1)S(1)}, u32[]{:S(2)}, u32[]{:S(2)}) collective-permute-start(bf16[96,1024]{1,0:T(8,128)(2,1)S(1)} %bitcast.243), channel_id=1, source_target_pairs={{0,1},{1,0},{2,3},{3,2},{4,5},{5,4},{6,7},{7,6},{8,9},{9,8},{10,11... | collective-permute-start | bytes 589832 | tf_op jit(solution)/shard_map/ppermute | solution.py:49
  92.5 7.8 %collective-permute-start.18 = (bf16[96,1024]{1,0:T(8,128)(2,1)S(1)}, bf16[96,1024]{1,0:T(8,128)(2,1)S(1)}, u32[]{:S(2)}, u32[]{:S(2)}) collective-permute-start(bf16[96,1024]{1,0:T(8,128)(2,1)S(1)} %bitcast.240), channel_id=1, source_target_pairs={{0,1},{1,0},{2,3},{3,2},{4,5},{5,4},{6,7},{7,6},{8,9},{9,8},{10,11... | collective-permute-start | bytes 589832 | tf_op jit(solution)/shard_map/ppermute | solution.py:49
  94.0 10.5 %collective-permute-start.14 = (bf16[96,1024]{1,0:T(8,128)(2,1)S(1)}, bf16[96,1024]{1,0:T(8,128)(2,1)S(1)}, u32[]{:S(2)}, u32[]{:S(2)}) collective-permute-start(bf16[96,1024]{1,0:T(8,128)(2,1)S(1)} %bitcast.237), channel_id=1, source_target_pairs={{0,1},{1,0},{2,3},{3,2},{4,5},{5,4},{6,7},{7,6},{8,9},{9,8},{10,11... | collective-permute-start | bytes 589832 | tf_op jit(solution)/shard_map/ppermute | solution.py:49
  95.6 24.8 %collective-permute-start.12 = (bf16[96,1024]{1,0:T(8,128)(2,1)S(1)}, bf16[96,1024]{1,0:T(8,128)(2,1)S(1)}, u32[]{:S(2)}, u32[]{:S(2)}) collective-permute-start(bf16[96,1024]{1,0:T(8,128)(2,1)S(1)} %convolution_convert_fusion.4), channel_id=1, source_target_pairs={{0,1},{1,0},{2,3},{3,2},{4,5},{5,4},{6,7},{7,6},{8,9},{9,8},{10,11... | collective-permute-start | bytes 589832 | tf_op jit(solution)/shard_map/ppermute | solution.py:49
  98.9 14.0 %collective-permute-start.23 = (bf16[96,1024]{1,0:T(8,128)(2,1)S(1)}, bf16[96,1024]{1,0:T(8,128)(2,1)S(1)}, u32[]{:S(2)}, u32[]{:S(2)}) collective-permute-start(bf16[96,1024]{1,0:T(8,128)(2,1)S(1)} %convolution_convert_fusion.1), channel_id=1, source_target_pairs={{0,1},{1,0},{2,3},{3,2},{4,5},{5,4},{6,7},{7,6},{8,9},{9,8},{10,11... | collective-permute-start | bytes 589832 | tf_op jit(solution)/shard_map/ppermute | solution.py:49
  102.1 15.1 %collective-permute-start.19 = (bf16[96,1024]{1,0:T(8,128)(2,1)S(1)}, bf16[96,1024]{1,0:T(8,128)(2,1)S(1)}, u32[]{:S(2)}, u32[]{:S(2)}) collective-permute-start(bf16[96,1024]{1,0:T(8,128)(2,1)S(1)} %convolution_convert_fusion.2), channel_id=1, source_target_pairs={{0,1},{1,0},{2,3},{3,2},{4,5},{5,4},{6,7},{7,6},{8,9},{9,8},{10,11... | collective-permute-start | bytes 589832 | tf_op jit(solution)/shard_map/ppermute | solution.py:49
  106.3 13.7 %collective-permute-start.15 = (bf16[96,1024]{1,0:T(8,128)(2,1)S(1)}, bf16[96,1024]{1,0:T(8,128)(2,1)S(1)}, u32[]{:S(2)}, u32[]{:S(2)}) collective-permute-start(bf16[96,1024]{1,0:T(8,128)(2,1)S(1)} %convolution_convert_fusion.3), channel_id=1, source_target_pairs={{0,1},{1,0},{2,3},{3,2},{4,5},{5,4},{6,7},{7,6},{8,9},{9,8},{10,11... | collective-permute-start | bytes 589832 | tf_op jit(solution)/shard_map/ppermute | solution.py:49
  113.2 8.9 %collective-permute-start.24 = (bf16[2,48,1024]{2,1,0:T(8,128)(2,1)S(1)}, bf16[2,48,1024]{2,1,0:T(8,128)(2,1)S(1)}, u32[]{:S(2)}, u32[]{:S(2)}) collective-permute-start(bf16[2,48,1024]{2,1,0:T(8,128)(2,1)S(1)} %bitcast.246), channel_id=1, source_target_pairs={{0,4},{2,6},{4,8},{6,10},{8,12},{10,14},{12,0},{14,2},{1,5},{3,7},... | collective-permute-start | bytes 589832 | tf_op jit(solution)/shard_map/ppermute | solution.py:171
  117.5 11.0 %collective-permute-start.20 = (bf16[2,48,1024]{2,1,0:T(8,128)(2,1)S(1)}, bf16[2,48,1024]{2,1,0:T(8,128)(2,1)S(1)}, u32[]{:S(2)}, u32[]{:S(2)}) collective-permute-start(bf16[2,48,1024]{2,1,0:T(8,128)(2,1)S(1)} %bitcast.247), channel_id=1, source_target_pairs={{0,8},{2,10},{4,12},{6,14},{8,0},{10,2},{12,4},{14,6},{1,9},{3,11}... | collective-permute-start | bytes 589832 | tf_op jit(solution)/shard_map/ppermute | solution.py:171
  120.3 9.5 %collective-permute-start.16 = (bf16[2,48,1024]{2,1,0:T(8,128)(2,1)S(1)}, bf16[2,48,1024]{2,1,0:T(8,128)(2,1)S(1)}, u32[]{:S(2)}, u32[]{:S(2)}) collective-permute-start(bf16[2,48,1024]{2,1,0:T(8,128)(2,1)S(1)} %bitcast.248), channel_id=1, source_target_pairs={{0,12},{2,14},{4,0},{6,2},{8,4},{10,6},{12,8},{14,10},{1,13},{3,15... | collective-permute-start | bytes 589832 | tf_op jit(solution)/shard_map/ppermute | solution.py:171
  129.9 2.8 %collective-permute-start.25 = (bf16[4,48,1024]{2,1,0:T(8,128)(2,1)S(1)}, bf16[4,48,1024]{2,1,0:T(8,128)(2,1)S(1)}, u32[]{:S(2)}, u32[]{:S(2)}) collective-permute-start(bf16[4,48,1024]{2,1,0:T(8,128)(2,1)S(1)} %get-tuple-element.12), channel_id=1, source_target_pairs={{0,2},{2,0},{4,6},{6,4},{8,10},{10,8},{12,14},{14,12},{1,3},{3,1},... | collective-permute-start | bytes 1179656 | tf_op jit(solution)/shard_map/ppermute | solution.py:173
  133.4 4.3 %collective-permute-start.26 = (bf16[32,1024]{1,0:T(8,128)(2,1)S(1)}, bf16[32,1024]{1,0:T(8,128)(2,1)S(1)}, u32[]{:S(2)}, u32[]{:S(2)}) collective-permute-start(bf16[32,1024]{1,0:T(8,128)(2,1)S(1)} %select_convert_fusion.1), channel_id=1, source_target_pairs={{0,1},{1,0},{2,3},{3,2},{4,5},{5,4},{6,7},{7,6},{8,9},{9,8},{10,11... | collective-permute-start | bytes 196616 | tf_op jit(solution)/shard_map/ppermute | solution.py:49
  (10 other events, 33.7 us)

commit v12 on v10

--- a/solution.py
+++ b/solution.py
@@ -199,6 +199,14 @@
     return jnp.concatenate([own, partner]), src_ctx
 
 
+def unrotate_blocks(blocks, n_ctx, my_ctx):
+    n_chip = n_ctx // 2
+    ctx_ids = jnp.arange(n_ctx, dtype=jnp.int32)
+    other_core = (ctx_ids % 2 != my_ctx % 2).astype(jnp.int32)
+    block_of = other_core * n_chip + (my_ctx // 2 - ctx_ids // 2) % n_chip
+    return jnp.take(blocks, block_of, axis=0)
+
+
 def local(
     query_states,
     key_states,
@@ -227,7 +235,13 @@
     query_three = query_states[0].reshape(tok_here, heads_dev, HD)
     run_max = jnp.full((heads_dev, tok_here), NEG, jnp.float32)
     kv_here = jnp.concatenate([key_states[0], value_states[0]], axis=1)
-    kv_blocks, src_ctx = ctx_gather_blocks(kv_here, n_ctx, my_ctx)
+    weight_rows = out_weight.reshape(-1, 2 * feat_width)
+    both_blocks, src_ctx = ctx_gather_blocks(
+        jnp.concatenate([kv_here, weight_rows], axis=0), n_ctx, my_ctx
+    )
+    kv_blocks = both_blocks[:, :tok_here]
+    weight_blocks = both_blocks[:, tok_here:].reshape(n_ctx, out_weight.shape[0], feat_width)
+    weight_all = unrotate_blocks(weight_blocks, n_ctx, my_ctx).reshape(-1, feat_width)
     kv_all = kv_blocks.reshape(n_ctx * tok_here, 2 * feat_width)
     key_two = kv_all[:, :feat_width]
     value_two = kv_all[:, feat_width:]
@@ -262,7 +276,7 @@
     out_parts = jnp.einsum(
         "tc,oc->to",
         mixed,
-        lax.all_gather(out_weight, "ctx", axis=0, tiled=True),
+        weight_all,
         preferred_element_type=jnp.float32,
     )
     head_total = exp_reduce_rows(out_parts)

time: 131 us -> 151 us (1.15)
  local copies, waits for them, and re-layouts: 5.63 us -> 22.2 us
  between operations: 15.2 us -> 1.91 us
  waiting for transfers between devices: 58.7 us -> 69.1 us
  other arithmetic: 5.71 us -> 9.73 us
    ppermute x3, waiting for transfers between devices: 2.34 us -> 22.7 us  [ctx_gather_blocks(): stack.append(lax.ppermute(rows, 'ctx', perm=perm))]
    all_gather x1 -> x0, waiting for transfers between devices: 16.7 us -> none  [local(): lax.all_gather(out_weight, 'ctx', axis=0, tiled=True)]
    ppermute x3, starting transfers between devices: 9.49 us -> 0.37 us  [moe_column_halves(): returned[shift] = lax.ppermute(summed[idx], 'ctx', perm=perm)]
    ppermute x3, starting transfers between devices: 3.83 us -> 10.6 us  [moe_column_halves(): arrived.append(lax.ppermute(pairs[shift], 'ctx', perm=perm))]
    ppermute x11, waiting for transfers between devices: 17.5 us -> 22.1 us  [exp_swap(): return lax.ppermute(x, 'exp', perm=[(0, 1), (1, 0)])]
    ppermute x3, waiting for transfers between devices: 9.32 us -> 13.4 us  [moe_column_halves(): arrived.append(lax.ppermute(pairs[shift], 'ctx', perm=perm))]
    slice x2, local copies, waits for them, and re-layouts: 0.29 us -> 4.33 us  [local(): key_two = kv_all[:, :feat_width]]
    reshape x0 -> x2, local copies, waits for them, and re-layouts: none -> 3.83 us  [the longest x1 2.67 us: local(): both_blocks[:, tok_here:].reshape(n_ctx, out_weight.shape[0], feat_width)]
  transfers between devices with their start and end apart: 24 -> 23, of which waited for: 14 -> 16; matrix products, arithmetic and copies ran while one was open for 13% -> 10% of each run, Pallas kernels for 0% -> 0%
where the time goes in v12:
time: 151 us; the launch traced here: 150 us
  waiting for transfers between devices  69.1 us (46%)
  starting transfers between devices  33.2 us (22%)
  local copies, waits for them, and re-layouts  22.2 us (15%)
  matrix products  13.9 us (9%)
  other arithmetic  9.73 us (6%)
  between operations  1.91 us (1%)
    ppermute x3, waiting for transfers between devices, ctx_gather_blocks(): stack.append(lax.ppermute(rows, 'ctx', perm=perm))  22.7 us
    ppermute x11, waiting for transfers between devices, exp_swap(): return lax.ppermute(x, 'exp', perm=[(0, 1), (1, 0)])  22.1 us
    ppermute x11, starting transfers between devices, exp_swap(): return lax.ppermute(x, 'exp', perm=[(0, 1), (1, 0)])  15.1 us
    ppermute x3, waiting for transfers between devices, moe_column_halves(): arrived.append(lax.ppermute(pairs[shift], 'ctx', perm=perm))  13.4 us
    ppermute x3, starting transfers between devices, moe_column_halves(): arrived.append(lax.ppermute(pairs[shift], 'ctx', perm=perm))  10.6 us
    ppermute x3, waiting for transfers between devices, moe_column_halves(): returned[shift] = lax.ppermute(summed[idx], 'ctx', perm=perm)  8.77 us
    ppermute x3, starting transfers between devices, ctx_gather_blocks(): stack.append(lax.ppermute(rows, 'ctx', perm=perm))  6.96 us
    slice x2, local copies, waits for them, and re-layouts, local(): key_two = kv_all[:, :feat_width]  4.33 us
  transfers between devices with their start and end apart: 23, of which 16 were waited for; matrix products, arithmetic and copies ran while one was open for 10% of the time, Pallas kernels for 0%

profile of v12, /device:TPU:0, one launch (start us, length us, event | category | flops | bytes accessed | tf_op | source)
XLA Modules:
  0.0 150.1 jit_solution(12203410121830596144)
XLA Ops:
  1.8 1.7 %fusion.174 = (bf16[1,192,1024]{2,1,0:T(8,128)(2,1)}, bf16[192,1024]{1,0:T(8,128)(2,1)S(1)}) fusion(bf16[128,1024]{1,0:T(8,128)(2,1)S(1)} %reshape.494, bf16[64,512]{1,0:T(8,128)(2,1)} %bitcast.218, bf16[64,512]{1,0:T(8,128)(2,1)} %bitcast.220), kind=kLoop, calls=%fused_computation.287 | loop fusion | flops 1179648 | bytes 1179648 | tf_op jit(solution)/shard_map/stack | solution.py:194
  3.5 3.0 %collective-permute-start = (bf16[192,1024]{1,0:T(8,128)(2,1)S(1)}, bf16[192,1024]{1,0:T(8,128)(2,1)S(1)}, u32[]{:S(2)}, u32[]{:S(2)}) collective-permute-start(bf16[192,1024]{1,0:T(8,128)(2,1)S(1)} %get-tuple-element.20), channel_id=1, source_target_pairs={{0,4},{2,6},{4,8},{6,10},{8,12},{10,14},{12,0},{14,2},{1,5},{3,7},... | collective-permute-start | bytes 1179656 | tf_op jit(solution)/shard_map/ppermute | solution.py:193
  6.6 2.6 %collective-permute-start.1 = (bf16[192,1024]{1,0:T(8,128)(2,1)S(1)}, bf16[192,1024]{1,0:T(8,128)(2,1)S(1)}, u32[]{:S(2)}, u32[]{:S(2)}) collective-permute-start(bf16[192,1024]{1,0:T(8,128)(2,1)S(1)} %get-tuple-element.20), channel_id=1, source_target_pairs={{0,8},{2,10},{4,12},{6,14},{8,0},{10,2},{12,4},{14,6},{1,9},{3,11}... | collective-permute-start | bytes 1179656 | tf_op jit(solution)/shard_map/ppermute | solution.py:193
  12.0 6.7 %collective-permute-done = bf16[192,1024]{1,0:T(8,128)(2,1)S(1)} collective-permute-done((bf16[192,1024]{1,0:T(8,128)(2,1)S(1)}, bf16[192,1024]{1,0:T(8,128)(2,1)S(1)}, u32[]{:S(2)}, u32[]{:S(2)}) %collective-permute-start) | collective-permute-done | bytes 393248 | tf_op jit(solution)/shard_map/ppermute | solution.py:193
  18.7 16.0 %collective-permute-done.1 = bf16[192,1024]{1,0:T(8,128)(2,1)S(1)} collective-permute-done((bf16[192,1024]{1,0:T(8,128)(2,1)S(1)}, bf16[192,1024]{1,0:T(8,128)(2,1)S(1)}, u32[]{:S(2)}, u32[]{:S(2)}) %collective-permute-start.1) | collective-permute-done | bytes 393248 | tf_op jit(solution)/shard_map/ppermute | solution.py:193
  35.6 1.6 %pad_maximum_fusion = bf16[4,192,1024]{2,1,0:T(8,128)(2,1)S(1)} fusion(bf16[1,192,1024]{2,1,0:T(8,128)(2,1)} %bitcast.213, bf16[1,192,1024]{2,1,0:T(8,128)(2,1)} %bitcast.212, bf16[1,192,1024]{2,1,0:T(8,128)(2,1)} %bitcast.211, bf16[1,192,1024]{2,1,0:T(8,128)(2,1)} %get-tuple-element.19), kind=kLoop, calls=%fused_computation.2 | loop fusion | flops 2359296 | bytes 3145728 | tf_op jit(solution)/shard_map/stack | solution.py:194
  41.3 1.5 %constant_dynamic-update-slice_fusion = bf16[8,192,1024]{2,1,0:T(8,128)(2,1)S(1)} fusion(bf16[8,192,1024]{2,1,0:T(8,128)(2,1)S(1)} %constant_dynamic-update-slice_fusion.1, bf16[4,192,1024]{2,1,0:T(8,128)(2,1)} %collective-permute-done.3), kind=kLoop, calls=%fused_computation.176 | loop fusion | bytes 3145728 | tf_op jit(solution)/shard_map/concatenate | solution.py:199
  45.4 2.7 %reshape.499 = bf16[8,256,512]{2,1,0:T(8,128)(2,1)S(1)} reshape(bf16[8,128,1024]{2,1,0:T(8,128)(2,1)} %slice.87) | data formatting | bytes 4194304 | tf_op jit(solution)/shard_map/reshape | solution.py:243
  48.1 2.3 %fusion.177 = (bf16[512,512]{1,0:T(8,128)(2,1)}, bf16[512,512]{1,0:T(8,128)(2,1)}) fusion(bf16[512,1024]{1,0:T(8,128)(2,1)} %bitcast.203), kind=kLoop, calls=%fused_computation.288 | loop fusion | bytes 2097152 | tf_op jit(solution)/shard_map/slice | solution.py:246
  50.4 2.1 %copy.50 = bf16[512,512]{0,1:T(8,128)(2,1)} copy(bf16[512,512]{1,0:T(8,128)(2,1)} %get-tuple-element.10) | data formatting | bytes 1048576 | tf_op jit(solution)/shard_map/slice | solution.py:247
  52.4 2.1 %copy.47 = bf16[512,512]{0,1:T(8,128)(2,1)} copy(bf16[512,512]{1,0:T(8,128)(2,1)} %get-tuple-element.9) | data formatting | bytes 1048576 | tf_op jit(solution)/shard_map/slice | solution.py:246
  54.5 2.1 %fusion.179 = (f32[4,64]{1,0:T(4,128)S(1)}, f32[4,64,512]{2,1,0:T(8,128)}) fusion(bf16[512,4,128]{0,2,1:T(8,128)(2,1)} %bitcast.207, bf16[64,4,128]{2,1,0:T(4,128)(2,1)} %reshape_squeeze.9, pred[64,512]{1,0:T(8,128)(4,1)} %compare_and_fusion), kind=kOutput, calls=%fused_computation.290 | convolution fusion | flops 33947392 | bytes 1147904 | tf_op jit(solution)/shard_map/qhd,khd->hqk/dot_general | solution.py:258
  56.5 2.0 %gather_fusion = bf16[8,256,512]{2,1,0:T(8,128)(2,1)} fusion(bf16[8,256,512]{2,1,0:T(8,128)(2,1)S(1)} %reshape.499, s32[1024]{0:T(1024)S(1)} %pad_clamp_fusion), kind=kCustom, calls=%fused_computation | custom fusion | bytes 4194336 | tf_op jit(solution)/shard_map/jit(_take)/gather | solution.py:207
  58.6 1.9 %broadcast_select_fusion = bf16[8,256,512]{2,1,0:T(8,128)(2,1)S(1)} fusion(bf16[8,256,512]{2,1,0:T(8,128)(2,1)} %gather_fusion, pred[8]{0:T(512)(128)(4,1)S(1)} %compare_and_fusion.1), kind=kLoop, calls=%fused_computation.1 | loop fusion | flops 1048576 | bytes 4194312 | tf_op jit(solution)/shard_map/jit(_take)/select_n | solution.py:207
  62.0 1.6 %collective-permute-start.4 = (bf16[32,2048]{1,0:T(8,128)(2,1)S(1)}, bf16[32,2048]{1,0:T(8,128)(2,1)S(1)}, u32[]{:S(2)}, u32[]{:S(2)}) collective-permute-start(bf16[32,2048]{1,0:T(8,128)(2,1)S(1)} %select_convert_fusion), channel_id=1, source_target_pairs={{0,1},{1,0},{2,3},{3,2},{4,5},{5,4},{6,7},{7,6},{8,9},{9,8},{10,11... | collective-permute-start | bytes 393224 | tf_op jit(solution)/shard_map/ppermute | solution.py:49
  63.7 4.2 %collective-permute-done.4 = bf16[32,2048]{1,0:T(8,128)(2,1)S(1)} collective-permute-done((bf16[32,2048]{1,0:T(8,128)(2,1)S(1)}, bf16[32,2048]{1,0:T(8,128)(2,1)S(1)}, u32[]{:S(2)}, u32[]{:S(2)}) %collective-permute-start.4) | collective-permute-done | bytes 131104 | tf_op jit(solution)/shard_map/ppermute | solution.py:49
  68.3 1.6 %collective-permute-start.5 = (bf16[32,1024]{1,0:T(8,128)(2,1)S(1)}, bf16[32,1024]{1,0:T(8,128)(2,1)S(1)}, u32[]{:S(2)}, u32[]{:S(2)}) collective-permute-start(bf16[32,1024]{1,0:T(8,128)(2,1)S(1)} %get-tuple-element.22), channel_id=1, source_target_pairs={{0,1},{1,0},{2,3},{3,2},{4,5},{5,4},{6,7},{7,6},{8,9},{9,8},{10,11... | collective-permute-start | bytes 196616 | tf_op jit(solution)/shard_map/ppermute | solution.py:49
  70.0 2.6 %collective-permute-done.5 = bf16[32,1024]{1,0:T(8,128)(2,1)S(1)} collective-permute-done((bf16[32,1024]{1,0:T(8,128)(2,1)S(1)}, bf16[32,1024]{1,0:T(8,128)(2,1)S(1)}, u32[]{:S(2)}, u32[]{:S(2)}) %collective-permute-start.5) | collective-permute-done | bytes 65568 | tf_op jit(solution)/shard_map/ppermute | solution.py:49
  73.8 2.1 %collective-permute-done.6 = bf16[4,48,1024]{2,1,0:T(8,128)(2,1)} collective-permute-done((bf16[4,48,1024]{2,1,0:T(8,128)(2,1)}, bf16[4,48,1024]{2,1,0:T(8,128)(2,1)}, u32[]{:S(2)}, u32[]{:S(2)}) %collective-permute-start.6) | collective-permute-done | bytes 393248 | tf_op jit(solution)/shard_map/ppermute | solution.py:133
  77.0 10.0 %collective-permute-start.17 = (bf16[2,48,1024]{2,1,0:T(8,128)(2,1)S(1)}, bf16[2,48,1024]{2,1,0:T(8,128)(2,1)S(1)}, u32[]{:S(2)}, u32[]{:S(2)}) collective-permute-start(bf16[2,48,1024]{2,1,0:T(8,128)(2,1)S(1)} %get-tuple-element.15), channel_id=1, source_target_pairs={{0,12},{2,14},{4,0},{6,2},{8,4},{10,6},{12,8},{14,10},{1,13},{3,15... | collective-permute-start | bytes 589832 | tf_op jit(solution)/shard_map/ppermute | solution.py:138
  87.6 1.5 %collective-permute-start.7 = (bf16[96,1024]{1,0:T(8,128)(2,1)S(1)}, bf16[96,1024]{1,0:T(8,128)(2,1)S(1)}, u32[]{:S(2)}, u32[]{:S(2)}) collective-permute-start(bf16[96,1024]{1,0:T(8,128)(2,1)S(1)} %bitcast.208), channel_id=1, source_target_pairs={{0,1},{1,0},{2,3},{3,2},{4,5},{5,4},{6,7},{7,6},{8,9},{9,8},{10,11... | collective-permute-start | bytes 589832 | tf_op jit(solution)/shard_map/ppermute | solution.py:49
  89.8 2.4 %collective-permute-done.17 = bf16[2,48,1024]{2,1,0:T(8,128)(2,1)S(1)} collective-permute-done((bf16[2,48,1024]{2,1,0:T(8,128)(2,1)S(1)}, bf16[2,48,1024]{2,1,0:T(8,128)(2,1)S(1)}, u32[]{:S(2)}, u32[]{:S(2)}) %collective-permute-start.17) | collective-permute-done | bytes 196640 | tf_op jit(solution)/shard_map/ppermute | solution.py:138
  93.8 11.0 %collective-permute-done.13 = bf16[2,48,1024]{2,1,0:T(8,128)(2,1)S(1)} collective-permute-done((bf16[2,48,1024]{2,1,0:T(8,128)(2,1)S(1)}, bf16[2,48,1024]{2,1,0:T(8,128)(2,1)S(1)}, u32[]{:S(2)}, u32[]{:S(2)}) %collective-permute-start.13) | collective-permute-done | bytes 196640 | tf_op jit(solution)/shard_map/ppermute | solution.py:138
  107.9 1.6 %collective-permute-start.8 = (bf16[96,1024]{1,0:T(8,128)(2,1)S(1)}, bf16[96,1024]{1,0:T(8,128)(2,1)S(1)}, u32[]{:S(2)}, u32[]{:S(2)}) collective-permute-start(bf16[96,1024]{1,0:T(8,128)(2,1)S(1)} %convolution_convert_fusion.4), channel_id=1, source_target_pairs={{0,1},{1,0},{2,3},{3,2},{4,5},{5,4},{6,7},{7,6},{8,9},{9,8},{10,11... | collective-permute-start | bytes 589832 | tf_op jit(solution)/shard_map/ppermute | solution.py:49
  114.4 1.6 %collective-permute-start.15 = (bf16[96,1024]{1,0:T(8,128)(2,1)S(1)}, bf16[96,1024]{1,0:T(8,128)(2,1)S(1)}, u32[]{:S(2)}, u32[]{:S(2)}) collective-permute-start(bf16[96,1024]{1,0:T(8,128)(2,1)S(1)} %convolution_convert_fusion.2), channel_id=1, source_target_pairs={{0,1},{1,0},{2,3},{3,2},{4,5},{5,4},{6,7},{7,6},{8,9},{9,8},{10,11... | collective-permute-start | bytes 589832 | tf_op jit(solution)/shard_map/ppermute | solution.py:49
  118.7 1.6 %collective-permute-start.11 = (bf16[96,1024]{1,0:T(8,128)(2,1)S(1)}, bf16[96,1024]{1,0:T(8,128)(2,1)S(1)}, u32[]{:S(2)}, u32[]{:S(2)}) collective-permute-start(bf16[96,1024]{1,0:T(8,128)(2,1)S(1)} %convolution_convert_fusion.3), channel_id=1, source_target_pairs={{0,1},{1,0},{2,3},{3,2},{4,5},{5,4},{6,7},{7,6},{8,9},{9,8},{10,11... | collective-permute-start | bytes 589832 | tf_op jit(solution)/shard_map/ppermute | solution.py:49
  120.2 5.1 %collective-permute-done.19 = bf16[96,1024]{1,0:T(8,128)(2,1)S(1)} collective-permute-done((bf16[96,1024]{1,0:T(8,128)(2,1)S(1)}, bf16[96,1024]{1,0:T(8,128)(2,1)S(1)}, u32[]{:S(2)}, u32[]{:S(2)}) %collective-permute-start.19) | collective-permute-done | bytes 196640 | tf_op jit(solution)/shard_map/ppermute | solution.py:49
  125.8 3.7 %collective-permute-done.15 = bf16[96,1024]{1,0:T(8,128)(2,1)S(1)} collective-permute-done((bf16[96,1024]{1,0:T(8,128)(2,1)S(1)}, bf16[96,1024]{1,0:T(8,128)(2,1)S(1)}, u32[]{:S(2)}, u32[]{:S(2)}) %collective-permute-start.15) | collective-permute-done | bytes 196640 | tf_op jit(solution)/shard_map/ppermute | solution.py:49
  129.9 2.1 %collective-permute-done.11 = bf16[96,1024]{1,0:T(8,128)(2,1)S(1)} collective-permute-done((bf16[96,1024]{1,0:T(8,128)(2,1)S(1)}, bf16[96,1024]{1,0:T(8,128)(2,1)S(1)}, u32[]{:S(2)}, u32[]{:S(2)}) %collective-permute-start.11) | collective-permute-done | bytes 196640 | tf_op jit(solution)/shard_map/ppermute | solution.py:49
  133.4 6.8 %collective-permute-done.16 = bf16[2,48,1024]{2,1,0:T(8,128)(2,1)S(1)} collective-permute-done((bf16[2,48,1024]{2,1,0:T(8,128)(2,1)S(1)}, bf16[2,48,1024]{2,1,0:T(8,128)(2,1)S(1)}, u32[]{:S(2)}, u32[]{:S(2)}) %collective-permute-start.16) | collective-permute-done | bytes 196640 | tf_op jit(solution)/shard_map/ppermute | solution.py:171
  145.0 1.6 %collective-permute-start.22 = (bf16[32,1024]{1,0:T(8,128)(2,1)S(1)}, bf16[32,1024]{1,0:T(8,128)(2,1)S(1)}, u32[]{:S(2)}, u32[]{:S(2)}) collective-permute-start(bf16[32,1024]{1,0:T(8,128)(2,1)S(1)} %select_convert_fusion.1), channel_id=1, source_target_pairs={{0,1},{1,0},{2,3},{3,2},{4,5},{5,4},{6,7},{7,6},{8,9},{9,8},{10,11... | collective-permute-start | bytes 196616 | tf_op jit(solution)/shard_map/ppermute | solution.py:49
  146.6 2.7 %collective-permute-done.22 = bf16[32,1024]{1,0:T(8,128)(2,1)S(1)} collective-permute-done((bf16[32,1024]{1,0:T(8,128)(2,1)S(1)}, bf16[32,1024]{1,0:T(8,128)(2,1)S(1)}, u32[]{:S(2)}, u32[]{:S(2)}) %collective-permute-start.22) | collective-permute-done | bytes 65568 | tf_op jit(solution)/shard_map/ppermute | solution.py:49
  (146 shorter events, 36.2 us)
Async XLA Ops:
  0.6 107.0 %copy-start = (bf16[1,352,2048]{2,1,0:T(8,128)(2,1)S(1)}, bf16[1,352,2048]{2,1,0:T(8,128)(2,1)}, u32[]{:S(2)}) copy-start(bf16[1,352,2048]{2,1,0:T(8,128)(2,1)} %param.20) | copy-start | bytes 4325380
  0.6 9.9 %copy-start.21 = (s32[1,64,4]{1,2,0:T(4,128)S(1)}, s32[1,64,4]{1,2,0:T(4,128)}, u32[]{:S(2)}) copy-start(s32[1,64,4]{1,2,0:T(4,128)} %param.21) | copy-start | bytes 3076
  3.5 15.1 %collective-permute-start = (bf16[192,1024]{1,0:T(8,128)(2,1)S(1)}, bf16[192,1024]{1,0:T(8,128)(2,1)S(1)}, u32[]{:S(2)}, u32[]{:S(2)}) collective-permute-start(bf16[192,1024]{1,0:T(8,128)(2,1)S(1)} %get-tuple-element.20), channel_id=1, source_target_pairs={{0,4},{2,6},{4,8},{6,10},{8,12},{10,14},{12,0},{14,2},{1,5},{3,7},... | collective-permute-start | bytes 1179656 | tf_op jit(solution)/shard_map/ppermute | solution.py:193
  6.6 28.1 %collective-permute-start.1 = (bf16[192,1024]{1,0:T(8,128)(2,1)S(1)}, bf16[192,1024]{1,0:T(8,128)(2,1)S(1)}, u32[]{:S(2)}, u32[]{:S(2)}) collective-permute-start(bf16[192,1024]{1,0:T(8,128)(2,1)S(1)} %get-tuple-element.20), channel_id=1, source_target_pairs={{0,8},{2,10},{4,12},{6,14},{8,0},{10,2},{12,4},{14,6},{1,9},{3,11}... | collective-permute-start | bytes 1179656 | tf_op jit(solution)/shard_map/ppermute | solution.py:193
  9.2 25.5 %collective-permute-start.2 = (bf16[192,1024]{1,0:T(8,128)(2,1)S(1)}, bf16[192,1024]{1,0:T(8,128)(2,1)S(1)}, u32[]{:S(2)}, u32[]{:S(2)}) collective-permute-start(bf16[192,1024]{1,0:T(8,128)(2,1)S(1)} %get-tuple-element.20), channel_id=1, source_target_pairs={{0,12},{2,14},{4,0},{6,2},{8,4},{10,6},{12,8},{14,10},{1,13},{3,15... | collective-permute-start | bytes 1179656 | tf_op jit(solution)/shard_map/ppermute | solution.py:193
  10.6 24.1 %copy-start.10 = (s32[1,64,4]{2,1,0:T(8,128)}, s32[1,64,4]{2,1,0:T(8,128)S(1)}, u32[]{:S(2)}) copy-start(s32[1,64,4]{2,1,0:T(8,128)S(1)} %copy.53) | copy-start | bytes 3076
  18.7 16.0 %copy-start.5 = (bf16[192,1024]{1,0:T(8,128)(2,1)}, bf16[192,1024]{1,0:T(8,128)(2,1)S(1)}, u32[]{:S(2)}) copy-start(bf16[192,1024]{1,0:T(8,128)(2,1)S(1)} %collective-permute-done) | copy-start | bytes 1179652
  37.2 4.1 %collective-permute-start.3 = (bf16[4,192,1024]{2,1,0:T(8,128)(2,1)S(1)}, bf16[4,192,1024]{2,1,0:T(8,128)(2,1)}, u32[]{:S(2)}, u32[]{:S(2)}) collective-permute-start(bf16[4,192,1024]{2,1,0:T(8,128)(2,1)S(1)} %pad_maximum_fusion), channel_id=1, source_target_pairs={{0,2},{2,0},{4,6},{6,4},{8,10},{10,8},{12,14},{14,12},{1,3},{3,1},... | collective-permute-start | bytes 4718600 | tf_op jit(solution)/shard_map/ppermute | solution.py:195
  61.2 6.8 %copy-start.17 = (bf16[1,32,2048]{2,1,0:T(8,128)(2,1)S(1)}, bf16[1,32,2048]{2,1,0:T(8,128)(2,1)}, u32[]{:S(2)}) copy-start(bf16[1,32,2048]{2,1,0:T(8,128)(2,1)} %param.15) | copy-start | bytes 393220
  61.2 7.0 %copy-start.19 = (f32[2048]{0:T(1024)S(1)}, f32[2048]{0:T(1024)}, u32[]{:S(2)}) copy-start(f32[2048]{0:T(1024)} %param.17) | copy-start | bytes 24580
  61.9 7.9 %copy-start.20 = (f32[1,64,4]{1,2,0:T(4,128)S(1)}, f32[1,64,4]{1,2,0:T(4,128)}, u32[]{:S(2)}) copy-start(f32[1,64,4]{1,2,0:T(4,128)} %param.22) | copy-start | bytes 3076
  62.0 6.0 %collective-permute-start.4 = (bf16[32,2048]{1,0:T(8,128)(2,1)S(1)}, bf16[32,2048]{1,0:T(8,128)(2,1)S(1)}, u32[]{:S(2)}, u32[]{:S(2)}) collective-permute-start(bf16[32,2048]{1,0:T(8,128)(2,1)S(1)} %select_convert_fusion), channel_id=1, source_target_pairs={{0,1},{1,0},{2,3},{3,2},{4,5},{5,4},{6,7},{7,6},{8,9},{9,8},{10,11... | collective-permute-start | bytes 393224 | tf_op jit(solution)/shard_map/ppermute | solution.py:49
  68.3 4.3 %collective-permute-start.5 = (bf16[32,1024]{1,0:T(8,128)(2,1)S(1)}, bf16[32,1024]{1,0:T(8,128)(2,1)S(1)}, u32[]{:S(2)}, u32[]{:S(2)}) collective-permute-start(bf16[32,1024]{1,0:T(8,128)(2,1)S(1)} %get-tuple-element.22), channel_id=1, source_target_pairs={{0,1},{1,0},{2,3},{3,2},{4,5},{5,4},{6,7},{7,6},{8,9},{9,8},{10,11... | collective-permute-start | bytes 196616 | tf_op jit(solution)/shard_map/ppermute | solution.py:49
  73.0 16.1 %copy-start.1 = (bf16[1,2048,352]{1,2,0:T(8,128)(2,1)S(1)}, bf16[1,2048,352]{1,2,0:T(8,128)(2,1)}, u32[]{:S(2)}) copy-start(bf16[1,2048,352]{1,2,0:T(8,128)(2,1)} %param.18) | copy-start | bytes 4325380
  73.8 2.1 %collective-permute-start.6 = (bf16[4,48,1024]{2,1,0:T(8,128)(2,1)}, bf16[4,48,1024]{2,1,0:T(8,128)(2,1)}, u32[]{:S(2)}, u32[]{:S(2)}) collective-permute-start(bf16[4,48,1024]{2,1,0:T(8,128)(2,1)} %bitcast.21), channel_id=1, source_target_pairs={{0,2},{2,0},{4,6},{6,4},{8,10},{10,8},{12,14},{14,12},{1,3},{3,1},... | collective-permute-start | bytes 1179656 | tf_op jit(solution)/shard_map/ppermute | solution.py:133
  73.8 15.7 %copy-start.2 = (bf16[1,2048,352]{1,2,0:T(8,128)(2,1)S(1)}, bf16[1,2048,352]{1,2,0:T(8,128)(2,1)}, u32[]{:S(2)}) copy-start(bf16[1,2048,352]{1,2,0:T(8,128)(2,1)} %param.19) | copy-start | bytes 4325380
  77.0 15.3 %collective-permute-start.17 = (bf16[2,48,1024]{2,1,0:T(8,128)(2,1)S(1)}, bf16[2,48,1024]{2,1,0:T(8,128)(2,1)S(1)}, u32[]{:S(2)}, u32[]{:S(2)}) collective-permute-start(bf16[2,48,1024]{2,1,0:T(8,128)(2,1)S(1)} %get-tuple-element.15), channel_id=1, source_target_pairs={{0,12},{2,14},{4,0},{6,2},{8,4},{10,6},{12,8},{14,10},{1,13},{3,15... | collective-permute-start | bytes 589832 | tf_op jit(solution)/shard_map/ppermute | solution.py:138
  86.9 17.9 %collective-permute-start.13 = (bf16[2,48,1024]{2,1,0:T(8,128)(2,1)S(1)}, bf16[2,48,1024]{2,1,0:T(8,128)(2,1)S(1)}, u32[]{:S(2)}, u32[]{:S(2)}) collective-permute-start(bf16[2,48,1024]{2,1,0:T(8,128)(2,1)S(1)} %get-tuple-element.16), channel_id=1, source_target_pairs={{0,8},{2,10},{4,12},{6,14},{8,0},{10,2},{12,4},{14,6},{1,9},{3,11}... | collective-permute-start | bytes 589832 | tf_op jit(solution)/shard_map/ppermute | solution.py:138
  87.3 19.1 %collective-permute-start.9 = (bf16[2,48,1024]{2,1,0:T(8,128)(2,1)S(1)}, bf16[2,48,1024]{2,1,0:T(8,128)(2,1)S(1)}, u32[]{:S(2)}, u32[]{:S(2)}) collective-permute-start(bf16[2,48,1024]{2,1,0:T(8,128)(2,1)S(1)} %get-tuple-element.14), channel_id=1, source_target_pairs={{0,4},{2,6},{4,8},{6,10},{8,12},{10,14},{12,0},{14,2},{1,5},{3,7},... | collective-permute-start | bytes 589832 | tf_op jit(solution)/shard_map/ppermute | solution.py:138
  87.6 19.3 %collective-permute-start.7 = (bf16[96,1024]{1,0:T(8,128)(2,1)S(1)}, bf16[96,1024]{1,0:T(8,128)(2,1)S(1)}, u32[]{:S(2)}, u32[]{:S(2)}) collective-permute-start(bf16[96,1024]{1,0:T(8,128)(2,1)S(1)} %bitcast.208), channel_id=1, source_target_pairs={{0,1},{1,0},{2,3},{3,2},{4,5},{5,4},{6,7},{7,6},{8,9},{9,8},{10,11... | collective-permute-start | bytes 589832 | tf_op jit(solution)/shard_map/ppermute | solution.py:49
  92.3 17.2 %collective-permute-start.18 = (bf16[96,1024]{1,0:T(8,128)(2,1)S(1)}, bf16[96,1024]{1,0:T(8,128)(2,1)S(1)}, u32[]{:S(2)}, u32[]{:S(2)}) collective-permute-start(bf16[96,1024]{1,0:T(8,128)(2,1)S(1)} %bitcast.231), channel_id=1, source_target_pairs={{0,1},{1,0},{2,3},{3,2},{4,5},{5,4},{6,7},{7,6},{8,9},{9,8},{10,11... | collective-permute-start | bytes 589832 | tf_op jit(solution)/shard_map/ppermute | solution.py:49
  104.8 7.8 %collective-permute-start.14 = (bf16[96,1024]{1,0:T(8,128)(2,1)S(1)}, bf16[96,1024]{1,0:T(8,128)(2,1)S(1)}, u32[]{:S(2)}, u32[]{:S(2)}) collective-permute-start(bf16[96,1024]{1,0:T(8,128)(2,1)S(1)} %bitcast.228), channel_id=1, source_target_pairs={{0,1},{1,0},{2,3},{3,2},{4,5},{5,4},{6,7},{7,6},{8,9},{9,8},{10,11... | collective-permute-start | bytes 589832 | tf_op jit(solution)/shard_map/ppermute | solution.py:49
  106.3 10.5 %collective-permute-start.10 = (bf16[96,1024]{1,0:T(8,128)(2,1)S(1)}, bf16[96,1024]{1,0:T(8,128)(2,1)S(1)}, u32[]{:S(2)}, u32[]{:S(2)}) collective-permute-start(bf16[96,1024]{1,0:T(8,128)(2,1)S(1)} %bitcast.225), channel_id=1, source_target_pairs={{0,1},{1,0},{2,3},{3,2},{4,5},{5,4},{6,7},{7,6},{8,9},{9,8},{10,11... | collective-permute-start | bytes 589832 | tf_op jit(solution)/shard_map/ppermute | solution.py:49
  107.9 24.5 %collective-permute-start.8 = (bf16[96,1024]{1,0:T(8,128)(2,1)S(1)}, bf16[96,1024]{1,0:T(8,128)(2,1)S(1)}, u32[]{:S(2)}, u32[]{:S(2)}) collective-permute-start(bf16[96,1024]{1,0:T(8,128)(2,1)S(1)} %convolution_convert_fusion.4), channel_id=1, source_target_pairs={{0,1},{1,0},{2,3},{3,2},{4,5},{5,4},{6,7},{7,6},{8,9},{9,8},{10,11... | collective-permute-start | bytes 589832 | tf_op jit(solution)/shard_map/ppermute | solution.py:49
  111.3 14.0 %collective-permute-start.19 = (bf16[96,1024]{1,0:T(8,128)(2,1)S(1)}, bf16[96,1024]{1,0:T(8,128)(2,1)S(1)}, u32[]{:S(2)}, u32[]{:S(2)}) collective-permute-start(bf16[96,1024]{1,0:T(8,128)(2,1)S(1)} %convolution_convert_fusion.1), channel_id=1, source_target_pairs={{0,1},{1,0},{2,3},{3,2},{4,5},{5,4},{6,7},{7,6},{8,9},{9,8},{10,11... | collective-permute-start | bytes 589832 | tf_op jit(solution)/shard_map/ppermute | solution.py:49
  114.4 15.1 %collective-permute-start.15 = (bf16[96,1024]{1,0:T(8,128)(2,1)S(1)}, bf16[96,1024]{1,0:T(8,128)(2,1)S(1)}, u32[]{:S(2)}, u32[]{:S(2)}) collective-permute-start(bf16[96,1024]{1,0:T(8,128)(2,1)S(1)} %convolution_convert_fusion.2), channel_id=1, source_target_pairs={{0,1},{1,0},{2,3},{3,2},{4,5},{5,4},{6,7},{7,6},{8,9},{9,8},{10,11... | collective-permute-start | bytes 589832 | tf_op jit(solution)/shard_map/ppermute | solution.py:49
  118.7 13.4 %collective-permute-start.11 = (bf16[96,1024]{1,0:T(8,128)(2,1)S(1)}, bf16[96,1024]{1,0:T(8,128)(2,1)S(1)}, u32[]{:S(2)}, u32[]{:S(2)}) collective-permute-start(bf16[96,1024]{1,0:T(8,128)(2,1)S(1)} %convolution_convert_fusion.3), channel_id=1, source_target_pairs={{0,1},{1,0},{2,3},{3,2},{4,5},{5,4},{6,7},{7,6},{8,9},{9,8},{10,11... | collective-permute-start | bytes 589832 | tf_op jit(solution)/shard_map/ppermute | solution.py:49
  125.6 7.8 %collective-permute-start.20 = (bf16[2,48,1024]{2,1,0:T(8,128)(2,1)S(1)}, bf16[2,48,1024]{2,1,0:T(8,128)(2,1)S(1)}, u32[]{:S(2)}, u32[]{:S(2)}) collective-permute-start(bf16[2,48,1024]{2,1,0:T(8,128)(2,1)S(1)} %bitcast.234), channel_id=1, source_target_pairs={{0,4},{2,6},{4,8},{6,10},{8,12},{10,14},{12,0},{14,2},{1,5},{3,7},... | collective-permute-start | bytes 589832 | tf_op jit(solution)/shard_map/ppermute | solution.py:171
  129.8 10.5 %collective-permute-start.16 = (bf16[2,48,1024]{2,1,0:T(8,128)(2,1)S(1)}, bf16[2,48,1024]{2,1,0:T(8,128)(2,1)S(1)}, u32[]{:S(2)}, u32[]{:S(2)}) collective-permute-start(bf16[2,48,1024]{2,1,0:T(8,128)(2,1)S(1)} %bitcast.235), channel_id=1, source_target_pairs={{0,8},{2,10},{4,12},{6,14},{8,0},{10,2},{12,4},{14,6},{1,9},{3,11}... | collective-permute-start | bytes 589832 | tf_op jit(solution)/shard_map/ppermute | solution.py:171
  132.3 9.1 %collective-permute-start.12 = (bf16[2,48,1024]{2,1,0:T(8,128)(2,1)S(1)}, bf16[2,48,1024]{2,1,0:T(8,128)(2,1)S(1)}, u32[]{:S(2)}, u32[]{:S(2)}) collective-permute-start(bf16[2,48,1024]{2,1,0:T(8,128)(2,1)S(1)} %bitcast.236), channel_id=1, source_target_pairs={{0,12},{2,14},{4,0},{6,2},{8,4},{10,6},{12,8},{14,10},{1,13},{3,15... | collective-permute-start | bytes 589832 | tf_op jit(solution)/shard_map/ppermute | solution.py:171
  141.6 2.8 %collective-permute-start.21 = (bf16[4,48,1024]{2,1,0:T(8,128)(2,1)S(1)}, bf16[4,48,1024]{2,1,0:T(8,128)(2,1)S(1)}, u32[]{:S(2)}, u32[]{:S(2)}) collective-permute-start(bf16[4,48,1024]{2,1,0:T(8,128)(2,1)S(1)} %get-tuple-element.12), channel_id=1, source_target_pairs={{0,2},{2,0},{4,6},{6,4},{8,10},{10,8},{12,14},{14,12},{1,3},{3,1},... | collective-permute-start | bytes 1179656 | tf_op jit(solution)/shard_map/ppermute | solution.py:173
  145.0 4.3 %collective-permute-start.22 = (bf16[32,1024]{1,0:T(8,128)(2,1)S(1)}, bf16[32,1024]{1,0:T(8,128)(2,1)S(1)}, u32[]{:S(2)}, u32[]{:S(2)}) collective-permute-start(bf16[32,1024]{1,0:T(8,128)(2,1)S(1)} %select_convert_fusion.1), channel_id=1, source_target_pairs={{0,1},{1,0},{2,3},{3,2},{4,5},{5,4},{6,7},{7,6},{8,9},{9,8},{10,11... | collective-permute-start | bytes 196616 | tf_op jit(solution)/shard_map/ppermute | solution.py:49
  (13 other events, 27.7 us)

commit v13 on v11

--- a/solution.py
+++ b/solution.py
@@ -239,6 +239,7 @@
     run_max = jnp.full((heads_dev, tok_here), NEG, jnp.float32)
     kv_here = jnp.concatenate([key_states[0], value_states[0]], axis=1)
     kv_blocks, src_ctx = ctx_gather_blocks(kv_here, n_ctx, my_ctx)
+    kv_blocks, weight_after = lax.optimization_barrier((kv_blocks, out_weight))
     kv_all = kv_blocks.reshape(n_ctx * tok_here, 2 * feat_width)
     key_two = kv_all[:, :feat_width]
     value_two = kv_all[:, feat_width:]
@@ -273,7 +274,7 @@
     out_parts = jnp.einsum(
         "tc,oc->to",
         mixed,
-        gather_out_weight(out_weight, n_ctx, my_ctx),
+        gather_out_weight(weight_after, n_ctx, my_ctx),
         preferred_element_type=jnp.float32,
     )
     head_total = exp_reduce_rows(out_parts)

time: 139 us -> 137 us (0.986)
  waiting for transfers between devices: 67.9 us -> 58.4 us
  starting transfers between devices: 31.1 us -> 38.4 us
    ppermute x3, starting transfers between devices: 0.19 us -> 8.28 us  [moe_column_halves(): returned[shift] = lax.ppermute(summed[idx], 'ctx', perm=perm)]
    ppermute x11, waiting for transfers between devices: 22.6 us -> 17.1 us  [exp_swap(): return lax.ppermute(x, 'exp', perm=[(0, 1), (1, 0)])]
    ppermute x6, starting transfers between devices: 9.55 us -> 13.9 us  [ctx_gather_blocks(): stack.append(lax.ppermute(rows, 'ctx', perm=perm))]
    ppermute x6, waiting for transfers between devices: 22.1 us -> 18.9 us  [ctx_gather_blocks(): stack.append(lax.ppermute(rows, 'ctx', perm=perm))]
    ppermute x11, starting transfers between devices: 15.1 us -> 12.2 us  [exp_swap(): return lax.ppermute(x, 'exp', perm=[(0, 1), (1, 0)])]
    ppermute x3, starting transfers between devices: 6.03 us -> 3.83 us  [moe_column_halves(): arrived.append(lax.ppermute(pairs[shift], 'ctx', perm=perm))]
    ppermute x2, waiting for transfers between devices: 0.01 us -> 1.84 us  [ctx_gather_blocks(): partner = lax.ppermute(own, 'ctx', perm=[(i, i ^ 1) for i in range(n_ctx)])]
    ppermute x3, waiting for transfers between devices: 12 us -> 10.4 us  [moe_column_halves(): arrived.append(lax.ppermute(pairs[shift], 'ctx', perm=perm))]
where the time goes in v13:
time: 137 us
  waiting for transfers between devices  58.4 us (43%)
  starting transfers between devices  38.4 us (28%)
  matrix products  14.8 us (11%)
  local copies, waits for them, and re-layouts  14.6 us (11%)
  other arithmetic  8.64 us (6%)
  between operations  1.89 us (1%)
    ppermute x6, waiting for transfers between devices, ctx_gather_blocks(): stack.append(lax.ppermute(rows, 'ctx', perm=perm))  18.9 us
    ppermute x11, waiting for transfers between devices, exp_swap(): return lax.ppermute(x, 'exp', perm=[(0, 1), (1, 0)])  17.1 us
    ppermute x6, starting transfers between devices, ctx_gather_blocks(): stack.append(lax.ppermute(rows, 'ctx', perm=perm))  13.9 us
    ppermute x11, starting transfers between devices, exp_swap(): return lax.ppermute(x, 'exp', perm=[(0, 1), (1, 0)])  12.2 us
    ppermute x3, waiting for transfers between devices, moe_column_halves(): arrived.append(lax.ppermute(pairs[shift], 'ctx', perm=perm))  10.4 us
    ppermute x3, starting transfers between devices, moe_column_halves(): returned[shift] = lax.ppermute(summed[idx], 'ctx', perm=perm)  8.28 us
    ppermute x3, waiting for transfers between devices, moe_column_halves(): returned[shift] = lax.ppermute(summed[idx], 'ctx', perm=perm)  8.01 us
    unnamed x36, local copies, waits for them, and re-layouts  7.15 us
  transfers between devices with their start and end apart: 27, of which 16 were waited for; matrix products, arithmetic and copies ran while one was open for 19% of the time, Pallas kernels for 0%

profile of v13, /device:TPU:0, one launch (start us, length us, event | category | flops | bytes accessed | tf_op | source)
XLA Modules:
  0.0 136.8 jit_solution(4229455328664236758)
XLA Ops:
  1.7 4.1 %collective-permute-start.1 = (bf16[64,1024]{1,0:T(8,128)(2,1)S(1)}, bf16[64,1024]{1,0:T(8,128)(2,1)S(1)}, u32[]{:S(2)}, u32[]{:S(2)}) collective-permute-start(bf16[64,1024]{1,0:T(8,128)(2,1)S(1)} %get-tuple-element.26), channel_id=1, source_target_pairs={{0,8},{2,10},{4,12},{6,14},{8,0},{10,2},{12,4},{14,6},{1,9},{3,11}... | collective-permute-start | bytes 393224 | tf_op jit(solution)/shard_map/ppermute | solution.py:193
  5.8 1.6 %collective-permute-start = (bf16[64,1024]{1,0:T(8,128)(2,1)S(1)}, bf16[64,1024]{1,0:T(8,128)(2,1)S(1)}, u32[]{:S(2)}, u32[]{:S(2)}) collective-permute-start(bf16[64,1024]{1,0:T(8,128)(2,1)S(1)} %get-tuple-element.26), channel_id=1, source_target_pairs={{0,4},{2,6},{4,8},{6,10},{8,12},{10,14},{12,0},{14,2},{1,5},{3,7},... | collective-permute-start | bytes 393224 | tf_op jit(solution)/shard_map/ppermute | solution.py:193
  7.3 2.2 %collective-permute-start.2 = (bf16[64,1024]{1,0:T(8,128)(2,1)S(1)}, bf16[64,1024]{1,0:T(8,128)(2,1)S(1)}, u32[]{:S(2)}, u32[]{:S(2)}) collective-permute-start(bf16[64,1024]{1,0:T(8,128)(2,1)S(1)} %get-tuple-element.26), channel_id=1, source_target_pairs={{0,12},{2,14},{4,0},{6,2},{8,4},{10,6},{12,8},{14,10},{1,13},{3,15... | collective-permute-start | bytes 393224 | tf_op jit(solution)/shard_map/ppermute | solution.py:193
  14.0 1.5 %reshape_squeeze.9 = bf16[64,4,128]{2,1,0:T(4,128)(2,1)} reshape(bf16[1,64,512]{2,1,0:T(8,128)(2,1)} %param.12) | data formatting | bytes 131072 | tf_op jit(solution)/shard_map/reshape;squeeze | solution.py:238
  16.7 1.8 %collective-permute-done.3 = bf16[4,64,1024]{2,1,0:T(8,128)(2,1)S(1)} collective-permute-done((bf16[4,64,1024]{2,1,0:T(8,128)(2,1)S(1)}, bf16[4,64,1024]{2,1,0:T(8,128)(2,1)S(1)}, u32[]{:S(2)}, u32[]{:S(2)}) %collective-permute-start.3) | collective-permute-done | bytes 524320 | tf_op jit(solution)/shard_map/ppermute | solution.py:195
  18.6 2.1 %collective-permute-start.6 = (bf16[256,512]{1,0:T(8,128)(2,1)S(1)}, bf16[256,512]{1,0:T(8,128)(2,1)S(1)}, u32[]{:S(2)}, u32[]{:S(2)}) collective-permute-start(bf16[256,512]{1,0:T(8,128)(2,1)S(1)} %copy-done.5), channel_id=1, source_target_pairs={{0,12},{2,14},{4,0},{6,2},{8,4},{10,6},{12,8},{14,10},{1,13},{3,15... | collective-permute-start | bytes 786440 | tf_op jit(solution)/shard_map/ppermute | solution.py:193
  20.7 1.9 %collective-permute-start.5 = (bf16[256,512]{1,0:T(8,128)(2,1)S(1)}, bf16[256,512]{1,0:T(8,128)(2,1)}, u32[]{:S(2)}, u32[]{:S(2)}) collective-permute-start(bf16[256,512]{1,0:T(8,128)(2,1)S(1)} %copy-done.5), channel_id=1, source_target_pairs={{0,8},{2,10},{4,12},{6,14},{8,0},{10,2},{12,4},{14,6},{1,9},{3,11}... | collective-permute-start | bytes 786440 | tf_op jit(solution)/shard_map/ppermute | solution.py:193
  22.6 1.9 %collective-permute-start.4 = (bf16[256,512]{1,0:T(8,128)(2,1)S(1)}, bf16[256,512]{1,0:T(8,128)(2,1)}, u32[]{:S(2)}, u32[]{:S(2)}) collective-permute-start(bf16[256,512]{1,0:T(8,128)(2,1)S(1)} %copy-done.5), channel_id=1, source_target_pairs={{0,4},{2,6},{4,8},{6,10},{8,12},{10,14},{12,0},{14,2},{1,5},{3,7},... | collective-permute-start | bytes 786440 | tf_op jit(solution)/shard_map/ppermute | solution.py:193
  27.4 18.6 %collective-permute-done.5 = bf16[256,512]{1,0:T(8,128)(2,1)} collective-permute-done((bf16[256,512]{1,0:T(8,128)(2,1)S(1)}, bf16[256,512]{1,0:T(8,128)(2,1)}, u32[]{:S(2)}, u32[]{:S(2)}) %collective-permute-start.5) | collective-permute-done | bytes 262176 | tf_op jit(solution)/shard_map/ppermute | solution.py:193
  49.0 1.7 %constant_dynamic-update-slice_fusion.8 = bf16[8,256,512]{2,1,0:T(8,128)(2,1)} fusion(bf16[8,256,512]{2,1,0:T(8,128)(2,1)} %constant_dynamic-update-slice_fusion.9, bf16[256,512]{1,0:T(8,128)(2,1)} %collective-permute-done.4), kind=kLoop, calls=%fused_computation.185 | loop fusion | bytes 524288
  50.7 1.7 %constant_dynamic-update-slice_fusion.7 = bf16[8,256,512]{2,1,0:T(8,128)(2,1)} fusion(bf16[8,256,512]{2,1,0:T(8,128)(2,1)} %constant_dynamic-update-slice_fusion.8, bf16[256,512]{1,0:T(8,128)(2,1)} %collective-permute-done.5), kind=kLoop, calls=%fused_computation.184 | loop fusion | bytes 524288
  54.1 2.3 %gather_fusion = bf16[8,256,512]{2,1,0:T(8,128)(2,1)S(1)} fusion(bf16[8,256,512]{2,1,0:T(8,128)(2,1)} %constant_dynamic-update-slice_fusion.5, s32[1024]{0:T(1024)S(1)} %pad_clamp_fusion), kind=kCustom, calls=%fused_computation | custom fusion | bytes 4194336 | tf_op jit(solution)/shard_map/jit(_take)/gather | solution.py:210
  58.0 1.6 %collective-permute-start.8 = (bf16[32,2048]{1,0:T(8,128)(2,1)S(1)}, bf16[32,2048]{1,0:T(8,128)(2,1)S(1)}, u32[]{:S(2)}, u32[]{:S(2)}) collective-permute-start(bf16[32,2048]{1,0:T(8,128)(2,1)S(1)} %select_convert_fusion), channel_id=1, source_target_pairs={{0,1},{1,0},{2,3},{3,2},{4,5},{5,4},{6,7},{7,6},{8,9},{9,8},{10,11... | collective-permute-start | bytes 393224 | tf_op jit(solution)/shard_map/ppermute | solution.py:49
  59.8 4.2 %collective-permute-done.8 = bf16[32,2048]{1,0:T(8,128)(2,1)S(1)} collective-permute-done((bf16[32,2048]{1,0:T(8,128)(2,1)S(1)}, bf16[32,2048]{1,0:T(8,128)(2,1)S(1)}, u32[]{:S(2)}, u32[]{:S(2)}) %collective-permute-start.8) | collective-permute-done | bytes 131104 | tf_op jit(solution)/shard_map/ppermute | solution.py:49
  64.3 1.6 %collective-permute-start.9 = (bf16[32,1024]{1,0:T(8,128)(2,1)S(1)}, bf16[32,1024]{1,0:T(8,128)(2,1)S(1)}, u32[]{:S(2)}, u32[]{:S(2)}) collective-permute-start(bf16[32,1024]{1,0:T(8,128)(2,1)S(1)} %get-tuple-element.24), channel_id=1, source_target_pairs={{0,1},{1,0},{2,3},{3,2},{4,5},{5,4},{6,7},{7,6},{8,9},{9,8},{10,11... | collective-permute-start | bytes 196616 | tf_op jit(solution)/shard_map/ppermute | solution.py:49
  66.0 2.6 %collective-permute-done.9 = bf16[32,1024]{1,0:T(8,128)(2,1)S(1)} collective-permute-done((bf16[32,1024]{1,0:T(8,128)(2,1)S(1)}, bf16[32,1024]{1,0:T(8,128)(2,1)S(1)}, u32[]{:S(2)}, u32[]{:S(2)}) %collective-permute-start.9) | collective-permute-done | bytes 65568 | tf_op jit(solution)/shard_map/ppermute | solution.py:49
  69.8 2.1 %collective-permute-done.10 = bf16[4,48,1024]{2,1,0:T(8,128)(2,1)} collective-permute-done((bf16[4,48,1024]{2,1,0:T(8,128)(2,1)}, bf16[4,48,1024]{2,1,0:T(8,128)(2,1)}, u32[]{:S(2)}, u32[]{:S(2)}) %collective-permute-start.10) | collective-permute-done | bytes 393248 | tf_op jit(solution)/shard_map/ppermute | solution.py:133
  73.0 1.6 %collective-permute-start.11 = (bf16[96,1024]{1,0:T(8,128)(2,1)S(1)}, bf16[96,1024]{1,0:T(8,128)(2,1)S(1)}, u32[]{:S(2)}, u32[]{:S(2)}) collective-permute-start(bf16[96,1024]{1,0:T(8,128)(2,1)S(1)} %bitcast.213), channel_id=1, source_target_pairs={{0,1},{1,0},{2,3},{3,2},{4,5},{5,4},{6,7},{7,6},{8,9},{9,8},{10,11... | collective-permute-start | bytes 589832 | tf_op jit(solution)/shard_map/ppermute | solution.py:49
  74.6 3.8 %collective-permute-start.21 = (bf16[2,48,1024]{2,1,0:T(8,128)(2,1)S(1)}, bf16[2,48,1024]{2,1,0:T(8,128)(2,1)S(1)}, u32[]{:S(2)}, u32[]{:S(2)}) collective-permute-start(bf16[2,48,1024]{2,1,0:T(8,128)(2,1)S(1)} %get-tuple-element.19), channel_id=1, source_target_pairs={{0,12},{2,14},{4,0},{6,2},{8,4},{10,6},{12,8},{14,10},{1,13},{3,15... | collective-permute-start | bytes 589832 | tf_op jit(solution)/shard_map/ppermute | solution.py:138
  78.4 1.6 %fusion.29 = f32[96,352]{1,0:T(8,128)S(1)} fusion(bf16[96,1024]{1,0:T(8,128)(2,1)S(1)} %bitcast.214, bf16[1,2048,352]{1,2,0:T(8,128)(2,1)} %param.19, s32[]{:T(128)S(6)} %select_n.327), kind=kOutput, calls=%fused_computation.57 | convolution fusion | flops 69206016 | bytes 1052676 | tf_op jit(solution)/shard_map/dot_general | solution.py:157
  80.4 3.8 %collective-permute-done.13 = bf16[2,48,1024]{2,1,0:T(8,128)(2,1)S(1)} collective-permute-done((bf16[2,48,1024]{2,1,0:T(8,128)(2,1)S(1)}, bf16[2,48,1024]{2,1,0:T(8,128)(2,1)S(1)}, u32[]{:S(2)}, u32[]{:S(2)}) %collective-permute-start.13) | collective-permute-done | bytes 196640 | tf_op jit(solution)/shard_map/ppermute | solution.py:138
  85.7 1.6 %collective-permute-start.12 = (bf16[96,1024]{1,0:T(8,128)(2,1)S(1)}, bf16[96,1024]{1,0:T(8,128)(2,1)S(1)}, u32[]{:S(2)}, u32[]{:S(2)}) collective-permute-start(bf16[96,1024]{1,0:T(8,128)(2,1)S(1)} %convolution_convert_fusion.4), channel_id=1, source_target_pairs={{0,1},{1,0},{2,3},{3,2},{4,5},{5,4},{6,7},{7,6},{8,9},{9,8},{10,11... | collective-permute-start | bytes 589832 | tf_op jit(solution)/shard_map/ppermute | solution.py:49
  87.8 6.6 %collective-permute-done.17 = bf16[2,48,1024]{2,1,0:T(8,128)(2,1)S(1)} collective-permute-done((bf16[2,48,1024]{2,1,0:T(8,128)(2,1)S(1)}, bf16[2,48,1024]{2,1,0:T(8,128)(2,1)S(1)}, u32[]{:S(2)}, u32[]{:S(2)}) %collective-permute-start.17) | collective-permute-done | bytes 196640 | tf_op jit(solution)/shard_map/ppermute | solution.py:138
  96.8 1.6 %collective-permute-start.15 = (bf16[96,1024]{1,0:T(8,128)(2,1)S(1)}, bf16[96,1024]{1,0:T(8,128)(2,1)S(1)}, u32[]{:S(2)}, u32[]{:S(2)}) collective-permute-start(bf16[96,1024]{1,0:T(8,128)(2,1)S(1)} %convolution_convert_fusion.3), channel_id=1, source_target_pairs={{0,1},{1,0},{2,3},{3,2},{4,5},{5,4},{6,7},{7,6},{8,9},{9,8},{10,11... | collective-permute-start | bytes 589832 | tf_op jit(solution)/shard_map/ppermute | solution.py:49
  101.7 1.3 collective-permute-done.18
  105.9 1.3 collective-permute-done.15
  108.1 3.4 %collective-permute-done.23 = bf16[96,1024]{1,0:T(8,128)(2,1)S(1)} collective-permute-done((bf16[96,1024]{1,0:T(8,128)(2,1)S(1)}, bf16[96,1024]{1,0:T(8,128)(2,1)S(1)}, u32[]{:S(2)}, u32[]{:S(2)}) %collective-permute-start.23) | collective-permute-done | bytes 196640 | tf_op jit(solution)/shard_map/ppermute | solution.py:49
  111.8 2.8 %collective-permute-start.24 = (bf16[2,48,1024]{2,1,0:T(8,128)(2,1)S(1)}, bf16[2,48,1024]{2,1,0:T(8,128)(2,1)S(1)}, u32[]{:S(2)}, u32[]{:S(2)}) collective-permute-start(bf16[2,48,1024]{2,1,0:T(8,128)(2,1)S(1)} %bitcast.245), channel_id=1, source_target_pairs={{0,4},{2,6},{4,8},{6,10},{8,12},{10,14},{12,0},{14,2},{1,5},{3,7},... | collective-permute-start | bytes 589832 | tf_op jit(solution)/shard_map/ppermute | solution.py:171
  114.9 4.9 %collective-permute-start.20 = (bf16[2,48,1024]{2,1,0:T(8,128)(2,1)S(1)}, bf16[2,48,1024]{2,1,0:T(8,128)(2,1)S(1)}, u32[]{:S(2)}, u32[]{:S(2)}) collective-permute-start(bf16[2,48,1024]{2,1,0:T(8,128)(2,1)S(1)} %bitcast.246), channel_id=1, source_target_pairs={{0,8},{2,10},{4,12},{6,14},{8,0},{10,2},{12,4},{14,6},{1,9},{3,11}... | collective-permute-start | bytes 589832 | tf_op jit(solution)/shard_map/ppermute | solution.py:171
  120.1 1.8 %collective-permute-done.24 = bf16[2,48,1024]{2,1,0:T(8,128)(2,1)S(1)} collective-permute-done((bf16[2,48,1024]{2,1,0:T(8,128)(2,1)S(1)}, bf16[2,48,1024]{2,1,0:T(8,128)(2,1)S(1)}, u32[]{:S(2)}, u32[]{:S(2)}) %collective-permute-start.24) | collective-permute-done | bytes 196640 | tf_op jit(solution)/shard_map/ppermute | solution.py:171
  122.0 6.2 %collective-permute-done.20 = bf16[2,48,1024]{2,1,0:T(8,128)(2,1)S(1)} collective-permute-done((bf16[2,48,1024]{2,1,0:T(8,128)(2,1)S(1)}, bf16[2,48,1024]{2,1,0:T(8,128)(2,1)S(1)}, u32[]{:S(2)}, u32[]{:S(2)}) %collective-permute-start.20) | collective-permute-done | bytes 196640 | tf_op jit(solution)/shard_map/ppermute | solution.py:171
  132.3 3.7 %collective-permute-done.26 = bf16[32,1024]{1,0:T(8,128)(2,1)S(1)} collective-permute-done((bf16[32,1024]{1,0:T(8,128)(2,1)S(1)}, bf16[32,1024]{1,0:T(8,128)(2,1)S(1)}, u32[]{:S(2)}, u32[]{:S(2)}) %collective-permute-start.26) | collective-permute-done | bytes 65568 | tf_op jit(solution)/shard_map/ppermute | solution.py:49
  (140 shorter events, 35.2 us)
Async XLA Ops:
  0.6 84.8 %copy-start = (bf16[1,352,2048]{2,1,0:T(8,128)(2,1)S(1)}, bf16[1,352,2048]{2,1,0:T(8,128)(2,1)}, u32[]{:S(2)}) copy-start(bf16[1,352,2048]{2,1,0:T(8,128)(2,1)} %param.20) | copy-start | bytes 4325380
  1.7 14.7 %collective-permute-start.1 = (bf16[64,1024]{1,0:T(8,128)(2,1)S(1)}, bf16[64,1024]{1,0:T(8,128)(2,1)S(1)}, u32[]{:S(2)}, u32[]{:S(2)}) collective-permute-start(bf16[64,1024]{1,0:T(8,128)(2,1)S(1)} %get-tuple-element.26), channel_id=1, source_target_pairs={{0,8},{2,10},{4,12},{6,14},{8,0},{10,2},{12,4},{14,6},{1,9},{3,11}... | collective-permute-start | bytes 393224 | tf_op jit(solution)/shard_map/ppermute | solution.py:193
  5.8 10.6 %collective-permute-start = (bf16[64,1024]{1,0:T(8,128)(2,1)S(1)}, bf16[64,1024]{1,0:T(8,128)(2,1)S(1)}, u32[]{:S(2)}, u32[]{:S(2)}) collective-permute-start(bf16[64,1024]{1,0:T(8,128)(2,1)S(1)} %get-tuple-element.26), channel_id=1, source_target_pairs={{0,4},{2,6},{4,8},{6,10},{8,12},{10,14},{12,0},{14,2},{1,5},{3,7},... | collective-permute-start | bytes 393224 | tf_op jit(solution)/shard_map/ppermute | solution.py:193
  7.3 9.1 %collective-permute-start.2 = (bf16[64,1024]{1,0:T(8,128)(2,1)S(1)}, bf16[64,1024]{1,0:T(8,128)(2,1)S(1)}, u32[]{:S(2)}, u32[]{:S(2)}) collective-permute-start(bf16[64,1024]{1,0:T(8,128)(2,1)S(1)} %get-tuple-element.26), channel_id=1, source_target_pairs={{0,12},{2,14},{4,0},{6,2},{8,4},{10,6},{12,8},{14,10},{1,13},{3,15... | collective-permute-start | bytes 393224 | tf_op jit(solution)/shard_map/ppermute | solution.py:193
  10.4 8.2 %copy-start.6 = (s32[1,64,4]{2,1,0:T(8,128)}, s32[1,64,4]{2,1,0:T(8,128)S(1)}, u32[]{:S(2)}) copy-start(s32[1,64,4]{2,1,0:T(8,128)S(1)} %copy.46) | copy-start | bytes 3076
  16.5 2.0 %collective-permute-start.3 = (bf16[4,64,1024]{2,1,0:T(8,128)(2,1)S(1)}, bf16[4,64,1024]{2,1,0:T(8,128)(2,1)S(1)}, u32[]{:S(2)}, u32[]{:S(2)}) collective-permute-start(bf16[4,64,1024]{2,1,0:T(8,128)(2,1)S(1)} %pad_maximum_fusion.3), channel_id=1, source_target_pairs={{0,2},{2,0},{4,6},{6,4},{8,10},{10,8},{12,14},{14,12},{1,3},{3,1},... | collective-permute-start | bytes 1572872 | tf_op jit(solution)/shard_map/ppermute | solution.py:195
  18.6 8.9 %collective-permute-start.6 = (bf16[256,512]{1,0:T(8,128)(2,1)S(1)}, bf16[256,512]{1,0:T(8,128)(2,1)S(1)}, u32[]{:S(2)}, u32[]{:S(2)}) collective-permute-start(bf16[256,512]{1,0:T(8,128)(2,1)S(1)} %copy-done.5), channel_id=1, source_target_pairs={{0,12},{2,14},{4,0},{6,2},{8,4},{10,6},{12,8},{14,10},{1,13},{3,15... | collective-permute-start | bytes 786440 | tf_op jit(solution)/shard_map/ppermute | solution.py:193
  20.7 25.4 %collective-permute-start.5 = (bf16[256,512]{1,0:T(8,128)(2,1)S(1)}, bf16[256,512]{1,0:T(8,128)(2,1)}, u32[]{:S(2)}, u32[]{:S(2)}) collective-permute-start(bf16[256,512]{1,0:T(8,128)(2,1)S(1)} %copy-done.5), channel_id=1, source_target_pairs={{0,8},{2,10},{4,12},{6,14},{8,0},{10,2},{12,4},{14,6},{1,9},{3,11}... | collective-permute-start | bytes 786440 | tf_op jit(solution)/shard_map/ppermute | solution.py:193
  22.6 23.5 %collective-permute-start.4 = (bf16[256,512]{1,0:T(8,128)(2,1)S(1)}, bf16[256,512]{1,0:T(8,128)(2,1)}, u32[]{:S(2)}, u32[]{:S(2)}) collective-permute-start(bf16[256,512]{1,0:T(8,128)(2,1)S(1)} %copy-done.5), channel_id=1, source_target_pairs={{0,4},{2,6},{4,8},{6,10},{8,12},{10,14},{12,0},{14,2},{1,5},{3,7},... | collective-permute-start | bytes 786440 | tf_op jit(solution)/shard_map/ppermute | solution.py:193
  26.2 21.1 %copy-start.8 = (pred[64,512]{1,0:T(8,128)(4,1)S(1)}, pred[64,512]{1,0:T(8,128)(4,1)}, u32[]{:S(2)}) copy-start(pred[64,512]{1,0:T(8,128)(4,1)} %compare_and_fusion) | copy-start | bytes 98308
  47.2 5.9 %collective-permute-start.7 = (bf16[4,256,512]{2,1,0:T(8,128)(2,1)S(1)}, bf16[4,256,512]{2,1,0:T(8,128)(2,1)S(1)}, u32[]{:S(2)}, u32[]{:S(2)}) collective-permute-start(bf16[4,256,512]{2,1,0:T(8,128)(2,1)S(1)} %pad_maximum_fusion), channel_id=1, source_target_pairs={{0,2},{2,0},{4,6},{6,4},{8,10},{10,8},{12,14},{14,12},{1,3},{3,1},... | collective-permute-start | bytes 3145736 | tf_op jit(solution)/shard_map/ppermute | solution.py:195
  58.0 7.9 %copy-start.13 = (f32[1,64,4]{1,2,0:T(4,128)S(1)}, f32[1,64,4]{1,2,0:T(4,128)}, u32[]{:S(2)}) copy-start(f32[1,64,4]{1,2,0:T(4,128)} %param.22) | copy-start | bytes 3076
  58.0 6.0 %collective-permute-start.8 = (bf16[32,2048]{1,0:T(8,128)(2,1)S(1)}, bf16[32,2048]{1,0:T(8,128)(2,1)S(1)}, u32[]{:S(2)}, u32[]{:S(2)}) collective-permute-start(bf16[32,2048]{1,0:T(8,128)(2,1)S(1)} %select_convert_fusion), channel_id=1, source_target_pairs={{0,1},{1,0},{2,3},{3,2},{4,5},{5,4},{6,7},{7,6},{8,9},{9,8},{10,11... | collective-permute-start | bytes 393224 | tf_op jit(solution)/shard_map/ppermute | solution.py:49
  64.3 4.3 %collective-permute-start.9 = (bf16[32,1024]{1,0:T(8,128)(2,1)S(1)}, bf16[32,1024]{1,0:T(8,128)(2,1)S(1)}, u32[]{:S(2)}, u32[]{:S(2)}) collective-permute-start(bf16[32,1024]{1,0:T(8,128)(2,1)S(1)} %get-tuple-element.24), channel_id=1, source_target_pairs={{0,1},{1,0},{2,3},{3,2},{4,5},{5,4},{6,7},{7,6},{8,9},{9,8},{10,11... | collective-permute-start | bytes 196616 | tf_op jit(solution)/shard_map/ppermute | solution.py:49
  69.8 10.2 %copy-start.1 = (bf16[1,2048,352]{1,2,0:T(8,128)(2,1)S(1)}, bf16[1,2048,352]{1,2,0:T(8,128)(2,1)}, u32[]{:S(2)}) copy-start(bf16[1,2048,352]{1,2,0:T(8,128)(2,1)} %param.18) | copy-start | bytes 4325380
  69.8 2.1 %collective-permute-start.10 = (bf16[4,48,1024]{2,1,0:T(8,128)(2,1)}, bf16[4,48,1024]{2,1,0:T(8,128)(2,1)}, u32[]{:S(2)}, u32[]{:S(2)}) collective-permute-start(bf16[4,48,1024]{2,1,0:T(8,128)(2,1)} %bitcast.25), channel_id=1, source_target_pairs={{0,2},{2,0},{4,6},{6,4},{8,10},{10,8},{12,14},{14,12},{1,3},{3,1},... | collective-permute-start | bytes 1179656 | tf_op jit(solution)/shard_map/ppermute | solution.py:133
  73.0 11.7 %collective-permute-start.11 = (bf16[96,1024]{1,0:T(8,128)(2,1)S(1)}, bf16[96,1024]{1,0:T(8,128)(2,1)S(1)}, u32[]{:S(2)}, u32[]{:S(2)}) collective-permute-start(bf16[96,1024]{1,0:T(8,128)(2,1)S(1)} %bitcast.213), channel_id=1, source_target_pairs={{0,1},{1,0},{2,3},{3,2},{4,5},{5,4},{6,7},{7,6},{8,9},{9,8},{10,11... | collective-permute-start | bytes 589832 | tf_op jit(solution)/shard_map/ppermute | solution.py:49
  74.6 9.6 %collective-permute-start.13 = (bf16[2,48,1024]{2,1,0:T(8,128)(2,1)S(1)}, bf16[2,48,1024]{2,1,0:T(8,128)(2,1)S(1)}, u32[]{:S(2)}, u32[]{:S(2)}) collective-permute-start(bf16[2,48,1024]{2,1,0:T(8,128)(2,1)S(1)} %get-tuple-element.18), channel_id=1, source_target_pairs={{0,4},{2,6},{4,8},{6,10},{8,12},{10,14},{12,0},{14,2},{1,5},{3,7},... | collective-permute-start | bytes 589832 | tf_op jit(solution)/shard_map/ppermute | solution.py:138
  74.6 12.7 %collective-permute-start.21 = (bf16[2,48,1024]{2,1,0:T(8,128)(2,1)S(1)}, bf16[2,48,1024]{2,1,0:T(8,128)(2,1)S(1)}, u32[]{:S(2)}, u32[]{:S(2)}) collective-permute-start(bf16[2,48,1024]{2,1,0:T(8,128)(2,1)S(1)} %get-tuple-element.19), channel_id=1, source_target_pairs={{0,12},{2,14},{4,0},{6,2},{8,4},{10,6},{12,8},{14,10},{1,13},{3,15... | collective-permute-start | bytes 589832 | tf_op jit(solution)/shard_map/ppermute | solution.py:138
  78.4 16.1 %collective-permute-start.17 = (bf16[2,48,1024]{2,1,0:T(8,128)(2,1)S(1)}, bf16[2,48,1024]{2,1,0:T(8,128)(2,1)S(1)}, u32[]{:S(2)}, u32[]{:S(2)}) collective-permute-start(bf16[2,48,1024]{2,1,0:T(8,128)(2,1)S(1)} %get-tuple-element.20), channel_id=1, source_target_pairs={{0,8},{2,10},{4,12},{6,14},{8,0},{10,2},{12,4},{14,6},{1,9},{3,11}... | collective-permute-start | bytes 589832 | tf_op jit(solution)/shard_map/ppermute | solution.py:138
  84.2 10.8 %collective-permute-start.14 = (bf16[96,1024]{1,0:T(8,128)(2,1)S(1)}, bf16[96,1024]{1,0:T(8,128)(2,1)S(1)}, u32[]{:S(2)}, u32[]{:S(2)}) collective-permute-start(bf16[96,1024]{1,0:T(8,128)(2,1)S(1)} %bitcast.241), channel_id=1, source_target_pairs={{0,1},{1,0},{2,3},{3,2},{4,5},{5,4},{6,7},{7,6},{8,9},{9,8},{10,11... | collective-permute-start | bytes 589832 | tf_op jit(solution)/shard_map/ppermute | solution.py:49
  85.7 34.1 %collective-permute-start.12 = (bf16[96,1024]{1,0:T(8,128)(2,1)S(1)}, bf16[96,1024]{1,0:T(8,128)(2,1)S(1)}, u32[]{:S(2)}, u32[]{:S(2)}) collective-permute-start(bf16[96,1024]{1,0:T(8,128)(2,1)S(1)} %convolution_convert_fusion.4), channel_id=1, source_target_pairs={{0,1},{1,0},{2,3},{3,2},{4,5},{5,4},{6,7},{7,6},{8,9},{9,8},{10,11... | collective-permute-start | bytes 589832 | tf_op jit(solution)/shard_map/ppermute | solution.py:49
  87.3 11.5 %collective-permute-start.22 = (bf16[96,1024]{1,0:T(8,128)(2,1)S(1)}, bf16[96,1024]{1,0:T(8,128)(2,1)S(1)}, u32[]{:S(2)}, u32[]{:S(2)}) collective-permute-start(bf16[96,1024]{1,0:T(8,128)(2,1)S(1)} %bitcast.238), channel_id=1, source_target_pairs={{0,1},{1,0},{2,3},{3,2},{4,5},{5,4},{6,7},{7,6},{8,9},{9,8},{10,11... | collective-permute-start | bytes 589832 | tf_op jit(solution)/shard_map/ppermute | solution.py:49
  94.5 8.6 %collective-permute-start.18 = (bf16[96,1024]{1,0:T(8,128)(2,1)S(1)}, bf16[96,1024]{1,0:T(8,128)(2,1)S(1)}, u32[]{:S(2)}, u32[]{:S(2)}) collective-permute-start(bf16[96,1024]{1,0:T(8,128)(2,1)S(1)} %bitcast.235), channel_id=1, source_target_pairs={{0,1},{1,0},{2,3},{3,2},{4,5},{5,4},{6,7},{7,6},{8,9},{9,8},{10,11... | collective-permute-start | bytes 589832 | tf_op jit(solution)/shard_map/ppermute | solution.py:49
  96.8 10.5 %collective-permute-start.15 = (bf16[96,1024]{1,0:T(8,128)(2,1)S(1)}, bf16[96,1024]{1,0:T(8,128)(2,1)S(1)}, u32[]{:S(2)}, u32[]{:S(2)}) collective-permute-start(bf16[96,1024]{1,0:T(8,128)(2,1)S(1)} %convolution_convert_fusion.3), channel_id=1, source_target_pairs={{0,1},{1,0},{2,3},{3,2},{4,5},{5,4},{6,7},{7,6},{8,9},{9,8},{10,11... | collective-permute-start | bytes 589832 | tf_op jit(solution)/shard_map/ppermute | solution.py:49
  100.6 10.9 %collective-permute-start.23 = (bf16[96,1024]{1,0:T(8,128)(2,1)S(1)}, bf16[96,1024]{1,0:T(8,128)(2,1)S(1)}, u32[]{:S(2)}, u32[]{:S(2)}) collective-permute-start(bf16[96,1024]{1,0:T(8,128)(2,1)S(1)} %convolution_convert_fusion.1), channel_id=1, source_target_pairs={{0,1},{1,0},{2,3},{3,2},{4,5},{5,4},{6,7},{7,6},{8,9},{9,8},{10,11... | collective-permute-start | bytes 589832 | tf_op jit(solution)/shard_map/ppermute | solution.py:49
  104.8 9.8 %collective-permute-start.19 = (bf16[96,1024]{1,0:T(8,128)(2,1)S(1)}, bf16[96,1024]{1,0:T(8,128)(2,1)S(1)}, u32[]{:S(2)}, u32[]{:S(2)}) collective-permute-start(bf16[96,1024]{1,0:T(8,128)(2,1)S(1)} %convolution_convert_fusion.2), channel_id=1, source_target_pairs={{0,1},{1,0},{2,3},{3,2},{4,5},{5,4},{6,7},{7,6},{8,9},{9,8},{10,11... | collective-permute-start | bytes 589832 | tf_op jit(solution)/shard_map/ppermute | solution.py:49
  107.5 12.6 %collective-permute-start.16 = (bf16[2,48,1024]{2,1,0:T(8,128)(2,1)S(1)}, bf16[2,48,1024]{2,1,0:T(8,128)(2,1)S(1)}, u32[]{:S(2)}, u32[]{:S(2)}) collective-permute-start(bf16[2,48,1024]{2,1,0:T(8,128)(2,1)S(1)} %bitcast.244), channel_id=1, source_target_pairs={{0,12},{2,14},{4,0},{6,2},{8,4},{10,6},{12,8},{14,10},{1,13},{3,15... | collective-permute-start | bytes 589832 | tf_op jit(solution)/shard_map/ppermute | solution.py:171
  111.8 10.2 %collective-permute-start.24 = (bf16[2,48,1024]{2,1,0:T(8,128)(2,1)S(1)}, bf16[2,48,1024]{2,1,0:T(8,128)(2,1)S(1)}, u32[]{:S(2)}, u32[]{:S(2)}) collective-permute-start(bf16[2,48,1024]{2,1,0:T(8,128)(2,1)S(1)} %bitcast.245), channel_id=1, source_target_pairs={{0,4},{2,6},{4,8},{6,10},{8,12},{10,14},{12,0},{14,2},{1,5},{3,7},... | collective-permute-start | bytes 589832 | tf_op jit(solution)/shard_map/ppermute | solution.py:171
  114.9 13.2 %collective-permute-start.20 = (bf16[2,48,1024]{2,1,0:T(8,128)(2,1)S(1)}, bf16[2,48,1024]{2,1,0:T(8,128)(2,1)S(1)}, u32[]{:S(2)}, u32[]{:S(2)}) collective-permute-start(bf16[2,48,1024]{2,1,0:T(8,128)(2,1)S(1)} %bitcast.246), channel_id=1, source_target_pairs={{0,8},{2,10},{4,12},{6,14},{8,0},{10,2},{12,4},{14,6},{1,9},{3,11}... | collective-permute-start | bytes 589832 | tf_op jit(solution)/shard_map/ppermute | solution.py:171
  128.3 2.8 %collective-permute-start.25 = (bf16[4,48,1024]{2,1,0:T(8,128)(2,1)S(1)}, bf16[4,48,1024]{2,1,0:T(8,128)(2,1)S(1)}, u32[]{:S(2)}, u32[]{:S(2)}) collective-permute-start(bf16[4,48,1024]{2,1,0:T(8,128)(2,1)S(1)} %get-tuple-element.16), channel_id=1, source_target_pairs={{0,2},{2,0},{4,6},{6,4},{8,10},{10,8},{12,14},{14,12},{1,3},{3,1},... | collective-permute-start | bytes 1179656 | tf_op jit(solution)/shard_map/ppermute | solution.py:173
  131.7 4.3 %collective-permute-start.26 = (bf16[32,1024]{1,0:T(8,128)(2,1)S(1)}, bf16[32,1024]{1,0:T(8,128)(2,1)S(1)}, u32[]{:S(2)}, u32[]{:S(2)}) collective-permute-start(bf16[32,1024]{1,0:T(8,128)(2,1)S(1)} %select_convert_fusion.1), channel_id=1, source_target_pairs={{0,1},{1,0},{2,3},{3,2},{4,5},{5,4},{6,7},{7,6},{8,9},{9,8},{10,11... | collective-permute-start | bytes 196616 | tf_op jit(solution)/shard_map/ppermute | solution.py:49
  (9 other events, 35.3 us)

commit v14 on v10

--- a/solution.py
+++ b/solution.py
@@ -116,8 +116,7 @@
     my_exp = lax.axis_index("exp")
     first = my_exp == 0
     half_d = normed.shape[1] // 2
-    my_cols, other_cols = halves(normed, first, 1)
-    tokens_cols = join(my_cols, exp_swap(other_cols), first, 0)
+    tokens_cols = halves(normed, first, 1)[0]
     tok_count = tokens_cols.shape[0]
     my_ctx = lax.axis_index("ctx")
     n_chip = n_ctx // 2
@@ -265,9 +264,17 @@
         lax.all_gather(out_weight, "ctx", axis=0, tiled=True),
         preferred_element_type=jnp.float32,
     )
-    head_total = exp_reduce_rows(out_parts)
-    stream = (residual[0].astype(jnp.float32) + head_total).astype(jnp.bfloat16)
-    stream_f = stream.astype(jnp.float32)
+    if lax.axis_size("exp") == 2:
+        first_exp = lax.axis_index("exp") == 0
+        residual_all = join(residual[0], exp_swap(residual[0]), first_exp, 0)
+        head_all = out_parts + exp_swap(out_parts.astype(jnp.bfloat16)).astype(jnp.float32)
+        stream_all = (residual_all.astype(jnp.float32) + head_all).astype(jnp.bfloat16)
+        stream = halves(stream_all, first_exp, 0)[0]
+        stream_f = stream_all.astype(jnp.float32)
+    else:
+        head_total = exp_reduce_rows(out_parts)
+        stream = (residual[0].astype(jnp.float32) + head_total).astype(jnp.bfloat16)
+        stream_f = stream.astype(jnp.float32)
     mean_sq = jnp.mean(stream_f * stream_f, axis=1, keepdims=True)
     normed = (stream_f * lax.rsqrt(mean_sq + EPS) * norm_gain).astype(jnp.bfloat16)
     capacity = min(tok_here, 2 * max(1, 3 * tok_here * TOP // (4 * n_ctx)))

time: 131 us -> 130 us (level)
  waiting for transfers between devices: 58.7 us -> 56.8 us
    ppermute x3, waiting for transfers between devices: 2.34 us -> 0.9 us  [ctx_gather_blocks(): stack.append(lax.ppermute(rows, 'ctx', perm=perm))]
    unnamed x20 -> x22, local copies, waits for them, and re-layouts: 2.69 us -> 2.68 us
  transfers between devices with their start and end apart: 24 -> 24, of which waited for: 14 -> 12; matrix products, arithmetic and copies ran while one was open for 13% -> 15% of each run, Pallas kernels for 0% -> 0%
where the time goes in v14:
time: 130 us
  waiting for transfers between devices  56.8 us (44%)
  starting transfers between devices  32.3 us (25%)
  between operations  15.2 us (12%)
  matrix products  13.7 us (11%)
  other arithmetic  6.37 us (5%)
  local copies, waits for them, and re-layouts  5.6 us (4%)
    ppermute x11, waiting for transfers between devices, exp_swap(): return lax.ppermute(x, 'exp', perm=[(0, 1), (1, 0)])  17.2 us
    all_gather x1, waiting for transfers between devices, local(): lax.all_gather(out_weight, 'ctx', axis=0, tiled=True)  16.7 us
    ppermute x11, starting transfers between devices, exp_swap(): return lax.ppermute(x, 'exp', perm=[(0, 1), (1, 0)])  10.8 us
    ppermute x3, starting transfers between devices, moe_column_halves(): returned[shift] = lax.ppermute(summed[idx], 'ctx', perm=perm)  10.2 us
    ppermute x3, waiting for transfers between devices, moe_column_halves(): arrived.append(lax.ppermute(pairs[shift], 'ctx', perm=perm))  9.17 us
    ppermute x3, waiting for transfers between devices, moe_column_halves(): returned[shift] = lax.ppermute(summed[idx], 'ctx', perm=perm)  8.24 us
    ppermute x3, starting transfers between devices, ctx_gather_blocks(): stack.append(lax.ppermute(rows, 'ctx', perm=perm))  7.03 us
    ppermute x3, starting transfers between devices, moe_column_halves(): arrived.append(lax.ppermute(pairs[shift], 'ctx', perm=perm))  4.02 us
  transfers between devices with their start and end apart: 24, of which 12 were waited for; matrix products, arithmetic and copies ran while one was open for 15% of the time, Pallas kernels for 0%

profile of v14, /device:TPU:0, one launch (start us, length us, event | category | flops | bytes accessed | tf_op | source)
XLA Modules:
  0.0 129.9 jit_solution(8729049335269773652)
XLA Ops:
  7.9 0.9 fusion.162
  8.8 3.1 %collective-permute-start.1 = (bf16[64,1024]{1,0:T(8,128)(2,1)S(1)}, bf16[64,1024]{1,0:T(8,128)(2,1)S(1)}, u32[]{:S(2)}, u32[]{:S(2)}) collective-permute-start(bf16[64,1024]{1,0:T(8,128)(2,1)S(1)} %get-tuple-element.20), channel_id=1, source_target_pairs={{0,4},{2,6},{4,8},{6,10},{8,12},{10,14},{12,0},{14,2},{1,5},{3,7},... | collective-permute-start | bytes 393224 | tf_op jit(solution)/shard_map/ppermute | solution.py:192
  11.9 2.6 %collective-permute-start.2 = (bf16[64,1024]{1,0:T(8,128)(2,1)S(1)}, bf16[64,1024]{1,0:T(8,128)(2,1)S(1)}, u32[]{:S(2)}, u32[]{:S(2)}) collective-permute-start(bf16[64,1024]{1,0:T(8,128)(2,1)S(1)} %get-tuple-element.20), channel_id=1, source_target_pairs={{0,8},{2,10},{4,12},{6,14},{8,0},{10,2},{12,4},{14,6},{1,9},{3,11}... | collective-permute-start | bytes 393224 | tf_op jit(solution)/shard_map/ppermute | solution.py:192
  14.5 1.4 %collective-permute-start.3 = (bf16[64,1024]{1,0:T(8,128)(2,1)S(1)}, bf16[64,1024]{1,0:T(8,128)(2,1)S(1)}, u32[]{:S(2)}, u32[]{:S(2)}) collective-permute-start(bf16[64,1024]{1,0:T(8,128)(2,1)S(1)} %get-tuple-element.20), channel_id=1, source_target_pairs={{0,12},{2,14},{4,0},{6,2},{8,4},{10,6},{12,8},{14,10},{1,13},{3,15... | collective-permute-start | bytes 393224 | tf_op jit(solution)/shard_map/ppermute | solution.py:192
  15.8 1.5 %collective-permute-start = (bf16[32,2048]{1,0:T(8,128)(2,1)}, bf16[32,2048]{1,0:T(8,128)(2,1)S(1)}, u32[]{:S(2)}, u32[]{:S(2)}) collective-permute-start(bf16[32,2048]{1,0:T(8,128)(2,1)} %bitcast.232), channel_id=1, source_target_pairs={{0,1},{1,0},{2,3},{3,2},{4,5},{5,4},{6,7},{7,6},{8,9},{9,8},{10,11... | collective-permute-start | bytes 393224 | tf_op jit(solution)/shard_map/ppermute | solution.py:49
  21.3 0.9 constant_dynamic-update-slice_fusion.4
  22.2 0.9 collective-permute-done.2
  23.3 1.8 %collective-permute-done.4 = bf16[4,64,1024]{2,1,0:T(8,128)(2,1)S(1)} collective-permute-done((bf16[4,64,1024]{2,1,0:T(8,128)(2,1)S(1)}, bf16[4,64,1024]{2,1,0:T(8,128)(2,1)S(1)}, u32[]{:S(2)}, u32[]{:S(2)}) %collective-permute-start.4) | collective-permute-done | bytes 524320 | tf_op jit(solution)/shard_map/ppermute | solution.py:194
  27.5 16.7 %all-gather.2.cloned.1.call-done = bf16[2048,512]{1,0:T(8,128)(2,1)} async-done(((bf16[256,512]{1,0:T(8,128)(2,1)}), bf16[2048,512]{1,0:T(8,128)(2,1)}) %all-gather.2.cloned.1.call-update) | async-done | bytes 2097168 | tf_op jit(solution)/shard_map/all_gather | solution.py:264
  44.2 2.3 %fusion.167 = (bf16[64,2048]{1,0:T(8,128)(2,1)S(1)}, f32[64,2048]{1,0:T(8,128)S(1)}) fusion(bf16[2048,512]{1,0:T(8,128)(2,1)} %all-gather.2.cloned.1.call-done, bf16[4,8,8,128]{3,2,1,0:T(8,128)(2,1)S(1)} %fusion.4), kind=kOutput, calls=%fused_computation.255 | convolution fusion | flops 134348800 | bytes 2949120 | tf_op jit(solution)/shard_map/tc,oc->to/dot_general | solution.py:261
  46.6 1.6 %collective-permute-start.5 = (bf16[64,2048]{1,0:T(8,128)(2,1)S(1)}, bf16[64,2048]{1,0:T(8,128)(2,1)S(1)}, u32[]{:S(2)}, u32[]{:S(2)}) collective-permute-start(bf16[64,2048]{1,0:T(8,128)(2,1)S(1)} %get-tuple-element.23), channel_id=1, source_target_pairs={{0,1},{1,0},{2,3},{3,2},{4,5},{5,4},{6,7},{7,6},{8,9},{9,8},{10,11... | collective-permute-start | bytes 786440 | tf_op jit(solution)/shard_map/ppermute | solution.py:49
  49.1 6.0 %collective-permute-done.5 = bf16[64,2048]{1,0:T(8,128)(2,1)S(1)} collective-permute-done((bf16[64,2048]{1,0:T(8,128)(2,1)S(1)}, bf16[64,2048]{1,0:T(8,128)(2,1)S(1)}, u32[]{:S(2)}, u32[]{:S(2)}) %collective-permute-start.5) | collective-permute-done | bytes 262176 | tf_op jit(solution)/shard_map/ppermute | solution.py:49
  56.7 2.1 %collective-permute-done.6 = bf16[4,48,1024]{2,1,0:T(8,128)(2,1)} collective-permute-done((bf16[4,48,1024]{2,1,0:T(8,128)(2,1)}, bf16[4,48,1024]{2,1,0:T(8,128)(2,1)}, u32[]{:S(2)}, u32[]{:S(2)}) %collective-permute-start.6) | collective-permute-done | bytes 393248 | tf_op jit(solution)/shard_map/ppermute | solution.py:132
  58.8 1.1 fusion.80
  59.9 1.6 %collective-permute-start.7 = (bf16[96,1024]{1,0:T(8,128)(2,1)S(1)}, bf16[96,1024]{1,0:T(8,128)(2,1)S(1)}, u32[]{:S(2)}, u32[]{:S(2)}) collective-permute-start(bf16[96,1024]{1,0:T(8,128)(2,1)S(1)} %bitcast.200), channel_id=1, source_target_pairs={{0,1},{1,0},{2,3},{3,2},{4,5},{5,4},{6,7},{7,6},{8,9},{9,8},{10,11... | collective-permute-start | bytes 589832 | tf_op jit(solution)/shard_map/ppermute | solution.py:49
  61.9 1.4 %collective-permute-start.13 = (bf16[2,48,1024]{2,1,0:T(8,128)(2,1)S(1)}, bf16[2,48,1024]{2,1,0:T(8,128)(2,1)S(1)}, u32[]{:S(2)}, u32[]{:S(2)}) collective-permute-start(bf16[2,48,1024]{2,1,0:T(8,128)(2,1)S(1)} %get-tuple-element.16), channel_id=1, source_target_pairs={{0,8},{2,10},{4,12},{6,14},{8,0},{10,2},{12,4},{14,6},{1,9},{3,11}... | collective-permute-start | bytes 589832 | tf_op jit(solution)/shard_map/ppermute | solution.py:137
  63.3 2.2 %collective-permute-start.17 = (bf16[2,48,1024]{2,1,0:T(8,128)(2,1)S(1)}, bf16[2,48,1024]{2,1,0:T(8,128)(2,1)S(1)}, u32[]{:S(2)}, u32[]{:S(2)}) collective-permute-start(bf16[2,48,1024]{2,1,0:T(8,128)(2,1)S(1)} %get-tuple-element.15), channel_id=1, source_target_pairs={{0,12},{2,14},{4,0},{6,2},{8,4},{10,6},{12,8},{14,10},{1,13},{3,15... | collective-permute-start | bytes 589832 | tf_op jit(solution)/shard_map/ppermute | solution.py:137
  66.2 4.9 %collective-permute-done.9 = bf16[2,48,1024]{2,1,0:T(8,128)(2,1)S(1)} collective-permute-done((bf16[2,48,1024]{2,1,0:T(8,128)(2,1)S(1)}, bf16[2,48,1024]{2,1,0:T(8,128)(2,1)S(1)}, u32[]{:S(2)}, u32[]{:S(2)}) %collective-permute-start.9) | collective-permute-done | bytes 196640 | tf_op jit(solution)/shard_map/ppermute | solution.py:137
  72.7 1.6 %collective-permute-start.8 = (bf16[96,1024]{1,0:T(8,128)(2,1)S(1)}, bf16[96,1024]{1,0:T(8,128)(2,1)S(1)}, u32[]{:S(2)}, u32[]{:S(2)}) collective-permute-start(bf16[96,1024]{1,0:T(8,128)(2,1)S(1)} %convolution_convert_fusion.4), channel_id=1, source_target_pairs={{0,1},{1,0},{2,3},{3,2},{4,5},{5,4},{6,7},{7,6},{8,9},{9,8},{10,11... | collective-permute-start | bytes 589832 | tf_op jit(solution)/shard_map/ppermute | solution.py:49
  74.3 4.3 %collective-permute-done.13 = bf16[2,48,1024]{2,1,0:T(8,128)(2,1)S(1)} collective-permute-done((bf16[2,48,1024]{2,1,0:T(8,128)(2,1)S(1)}, bf16[2,48,1024]{2,1,0:T(8,128)(2,1)S(1)}, u32[]{:S(2)}, u32[]{:S(2)}) %collective-permute-start.13) | collective-permute-done | bytes 196640 | tf_op jit(solution)/shard_map/ppermute | solution.py:137
  79.0 1.5 %collective-permute-start.18 = (bf16[96,1024]{1,0:T(8,128)(2,1)S(1)}, bf16[96,1024]{1,0:T(8,128)(2,1)S(1)}, u32[]{:S(2)}, u32[]{:S(2)}) collective-permute-start(bf16[96,1024]{1,0:T(8,128)(2,1)S(1)} %bitcast.220), channel_id=1, source_target_pairs={{0,1},{1,0},{2,3},{3,2},{4,5},{5,4},{6,7},{7,6},{8,9},{9,8},{10,11... | collective-permute-start | bytes 589832 | tf_op jit(solution)/shard_map/ppermute | solution.py:49
  82.9 3.5 %collective-permute-done.14 = bf16[96,1024]{1,0:T(8,128)(2,1)S(1)} collective-permute-done((bf16[96,1024]{1,0:T(8,128)(2,1)S(1)}, bf16[96,1024]{1,0:T(8,128)(2,1)S(1)}, u32[]{:S(2)}, u32[]{:S(2)}) %collective-permute-start.14) | collective-permute-done | bytes 196640 | tf_op jit(solution)/shard_map/ppermute | solution.py:49
  88.7 1.9 %collective-permute-done.18 = bf16[96,1024]{1,0:T(8,128)(2,1)S(1)} collective-permute-done((bf16[96,1024]{1,0:T(8,128)(2,1)S(1)}, bf16[96,1024]{1,0:T(8,128)(2,1)S(1)}, u32[]{:S(2)}, u32[]{:S(2)}) %collective-permute-start.18) | collective-permute-done | bytes 196640 | tf_op jit(solution)/shard_map/ppermute | solution.py:49
  92.9 1.9 %collective-permute-done.11 = bf16[96,1024]{1,0:T(8,128)(2,1)S(1)} collective-permute-done((bf16[96,1024]{1,0:T(8,128)(2,1)S(1)}, bf16[96,1024]{1,0:T(8,128)(2,1)S(1)}, u32[]{:S(2)}, u32[]{:S(2)}) %collective-permute-start.11) | collective-permute-done | bytes 196640 | tf_op jit(solution)/shard_map/ppermute | solution.py:49
  95.1 4.3 %collective-permute-start.12 = (bf16[2,48,1024]{2,1,0:T(8,128)(2,1)S(1)}, bf16[2,48,1024]{2,1,0:T(8,128)(2,1)S(1)}, u32[]{:S(2)}, u32[]{:S(2)}) collective-permute-start(bf16[2,48,1024]{2,1,0:T(8,128)(2,1)S(1)} %bitcast.229), channel_id=1, source_target_pairs={{0,12},{2,14},{4,0},{6,2},{8,4},{10,6},{12,8},{14,10},{1,13},{3,15... | collective-permute-start | bytes 589832 | tf_op jit(solution)/shard_map/ppermute | solution.py:170
  99.7 4.1 %collective-permute-start.16 = (bf16[2,48,1024]{2,1,0:T(8,128)(2,1)S(1)}, bf16[2,48,1024]{2,1,0:T(8,128)(2,1)S(1)}, u32[]{:S(2)}, u32[]{:S(2)}) collective-permute-start(bf16[2,48,1024]{2,1,0:T(8,128)(2,1)S(1)} %bitcast.230), channel_id=1, source_target_pairs={{0,8},{2,10},{4,12},{6,14},{8,0},{10,2},{12,4},{14,6},{1,9},{3,11}... | collective-permute-start | bytes 589832 | tf_op jit(solution)/shard_map/ppermute | solution.py:170
  104.0 1.8 %collective-permute-start.20 = (bf16[2,48,1024]{2,1,0:T(8,128)(2,1)S(1)}, bf16[2,48,1024]{2,1,0:T(8,128)(2,1)S(1)}, u32[]{:S(2)}, u32[]{:S(2)}) collective-permute-start(bf16[2,48,1024]{2,1,0:T(8,128)(2,1)S(1)} %bitcast.231), channel_id=1, source_target_pairs={{0,4},{2,6},{4,8},{6,10},{8,12},{10,14},{12,0},{14,2},{1,5},{3,7},... | collective-permute-start | bytes 589832 | tf_op jit(solution)/shard_map/ppermute | solution.py:170
  106.2 8.2 %collective-permute-done.16 = bf16[2,48,1024]{2,1,0:T(8,128)(2,1)S(1)} collective-permute-done((bf16[2,48,1024]{2,1,0:T(8,128)(2,1)S(1)}, bf16[2,48,1024]{2,1,0:T(8,128)(2,1)S(1)}, u32[]{:S(2)}, u32[]{:S(2)}) %collective-permute-start.16) | collective-permute-done | bytes 196640 | tf_op jit(solution)/shard_map/ppermute | solution.py:170
  114.7 1.0 copy-done.4
  115.7 0.9 fusion.5
  116.5 0.9 fusion.6
  118.4 4.0 %collective-permute-done.22 = bf16[32,1024]{1,0:T(8,128)(2,1)S(1)} collective-permute-done((bf16[32,1024]{1,0:T(8,128)(2,1)S(1)}, bf16[32,1024]{1,0:T(8,128)(2,1)S(1)}, u32[]{:S(2)}, u32[]{:S(2)}) %collective-permute-start.22) | collective-permute-done | bytes 65568 | tf_op jit(solution)/shard_map/ppermute | solution.py:49
  (112 shorter events, 22.2 us)
Async XLA Ops:
  7.2 65.2 %copy-start = (bf16[1,352,2048]{2,1,0:T(8,128)(2,1)S(1)}, bf16[1,352,2048]{2,1,0:T(8,128)(2,1)}, u32[]{:S(2)}) copy-start(bf16[1,352,2048]{2,1,0:T(8,128)(2,1)} %param.20) | copy-start | bytes 4325380
  7.2 37.1 %all-gather.2.cloned.1.call-start = ((), (), s32[]{:S(2)}) async-start(), calls=%async_computation | async-start | bytes 2359296 | tf_op jit(solution)/shard_map/all_gather | solution.py:264
  8.8 13.4 %collective-permute-start.1 = (bf16[64,1024]{1,0:T(8,128)(2,1)S(1)}, bf16[64,1024]{1,0:T(8,128)(2,1)S(1)}, u32[]{:S(2)}, u32[]{:S(2)}) collective-permute-start(bf16[64,1024]{1,0:T(8,128)(2,1)S(1)} %get-tuple-element.20), channel_id=1, source_target_pairs={{0,4},{2,6},{4,8},{6,10},{8,12},{10,14},{12,0},{14,2},{1,5},{3,7},... | collective-permute-start | bytes 393224 | tf_op jit(solution)/shard_map/ppermute | solution.py:192
  11.9 11.2 %collective-permute-start.2 = (bf16[64,1024]{1,0:T(8,128)(2,1)S(1)}, bf16[64,1024]{1,0:T(8,128)(2,1)S(1)}, u32[]{:S(2)}, u32[]{:S(2)}) collective-permute-start(bf16[64,1024]{1,0:T(8,128)(2,1)S(1)} %get-tuple-element.20), channel_id=1, source_target_pairs={{0,8},{2,10},{4,12},{6,14},{8,0},{10,2},{12,4},{14,6},{1,9},{3,11}... | collective-permute-start | bytes 393224 | tf_op jit(solution)/shard_map/ppermute | solution.py:192
  14.5 8.6 %collective-permute-start.3 = (bf16[64,1024]{1,0:T(8,128)(2,1)S(1)}, bf16[64,1024]{1,0:T(8,128)(2,1)S(1)}, u32[]{:S(2)}, u32[]{:S(2)}) collective-permute-start(bf16[64,1024]{1,0:T(8,128)(2,1)S(1)} %get-tuple-element.20), channel_id=1, source_target_pairs={{0,12},{2,14},{4,0},{6,2},{8,4},{10,6},{12,8},{14,10},{1,13},{3,15... | collective-permute-start | bytes 393224 | tf_op jit(solution)/shard_map/ppermute | solution.py:192
  15.8 33.3 %collective-permute-start = (bf16[32,2048]{1,0:T(8,128)(2,1)}, bf16[32,2048]{1,0:T(8,128)(2,1)S(1)}, u32[]{:S(2)}, u32[]{:S(2)}) collective-permute-start(bf16[32,2048]{1,0:T(8,128)(2,1)} %bitcast.232), channel_id=1, source_target_pairs={{0,1},{1,0},{2,3},{3,2},{4,5},{5,4},{6,7},{7,6},{8,9},{9,8},{10,11... | collective-permute-start | bytes 393224 | tf_op jit(solution)/shard_map/ppermute | solution.py:49
  23.2 2.0 %collective-permute-start.4 = (bf16[4,64,1024]{2,1,0:T(8,128)(2,1)S(1)}, bf16[4,64,1024]{2,1,0:T(8,128)(2,1)S(1)}, u32[]{:S(2)}, u32[]{:S(2)}) collective-permute-start(bf16[4,64,1024]{2,1,0:T(8,128)(2,1)S(1)} %pad_maximum_fusion.2), channel_id=1, source_target_pairs={{0,2},{2,0},{4,6},{6,4},{8,10},{10,8},{12,14},{14,12},{1,3},{3,1},... | collective-permute-start | bytes 1572872 | tf_op jit(solution)/shard_map/ppermute | solution.py:194
  27.5 20.8 %copy-start.8 = (f32[1,64,4]{1,2,0:T(4,128)S(1)}, f32[1,64,4]{1,2,0:T(4,128)}, u32[]{:S(2)}) copy-start(f32[1,64,4]{1,2,0:T(4,128)} %param.22) | copy-start | bytes 3076
  27.5 27.6 %copy-start.6 = (bf16[1,32,2048]{2,1,0:T(8,128)(2,1)S(1)}, bf16[1,32,2048]{2,1,0:T(8,128)(2,1)}, u32[]{:S(2)}) copy-start(bf16[1,32,2048]{2,1,0:T(8,128)(2,1)} %param.15) | copy-start | bytes 393220
  46.6 8.8 %copy-start.7 = (f32[2048]{0:T(1024)S(1)}, f32[2048]{0:T(1024)}, u32[]{:S(2)}) copy-start(f32[2048]{0:T(1024)} %param.17) | copy-start | bytes 24580
  46.6 8.5 %collective-permute-start.5 = (bf16[64,2048]{1,0:T(8,128)(2,1)S(1)}, bf16[64,2048]{1,0:T(8,128)(2,1)S(1)}, u32[]{:S(2)}, u32[]{:S(2)}) collective-permute-start(bf16[64,2048]{1,0:T(8,128)(2,1)S(1)} %get-tuple-element.23), channel_id=1, source_target_pairs={{0,1},{1,0},{2,3},{3,2},{4,5},{5,4},{6,7},{7,6},{8,9},{9,8},{10,11... | collective-permute-start | bytes 786440 | tf_op jit(solution)/shard_map/ppermute | solution.py:49
  55.9 9.6 %copy-start.1 = (bf16[1,2048,352]{1,2,0:T(8,128)(2,1)S(1)}, bf16[1,2048,352]{1,2,0:T(8,128)(2,1)}, u32[]{:S(2)}) copy-start(bf16[1,2048,352]{1,2,0:T(8,128)(2,1)} %param.18) | copy-start | bytes 4325380
  56.7 2.1 %collective-permute-start.6 = (bf16[4,48,1024]{2,1,0:T(8,128)(2,1)}, bf16[4,48,1024]{2,1,0:T(8,128)(2,1)}, u32[]{:S(2)}, u32[]{:S(2)}) collective-permute-start(bf16[4,48,1024]{2,1,0:T(8,128)(2,1)} %bitcast.19), channel_id=1, source_target_pairs={{0,2},{2,0},{4,6},{6,4},{8,10},{10,8},{12,14},{14,12},{1,3},{3,1},... | collective-permute-start | bytes 1179656 | tf_op jit(solution)/shard_map/ppermute | solution.py:132
  56.7 9.1 %copy-start.2 = (bf16[1,2048,352]{1,2,0:T(8,128)(2,1)S(1)}, bf16[1,2048,352]{1,2,0:T(8,128)(2,1)}, u32[]{:S(2)}) copy-start(bf16[1,2048,352]{1,2,0:T(8,128)(2,1)} %param.19) | copy-start | bytes 4325380
  59.9 11.8 %collective-permute-start.7 = (bf16[96,1024]{1,0:T(8,128)(2,1)S(1)}, bf16[96,1024]{1,0:T(8,128)(2,1)S(1)}, u32[]{:S(2)}, u32[]{:S(2)}) collective-permute-start(bf16[96,1024]{1,0:T(8,128)(2,1)S(1)} %bitcast.200), channel_id=1, source_target_pairs={{0,1},{1,0},{2,3},{3,2},{4,5},{5,4},{6,7},{7,6},{8,9},{9,8},{10,11... | collective-permute-start | bytes 589832 | tf_op jit(solution)/shard_map/ppermute | solution.py:49
  61.4 9.7 %collective-permute-start.9 = (bf16[2,48,1024]{2,1,0:T(8,128)(2,1)S(1)}, bf16[2,48,1024]{2,1,0:T(8,128)(2,1)S(1)}, u32[]{:S(2)}, u32[]{:S(2)}) collective-permute-start(bf16[2,48,1024]{2,1,0:T(8,128)(2,1)S(1)} %get-tuple-element.14), channel_id=1, source_target_pairs={{0,4},{2,6},{4,8},{6,10},{8,12},{10,14},{12,0},{14,2},{1,5},{3,7},... | collective-permute-start | bytes 589832 | tf_op jit(solution)/shard_map/ppermute | solution.py:137
  61.9 16.6 %collective-permute-start.13 = (bf16[2,48,1024]{2,1,0:T(8,128)(2,1)S(1)}, bf16[2,48,1024]{2,1,0:T(8,128)(2,1)S(1)}, u32[]{:S(2)}, u32[]{:S(2)}) collective-permute-start(bf16[2,48,1024]{2,1,0:T(8,128)(2,1)S(1)} %get-tuple-element.16), channel_id=1, source_target_pairs={{0,8},{2,10},{4,12},{6,14},{8,0},{10,2},{12,4},{14,6},{1,9},{3,11}... | collective-permute-start | bytes 589832 | tf_op jit(solution)/shard_map/ppermute | solution.py:137
  63.3 15.7 %collective-permute-start.17 = (bf16[2,48,1024]{2,1,0:T(8,128)(2,1)S(1)}, bf16[2,48,1024]{2,1,0:T(8,128)(2,1)S(1)}, u32[]{:S(2)}, u32[]{:S(2)}) collective-permute-start(bf16[2,48,1024]{2,1,0:T(8,128)(2,1)S(1)} %get-tuple-element.15), channel_id=1, source_target_pairs={{0,12},{2,14},{4,0},{6,2},{8,4},{10,6},{12,8},{14,10},{1,13},{3,15... | collective-permute-start | bytes 589832 | tf_op jit(solution)/shard_map/ppermute | solution.py:137
  71.1 9.4 %collective-permute-start.10 = (bf16[96,1024]{1,0:T(8,128)(2,1)S(1)}, bf16[96,1024]{1,0:T(8,128)(2,1)S(1)}, u32[]{:S(2)}, u32[]{:S(2)}) collective-permute-start(bf16[96,1024]{1,0:T(8,128)(2,1)S(1)} %bitcast.226), channel_id=1, source_target_pairs={{0,1},{1,0},{2,3},{3,2},{4,5},{5,4},{6,7},{7,6},{8,9},{9,8},{10,11... | collective-permute-start | bytes 589832 | tf_op jit(solution)/shard_map/ppermute | solution.py:49
  72.7 33.2 %collective-permute-start.8 = (bf16[96,1024]{1,0:T(8,128)(2,1)S(1)}, bf16[96,1024]{1,0:T(8,128)(2,1)S(1)}, u32[]{:S(2)}, u32[]{:S(2)}) collective-permute-start(bf16[96,1024]{1,0:T(8,128)(2,1)S(1)} %convolution_convert_fusion.4), channel_id=1, source_target_pairs={{0,1},{1,0},{2,3},{3,2},{4,5},{5,4},{6,7},{7,6},{8,9},{9,8},{10,11... | collective-permute-start | bytes 589832 | tf_op jit(solution)/shard_map/ppermute | solution.py:49
  78.5 7.8 %collective-permute-start.14 = (bf16[96,1024]{1,0:T(8,128)(2,1)S(1)}, bf16[96,1024]{1,0:T(8,128)(2,1)S(1)}, u32[]{:S(2)}, u32[]{:S(2)}) collective-permute-start(bf16[96,1024]{1,0:T(8,128)(2,1)S(1)} %bitcast.223), channel_id=1, source_target_pairs={{0,1},{1,0},{2,3},{3,2},{4,5},{5,4},{6,7},{7,6},{8,9},{9,8},{10,11... | collective-permute-start | bytes 589832 | tf_op jit(solution)/shard_map/ppermute | solution.py:49
  79.0 11.5 %collective-permute-start.18 = (bf16[96,1024]{1,0:T(8,128)(2,1)S(1)}, bf16[96,1024]{1,0:T(8,128)(2,1)S(1)}, u32[]{:S(2)}, u32[]{:S(2)}) collective-permute-start(bf16[96,1024]{1,0:T(8,128)(2,1)S(1)} %bitcast.220), channel_id=1, source_target_pairs={{0,1},{1,0},{2,3},{3,2},{4,5},{5,4},{6,7},{7,6},{8,9},{9,8},{10,11... | collective-permute-start | bytes 589832 | tf_op jit(solution)/shard_map/ppermute | solution.py:49
  82.3 12.4 %collective-permute-start.11 = (bf16[96,1024]{1,0:T(8,128)(2,1)S(1)}, bf16[96,1024]{1,0:T(8,128)(2,1)S(1)}, u32[]{:S(2)}, u32[]{:S(2)}) collective-permute-start(bf16[96,1024]{1,0:T(8,128)(2,1)S(1)} %convolution_convert_fusion.3), channel_id=1, source_target_pairs={{0,1},{1,0},{2,3},{3,2},{4,5},{5,4},{6,7},{7,6},{8,9},{9,8},{10,11... | collective-permute-start | bytes 589832 | tf_op jit(solution)/shard_map/ppermute | solution.py:49
  88.1 11.2 %collective-permute-start.15 = (bf16[96,1024]{1,0:T(8,128)(2,1)S(1)}, bf16[96,1024]{1,0:T(8,128)(2,1)S(1)}, u32[]{:S(2)}, u32[]{:S(2)}) collective-permute-start(bf16[96,1024]{1,0:T(8,128)(2,1)S(1)} %convolution_convert_fusion.2), channel_id=1, source_target_pairs={{0,1},{1,0},{2,3},{3,2},{4,5},{5,4},{6,7},{7,6},{8,9},{9,8},{10,11... | collective-permute-start | bytes 589832 | tf_op jit(solution)/shard_map/ppermute | solution.py:49
  92.4 11.4 %collective-permute-start.19 = (bf16[96,1024]{1,0:T(8,128)(2,1)S(1)}, bf16[96,1024]{1,0:T(8,128)(2,1)S(1)}, u32[]{:S(2)}, u32[]{:S(2)}) collective-permute-start(bf16[96,1024]{1,0:T(8,128)(2,1)S(1)} %convolution_convert_fusion.1), channel_id=1, source_target_pairs={{0,1},{1,0},{2,3},{3,2},{4,5},{5,4},{6,7},{7,6},{8,9},{9,8},{10,11... | collective-permute-start | bytes 589832 | tf_op jit(solution)/shard_map/ppermute | solution.py:49
  95.1 11.1 %collective-permute-start.12 = (bf16[2,48,1024]{2,1,0:T(8,128)(2,1)S(1)}, bf16[2,48,1024]{2,1,0:T(8,128)(2,1)S(1)}, u32[]{:S(2)}, u32[]{:S(2)}) collective-permute-start(bf16[2,48,1024]{2,1,0:T(8,128)(2,1)S(1)} %bitcast.229), channel_id=1, source_target_pairs={{0,12},{2,14},{4,0},{6,2},{8,4},{10,6},{12,8},{14,10},{1,13},{3,15... | collective-permute-start | bytes 589832 | tf_op jit(solution)/shard_map/ppermute | solution.py:170
  99.7 14.8 %collective-permute-start.16 = (bf16[2,48,1024]{2,1,0:T(8,128)(2,1)S(1)}, bf16[2,48,1024]{2,1,0:T(8,128)(2,1)S(1)}, u32[]{:S(2)}, u32[]{:S(2)}) collective-permute-start(bf16[2,48,1024]{2,1,0:T(8,128)(2,1)S(1)} %bitcast.230), channel_id=1, source_target_pairs={{0,8},{2,10},{4,12},{6,14},{8,0},{10,2},{12,4},{14,6},{1,9},{3,11}... | collective-permute-start | bytes 589832 | tf_op jit(solution)/shard_map/ppermute | solution.py:170
  104.0 10.4 %collective-permute-start.20 = (bf16[2,48,1024]{2,1,0:T(8,128)(2,1)S(1)}, bf16[2,48,1024]{2,1,0:T(8,128)(2,1)S(1)}, u32[]{:S(2)}, u32[]{:S(2)}) collective-permute-start(bf16[2,48,1024]{2,1,0:T(8,128)(2,1)S(1)} %bitcast.231), channel_id=1, source_target_pairs={{0,4},{2,6},{4,8},{6,10},{8,12},{10,14},{12,0},{14,2},{1,5},{3,7},... | collective-permute-start | bytes 589832 | tf_op jit(solution)/shard_map/ppermute | solution.py:170
  114.4 1.2 copy-start.4
  114.6 2.9 %copy-start.5 = (f32[384,64]{0,1:T(8,128)S(1)}, f32[384,64]{0,1:T(8,128)}, u32[]{:S(2)}) copy-start(f32[384,64]{0,1:T(8,128)} %get-tuple-element.4) | copy-start | bytes 294916
  114.6 2.8 %collective-permute-start.21 = (bf16[4,48,1024]{2,1,0:T(8,128)(2,1)S(1)}, bf16[4,48,1024]{2,1,0:T(8,128)(2,1)S(1)}, u32[]{:S(2)}, u32[]{:S(2)}) collective-permute-start(bf16[4,48,1024]{2,1,0:T(8,128)(2,1)S(1)} %get-tuple-element.12), channel_id=1, source_target_pairs={{0,2},{2,0},{4,6},{6,4},{8,10},{10,8},{12,14},{14,12},{1,3},{3,1},... | collective-permute-start | bytes 1179656 | tf_op jit(solution)/shard_map/ppermute | solution.py:172
  118.0 4.3 %collective-permute-start.22 = (bf16[32,1024]{1,0:T(8,128)(2,1)S(1)}, bf16[32,1024]{1,0:T(8,128)(2,1)S(1)}, u32[]{:S(2)}, u32[]{:S(2)}) collective-permute-start(bf16[32,1024]{1,0:T(8,128)(2,1)S(1)} %select_convert_fusion), channel_id=1, source_target_pairs={{0,1},{1,0},{2,3},{3,2},{4,5},{5,4},{6,7},{7,6},{8,9},{9,8},{10,11... | collective-permute-start | bytes 196616 | tf_op jit(solution)/shard_map/ppermute | solution.py:49
  (1 other events, 1.0 us)
Sparse Core Ops, SparseCore 0:
  9.6 34.5 all-gather.1

commit v15 on v14

--- a/solution.py
+++ b/solution.py
@@ -146,22 +146,28 @@
     per_group = 1 if n_chip <= 4 else n_chip // 2
     n_groups = n_chip // per_group
     returned = [None] * n_chip
+    split_cores = n_chip <= 4
     for group in range(n_groups):
         shifts = range(group * per_group, (group + 1) * per_group)
-        block = jnp.concatenate([arrived[k] for k in shifts], axis=0).reshape(-1, half_d)
-        partner_cols = exp_swap(block)
-        gate_act = jnp.dot(block, gate_mine, preferred_element_type=jnp.float32) + jnp.dot(
-            partner_cols, gate_other, preferred_element_type=jnp.float32
-        )
-        up_act = jnp.dot(block, up_mine, preferred_element_type=jnp.float32) + jnp.dot(
-            partner_cols, up_other, preferred_element_type=jnp.float32
-        )
-        hidden = (jax.nn.silu(gate_act) * up_act).astype(jnp.bfloat16)
-        out_other = jnp.dot(hidden, down_other, preferred_element_type=jnp.float32)
-        got_other = exp_swap(out_other.astype(jnp.bfloat16))
-        out_mine = jnp.dot(hidden, down_mine, preferred_element_type=jnp.float32)
-        summed = (out_mine + got_other.astype(jnp.float32)).astype(jnp.bfloat16)
-        summed = summed.reshape(per_group, 2, capacity, half_d)
+        if split_cores:
+            pieces = [arrived[k][side] for k in shifts for side in range(2)]
+        else:
+            pieces = [jnp.concatenate([arrived[k] for k in shifts], axis=0).reshape(-1, half_d)]
+        outs = []
+        for block in pieces:
+            partner_cols = exp_swap(block)
+            gate_act = jnp.dot(block, gate_mine, preferred_element_type=jnp.float32) + jnp.dot(
+                partner_cols, gate_other, preferred_element_type=jnp.float32
+            )
+            up_act = jnp.dot(block, up_mine, preferred_element_type=jnp.float32) + jnp.dot(
+                partner_cols, up_other, preferred_element_type=jnp.float32
+            )
+            hidden = (jax.nn.silu(gate_act) * up_act).astype(jnp.bfloat16)
+            out_other = jnp.dot(hidden, down_other, preferred_element_type=jnp.float32)
+            got_other = exp_swap(out_other.astype(jnp.bfloat16))
+            out_mine = jnp.dot(hidden, down_mine, preferred_element_type=jnp.float32)
+            outs.append((out_mine + got_other.astype(jnp.float32)).astype(jnp.bfloat16))
+        summed = jnp.concatenate(outs, axis=0).reshape(per_group, 2, capacity, half_d)
         for idx, shift in enumerate(shifts):
             if shift == 0:
                 returned[shift] = summed[idx]

time: 130 us -> 138 us (1.062)
  starting transfers between devices: 32.3 us -> 41.2 us
  matrix products: 13.7 us -> 20.6 us
  waiting for transfers between devices: 56.8 us -> 50.5 us
  other arithmetic: 6.37 us -> 4.73 us
    ppermute x11 -> x19, starting transfers between devices: 10.8 us -> 22.6 us  [exp_swap(): return lax.ppermute(x, 'exp', perm=[(0, 1), (1, 0)])]
    ppermute x3, waiting for transfers between devices: 9.17 us -> 5.76 us  [moe_column_halves(): arrived.append(lax.ppermute(pairs[shift], 'ctx', perm=perm))]
    ppermute x3, starting transfers between devices: 10.2 us -> 7.19 us  [moe_column_halves(): returned[shift] = lax.ppermute(summed[idx], 'ctx', perm=perm)]
    ppermute x11 -> x19, waiting for transfers between devices: 17.2 us -> 15 us  [exp_swap(): return lax.ppermute(x, 'exp', perm=[(0, 1), (1, 0)])]
    ppermute x1, waiting for transfers between devices: 2.06 us -> 0.01 us  [moe_column_halves(): from_partner = lax.ppermute(send_rows[1], 'ctx', perm=core_swap)]
    ppermute x3, waiting for transfers between devices: 8.24 us -> 9.63 us  [moe_column_halves(): returned[shift] = lax.ppermute(summed[idx], 'ctx', perm=perm)]
    dot_general x4 -> x8, matrix products: 1.46 us -> 2.79 us  [moe_column_halves(): jnp.dot(block, up_mine, preferred_element_type=jnp.float32)]
    dot_general x4 -> x8, matrix products: 1.45 us -> 2.77 us  [moe_column_halves(): jnp.dot(block, gate_mine, preferred_element_type=jnp.float32)]
  transfers between devices with their start and end apart: 24 -> 32, of which waited for: 12 -> 11; matrix products, arithmetic and copies ran while one was open for 15% -> 19% of each run, Pallas kernels for 0% -> 0%
where the time goes in v15:
time: 138 us; the launch traced here: 137 us
  waiting for transfers between devices  50.5 us (37%)
  starting transfers between devices  41.2 us (30%)
  matrix products  20.6 us (15%)
  between operations  15.5 us (11%)
  local copies, waits for them, and re-layouts  4.94 us (4%)
  other arithmetic  4.73 us (3%)
    ppermute x19, starting transfers between devices, exp_swap(): return lax.ppermute(x, 'exp', perm=[(0, 1), (1, 0)])  22.6 us
    all_gather x1, waiting for transfers between devices, local(): lax.all_gather(out_weight, 'ctx', axis=0, tiled=True)  16.7 us
    ppermute x19, waiting for transfers between devices, exp_swap(): return lax.ppermute(x, 'exp', perm=[(0, 1), (1, 0)])  15 us
    ppermute x3, waiting for transfers between devices, moe_column_halves(): returned[shift] = lax.ppermute(summed[idx], 'ctx', perm=perm)  9.63 us
    ppermute x3, starting transfers between devices, moe_column_halves(): returned[shift] = lax.ppermute(summed[idx], 'ctx', perm=perm)  7.19 us
    ppermute x3, starting transfers between devices, ctx_gather_blocks(): stack.append(lax.ppermute(rows, 'ctx', perm=perm))  7.03 us
    ppermute x3, waiting for transfers between devices, moe_column_halves(): arrived.append(lax.ppermute(pairs[shift], 'ctx', perm=perm))  5.76 us
    ppermute x3, starting transfers between devices, moe_column_halves(): arrived.append(lax.ppermute(pairs[shift], 'ctx', perm=perm))  4.07 us
  transfers between devices with their start and end apart: 32, of which 11 were waited for; matrix products, arithmetic and copies ran while one was open for 19% of the time, Pallas kernels for 0%

profile of v15, /device:TPU:0, one launch (start us, length us, event | category | flops | bytes accessed | tf_op | source)
XLA Modules:
  0.0 137.5 jit_solution(16913183355729350550)
XLA Ops:
  7.9 0.9 fusion.259
  8.8 3.1 %collective-permute-start.1 = (bf16[64,1024]{1,0:T(8,128)(2,1)S(1)}, bf16[64,1024]{1,0:T(8,128)(2,1)S(1)}, u32[]{:S(2)}, u32[]{:S(2)}) collective-permute-start(bf16[64,1024]{1,0:T(8,128)(2,1)S(1)} %get-tuple-element.25), channel_id=1, source_target_pairs={{0,4},{2,6},{4,8},{6,10},{8,12},{10,14},{12,0},{14,2},{1,5},{3,7},... | collective-permute-start | bytes 393224 | tf_op jit(solution)/shard_map/ppermute | solution.py:198
  11.9 2.6 %collective-permute-start.2 = (bf16[64,1024]{1,0:T(8,128)(2,1)S(1)}, bf16[64,1024]{1,0:T(8,128)(2,1)S(1)}, u32[]{:S(2)}, u32[]{:S(2)}) collective-permute-start(bf16[64,1024]{1,0:T(8,128)(2,1)S(1)} %get-tuple-element.25), channel_id=1, source_target_pairs={{0,8},{2,10},{4,12},{6,14},{8,0},{10,2},{12,4},{14,6},{1,9},{3,11}... | collective-permute-start | bytes 393224 | tf_op jit(solution)/shard_map/ppermute | solution.py:198
  14.5 1.4 collective-permute-start.3
  15.8 1.5 %collective-permute-start = (bf16[32,2048]{1,0:T(8,128)(2,1)}, bf16[32,2048]{1,0:T(8,128)(2,1)S(1)}, u32[]{:S(2)}, u32[]{:S(2)}) collective-permute-start(bf16[32,2048]{1,0:T(8,128)(2,1)} %bitcast.316), channel_id=1, source_target_pairs={{0,1},{1,0},{2,3},{3,2},{4,5},{5,4},{6,7},{7,6},{8,9},{9,8},{10,11... | collective-permute-start | bytes 393224 | tf_op jit(solution)/shard_map/ppermute | solution.py:49
  22.2 0.9 collective-permute-done.2
  23.3 1.8 %collective-permute-done.4 = bf16[4,64,1024]{2,1,0:T(8,128)(2,1)S(1)} collective-permute-done((bf16[4,64,1024]{2,1,0:T(8,128)(2,1)S(1)}, bf16[4,64,1024]{2,1,0:T(8,128)(2,1)S(1)}, u32[]{:S(2)}, u32[]{:S(2)}) %collective-permute-start.4) | collective-permute-done | bytes 524320 | tf_op jit(solution)/shard_map/ppermute | solution.py:200
  27.6 16.7 %all-gather.2.cloned.1.call-done = bf16[2048,512]{1,0:T(8,128)(2,1)} async-done(((bf16[256,512]{1,0:T(8,128)(2,1)}), bf16[2048,512]{1,0:T(8,128)(2,1)}) %all-gather.2.cloned.1.call-update) | async-done | bytes 2097168 | tf_op jit(solution)/shard_map/all_gather | solution.py:270
  44.2 2.3 %fusion.264 = (bf16[64,2048]{1,0:T(8,128)(2,1)S(1)}, f32[64,2048]{1,0:T(8,128)S(1)}) fusion(bf16[2048,512]{1,0:T(8,128)(2,1)} %all-gather.2.cloned.1.call-done, bf16[4,8,8,128]{3,2,1,0:T(8,128)(2,1)S(1)} %fusion.5), kind=kOutput, calls=%fused_computation.364 | convolution fusion | flops 134348800 | bytes 2949120 | tf_op jit(solution)/shard_map/tc,oc->to/dot_general | solution.py:267
  46.6 1.6 %collective-permute-start.5 = (bf16[64,2048]{1,0:T(8,128)(2,1)S(1)}, bf16[64,2048]{1,0:T(8,128)(2,1)S(1)}, u32[]{:S(2)}, u32[]{:S(2)}) collective-permute-start(bf16[64,2048]{1,0:T(8,128)(2,1)S(1)} %get-tuple-element.28), channel_id=1, source_target_pairs={{0,1},{1,0},{2,3},{3,2},{4,5},{5,4},{6,7},{7,6},{8,9},{9,8},{10,11... | collective-permute-start | bytes 786440 | tf_op jit(solution)/shard_map/ppermute | solution.py:49
  48.5 6.6 %collective-permute-done.5 = bf16[64,2048]{1,0:T(8,128)(2,1)S(1)} collective-permute-done((bf16[64,2048]{1,0:T(8,128)(2,1)S(1)}, bf16[64,2048]{1,0:T(8,128)(2,1)S(1)}, u32[]{:S(2)}, u32[]{:S(2)}) %collective-permute-start.5) | collective-permute-done | bytes 262176 | tf_op jit(solution)/shard_map/ppermute | solution.py:49
  56.0 1.6 %collective-permute-start.6 = (bf16[48,1024]{1,0:T(8,128)(2,1)S(1)}, bf16[48,1024]{1,0:T(8,128)(2,1)S(1)}, u32[]{:S(2)}, u32[]{:S(2)}) collective-permute-start(bf16[48,1024]{1,0:T(8,128)(2,1)S(1)} %slice.119), channel_id=1, source_target_pairs={{0,1},{1,0},{2,3},{3,2},{4,5},{5,4},{6,7},{7,6},{8,9},{9,8},{10,11... | collective-permute-start | bytes 294920 | tf_op jit(solution)/shard_map/ppermute | solution.py:49
  58.4 2.3 %collective-permute-done.6 = bf16[48,1024]{1,0:T(8,128)(2,1)S(1)} collective-permute-done((bf16[48,1024]{1,0:T(8,128)(2,1)S(1)}, bf16[48,1024]{1,0:T(8,128)(2,1)S(1)}, u32[]{:S(2)}, u32[]{:S(2)}) %collective-permute-start.6) | collective-permute-done | bytes 98336 | tf_op jit(solution)/shard_map/ppermute | solution.py:49
  61.6 1.6 %collective-permute-start.7 = (bf16[48,1024]{1,0:T(8,128)(2,1)S(1)}, bf16[48,1024]{1,0:T(8,128)(2,1)S(1)}, u32[]{:S(2)}, u32[]{:S(2)}) collective-permute-start(bf16[48,1024]{1,0:T(8,128)(2,1)S(1)} %convolution_convert_fusion.8), channel_id=1, source_target_pairs={{0,1},{1,0},{2,3},{3,2},{4,5},{5,4},{6,7},{7,6},{8,9},{9,8},{10,11... | collective-permute-start | bytes 294920 | tf_op jit(solution)/shard_map/ppermute | solution.py:49
  63.2 3.1 %collective-permute-done.7 = bf16[48,1024]{1,0:T(8,128)(2,1)S(1)} collective-permute-done((bf16[48,1024]{1,0:T(8,128)(2,1)S(1)}, bf16[48,1024]{1,0:T(8,128)(2,1)S(1)}, u32[]{:S(2)}, u32[]{:S(2)}) %collective-permute-start.7) | collective-permute-done | bytes 98336 | tf_op jit(solution)/shard_map/ppermute | solution.py:49
  66.6 1.6 %collective-permute-start.9 = (bf16[48,1024]{1,0:T(8,128)(2,1)S(1)}, bf16[48,1024]{1,0:T(8,128)(2,1)S(1)}, u32[]{:S(2)}, u32[]{:S(2)}) collective-permute-start(bf16[48,1024]{1,0:T(8,128)(2,1)S(1)} %slice_bitcast_fusion.8), channel_id=1, source_target_pairs={{0,1},{1,0},{2,3},{3,2},{4,5},{5,4},{6,7},{7,6},{8,9},{9,8},{10,11... | collective-permute-start | bytes 294920 | tf_op jit(solution)/shard_map/ppermute | solution.py:49
  68.8 1.4 collective-permute-start.17
  70.1 2.2 %collective-permute-start.23 = (bf16[2,48,1024]{2,1,0:T(8,128)(2,1)S(1)}, bf16[2,48,1024]{2,1,0:T(8,128)(2,1)S(1)}, u32[]{:S(2)}, u32[]{:S(2)}) collective-permute-start(bf16[2,48,1024]{2,1,0:T(8,128)(2,1)S(1)} %get-tuple-element.15), channel_id=1, source_target_pairs={{0,12},{2,14},{4,0},{6,2},{8,4},{10,6},{12,8},{14,10},{1,13},{3,15... | collective-permute-start | bytes 589832 | tf_op jit(solution)/shard_map/ppermute | solution.py:137
  74.5 3.5 %collective-permute-done.11 = bf16[2,48,1024]{2,1,0:T(8,128)(2,1)S(1)} collective-permute-done((bf16[2,48,1024]{2,1,0:T(8,128)(2,1)S(1)}, bf16[2,48,1024]{2,1,0:T(8,128)(2,1)S(1)}, u32[]{:S(2)}, u32[]{:S(2)}) %collective-permute-start.11) | collective-permute-done | bytes 196640 | tf_op jit(solution)/shard_map/ppermute | solution.py:137
  78.6 1.5 %collective-permute-start.14 = (bf16[48,1024]{1,0:T(8,128)(2,1)S(1)}, bf16[48,1024]{1,0:T(8,128)(2,1)S(1)}, u32[]{:S(2)}, u32[]{:S(2)}) collective-permute-start(bf16[48,1024]{1,0:T(8,128)(2,1)S(1)} %get-tuple-element.19), channel_id=1, source_target_pairs={{0,1},{1,0},{2,3},{3,2},{4,5},{5,4},{6,7},{7,6},{8,9},{9,8},{10,11... | collective-permute-start | bytes 294920 | tf_op jit(solution)/shard_map/ppermute | solution.py:49
  80.1 2.3 %collective-permute-done.17 = bf16[2,48,1024]{2,1,0:T(8,128)(2,1)S(1)} collective-permute-done((bf16[2,48,1024]{2,1,0:T(8,128)(2,1)S(1)}, bf16[2,48,1024]{2,1,0:T(8,128)(2,1)S(1)}, u32[]{:S(2)}, u32[]{:S(2)}) %collective-permute-start.17) | collective-permute-done | bytes 196640 | tf_op jit(solution)/shard_map/ppermute | solution.py:137
  83.0 1.5 %collective-permute-start.20 = (bf16[48,1024]{1,0:T(8,128)(2,1)S(1)}, bf16[48,1024]{1,0:T(8,128)(2,1)S(1)}, u32[]{:S(2)}, u32[]{:S(2)}) collective-permute-start(bf16[48,1024]{1,0:T(8,128)(2,1)S(1)} %get-tuple-element.21), channel_id=1, source_target_pairs={{0,1},{1,0},{2,3},{3,2},{4,5},{5,4},{6,7},{7,6},{8,9},{9,8},{10,11... | collective-permute-start | bytes 294920 | tf_op jit(solution)/shard_map/ppermute | solution.py:49
  86.8 1.6 %collective-permute-start.26 = (bf16[48,1024]{1,0:T(8,128)(2,1)S(1)}, bf16[48,1024]{1,0:T(8,128)(2,1)S(1)}, u32[]{:S(2)}, u32[]{:S(2)}) collective-permute-start(bf16[48,1024]{1,0:T(8,128)(2,1)S(1)} %get-tuple-element.23), channel_id=1, source_target_pairs={{0,1},{1,0},{2,3},{3,2},{4,5},{5,4},{6,7},{7,6},{8,9},{9,8},{10,11... | collective-permute-start | bytes 294920 | tf_op jit(solution)/shard_map/ppermute | solution.py:49
  92.3 1.6 %collective-permute-start.15 = (bf16[48,1024]{1,0:T(8,128)(2,1)S(1)}, bf16[48,1024]{1,0:T(8,128)(2,1)S(1)}, u32[]{:S(2)}, u32[]{:S(2)}) collective-permute-start(bf16[48,1024]{1,0:T(8,128)(2,1)S(1)} %convolution_convert_fusion.5), channel_id=1, source_target_pairs={{0,1},{1,0},{2,3},{3,2},{4,5},{5,4},{6,7},{7,6},{8,9},{9,8},{10,11... | collective-permute-start | bytes 294920 | tf_op jit(solution)/shard_map/ppermute | solution.py:49
  97.8 1.6 %collective-permute-start.21 = (bf16[48,1024]{1,0:T(8,128)(2,1)S(1)}, bf16[48,1024]{1,0:T(8,128)(2,1)S(1)}, u32[]{:S(2)}, u32[]{:S(2)}) collective-permute-start(bf16[48,1024]{1,0:T(8,128)(2,1)S(1)} %convolution_convert_fusion.3), channel_id=1, source_target_pairs={{0,1},{1,0},{2,3},{3,2},{4,5},{5,4},{6,7},{7,6},{8,9},{9,8},{10,11... | collective-permute-start | bytes 294920 | tf_op jit(solution)/shard_map/ppermute | solution.py:49
  101.9 1.6 %collective-permute-start.27 = (bf16[48,1024]{1,0:T(8,128)(2,1)S(1)}, bf16[48,1024]{1,0:T(8,128)(2,1)S(1)}, u32[]{:S(2)}, u32[]{:S(2)}) collective-permute-start(bf16[48,1024]{1,0:T(8,128)(2,1)S(1)} %convolution_convert_fusion.1), channel_id=1, source_target_pairs={{0,1},{1,0},{2,3},{3,2},{4,5},{5,4},{6,7},{7,6},{8,9},{9,8},{10,11... | collective-permute-start | bytes 294920 | tf_op jit(solution)/shard_map/ppermute | solution.py:49
  103.8 4.5 %collective-permute-start.16 = (bf16[2,48,1024]{2,1,0:T(8,128)(2,1)S(1)}, bf16[2,48,1024]{2,1,0:T(8,128)(2,1)S(1)}, u32[]{:S(2)}, u32[]{:S(2)}) collective-permute-start(bf16[2,48,1024]{2,1,0:T(8,128)(2,1)S(1)} %bitcast.313), channel_id=1, source_target_pairs={{0,12},{2,14},{4,0},{6,2},{8,4},{10,6},{12,8},{14,10},{1,13},{3,15... | collective-permute-start | bytes 589832 | tf_op jit(solution)/shard_map/ppermute | solution.py:176
  110.0 2.1 %collective-permute-start.28 = (bf16[2,48,1024]{2,1,0:T(8,128)(2,1)S(1)}, bf16[2,48,1024]{2,1,0:T(8,128)(2,1)S(1)}, u32[]{:S(2)}, u32[]{:S(2)}) collective-permute-start(bf16[2,48,1024]{2,1,0:T(8,128)(2,1)S(1)} %bitcast.315), channel_id=1, source_target_pairs={{0,4},{2,6},{4,8},{6,10},{8,12},{10,14},{12,0},{14,2},{1,5},{3,7},... | collective-permute-start | bytes 589832 | tf_op jit(solution)/shard_map/ppermute | solution.py:176
  113.0 9.0 %collective-permute-done.22 = bf16[2,48,1024]{2,1,0:T(8,128)(2,1)S(1)} collective-permute-done((bf16[2,48,1024]{2,1,0:T(8,128)(2,1)S(1)}, bf16[2,48,1024]{2,1,0:T(8,128)(2,1)S(1)}, u32[]{:S(2)}, u32[]{:S(2)}) %collective-permute-start.22) | collective-permute-done | bytes 196640 | tf_op jit(solution)/shard_map/ppermute | solution.py:176
  122.2 1.0 copy-done.4
  125.6 1.4 %collective-permute-start.30 = (bf16[32,1024]{1,0:T(8,128)(2,1)S(1)}, bf16[32,1024]{1,0:T(8,128)(2,1)S(1)}, u32[]{:S(2)}, u32[]{:S(2)}) collective-permute-start(bf16[32,1024]{1,0:T(8,128)(2,1)S(1)} %select_convert_fusion), channel_id=1, source_target_pairs={{0,1},{1,0},{2,3},{3,2},{4,5},{5,4},{6,7},{7,6},{8,9},{9,8},{10,11... | collective-permute-start | bytes 196616 | tf_op jit(solution)/shard_map/ppermute | solution.py:49
  127.0 2.9 %collective-permute-done.30 = bf16[32,1024]{1,0:T(8,128)(2,1)S(1)} collective-permute-done((bf16[32,1024]{1,0:T(8,128)(2,1)S(1)}, bf16[32,1024]{1,0:T(8,128)(2,1)S(1)}, u32[]{:S(2)}, u32[]{:S(2)}) %collective-permute-start.30) | collective-permute-done | bytes 65568 | tf_op jit(solution)/shard_map/ppermute | solution.py:49
  (159 shorter events, 32.9 us)
Async XLA Ops:
  7.2 37.1 %all-gather.2.cloned.1.call-start = ((), (), s32[]{:S(2)}) async-start(), calls=%async_computation | async-start | bytes 2359296 | tf_op jit(solution)/shard_map/all_gather | solution.py:270
  8.8 13.4 %collective-permute-start.1 = (bf16[64,1024]{1,0:T(8,128)(2,1)S(1)}, bf16[64,1024]{1,0:T(8,128)(2,1)S(1)}, u32[]{:S(2)}, u32[]{:S(2)}) collective-permute-start(bf16[64,1024]{1,0:T(8,128)(2,1)S(1)} %get-tuple-element.25), channel_id=1, source_target_pairs={{0,4},{2,6},{4,8},{6,10},{8,12},{10,14},{12,0},{14,2},{1,5},{3,7},... | collective-permute-start | bytes 393224 | tf_op jit(solution)/shard_map/ppermute | solution.py:198
  11.9 11.2 %collective-permute-start.2 = (bf16[64,1024]{1,0:T(8,128)(2,1)S(1)}, bf16[64,1024]{1,0:T(8,128)(2,1)S(1)}, u32[]{:S(2)}, u32[]{:S(2)}) collective-permute-start(bf16[64,1024]{1,0:T(8,128)(2,1)S(1)} %get-tuple-element.25), channel_id=1, source_target_pairs={{0,8},{2,10},{4,12},{6,14},{8,0},{10,2},{12,4},{14,6},{1,9},{3,11}... | collective-permute-start | bytes 393224 | tf_op jit(solution)/shard_map/ppermute | solution.py:198
  14.5 8.6 %collective-permute-start.3 = (bf16[64,1024]{1,0:T(8,128)(2,1)S(1)}, bf16[64,1024]{1,0:T(8,128)(2,1)S(1)}, u32[]{:S(2)}, u32[]{:S(2)}) collective-permute-start(bf16[64,1024]{1,0:T(8,128)(2,1)S(1)} %get-tuple-element.25), channel_id=1, source_target_pairs={{0,12},{2,14},{4,0},{6,2},{8,4},{10,6},{12,8},{14,10},{1,13},{3,15... | collective-permute-start | bytes 393224 | tf_op jit(solution)/shard_map/ppermute | solution.py:198
  15.8 32.6 %collective-permute-start = (bf16[32,2048]{1,0:T(8,128)(2,1)}, bf16[32,2048]{1,0:T(8,128)(2,1)S(1)}, u32[]{:S(2)}, u32[]{:S(2)}) collective-permute-start(bf16[32,2048]{1,0:T(8,128)(2,1)} %bitcast.316), channel_id=1, source_target_pairs={{0,1},{1,0},{2,3},{3,2},{4,5},{5,4},{6,7},{7,6},{8,9},{9,8},{10,11... | collective-permute-start | bytes 393224 | tf_op jit(solution)/shard_map/ppermute | solution.py:49
  23.2 2.0 %collective-permute-start.4 = (bf16[4,64,1024]{2,1,0:T(8,128)(2,1)S(1)}, bf16[4,64,1024]{2,1,0:T(8,128)(2,1)S(1)}, u32[]{:S(2)}, u32[]{:S(2)}) collective-permute-start(bf16[4,64,1024]{2,1,0:T(8,128)(2,1)S(1)} %pad_maximum_fusion.2), channel_id=1, source_target_pairs={{0,2},{2,0},{4,6},{6,4},{8,10},{10,8},{12,14},{14,12},{1,3},{3,1},... | collective-permute-start | bytes 1572872 | tf_op jit(solution)/shard_map/ppermute | solution.py:200
  46.6 8.5 %collective-permute-start.5 = (bf16[64,2048]{1,0:T(8,128)(2,1)S(1)}, bf16[64,2048]{1,0:T(8,128)(2,1)S(1)}, u32[]{:S(2)}, u32[]{:S(2)}) collective-permute-start(bf16[64,2048]{1,0:T(8,128)(2,1)S(1)} %get-tuple-element.28), channel_id=1, source_target_pairs={{0,1},{1,0},{2,3},{3,2},{4,5},{5,4},{6,7},{7,6},{8,9},{9,8},{10,11... | collective-permute-start | bytes 786440 | tf_op jit(solution)/shard_map/ppermute | solution.py:49
  56.0 4.7 %collective-permute-start.6 = (bf16[48,1024]{1,0:T(8,128)(2,1)S(1)}, bf16[48,1024]{1,0:T(8,128)(2,1)S(1)}, u32[]{:S(2)}, u32[]{:S(2)}) collective-permute-start(bf16[48,1024]{1,0:T(8,128)(2,1)S(1)} %slice.119), channel_id=1, source_target_pairs={{0,1},{1,0},{2,3},{3,2},{4,5},{5,4},{6,7},{7,6},{8,9},{9,8},{10,11... | collective-permute-start | bytes 294920 | tf_op jit(solution)/shard_map/ppermute | solution.py:49
  58.3 8.3 %collective-permute-start.8 = (bf16[4,48,1024]{2,1,0:T(8,128)(2,1)S(1)}, bf16[4,48,1024]{2,1,0:T(8,128)(2,1)S(1)}, u32[]{:S(2)}, u32[]{:S(2)}) collective-permute-start(bf16[4,48,1024]{2,1,0:T(8,128)(2,1)S(1)} %bitcast.304), channel_id=1, source_target_pairs={{0,2},{2,0},{4,6},{6,4},{8,10},{10,8},{12,14},{14,12},{1,3},{3,1},... | collective-permute-start | bytes 1179656 | tf_op jit(solution)/shard_map/ppermute | solution.py:132
  61.6 4.7 %collective-permute-start.7 = (bf16[48,1024]{1,0:T(8,128)(2,1)S(1)}, bf16[48,1024]{1,0:T(8,128)(2,1)S(1)}, u32[]{:S(2)}, u32[]{:S(2)}) collective-permute-start(bf16[48,1024]{1,0:T(8,128)(2,1)S(1)} %convolution_convert_fusion.8), channel_id=1, source_target_pairs={{0,1},{1,0},{2,3},{3,2},{4,5},{5,4},{6,7},{7,6},{8,9},{9,8},{10,11... | collective-permute-start | bytes 294920 | tf_op jit(solution)/shard_map/ppermute | solution.py:49
  66.6 5.7 %collective-permute-start.9 = (bf16[48,1024]{1,0:T(8,128)(2,1)S(1)}, bf16[48,1024]{1,0:T(8,128)(2,1)S(1)}, u32[]{:S(2)}, u32[]{:S(2)}) collective-permute-start(bf16[48,1024]{1,0:T(8,128)(2,1)S(1)} %slice_bitcast_fusion.8), channel_id=1, source_target_pairs={{0,1},{1,0},{2,3},{3,2},{4,5},{5,4},{6,7},{7,6},{8,9},{9,8},{10,11... | collective-permute-start | bytes 294920 | tf_op jit(solution)/shard_map/ppermute | solution.py:49
  68.2 9.7 %collective-permute-start.11 = (bf16[2,48,1024]{2,1,0:T(8,128)(2,1)S(1)}, bf16[2,48,1024]{2,1,0:T(8,128)(2,1)S(1)}, u32[]{:S(2)}, u32[]{:S(2)}) collective-permute-start(bf16[2,48,1024]{2,1,0:T(8,128)(2,1)S(1)} %get-tuple-element.13), channel_id=1, source_target_pairs={{0,4},{2,6},{4,8},{6,10},{8,12},{10,14},{12,0},{14,2},{1,5},{3,7},... | collective-permute-start | bytes 589832 | tf_op jit(solution)/shard_map/ppermute | solution.py:137
  68.8 13.6 %collective-permute-start.17 = (bf16[2,48,1024]{2,1,0:T(8,128)(2,1)S(1)}, bf16[2,48,1024]{2,1,0:T(8,128)(2,1)S(1)}, u32[]{:S(2)}, u32[]{:S(2)}) collective-permute-start(bf16[2,48,1024]{2,1,0:T(8,128)(2,1)S(1)} %get-tuple-element.14), channel_id=1, source_target_pairs={{0,8},{2,10},{4,12},{6,14},{8,0},{10,2},{12,4},{14,6},{1,9},{3,11}... | collective-permute-start | bytes 589832 | tf_op jit(solution)/shard_map/ppermute | solution.py:137
  70.1 12.8 %collective-permute-start.23 = (bf16[2,48,1024]{2,1,0:T(8,128)(2,1)S(1)}, bf16[2,48,1024]{2,1,0:T(8,128)(2,1)S(1)}, u32[]{:S(2)}, u32[]{:S(2)}) collective-permute-start(bf16[2,48,1024]{2,1,0:T(8,128)(2,1)S(1)} %get-tuple-element.15), channel_id=1, source_target_pairs={{0,12},{2,14},{4,0},{6,2},{8,4},{10,6},{12,8},{14,10},{1,13},{3,15... | collective-permute-start | bytes 589832 | tf_op jit(solution)/shard_map/ppermute | solution.py:137
  74.0 38.1 %collective-permute-start.10 = (bf16[48,1024]{1,0:T(8,128)(2,1)S(1)}, bf16[48,1024]{1,0:T(8,128)(2,1)S(1)}, u32[]{:S(2)}, u32[]{:S(2)}) collective-permute-start(bf16[48,1024]{1,0:T(8,128)(2,1)S(1)} %convolution_convert_fusion.7), channel_id=1, source_target_pairs={{0,1},{1,0},{2,3},{3,2},{4,5},{5,4},{6,7},{7,6},{8,9},{9,8},{10,11... | collective-permute-start | bytes 294920 | tf_op jit(solution)/shard_map/ppermute | solution.py:49
  78.0 6.5 %collective-permute-start.12 = (bf16[48,1024]{1,0:T(8,128)(2,1)S(1)}, bf16[48,1024]{1,0:T(8,128)(2,1)S(1)}, u32[]{:S(2)}, u32[]{:S(2)}) collective-permute-start(bf16[48,1024]{1,0:T(8,128)(2,1)S(1)} %get-tuple-element.18), channel_id=1, source_target_pairs={{0,1},{1,0},{2,3},{3,2},{4,5},{5,4},{6,7},{7,6},{8,9},{9,8},{10,11... | collective-permute-start | bytes 294920 | tf_op jit(solution)/shard_map/ppermute | solution.py:49
  78.6 8.2 %collective-permute-start.14 = (bf16[48,1024]{1,0:T(8,128)(2,1)S(1)}, bf16[48,1024]{1,0:T(8,128)(2,1)S(1)}, u32[]{:S(2)}, u32[]{:S(2)}) collective-permute-start(bf16[48,1024]{1,0:T(8,128)(2,1)S(1)} %get-tuple-element.19), channel_id=1, source_target_pairs={{0,1},{1,0},{2,3},{3,2},{4,5},{5,4},{6,7},{7,6},{8,9},{9,8},{10,11... | collective-permute-start | bytes 294920 | tf_op jit(solution)/shard_map/ppermute | solution.py:49
  82.4 7.6 %collective-permute-start.18 = (bf16[48,1024]{1,0:T(8,128)(2,1)S(1)}, bf16[48,1024]{1,0:T(8,128)(2,1)S(1)}, u32[]{:S(2)}, u32[]{:S(2)}) collective-permute-start(bf16[48,1024]{1,0:T(8,128)(2,1)S(1)} %get-tuple-element.20), channel_id=1, source_target_pairs={{0,1},{1,0},{2,3},{3,2},{4,5},{5,4},{6,7},{7,6},{8,9},{9,8},{10,11... | collective-permute-start | bytes 294920 | tf_op jit(solution)/shard_map/ppermute | solution.py:49
  83.0 9.3 %collective-permute-start.20 = (bf16[48,1024]{1,0:T(8,128)(2,1)S(1)}, bf16[48,1024]{1,0:T(8,128)(2,1)S(1)}, u32[]{:S(2)}, u32[]{:S(2)}) collective-permute-start(bf16[48,1024]{1,0:T(8,128)(2,1)S(1)} %get-tuple-element.21), channel_id=1, source_target_pairs={{0,1},{1,0},{2,3},{3,2},{4,5},{5,4},{6,7},{7,6},{8,9},{9,8},{10,11... | collective-permute-start | bytes 294920 | tf_op jit(solution)/shard_map/ppermute | solution.py:49
  84.5 11.0 %collective-permute-start.24 = (bf16[48,1024]{1,0:T(8,128)(2,1)S(1)}, bf16[48,1024]{1,0:T(8,128)(2,1)S(1)}, u32[]{:S(2)}, u32[]{:S(2)}) collective-permute-start(bf16[48,1024]{1,0:T(8,128)(2,1)S(1)} %get-tuple-element.22), channel_id=1, source_target_pairs={{0,1},{1,0},{2,3},{3,2},{4,5},{5,4},{6,7},{7,6},{8,9},{9,8},{10,11... | collective-permute-start | bytes 294920 | tf_op jit(solution)/shard_map/ppermute | solution.py:49
  86.8 11.0 %collective-permute-start.26 = (bf16[48,1024]{1,0:T(8,128)(2,1)S(1)}, bf16[48,1024]{1,0:T(8,128)(2,1)S(1)}, u32[]{:S(2)}, u32[]{:S(2)}) collective-permute-start(bf16[48,1024]{1,0:T(8,128)(2,1)S(1)} %get-tuple-element.23), channel_id=1, source_target_pairs={{0,1},{1,0},{2,3},{3,2},{4,5},{5,4},{6,7},{7,6},{8,9},{9,8},{10,11... | collective-permute-start | bytes 294920 | tf_op jit(solution)/shard_map/ppermute | solution.py:49
  90.0 11.0 %collective-permute-start.13 = (bf16[48,1024]{1,0:T(8,128)(2,1)S(1)}, bf16[48,1024]{1,0:T(8,128)(2,1)S(1)}, u32[]{:S(2)}, u32[]{:S(2)}) collective-permute-start(bf16[48,1024]{1,0:T(8,128)(2,1)S(1)} %convolution_convert_fusion.6), channel_id=1, source_target_pairs={{0,1},{1,0},{2,3},{3,2},{4,5},{5,4},{6,7},{7,6},{8,9},{9,8},{10,11... | collective-permute-start | bytes 294920 | tf_op jit(solution)/shard_map/ppermute | solution.py:49
  92.3 9.6 %collective-permute-start.15 = (bf16[48,1024]{1,0:T(8,128)(2,1)S(1)}, bf16[48,1024]{1,0:T(8,128)(2,1)S(1)}, u32[]{:S(2)}, u32[]{:S(2)}) collective-permute-start(bf16[48,1024]{1,0:T(8,128)(2,1)S(1)} %convolution_convert_fusion.5), channel_id=1, source_target_pairs={{0,1},{1,0},{2,3},{3,2},{4,5},{5,4},{6,7},{7,6},{8,9},{9,8},{10,11... | collective-permute-start | bytes 294920 | tf_op jit(solution)/shard_map/ppermute | solution.py:49
  95.6 8.2 %collective-permute-start.19 = (bf16[48,1024]{1,0:T(8,128)(2,1)S(1)}, bf16[48,1024]{1,0:T(8,128)(2,1)S(1)}, u32[]{:S(2)}, u32[]{:S(2)}) collective-permute-start(bf16[48,1024]{1,0:T(8,128)(2,1)S(1)} %convolution_convert_fusion.4), channel_id=1, source_target_pairs={{0,1},{1,0},{2,3},{3,2},{4,5},{5,4},{6,7},{7,6},{8,9},{9,8},{10,11... | collective-permute-start | bytes 294920 | tf_op jit(solution)/shard_map/ppermute | solution.py:49
  97.8 10.7 %collective-permute-start.21 = (bf16[48,1024]{1,0:T(8,128)(2,1)S(1)}, bf16[48,1024]{1,0:T(8,128)(2,1)S(1)}, u32[]{:S(2)}, u32[]{:S(2)}) collective-permute-start(bf16[48,1024]{1,0:T(8,128)(2,1)S(1)} %convolution_convert_fusion.3), channel_id=1, source_target_pairs={{0,1},{1,0},{2,3},{3,2},{4,5},{5,4},{6,7},{7,6},{8,9},{9,8},{10,11... | collective-permute-start | bytes 294920 | tf_op jit(solution)/shard_map/ppermute | solution.py:49
  101.1 8.4 %collective-permute-start.25 = (bf16[48,1024]{1,0:T(8,128)(2,1)S(1)}, bf16[48,1024]{1,0:T(8,128)(2,1)S(1)}, u32[]{:S(2)}, u32[]{:S(2)}) collective-permute-start(bf16[48,1024]{1,0:T(8,128)(2,1)S(1)} %convolution_convert_fusion.2), channel_id=1, source_target_pairs={{0,1},{1,0},{2,3},{3,2},{4,5},{5,4},{6,7},{7,6},{8,9},{9,8},{10,11... | collective-permute-start | bytes 294920 | tf_op jit(solution)/shard_map/ppermute | solution.py:49
  101.9 7.8 %collective-permute-start.27 = (bf16[48,1024]{1,0:T(8,128)(2,1)S(1)}, bf16[48,1024]{1,0:T(8,128)(2,1)S(1)}, u32[]{:S(2)}, u32[]{:S(2)}) collective-permute-start(bf16[48,1024]{1,0:T(8,128)(2,1)S(1)} %convolution_convert_fusion.1), channel_id=1, source_target_pairs={{0,1},{1,0},{2,3},{3,2},{4,5},{5,4},{6,7},{7,6},{8,9},{9,8},{10,11... | collective-permute-start | bytes 294920 | tf_op jit(solution)/shard_map/ppermute | solution.py:49
  103.8 9.2 %collective-permute-start.16 = (bf16[2,48,1024]{2,1,0:T(8,128)(2,1)S(1)}, bf16[2,48,1024]{2,1,0:T(8,128)(2,1)S(1)}, u32[]{:S(2)}, u32[]{:S(2)}) collective-permute-start(bf16[2,48,1024]{2,1,0:T(8,128)(2,1)S(1)} %bitcast.313), channel_id=1, source_target_pairs={{0,12},{2,14},{4,0},{6,2},{8,4},{10,6},{12,8},{14,10},{1,13},{3,15... | collective-permute-start | bytes 589832 | tf_op jit(solution)/shard_map/ppermute | solution.py:176
  108.8 13.1 %collective-permute-start.22 = (bf16[2,48,1024]{2,1,0:T(8,128)(2,1)S(1)}, bf16[2,48,1024]{2,1,0:T(8,128)(2,1)S(1)}, u32[]{:S(2)}, u32[]{:S(2)}) collective-permute-start(bf16[2,48,1024]{2,1,0:T(8,128)(2,1)S(1)} %bitcast.314), channel_id=1, source_target_pairs={{0,8},{2,10},{4,12},{6,14},{8,0},{10,2},{12,4},{14,6},{1,9},{3,11}... | collective-permute-start | bytes 589832 | tf_op jit(solution)/shard_map/ppermute | solution.py:176
  110.0 12.0 %collective-permute-start.28 = (bf16[2,48,1024]{2,1,0:T(8,128)(2,1)S(1)}, bf16[2,48,1024]{2,1,0:T(8,128)(2,1)S(1)}, u32[]{:S(2)}, u32[]{:S(2)}) collective-permute-start(bf16[2,48,1024]{2,1,0:T(8,128)(2,1)S(1)} %bitcast.315), channel_id=1, source_target_pairs={{0,4},{2,6},{4,8},{6,10},{8,12},{10,14},{12,0},{14,2},{1,5},{3,7},... | collective-permute-start | bytes 589832 | tf_op jit(solution)/shard_map/ppermute | solution.py:176
  122.1 2.8 %collective-permute-start.29 = (bf16[4,48,1024]{2,1,0:T(8,128)(2,1)S(1)}, bf16[4,48,1024]{2,1,0:T(8,128)(2,1)S(1)}, u32[]{:S(2)}, u32[]{:S(2)}) collective-permute-start(bf16[4,48,1024]{2,1,0:T(8,128)(2,1)S(1)} %get-tuple-element.12), channel_id=1, source_target_pairs={{0,2},{2,0},{4,6},{6,4},{8,10},{10,8},{12,14},{14,12},{1,3},{3,1},... | collective-permute-start | bytes 1179656 | tf_op jit(solution)/shard_map/ppermute | solution.py:178
  125.6 4.3 %collective-permute-start.30 = (bf16[32,1024]{1,0:T(8,128)(2,1)S(1)}, bf16[32,1024]{1,0:T(8,128)(2,1)S(1)}, u32[]{:S(2)}, u32[]{:S(2)}) collective-permute-start(bf16[32,1024]{1,0:T(8,128)(2,1)S(1)} %select_convert_fusion), channel_id=1, source_target_pairs={{0,1},{1,0},{2,3},{3,2},{4,5},{5,4},{6,7},{7,6},{8,9},{9,8},{10,11... | collective-permute-start | bytes 196616 | tf_op jit(solution)/shard_map/ppermute | solution.py:49
  (8 other events, 117.6 us)
Sparse Core Ops, SparseCore 0:
  9.6 34.5 all-gather.1

commit v16 on v15

--- a/solution.py
+++ b/solution.py
@@ -122,19 +122,29 @@
     n_chip = n_ctx // 2
     my_chip = my_ctx // 2
     my_core = my_ctx % 2
-    send_rows = jnp.dot(
-        dispatch.astype(jnp.bfloat16),
+    dispatch_parts = dispatch.reshape(2, n_chip, capacity, tok_count)
+    full_d = normed.shape[1]
+    near = jnp.dot(
+        dispatch_parts[:, 0].reshape(2 * capacity, tok_count).astype(jnp.bfloat16),
+        normed,
+        preferred_element_type=jnp.float32,
+    ).astype(jnp.bfloat16)
+    near = near.reshape(2, capacity, full_d)
+    far = jnp.dot(
+        dispatch_parts[:, 1:].reshape(2 * (n_chip - 1) * capacity, tok_count).astype(jnp.bfloat16),
         tokens_cols,
         preferred_element_type=jnp.float32,
     ).astype(jnp.bfloat16)
-    send_rows = send_rows.reshape(2, n_chip, capacity, half_d)
+    far = far.reshape(2, n_chip - 1, capacity, half_d)
     core_swap = [(i, i ^ 1) for i in range(n_ctx)]
-    from_partner = lax.ppermute(send_rows[1], "ctx", perm=core_swap)
-    pairs = jnp.stack([send_rows[0], from_partner], axis=1)
-    arrived = [pairs[0]]
+    near_in = jnp.concatenate(
+        [near[0], lax.ppermute(near[1], "ctx", perm=core_swap)], axis=0
+    )
+    far_pairs = jnp.stack([far[0], lax.ppermute(far[1], "ctx", perm=core_swap)], axis=1)
+    arrived = [None]
     for shift in range(1, n_chip):
         perm = [(i, ((i // 2 + shift) % n_chip) * 2 + i % 2) for i in range(n_ctx)]
-        arrived.append(lax.ppermute(pairs[shift], "ctx", perm=perm))
+        arrived.append(lax.ppermute(far_pairs[shift - 1], "ctx", perm=perm))
     my_start = my_exp * half_d
     other_start = (1 - my_exp) * half_d
     gate_mine = lax.dynamic_slice_in_dim(gate_matrix, my_start, half_d, axis=0)
@@ -143,18 +153,17 @@
     up_other = lax.dynamic_slice_in_dim(up_matrix, other_start, half_d, axis=0)
     down_other = lax.dynamic_slice_in_dim(down_matrix, other_start, half_d, axis=1)
     down_mine = lax.dynamic_slice_in_dim(down_matrix, my_start, half_d, axis=1)
-    per_group = 1 if n_chip <= 4 else n_chip // 2
-    n_groups = n_chip // per_group
+    if n_chip <= 4:
+        groups = [[0]] + [[k] for k in range(1, n_chip)]
+    else:
+        groups = [[0], list(range(1, n_chip // 2)), list(range(n_chip // 2, n_chip))]
     returned = [None] * n_chip
-    split_cores = n_chip <= 4
-    for group in range(n_groups):
-        shifts = range(group * per_group, (group + 1) * per_group)
-        if split_cores:
-            pieces = [arrived[k][side] for k in shifts for side in range(2)]
+    for shifts in groups:
+        if shifts == [0]:
+            gate_act = jnp.dot(near_in, gate_matrix, preferred_element_type=jnp.float32)
+            up_act = jnp.dot(near_in, up_matrix, preferred_element_type=jnp.float32)
         else:
-            pieces = [jnp.concatenate([arrived[k] for k in shifts], axis=0).reshape(-1, half_d)]
-        outs = []
-        for block in pieces:
+            block = jnp.concatenate([arrived[k] for k in shifts], axis=0).reshape(-1, half_d)
             partner_cols = exp_swap(block)
             gate_act = jnp.dot(block, gate_mine, preferred_element_type=jnp.float32) + jnp.dot(
                 partner_cols, gate_other, preferred_element_type=jnp.float32
@@ -162,12 +171,12 @@
             up_act = jnp.dot(block, up_mine, preferred_element_type=jnp.float32) + jnp.dot(
                 partner_cols, up_other, preferred_element_type=jnp.float32
             )
-            hidden = (jax.nn.silu(gate_act) * up_act).astype(jnp.bfloat16)
-            out_other = jnp.dot(hidden, down_other, preferred_element_type=jnp.float32)
-            got_other = exp_swap(out_other.astype(jnp.bfloat16))
-            out_mine = jnp.dot(hidden, down_mine, preferred_element_type=jnp.float32)
-            outs.append((out_mine + got_other.astype(jnp.float32)).astype(jnp.bfloat16))
-        summed = jnp.concatenate(outs, axis=0).reshape(per_group, 2, capacity, half_d)
+        hidden = (jax.nn.silu(gate_act) * up_act).astype(jnp.bfloat16)
+        out_other = jnp.dot(hidden, down_other, preferred_element_type=jnp.float32)
+        got_other = exp_swap(out_other.astype(jnp.bfloat16))
+        out_mine = jnp.dot(hidden, down_mine, preferred_element_type=jnp.float32)
+        summed = (out_mine + got_other.astype(jnp.float32)).astype(jnp.bfloat16)
+        summed = summed.reshape(len(shifts), 2, capacity, half_d)
         for idx, shift in enumerate(shifts):
             if shift == 0:
                 returned[shift] = summed[idx]

time: 138 us -> 130 us (0.942)
  starting transfers between devices: 41.2 us -> 31.6 us
  matrix products: 20.6 us -> 15.7 us
  waiting for transfers between devices: 50.5 us -> 54 us
  local copies, waits for them, and re-layouts: 4.94 us -> 6.87 us
    ppermute x19 -> x10, starting transfers between devices: 22.6 us -> 13.8 us  [exp_swap(): return lax.ppermute(x, 'exp', perm=[(0, 1), (1, 0)])]
    ppermute x4 -> x5, waiting for transfers between devices: 5.76 us -> 9.65 us  [the longest x3 9.43 us: moe_column_halves(): arrived.append(lax.ppermute(far_pairs[shift - 1], 'ctx', perm=perm))]
    dot_general x1 -> x4, matrix products: 0.39 us -> 3.76 us  [the longest x1 1.72 us: moe_column_halves(): gate_act = jnp.dot(near_in, gate_matrix, preferred_element_type=jnp.float32)]
    slice x3 -> x7, local copies, waits for them, and re-layouts: 0.27 us -> 2.12 us  [the longest x1 0.8 us: moe_column_halves(): near[0]]
    dot_general x8 -> x3, matrix products: 2.79 us -> 1.1 us  [moe_column_halves(): jnp.dot(block, up_mine, preferred_element_type=jnp.float32)]
    dot_general x8 -> x3, matrix products: 2.77 us -> 1.09 us  [moe_column_halves(): jnp.dot(block, gate_mine, preferred_element_type=jnp.float32)]
    dot_general x8 -> x3, matrix products: 2.76 us -> 1.08 us  [moe_column_halves(): jnp.dot(partner_cols, up_other, preferred_element_type=jnp.float32)]
    dot_general x8 -> x3, matrix products: 2.71 us -> 1.06 us  [moe_column_halves(): jnp.dot(partner_cols, gate_other, preferred_element_type=jnp.float32)]
  transfers between devices with their start and end apart: 32 -> 24, of which waited for: 11 -> 13; matrix products, arithmetic and copies ran while one was open for 19% -> 17% of each run, Pallas kernels for 0% -> 0%
where the time goes in v16:
time: 130 us; the launch traced here: 129 us
  waiting for transfers between devices  54 us (42%)
  starting transfers between devices  31.6 us (24%)
  matrix products  15.7 us (12%)
  between operations  15.2 us (12%)
  local copies, waits for them, and re-layouts  6.87 us (5%)
  other arithmetic  5.67 us (4%)
    all_gather x1, waiting for transfers between devices, local(): lax.all_gather(out_weight, 'ctx', axis=0, tiled=True)  16.7 us
    ppermute x10, waiting for transfers between devices, exp_swap(): return lax.ppermute(x, 'exp', perm=[(0, 1), (1, 0)])  15.2 us
    ppermute x10, starting transfers between devices, exp_swap(): return lax.ppermute(x, 'exp', perm=[(0, 1), (1, 0)])  13.8 us
    ppermute x3, waiting for transfers between devices, moe_column_halves(): arrived.append(lax.ppermute(far_pairs[shift - 1], 'ctx', perm=perm))  9.43 us
    ppermute x3, waiting for transfers between devices, moe_column_halves(): returned[shift] = lax.ppermute(summed[idx], 'ctx', perm=perm)  9.05 us
    ppermute x3, starting transfers between devices, ctx_gather_blocks(): stack.append(lax.ppermute(rows, 'ctx', perm=perm))  7.03 us
    ppermute x3, starting transfers between devices, moe_column_halves(): returned[shift] = lax.ppermute(summed[idx], 'ctx', perm=perm)  6.11 us
    ppermute x3, starting transfers between devices, moe_column_halves(): arrived.append(lax.ppermute(far_pairs[shift - 1], 'ctx', perm=perm))  4.01 us
  transfers between devices with their start and end apart: 24, of which 13 were waited for; matrix products, arithmetic and copies ran while one was open for 17% of the time, Pallas kernels for 0%

profile of v16, /device:TPU:0, one launch (start us, length us, event | category | flops | bytes accessed | tf_op | source)
XLA Modules:
  0.0 129.1 jit_solution(16408924482554780846)
XLA Ops:
  7.9 0.9 fusion.152
  8.8 3.1 %collective-permute-start.1 = (bf16[64,1024]{1,0:T(8,128)(2,1)S(1)}, bf16[64,1024]{1,0:T(8,128)(2,1)S(1)}, u32[]{:S(2)}, u32[]{:S(2)}) collective-permute-start(bf16[64,1024]{1,0:T(8,128)(2,1)S(1)} %get-tuple-element.21), channel_id=1, source_target_pairs={{0,4},{2,6},{4,8},{6,10},{8,12},{10,14},{12,0},{14,2},{1,5},{3,7},... | collective-permute-start | bytes 393224 | tf_op jit(solution)/shard_map/ppermute | solution.py:207
  11.9 2.6 %collective-permute-start.2 = (bf16[64,1024]{1,0:T(8,128)(2,1)S(1)}, bf16[64,1024]{1,0:T(8,128)(2,1)S(1)}, u32[]{:S(2)}, u32[]{:S(2)}) collective-permute-start(bf16[64,1024]{1,0:T(8,128)(2,1)S(1)} %get-tuple-element.21), channel_id=1, source_target_pairs={{0,8},{2,10},{4,12},{6,14},{8,0},{10,2},{12,4},{14,6},{1,9},{3,11}... | collective-permute-start | bytes 393224 | tf_op jit(solution)/shard_map/ppermute | solution.py:207
  14.5 1.4 %collective-permute-start.3 = (bf16[64,1024]{1,0:T(8,128)(2,1)S(1)}, bf16[64,1024]{1,0:T(8,128)(2,1)S(1)}, u32[]{:S(2)}, u32[]{:S(2)}) collective-permute-start(bf16[64,1024]{1,0:T(8,128)(2,1)S(1)} %get-tuple-element.21), channel_id=1, source_target_pairs={{0,12},{2,14},{4,0},{6,2},{8,4},{10,6},{12,8},{14,10},{1,13},{3,15... | collective-permute-start | bytes 393224 | tf_op jit(solution)/shard_map/ppermute | solution.py:207
  15.8 1.5 %collective-permute-start = (bf16[32,2048]{1,0:T(8,128)(2,1)}, bf16[32,2048]{1,0:T(8,128)(2,1)S(1)}, u32[]{:S(2)}, u32[]{:S(2)}) collective-permute-start(bf16[32,2048]{1,0:T(8,128)(2,1)} %bitcast.229), channel_id=1, source_target_pairs={{0,1},{1,0},{2,3},{3,2},{4,5},{5,4},{6,7},{7,6},{8,9},{9,8},{10,11... | collective-permute-start | bytes 393224 | tf_op jit(solution)/shard_map/ppermute | solution.py:49
  22.2 0.9 collective-permute-done.2
  23.3 1.8 %collective-permute-done.4 = bf16[4,64,1024]{2,1,0:T(8,128)(2,1)S(1)} collective-permute-done((bf16[4,64,1024]{2,1,0:T(8,128)(2,1)S(1)}, bf16[4,64,1024]{2,1,0:T(8,128)(2,1)S(1)}, u32[]{:S(2)}, u32[]{:S(2)}) %collective-permute-start.4) | collective-permute-done | bytes 524320 | tf_op jit(solution)/shard_map/ppermute | solution.py:209
  25.3 0.9 copy-done.3
  27.6 16.7 %all-gather.2.cloned.1.call-done = bf16[2048,512]{1,0:T(8,128)(2,1)} async-done(((bf16[256,512]{1,0:T(8,128)(2,1)}), bf16[2048,512]{1,0:T(8,128)(2,1)}) %all-gather.2.cloned.1.call-update) | async-done | bytes 2097168 | tf_op jit(solution)/shard_map/all_gather | solution.py:279
  44.2 2.3 %fusion.158 = (bf16[64,2048]{1,0:T(8,128)(2,1)S(1)}, f32[64,2048]{1,0:T(8,128)S(1)}) fusion(bf16[2048,512]{1,0:T(8,128)(2,1)} %all-gather.2.cloned.1.call-done, bf16[4,8,8,128]{3,2,1,0:T(8,128)(2,1)S(1)} %fusion.8), kind=kOutput, calls=%fused_computation.244 | convolution fusion | flops 134348800 | bytes 2949120 | tf_op jit(solution)/shard_map/tc,oc->to/dot_general | solution.py:276
  46.6 1.6 %collective-permute-start.5 = (bf16[64,2048]{1,0:T(8,128)(2,1)S(1)}, bf16[64,2048]{1,0:T(8,128)(2,1)S(1)}, u32[]{:S(2)}, u32[]{:S(2)}) collective-permute-start(bf16[64,2048]{1,0:T(8,128)(2,1)S(1)} %get-tuple-element.24), channel_id=1, source_target_pairs={{0,1},{1,0},{2,3},{3,2},{4,5},{5,4},{6,7},{7,6},{8,9},{9,8},{10,11... | collective-permute-start | bytes 786440 | tf_op jit(solution)/shard_map/ppermute | solution.py:49
  49.0 6.1 %collective-permute-done.5 = bf16[64,2048]{1,0:T(8,128)(2,1)S(1)} collective-permute-done((bf16[64,2048]{1,0:T(8,128)(2,1)S(1)}, bf16[64,2048]{1,0:T(8,128)(2,1)S(1)}, u32[]{:S(2)}, u32[]{:S(2)}) %collective-permute-start.5) | collective-permute-done | bytes 262176 | tf_op jit(solution)/shard_map/ppermute | solution.py:49
  58.4 1.7 %fusion.2 = f32[96,352]{1,0:T(8,128)S(1)} fusion(bf16[1,2048,352]{1,2,0:T(8,128)(2,1)S(1)} %copy-done.1, bf16[48,2048]{1,0:T(8,128)(2,1)} %collective-permute-done.6, bf16[48,2048]{1,0:T(8,128)(2,1)} %get-tuple-element.18), kind=kOutput, calls=%fused_computation.3 | convolution fusion | flops 139198464 | bytes 1970176 | tf_op jit(solution)/shard_map/dot_general | solution.py:163
  60.1 1.0 fusion.75
  61.5 1.5 %multiply_convert_fusion.3 = bf16[96,352]{1,0:T(8,128)(2,1)S(1)} fusion(f32[96,352]{1,0:T(8,128)S(1)} %fusion.2, bf16[1,2048,352]{1,2,0:T(8,128)(2,1)S(1)} %copy-done.2, bf16[48,2048]{1,0:T(8,128)(2,1)} %collective-permute-done.6, bf16[48,2048]{1,0:T(8,128)(2,1)S(1)} %copy-done.5), kind=kOutput, calls=%fused_computation.121 | convolution fusion | flops 139401216 | bytes 2037760 | tf_op jit(solution)/shard_map/dot_general | solution.py:164
  63.0 2.0 %collective-permute-start.13 = (bf16[2,48,1024]{2,1,0:T(8,128)(2,1)S(1)}, bf16[2,48,1024]{2,1,0:T(8,128)(2,1)S(1)}, u32[]{:S(2)}, u32[]{:S(2)}) collective-permute-start(bf16[2,48,1024]{2,1,0:T(8,128)(2,1)S(1)} %get-tuple-element.15), channel_id=1, source_target_pairs={{0,8},{2,10},{4,12},{6,14},{8,0},{10,2},{12,4},{14,6},{1,9},{3,11}... | collective-permute-start | bytes 589832 | tf_op jit(solution)/shard_map/ppermute | solution.py:147
  65.0 1.7 %collective-permute-start.17 = (bf16[2,48,1024]{2,1,0:T(8,128)(2,1)S(1)}, bf16[2,48,1024]{2,1,0:T(8,128)(2,1)S(1)}, u32[]{:S(2)}, u32[]{:S(2)}) collective-permute-start(bf16[2,48,1024]{2,1,0:T(8,128)(2,1)S(1)} %get-tuple-element.14), channel_id=1, source_target_pairs={{0,12},{2,14},{4,0},{6,2},{8,4},{10,6},{12,8},{14,10},{1,13},{3,15... | collective-permute-start | bytes 589832 | tf_op jit(solution)/shard_map/ppermute | solution.py:147
  66.7 4.2 %collective-permute-done.9 = bf16[2,48,1024]{2,1,0:T(8,128)(2,1)S(1)} collective-permute-done((bf16[2,48,1024]{2,1,0:T(8,128)(2,1)S(1)}, bf16[2,48,1024]{2,1,0:T(8,128)(2,1)S(1)}, u32[]{:S(2)}, u32[]{:S(2)}) %collective-permute-start.9) | collective-permute-done | bytes 196640 | tf_op jit(solution)/shard_map/ppermute | solution.py:147
  70.8 1.5 %collective-permute-start.10 = (bf16[96,1024]{1,0:T(8,128)(2,1)S(1)}, bf16[96,1024]{1,0:T(8,128)(2,1)S(1)}, u32[]{:S(2)}, u32[]{:S(2)}) collective-permute-start(bf16[96,1024]{1,0:T(8,128)(2,1)S(1)} %bitcast.223), channel_id=1, source_target_pairs={{0,1},{1,0},{2,3},{3,2},{4,5},{5,4},{6,7},{7,6},{8,9},{9,8},{10,11... | collective-permute-start | bytes 589832 | tf_op jit(solution)/shard_map/ppermute | solution.py:49
  73.2 5.2 %collective-permute-done.13 = bf16[2,48,1024]{2,1,0:T(8,128)(2,1)S(1)} collective-permute-done((bf16[2,48,1024]{2,1,0:T(8,128)(2,1)S(1)}, bf16[2,48,1024]{2,1,0:T(8,128)(2,1)S(1)}, u32[]{:S(2)}, u32[]{:S(2)}) %collective-permute-start.13) | collective-permute-done | bytes 196640 | tf_op jit(solution)/shard_map/ppermute | solution.py:147
  78.5 1.5 %collective-permute-start.14 = (bf16[96,1024]{1,0:T(8,128)(2,1)S(1)}, bf16[96,1024]{1,0:T(8,128)(2,1)S(1)}, u32[]{:S(2)}, u32[]{:S(2)}) collective-permute-start(bf16[96,1024]{1,0:T(8,128)(2,1)S(1)} %bitcast.220), channel_id=1, source_target_pairs={{0,1},{1,0},{2,3},{3,2},{4,5},{5,4},{6,7},{7,6},{8,9},{9,8},{10,11... | collective-permute-start | bytes 589832 | tf_op jit(solution)/shard_map/ppermute | solution.py:49
  82.3 1.6 %collective-permute-start.11 = (bf16[96,1024]{1,0:T(8,128)(2,1)S(1)}, bf16[96,1024]{1,0:T(8,128)(2,1)S(1)}, u32[]{:S(2)}, u32[]{:S(2)}) collective-permute-start(bf16[96,1024]{1,0:T(8,128)(2,1)S(1)} %convolution_convert_fusion.4), channel_id=1, source_target_pairs={{0,1},{1,0},{2,3},{3,2},{4,5},{5,4},{6,7},{7,6},{8,9},{9,8},{10,11... | collective-permute-start | bytes 589832 | tf_op jit(solution)/shard_map/ppermute | solution.py:49
  83.9 2.4 %collective-permute-done.14 = bf16[96,1024]{1,0:T(8,128)(2,1)S(1)} collective-permute-done((bf16[96,1024]{1,0:T(8,128)(2,1)S(1)}, bf16[96,1024]{1,0:T(8,128)(2,1)S(1)}, u32[]{:S(2)}, u32[]{:S(2)}) %collective-permute-start.14) | collective-permute-done | bytes 196640 | tf_op jit(solution)/shard_map/ppermute | solution.py:49
  88.0 1.6 %collective-permute-start.15 = (bf16[96,1024]{1,0:T(8,128)(2,1)S(1)}, bf16[96,1024]{1,0:T(8,128)(2,1)S(1)}, u32[]{:S(2)}, u32[]{:S(2)}) collective-permute-start(bf16[96,1024]{1,0:T(8,128)(2,1)S(1)} %convolution_convert_fusion.3), channel_id=1, source_target_pairs={{0,1},{1,0},{2,3},{3,2},{4,5},{5,4},{6,7},{7,6},{8,9},{9,8},{10,11... | collective-permute-start | bytes 589832 | tf_op jit(solution)/shard_map/ppermute | solution.py:49
  92.2 1.6 %collective-permute-start.19 = (bf16[96,1024]{1,0:T(8,128)(2,1)S(1)}, bf16[96,1024]{1,0:T(8,128)(2,1)S(1)}, u32[]{:S(2)}, u32[]{:S(2)}) collective-permute-start(bf16[96,1024]{1,0:T(8,128)(2,1)S(1)} %convolution_convert_fusion.2), channel_id=1, source_target_pairs={{0,1},{1,0},{2,3},{3,2},{4,5},{5,4},{6,7},{7,6},{8,9},{9,8},{10,11... | collective-permute-start | bytes 589832 | tf_op jit(solution)/shard_map/ppermute | solution.py:49
  95.0 4.1 %collective-permute-start.12 = (bf16[2,48,1024]{2,1,0:T(8,128)(2,1)S(1)}, bf16[2,48,1024]{2,1,0:T(8,128)(2,1)S(1)}, u32[]{:S(2)}, u32[]{:S(2)}) collective-permute-start(bf16[2,48,1024]{2,1,0:T(8,128)(2,1)S(1)} %bitcast.226), channel_id=1, source_target_pairs={{0,12},{2,14},{4,0},{6,2},{8,4},{10,6},{12,8},{14,10},{1,13},{3,15... | collective-permute-start | bytes 589832 | tf_op jit(solution)/shard_map/ppermute | solution.py:185
  99.5 2.6 %collective-permute-done.19 = bf16[96,1024]{1,0:T(8,128)(2,1)S(1)} collective-permute-done((bf16[96,1024]{1,0:T(8,128)(2,1)S(1)}, bf16[96,1024]{1,0:T(8,128)(2,1)S(1)}, u32[]{:S(2)}, u32[]{:S(2)}) %collective-permute-start.19) | collective-permute-done | bytes 196640 | tf_op jit(solution)/shard_map/ppermute | solution.py:49
  102.4 1.9 %collective-permute-start.20 = (bf16[2,48,1024]{2,1,0:T(8,128)(2,1)S(1)}, bf16[2,48,1024]{2,1,0:T(8,128)(2,1)S(1)}, u32[]{:S(2)}, u32[]{:S(2)}) collective-permute-start(bf16[2,48,1024]{2,1,0:T(8,128)(2,1)S(1)} %bitcast.228), channel_id=1, source_target_pairs={{0,4},{2,6},{4,8},{6,10},{8,12},{10,14},{12,0},{14,2},{1,5},{3,7},... | collective-permute-start | bytes 589832 | tf_op jit(solution)/shard_map/ppermute | solution.py:185
  104.6 9.0 %collective-permute-done.16 = bf16[2,48,1024]{2,1,0:T(8,128)(2,1)S(1)} collective-permute-done((bf16[2,48,1024]{2,1,0:T(8,128)(2,1)S(1)}, bf16[2,48,1024]{2,1,0:T(8,128)(2,1)S(1)}, u32[]{:S(2)}, u32[]{:S(2)}) %collective-permute-start.16) | collective-permute-done | bytes 196640 | tf_op jit(solution)/shard_map/ppermute | solution.py:185
  113.9 1.0 copy-done.4
  117.2 1.9 %collective-permute-start.22 = (bf16[32,1024]{1,0:T(8,128)(2,1)S(1)}, bf16[32,1024]{1,0:T(8,128)(2,1)S(1)}, u32[]{:S(2)}, u32[]{:S(2)}) collective-permute-start(bf16[32,1024]{1,0:T(8,128)(2,1)S(1)} %select_convert_fusion), channel_id=1, source_target_pairs={{0,1},{1,0},{2,3},{3,2},{4,5},{5,4},{6,7},{7,6},{8,9},{9,8},{10,11... | collective-permute-start | bytes 196616 | tf_op jit(solution)/shard_map/ppermute | solution.py:49
  119.1 2.5 %collective-permute-done.22 = bf16[32,1024]{1,0:T(8,128)(2,1)S(1)} collective-permute-done((bf16[32,1024]{1,0:T(8,128)(2,1)S(1)}, bf16[32,1024]{1,0:T(8,128)(2,1)S(1)}, u32[]{:S(2)}, u32[]{:S(2)}) %collective-permute-start.22) | collective-permute-done | bytes 65568 | tf_op jit(solution)/shard_map/ppermute | solution.py:49
  (117 shorter events, 23.7 us)
Async XLA Ops:
  7.2 65.2 %copy-start = (bf16[1,352,2048]{2,1,0:T(8,128)(2,1)S(1)}, bf16[1,352,2048]{2,1,0:T(8,128)(2,1)}, u32[]{:S(2)}) copy-start(bf16[1,352,2048]{2,1,0:T(8,128)(2,1)} %param.20) | copy-start | bytes 4325380
  7.2 37.1 %all-gather.2.cloned.1.call-start = ((), (), s32[]{:S(2)}) async-start(), calls=%async_computation | async-start | bytes 2359296 | tf_op jit(solution)/shard_map/all_gather | solution.py:279
  8.8 13.4 %collective-permute-start.1 = (bf16[64,1024]{1,0:T(8,128)(2,1)S(1)}, bf16[64,1024]{1,0:T(8,128)(2,1)S(1)}, u32[]{:S(2)}, u32[]{:S(2)}) collective-permute-start(bf16[64,1024]{1,0:T(8,128)(2,1)S(1)} %get-tuple-element.21), channel_id=1, source_target_pairs={{0,4},{2,6},{4,8},{6,10},{8,12},{10,14},{12,0},{14,2},{1,5},{3,7},... | collective-permute-start | bytes 393224 | tf_op jit(solution)/shard_map/ppermute | solution.py:207
  11.9 11.2 %collective-permute-start.2 = (bf16[64,1024]{1,0:T(8,128)(2,1)S(1)}, bf16[64,1024]{1,0:T(8,128)(2,1)S(1)}, u32[]{:S(2)}, u32[]{:S(2)}) collective-permute-start(bf16[64,1024]{1,0:T(8,128)(2,1)S(1)} %get-tuple-element.21), channel_id=1, source_target_pairs={{0,8},{2,10},{4,12},{6,14},{8,0},{10,2},{12,4},{14,6},{1,9},{3,11}... | collective-permute-start | bytes 393224 | tf_op jit(solution)/shard_map/ppermute | solution.py:207
  14.5 8.6 %collective-permute-start.3 = (bf16[64,1024]{1,0:T(8,128)(2,1)S(1)}, bf16[64,1024]{1,0:T(8,128)(2,1)S(1)}, u32[]{:S(2)}, u32[]{:S(2)}) collective-permute-start(bf16[64,1024]{1,0:T(8,128)(2,1)S(1)} %get-tuple-element.21), channel_id=1, source_target_pairs={{0,12},{2,14},{4,0},{6,2},{8,4},{10,6},{12,8},{14,10},{1,13},{3,15... | collective-permute-start | bytes 393224 | tf_op jit(solution)/shard_map/ppermute | solution.py:207
  15.8 33.2 %collective-permute-start = (bf16[32,2048]{1,0:T(8,128)(2,1)}, bf16[32,2048]{1,0:T(8,128)(2,1)S(1)}, u32[]{:S(2)}, u32[]{:S(2)}) collective-permute-start(bf16[32,2048]{1,0:T(8,128)(2,1)} %bitcast.229), channel_id=1, source_target_pairs={{0,1},{1,0},{2,3},{3,2},{4,5},{5,4},{6,7},{7,6},{8,9},{9,8},{10,11... | collective-permute-start | bytes 393224 | tf_op jit(solution)/shard_map/ppermute | solution.py:49
  23.2 2.0 %collective-permute-start.4 = (bf16[4,64,1024]{2,1,0:T(8,128)(2,1)S(1)}, bf16[4,64,1024]{2,1,0:T(8,128)(2,1)S(1)}, u32[]{:S(2)}, u32[]{:S(2)}) collective-permute-start(bf16[4,64,1024]{2,1,0:T(8,128)(2,1)S(1)} %pad_maximum_fusion.2), channel_id=1, source_target_pairs={{0,2},{2,0},{4,6},{6,4},{8,10},{10,8},{12,14},{14,12},{1,3},{3,1},... | collective-permute-start | bytes 1572872 | tf_op jit(solution)/shard_map/ppermute | solution.py:209
  27.5 20.8 %copy-start.8 = (f32[1,64,4]{1,2,0:T(4,128)S(1)}, f32[1,64,4]{1,2,0:T(4,128)}, u32[]{:S(2)}) copy-start(f32[1,64,4]{1,2,0:T(4,128)} %param.22) | copy-start | bytes 3076
  27.5 27.6 %copy-start.6 = (bf16[1,32,2048]{2,1,0:T(8,128)(2,1)S(1)}, bf16[1,32,2048]{2,1,0:T(8,128)(2,1)}, u32[]{:S(2)}) copy-start(bf16[1,32,2048]{2,1,0:T(8,128)(2,1)} %param.15) | copy-start | bytes 393220
  46.6 8.8 %copy-start.7 = (f32[2048]{0:T(1024)S(1)}, f32[2048]{0:T(1024)}, u32[]{:S(2)}) copy-start(f32[2048]{0:T(1024)} %param.17) | copy-start | bytes 24580
  46.6 8.5 %collective-permute-start.5 = (bf16[64,2048]{1,0:T(8,128)(2,1)S(1)}, bf16[64,2048]{1,0:T(8,128)(2,1)S(1)}, u32[]{:S(2)}, u32[]{:S(2)}) collective-permute-start(bf16[64,2048]{1,0:T(8,128)(2,1)S(1)} %get-tuple-element.24), channel_id=1, source_target_pairs={{0,1},{1,0},{2,3},{3,2},{4,5},{5,4},{6,7},{7,6},{8,9},{9,8},{10,11... | collective-permute-start | bytes 786440 | tf_op jit(solution)/shard_map/ppermute | solution.py:49
  55.8 2.6 %copy-start.1 = (bf16[1,2048,352]{1,2,0:T(8,128)(2,1)S(1)}, bf16[1,2048,352]{1,2,0:T(8,128)(2,1)}, u32[]{:S(2)}) copy-start(bf16[1,2048,352]{1,2,0:T(8,128)(2,1)} %param.18) | copy-start | bytes 4325380
  56.6 1.8 %collective-permute-start.6 = (bf16[48,2048]{1,0:T(8,128)(2,1)}, bf16[48,2048]{1,0:T(8,128)(2,1)}, u32[]{:S(2)}, u32[]{:S(2)}) collective-permute-start(bf16[48,2048]{1,0:T(8,128)(2,1)} %get-tuple-element.19), channel_id=1, source_target_pairs={{0,2},{2,0},{4,6},{6,4},{8,10},{10,8},{12,14},{14,12},{1,3},{3,1},... | collective-permute-start | bytes 589832 | tf_op jit(solution)/shard_map/ppermute | solution.py:141
  57.6 2.5 %collective-permute-start.8 = (bf16[3,48,1024]{2,1,0:T(8,128)(2,1)}, bf16[3,48,1024]{2,1,0:T(8,128)(2,1)}, u32[]{:S(2)}, u32[]{:S(2)}) collective-permute-start(bf16[3,48,1024]{2,1,0:T(8,128)(2,1)} %bitcast.26), channel_id=1, source_target_pairs={{0,2},{2,0},{4,6},{6,4},{8,10},{10,8},{12,14},{14,12},{1,3},{3,1},... | collective-permute-start | bytes 884744 | tf_op jit(solution)/shard_map/ppermute | solution.py:143
  58.4 3.1 %copy-start.2 = (bf16[1,2048,352]{1,2,0:T(8,128)(2,1)S(1)}, bf16[1,2048,352]{1,2,0:T(8,128)(2,1)}, u32[]{:S(2)}) copy-start(bf16[1,2048,352]{1,2,0:T(8,128)(2,1)} %param.19) | copy-start | bytes 4325380
  58.4 3.1 %copy-start.5 = (bf16[48,2048]{1,0:T(8,128)(2,1)S(1)}, bf16[48,2048]{1,0:T(8,128)(2,1)}, u32[]{:S(2)}) copy-start(bf16[48,2048]{1,0:T(8,128)(2,1)} %get-tuple-element.18) | copy-start | bytes 589828
  61.1 9.7 %collective-permute-start.9 = (bf16[2,48,1024]{2,1,0:T(8,128)(2,1)S(1)}, bf16[2,48,1024]{2,1,0:T(8,128)(2,1)S(1)}, u32[]{:S(2)}, u32[]{:S(2)}) collective-permute-start(bf16[2,48,1024]{2,1,0:T(8,128)(2,1)S(1)} %get-tuple-element.13), channel_id=1, source_target_pairs={{0,4},{2,6},{4,8},{6,10},{8,12},{10,14},{12,0},{14,2},{1,5},{3,7},... | collective-permute-start | bytes 589832 | tf_op jit(solution)/shard_map/ppermute | solution.py:147
  63.0 15.5 %collective-permute-start.13 = (bf16[2,48,1024]{2,1,0:T(8,128)(2,1)S(1)}, bf16[2,48,1024]{2,1,0:T(8,128)(2,1)S(1)}, u32[]{:S(2)}, u32[]{:S(2)}) collective-permute-start(bf16[2,48,1024]{2,1,0:T(8,128)(2,1)S(1)} %get-tuple-element.15), channel_id=1, source_target_pairs={{0,8},{2,10},{4,12},{6,14},{8,0},{10,2},{12,4},{14,6},{1,9},{3,11}... | collective-permute-start | bytes 589832 | tf_op jit(solution)/shard_map/ppermute | solution.py:147
  65.0 15.0 %collective-permute-start.17 = (bf16[2,48,1024]{2,1,0:T(8,128)(2,1)S(1)}, bf16[2,48,1024]{2,1,0:T(8,128)(2,1)S(1)}, u32[]{:S(2)}, u32[]{:S(2)}) collective-permute-start(bf16[2,48,1024]{2,1,0:T(8,128)(2,1)S(1)} %get-tuple-element.14), channel_id=1, source_target_pairs={{0,12},{2,14},{4,0},{6,2},{8,4},{10,6},{12,8},{14,10},{1,13},{3,15... | collective-permute-start | bytes 589832 | tf_op jit(solution)/shard_map/ppermute | solution.py:147
  70.8 9.7 %collective-permute-start.10 = (bf16[96,1024]{1,0:T(8,128)(2,1)S(1)}, bf16[96,1024]{1,0:T(8,128)(2,1)S(1)}, u32[]{:S(2)}, u32[]{:S(2)}) collective-permute-start(bf16[96,1024]{1,0:T(8,128)(2,1)S(1)} %bitcast.223), channel_id=1, source_target_pairs={{0,1},{1,0},{2,3},{3,2},{4,5},{5,4},{6,7},{7,6},{8,9},{9,8},{10,11... | collective-permute-start | bytes 589832 | tf_op jit(solution)/shard_map/ppermute | solution.py:49
  72.7 31.6 %collective-permute-start.7 = (bf16[96,1024]{1,0:T(8,128)(2,1)S(1)}, bf16[96,1024]{1,0:T(8,128)(2,1)S(1)}, u32[]{:S(2)}, u32[]{:S(2)}) collective-permute-start(bf16[96,1024]{1,0:T(8,128)(2,1)S(1)} %convolution_convert_fusion.5), channel_id=1, source_target_pairs={{0,1},{1,0},{2,3},{3,2},{4,5},{5,4},{6,7},{7,6},{8,9},{9,8},{10,11... | collective-permute-start | bytes 589832 | tf_op jit(solution)/shard_map/ppermute | solution.py:49
  78.5 7.8 %collective-permute-start.14 = (bf16[96,1024]{1,0:T(8,128)(2,1)S(1)}, bf16[96,1024]{1,0:T(8,128)(2,1)S(1)}, u32[]{:S(2)}, u32[]{:S(2)}) collective-permute-start(bf16[96,1024]{1,0:T(8,128)(2,1)S(1)} %bitcast.220), channel_id=1, source_target_pairs={{0,1},{1,0},{2,3},{3,2},{4,5},{5,4},{6,7},{7,6},{8,9},{9,8},{10,11... | collective-permute-start | bytes 589832 | tf_op jit(solution)/shard_map/ppermute | solution.py:49
  80.0 10.5 %collective-permute-start.18 = (bf16[96,1024]{1,0:T(8,128)(2,1)S(1)}, bf16[96,1024]{1,0:T(8,128)(2,1)S(1)}, u32[]{:S(2)}, u32[]{:S(2)}) collective-permute-start(bf16[96,1024]{1,0:T(8,128)(2,1)S(1)} %bitcast.217), channel_id=1, source_target_pairs={{0,1},{1,0},{2,3},{3,2},{4,5},{5,4},{6,7},{7,6},{8,9},{9,8},{10,11... | collective-permute-start | bytes 589832 | tf_op jit(solution)/shard_map/ppermute | solution.py:49
  82.3 12.4 %collective-permute-start.11 = (bf16[96,1024]{1,0:T(8,128)(2,1)S(1)}, bf16[96,1024]{1,0:T(8,128)(2,1)S(1)}, u32[]{:S(2)}, u32[]{:S(2)}) collective-permute-start(bf16[96,1024]{1,0:T(8,128)(2,1)S(1)} %convolution_convert_fusion.4), channel_id=1, source_target_pairs={{0,1},{1,0},{2,3},{3,2},{4,5},{5,4},{6,7},{7,6},{8,9},{9,8},{10,11... | collective-permute-start | bytes 589832 | tf_op jit(solution)/shard_map/ppermute | solution.py:49
  88.0 11.1 %collective-permute-start.15 = (bf16[96,1024]{1,0:T(8,128)(2,1)S(1)}, bf16[96,1024]{1,0:T(8,128)(2,1)S(1)}, u32[]{:S(2)}, u32[]{:S(2)}) collective-permute-start(bf16[96,1024]{1,0:T(8,128)(2,1)S(1)} %convolution_convert_fusion.3), channel_id=1, source_target_pairs={{0,1},{1,0},{2,3},{3,2},{4,5},{5,4},{6,7},{7,6},{8,9},{9,8},{10,11... | collective-permute-start | bytes 589832 | tf_op jit(solution)/shard_map/ppermute | solution.py:49
  92.2 9.8 %collective-permute-start.19 = (bf16[96,1024]{1,0:T(8,128)(2,1)S(1)}, bf16[96,1024]{1,0:T(8,128)(2,1)S(1)}, u32[]{:S(2)}, u32[]{:S(2)}) collective-permute-start(bf16[96,1024]{1,0:T(8,128)(2,1)S(1)} %convolution_convert_fusion.2), channel_id=1, source_target_pairs={{0,1},{1,0},{2,3},{3,2},{4,5},{5,4},{6,7},{7,6},{8,9},{9,8},{10,11... | collective-permute-start | bytes 589832 | tf_op jit(solution)/shard_map/ppermute | solution.py:49
  95.0 9.6 %collective-permute-start.12 = (bf16[2,48,1024]{2,1,0:T(8,128)(2,1)S(1)}, bf16[2,48,1024]{2,1,0:T(8,128)(2,1)S(1)}, u32[]{:S(2)}, u32[]{:S(2)}) collective-permute-start(bf16[2,48,1024]{2,1,0:T(8,128)(2,1)S(1)} %bitcast.226), channel_id=1, source_target_pairs={{0,12},{2,14},{4,0},{6,2},{8,4},{10,6},{12,8},{14,10},{1,13},{3,15... | collective-permute-start | bytes 589832 | tf_op jit(solution)/shard_map/ppermute | solution.py:185
  99.4 14.2 %collective-permute-start.16 = (bf16[2,48,1024]{2,1,0:T(8,128)(2,1)S(1)}, bf16[2,48,1024]{2,1,0:T(8,128)(2,1)S(1)}, u32[]{:S(2)}, u32[]{:S(2)}) collective-permute-start(bf16[2,48,1024]{2,1,0:T(8,128)(2,1)S(1)} %bitcast.227), channel_id=1, source_target_pairs={{0,8},{2,10},{4,12},{6,14},{8,0},{10,2},{12,4},{14,6},{1,9},{3,11}... | collective-permute-start | bytes 589832 | tf_op jit(solution)/shard_map/ppermute | solution.py:185
  102.4 11.3 %collective-permute-start.20 = (bf16[2,48,1024]{2,1,0:T(8,128)(2,1)S(1)}, bf16[2,48,1024]{2,1,0:T(8,128)(2,1)S(1)}, u32[]{:S(2)}, u32[]{:S(2)}) collective-permute-start(bf16[2,48,1024]{2,1,0:T(8,128)(2,1)S(1)} %bitcast.228), channel_id=1, source_target_pairs={{0,4},{2,6},{4,8},{6,10},{8,12},{10,14},{12,0},{14,2},{1,5},{3,7},... | collective-permute-start | bytes 589832 | tf_op jit(solution)/shard_map/ppermute | solution.py:185
  113.6 1.2 copy-start.4
  113.8 2.8 %collective-permute-start.21 = (bf16[4,48,1024]{2,1,0:T(8,128)(2,1)S(1)}, bf16[4,48,1024]{2,1,0:T(8,128)(2,1)S(1)}, u32[]{:S(2)}, u32[]{:S(2)}) collective-permute-start(bf16[4,48,1024]{2,1,0:T(8,128)(2,1)S(1)} %get-tuple-element.12), channel_id=1, source_target_pairs={{0,2},{2,0},{4,6},{6,4},{8,10},{10,8},{12,14},{14,12},{1,3},{3,1},... | collective-permute-start | bytes 1179656 | tf_op jit(solution)/shard_map/ppermute | solution.py:187
  117.2 4.3 %collective-permute-start.22 = (bf16[32,1024]{1,0:T(8,128)(2,1)S(1)}, bf16[32,1024]{1,0:T(8,128)(2,1)S(1)}, u32[]{:S(2)}, u32[]{:S(2)}) collective-permute-start(bf16[32,1024]{1,0:T(8,128)(2,1)S(1)} %select_convert_fusion), channel_id=1, source_target_pairs={{0,1},{1,0},{2,3},{3,2},{4,5},{5,4},{6,7},{7,6},{8,9},{9,8},{10,11... | collective-permute-start | bytes 196616 | tf_op jit(solution)/shard_map/ppermute | solution.py:49
  (1 other events, 1.0 us)
Sparse Core Ops, SparseCore 0:
  9.6 34.5 all-gather.1

commit v17 on v16

--- a/solution.py
+++ b/solution.py
@@ -137,10 +137,16 @@
     ).astype(jnp.bfloat16)
     far = far.reshape(2, n_chip - 1, capacity, half_d)
     core_swap = [(i, i ^ 1) for i in range(n_ctx)]
+    near_rows = capacity * full_d // half_d
+    to_partner = jnp.concatenate(
+        [near[1].reshape(near_rows, half_d), far[1].reshape(-1, half_d)], axis=0
+    )
+    from_partner = lax.ppermute(to_partner, "ctx", perm=core_swap)
     near_in = jnp.concatenate(
-        [near[0], lax.ppermute(near[1], "ctx", perm=core_swap)], axis=0
-    )
-    far_pairs = jnp.stack([far[0], lax.ppermute(far[1], "ctx", perm=core_swap)], axis=1)
+        [near[0], from_partner[:near_rows].reshape(capacity, full_d)], axis=0
+    )
+    far_from_partner = from_partner[near_rows:].reshape(n_chip - 1, capacity, half_d)
+    far_pairs = jnp.stack([far[0], far_from_partner], axis=1)
     arrived = [None]
     for shift in range(1, n_chip):
         perm = [(i, ((i // 2 + shift) % n_chip) * 2 + i % 2) for i in range(n_ctx)]

time: 130 us -> 135 us (1.038)
  local copies, waits for them, and re-layouts: 6.87 us -> 10.5 us
  starting transfers between devices: 31.6 us -> 34.6 us
  matrix products: 15.7 us -> 13.6 us
    ppermute x3, starting transfers between devices: 6.11 us -> 9.7 us  [moe_column_halves(): returned[shift] = lax.ppermute(summed[idx], 'ctx', perm=perm)]
    ppermute x10, waiting for transfers between devices: 15.2 us -> 12.7 us  [exp_swap(): return lax.ppermute(x, 'exp', perm=[(0, 1), (1, 0)])]
    ppermute x2 -> x1, waiting for transfers between devices: 0.23 us -> 2.2 us  [moe_column_halves(): from_partner = lax.ppermute(to_partner, 'ctx', perm=core_swap)]
    slice x2 -> x4, local copies, waits for them, and re-layouts: 0.96 us -> 2.9 us  [the longest x1 1.62 us: moe_column_halves(): from_partner[:near_rows].reshape(capacity, full_d)]
    reshape x0 -> x1, local copies, waits for them, and re-layouts: none -> 1.69 us  [moe_column_halves(): from_partner[:near_rows].reshape(capacity, full_d)]
  transfers between devices with their start and end apart: 24 -> 23, of which waited for: 13 -> 12; matrix products, arithmetic and copies ran while one was open for 17% -> 14% of each run, Pallas kernels for 0% -> 0%
where the time goes in v17:
time: 135 us; the launch traced here: 134 us
  waiting for transfers between devices  53.8 us (40%)
  starting transfers between devices  34.6 us (26%)
  between operations  15.3 us (11%)
  matrix products  13.6 us (10%)
  local copies, waits for them, and re-layouts  10.5 us (8%)
  other arithmetic  6.49 us (5%)
    all_gather x1, waiting for transfers between devices, local(): lax.all_gather(out_weight, 'ctx', axis=0, tiled=True)  16.7 us
    ppermute x10, starting transfers between devices, exp_swap(): return lax.ppermute(x, 'exp', perm=[(0, 1), (1, 0)])  13.8 us
    ppermute x10, waiting for transfers between devices, exp_swap(): return lax.ppermute(x, 'exp', perm=[(0, 1), (1, 0)])  12.7 us
    ppermute x3, waiting for transfers between devices, moe_column_halves(): arrived.append(lax.ppermute(far_pairs[shift - 1], 'ctx', perm=perm))  9.91 us
    ppermute x3, starting transfers between devices, moe_column_halves(): returned[shift] = lax.ppermute(summed[idx], 'ctx', perm=perm)  9.7 us
    ppermute x3, waiting for transfers between devices, moe_column_halves(): returned[shift] = lax.ppermute(summed[idx], 'ctx', perm=perm)  8.92 us
    ppermute x3, starting transfers between devices, ctx_gather_blocks(): stack.append(lax.ppermute(rows, 'ctx', perm=perm))  7.03 us
    ppermute x3, starting transfers between devices, moe_column_halves(): arrived.append(lax.ppermute(far_pairs[shift - 1], 'ctx', perm=perm))  3.88 us
  transfers between devices with their start and end apart: 23, of which 12 were waited for; matrix products, arithmetic and copies ran while one was open for 14% of the time, Pallas kernels for 0%

profile of v17, /device:TPU:0, one launch (start us, length us, event | category | flops | bytes accessed | tf_op | source)
XLA Modules:
  0.0 134.3 jit_solution(12116660633230872078)
XLA Ops:
  8.8 3.1 %collective-permute-start.1 = (bf16[64,1024]{1,0:T(8,128)(2,1)S(1)}, bf16[64,1024]{1,0:T(8,128)(2,1)S(1)}, u32[]{:S(2)}, u32[]{:S(2)}) collective-permute-start(bf16[64,1024]{1,0:T(8,128)(2,1)S(1)} %get-tuple-element.21), channel_id=1, source_target_pairs={{0,4},{2,6},{4,8},{6,10},{8,12},{10,14},{12,0},{14,2},{1,5},{3,7},... | collective-permute-start | bytes 393224 | tf_op jit(solution)/shard_map/ppermute | solution.py:213
  11.9 2.6 %collective-permute-start.2 = (bf16[64,1024]{1,0:T(8,128)(2,1)S(1)}, bf16[64,1024]{1,0:T(8,128)(2,1)S(1)}, u32[]{:S(2)}, u32[]{:S(2)}) collective-permute-start(bf16[64,1024]{1,0:T(8,128)(2,1)S(1)} %get-tuple-element.21), channel_id=1, source_target_pairs={{0,8},{2,10},{4,12},{6,14},{8,0},{10,2},{12,4},{14,6},{1,9},{3,11}... | collective-permute-start | bytes 393224 | tf_op jit(solution)/shard_map/ppermute | solution.py:213
  14.5 1.4 %collective-permute-start.3 = (bf16[64,1024]{1,0:T(8,128)(2,1)S(1)}, bf16[64,1024]{1,0:T(8,128)(2,1)S(1)}, u32[]{:S(2)}, u32[]{:S(2)}) collective-permute-start(bf16[64,1024]{1,0:T(8,128)(2,1)S(1)} %get-tuple-element.21), channel_id=1, source_target_pairs={{0,12},{2,14},{4,0},{6,2},{8,4},{10,6},{12,8},{14,10},{1,13},{3,15... | collective-permute-start | bytes 393224 | tf_op jit(solution)/shard_map/ppermute | solution.py:213
  15.8 1.5 %collective-permute-start = (bf16[32,2048]{1,0:T(8,128)(2,1)}, bf16[32,2048]{1,0:T(8,128)(2,1)}, u32[]{:S(2)}, u32[]{:S(2)}) collective-permute-start(bf16[32,2048]{1,0:T(8,128)(2,1)} %bitcast.231), channel_id=1, source_target_pairs={{0,1},{1,0},{2,3},{3,2},{4,5},{5,4},{6,7},{7,6},{8,9},{9,8},{10,11... | collective-permute-start | bytes 393224 | tf_op jit(solution)/shard_map/ppermute | solution.py:49
  22.2 0.9 collective-permute-done.2
  23.3 1.8 %collective-permute-done.4 = bf16[4,64,1024]{2,1,0:T(8,128)(2,1)S(1)} collective-permute-done((bf16[4,64,1024]{2,1,0:T(8,128)(2,1)S(1)}, bf16[4,64,1024]{2,1,0:T(8,128)(2,1)S(1)}, u32[]{:S(2)}, u32[]{:S(2)}) %collective-permute-start.4) | collective-permute-done | bytes 524320 | tf_op jit(solution)/shard_map/ppermute | solution.py:215
  27.6 16.7 %all-gather.2.cloned.1.call-done = bf16[2048,512]{1,0:T(8,128)(2,1)} async-done(((bf16[256,512]{1,0:T(8,128)(2,1)}), bf16[2048,512]{1,0:T(8,128)(2,1)}) %all-gather.2.cloned.1.call-update) | async-done | bytes 2097168 | tf_op jit(solution)/shard_map/all_gather | solution.py:285
  44.2 2.3 %fusion.162 = (bf16[64,2048]{1,0:T(8,128)(2,1)S(1)}, f32[64,2048]{1,0:T(8,128)S(1)}) fusion(bf16[2048,512]{1,0:T(8,128)(2,1)} %all-gather.2.cloned.1.call-done, bf16[4,8,8,128]{3,2,1,0:T(8,128)(2,1)S(1)} %fusion.14), kind=kOutput, calls=%fused_computation.246 | convolution fusion | flops 134348800 | bytes 2949120 | tf_op jit(solution)/shard_map/tc,oc->to/dot_general | solution.py:282
  46.6 1.6 %collective-permute-start.5 = (bf16[64,2048]{1,0:T(8,128)(2,1)S(1)}, bf16[64,2048]{1,0:T(8,128)(2,1)S(1)}, u32[]{:S(2)}, u32[]{:S(2)}) collective-permute-start(bf16[64,2048]{1,0:T(8,128)(2,1)S(1)} %get-tuple-element.24), channel_id=1, source_target_pairs={{0,1},{1,0},{2,3},{3,2},{4,5},{5,4},{6,7},{7,6},{8,9},{9,8},{10,11... | collective-permute-start | bytes 786440 | tf_op jit(solution)/shard_map/ppermute | solution.py:49
  49.0 6.1 %collective-permute-done.5 = bf16[64,2048]{1,0:T(8,128)(2,1)S(1)} collective-permute-done((bf16[64,2048]{1,0:T(8,128)(2,1)S(1)}, bf16[64,2048]{1,0:T(8,128)(2,1)S(1)}, u32[]{:S(2)}, u32[]{:S(2)}) %collective-permute-start.5) | collective-permute-done | bytes 262176 | tf_op jit(solution)/shard_map/ppermute | solution.py:49
  55.1 1.2 fusion.59
  58.7 2.2 %collective-permute-done.6 = bf16[240,1024]{1,0:T(8,128)(2,1)} collective-permute-done((bf16[240,1024]{1,0:T(8,128)(2,1)}, bf16[240,1024]{1,0:T(8,128)(2,1)}, u32[]{:S(2)}, u32[]{:S(2)}) %collective-permute-start.6) | collective-permute-done | bytes 491552 | tf_op jit(solution)/shard_map/ppermute | solution.py:144
  60.9 1.6 %slice.110 = bf16[96,1024]{1,0:T(8,128)(2,1)} slice(bf16[240,1024]{1,0:T(8,128)(2,1)} %collective-permute-done.6), slice={[0:96], [0:1024]} | slice | bytes 393216 | tf_op jit(solution)/shard_map/slice | solution.py:146
  62.5 1.7 %reshape.365 = bf16[48,2048]{1,0:T(8,128)(2,1)} reshape(bf16[96,1024]{1,0:T(8,128)(2,1)} %slice.110) | data formatting | bytes 393216 | tf_op jit(solution)/shard_map/reshape | solution.py:146
  64.2 1.0 slice.112
  65.6 1.9 %collective-permute-start.12 = (bf16[2,48,1024]{2,1,0:T(8,128)(2,1)S(1)}, bf16[2,48,1024]{2,1,0:T(8,128)(2,1)S(1)}, u32[]{:S(2)}, u32[]{:S(2)}) collective-permute-start(bf16[2,48,1024]{2,1,0:T(8,128)(2,1)S(1)} %get-tuple-element.15), channel_id=1, source_target_pairs={{0,8},{2,10},{4,12},{6,14},{8,0},{10,2},{12,4},{14,6},{1,9},{3,11}... | collective-permute-start | bytes 589832 | tf_op jit(solution)/shard_map/ppermute | solution.py:153
  67.6 1.6 %collective-permute-start.16 = (bf16[2,48,1024]{2,1,0:T(8,128)(2,1)S(1)}, bf16[2,48,1024]{2,1,0:T(8,128)(2,1)S(1)}, u32[]{:S(2)}, u32[]{:S(2)}) collective-permute-start(bf16[2,48,1024]{2,1,0:T(8,128)(2,1)S(1)} %get-tuple-element.14), channel_id=1, source_target_pairs={{0,12},{2,14},{4,0},{6,2},{8,4},{10,6},{12,8},{14,10},{1,13},{3,15... | collective-permute-start | bytes 589832 | tf_op jit(solution)/shard_map/ppermute | solution.py:153
  70.4 4.7 %collective-permute-done.8 = bf16[2,48,1024]{2,1,0:T(8,128)(2,1)S(1)} collective-permute-done((bf16[2,48,1024]{2,1,0:T(8,128)(2,1)S(1)}, bf16[2,48,1024]{2,1,0:T(8,128)(2,1)S(1)}, u32[]{:S(2)}, u32[]{:S(2)}) %collective-permute-start.8) | collective-permute-done | bytes 196640 | tf_op jit(solution)/shard_map/ppermute | solution.py:153
  75.1 1.5 %collective-permute-start.9 = (bf16[96,1024]{1,0:T(8,128)(2,1)S(1)}, bf16[96,1024]{1,0:T(8,128)(2,1)S(1)}, u32[]{:S(2)}, u32[]{:S(2)}) collective-permute-start(bf16[96,1024]{1,0:T(8,128)(2,1)S(1)} %bitcast.225), channel_id=1, source_target_pairs={{0,1},{1,0},{2,3},{3,2},{4,5},{5,4},{6,7},{7,6},{8,9},{9,8},{10,11... | collective-permute-start | bytes 589832 | tf_op jit(solution)/shard_map/ppermute | solution.py:49
  77.5 5.2 %collective-permute-done.12 = bf16[2,48,1024]{2,1,0:T(8,128)(2,1)S(1)} collective-permute-done((bf16[2,48,1024]{2,1,0:T(8,128)(2,1)S(1)}, bf16[2,48,1024]{2,1,0:T(8,128)(2,1)S(1)}, u32[]{:S(2)}, u32[]{:S(2)}) %collective-permute-start.12) | collective-permute-done | bytes 196640 | tf_op jit(solution)/shard_map/ppermute | solution.py:153
  82.7 1.5 %collective-permute-start.13 = (bf16[96,1024]{1,0:T(8,128)(2,1)S(1)}, bf16[96,1024]{1,0:T(8,128)(2,1)S(1)}, u32[]{:S(2)}, u32[]{:S(2)}) collective-permute-start(bf16[96,1024]{1,0:T(8,128)(2,1)S(1)} %bitcast.222), channel_id=1, source_target_pairs={{0,1},{1,0},{2,3},{3,2},{4,5},{5,4},{6,7},{7,6},{8,9},{9,8},{10,11... | collective-permute-start | bytes 589832 | tf_op jit(solution)/shard_map/ppermute | solution.py:49
  86.5 1.6 %collective-permute-start.10 = (bf16[96,1024]{1,0:T(8,128)(2,1)S(1)}, bf16[96,1024]{1,0:T(8,128)(2,1)S(1)}, u32[]{:S(2)}, u32[]{:S(2)}) collective-permute-start(bf16[96,1024]{1,0:T(8,128)(2,1)S(1)} %convolution_convert_fusion.4), channel_id=1, source_target_pairs={{0,1},{1,0},{2,3},{3,2},{4,5},{5,4},{6,7},{7,6},{8,9},{9,8},{10,11... | collective-permute-start | bytes 589832 | tf_op jit(solution)/shard_map/ppermute | solution.py:49
  88.1 2.4 %collective-permute-done.13 = bf16[96,1024]{1,0:T(8,128)(2,1)S(1)} collective-permute-done((bf16[96,1024]{1,0:T(8,128)(2,1)S(1)}, bf16[96,1024]{1,0:T(8,128)(2,1)S(1)}, u32[]{:S(2)}, u32[]{:S(2)}) %collective-permute-start.13) | collective-permute-done | bytes 196640 | tf_op jit(solution)/shard_map/ppermute | solution.py:49
  92.3 1.6 %collective-permute-start.14 = (bf16[96,1024]{1,0:T(8,128)(2,1)S(1)}, bf16[96,1024]{1,0:T(8,128)(2,1)S(1)}, u32[]{:S(2)}, u32[]{:S(2)}) collective-permute-start(bf16[96,1024]{1,0:T(8,128)(2,1)S(1)} %convolution_convert_fusion.3), channel_id=1, source_target_pairs={{0,1},{1,0},{2,3},{3,2},{4,5},{5,4},{6,7},{7,6},{8,9},{9,8},{10,11... | collective-permute-start | bytes 589832 | tf_op jit(solution)/shard_map/ppermute | solution.py:49
  96.5 1.6 %collective-permute-start.18 = (bf16[96,1024]{1,0:T(8,128)(2,1)S(1)}, bf16[96,1024]{1,0:T(8,128)(2,1)S(1)}, u32[]{:S(2)}, u32[]{:S(2)}) collective-permute-start(bf16[96,1024]{1,0:T(8,128)(2,1)S(1)} %convolution_convert_fusion.2), channel_id=1, source_target_pairs={{0,1},{1,0},{2,3},{3,2},{4,5},{5,4},{6,7},{7,6},{8,9},{9,8},{10,11... | collective-permute-start | bytes 589832 | tf_op jit(solution)/shard_map/ppermute | solution.py:49
  99.3 4.1 %collective-permute-start.11 = (bf16[2,48,1024]{2,1,0:T(8,128)(2,1)S(1)}, bf16[2,48,1024]{2,1,0:T(8,128)(2,1)S(1)}, u32[]{:S(2)}, u32[]{:S(2)}) collective-permute-start(bf16[2,48,1024]{2,1,0:T(8,128)(2,1)S(1)} %bitcast.228), channel_id=1, source_target_pairs={{0,12},{2,14},{4,0},{6,2},{8,4},{10,6},{12,8},{14,10},{1,13},{3,15... | collective-permute-start | bytes 589832 | tf_op jit(solution)/shard_map/ppermute | solution.py:191
  103.7 3.8 %collective-permute-start.15 = (bf16[2,48,1024]{2,1,0:T(8,128)(2,1)S(1)}, bf16[2,48,1024]{2,1,0:T(8,128)(2,1)S(1)}, u32[]{:S(2)}, u32[]{:S(2)}) collective-permute-start(bf16[2,48,1024]{2,1,0:T(8,128)(2,1)S(1)} %bitcast.229), channel_id=1, source_target_pairs={{0,8},{2,10},{4,12},{6,14},{8,0},{10,2},{12,4},{14,6},{1,9},{3,11}... | collective-permute-start | bytes 589832 | tf_op jit(solution)/shard_map/ppermute | solution.py:191
  107.7 1.8 %collective-permute-start.19 = (bf16[2,48,1024]{2,1,0:T(8,128)(2,1)S(1)}, bf16[2,48,1024]{2,1,0:T(8,128)(2,1)S(1)}, u32[]{:S(2)}, u32[]{:S(2)}) collective-permute-start(bf16[2,48,1024]{2,1,0:T(8,128)(2,1)S(1)} %bitcast.230), channel_id=1, source_target_pairs={{0,4},{2,6},{4,8},{6,10},{8,12},{10,14},{12,0},{14,2},{1,5},{3,7},... | collective-permute-start | bytes 589832 | tf_op jit(solution)/shard_map/ppermute | solution.py:191
  109.9 8.9 %collective-permute-done.15 = bf16[2,48,1024]{2,1,0:T(8,128)(2,1)S(1)} collective-permute-done((bf16[2,48,1024]{2,1,0:T(8,128)(2,1)S(1)}, bf16[2,48,1024]{2,1,0:T(8,128)(2,1)S(1)}, u32[]{:S(2)}, u32[]{:S(2)}) %collective-permute-start.15) | collective-permute-done | bytes 196640 | tf_op jit(solution)/shard_map/ppermute | solution.py:191
  119.1 1.0 copy-done.4
  122.4 1.8 %collective-permute-start.21 = (bf16[32,1024]{1,0:T(8,128)(2,1)S(1)}, bf16[32,1024]{1,0:T(8,128)(2,1)S(1)}, u32[]{:S(2)}, u32[]{:S(2)}) collective-permute-start(bf16[32,1024]{1,0:T(8,128)(2,1)S(1)} %select_convert_fusion), channel_id=1, source_target_pairs={{0,1},{1,0},{2,3},{3,2},{4,5},{5,4},{6,7},{7,6},{8,9},{9,8},{10,11... | collective-permute-start | bytes 196616 | tf_op jit(solution)/shard_map/ppermute | solution.py:49
  124.2 2.5 %collective-permute-done.21 = bf16[32,1024]{1,0:T(8,128)(2,1)S(1)} collective-permute-done((bf16[32,1024]{1,0:T(8,128)(2,1)S(1)}, bf16[32,1024]{1,0:T(8,128)(2,1)S(1)}, u32[]{:S(2)}, u32[]{:S(2)}) %collective-permute-start.21) | collective-permute-done | bytes 65568 | tf_op jit(solution)/shard_map/ppermute | solution.py:49
  (122 shorter events, 25.6 us)
Async XLA Ops:
  7.2 69.4 %copy-start = (bf16[1,352,2048]{2,1,0:T(8,128)(2,1)S(1)}, bf16[1,352,2048]{2,1,0:T(8,128)(2,1)}, u32[]{:S(2)}) copy-start(bf16[1,352,2048]{2,1,0:T(8,128)(2,1)} %param.20) | copy-start | bytes 4325380
  7.2 37.1 %all-gather.2.cloned.1.call-start = ((), (), s32[]{:S(2)}) async-start(), calls=%async_computation | async-start | bytes 2359296 | tf_op jit(solution)/shard_map/all_gather | solution.py:285
  8.8 13.4 %collective-permute-start.1 = (bf16[64,1024]{1,0:T(8,128)(2,1)S(1)}, bf16[64,1024]{1,0:T(8,128)(2,1)S(1)}, u32[]{:S(2)}, u32[]{:S(2)}) collective-permute-start(bf16[64,1024]{1,0:T(8,128)(2,1)S(1)} %get-tuple-element.21), channel_id=1, source_target_pairs={{0,4},{2,6},{4,8},{6,10},{8,12},{10,14},{12,0},{14,2},{1,5},{3,7},... | collective-permute-start | bytes 393224 | tf_op jit(solution)/shard_map/ppermute | solution.py:213
  11.9 11.2 %collective-permute-start.2 = (bf16[64,1024]{1,0:T(8,128)(2,1)S(1)}, bf16[64,1024]{1,0:T(8,128)(2,1)S(1)}, u32[]{:S(2)}, u32[]{:S(2)}) collective-permute-start(bf16[64,1024]{1,0:T(8,128)(2,1)S(1)} %get-tuple-element.21), channel_id=1, source_target_pairs={{0,8},{2,10},{4,12},{6,14},{8,0},{10,2},{12,4},{14,6},{1,9},{3,11}... | collective-permute-start | bytes 393224 | tf_op jit(solution)/shard_map/ppermute | solution.py:213
  14.5 8.6 %collective-permute-start.3 = (bf16[64,1024]{1,0:T(8,128)(2,1)S(1)}, bf16[64,1024]{1,0:T(8,128)(2,1)S(1)}, u32[]{:S(2)}, u32[]{:S(2)}) collective-permute-start(bf16[64,1024]{1,0:T(8,128)(2,1)S(1)} %get-tuple-element.21), channel_id=1, source_target_pairs={{0,12},{2,14},{4,0},{6,2},{8,4},{10,6},{12,8},{14,10},{1,13},{3,15... | collective-permute-start | bytes 393224 | tf_op jit(solution)/shard_map/ppermute | solution.py:213
  15.8 33.2 %collective-permute-start = (bf16[32,2048]{1,0:T(8,128)(2,1)}, bf16[32,2048]{1,0:T(8,128)(2,1)}, u32[]{:S(2)}, u32[]{:S(2)}) collective-permute-start(bf16[32,2048]{1,0:T(8,128)(2,1)} %bitcast.231), channel_id=1, source_target_pairs={{0,1},{1,0},{2,3},{3,2},{4,5},{5,4},{6,7},{7,6},{8,9},{9,8},{10,11... | collective-permute-start | bytes 393224 | tf_op jit(solution)/shard_map/ppermute | solution.py:49
  23.2 2.0 %collective-permute-start.4 = (bf16[4,64,1024]{2,1,0:T(8,128)(2,1)S(1)}, bf16[4,64,1024]{2,1,0:T(8,128)(2,1)S(1)}, u32[]{:S(2)}, u32[]{:S(2)}) collective-permute-start(bf16[4,64,1024]{2,1,0:T(8,128)(2,1)S(1)} %pad_maximum_fusion.2), channel_id=1, source_target_pairs={{0,2},{2,0},{4,6},{6,4},{8,10},{10,8},{12,14},{14,12},{1,3},{3,1},... | collective-permute-start | bytes 1572872 | tf_op jit(solution)/shard_map/ppermute | solution.py:215
  27.5 20.8 %copy-start.9 = (f32[1,64,4]{1,2,0:T(4,128)S(1)}, f32[1,64,4]{1,2,0:T(4,128)}, u32[]{:S(2)}) copy-start(f32[1,64,4]{1,2,0:T(4,128)} %param.22) | copy-start | bytes 3076
  27.5 27.6 %copy-start.7 = (bf16[1,32,2048]{2,1,0:T(8,128)(2,1)S(1)}, bf16[1,32,2048]{2,1,0:T(8,128)(2,1)}, u32[]{:S(2)}) copy-start(bf16[1,32,2048]{2,1,0:T(8,128)(2,1)} %param.15) | copy-start | bytes 393220
  46.6 9.8 %copy-start.8 = (f32[2048]{0:T(1024)S(1)}, f32[2048]{0:T(1024)}, u32[]{:S(2)}) copy-start(f32[2048]{0:T(1024)} %param.17) | copy-start | bytes 24580
  46.6 8.5 %collective-permute-start.5 = (bf16[64,2048]{1,0:T(8,128)(2,1)S(1)}, bf16[64,2048]{1,0:T(8,128)(2,1)S(1)}, u32[]{:S(2)}, u32[]{:S(2)}) collective-permute-start(bf16[64,2048]{1,0:T(8,128)(2,1)S(1)} %get-tuple-element.24), channel_id=1, source_target_pairs={{0,1},{1,0},{2,3},{3,2},{4,5},{5,4},{6,7},{7,6},{8,9},{9,8},{10,11... | collective-permute-start | bytes 786440 | tf_op jit(solution)/shard_map/ppermute | solution.py:49
  58.7 10.5 %copy-start.1 = (bf16[1,2048,352]{1,2,0:T(8,128)(2,1)S(1)}, bf16[1,2048,352]{1,2,0:T(8,128)(2,1)}, u32[]{:S(2)}) copy-start(bf16[1,2048,352]{1,2,0:T(8,128)(2,1)} %param.18) | copy-start | bytes 4325380
  58.7 2.2 %collective-permute-start.6 = (bf16[240,1024]{1,0:T(8,128)(2,1)}, bf16[240,1024]{1,0:T(8,128)(2,1)}, u32[]{:S(2)}, u32[]{:S(2)}) collective-permute-start(bf16[240,1024]{1,0:T(8,128)(2,1)} %pad_maximum_fusion.3), channel_id=1, source_target_pairs={{0,2},{2,0},{4,6},{6,4},{8,10},{10,8},{12,14},{14,12},{1,3},{3,1},... | collective-permute-start | bytes 1474568 | tf_op jit(solution)/shard_map/ppermute | solution.py:144
  64.2 5.0 %copy-start.5 = (bf16[48,2048]{1,0:T(8,128)(2,1)S(1)}, bf16[48,2048]{1,0:T(8,128)(2,1)}, u32[]{:S(2)}) copy-start(bf16[48,2048]{1,0:T(8,128)(2,1)} %reshape.365) | copy-start | bytes 589828
  64.2 5.0 %copy-start.6 = (bf16[48,2048]{1,0:T(8,128)(2,1)S(1)}, bf16[48,2048]{1,0:T(8,128)(2,1)}, u32[]{:S(2)}) copy-start(bf16[48,2048]{1,0:T(8,128)(2,1)} %get-tuple-element.18) | copy-start | bytes 589828
  65.3 4.5 %copy-start.2 = (bf16[1,2048,352]{1,2,0:T(8,128)(2,1)S(1)}, bf16[1,2048,352]{1,2,0:T(8,128)(2,1)}, u32[]{:S(2)}) copy-start(bf16[1,2048,352]{1,2,0:T(8,128)(2,1)} %param.19) | copy-start | bytes 4325380
  65.3 9.7 %collective-permute-start.8 = (bf16[2,48,1024]{2,1,0:T(8,128)(2,1)S(1)}, bf16[2,48,1024]{2,1,0:T(8,128)(2,1)S(1)}, u32[]{:S(2)}, u32[]{:S(2)}) collective-permute-start(bf16[2,48,1024]{2,1,0:T(8,128)(2,1)S(1)} %get-tuple-element.13), channel_id=1, source_target_pairs={{0,4},{2,6},{4,8},{6,10},{8,12},{10,14},{12,0},{14,2},{1,5},{3,7},... | collective-permute-start | bytes 589832 | tf_op jit(solution)/shard_map/ppermute | solution.py:153
  65.6 17.1 %collective-permute-start.12 = (bf16[2,48,1024]{2,1,0:T(8,128)(2,1)S(1)}, bf16[2,48,1024]{2,1,0:T(8,128)(2,1)S(1)}, u32[]{:S(2)}, u32[]{:S(2)}) collective-permute-start(bf16[2,48,1024]{2,1,0:T(8,128)(2,1)S(1)} %get-tuple-element.15), channel_id=1, source_target_pairs={{0,8},{2,10},{4,12},{6,14},{8,0},{10,2},{12,4},{14,6},{1,9},{3,11}... | collective-permute-start | bytes 589832 | tf_op jit(solution)/shard_map/ppermute | solution.py:153
  67.6 16.7 %collective-permute-start.16 = (bf16[2,48,1024]{2,1,0:T(8,128)(2,1)S(1)}, bf16[2,48,1024]{2,1,0:T(8,128)(2,1)S(1)}, u32[]{:S(2)}, u32[]{:S(2)}) collective-permute-start(bf16[2,48,1024]{2,1,0:T(8,128)(2,1)S(1)} %get-tuple-element.14), channel_id=1, source_target_pairs={{0,12},{2,14},{4,0},{6,2},{8,4},{10,6},{12,8},{14,10},{1,13},{3,15... | collective-permute-start | bytes 589832 | tf_op jit(solution)/shard_map/ppermute | solution.py:153
  75.1 9.7 %collective-permute-start.9 = (bf16[96,1024]{1,0:T(8,128)(2,1)S(1)}, bf16[96,1024]{1,0:T(8,128)(2,1)S(1)}, u32[]{:S(2)}, u32[]{:S(2)}) collective-permute-start(bf16[96,1024]{1,0:T(8,128)(2,1)S(1)} %bitcast.225), channel_id=1, source_target_pairs={{0,1},{1,0},{2,3},{3,2},{4,5},{5,4},{6,7},{7,6},{8,9},{9,8},{10,11... | collective-permute-start | bytes 589832 | tf_op jit(solution)/shard_map/ppermute | solution.py:49
  76.9 32.7 %collective-permute-start.7 = (bf16[96,1024]{1,0:T(8,128)(2,1)S(1)}, bf16[96,1024]{1,0:T(8,128)(2,1)S(1)}, u32[]{:S(2)}, u32[]{:S(2)}) collective-permute-start(bf16[96,1024]{1,0:T(8,128)(2,1)S(1)} %convolution_convert_fusion.5), channel_id=1, source_target_pairs={{0,1},{1,0},{2,3},{3,2},{4,5},{5,4},{6,7},{7,6},{8,9},{9,8},{10,11... | collective-permute-start | bytes 589832 | tf_op jit(solution)/shard_map/ppermute | solution.py:49
  82.7 7.8 %collective-permute-start.13 = (bf16[96,1024]{1,0:T(8,128)(2,1)S(1)}, bf16[96,1024]{1,0:T(8,128)(2,1)S(1)}, u32[]{:S(2)}, u32[]{:S(2)}) collective-permute-start(bf16[96,1024]{1,0:T(8,128)(2,1)S(1)} %bitcast.222), channel_id=1, source_target_pairs={{0,1},{1,0},{2,3},{3,2},{4,5},{5,4},{6,7},{7,6},{8,9},{9,8},{10,11... | collective-permute-start | bytes 589832 | tf_op jit(solution)/shard_map/ppermute | solution.py:49
  84.2 10.5 %collective-permute-start.17 = (bf16[96,1024]{1,0:T(8,128)(2,1)S(1)}, bf16[96,1024]{1,0:T(8,128)(2,1)S(1)}, u32[]{:S(2)}, u32[]{:S(2)}) collective-permute-start(bf16[96,1024]{1,0:T(8,128)(2,1)S(1)} %bitcast.219), channel_id=1, source_target_pairs={{0,1},{1,0},{2,3},{3,2},{4,5},{5,4},{6,7},{7,6},{8,9},{9,8},{10,11... | collective-permute-start | bytes 589832 | tf_op jit(solution)/shard_map/ppermute | solution.py:49
  86.5 12.5 %collective-permute-start.10 = (bf16[96,1024]{1,0:T(8,128)(2,1)S(1)}, bf16[96,1024]{1,0:T(8,128)(2,1)S(1)}, u32[]{:S(2)}, u32[]{:S(2)}) collective-permute-start(bf16[96,1024]{1,0:T(8,128)(2,1)S(1)} %convolution_convert_fusion.4), channel_id=1, source_target_pairs={{0,1},{1,0},{2,3},{3,2},{4,5},{5,4},{6,7},{7,6},{8,9},{9,8},{10,11... | collective-permute-start | bytes 589832 | tf_op jit(solution)/shard_map/ppermute | solution.py:49
  92.3 11.1 %collective-permute-start.14 = (bf16[96,1024]{1,0:T(8,128)(2,1)S(1)}, bf16[96,1024]{1,0:T(8,128)(2,1)S(1)}, u32[]{:S(2)}, u32[]{:S(2)}) collective-permute-start(bf16[96,1024]{1,0:T(8,128)(2,1)S(1)} %convolution_convert_fusion.3), channel_id=1, source_target_pairs={{0,1},{1,0},{2,3},{3,2},{4,5},{5,4},{6,7},{7,6},{8,9},{9,8},{10,11... | collective-permute-start | bytes 589832 | tf_op jit(solution)/shard_map/ppermute | solution.py:49
  96.5 10.9 %collective-permute-start.18 = (bf16[96,1024]{1,0:T(8,128)(2,1)S(1)}, bf16[96,1024]{1,0:T(8,128)(2,1)S(1)}, u32[]{:S(2)}, u32[]{:S(2)}) collective-permute-start(bf16[96,1024]{1,0:T(8,128)(2,1)S(1)} %convolution_convert_fusion.2), channel_id=1, source_target_pairs={{0,1},{1,0},{2,3},{3,2},{4,5},{5,4},{6,7},{7,6},{8,9},{9,8},{10,11... | collective-permute-start | bytes 589832 | tf_op jit(solution)/shard_map/ppermute | solution.py:49
  99.3 10.6 %collective-permute-start.11 = (bf16[2,48,1024]{2,1,0:T(8,128)(2,1)S(1)}, bf16[2,48,1024]{2,1,0:T(8,128)(2,1)S(1)}, u32[]{:S(2)}, u32[]{:S(2)}) collective-permute-start(bf16[2,48,1024]{2,1,0:T(8,128)(2,1)S(1)} %bitcast.228), channel_id=1, source_target_pairs={{0,12},{2,14},{4,0},{6,2},{8,4},{10,6},{12,8},{14,10},{1,13},{3,15... | collective-permute-start | bytes 589832 | tf_op jit(solution)/shard_map/ppermute | solution.py:191
  103.7 15.1 %collective-permute-start.15 = (bf16[2,48,1024]{2,1,0:T(8,128)(2,1)S(1)}, bf16[2,48,1024]{2,1,0:T(8,128)(2,1)S(1)}, u32[]{:S(2)}, u32[]{:S(2)}) collective-permute-start(bf16[2,48,1024]{2,1,0:T(8,128)(2,1)S(1)} %bitcast.229), channel_id=1, source_target_pairs={{0,8},{2,10},{4,12},{6,14},{8,0},{10,2},{12,4},{14,6},{1,9},{3,11}... | collective-permute-start | bytes 589832 | tf_op jit(solution)/shard_map/ppermute | solution.py:191
  107.7 11.1 %collective-permute-start.19 = (bf16[2,48,1024]{2,1,0:T(8,128)(2,1)S(1)}, bf16[2,48,1024]{2,1,0:T(8,128)(2,1)S(1)}, u32[]{:S(2)}, u32[]{:S(2)}) collective-permute-start(bf16[2,48,1024]{2,1,0:T(8,128)(2,1)S(1)} %bitcast.230), channel_id=1, source_target_pairs={{0,4},{2,6},{4,8},{6,10},{8,12},{10,14},{12,0},{14,2},{1,5},{3,7},... | collective-permute-start | bytes 589832 | tf_op jit(solution)/shard_map/ppermute | solution.py:191
  118.8 1.2 copy-start.4
  119.0 2.8 %collective-permute-start.20 = (bf16[4,48,1024]{2,1,0:T(8,128)(2,1)S(1)}, bf16[4,48,1024]{2,1,0:T(8,128)(2,1)S(1)}, u32[]{:S(2)}, u32[]{:S(2)}) collective-permute-start(bf16[4,48,1024]{2,1,0:T(8,128)(2,1)S(1)} %get-tuple-element.12), channel_id=1, source_target_pairs={{0,2},{2,0},{4,6},{6,4},{8,10},{10,8},{12,14},{14,12},{1,3},{3,1},... | collective-permute-start | bytes 1179656 | tf_op jit(solution)/shard_map/ppermute | solution.py:193
  122.4 4.3 %collective-permute-start.21 = (bf16[32,1024]{1,0:T(8,128)(2,1)S(1)}, bf16[32,1024]{1,0:T(8,128)(2,1)S(1)}, u32[]{:S(2)}, u32[]{:S(2)}) collective-permute-start(bf16[32,1024]{1,0:T(8,128)(2,1)S(1)} %select_convert_fusion), channel_id=1, source_target_pairs={{0,1},{1,0},{2,3},{3,2},{4,5},{5,4},{6,7},{7,6},{8,9},{9,8},{10,11... | collective-permute-start | bytes 196616 | tf_op jit(solution)/shard_map/ppermute | solution.py:49
  (1 other events, 1.0 us)
Sparse Core Ops, SparseCore 0:
  9.6 34.5 all-gather.1

commit v18 on v16

--- a/solution.py
+++ b/solution.py
@@ -154,7 +154,7 @@
     down_other = lax.dynamic_slice_in_dim(down_matrix, other_start, half_d, axis=1)
     down_mine = lax.dynamic_slice_in_dim(down_matrix, my_start, half_d, axis=1)
     if n_chip <= 4:
-        groups = [[0]] + [[k] for k in range(1, n_chip)]
+        groups = [[0], [1], list(range(2, n_chip))] if n_chip > 2 else [[0], [1]]
     else:
         groups = [[0], list(range(1, n_chip // 2)), list(range(n_chip // 2, n_chip))]
     returned = [None] * n_chip

time: 130 us -> 134 us (1.031)
  waiting for transfers between devices: 54 us -> 59.5 us
  matrix products: 15.7 us -> 14 us
    ppermute x10 -> x8, waiting for transfers between devices: 15.2 us -> 21.6 us  [exp_swap(): return lax.ppermute(x, 'exp', perm=[(0, 1), (1, 0)])]
    ppermute x10 -> x8, starting transfers between devices: 13.8 us -> 10.5 us  [exp_swap(): return lax.ppermute(x, 'exp', perm=[(0, 1), (1, 0)])]
    ppermute x3, starting transfers between devices: 6.11 us -> 9.06 us  [moe_column_halves(): returned[shift] = lax.ppermute(summed[idx], 'ctx', perm=perm)]
  transfers between devices with their start and end apart: 24 -> 22, of which waited for: 13 -> 11; matrix products, arithmetic and copies ran while one was open for 17% -> 16% of each run, Pallas kernels for 0% -> 0%
where the time goes in v18:
time: 134 us
  waiting for transfers between devices  59.5 us (44%)
  starting transfers between devices  31.3 us (23%)
  between operations  15.2 us (11%)
  matrix products  14 us (10%)
  local copies, waits for them, and re-layouts  6.87 us (5%)
  other arithmetic  6.81 us (5%)
    ppermute x8, waiting for transfers between devices, exp_swap(): return lax.ppermute(x, 'exp', perm=[(0, 1), (1, 0)])  21.6 us
    all_gather x1, waiting for transfers between devices, local(): lax.all_gather(out_weight, 'ctx', axis=0, tiled=True)  16.7 us
    ppermute x8, starting transfers between devices, exp_swap(): return lax.ppermute(x, 'exp', perm=[(0, 1), (1, 0)])  10.5 us
    ppermute x3, starting transfers between devices, moe_column_halves(): returned[shift] = lax.ppermute(summed[idx], 'ctx', perm=perm)  9.06 us
    ppermute x3, waiting for transfers between devices, moe_column_halves(): arrived.append(lax.ppermute(far_pairs[shift - 1], 'ctx', perm=perm))  8.67 us
    ppermute x3, waiting for transfers between devices, moe_column_halves(): returned[shift] = lax.ppermute(summed[idx], 'ctx', perm=perm)  8.5 us
    ppermute x3, starting transfers between devices, ctx_gather_blocks(): stack.append(lax.ppermute(rows, 'ctx', perm=perm))  7.03 us
    ppermute x3, starting transfers between devices, moe_column_halves(): arrived.append(lax.ppermute(far_pairs[shift - 1], 'ctx', perm=perm))  4.01 us
  transfers between devices with their start and end apart: 22, of which 11 were waited for; matrix products, arithmetic and copies ran while one was open for 16% of the time, Pallas kernels for 0%

profile of v18, /device:TPU:0, one launch (start us, length us, event | category | flops | bytes accessed | tf_op | source)
XLA Modules:
  0.0 133.6 jit_solution(14344490270678056278)
XLA Ops:
  7.9 0.9 fusion.127
  8.8 3.1 %collective-permute-start.1 = (bf16[64,1024]{1,0:T(8,128)(2,1)S(1)}, bf16[64,1024]{1,0:T(8,128)(2,1)S(1)}, u32[]{:S(2)}, u32[]{:S(2)}) collective-permute-start(bf16[64,1024]{1,0:T(8,128)(2,1)S(1)} %get-tuple-element.23), channel_id=1, source_target_pairs={{0,4},{2,6},{4,8},{6,10},{8,12},{10,14},{12,0},{14,2},{1,5},{3,7},... | collective-permute-start | bytes 393224 | tf_op jit(solution)/shard_map/ppermute | solution.py:207
  11.9 2.6 %collective-permute-start.2 = (bf16[64,1024]{1,0:T(8,128)(2,1)S(1)}, bf16[64,1024]{1,0:T(8,128)(2,1)S(1)}, u32[]{:S(2)}, u32[]{:S(2)}) collective-permute-start(bf16[64,1024]{1,0:T(8,128)(2,1)S(1)} %get-tuple-element.23), channel_id=1, source_target_pairs={{0,8},{2,10},{4,12},{6,14},{8,0},{10,2},{12,4},{14,6},{1,9},{3,11}... | collective-permute-start | bytes 393224 | tf_op jit(solution)/shard_map/ppermute | solution.py:207
  14.5 1.4 %collective-permute-start.3 = (bf16[64,1024]{1,0:T(8,128)(2,1)S(1)}, bf16[64,1024]{1,0:T(8,128)(2,1)S(1)}, u32[]{:S(2)}, u32[]{:S(2)}) collective-permute-start(bf16[64,1024]{1,0:T(8,128)(2,1)S(1)} %get-tuple-element.23), channel_id=1, source_target_pairs={{0,12},{2,14},{4,0},{6,2},{8,4},{10,6},{12,8},{14,10},{1,13},{3,15... | collective-permute-start | bytes 393224 | tf_op jit(solution)/shard_map/ppermute | solution.py:207
  15.8 1.5 %collective-permute-start = (bf16[32,2048]{1,0:T(8,128)(2,1)}, bf16[32,2048]{1,0:T(8,128)(2,1)}, u32[]{:S(2)}, u32[]{:S(2)}) collective-permute-start(bf16[32,2048]{1,0:T(8,128)(2,1)} %bitcast.203), channel_id=1, source_target_pairs={{0,1},{1,0},{2,3},{3,2},{4,5},{5,4},{6,7},{7,6},{8,9},{9,8},{10,11... | collective-permute-start | bytes 393224 | tf_op jit(solution)/shard_map/ppermute | solution.py:49
  21.3 0.9 constant_dynamic-update-slice_fusion.4
  22.2 0.9 collective-permute-done.2
  23.3 1.8 %collective-permute-done.4 = bf16[4,64,1024]{2,1,0:T(8,128)(2,1)S(1)} collective-permute-done((bf16[4,64,1024]{2,1,0:T(8,128)(2,1)S(1)}, bf16[4,64,1024]{2,1,0:T(8,128)(2,1)S(1)}, u32[]{:S(2)}, u32[]{:S(2)}) %collective-permute-start.4) | collective-permute-done | bytes 524320 | tf_op jit(solution)/shard_map/ppermute | solution.py:209
  27.5 16.7 %all-gather.2.cloned.1.call-done = bf16[2048,512]{1,0:T(8,128)(2,1)} async-done(((bf16[256,512]{1,0:T(8,128)(2,1)}), bf16[2048,512]{1,0:T(8,128)(2,1)}) %all-gather.2.cloned.1.call-update) | async-done | bytes 2097168 | tf_op jit(solution)/shard_map/all_gather | solution.py:279
  44.2 2.3 %fusion.134 = (bf16[64,2048]{1,0:T(8,128)(2,1)S(1)}, f32[64,2048]{1,0:T(8,128)S(1)}) fusion(bf16[2048,512]{1,0:T(8,128)(2,1)} %all-gather.2.cloned.1.call-done, bf16[4,8,8,128]{3,2,1,0:T(8,128)(2,1)S(1)} %fusion.10), kind=kOutput, calls=%fused_computation.221 | convolution fusion | flops 134348800 | bytes 2949120 | tf_op jit(solution)/shard_map/tc,oc->to/dot_general | solution.py:276
  46.6 1.6 %collective-permute-start.5 = (bf16[64,2048]{1,0:T(8,128)(2,1)S(1)}, bf16[64,2048]{1,0:T(8,128)(2,1)S(1)}, u32[]{:S(2)}, u32[]{:S(2)}) collective-permute-start(bf16[64,2048]{1,0:T(8,128)(2,1)S(1)} %get-tuple-element.26), channel_id=1, source_target_pairs={{0,1},{1,0},{2,3},{3,2},{4,5},{5,4},{6,7},{7,6},{8,9},{9,8},{10,11... | collective-permute-start | bytes 786440 | tf_op jit(solution)/shard_map/ppermute | solution.py:49
  49.0 6.1 %collective-permute-done.5 = bf16[64,2048]{1,0:T(8,128)(2,1)S(1)} collective-permute-done((bf16[64,2048]{1,0:T(8,128)(2,1)S(1)}, bf16[64,2048]{1,0:T(8,128)(2,1)S(1)}, u32[]{:S(2)}, u32[]{:S(2)}) %collective-permute-start.5) | collective-permute-done | bytes 262176 | tf_op jit(solution)/shard_map/ppermute | solution.py:49
  55.1 1.2 fusion.50
  59.7 1.2 fusion.64
  61.2 1.6 %fusion.2 = f32[96,352]{1,0:T(8,128)S(1)} fusion(bf16[1,2048,352]{1,2,0:T(8,128)(2,1)S(1)} %copy-done.1, bf16[48,2048]{1,0:T(8,128)(2,1)} %collective-permute-done.6, bf16[48,2048]{1,0:T(8,128)(2,1)} %get-tuple-element.18), kind=kOutput, calls=%fused_computation.3 | convolution fusion | flops 139198464 | bytes 1970176 | tf_op jit(solution)/shard_map/dot_general | solution.py:163
  62.8 2.0 %collective-permute-start.13 = (bf16[2,48,1024]{2,1,0:T(8,128)(2,1)S(1)}, bf16[2,48,1024]{2,1,0:T(8,128)(2,1)S(1)}, u32[]{:S(2)}, u32[]{:S(2)}) collective-permute-start(bf16[2,48,1024]{2,1,0:T(8,128)(2,1)S(1)} %get-tuple-element.15), channel_id=1, source_target_pairs={{0,8},{2,10},{4,12},{6,14},{8,0},{10,2},{12,4},{14,6},{1,9},{3,11}... | collective-permute-start | bytes 589832 | tf_op jit(solution)/shard_map/ppermute | solution.py:147
  64.8 1.7 %collective-permute-start.14 = (bf16[2,48,1024]{2,1,0:T(8,128)(2,1)S(1)}, bf16[2,48,1024]{2,1,0:T(8,128)(2,1)S(1)}, u32[]{:S(2)}, u32[]{:S(2)}) collective-permute-start(bf16[2,48,1024]{2,1,0:T(8,128)(2,1)S(1)} %get-tuple-element.14), channel_id=1, source_target_pairs={{0,12},{2,14},{4,0},{6,2},{8,4},{10,6},{12,8},{14,10},{1,13},{3,15... | collective-permute-start | bytes 589832 | tf_op jit(solution)/shard_map/ppermute | solution.py:147
  66.5 4.1 %collective-permute-done.9 = bf16[2,48,1024]{2,1,0:T(8,128)(2,1)S(1)} collective-permute-done((bf16[2,48,1024]{2,1,0:T(8,128)(2,1)S(1)}, bf16[2,48,1024]{2,1,0:T(8,128)(2,1)S(1)}, u32[]{:S(2)}, u32[]{:S(2)}) %collective-permute-start.9) | collective-permute-done | bytes 196640 | tf_op jit(solution)/shard_map/ppermute | solution.py:147
  70.6 1.5 %collective-permute-start.10 = (bf16[96,1024]{1,0:T(8,128)(2,1)S(1)}, bf16[96,1024]{1,0:T(8,128)(2,1)S(1)}, u32[]{:S(2)}, u32[]{:S(2)}) collective-permute-start(bf16[96,1024]{1,0:T(8,128)(2,1)S(1)} %bitcast.199), channel_id=1, source_target_pairs={{0,1},{1,0},{2,3},{3,2},{4,5},{5,4},{6,7},{7,6},{8,9},{9,8},{10,11... | collective-permute-start | bytes 589832 | tf_op jit(solution)/shard_map/ppermute | solution.py:49
  72.1 1.5 %multiply_convert_fusion.1 = bf16[96,352]{1,0:T(8,128)(2,1)S(1)} fusion(f32[96,352]{1,0:T(8,128)S(1)} %fusion.2, bf16[1,2048,352]{1,2,0:T(8,128)(2,1)S(1)} %copy-done.2, bf16[48,2048]{1,0:T(8,128)(2,1)} %collective-permute-done.6, bf16[48,2048]{1,0:T(8,128)(2,1)S(1)} %copy-done.5), kind=kOutput, calls=%fused_computation.103 | convolution fusion | flops 139401216 | bytes 2037760 | tf_op jit(solution)/shard_map/dot_general | solution.py:164
  73.6 4.6 %collective-permute-done.13 = bf16[2,48,1024]{2,1,0:T(8,128)(2,1)S(1)} collective-permute-done((bf16[2,48,1024]{2,1,0:T(8,128)(2,1)S(1)}, bf16[2,48,1024]{2,1,0:T(8,128)(2,1)S(1)}, u32[]{:S(2)}, u32[]{:S(2)}) %collective-permute-start.13) | collective-permute-done | bytes 196640 | tf_op jit(solution)/shard_map/ppermute | solution.py:147
  78.3 1.6 %collective-permute-start.15 = (bf16[192,1024]{1,0:T(8,128)(2,1)S(1)}, bf16[192,1024]{1,0:T(8,128)(2,1)S(1)}, u32[]{:S(2)}, u32[]{:S(2)}) collective-permute-start(bf16[192,1024]{1,0:T(8,128)(2,1)S(1)} %bitcast.176), channel_id=1, source_target_pairs={{0,1},{1,0},{2,3},{3,2},{4,5},{5,4},{6,7},{7,6},{8,9},{9,8},{10,11... | collective-permute-start | bytes 1179656 | tf_op jit(solution)/shard_map/ppermute | solution.py:49
  82.2 8.1 %collective-permute-done.15 = bf16[192,1024]{1,0:T(8,128)(2,1)S(1)} collective-permute-done((bf16[192,1024]{1,0:T(8,128)(2,1)S(1)}, bf16[192,1024]{1,0:T(8,128)(2,1)S(1)}, u32[]{:S(2)}, u32[]{:S(2)}) %collective-permute-start.15) | collective-permute-done | bytes 393248 | tf_op jit(solution)/shard_map/ppermute | solution.py:49
  92.5 1.6 %collective-permute-start.16 = (bf16[192,1024]{1,0:T(8,128)(2,1)S(1)}, bf16[192,1024]{1,0:T(8,128)(2,1)S(1)}, u32[]{:S(2)}, u32[]{:S(2)}) collective-permute-start(bf16[192,1024]{1,0:T(8,128)(2,1)S(1)} %convolution_convert_fusion.2), channel_id=1, source_target_pairs={{0,1},{1,0},{2,3},{3,2},{4,5},{5,4},{6,7},{7,6},{8,9},{9,8},{10,11... | collective-permute-start | bytes 1179656 | tf_op jit(solution)/shard_map/ppermute | solution.py:49
  95.2 4.2 %collective-permute-start.12 = (bf16[2,48,1024]{2,1,0:T(8,128)(2,1)S(1)}, bf16[2,48,1024]{2,1,0:T(8,128)(2,1)S(1)}, u32[]{:S(2)}, u32[]{:S(2)}) collective-permute-start(bf16[2,48,1024]{2,1,0:T(8,128)(2,1)S(1)} %bitcast.202), channel_id=1, source_target_pairs={{0,12},{2,14},{4,0},{6,2},{8,4},{10,6},{12,8},{14,10},{1,13},{3,15... | collective-permute-start | bytes 589832 | tf_op jit(solution)/shard_map/ppermute | solution.py:185
  99.4 4.6 %collective-permute-done.16 = bf16[192,1024]{1,0:T(8,128)(2,1)S(1)} collective-permute-done((bf16[192,1024]{1,0:T(8,128)(2,1)S(1)}, bf16[192,1024]{1,0:T(8,128)(2,1)S(1)}, u32[]{:S(2)}, u32[]{:S(2)}) %collective-permute-start.16) | collective-permute-done | bytes 393248 | tf_op jit(solution)/shard_map/ppermute | solution.py:49
  104.4 3.8 %collective-permute-start.17 = (bf16[2,48,1024]{2,1,0:T(8,128)(2,1)S(1)}, bf16[2,48,1024]{2,1,0:T(8,128)(2,1)S(1)}, u32[]{:S(2)}, u32[]{:S(2)}) collective-permute-start(bf16[2,48,1024]{2,1,0:T(8,128)(2,1)S(1)} %bitcast.198), channel_id=1, source_target_pairs={{0,8},{2,10},{4,12},{6,14},{8,0},{10,2},{12,4},{14,6},{1,9},{3,11}... | collective-permute-start | bytes 589832 | tf_op jit(solution)/shard_map/ppermute | solution.py:185
  108.3 1.1 collective-permute-start.18
  109.6 8.5 %collective-permute-done.17 = bf16[2,48,1024]{2,1,0:T(8,128)(2,1)S(1)} collective-permute-done((bf16[2,48,1024]{2,1,0:T(8,128)(2,1)S(1)}, bf16[2,48,1024]{2,1,0:T(8,128)(2,1)S(1)}, u32[]{:S(2)}, u32[]{:S(2)}) %collective-permute-start.17) | collective-permute-done | bytes 196640 | tf_op jit(solution)/shard_map/ppermute | solution.py:185
  118.4 1.0 copy-done.4
  121.7 1.6 %collective-permute-start.20 = (bf16[32,1024]{1,0:T(8,128)(2,1)S(1)}, bf16[32,1024]{1,0:T(8,128)(2,1)S(1)}, u32[]{:S(2)}, u32[]{:S(2)}) collective-permute-start(bf16[32,1024]{1,0:T(8,128)(2,1)S(1)} %select_convert_fusion), channel_id=1, source_target_pairs={{0,1},{1,0},{2,3},{3,2},{4,5},{5,4},{6,7},{7,6},{8,9},{9,8},{10,11... | collective-permute-start | bytes 196616 | tf_op jit(solution)/shard_map/ppermute | solution.py:49
  123.3 2.7 %collective-permute-done.20 = bf16[32,1024]{1,0:T(8,128)(2,1)S(1)} collective-permute-done((bf16[32,1024]{1,0:T(8,128)(2,1)S(1)}, bf16[32,1024]{1,0:T(8,128)(2,1)S(1)}, u32[]{:S(2)}, u32[]{:S(2)}) %collective-permute-start.20) | collective-permute-done | bytes 65568 | tf_op jit(solution)/shard_map/ppermute | solution.py:49
  (109 shorter events, 20.6 us)
Async XLA Ops:
  7.2 74.2 %copy-start = (bf16[1,352,2048]{2,1,0:T(8,128)(2,1)S(1)}, bf16[1,352,2048]{2,1,0:T(8,128)(2,1)}, u32[]{:S(2)}) copy-start(bf16[1,352,2048]{2,1,0:T(8,128)(2,1)} %param.20) | copy-start | bytes 4325380
  7.2 37.1 %all-gather.2.cloned.1.call-start = ((), (), s32[]{:S(2)}) async-start(), calls=%async_computation | async-start | bytes 2359296 | tf_op jit(solution)/shard_map/all_gather | solution.py:279
  8.8 13.4 %collective-permute-start.1 = (bf16[64,1024]{1,0:T(8,128)(2,1)S(1)}, bf16[64,1024]{1,0:T(8,128)(2,1)S(1)}, u32[]{:S(2)}, u32[]{:S(2)}) collective-permute-start(bf16[64,1024]{1,0:T(8,128)(2,1)S(1)} %get-tuple-element.23), channel_id=1, source_target_pairs={{0,4},{2,6},{4,8},{6,10},{8,12},{10,14},{12,0},{14,2},{1,5},{3,7},... | collective-permute-start | bytes 393224 | tf_op jit(solution)/shard_map/ppermute | solution.py:207
  11.9 11.2 %collective-permute-start.2 = (bf16[64,1024]{1,0:T(8,128)(2,1)S(1)}, bf16[64,1024]{1,0:T(8,128)(2,1)S(1)}, u32[]{:S(2)}, u32[]{:S(2)}) collective-permute-start(bf16[64,1024]{1,0:T(8,128)(2,1)S(1)} %get-tuple-element.23), channel_id=1, source_target_pairs={{0,8},{2,10},{4,12},{6,14},{8,0},{10,2},{12,4},{14,6},{1,9},{3,11}... | collective-permute-start | bytes 393224 | tf_op jit(solution)/shard_map/ppermute | solution.py:207
  14.5 8.6 %collective-permute-start.3 = (bf16[64,1024]{1,0:T(8,128)(2,1)S(1)}, bf16[64,1024]{1,0:T(8,128)(2,1)S(1)}, u32[]{:S(2)}, u32[]{:S(2)}) collective-permute-start(bf16[64,1024]{1,0:T(8,128)(2,1)S(1)} %get-tuple-element.23), channel_id=1, source_target_pairs={{0,12},{2,14},{4,0},{6,2},{8,4},{10,6},{12,8},{14,10},{1,13},{3,15... | collective-permute-start | bytes 393224 | tf_op jit(solution)/shard_map/ppermute | solution.py:207
  15.8 33.2 %collective-permute-start = (bf16[32,2048]{1,0:T(8,128)(2,1)}, bf16[32,2048]{1,0:T(8,128)(2,1)}, u32[]{:S(2)}, u32[]{:S(2)}) collective-permute-start(bf16[32,2048]{1,0:T(8,128)(2,1)} %bitcast.203), channel_id=1, source_target_pairs={{0,1},{1,0},{2,3},{3,2},{4,5},{5,4},{6,7},{7,6},{8,9},{9,8},{10,11... | collective-permute-start | bytes 393224 | tf_op jit(solution)/shard_map/ppermute | solution.py:49
  23.2 2.0 %collective-permute-start.4 = (bf16[4,64,1024]{2,1,0:T(8,128)(2,1)S(1)}, bf16[4,64,1024]{2,1,0:T(8,128)(2,1)S(1)}, u32[]{:S(2)}, u32[]{:S(2)}) collective-permute-start(bf16[4,64,1024]{2,1,0:T(8,128)(2,1)S(1)} %pad_maximum_fusion.2), channel_id=1, source_target_pairs={{0,2},{2,0},{4,6},{6,4},{8,10},{10,8},{12,14},{14,12},{1,3},{3,1},... | collective-permute-start | bytes 1572872 | tf_op jit(solution)/shard_map/ppermute | solution.py:209
  25.2 1.0 copy-start.3
  27.5 20.8 %copy-start.8 = (f32[1,64,4]{1,2,0:T(4,128)S(1)}, f32[1,64,4]{1,2,0:T(4,128)}, u32[]{:S(2)}) copy-start(f32[1,64,4]{1,2,0:T(4,128)} %param.22) | copy-start | bytes 3076
  27.5 27.6 %copy-start.6 = (bf16[1,32,2048]{2,1,0:T(8,128)(2,1)S(1)}, bf16[1,32,2048]{2,1,0:T(8,128)(2,1)}, u32[]{:S(2)}) copy-start(bf16[1,32,2048]{2,1,0:T(8,128)(2,1)} %param.15) | copy-start | bytes 393220
  46.6 9.8 %copy-start.7 = (f32[2048]{0:T(1024)S(1)}, f32[2048]{0:T(1024)}, u32[]{:S(2)}) copy-start(f32[2048]{0:T(1024)} %param.17) | copy-start | bytes 24580
  46.6 8.5 %collective-permute-start.5 = (bf16[64,2048]{1,0:T(8,128)(2,1)S(1)}, bf16[64,2048]{1,0:T(8,128)(2,1)S(1)}, u32[]{:S(2)}, u32[]{:S(2)}) collective-permute-start(bf16[64,2048]{1,0:T(8,128)(2,1)S(1)} %get-tuple-element.26), channel_id=1, source_target_pairs={{0,1},{1,0},{2,3},{3,2},{4,5},{5,4},{6,7},{7,6},{8,9},{9,8},{10,11... | collective-permute-start | bytes 786440 | tf_op jit(solution)/shard_map/ppermute | solution.py:49
  57.0 4.2 %copy-start.1 = (bf16[1,2048,352]{1,2,0:T(8,128)(2,1)S(1)}, bf16[1,2048,352]{1,2,0:T(8,128)(2,1)}, u32[]{:S(2)}) copy-start(bf16[1,2048,352]{1,2,0:T(8,128)(2,1)} %param.18) | copy-start | bytes 4325380
  57.8 1.9 %collective-permute-start.8 = (bf16[3,48,1024]{2,1,0:T(8,128)(2,1)}, bf16[3,48,1024]{2,1,0:T(8,128)(2,1)}, u32[]{:S(2)}, u32[]{:S(2)}) collective-permute-start(bf16[3,48,1024]{2,1,0:T(8,128)(2,1)} %bitcast.26), channel_id=1, source_target_pairs={{0,2},{2,0},{4,6},{6,4},{8,10},{10,8},{12,14},{14,12},{1,3},{3,1},... | collective-permute-start | bytes 884744 | tf_op jit(solution)/shard_map/ppermute | solution.py:143
  58.6 2.6 %collective-permute-start.6 = (bf16[48,2048]{1,0:T(8,128)(2,1)}, bf16[48,2048]{1,0:T(8,128)(2,1)}, u32[]{:S(2)}, u32[]{:S(2)}) collective-permute-start(bf16[48,2048]{1,0:T(8,128)(2,1)} %get-tuple-element.19), channel_id=1, source_target_pairs={{0,2},{2,0},{4,6},{6,4},{8,10},{10,8},{12,14},{14,12},{1,3},{3,1},... | collective-permute-start | bytes 589832 | tf_op jit(solution)/shard_map/ppermute | solution.py:141
  59.7 12.4 %copy-start.2 = (bf16[1,2048,352]{1,2,0:T(8,128)(2,1)S(1)}, bf16[1,2048,352]{1,2,0:T(8,128)(2,1)}, u32[]{:S(2)}) copy-start(bf16[1,2048,352]{1,2,0:T(8,128)(2,1)} %param.19) | copy-start | bytes 4325380
  59.7 12.4 %copy-start.5 = (bf16[48,2048]{1,0:T(8,128)(2,1)S(1)}, bf16[48,2048]{1,0:T(8,128)(2,1)}, u32[]{:S(2)}) copy-start(bf16[48,2048]{1,0:T(8,128)(2,1)} %get-tuple-element.18) | copy-start | bytes 589828
  60.9 9.7 %collective-permute-start.9 = (bf16[2,48,1024]{2,1,0:T(8,128)(2,1)S(1)}, bf16[2,48,1024]{2,1,0:T(8,128)(2,1)S(1)}, u32[]{:S(2)}, u32[]{:S(2)}) collective-permute-start(bf16[2,48,1024]{2,1,0:T(8,128)(2,1)S(1)} %get-tuple-element.13), channel_id=1, source_target_pairs={{0,4},{2,6},{4,8},{6,10},{8,12},{10,14},{12,0},{14,2},{1,5},{3,7},... | collective-permute-start | bytes 589832 | tf_op jit(solution)/shard_map/ppermute | solution.py:147
  62.8 15.4 %collective-permute-start.13 = (bf16[2,48,1024]{2,1,0:T(8,128)(2,1)S(1)}, bf16[2,48,1024]{2,1,0:T(8,128)(2,1)S(1)}, u32[]{:S(2)}, u32[]{:S(2)}) collective-permute-start(bf16[2,48,1024]{2,1,0:T(8,128)(2,1)S(1)} %get-tuple-element.15), channel_id=1, source_target_pairs={{0,8},{2,10},{4,12},{6,14},{8,0},{10,2},{12,4},{14,6},{1,9},{3,11}... | collective-permute-start | bytes 589832 | tf_op jit(solution)/shard_map/ppermute | solution.py:147
  64.8 13.4 %collective-permute-start.14 = (bf16[2,48,1024]{2,1,0:T(8,128)(2,1)S(1)}, bf16[2,48,1024]{2,1,0:T(8,128)(2,1)S(1)}, u32[]{:S(2)}, u32[]{:S(2)}) collective-permute-start(bf16[2,48,1024]{2,1,0:T(8,128)(2,1)S(1)} %get-tuple-element.14), channel_id=1, source_target_pairs={{0,12},{2,14},{4,0},{6,2},{8,4},{10,6},{12,8},{14,10},{1,13},{3,15... | collective-permute-start | bytes 589832 | tf_op jit(solution)/shard_map/ppermute | solution.py:147
  70.6 9.2 %collective-permute-start.10 = (bf16[96,1024]{1,0:T(8,128)(2,1)S(1)}, bf16[96,1024]{1,0:T(8,128)(2,1)S(1)}, u32[]{:S(2)}, u32[]{:S(2)}) collective-permute-start(bf16[96,1024]{1,0:T(8,128)(2,1)S(1)} %bitcast.199), channel_id=1, source_target_pairs={{0,1},{1,0},{2,3},{3,2},{4,5},{5,4},{6,7},{7,6},{8,9},{9,8},{10,11... | collective-permute-start | bytes 589832 | tf_op jit(solution)/shard_map/ppermute | solution.py:49
  78.3 12.1 %collective-permute-start.15 = (bf16[192,1024]{1,0:T(8,128)(2,1)S(1)}, bf16[192,1024]{1,0:T(8,128)(2,1)S(1)}, u32[]{:S(2)}, u32[]{:S(2)}) collective-permute-start(bf16[192,1024]{1,0:T(8,128)(2,1)S(1)} %bitcast.176), channel_id=1, source_target_pairs={{0,1},{1,0},{2,3},{3,2},{4,5},{5,4},{6,7},{7,6},{8,9},{9,8},{10,11... | collective-permute-start | bytes 1179656 | tf_op jit(solution)/shard_map/ppermute | solution.py:49
  81.6 13.3 %collective-permute-start.11 = (bf16[96,1024]{1,0:T(8,128)(2,1)S(1)}, bf16[96,1024]{1,0:T(8,128)(2,1)S(1)}, u32[]{:S(2)}, u32[]{:S(2)}) collective-permute-start(bf16[96,1024]{1,0:T(8,128)(2,1)S(1)} %convolution_convert_fusion.3), channel_id=1, source_target_pairs={{0,1},{1,0},{2,3},{3,2},{4,5},{5,4},{6,7},{7,6},{8,9},{9,8},{10,11... | collective-permute-start | bytes 589832 | tf_op jit(solution)/shard_map/ppermute | solution.py:49
  92.5 11.5 %collective-permute-start.16 = (bf16[192,1024]{1,0:T(8,128)(2,1)S(1)}, bf16[192,1024]{1,0:T(8,128)(2,1)S(1)}, u32[]{:S(2)}, u32[]{:S(2)}) collective-permute-start(bf16[192,1024]{1,0:T(8,128)(2,1)S(1)} %convolution_convert_fusion.2), channel_id=1, source_target_pairs={{0,1},{1,0},{2,3},{3,2},{4,5},{5,4},{6,7},{7,6},{8,9},{9,8},{10,11... | collective-permute-start | bytes 1179656 | tf_op jit(solution)/shard_map/ppermute | solution.py:49
  94.4 15.0 %collective-permute-start.7 = (bf16[96,1024]{1,0:T(8,128)(2,1)S(1)}, bf16[96,1024]{1,0:T(8,128)(2,1)S(1)}, u32[]{:S(2)}, u32[]{:S(2)}) collective-permute-start(bf16[96,1024]{1,0:T(8,128)(2,1)S(1)} %convolution_convert_fusion.4), channel_id=1, source_target_pairs={{0,1},{1,0},{2,3},{3,2},{4,5},{5,4},{6,7},{7,6},{8,9},{9,8},{10,11... | collective-permute-start | bytes 589832 | tf_op jit(solution)/shard_map/ppermute | solution.py:49
  95.2 14.4 %collective-permute-start.12 = (bf16[2,48,1024]{2,1,0:T(8,128)(2,1)S(1)}, bf16[2,48,1024]{2,1,0:T(8,128)(2,1)S(1)}, u32[]{:S(2)}, u32[]{:S(2)}) collective-permute-start(bf16[2,48,1024]{2,1,0:T(8,128)(2,1)S(1)} %bitcast.202), channel_id=1, source_target_pairs={{0,12},{2,14},{4,0},{6,2},{8,4},{10,6},{12,8},{14,10},{1,13},{3,15... | collective-permute-start | bytes 589832 | tf_op jit(solution)/shard_map/ppermute | solution.py:185
  104.4 13.7 %collective-permute-start.17 = (bf16[2,48,1024]{2,1,0:T(8,128)(2,1)S(1)}, bf16[2,48,1024]{2,1,0:T(8,128)(2,1)S(1)}, u32[]{:S(2)}, u32[]{:S(2)}) collective-permute-start(bf16[2,48,1024]{2,1,0:T(8,128)(2,1)S(1)} %bitcast.198), channel_id=1, source_target_pairs={{0,8},{2,10},{4,12},{6,14},{8,0},{10,2},{12,4},{14,6},{1,9},{3,11}... | collective-permute-start | bytes 589832 | tf_op jit(solution)/shard_map/ppermute | solution.py:185
  108.3 9.9 %collective-permute-start.18 = (bf16[2,48,1024]{2,1,0:T(8,128)(2,1)S(1)}, bf16[2,48,1024]{2,1,0:T(8,128)(2,1)S(1)}, u32[]{:S(2)}, u32[]{:S(2)}) collective-permute-start(bf16[2,48,1024]{2,1,0:T(8,128)(2,1)S(1)} %bitcast.197), channel_id=1, source_target_pairs={{0,4},{2,6},{4,8},{6,10},{8,12},{10,14},{12,0},{14,2},{1,5},{3,7},... | collective-permute-start | bytes 589832 | tf_op jit(solution)/shard_map/ppermute | solution.py:185
  118.1 1.2 copy-start.4
  118.3 2.8 %collective-permute-start.19 = (bf16[4,48,1024]{2,1,0:T(8,128)(2,1)S(1)}, bf16[4,48,1024]{2,1,0:T(8,128)(2,1)S(1)}, u32[]{:S(2)}, u32[]{:S(2)}) collective-permute-start(bf16[4,48,1024]{2,1,0:T(8,128)(2,1)S(1)} %get-tuple-element.12), channel_id=1, source_target_pairs={{0,2},{2,0},{4,6},{6,4},{8,10},{10,8},{12,14},{14,12},{1,3},{3,1},... | collective-permute-start | bytes 1179656 | tf_op jit(solution)/shard_map/ppermute | solution.py:187
  121.7 4.3 %collective-permute-start.20 = (bf16[32,1024]{1,0:T(8,128)(2,1)S(1)}, bf16[32,1024]{1,0:T(8,128)(2,1)S(1)}, u32[]{:S(2)}, u32[]{:S(2)}) collective-permute-start(bf16[32,1024]{1,0:T(8,128)(2,1)S(1)} %select_convert_fusion), channel_id=1, source_target_pairs={{0,1},{1,0},{2,3},{3,2},{4,5},{5,4},{6,7},{7,6},{8,9},{9,8},{10,11... | collective-permute-start | bytes 196616 | tf_op jit(solution)/shard_map/ppermute | solution.py:49
Sparse Core Ops, SparseCore 0:
  9.6 34.5 all-gather.1

commit v19 on v16

--- a/solution.py
+++ b/solution.py
@@ -158,6 +158,7 @@
     else:
         groups = [[0], list(range(1, n_chip // 2)), list(range(n_chip // 2, n_chip))]
     returned = [None] * n_chip
+    returned_partner = [None] * n_chip
     for shifts in groups:
         if shifts == [0]:
             gate_act = jnp.dot(near_in, gate_matrix, preferred_element_type=jnp.float32)
@@ -179,13 +180,15 @@
         summed = summed.reshape(len(shifts), 2, capacity, half_d)
         for idx, shift in enumerate(shifts):
             if shift == 0:
-                returned[shift] = summed[idx]
+                returned[shift] = summed[idx][0]
+                returned_partner[shift] = lax.ppermute(summed[idx][1], "ctx", perm=core_swap)
             else:
                 perm = [(i, ((i // 2 - shift) % n_chip) * 2 + i % 2) for i in range(n_ctx)]
-                returned[shift] = lax.ppermute(summed[idx], "ctx", perm=perm)
-    back = jnp.stack(returned)
-    partner_res = lax.ppermute(back[:, 1], "ctx", perm=core_swap)
-    served = jnp.stack([back[:, 0], partner_res]).reshape(n_ctx * capacity, half_d)
+                returned[shift] = lax.ppermute(summed[idx][0], "ctx", perm=perm)
+                perm = [(i, ((i // 2 - shift) % n_chip) * 2 + 1 - i % 2) for i in range(n_ctx)]
+                returned_partner[shift] = lax.ppermute(summed[idx][1], "ctx", perm=perm)
+    served = jnp.stack([jnp.stack(returned), jnp.stack(returned_partner)])
+    served = served.reshape(n_ctx * capacity, half_d)
     moe_half = jnp.dot(
         combine,
         served.astype(jnp.float32),

time: 130 us -> 129 us (level)
  waiting for transfers between devices: 54 us -> 59 us
  local copies, waits for them, and re-layouts: 6.87 us -> 4.44 us
  matrix products: 15.7 us -> 13.6 us
    ppermute x4 -> x7, starting transfers between devices: 6.18 us -> 11.1 us  [the longest x3 6.63 us: moe_column_halves(): returned[shift] = lax.ppermute(summed[idx][0], 'ctx', perm=perm)]
    ppermute x10, starting transfers between devices: 13.8 us -> 9.21 us  [exp_swap(): return lax.ppermute(x, 'exp', perm=[(0, 1), (1, 0)])]
    ppermute x10, waiting for transfers between devices: 15.2 us -> 19.5 us  [exp_swap(): return lax.ppermute(x, 'exp', perm=[(0, 1), (1, 0)])]
    unnamed x22 -> x20, local copies, waits for them, and re-layouts: 2.69 us -> 1.74 us
    ppermute x4 -> x7, waiting for transfers between devices: 9.05 us -> 8.48 us  [the longest x3 8.23 us: moe_column_halves(): returned_partner[shift] = lax.ppermute(summed[idx][1], 'ctx', perm=perm)]
  transfers between devices with their start and end apart: 24 -> 27, of which waited for: 13 -> 15; matrix products, arithmetic and copies ran while one was open for 17% -> 15% of each run, Pallas kernels for 0% -> 0%
where the time goes in v19:
time: 129 us
  waiting for transfers between devices  59 us (46%)
  starting transfers between devices  32.1 us (25%)
  between operations  15.3 us (12%)
  matrix products  13.6 us (11%)
  other arithmetic  4.67 us (4%)
  local copies, waits for them, and re-layouts  4.44 us (3%)
    ppermute x10, waiting for transfers between devices, exp_swap(): return lax.ppermute(x, 'exp', perm=[(0, 1), (1, 0)])  19.5 us
    all_gather x1, waiting for transfers between devices, local(): lax.all_gather(out_weight, 'ctx', axis=0, tiled=True)  16.7 us
    ppermute x3, waiting for transfers between devices, moe_column_halves(): arrived.append(lax.ppermute(far_pairs[shift - 1], 'ctx', perm=perm))  10.4 us
    ppermute x10, starting transfers between devices, exp_swap(): return lax.ppermute(x, 'exp', perm=[(0, 1), (1, 0)])  9.21 us
    ppermute x3, waiting for transfers between devices, moe_column_halves(): returned_partner[shift] = lax.ppermute(summed[idx][1], 'ctx', perm=perm)  8.23 us
    ppermute x3, starting transfers between devices, ctx_gather_blocks(): stack.append(lax.ppermute(rows, 'ctx', perm=perm))  7.03 us
    ppermute x3, starting transfers between devices, moe_column_halves(): returned[shift] = lax.ppermute(summed[idx][0], 'ctx', perm=perm)  6.63 us
    ppermute x3, starting transfers between devices, moe_column_halves(): returned_partner[shift] = lax.ppermute(summed[idx][1], 'ctx', perm=perm)  4.39 us
  transfers between devices with their start and end apart: 27, of which 15 were waited for; matrix products, arithmetic and copies ran while one was open for 15% of the time, Pallas kernels for 0%

profile of v19, /device:TPU:0, one launch (start us, length us, event | category | flops | bytes accessed | tf_op | source)
XLA Modules:
  0.0 129.2 jit_solution(5610192422913274780)
XLA Ops:
  7.9 0.9 fusion.152
  8.8 3.1 %collective-permute-start.1 = (bf16[64,1024]{1,0:T(8,128)(2,1)S(1)}, bf16[64,1024]{1,0:T(8,128)(2,1)S(1)}, u32[]{:S(2)}, u32[]{:S(2)}) collective-permute-start(bf16[64,1024]{1,0:T(8,128)(2,1)S(1)} %get-tuple-element.27), channel_id=1, source_target_pairs={{0,4},{2,6},{4,8},{6,10},{8,12},{10,14},{12,0},{14,2},{1,5},{3,7},... | collective-permute-start | bytes 393224 | tf_op jit(solution)/shard_map/ppermute | solution.py:210
  11.9 2.6 %collective-permute-start.2 = (bf16[64,1024]{1,0:T(8,128)(2,1)S(1)}, bf16[64,1024]{1,0:T(8,128)(2,1)S(1)}, u32[]{:S(2)}, u32[]{:S(2)}) collective-permute-start(bf16[64,1024]{1,0:T(8,128)(2,1)S(1)} %get-tuple-element.27), channel_id=1, source_target_pairs={{0,8},{2,10},{4,12},{6,14},{8,0},{10,2},{12,4},{14,6},{1,9},{3,11}... | collective-permute-start | bytes 393224 | tf_op jit(solution)/shard_map/ppermute | solution.py:210
  14.5 1.4 %collective-permute-start.3 = (bf16[64,1024]{1,0:T(8,128)(2,1)S(1)}, bf16[64,1024]{1,0:T(8,128)(2,1)S(1)}, u32[]{:S(2)}, u32[]{:S(2)}) collective-permute-start(bf16[64,1024]{1,0:T(8,128)(2,1)S(1)} %get-tuple-element.27), channel_id=1, source_target_pairs={{0,12},{2,14},{4,0},{6,2},{8,4},{10,6},{12,8},{14,10},{1,13},{3,15... | collective-permute-start | bytes 393224 | tf_op jit(solution)/shard_map/ppermute | solution.py:210
  15.8 1.5 %collective-permute-start = (bf16[32,2048]{1,0:T(8,128)(2,1)}, bf16[32,2048]{1,0:T(8,128)(2,1)S(1)}, u32[]{:S(2)}, u32[]{:S(2)}) collective-permute-start(bf16[32,2048]{1,0:T(8,128)(2,1)} %bitcast.222), channel_id=1, source_target_pairs={{0,1},{1,0},{2,3},{3,2},{4,5},{5,4},{6,7},{7,6},{8,9},{9,8},{10,11... | collective-permute-start | bytes 393224 | tf_op jit(solution)/shard_map/ppermute | solution.py:49
  21.3 0.9 constant_dynamic-update-slice_fusion.4
  22.2 0.9 collective-permute-done.2
  23.3 1.8 %collective-permute-done.4 = bf16[4,64,1024]{2,1,0:T(8,128)(2,1)S(1)} collective-permute-done((bf16[4,64,1024]{2,1,0:T(8,128)(2,1)S(1)}, bf16[4,64,1024]{2,1,0:T(8,128)(2,1)S(1)}, u32[]{:S(2)}, u32[]{:S(2)}) %collective-permute-start.4) | collective-permute-done | bytes 524320 | tf_op jit(solution)/shard_map/ppermute | solution.py:212
  25.3 0.9 copy-done.3
  27.6 16.7 %all-gather.2.cloned.1.call-done = bf16[2048,512]{1,0:T(8,128)(2,1)} async-done(((bf16[256,512]{1,0:T(8,128)(2,1)}), bf16[2048,512]{1,0:T(8,128)(2,1)}) %all-gather.2.cloned.1.call-update) | async-done | bytes 2097168 | tf_op jit(solution)/shard_map/all_gather | solution.py:282
  44.2 2.3 %fusion.161 = (bf16[64,2048]{1,0:T(8,128)(2,1)S(1)}, f32[64,2048]{1,0:T(8,128)S(1)}) fusion(bf16[2048,512]{1,0:T(8,128)(2,1)} %all-gather.2.cloned.1.call-done, bf16[4,8,8,128]{3,2,1,0:T(8,128)(2,1)S(1)} %fusion.8), kind=kOutput, calls=%fused_computation.247 | convolution fusion | flops 134348800 | bytes 2949120 | tf_op jit(solution)/shard_map/tc,oc->to/dot_general | solution.py:279
  46.6 1.6 %collective-permute-start.5 = (bf16[64,2048]{1,0:T(8,128)(2,1)S(1)}, bf16[64,2048]{1,0:T(8,128)(2,1)S(1)}, u32[]{:S(2)}, u32[]{:S(2)}) collective-permute-start(bf16[64,2048]{1,0:T(8,128)(2,1)S(1)} %get-tuple-element.30), channel_id=1, source_target_pairs={{0,1},{1,0},{2,3},{3,2},{4,5},{5,4},{6,7},{7,6},{8,9},{9,8},{10,11... | collective-permute-start | bytes 786440 | tf_op jit(solution)/shard_map/ppermute | solution.py:49
  49.0 6.1 %collective-permute-done.5 = bf16[64,2048]{1,0:T(8,128)(2,1)S(1)} collective-permute-done((bf16[64,2048]{1,0:T(8,128)(2,1)S(1)}, bf16[64,2048]{1,0:T(8,128)(2,1)S(1)}, u32[]{:S(2)}, u32[]{:S(2)}) %collective-permute-start.5) | collective-permute-done | bytes 262176 | tf_op jit(solution)/shard_map/ppermute | solution.py:49
  58.8 1.6 %collective-permute-start.7 = (bf16[96,1024]{1,0:T(8,128)(2,1)S(1)}, bf16[96,1024]{1,0:T(8,128)(2,1)S(1)}, u32[]{:S(2)}, u32[]{:S(2)}) collective-permute-start(bf16[96,1024]{1,0:T(8,128)(2,1)S(1)} %convolution_convert_fusion.5), channel_id=1, source_target_pairs={{0,1},{1,0},{2,3},{3,2},{4,5},{5,4},{6,7},{7,6},{8,9},{9,8},{10,11... | collective-permute-start | bytes 589832 | tf_op jit(solution)/shard_map/ppermute | solution.py:49
  61.0 0.9 fusion.10
  61.9 0.9 fusion.9
  62.7 1.4 %collective-permute-start.13 = (bf16[2,48,1024]{2,1,0:T(8,128)(2,1)S(1)}, bf16[2,48,1024]{2,1,0:T(8,128)(2,1)S(1)}, u32[]{:S(2)}, u32[]{:S(2)}) collective-permute-start(bf16[2,48,1024]{2,1,0:T(8,128)(2,1)S(1)} %get-tuple-element.13), channel_id=1, source_target_pairs={{0,8},{2,10},{4,12},{6,14},{8,0},{10,2},{12,4},{14,6},{1,9},{3,11}... | collective-permute-start | bytes 589832 | tf_op jit(solution)/shard_map/ppermute | solution.py:147
  64.1 2.2 %collective-permute-start.17 = (bf16[2,48,1024]{2,1,0:T(8,128)(2,1)S(1)}, bf16[2,48,1024]{2,1,0:T(8,128)(2,1)S(1)}, u32[]{:S(2)}, u32[]{:S(2)}) collective-permute-start(bf16[2,48,1024]{2,1,0:T(8,128)(2,1)S(1)} %get-tuple-element.12), channel_id=1, source_target_pairs={{0,12},{2,14},{4,0},{6,2},{8,4},{10,6},{12,8},{14,10},{1,13},{3,15... | collective-permute-start | bytes 589832 | tf_op jit(solution)/shard_map/ppermute | solution.py:147
  66.3 3.9 %collective-permute-done.9 = bf16[2,48,1024]{2,1,0:T(8,128)(2,1)S(1)} collective-permute-done((bf16[2,48,1024]{2,1,0:T(8,128)(2,1)S(1)}, bf16[2,48,1024]{2,1,0:T(8,128)(2,1)S(1)}, u32[]{:S(2)}, u32[]{:S(2)}) %collective-permute-start.9) | collective-permute-done | bytes 196640 | tf_op jit(solution)/shard_map/ppermute | solution.py:147
  71.0 6.5 %collective-permute-done.13 = bf16[2,48,1024]{2,1,0:T(8,128)(2,1)S(1)} collective-permute-done((bf16[2,48,1024]{2,1,0:T(8,128)(2,1)S(1)}, bf16[2,48,1024]{2,1,0:T(8,128)(2,1)S(1)}, u32[]{:S(2)}, u32[]{:S(2)}) %collective-permute-start.13) | collective-permute-done | bytes 196640 | tf_op jit(solution)/shard_map/ppermute | solution.py:147
  78.0 1.5 %collective-permute-start.18 = (bf16[96,1024]{1,0:T(8,128)(2,1)S(1)}, bf16[96,1024]{1,0:T(8,128)(2,1)S(1)}, u32[]{:S(2)}, u32[]{:S(2)}) collective-permute-start(bf16[96,1024]{1,0:T(8,128)(2,1)S(1)} %bitcast.213), channel_id=1, source_target_pairs={{0,1},{1,0},{2,3},{3,2},{4,5},{5,4},{6,7},{7,6},{8,9},{9,8},{10,11... | collective-permute-start | bytes 589832 | tf_op jit(solution)/shard_map/ppermute | solution.py:49
  81.9 3.4 %collective-permute-done.14 = bf16[96,1024]{1,0:T(8,128)(2,1)S(1)} collective-permute-done((bf16[96,1024]{1,0:T(8,128)(2,1)S(1)}, bf16[96,1024]{1,0:T(8,128)(2,1)S(1)}, u32[]{:S(2)}, u32[]{:S(2)}) %collective-permute-start.14) | collective-permute-done | bytes 196640 | tf_op jit(solution)/shard_map/ppermute | solution.py:49
  87.6 1.9 %collective-permute-done.18 = bf16[96,1024]{1,0:T(8,128)(2,1)S(1)} collective-permute-done((bf16[96,1024]{1,0:T(8,128)(2,1)S(1)}, bf16[96,1024]{1,0:T(8,128)(2,1)S(1)}, u32[]{:S(2)}, u32[]{:S(2)}) %collective-permute-start.18) | collective-permute-done | bytes 196640 | tf_op jit(solution)/shard_map/ppermute | solution.py:49
  91.8 1.9 %collective-permute-done.11 = bf16[96,1024]{1,0:T(8,128)(2,1)S(1)} collective-permute-done((bf16[96,1024]{1,0:T(8,128)(2,1)S(1)}, bf16[96,1024]{1,0:T(8,128)(2,1)S(1)}, u32[]{:S(2)}, u32[]{:S(2)}) %collective-permute-start.11) | collective-permute-done | bytes 196640 | tf_op jit(solution)/shard_map/ppermute | solution.py:49
  94.0 4.4 %collective-permute-start.12 = (bf16[48,1024]{1,0:T(8,128)(2,1)S(1)}, bf16[48,1024]{1,0:T(8,128)(2,1)S(1)}, u32[]{:S(2)}, u32[]{:S(2)}) collective-permute-start(bf16[48,1024]{1,0:T(8,128)(2,1)S(1)} %get-tuple-element.20), channel_id=1, source_target_pairs={{0,12},{2,14},{4,0},{6,2},{8,4},{10,6},{12,8},{14,10},{1,13},{3,15... | collective-permute-start | bytes 294920 | tf_op jit(solution)/shard_map/ppermute | solution.py:187
  98.8 2.3 %collective-permute-done.19 = bf16[96,1024]{1,0:T(8,128)(2,1)S(1)} collective-permute-done((bf16[96,1024]{1,0:T(8,128)(2,1)S(1)}, bf16[96,1024]{1,0:T(8,128)(2,1)S(1)}, u32[]{:S(2)}, u32[]{:S(2)}) %collective-permute-start.19) | collective-permute-done | bytes 196640 | tf_op jit(solution)/shard_map/ppermute | solution.py:49
  101.4 2.2 %collective-permute-start.20 = (bf16[48,1024]{1,0:T(8,128)(2,1)S(1)}, bf16[48,1024]{1,0:T(8,128)(2,1)S(1)}, u32[]{:S(2)}, u32[]{:S(2)}) collective-permute-start(bf16[48,1024]{1,0:T(8,128)(2,1)S(1)} %get-tuple-element.24), channel_id=1, source_target_pairs={{0,4},{2,6},{4,8},{6,10},{8,12},{10,14},{12,0},{14,2},{1,5},{3,7},... | collective-permute-start | bytes 294920 | tf_op jit(solution)/shard_map/ppermute | solution.py:187
  103.7 2.1 %collective-permute-start.22 = (bf16[48,1024]{1,0:T(8,128)(2,1)S(1)}, bf16[48,1024]{1,0:T(8,128)(2,1)S(1)}, u32[]{:S(2)}, u32[]{:S(2)}) collective-permute-start(bf16[48,1024]{1,0:T(8,128)(2,1)S(1)} %get-tuple-element.21), channel_id=1, source_target_pairs={{0,14},{2,12},{4,2},{6,0},{8,6},{10,4},{12,10},{14,8},{1,15},{3,13... | collective-permute-start | bytes 294920 | tf_op jit(solution)/shard_map/ppermute | solution.py:189
  106.4 1.7 %collective-permute-start.24 = (bf16[48,1024]{1,0:T(8,128)(2,1)S(1)}, bf16[48,1024]{1,0:T(8,128)(2,1)S(1)}, u32[]{:S(2)}, u32[]{:S(2)}) collective-permute-start(bf16[48,1024]{1,0:T(8,128)(2,1)S(1)} %get-tuple-element.25), channel_id=1, source_target_pairs={{0,6},{2,4},{4,10},{6,8},{8,14},{10,12},{12,2},{14,0},{1,7},{3,5},... | collective-permute-start | bytes 294920 | tf_op jit(solution)/shard_map/ppermute | solution.py:189
  108.4 1.0 collective-permute-done.22
  109.4 7.2 %collective-permute-done.23 = bf16[48,1024]{1,0:T(8,128)(2,1)S(1)} collective-permute-done((bf16[48,1024]{1,0:T(8,128)(2,1)S(1)}, bf16[48,1024]{1,0:T(8,128)(2,1)S(1)}, u32[]{:S(2)}, u32[]{:S(2)}) %collective-permute-start.23) | collective-permute-done | bytes 98336 | tf_op jit(solution)/shard_map/ppermute | solution.py:189
  117.6 4.0 %collective-permute-done.25 = bf16[32,1024]{1,0:T(8,128)(2,1)S(1)} collective-permute-done((bf16[32,1024]{1,0:T(8,128)(2,1)S(1)}, bf16[32,1024]{1,0:T(8,128)(2,1)S(1)}, u32[]{:S(2)}, u32[]{:S(2)}) %collective-permute-start.25) | collective-permute-done | bytes 65568 | tf_op jit(solution)/shard_map/ppermute | solution.py:49
  (125 shorter events, 22.4 us)
Async XLA Ops:
  7.2 51.3 %copy-start = (bf16[1,352,2048]{2,1,0:T(8,128)(2,1)S(1)}, bf16[1,352,2048]{2,1,0:T(8,128)(2,1)}, u32[]{:S(2)}) copy-start(bf16[1,352,2048]{2,1,0:T(8,128)(2,1)} %param.20) | copy-start | bytes 4325380
  7.2 37.1 %all-gather.2.cloned.1.call-start = ((), (), s32[]{:S(2)}) async-start(), calls=%async_computation | async-start | bytes 2359296 | tf_op jit(solution)/shard_map/all_gather | solution.py:282
  8.8 13.4 %collective-permute-start.1 = (bf16[64,1024]{1,0:T(8,128)(2,1)S(1)}, bf16[64,1024]{1,0:T(8,128)(2,1)S(1)}, u32[]{:S(2)}, u32[]{:S(2)}) collective-permute-start(bf16[64,1024]{1,0:T(8,128)(2,1)S(1)} %get-tuple-element.27), channel_id=1, source_target_pairs={{0,4},{2,6},{4,8},{6,10},{8,12},{10,14},{12,0},{14,2},{1,5},{3,7},... | collective-permute-start | bytes 393224 | tf_op jit(solution)/shard_map/ppermute | solution.py:210
  11.9 11.2 %collective-permute-start.2 = (bf16[64,1024]{1,0:T(8,128)(2,1)S(1)}, bf16[64,1024]{1,0:T(8,128)(2,1)S(1)}, u32[]{:S(2)}, u32[]{:S(2)}) collective-permute-start(bf16[64,1024]{1,0:T(8,128)(2,1)S(1)} %get-tuple-element.27), channel_id=1, source_target_pairs={{0,8},{2,10},{4,12},{6,14},{8,0},{10,2},{12,4},{14,6},{1,9},{3,11}... | collective-permute-start | bytes 393224 | tf_op jit(solution)/shard_map/ppermute | solution.py:210
  14.5 8.6 %collective-permute-start.3 = (bf16[64,1024]{1,0:T(8,128)(2,1)S(1)}, bf16[64,1024]{1,0:T(8,128)(2,1)S(1)}, u32[]{:S(2)}, u32[]{:S(2)}) collective-permute-start(bf16[64,1024]{1,0:T(8,128)(2,1)S(1)} %get-tuple-element.27), channel_id=1, source_target_pairs={{0,12},{2,14},{4,0},{6,2},{8,4},{10,6},{12,8},{14,10},{1,13},{3,15... | collective-permute-start | bytes 393224 | tf_op jit(solution)/shard_map/ppermute | solution.py:210
  15.8 33.2 %collective-permute-start = (bf16[32,2048]{1,0:T(8,128)(2,1)}, bf16[32,2048]{1,0:T(8,128)(2,1)S(1)}, u32[]{:S(2)}, u32[]{:S(2)}) collective-permute-start(bf16[32,2048]{1,0:T(8,128)(2,1)} %bitcast.222), channel_id=1, source_target_pairs={{0,1},{1,0},{2,3},{3,2},{4,5},{5,4},{6,7},{7,6},{8,9},{9,8},{10,11... | collective-permute-start | bytes 393224 | tf_op jit(solution)/shard_map/ppermute | solution.py:49
  23.2 2.0 %collective-permute-start.4 = (bf16[4,64,1024]{2,1,0:T(8,128)(2,1)S(1)}, bf16[4,64,1024]{2,1,0:T(8,128)(2,1)S(1)}, u32[]{:S(2)}, u32[]{:S(2)}) collective-permute-start(bf16[4,64,1024]{2,1,0:T(8,128)(2,1)S(1)} %pad_maximum_fusion.1), channel_id=1, source_target_pairs={{0,2},{2,0},{4,6},{6,4},{8,10},{10,8},{12,14},{14,12},{1,3},{3,1},... | collective-permute-start | bytes 1572872 | tf_op jit(solution)/shard_map/ppermute | solution.py:212
  27.5 20.8 %copy-start.7 = (f32[1,64,4]{1,2,0:T(4,128)S(1)}, f32[1,64,4]{1,2,0:T(4,128)}, u32[]{:S(2)}) copy-start(f32[1,64,4]{1,2,0:T(4,128)} %param.22) | copy-start | bytes 3076
  27.6 27.5 %copy-start.5 = (bf16[1,32,2048]{2,1,0:T(8,128)(2,1)S(1)}, bf16[1,32,2048]{2,1,0:T(8,128)(2,1)}, u32[]{:S(2)}) copy-start(bf16[1,32,2048]{2,1,0:T(8,128)(2,1)} %param.15) | copy-start | bytes 393220
  46.6 8.8 %copy-start.6 = (f32[2048]{0:T(1024)S(1)}, f32[2048]{0:T(1024)}, u32[]{:S(2)}) copy-start(f32[2048]{0:T(1024)} %param.17) | copy-start | bytes 24580
  46.6 8.5 %collective-permute-start.5 = (bf16[64,2048]{1,0:T(8,128)(2,1)S(1)}, bf16[64,2048]{1,0:T(8,128)(2,1)S(1)}, u32[]{:S(2)}, u32[]{:S(2)}) collective-permute-start(bf16[64,2048]{1,0:T(8,128)(2,1)S(1)} %get-tuple-element.30), channel_id=1, source_target_pairs={{0,1},{1,0},{2,3},{3,2},{4,5},{5,4},{6,7},{7,6},{8,9},{9,8},{10,11... | collective-permute-start | bytes 786440 | tf_op jit(solution)/shard_map/ppermute | solution.py:49
  55.8 1.5 %collective-permute-start.6 = (bf16[48,2048]{1,0:T(8,128)(2,1)S(1)}, bf16[48,2048]{1,0:T(8,128)(2,1)S(1)}, u32[]{:S(2)}, u32[]{:S(2)}) collective-permute-start(bf16[48,2048]{1,0:T(8,128)(2,1)S(1)} %get-tuple-element.17), channel_id=1, source_target_pairs={{0,2},{2,0},{4,6},{6,4},{8,10},{10,8},{12,14},{14,12},{1,3},{3,1},... | collective-permute-start | bytes 589832 | tf_op jit(solution)/shard_map/ppermute | solution.py:141
  56.2 4.2 %collective-permute-start.8 = (bf16[3,48,1024]{2,1,0:T(8,128)(2,1)S(1)}, bf16[3,48,1024]{2,1,0:T(8,128)(2,1)S(1)}, u32[]{:S(2)}, u32[]{:S(2)}) collective-permute-start(bf16[3,48,1024]{2,1,0:T(8,128)(2,1)S(1)} %bitcast.208), channel_id=1, source_target_pairs={{0,2},{2,0},{4,6},{6,4},{8,10},{10,8},{12,14},{14,12},{1,3},{3,1},... | collective-permute-start | bytes 884744 | tf_op jit(solution)/shard_map/ppermute | solution.py:143
  58.5 2.5 %copy-start.4 = (bf16[8,64,1024]{2,1,0:T(8,128)(2,1)S(1)}, bf16[8,64,1024]{2,1,0:T(8,128)(2,1)}, u32[]{:S(2)}) copy-start(bf16[8,64,1024]{2,1,0:T(8,128)(2,1)} %copy-done.3) | copy-start | bytes 3145732
  58.8 11.9 %collective-permute-start.7 = (bf16[96,1024]{1,0:T(8,128)(2,1)S(1)}, bf16[96,1024]{1,0:T(8,128)(2,1)S(1)}, u32[]{:S(2)}, u32[]{:S(2)}) collective-permute-start(bf16[96,1024]{1,0:T(8,128)(2,1)S(1)} %convolution_convert_fusion.5), channel_id=1, source_target_pairs={{0,1},{1,0},{2,3},{3,2},{4,5},{5,4},{6,7},{7,6},{8,9},{9,8},{10,11... | collective-permute-start | bytes 589832 | tf_op jit(solution)/shard_map/ppermute | solution.py:49
  60.4 9.7 %collective-permute-start.9 = (bf16[2,48,1024]{2,1,0:T(8,128)(2,1)S(1)}, bf16[2,48,1024]{2,1,0:T(8,128)(2,1)S(1)}, u32[]{:S(2)}, u32[]{:S(2)}) collective-permute-start(bf16[2,48,1024]{2,1,0:T(8,128)(2,1)S(1)} %get-tuple-element.11), channel_id=1, source_target_pairs={{0,4},{2,6},{4,8},{6,10},{8,12},{10,14},{12,0},{14,2},{1,5},{3,7},... | collective-permute-start | bytes 589832 | tf_op jit(solution)/shard_map/ppermute | solution.py:147
  62.7 14.7 %collective-permute-start.13 = (bf16[2,48,1024]{2,1,0:T(8,128)(2,1)S(1)}, bf16[2,48,1024]{2,1,0:T(8,128)(2,1)S(1)}, u32[]{:S(2)}, u32[]{:S(2)}) collective-permute-start(bf16[2,48,1024]{2,1,0:T(8,128)(2,1)S(1)} %get-tuple-element.13), channel_id=1, source_target_pairs={{0,8},{2,10},{4,12},{6,14},{8,0},{10,2},{12,4},{14,6},{1,9},{3,11}... | collective-permute-start | bytes 589832 | tf_op jit(solution)/shard_map/ppermute | solution.py:147
  64.1 13.9 %collective-permute-start.17 = (bf16[2,48,1024]{2,1,0:T(8,128)(2,1)S(1)}, bf16[2,48,1024]{2,1,0:T(8,128)(2,1)S(1)}, u32[]{:S(2)}, u32[]{:S(2)}) collective-permute-start(bf16[2,48,1024]{2,1,0:T(8,128)(2,1)S(1)} %get-tuple-element.12), channel_id=1, source_target_pairs={{0,12},{2,14},{4,0},{6,2},{8,4},{10,6},{12,8},{14,10},{1,13},{3,15... | collective-permute-start | bytes 589832 | tf_op jit(solution)/shard_map/ppermute | solution.py:147
  70.2 9.3 %collective-permute-start.10 = (bf16[96,1024]{1,0:T(8,128)(2,1)S(1)}, bf16[96,1024]{1,0:T(8,128)(2,1)S(1)}, u32[]{:S(2)}, u32[]{:S(2)}) collective-permute-start(bf16[96,1024]{1,0:T(8,128)(2,1)S(1)} %bitcast.219), channel_id=1, source_target_pairs={{0,1},{1,0},{2,3},{3,2},{4,5},{5,4},{6,7},{7,6},{8,9},{9,8},{10,11... | collective-permute-start | bytes 589832 | tf_op jit(solution)/shard_map/ppermute | solution.py:49
  77.5 7.8 %collective-permute-start.14 = (bf16[96,1024]{1,0:T(8,128)(2,1)S(1)}, bf16[96,1024]{1,0:T(8,128)(2,1)S(1)}, u32[]{:S(2)}, u32[]{:S(2)}) collective-permute-start(bf16[96,1024]{1,0:T(8,128)(2,1)S(1)} %bitcast.216), channel_id=1, source_target_pairs={{0,1},{1,0},{2,3},{3,2},{4,5},{5,4},{6,7},{7,6},{8,9},{9,8},{10,11... | collective-permute-start | bytes 589832 | tf_op jit(solution)/shard_map/ppermute | solution.py:49
  78.0 11.5 %collective-permute-start.18 = (bf16[96,1024]{1,0:T(8,128)(2,1)S(1)}, bf16[96,1024]{1,0:T(8,128)(2,1)S(1)}, u32[]{:S(2)}, u32[]{:S(2)}) collective-permute-start(bf16[96,1024]{1,0:T(8,128)(2,1)S(1)} %bitcast.213), channel_id=1, source_target_pairs={{0,1},{1,0},{2,3},{3,2},{4,5},{5,4},{6,7},{7,6},{8,9},{9,8},{10,11... | collective-permute-start | bytes 589832 | tf_op jit(solution)/shard_map/ppermute | solution.py:49
  81.3 12.4 %collective-permute-start.11 = (bf16[96,1024]{1,0:T(8,128)(2,1)S(1)}, bf16[96,1024]{1,0:T(8,128)(2,1)S(1)}, u32[]{:S(2)}, u32[]{:S(2)}) collective-permute-start(bf16[96,1024]{1,0:T(8,128)(2,1)S(1)} %convolution_convert_fusion.4), channel_id=1, source_target_pairs={{0,1},{1,0},{2,3},{3,2},{4,5},{5,4},{6,7},{7,6},{8,9},{9,8},{10,11... | collective-permute-start | bytes 589832 | tf_op jit(solution)/shard_map/ppermute | solution.py:49
  87.0 11.4 %collective-permute-start.15 = (bf16[96,1024]{1,0:T(8,128)(2,1)S(1)}, bf16[96,1024]{1,0:T(8,128)(2,1)S(1)}, u32[]{:S(2)}, u32[]{:S(2)}) collective-permute-start(bf16[96,1024]{1,0:T(8,128)(2,1)S(1)} %convolution_convert_fusion.3), channel_id=1, source_target_pairs={{0,1},{1,0},{2,3},{3,2},{4,5},{5,4},{6,7},{7,6},{8,9},{9,8},{10,11... | collective-permute-start | bytes 589832 | tf_op jit(solution)/shard_map/ppermute | solution.py:49
  91.3 9.8 %collective-permute-start.19 = (bf16[96,1024]{1,0:T(8,128)(2,1)S(1)}, bf16[96,1024]{1,0:T(8,128)(2,1)S(1)}, u32[]{:S(2)}, u32[]{:S(2)}) collective-permute-start(bf16[96,1024]{1,0:T(8,128)(2,1)S(1)} %convolution_convert_fusion.2), channel_id=1, source_target_pairs={{0,1},{1,0},{2,3},{3,2},{4,5},{5,4},{6,7},{7,6},{8,9},{9,8},{10,11... | collective-permute-start | bytes 589832 | tf_op jit(solution)/shard_map/ppermute | solution.py:49
  94.0 11.8 %collective-permute-start.12 = (bf16[48,1024]{1,0:T(8,128)(2,1)S(1)}, bf16[48,1024]{1,0:T(8,128)(2,1)S(1)}, u32[]{:S(2)}, u32[]{:S(2)}) collective-permute-start(bf16[48,1024]{1,0:T(8,128)(2,1)S(1)} %get-tuple-element.20), channel_id=1, source_target_pairs={{0,12},{2,14},{4,0},{6,2},{8,4},{10,6},{12,8},{14,10},{1,13},{3,15... | collective-permute-start | bytes 294920 | tf_op jit(solution)/shard_map/ppermute | solution.py:187
  98.7 7.7 %collective-permute-start.16 = (bf16[48,1024]{1,0:T(8,128)(2,1)S(1)}, bf16[48,1024]{1,0:T(8,128)(2,1)S(1)}, u32[]{:S(2)}, u32[]{:S(2)}) collective-permute-start(bf16[48,1024]{1,0:T(8,128)(2,1)S(1)} %get-tuple-element.22), channel_id=1, source_target_pairs={{0,8},{2,10},{4,12},{6,14},{8,0},{10,2},{12,4},{14,6},{1,9},{3,11}... | collective-permute-start | bytes 294920 | tf_op jit(solution)/shard_map/ppermute | solution.py:187
  101.4 6.9 %collective-permute-start.20 = (bf16[48,1024]{1,0:T(8,128)(2,1)S(1)}, bf16[48,1024]{1,0:T(8,128)(2,1)S(1)}, u32[]{:S(2)}, u32[]{:S(2)}) collective-permute-start(bf16[48,1024]{1,0:T(8,128)(2,1)S(1)} %get-tuple-element.24), channel_id=1, source_target_pairs={{0,4},{2,6},{4,8},{6,10},{8,12},{10,14},{12,0},{14,2},{1,5},{3,7},... | collective-permute-start | bytes 294920 | tf_op jit(solution)/shard_map/ppermute | solution.py:187
  103.6 4.8 %collective-permute-start.21 = (bf16[48,1024]{1,0:T(8,128)(2,1)S(1)}, bf16[48,1024]{1,0:T(8,128)(2,1)S(1)}, u32[]{:S(2)}, u32[]{:S(2)}) collective-permute-start(bf16[48,1024]{1,0:T(8,128)(2,1)S(1)} %get-tuple-element.19), channel_id=1, source_target_pairs={{0,2},{2,0},{4,6},{6,4},{8,10},{10,8},{12,14},{14,12},{1,3},{3,1},... | collective-permute-start | bytes 294920 | tf_op jit(solution)/shard_map/ppermute | solution.py:184
  103.7 5.7 %collective-permute-start.22 = (bf16[48,1024]{1,0:T(8,128)(2,1)S(1)}, bf16[48,1024]{1,0:T(8,128)(2,1)S(1)}, u32[]{:S(2)}, u32[]{:S(2)}) collective-permute-start(bf16[48,1024]{1,0:T(8,128)(2,1)S(1)} %get-tuple-element.21), channel_id=1, source_target_pairs={{0,14},{2,12},{4,2},{6,0},{8,6},{10,4},{12,10},{14,8},{1,15},{3,13... | collective-permute-start | bytes 294920 | tf_op jit(solution)/shard_map/ppermute | solution.py:189
  105.8 10.8 %collective-permute-start.23 = (bf16[48,1024]{1,0:T(8,128)(2,1)S(1)}, bf16[48,1024]{1,0:T(8,128)(2,1)S(1)}, u32[]{:S(2)}, u32[]{:S(2)}) collective-permute-start(bf16[48,1024]{1,0:T(8,128)(2,1)S(1)} %get-tuple-element.23), channel_id=1, source_target_pairs={{0,10},{2,8},{4,14},{6,12},{8,2},{10,0},{12,6},{14,4},{1,11},{3,9}... | collective-permute-start | bytes 294920 | tf_op jit(solution)/shard_map/ppermute | solution.py:189
  106.4 10.2 %collective-permute-start.24 = (bf16[48,1024]{1,0:T(8,128)(2,1)S(1)}, bf16[48,1024]{1,0:T(8,128)(2,1)S(1)}, u32[]{:S(2)}, u32[]{:S(2)}) collective-permute-start(bf16[48,1024]{1,0:T(8,128)(2,1)S(1)} %get-tuple-element.25), channel_id=1, source_target_pairs={{0,6},{2,4},{4,10},{6,8},{8,14},{10,12},{12,2},{14,0},{1,7},{3,5},... | collective-permute-start | bytes 294920 | tf_op jit(solution)/shard_map/ppermute | solution.py:189
  117.3 4.3 %collective-permute-start.25 = (bf16[32,1024]{1,0:T(8,128)(2,1)S(1)}, bf16[32,1024]{1,0:T(8,128)(2,1)S(1)}, u32[]{:S(2)}, u32[]{:S(2)}) collective-permute-start(bf16[32,1024]{1,0:T(8,128)(2,1)S(1)} %select_convert_fusion), channel_id=1, source_target_pairs={{0,1},{1,0},{2,3},{3,2},{4,5},{5,4},{6,7},{7,6},{8,9},{9,8},{10,11... | collective-permute-start | bytes 196616 | tf_op jit(solution)/shard_map/ppermute | solution.py:49
  (3 other events, 4.3 us)
Sparse Core Ops, SparseCore 0:
  9.6 34.5 all-gather.1

commit v20 on v19

--- a/solution.py
+++ b/solution.py
@@ -140,11 +140,13 @@
     near_in = jnp.concatenate(
         [near[0], lax.ppermute(near[1], "ctx", perm=core_swap)], axis=0
     )
-    far_pairs = jnp.stack([far[0], lax.ppermute(far[1], "ctx", perm=core_swap)], axis=1)
     arrived = [None]
     for shift in range(1, n_chip):
         perm = [(i, ((i // 2 + shift) % n_chip) * 2 + i % 2) for i in range(n_ctx)]
-        arrived.append(lax.ppermute(far_pairs[shift - 1], "ctx", perm=perm))
+        from_same = lax.ppermute(far[0][shift - 1], "ctx", perm=perm)
+        perm = [(i, ((i // 2 + shift) % n_chip) * 2 + 1 - i % 2) for i in range(n_ctx)]
+        from_other = lax.ppermute(far[1][shift - 1], "ctx", perm=perm)
+        arrived.append(jnp.stack([from_same, from_other]))
     my_start = my_exp * half_d
     other_start = (1 - my_exp) * half_d
     gate_mine = lax.dynamic_slice_in_dim(gate_matrix, my_start, half_d, axis=0)

time: 129 us -> 131 us (1.016)
  starting transfers between devices: 32.1 us -> 38.4 us
  waiting for transfers between devices: 59 us -> 54.5 us
    ppermute x10, starting transfers between devices: 9.21 us -> 15 us  [exp_swap(): return lax.ppermute(x, 'exp', perm=[(0, 1), (1, 0)])]
    ppermute x10, waiting for transfers between devices: 19.5 us -> 16.5 us  [exp_swap(): return lax.ppermute(x, 'exp', perm=[(0, 1), (1, 0)])]
    ppermute x4 -> x6, starting transfers between devices: 4.63 us -> 4.13 us  [the longest x3 3.46 us: moe_column_halves(): from_same = lax.ppermute(far[0][shift - 1], 'ctx', perm=perm)]
    ppermute x4 -> x6, waiting for transfers between devices: 10.4 us -> 10.1 us  [the longest x3 9.33 us: moe_column_halves(): from_same = lax.ppermute(far[0][shift - 1], 'ctx', perm=perm)]
  transfers between devices with their start and end apart: 27 -> 29, of which waited for: 15 -> 19; matrix products, arithmetic and copies ran while one was open for 15% -> 14% of each run, Pallas kernels for 0% -> 0%
where the time goes in v20:
time: 131 us
  waiting for transfers between devices  54.5 us (42%)
  starting transfers between devices  38.4 us (29%)
  between operations  15.3 us (12%)
  matrix products  14.3 us (11%)
  other arithmetic  4.61 us (4%)
  local copies, waits for them, and re-layouts  3.63 us (3%)
    ppermute x10, waiting for transfers between devices, exp_swap(): return lax.ppermute(x, 'exp', perm=[(0, 1), (1, 0)])  16.5 us
    all_gather x1, waiting for transfers between devices, local(): lax.all_gather(out_weight, 'ctx', axis=0, tiled=True)  16 us
    ppermute x10, starting transfers between devices, exp_swap(): return lax.ppermute(x, 'exp', perm=[(0, 1), (1, 0)])  15 us
    ppermute x3, waiting for transfers between devices, moe_column_halves(): from_same = lax.ppermute(far[0][shift - 1], 'ctx', perm=perm)  9.33 us
    ppermute x3, waiting for transfers between devices, moe_column_halves(): returned_partner[shift] = lax.ppermute(summed[idx][1], 'ctx', perm=perm)  8.24 us
    ppermute x3, starting transfers between devices, moe_column_halves(): returned[shift] = lax.ppermute(summed[idx][0], 'ctx', perm=perm)  7.64 us
    ppermute x3, starting transfers between devices, ctx_gather_blocks(): stack.append(lax.ppermute(rows, 'ctx', perm=perm))  7.01 us
    ppermute x3, starting transfers between devices, moe_column_halves(): from_same = lax.ppermute(far[0][shift - 1], 'ctx', perm=perm)  3.46 us
  transfers between devices with their start and end apart: 29, of which 19 were waited for; matrix products, arithmetic and copies ran while one was open for 14% of the time, Pallas kernels for 0%

profile of v20, /device:TPU:0, one launch (start us, length us, event | category | flops | bytes accessed | tf_op | source)
XLA Modules:
  0.0 130.6 jit_solution(16990774629276304825)
XLA Ops:
  7.3 1.0 fusion.147
  8.3 3.1 %collective-permute-start.1 = (bf16[64,1024]{1,0:T(8,128)(2,1)S(1)}, bf16[64,1024]{1,0:T(8,128)(2,1)S(1)}, u32[]{:S(2)}, u32[]{:S(2)}) collective-permute-start(bf16[64,1024]{1,0:T(8,128)(2,1)S(1)} %get-tuple-element.28), channel_id=1, source_target_pairs={{0,4},{2,6},{4,8},{6,10},{8,12},{10,14},{12,0},{14,2},{1,5},{3,7},... | collective-permute-start | bytes 393224 | tf_op jit(solution)/shard_map/ppermute | solution.py:212
  11.3 2.6 %collective-permute-start.2 = (bf16[64,1024]{1,0:T(8,128)(2,1)S(1)}, bf16[64,1024]{1,0:T(8,128)(2,1)S(1)}, u32[]{:S(2)}, u32[]{:S(2)}) collective-permute-start(bf16[64,1024]{1,0:T(8,128)(2,1)S(1)} %get-tuple-element.28), channel_id=1, source_target_pairs={{0,8},{2,10},{4,12},{6,14},{8,0},{10,2},{12,4},{14,6},{1,9},{3,11}... | collective-permute-start | bytes 393224 | tf_op jit(solution)/shard_map/ppermute | solution.py:212
  13.9 1.3 %collective-permute-start.3 = (bf16[64,1024]{1,0:T(8,128)(2,1)S(1)}, bf16[64,1024]{1,0:T(8,128)(2,1)S(1)}, u32[]{:S(2)}, u32[]{:S(2)}) collective-permute-start(bf16[64,1024]{1,0:T(8,128)(2,1)S(1)} %get-tuple-element.28), channel_id=1, source_target_pairs={{0,12},{2,14},{4,0},{6,2},{8,4},{10,6},{12,8},{14,10},{1,13},{3,15... | collective-permute-start | bytes 393224 | tf_op jit(solution)/shard_map/ppermute | solution.py:212
  15.3 1.6 %collective-permute-start = (bf16[32,2048]{1,0:T(8,128)(2,1)}, bf16[32,2048]{1,0:T(8,128)(2,1)S(1)}, u32[]{:S(2)}, u32[]{:S(2)}) collective-permute-start(bf16[32,2048]{1,0:T(8,128)(2,1)} %bitcast.210), channel_id=1, source_target_pairs={{0,1},{1,0},{2,3},{3,2},{4,5},{5,4},{6,7},{7,6},{8,9},{9,8},{10,11... | collective-permute-start | bytes 393224 | tf_op jit(solution)/shard_map/ppermute | solution.py:49
  21.6 1.0 collective-permute-done.2
  22.8 1.8 %collective-permute-done.4 = bf16[4,64,1024]{2,1,0:T(8,128)(2,1)S(1)} collective-permute-done((bf16[4,64,1024]{2,1,0:T(8,128)(2,1)S(1)}, bf16[4,64,1024]{2,1,0:T(8,128)(2,1)S(1)}, u32[]{:S(2)}, u32[]{:S(2)}) %collective-permute-start.4) | collective-permute-done | bytes 524320 | tf_op jit(solution)/shard_map/ppermute | solution.py:214
  26.6 1.0 fusion.14
  27.6 16.0 %all-gather.2.cloned.1.call-done = bf16[2048,512]{1,0:T(8,128)(2,1)} async-done(((bf16[256,512]{1,0:T(8,128)(2,1)}), bf16[2048,512]{1,0:T(8,128)(2,1)}) %all-gather.2.cloned.1.call-update) | async-done | bytes 2097168 | tf_op jit(solution)/shard_map/all_gather | solution.py:284
  43.6 2.4 %fusion.156 = (bf16[64,2048]{1,0:T(8,128)(2,1)S(1)}, f32[64,2048]{1,0:T(8,128)S(1)}) fusion(bf16[2048,512]{1,0:T(8,128)(2,1)} %all-gather.2.cloned.1.call-done, bf16[4,8,8,128]{3,2,1,0:T(8,128)(2,1)} %fusion.14), kind=kOutput, calls=%fused_computation.243 | convolution fusion | flops 134348800 | bytes 2949120 | tf_op jit(solution)/shard_map/tc,oc->to/dot_general | solution.py:281
  46.0 1.6 %collective-permute-start.5 = (bf16[64,2048]{1,0:T(8,128)(2,1)S(1)}, bf16[64,2048]{1,0:T(8,128)(2,1)S(1)}, u32[]{:S(2)}, u32[]{:S(2)}) collective-permute-start(bf16[64,2048]{1,0:T(8,128)(2,1)S(1)} %get-tuple-element.31), channel_id=1, source_target_pairs={{0,1},{1,0},{2,3},{3,2},{4,5},{5,4},{6,7},{7,6},{8,9},{9,8},{10,11... | collective-permute-start | bytes 786440 | tf_op jit(solution)/shard_map/ppermute | solution.py:49
  49.4 5.1 %collective-permute-done.5 = bf16[64,2048]{1,0:T(8,128)(2,1)S(1)} collective-permute-done((bf16[64,2048]{1,0:T(8,128)(2,1)S(1)}, bf16[64,2048]{1,0:T(8,128)(2,1)S(1)}, u32[]{:S(2)}, u32[]{:S(2)}) %collective-permute-start.5) | collective-permute-done | bytes 262176 | tf_op jit(solution)/shard_map/ppermute | solution.py:49
  56.4 1.2 collective-permute-start.6
  57.6 2.6 %collective-permute-start.13 = (bf16[48,1024]{1,0:T(8,128)(2,1)S(1)}, bf16[48,1024]{1,0:T(8,128)(2,1)S(1)}, u32[]{:S(2)}, u32[]{:S(2)}) collective-permute-start(bf16[48,1024]{1,0:T(8,128)(2,1)S(1)} %get-tuple-element.15), channel_id=1, source_target_pairs={{0,8},{2,10},{4,12},{6,14},{8,0},{10,2},{12,4},{14,6},{1,9},{3,11}... | collective-permute-start | bytes 294920 | tf_op jit(solution)/shard_map/ppermute | solution.py:146
  60.2 2.8 %collective-permute-done.8 = bf16[48,1024]{1,0:T(8,128)(2,1)S(1)} collective-permute-done((bf16[48,1024]{1,0:T(8,128)(2,1)S(1)}, bf16[48,1024]{1,0:T(8,128)(2,1)S(1)}, u32[]{:S(2)}, u32[]{:S(2)}) %collective-permute-start.8) | collective-permute-done | bytes 98336 | tf_op jit(solution)/shard_map/ppermute | solution.py:146
  64.1 6.6 %collective-permute-done.13 = bf16[48,1024]{1,0:T(8,128)(2,1)S(1)} collective-permute-done((bf16[48,1024]{1,0:T(8,128)(2,1)S(1)}, bf16[48,1024]{1,0:T(8,128)(2,1)S(1)}, u32[]{:S(2)}, u32[]{:S(2)}) %collective-permute-start.13) | collective-permute-done | bytes 98336 | tf_op jit(solution)/shard_map/ppermute | solution.py:146
  70.6 1.6 %collective-permute-start.10 = (bf16[96,1024]{1,0:T(8,128)(2,1)S(1)}, bf16[96,1024]{1,0:T(8,128)(2,1)S(1)}, u32[]{:S(2)}, u32[]{:S(2)}) collective-permute-start(bf16[96,1024]{1,0:T(8,128)(2,1)S(1)} %bitcast.198), channel_id=1, source_target_pairs={{0,1},{1,0},{2,3},{3,2},{4,5},{5,4},{6,7},{7,6},{8,9},{9,8},{10,11... | collective-permute-start | bytes 589832 | tf_op jit(solution)/shard_map/ppermute | solution.py:49
  72.6 1.6 %collective-permute-start.15 = (bf16[96,1024]{1,0:T(8,128)(2,1)S(1)}, bf16[96,1024]{1,0:T(8,128)(2,1)S(1)}, u32[]{:S(2)}, u32[]{:S(2)}) collective-permute-start(bf16[96,1024]{1,0:T(8,128)(2,1)S(1)} %bitcast.195), channel_id=1, source_target_pairs={{0,1},{1,0},{2,3},{3,2},{4,5},{5,4},{6,7},{7,6},{8,9},{9,8},{10,11... | collective-permute-start | bytes 589832 | tf_op jit(solution)/shard_map/ppermute | solution.py:49
  76.3 1.6 %collective-permute-start.7 = (bf16[96,1024]{1,0:T(8,128)(2,1)S(1)}, bf16[96,1024]{1,0:T(8,128)(2,1)S(1)}, u32[]{:S(2)}, u32[]{:S(2)}) collective-permute-start(bf16[96,1024]{1,0:T(8,128)(2,1)S(1)} %convolution_convert_fusion.5), channel_id=1, source_target_pairs={{0,1},{1,0},{2,3},{3,2},{4,5},{5,4},{6,7},{7,6},{8,9},{9,8},{10,11... | collective-permute-start | bytes 589832 | tf_op jit(solution)/shard_map/ppermute | solution.py:49
  80.2 1.6 %collective-permute-start.11 = (bf16[96,1024]{1,0:T(8,128)(2,1)S(1)}, bf16[96,1024]{1,0:T(8,128)(2,1)S(1)}, u32[]{:S(2)}, u32[]{:S(2)}) collective-permute-start(bf16[96,1024]{1,0:T(8,128)(2,1)S(1)} %convolution_convert_fusion.4), channel_id=1, source_target_pairs={{0,1},{1,0},{2,3},{3,2},{4,5},{5,4},{6,7},{7,6},{8,9},{9,8},{10,11... | collective-permute-start | bytes 589832 | tf_op jit(solution)/shard_map/ppermute | solution.py:49
  84.4 1.6 %collective-permute-start.16 = (bf16[96,1024]{1,0:T(8,128)(2,1)S(1)}, bf16[96,1024]{1,0:T(8,128)(2,1)S(1)}, u32[]{:S(2)}, u32[]{:S(2)}) collective-permute-start(bf16[96,1024]{1,0:T(8,128)(2,1)S(1)} %convolution_convert_fusion.3), channel_id=1, source_target_pairs={{0,1},{1,0},{2,3},{3,2},{4,5},{5,4},{6,7},{7,6},{8,9},{9,8},{10,11... | collective-permute-start | bytes 589832 | tf_op jit(solution)/shard_map/ppermute | solution.py:49
  88.6 1.6 %collective-permute-start.21 = (bf16[96,1024]{1,0:T(8,128)(2,1)S(1)}, bf16[96,1024]{1,0:T(8,128)(2,1)S(1)}, u32[]{:S(2)}, u32[]{:S(2)}) collective-permute-start(bf16[96,1024]{1,0:T(8,128)(2,1)S(1)} %convolution_convert_fusion.2), channel_id=1, source_target_pairs={{0,1},{1,0},{2,3},{3,2},{4,5},{5,4},{6,7},{7,6},{8,9},{9,8},{10,11... | collective-permute-start | bytes 589832 | tf_op jit(solution)/shard_map/ppermute | solution.py:49
  91.3 3.9 %collective-permute-done.11 = bf16[96,1024]{1,0:T(8,128)(2,1)S(1)} collective-permute-done((bf16[96,1024]{1,0:T(8,128)(2,1)S(1)}, bf16[96,1024]{1,0:T(8,128)(2,1)S(1)}, u32[]{:S(2)}, u32[]{:S(2)}) %collective-permute-start.11) | collective-permute-done | bytes 196640 | tf_op jit(solution)/shard_map/ppermute | solution.py:49
  95.6 4.9 %collective-permute-start.12 = (bf16[48,1024]{1,0:T(8,128)(2,1)S(1)}, bf16[48,1024]{1,0:T(8,128)(2,1)S(1)}, u32[]{:S(2)}, u32[]{:S(2)}) collective-permute-start(bf16[48,1024]{1,0:T(8,128)(2,1)S(1)} %get-tuple-element.21), channel_id=1, source_target_pairs={{0,12},{2,14},{4,0},{6,2},{8,4},{10,6},{12,8},{14,10},{1,13},{3,15... | collective-permute-start | bytes 294920 | tf_op jit(solution)/shard_map/ppermute | solution.py:189
  100.8 1.7 %collective-permute-done.21 = bf16[96,1024]{1,0:T(8,128)(2,1)S(1)} collective-permute-done((bf16[96,1024]{1,0:T(8,128)(2,1)S(1)}, bf16[96,1024]{1,0:T(8,128)(2,1)S(1)}, u32[]{:S(2)}, u32[]{:S(2)}) %collective-permute-start.21) | collective-permute-done | bytes 196640 | tf_op jit(solution)/shard_map/ppermute | solution.py:49
  102.9 2.7 %collective-permute-start.22 = (bf16[48,1024]{1,0:T(8,128)(2,1)S(1)}, bf16[48,1024]{1,0:T(8,128)(2,1)S(1)}, u32[]{:S(2)}, u32[]{:S(2)}) collective-permute-start(bf16[48,1024]{1,0:T(8,128)(2,1)S(1)} %get-tuple-element.25), channel_id=1, source_target_pairs={{0,4},{2,6},{4,8},{6,10},{8,12},{10,14},{12,0},{14,2},{1,5},{3,7},... | collective-permute-start | bytes 294920 | tf_op jit(solution)/shard_map/ppermute | solution.py:189
  105.7 1.6 %collective-permute-start.24 = (bf16[48,1024]{1,0:T(8,128)(2,1)S(1)}, bf16[48,1024]{1,0:T(8,128)(2,1)S(1)}, u32[]{:S(2)}, u32[]{:S(2)}) collective-permute-start(bf16[48,1024]{1,0:T(8,128)(2,1)S(1)} %get-tuple-element.22), channel_id=1, source_target_pairs={{0,14},{2,12},{4,2},{6,0},{8,6},{10,4},{12,10},{14,8},{1,15},{3,13... | collective-permute-start | bytes 294920 | tf_op jit(solution)/shard_map/ppermute | solution.py:191
  108.5 1.1 collective-permute-start.26
  109.8 1.9 %collective-permute-done.24 = bf16[48,1024]{1,0:T(8,128)(2,1)S(1)} collective-permute-done((bf16[48,1024]{1,0:T(8,128)(2,1)S(1)}, bf16[48,1024]{1,0:T(8,128)(2,1)S(1)}, u32[]{:S(2)}, u32[]{:S(2)}) %collective-permute-start.24) | collective-permute-done | bytes 98336 | tf_op jit(solution)/shard_map/ppermute | solution.py:191
  111.7 6.4 %collective-permute-done.25 = bf16[48,1024]{1,0:T(8,128)(2,1)S(1)} collective-permute-done((bf16[48,1024]{1,0:T(8,128)(2,1)S(1)}, bf16[48,1024]{1,0:T(8,128)(2,1)S(1)}, u32[]{:S(2)}, u32[]{:S(2)}) %collective-permute-start.25) | collective-permute-done | bytes 98336 | tf_op jit(solution)/shard_map/ppermute | solution.py:191
  118.7 1.6 %collective-permute-start.27 = (bf16[32,1024]{1,0:T(8,128)(2,1)S(1)}, bf16[32,1024]{1,0:T(8,128)(2,1)S(1)}, u32[]{:S(2)}, u32[]{:S(2)}) collective-permute-start(bf16[32,1024]{1,0:T(8,128)(2,1)S(1)} %select_convert_fusion), channel_id=1, source_target_pairs={{0,1},{1,0},{2,3},{3,2},{4,5},{5,4},{6,7},{7,6},{8,9},{9,8},{10,11... | collective-permute-start | bytes 196616 | tf_op jit(solution)/shard_map/ppermute | solution.py:49
  120.3 2.7 %collective-permute-done.27 = bf16[32,1024]{1,0:T(8,128)(2,1)S(1)} collective-permute-done((bf16[32,1024]{1,0:T(8,128)(2,1)S(1)}, bf16[32,1024]{1,0:T(8,128)(2,1)S(1)}, u32[]{:S(2)}, u32[]{:S(2)}) %collective-permute-start.27) | collective-permute-done | bytes 65568 | tf_op jit(solution)/shard_map/ppermute | solution.py:49
  (135 shorter events, 25.5 us)
Async XLA Ops:
  7.2 68.8 %copy-start = (bf16[1,352,2048]{2,1,0:T(8,128)(2,1)S(1)}, bf16[1,352,2048]{2,1,0:T(8,128)(2,1)}, u32[]{:S(2)}) copy-start(bf16[1,352,2048]{2,1,0:T(8,128)(2,1)} %param.20) | copy-start | bytes 4325380
  7.2 36.4 %all-gather.2.cloned.1.call-start = ((), (), s32[]{:S(2)}) async-start(), calls=%async_computation | async-start | bytes 2359296 | tf_op jit(solution)/shard_map/all_gather | solution.py:284
  8.3 13.3 %collective-permute-start.1 = (bf16[64,1024]{1,0:T(8,128)(2,1)S(1)}, bf16[64,1024]{1,0:T(8,128)(2,1)S(1)}, u32[]{:S(2)}, u32[]{:S(2)}) collective-permute-start(bf16[64,1024]{1,0:T(8,128)(2,1)S(1)} %get-tuple-element.28), channel_id=1, source_target_pairs={{0,4},{2,6},{4,8},{6,10},{8,12},{10,14},{12,0},{14,2},{1,5},{3,7},... | collective-permute-start | bytes 393224 | tf_op jit(solution)/shard_map/ppermute | solution.py:212
  11.3 11.2 %collective-permute-start.2 = (bf16[64,1024]{1,0:T(8,128)(2,1)S(1)}, bf16[64,1024]{1,0:T(8,128)(2,1)S(1)}, u32[]{:S(2)}, u32[]{:S(2)}) collective-permute-start(bf16[64,1024]{1,0:T(8,128)(2,1)S(1)} %get-tuple-element.28), channel_id=1, source_target_pairs={{0,8},{2,10},{4,12},{6,14},{8,0},{10,2},{12,4},{14,6},{1,9},{3,11}... | collective-permute-start | bytes 393224 | tf_op jit(solution)/shard_map/ppermute | solution.py:212
  13.9 8.6 %collective-permute-start.3 = (bf16[64,1024]{1,0:T(8,128)(2,1)S(1)}, bf16[64,1024]{1,0:T(8,128)(2,1)S(1)}, u32[]{:S(2)}, u32[]{:S(2)}) collective-permute-start(bf16[64,1024]{1,0:T(8,128)(2,1)S(1)} %get-tuple-element.28), channel_id=1, source_target_pairs={{0,12},{2,14},{4,0},{6,2},{8,4},{10,6},{12,8},{14,10},{1,13},{3,15... | collective-permute-start | bytes 393224 | tf_op jit(solution)/shard_map/ppermute | solution.py:212
  15.3 34.1 %collective-permute-start = (bf16[32,2048]{1,0:T(8,128)(2,1)}, bf16[32,2048]{1,0:T(8,128)(2,1)S(1)}, u32[]{:S(2)}, u32[]{:S(2)}) collective-permute-start(bf16[32,2048]{1,0:T(8,128)(2,1)} %bitcast.210), channel_id=1, source_target_pairs={{0,1},{1,0},{2,3},{3,2},{4,5},{5,4},{6,7},{7,6},{8,9},{9,8},{10,11... | collective-permute-start | bytes 393224 | tf_op jit(solution)/shard_map/ppermute | solution.py:49
  22.6 2.0 %collective-permute-start.4 = (bf16[4,64,1024]{2,1,0:T(8,128)(2,1)S(1)}, bf16[4,64,1024]{2,1,0:T(8,128)(2,1)S(1)}, u32[]{:S(2)}, u32[]{:S(2)}) collective-permute-start(bf16[4,64,1024]{2,1,0:T(8,128)(2,1)S(1)} %pad_maximum_fusion.1), channel_id=1, source_target_pairs={{0,2},{2,0},{4,6},{6,4},{8,10},{10,8},{12,14},{14,12},{1,3},{3,1},... | collective-permute-start | bytes 1572872 | tf_op jit(solution)/shard_map/ppermute | solution.py:214
  27.6 20.0 %copy-start.4 = (bf16[8,64,1024]{2,1,0:T(8,128)(2,1)S(1)}, bf16[8,64,1024]{2,1,0:T(8,128)(2,1)}, u32[]{:S(2)}) copy-start(bf16[8,64,1024]{2,1,0:T(8,128)(2,1)} %copy-done.3) | copy-start | bytes 3145732
  27.6 26.9 %copy-start.7 = (bf16[1,32,2048]{2,1,0:T(8,128)(2,1)S(1)}, bf16[1,32,2048]{2,1,0:T(8,128)(2,1)}, u32[]{:S(2)}) copy-start(bf16[1,32,2048]{2,1,0:T(8,128)(2,1)} %param.15) | copy-start | bytes 393220
  46.0 8.5 %collective-permute-start.5 = (bf16[64,2048]{1,0:T(8,128)(2,1)S(1)}, bf16[64,2048]{1,0:T(8,128)(2,1)S(1)}, u32[]{:S(2)}, u32[]{:S(2)}) collective-permute-start(bf16[64,2048]{1,0:T(8,128)(2,1)S(1)} %get-tuple-element.31), channel_id=1, source_target_pairs={{0,1},{1,0},{2,3},{3,2},{4,5},{5,4},{6,7},{7,6},{8,9},{9,8},{10,11... | collective-permute-start | bytes 786440 | tf_op jit(solution)/shard_map/ppermute | solution.py:49
  55.5 7.4 %collective-permute-start.8 = (bf16[48,1024]{1,0:T(8,128)(2,1)S(1)}, bf16[48,1024]{1,0:T(8,128)(2,1)S(1)}, u32[]{:S(2)}, u32[]{:S(2)}) collective-permute-start(bf16[48,1024]{1,0:T(8,128)(2,1)S(1)} %get-tuple-element.11), channel_id=1, source_target_pairs={{0,4},{2,6},{4,8},{6,10},{8,12},{10,14},{12,0},{14,2},{1,5},{3,7},... | collective-permute-start | bytes 294920 | tf_op jit(solution)/shard_map/ppermute | solution.py:146
  56.4 7.0 %collective-permute-start.9 = (bf16[48,1024]{1,0:T(8,128)(2,1)S(1)}, bf16[48,1024]{1,0:T(8,128)(2,1)S(1)}, u32[]{:S(2)}, u32[]{:S(2)}) collective-permute-start(bf16[48,1024]{1,0:T(8,128)(2,1)S(1)} %get-tuple-element.16), channel_id=1, source_target_pairs={{0,6},{2,4},{4,10},{6,8},{8,14},{10,12},{12,2},{14,0},{1,7},{3,5},... | collective-permute-start | bytes 294920 | tf_op jit(solution)/shard_map/ppermute | solution.py:148
  56.4 18.4 %collective-permute-start.6 = (bf16[48,2048]{1,0:T(8,128)(2,1)S(1)}, bf16[48,2048]{1,0:T(8,128)(2,1)S(1)}, u32[]{:S(2)}, u32[]{:S(2)}) collective-permute-start(bf16[48,2048]{1,0:T(8,128)(2,1)S(1)} %get-tuple-element.18), channel_id=1, source_target_pairs={{0,2},{2,0},{4,6},{6,4},{8,10},{10,8},{12,14},{14,12},{1,3},{3,1},... | collective-permute-start | bytes 589832 | tf_op jit(solution)/shard_map/ppermute | solution.py:141
  57.6 13.1 %collective-permute-start.13 = (bf16[48,1024]{1,0:T(8,128)(2,1)S(1)}, bf16[48,1024]{1,0:T(8,128)(2,1)S(1)}, u32[]{:S(2)}, u32[]{:S(2)}) collective-permute-start(bf16[48,1024]{1,0:T(8,128)(2,1)S(1)} %get-tuple-element.15), channel_id=1, source_target_pairs={{0,8},{2,10},{4,12},{6,14},{8,0},{10,2},{12,4},{14,6},{1,9},{3,11}... | collective-permute-start | bytes 294920 | tf_op jit(solution)/shard_map/ppermute | solution.py:146
  60.2 12.4 %collective-permute-start.14 = (bf16[48,1024]{1,0:T(8,128)(2,1)S(1)}, bf16[48,1024]{1,0:T(8,128)(2,1)S(1)}, u32[]{:S(2)}, u32[]{:S(2)}) collective-permute-start(bf16[48,1024]{1,0:T(8,128)(2,1)S(1)} %get-tuple-element.14), channel_id=1, source_target_pairs={{0,10},{2,8},{4,14},{6,12},{8,2},{10,0},{12,6},{14,4},{1,11},{3,9}... | collective-permute-start | bytes 294920 | tf_op jit(solution)/shard_map/ppermute | solution.py:148
  63.0 11.3 %collective-permute-start.18 = (bf16[48,1024]{1,0:T(8,128)(2,1)S(1)}, bf16[48,1024]{1,0:T(8,128)(2,1)S(1)}, u32[]{:S(2)}, u32[]{:S(2)}) collective-permute-start(bf16[48,1024]{1,0:T(8,128)(2,1)S(1)} %get-tuple-element.13), channel_id=1, source_target_pairs={{0,12},{2,14},{4,0},{6,2},{8,4},{10,6},{12,8},{14,10},{1,13},{3,15... | collective-permute-start | bytes 294920 | tf_op jit(solution)/shard_map/ppermute | solution.py:146
  63.4 10.9 %collective-permute-start.19 = (bf16[48,1024]{1,0:T(8,128)(2,1)S(1)}, bf16[48,1024]{1,0:T(8,128)(2,1)S(1)}, u32[]{:S(2)}, u32[]{:S(2)}) collective-permute-start(bf16[48,1024]{1,0:T(8,128)(2,1)S(1)} %get-tuple-element.12), channel_id=1, source_target_pairs={{0,14},{2,12},{4,2},{6,0},{8,6},{10,4},{12,10},{14,8},{1,15},{3,13... | collective-permute-start | bytes 294920 | tf_op jit(solution)/shard_map/ppermute | solution.py:148
  70.6 7.8 %collective-permute-start.10 = (bf16[96,1024]{1,0:T(8,128)(2,1)S(1)}, bf16[96,1024]{1,0:T(8,128)(2,1)S(1)}, u32[]{:S(2)}, u32[]{:S(2)}) collective-permute-start(bf16[96,1024]{1,0:T(8,128)(2,1)S(1)} %bitcast.198), channel_id=1, source_target_pairs={{0,1},{1,0},{2,3},{3,2},{4,5},{5,4},{6,7},{7,6},{8,9},{9,8},{10,11... | collective-permute-start | bytes 589832 | tf_op jit(solution)/shard_map/ppermute | solution.py:49
  72.6 10.0 %collective-permute-start.15 = (bf16[96,1024]{1,0:T(8,128)(2,1)S(1)}, bf16[96,1024]{1,0:T(8,128)(2,1)S(1)}, u32[]{:S(2)}, u32[]{:S(2)}) collective-permute-start(bf16[96,1024]{1,0:T(8,128)(2,1)S(1)} %bitcast.195), channel_id=1, source_target_pairs={{0,1},{1,0},{2,3},{3,2},{4,5},{5,4},{6,7},{7,6},{8,9},{9,8},{10,11... | collective-permute-start | bytes 589832 | tf_op jit(solution)/shard_map/ppermute | solution.py:49
  74.3 12.6 %collective-permute-start.20 = (bf16[96,1024]{1,0:T(8,128)(2,1)S(1)}, bf16[96,1024]{1,0:T(8,128)(2,1)S(1)}, u32[]{:S(2)}, u32[]{:S(2)}) collective-permute-start(bf16[96,1024]{1,0:T(8,128)(2,1)S(1)} %bitcast.192), channel_id=1, source_target_pairs={{0,1},{1,0},{2,3},{3,2},{4,5},{5,4},{6,7},{7,6},{8,9},{9,8},{10,11... | collective-permute-start | bytes 589832 | tf_op jit(solution)/shard_map/ppermute | solution.py:49
  76.3 14.8 %collective-permute-start.7 = (bf16[96,1024]{1,0:T(8,128)(2,1)S(1)}, bf16[96,1024]{1,0:T(8,128)(2,1)S(1)}, u32[]{:S(2)}, u32[]{:S(2)}) collective-permute-start(bf16[96,1024]{1,0:T(8,128)(2,1)S(1)} %convolution_convert_fusion.5), channel_id=1, source_target_pairs={{0,1},{1,0},{2,3},{3,2},{4,5},{5,4},{6,7},{7,6},{8,9},{9,8},{10,11... | collective-permute-start | bytes 589832 | tf_op jit(solution)/shard_map/ppermute | solution.py:49
  80.2 15.1 %collective-permute-start.11 = (bf16[96,1024]{1,0:T(8,128)(2,1)S(1)}, bf16[96,1024]{1,0:T(8,128)(2,1)S(1)}, u32[]{:S(2)}, u32[]{:S(2)}) collective-permute-start(bf16[96,1024]{1,0:T(8,128)(2,1)S(1)} %convolution_convert_fusion.4), channel_id=1, source_target_pairs={{0,1},{1,0},{2,3},{3,2},{4,5},{5,4},{6,7},{7,6},{8,9},{9,8},{10,11... | collective-permute-start | bytes 589832 | tf_op jit(solution)/shard_map/ppermute | solution.py:49
  84.4 16.1 %collective-permute-start.16 = (bf16[96,1024]{1,0:T(8,128)(2,1)S(1)}, bf16[96,1024]{1,0:T(8,128)(2,1)S(1)}, u32[]{:S(2)}, u32[]{:S(2)}) collective-permute-start(bf16[96,1024]{1,0:T(8,128)(2,1)S(1)} %convolution_convert_fusion.3), channel_id=1, source_target_pairs={{0,1},{1,0},{2,3},{3,2},{4,5},{5,4},{6,7},{7,6},{8,9},{9,8},{10,11... | collective-permute-start | bytes 589832 | tf_op jit(solution)/shard_map/ppermute | solution.py:49
  88.6 14.0 %collective-permute-start.21 = (bf16[96,1024]{1,0:T(8,128)(2,1)S(1)}, bf16[96,1024]{1,0:T(8,128)(2,1)S(1)}, u32[]{:S(2)}, u32[]{:S(2)}) collective-permute-start(bf16[96,1024]{1,0:T(8,128)(2,1)S(1)} %convolution_convert_fusion.2), channel_id=1, source_target_pairs={{0,1},{1,0},{2,3},{3,2},{4,5},{5,4},{6,7},{7,6},{8,9},{9,8},{10,11... | collective-permute-start | bytes 589832 | tf_op jit(solution)/shard_map/ppermute | solution.py:49
  95.6 11.7 %collective-permute-start.12 = (bf16[48,1024]{1,0:T(8,128)(2,1)S(1)}, bf16[48,1024]{1,0:T(8,128)(2,1)S(1)}, u32[]{:S(2)}, u32[]{:S(2)}) collective-permute-start(bf16[48,1024]{1,0:T(8,128)(2,1)S(1)} %get-tuple-element.21), channel_id=1, source_target_pairs={{0,12},{2,14},{4,0},{6,2},{8,4},{10,6},{12,8},{14,10},{1,13},{3,15... | collective-permute-start | bytes 294920 | tf_op jit(solution)/shard_map/ppermute | solution.py:189
  100.8 7.7 %collective-permute-start.17 = (bf16[48,1024]{1,0:T(8,128)(2,1)S(1)}, bf16[48,1024]{1,0:T(8,128)(2,1)S(1)}, u32[]{:S(2)}, u32[]{:S(2)}) collective-permute-start(bf16[48,1024]{1,0:T(8,128)(2,1)S(1)} %get-tuple-element.23), channel_id=1, source_target_pairs={{0,8},{2,10},{4,12},{6,14},{8,0},{10,2},{12,4},{14,6},{1,9},{3,11}... | collective-permute-start | bytes 294920 | tf_op jit(solution)/shard_map/ppermute | solution.py:189
  102.9 6.8 %collective-permute-start.22 = (bf16[48,1024]{1,0:T(8,128)(2,1)S(1)}, bf16[48,1024]{1,0:T(8,128)(2,1)S(1)}, u32[]{:S(2)}, u32[]{:S(2)}) collective-permute-start(bf16[48,1024]{1,0:T(8,128)(2,1)S(1)} %get-tuple-element.25), channel_id=1, source_target_pairs={{0,4},{2,6},{4,8},{6,10},{8,12},{10,14},{12,0},{14,2},{1,5},{3,7},... | collective-permute-start | bytes 294920 | tf_op jit(solution)/shard_map/ppermute | solution.py:189
  105.6 4.2 %collective-permute-start.23 = (bf16[48,1024]{1,0:T(8,128)(2,1)S(1)}, bf16[48,1024]{1,0:T(8,128)(2,1)S(1)}, u32[]{:S(2)}, u32[]{:S(2)}) collective-permute-start(bf16[48,1024]{1,0:T(8,128)(2,1)S(1)} %get-tuple-element.20), channel_id=1, source_target_pairs={{0,2},{2,0},{4,6},{6,4},{8,10},{10,8},{12,14},{14,12},{1,3},{3,1},... | collective-permute-start | bytes 294920 | tf_op jit(solution)/shard_map/ppermute | solution.py:186
  105.7 6.0 %collective-permute-start.24 = (bf16[48,1024]{1,0:T(8,128)(2,1)S(1)}, bf16[48,1024]{1,0:T(8,128)(2,1)S(1)}, u32[]{:S(2)}, u32[]{:S(2)}) collective-permute-start(bf16[48,1024]{1,0:T(8,128)(2,1)S(1)} %get-tuple-element.22), channel_id=1, source_target_pairs={{0,14},{2,12},{4,2},{6,0},{8,6},{10,4},{12,10},{14,8},{1,15},{3,13... | collective-permute-start | bytes 294920 | tf_op jit(solution)/shard_map/ppermute | solution.py:191
  107.3 10.8 %collective-permute-start.25 = (bf16[48,1024]{1,0:T(8,128)(2,1)S(1)}, bf16[48,1024]{1,0:T(8,128)(2,1)S(1)}, u32[]{:S(2)}, u32[]{:S(2)}) collective-permute-start(bf16[48,1024]{1,0:T(8,128)(2,1)S(1)} %get-tuple-element.24), channel_id=1, source_target_pairs={{0,10},{2,8},{4,14},{6,12},{8,2},{10,0},{12,6},{14,4},{1,11},{3,9}... | collective-permute-start | bytes 294920 | tf_op jit(solution)/shard_map/ppermute | solution.py:191
  108.5 9.6 %collective-permute-start.26 = (bf16[48,1024]{1,0:T(8,128)(2,1)S(1)}, bf16[48,1024]{1,0:T(8,128)(2,1)S(1)}, u32[]{:S(2)}, u32[]{:S(2)}) collective-permute-start(bf16[48,1024]{1,0:T(8,128)(2,1)S(1)} %get-tuple-element.26), channel_id=1, source_target_pairs={{0,6},{2,4},{4,10},{6,8},{8,14},{10,12},{12,2},{14,0},{1,7},{3,5},... | collective-permute-start | bytes 294920 | tf_op jit(solution)/shard_map/ppermute | solution.py:191
  118.7 4.3 %collective-permute-start.27 = (bf16[32,1024]{1,0:T(8,128)(2,1)S(1)}, bf16[32,1024]{1,0:T(8,128)(2,1)S(1)}, u32[]{:S(2)}, u32[]{:S(2)}) collective-permute-start(bf16[32,1024]{1,0:T(8,128)(2,1)S(1)} %select_convert_fusion), channel_id=1, source_target_pairs={{0,1},{1,0},{2,3},{3,2},{4,5},{5,4},{6,7},{7,6},{8,9},{9,8},{10,11... | collective-permute-start | bytes 196616 | tf_op jit(solution)/shard_map/ppermute | solution.py:49
  (7 other events, 83.2 us)
Sparse Core Ops, SparseCore 0:
  15.4 28.1 all-gather.1

commit v21 on v19

--- a/solution.py
+++ b/solution.py
@@ -189,11 +189,10 @@
                 returned_partner[shift] = lax.ppermute(summed[idx][1], "ctx", perm=perm)
     served = jnp.stack([jnp.stack(returned), jnp.stack(returned_partner)])
     served = served.reshape(n_ctx * capacity, half_d)
-    moe_half = jnp.dot(
-        combine,
-        served.astype(jnp.float32),
-        precision=lax.Precision.HIGHEST,
-        preferred_element_type=jnp.float32,
+    weight_hi = combine.astype(jnp.bfloat16)
+    weight_lo = (combine - weight_hi.astype(jnp.float32)).astype(jnp.bfloat16)
+    moe_half = jnp.dot(weight_hi, served, preferred_element_type=jnp.float32) + jnp.dot(
+        weight_lo, served, preferred_element_type=jnp.float32
     )
     my_tok, other_tok = halves(moe_half, first, 0)
     got_tok = exp_swap(other_tok.astype(jnp.bfloat16)).astype(jnp.float32)

time: 129 us -> 130 us (level)
  no operation moved by 1% of the time
where the time goes in v21:
time: 130 us; the launch traced here: 129 us
  waiting for transfers between devices  59 us (45%)
  starting transfers between devices  32.1 us (25%)
  between operations  15.3 us (12%)
  matrix products  13.6 us (10%)
  other arithmetic  4.67 us (4%)
  local copies, waits for them, and re-layouts  4.44 us (3%)
    ppermute x10, waiting for transfers between devices, exp_swap(): return lax.ppermute(x, 'exp', perm=[(0, 1), (1, 0)])  19.5 us
    all_gather x1, waiting for transfers between devices, local(): lax.all_gather(out_weight, 'ctx', axis=0, tiled=True)  16.7 us
    ppermute x3, waiting for transfers between devices, moe_column_halves(): arrived.append(lax.ppermute(far_pairs[shift - 1], 'ctx', perm=perm))  10.4 us
    ppermute x10, starting transfers between devices, exp_swap(): return lax.ppermute(x, 'exp', perm=[(0, 1), (1, 0)])  9.21 us
    ppermute x3, waiting for transfers between devices, moe_column_halves(): returned_partner[shift] = lax.ppermute(summed[idx][1], 'ctx', perm=perm)  8.23 us
    ppermute x3, starting transfers between devices, ctx_gather_blocks(): stack.append(lax.ppermute(rows, 'ctx', perm=perm))  7.03 us
    ppermute x3, starting transfers between devices, moe_column_halves(): returned[shift] = lax.ppermute(summed[idx][0], 'ctx', perm=perm)  6.63 us
    ppermute x3, starting transfers between devices, moe_column_halves(): returned_partner[shift] = lax.ppermute(summed[idx][1], 'ctx', perm=perm)  4.39 us
  transfers between devices with their start and end apart: 27, of which 15 were waited for; matrix products, arithmetic and copies ran while one was open for 15% of the time, Pallas kernels for 0%

profile of v21, /device:TPU:0, one launch (start us, length us, event | category | flops | bytes accessed | tf_op | source)
XLA Modules:
  0.0 129.2 jit_solution(17101360315431538145)
XLA Ops:
  7.9 0.9 fusion.155
  8.8 3.1 %collective-permute-start.1 = (bf16[64,1024]{1,0:T(8,128)(2,1)S(1)}, bf16[64,1024]{1,0:T(8,128)(2,1)S(1)}, u32[]{:S(2)}, u32[]{:S(2)}) collective-permute-start(bf16[64,1024]{1,0:T(8,128)(2,1)S(1)} %get-tuple-element.27), channel_id=1, source_target_pairs={{0,4},{2,6},{4,8},{6,10},{8,12},{10,14},{12,0},{14,2},{1,5},{3,7},... | collective-permute-start | bytes 393224 | tf_op jit(solution)/shard_map/ppermute | solution.py:209
  11.9 2.6 %collective-permute-start.2 = (bf16[64,1024]{1,0:T(8,128)(2,1)S(1)}, bf16[64,1024]{1,0:T(8,128)(2,1)S(1)}, u32[]{:S(2)}, u32[]{:S(2)}) collective-permute-start(bf16[64,1024]{1,0:T(8,128)(2,1)S(1)} %get-tuple-element.27), channel_id=1, source_target_pairs={{0,8},{2,10},{4,12},{6,14},{8,0},{10,2},{12,4},{14,6},{1,9},{3,11}... | collective-permute-start | bytes 393224 | tf_op jit(solution)/shard_map/ppermute | solution.py:209
  14.5 1.4 %collective-permute-start.3 = (bf16[64,1024]{1,0:T(8,128)(2,1)S(1)}, bf16[64,1024]{1,0:T(8,128)(2,1)S(1)}, u32[]{:S(2)}, u32[]{:S(2)}) collective-permute-start(bf16[64,1024]{1,0:T(8,128)(2,1)S(1)} %get-tuple-element.27), channel_id=1, source_target_pairs={{0,12},{2,14},{4,0},{6,2},{8,4},{10,6},{12,8},{14,10},{1,13},{3,15... | collective-permute-start | bytes 393224 | tf_op jit(solution)/shard_map/ppermute | solution.py:209
  15.8 1.5 %collective-permute-start = (bf16[32,2048]{1,0:T(8,128)(2,1)}, bf16[32,2048]{1,0:T(8,128)(2,1)S(1)}, u32[]{:S(2)}, u32[]{:S(2)}) collective-permute-start(bf16[32,2048]{1,0:T(8,128)(2,1)} %bitcast.242), channel_id=1, source_target_pairs={{0,1},{1,0},{2,3},{3,2},{4,5},{5,4},{6,7},{7,6},{8,9},{9,8},{10,11... | collective-permute-start | bytes 393224 | tf_op jit(solution)/shard_map/ppermute | solution.py:49
  21.3 0.9 constant_dynamic-update-slice_fusion.4
  22.2 0.9 collective-permute-done.2
  23.3 1.8 %collective-permute-done.4 = bf16[4,64,1024]{2,1,0:T(8,128)(2,1)S(1)} collective-permute-done((bf16[4,64,1024]{2,1,0:T(8,128)(2,1)S(1)}, bf16[4,64,1024]{2,1,0:T(8,128)(2,1)S(1)}, u32[]{:S(2)}, u32[]{:S(2)}) %collective-permute-start.4) | collective-permute-done | bytes 524320 | tf_op jit(solution)/shard_map/ppermute | solution.py:211
  25.3 0.9 copy-done.3
  27.6 16.7 %all-gather.2.cloned.1.call-done = bf16[2048,512]{1,0:T(8,128)(2,1)} async-done(((bf16[256,512]{1,0:T(8,128)(2,1)}), bf16[2048,512]{1,0:T(8,128)(2,1)}) %all-gather.2.cloned.1.call-update) | async-done | bytes 2097168 | tf_op jit(solution)/shard_map/all_gather | solution.py:281
  44.2 2.3 %fusion.165 = (bf16[64,2048]{1,0:T(8,128)(2,1)S(1)}, f32[64,2048]{1,0:T(8,128)S(1)}) fusion(bf16[2048,512]{1,0:T(8,128)(2,1)} %all-gather.2.cloned.1.call-done, bf16[4,8,8,128]{3,2,1,0:T(8,128)(2,1)S(1)} %fusion.8), kind=kOutput, calls=%fused_computation.252 | convolution fusion | flops 134348800 | bytes 2949120 | tf_op jit(solution)/shard_map/tc,oc->to/dot_general | solution.py:278
  46.6 1.6 %collective-permute-start.5 = (bf16[64,2048]{1,0:T(8,128)(2,1)S(1)}, bf16[64,2048]{1,0:T(8,128)(2,1)S(1)}, u32[]{:S(2)}, u32[]{:S(2)}) collective-permute-start(bf16[64,2048]{1,0:T(8,128)(2,1)S(1)} %get-tuple-element.30), channel_id=1, source_target_pairs={{0,1},{1,0},{2,3},{3,2},{4,5},{5,4},{6,7},{7,6},{8,9},{9,8},{10,11... | collective-permute-start | bytes 786440 | tf_op jit(solution)/shard_map/ppermute | solution.py:49
  49.0 6.1 %collective-permute-done.5 = bf16[64,2048]{1,0:T(8,128)(2,1)S(1)} collective-permute-done((bf16[64,2048]{1,0:T(8,128)(2,1)S(1)}, bf16[64,2048]{1,0:T(8,128)(2,1)S(1)}, u32[]{:S(2)}, u32[]{:S(2)}) %collective-permute-start.5) | collective-permute-done | bytes 262176 | tf_op jit(solution)/shard_map/ppermute | solution.py:49
  58.8 1.6 %collective-permute-start.7 = (bf16[96,1024]{1,0:T(8,128)(2,1)S(1)}, bf16[96,1024]{1,0:T(8,128)(2,1)S(1)}, u32[]{:S(2)}, u32[]{:S(2)}) collective-permute-start(bf16[96,1024]{1,0:T(8,128)(2,1)S(1)} %convolution_convert_fusion.5), channel_id=1, source_target_pairs={{0,1},{1,0},{2,3},{3,2},{4,5},{5,4},{6,7},{7,6},{8,9},{9,8},{10,11... | collective-permute-start | bytes 589832 | tf_op jit(solution)/shard_map/ppermute | solution.py:49
  61.0 0.9 fusion.10
  61.9 0.9 fusion.9
  62.7 1.4 %collective-permute-start.13 = (bf16[2,48,1024]{2,1,0:T(8,128)(2,1)S(1)}, bf16[2,48,1024]{2,1,0:T(8,128)(2,1)S(1)}, u32[]{:S(2)}, u32[]{:S(2)}) collective-permute-start(bf16[2,48,1024]{2,1,0:T(8,128)(2,1)S(1)} %get-tuple-element.13), channel_id=1, source_target_pairs={{0,8},{2,10},{4,12},{6,14},{8,0},{10,2},{12,4},{14,6},{1,9},{3,11}... | collective-permute-start | bytes 589832 | tf_op jit(solution)/shard_map/ppermute | solution.py:147
  64.1 2.2 %collective-permute-start.17 = (bf16[2,48,1024]{2,1,0:T(8,128)(2,1)S(1)}, bf16[2,48,1024]{2,1,0:T(8,128)(2,1)S(1)}, u32[]{:S(2)}, u32[]{:S(2)}) collective-permute-start(bf16[2,48,1024]{2,1,0:T(8,128)(2,1)S(1)} %get-tuple-element.12), channel_id=1, source_target_pairs={{0,12},{2,14},{4,0},{6,2},{8,4},{10,6},{12,8},{14,10},{1,13},{3,15... | collective-permute-start | bytes 589832 | tf_op jit(solution)/shard_map/ppermute | solution.py:147
  66.3 3.9 %collective-permute-done.9 = bf16[2,48,1024]{2,1,0:T(8,128)(2,1)S(1)} collective-permute-done((bf16[2,48,1024]{2,1,0:T(8,128)(2,1)S(1)}, bf16[2,48,1024]{2,1,0:T(8,128)(2,1)S(1)}, u32[]{:S(2)}, u32[]{:S(2)}) %collective-permute-start.9) | collective-permute-done | bytes 196640 | tf_op jit(solution)/shard_map/ppermute | solution.py:147
  71.0 6.5 %collective-permute-done.13 = bf16[2,48,1024]{2,1,0:T(8,128)(2,1)S(1)} collective-permute-done((bf16[2,48,1024]{2,1,0:T(8,128)(2,1)S(1)}, bf16[2,48,1024]{2,1,0:T(8,128)(2,1)S(1)}, u32[]{:S(2)}, u32[]{:S(2)}) %collective-permute-start.13) | collective-permute-done | bytes 196640 | tf_op jit(solution)/shard_map/ppermute | solution.py:147
  78.0 1.5 %collective-permute-start.18 = (bf16[96,1024]{1,0:T(8,128)(2,1)S(1)}, bf16[96,1024]{1,0:T(8,128)(2,1)S(1)}, u32[]{:S(2)}, u32[]{:S(2)}) collective-permute-start(bf16[96,1024]{1,0:T(8,128)(2,1)S(1)} %bitcast.233), channel_id=1, source_target_pairs={{0,1},{1,0},{2,3},{3,2},{4,5},{5,4},{6,7},{7,6},{8,9},{9,8},{10,11... | collective-permute-start | bytes 589832 | tf_op jit(solution)/shard_map/ppermute | solution.py:49
  81.9 3.4 %collective-permute-done.14 = bf16[96,1024]{1,0:T(8,128)(2,1)S(1)} collective-permute-done((bf16[96,1024]{1,0:T(8,128)(2,1)S(1)}, bf16[96,1024]{1,0:T(8,128)(2,1)S(1)}, u32[]{:S(2)}, u32[]{:S(2)}) %collective-permute-start.14) | collective-permute-done | bytes 196640 | tf_op jit(solution)/shard_map/ppermute | solution.py:49
  87.6 1.9 %collective-permute-done.18 = bf16[96,1024]{1,0:T(8,128)(2,1)S(1)} collective-permute-done((bf16[96,1024]{1,0:T(8,128)(2,1)S(1)}, bf16[96,1024]{1,0:T(8,128)(2,1)S(1)}, u32[]{:S(2)}, u32[]{:S(2)}) %collective-permute-start.18) | collective-permute-done | bytes 196640 | tf_op jit(solution)/shard_map/ppermute | solution.py:49
  91.8 1.9 %collective-permute-done.11 = bf16[96,1024]{1,0:T(8,128)(2,1)S(1)} collective-permute-done((bf16[96,1024]{1,0:T(8,128)(2,1)S(1)}, bf16[96,1024]{1,0:T(8,128)(2,1)S(1)}, u32[]{:S(2)}, u32[]{:S(2)}) %collective-permute-start.11) | collective-permute-done | bytes 196640 | tf_op jit(solution)/shard_map/ppermute | solution.py:49
  94.0 4.4 %collective-permute-start.12 = (bf16[48,1024]{1,0:T(8,128)(2,1)S(1)}, bf16[48,1024]{1,0:T(8,128)(2,1)S(1)}, u32[]{:S(2)}, u32[]{:S(2)}) collective-permute-start(bf16[48,1024]{1,0:T(8,128)(2,1)S(1)} %get-tuple-element.20), channel_id=1, source_target_pairs={{0,12},{2,14},{4,0},{6,2},{8,4},{10,6},{12,8},{14,10},{1,13},{3,15... | collective-permute-start | bytes 294920 | tf_op jit(solution)/shard_map/ppermute | solution.py:187
  98.8 2.3 %collective-permute-done.19 = bf16[96,1024]{1,0:T(8,128)(2,1)S(1)} collective-permute-done((bf16[96,1024]{1,0:T(8,128)(2,1)S(1)}, bf16[96,1024]{1,0:T(8,128)(2,1)S(1)}, u32[]{:S(2)}, u32[]{:S(2)}) %collective-permute-start.19) | collective-permute-done | bytes 196640 | tf_op jit(solution)/shard_map/ppermute | solution.py:49
  101.4 2.2 %collective-permute-start.20 = (bf16[48,1024]{1,0:T(8,128)(2,1)S(1)}, bf16[48,1024]{1,0:T(8,128)(2,1)S(1)}, u32[]{:S(2)}, u32[]{:S(2)}) collective-permute-start(bf16[48,1024]{1,0:T(8,128)(2,1)S(1)} %get-tuple-element.24), channel_id=1, source_target_pairs={{0,4},{2,6},{4,8},{6,10},{8,12},{10,14},{12,0},{14,2},{1,5},{3,7},... | collective-permute-start | bytes 294920 | tf_op jit(solution)/shard_map/ppermute | solution.py:187
  103.7 2.1 %collective-permute-start.22 = (bf16[48,1024]{1,0:T(8,128)(2,1)S(1)}, bf16[48,1024]{1,0:T(8,128)(2,1)S(1)}, u32[]{:S(2)}, u32[]{:S(2)}) collective-permute-start(bf16[48,1024]{1,0:T(8,128)(2,1)S(1)} %get-tuple-element.21), channel_id=1, source_target_pairs={{0,14},{2,12},{4,2},{6,0},{8,6},{10,4},{12,10},{14,8},{1,15},{3,13... | collective-permute-start | bytes 294920 | tf_op jit(solution)/shard_map/ppermute | solution.py:189
  106.4 1.7 %collective-permute-start.24 = (bf16[48,1024]{1,0:T(8,128)(2,1)S(1)}, bf16[48,1024]{1,0:T(8,128)(2,1)S(1)}, u32[]{:S(2)}, u32[]{:S(2)}) collective-permute-start(bf16[48,1024]{1,0:T(8,128)(2,1)S(1)} %get-tuple-element.25), channel_id=1, source_target_pairs={{0,6},{2,4},{4,10},{6,8},{8,14},{10,12},{12,2},{14,0},{1,7},{3,5},... | collective-permute-start | bytes 294920 | tf_op jit(solution)/shard_map/ppermute | solution.py:189
  108.4 1.0 collective-permute-done.22
  109.4 7.2 %collective-permute-done.23 = bf16[48,1024]{1,0:T(8,128)(2,1)S(1)} collective-permute-done((bf16[48,1024]{1,0:T(8,128)(2,1)S(1)}, bf16[48,1024]{1,0:T(8,128)(2,1)S(1)}, u32[]{:S(2)}, u32[]{:S(2)}) %collective-permute-start.23) | collective-permute-done | bytes 98336 | tf_op jit(solution)/shard_map/ppermute | solution.py:189
  117.7 4.0 %collective-permute-done.25 = bf16[32,1024]{1,0:T(8,128)(2,1)S(1)} collective-permute-done((bf16[32,1024]{1,0:T(8,128)(2,1)S(1)}, bf16[32,1024]{1,0:T(8,128)(2,1)S(1)}, u32[]{:S(2)}, u32[]{:S(2)}) %collective-permute-start.25) | collective-permute-done | bytes 65568 | tf_op jit(solution)/shard_map/ppermute | solution.py:49
  (126 shorter events, 22.4 us)
Async XLA Ops:
  7.2 51.3 %copy-start = (bf16[1,352,2048]{2,1,0:T(8,128)(2,1)S(1)}, bf16[1,352,2048]{2,1,0:T(8,128)(2,1)}, u32[]{:S(2)}) copy-start(bf16[1,352,2048]{2,1,0:T(8,128)(2,1)} %param.20) | copy-start | bytes 4325380
  7.2 37.1 %all-gather.2.cloned.1.call-start = ((), (), s32[]{:S(2)}) async-start(), calls=%async_computation | async-start | bytes 2359296 | tf_op jit(solution)/shard_map/all_gather | solution.py:281
  8.8 13.4 %collective-permute-start.1 = (bf16[64,1024]{1,0:T(8,128)(2,1)S(1)}, bf16[64,1024]{1,0:T(8,128)(2,1)S(1)}, u32[]{:S(2)}, u32[]{:S(2)}) collective-permute-start(bf16[64,1024]{1,0:T(8,128)(2,1)S(1)} %get-tuple-element.27), channel_id=1, source_target_pairs={{0,4},{2,6},{4,8},{6,10},{8,12},{10,14},{12,0},{14,2},{1,5},{3,7},... | collective-permute-start | bytes 393224 | tf_op jit(solution)/shard_map/ppermute | solution.py:209
  11.9 11.2 %collective-permute-start.2 = (bf16[64,1024]{1,0:T(8,128)(2,1)S(1)}, bf16[64,1024]{1,0:T(8,128)(2,1)S(1)}, u32[]{:S(2)}, u32[]{:S(2)}) collective-permute-start(bf16[64,1024]{1,0:T(8,128)(2,1)S(1)} %get-tuple-element.27), channel_id=1, source_target_pairs={{0,8},{2,10},{4,12},{6,14},{8,0},{10,2},{12,4},{14,6},{1,9},{3,11}... | collective-permute-start | bytes 393224 | tf_op jit(solution)/shard_map/ppermute | solution.py:209
  14.5 8.6 %collective-permute-start.3 = (bf16[64,1024]{1,0:T(8,128)(2,1)S(1)}, bf16[64,1024]{1,0:T(8,128)(2,1)S(1)}, u32[]{:S(2)}, u32[]{:S(2)}) collective-permute-start(bf16[64,1024]{1,0:T(8,128)(2,1)S(1)} %get-tuple-element.27), channel_id=1, source_target_pairs={{0,12},{2,14},{4,0},{6,2},{8,4},{10,6},{12,8},{14,10},{1,13},{3,15... | collective-permute-start | bytes 393224 | tf_op jit(solution)/shard_map/ppermute | solution.py:209
  15.8 33.2 %collective-permute-start = (bf16[32,2048]{1,0:T(8,128)(2,1)}, bf16[32,2048]{1,0:T(8,128)(2,1)S(1)}, u32[]{:S(2)}, u32[]{:S(2)}) collective-permute-start(bf16[32,2048]{1,0:T(8,128)(2,1)} %bitcast.242), channel_id=1, source_target_pairs={{0,1},{1,0},{2,3},{3,2},{4,5},{5,4},{6,7},{7,6},{8,9},{9,8},{10,11... | collective-permute-start | bytes 393224 | tf_op jit(solution)/shard_map/ppermute | solution.py:49
  23.2 2.0 %collective-permute-start.4 = (bf16[4,64,1024]{2,1,0:T(8,128)(2,1)S(1)}, bf16[4,64,1024]{2,1,0:T(8,128)(2,1)S(1)}, u32[]{:S(2)}, u32[]{:S(2)}) collective-permute-start(bf16[4,64,1024]{2,1,0:T(8,128)(2,1)S(1)} %pad_maximum_fusion.1), channel_id=1, source_target_pairs={{0,2},{2,0},{4,6},{6,4},{8,10},{10,8},{12,14},{14,12},{1,3},{3,1},... | collective-permute-start | bytes 1572872 | tf_op jit(solution)/shard_map/ppermute | solution.py:211
  27.5 20.8 %copy-start.7 = (f32[1,64,4]{1,2,0:T(4,128)S(1)}, f32[1,64,4]{1,2,0:T(4,128)}, u32[]{:S(2)}) copy-start(f32[1,64,4]{1,2,0:T(4,128)} %param.22) | copy-start | bytes 3076
  27.6 27.5 %copy-start.5 = (bf16[1,32,2048]{2,1,0:T(8,128)(2,1)S(1)}, bf16[1,32,2048]{2,1,0:T(8,128)(2,1)}, u32[]{:S(2)}) copy-start(bf16[1,32,2048]{2,1,0:T(8,128)(2,1)} %param.15) | copy-start | bytes 393220
  46.6 8.8 %copy-start.6 = (f32[2048]{0:T(1024)S(1)}, f32[2048]{0:T(1024)}, u32[]{:S(2)}) copy-start(f32[2048]{0:T(1024)} %param.17) | copy-start | bytes 24580
  46.6 8.5 %collective-permute-start.5 = (bf16[64,2048]{1,0:T(8,128)(2,1)S(1)}, bf16[64,2048]{1,0:T(8,128)(2,1)S(1)}, u32[]{:S(2)}, u32[]{:S(2)}) collective-permute-start(bf16[64,2048]{1,0:T(8,128)(2,1)S(1)} %get-tuple-element.30), channel_id=1, source_target_pairs={{0,1},{1,0},{2,3},{3,2},{4,5},{5,4},{6,7},{7,6},{8,9},{9,8},{10,11... | collective-permute-start | bytes 786440 | tf_op jit(solution)/shard_map/ppermute | solution.py:49
  55.8 1.5 %collective-permute-start.6 = (bf16[48,2048]{1,0:T(8,128)(2,1)S(1)}, bf16[48,2048]{1,0:T(8,128)(2,1)S(1)}, u32[]{:S(2)}, u32[]{:S(2)}) collective-permute-start(bf16[48,2048]{1,0:T(8,128)(2,1)S(1)} %get-tuple-element.17), channel_id=1, source_target_pairs={{0,2},{2,0},{4,6},{6,4},{8,10},{10,8},{12,14},{14,12},{1,3},{3,1},... | collective-permute-start | bytes 589832 | tf_op jit(solution)/shard_map/ppermute | solution.py:141
  56.2 4.2 %collective-permute-start.8 = (bf16[3,48,1024]{2,1,0:T(8,128)(2,1)S(1)}, bf16[3,48,1024]{2,1,0:T(8,128)(2,1)S(1)}, u32[]{:S(2)}, u32[]{:S(2)}) collective-permute-start(bf16[3,48,1024]{2,1,0:T(8,128)(2,1)S(1)} %bitcast.228), channel_id=1, source_target_pairs={{0,2},{2,0},{4,6},{6,4},{8,10},{10,8},{12,14},{14,12},{1,3},{3,1},... | collective-permute-start | bytes 884744 | tf_op jit(solution)/shard_map/ppermute | solution.py:143
  58.5 2.5 %copy-start.4 = (bf16[8,64,1024]{2,1,0:T(8,128)(2,1)S(1)}, bf16[8,64,1024]{2,1,0:T(8,128)(2,1)}, u32[]{:S(2)}) copy-start(bf16[8,64,1024]{2,1,0:T(8,128)(2,1)} %copy-done.3) | copy-start | bytes 3145732
  58.8 11.9 %collective-permute-start.7 = (bf16[96,1024]{1,0:T(8,128)(2,1)S(1)}, bf16[96,1024]{1,0:T(8,128)(2,1)S(1)}, u32[]{:S(2)}, u32[]{:S(2)}) collective-permute-start(bf16[96,1024]{1,0:T(8,128)(2,1)S(1)} %convolution_convert_fusion.5), channel_id=1, source_target_pairs={{0,1},{1,0},{2,3},{3,2},{4,5},{5,4},{6,7},{7,6},{8,9},{9,8},{10,11... | collective-permute-start | bytes 589832 | tf_op jit(solution)/shard_map/ppermute | solution.py:49
  60.4 9.7 %collective-permute-start.9 = (bf16[2,48,1024]{2,1,0:T(8,128)(2,1)S(1)}, bf16[2,48,1024]{2,1,0:T(8,128)(2,1)S(1)}, u32[]{:S(2)}, u32[]{:S(2)}) collective-permute-start(bf16[2,48,1024]{2,1,0:T(8,128)(2,1)S(1)} %get-tuple-element.11), channel_id=1, source_target_pairs={{0,4},{2,6},{4,8},{6,10},{8,12},{10,14},{12,0},{14,2},{1,5},{3,7},... | collective-permute-start | bytes 589832 | tf_op jit(solution)/shard_map/ppermute | solution.py:147
  62.7 14.7 %collective-permute-start.13 = (bf16[2,48,1024]{2,1,0:T(8,128)(2,1)S(1)}, bf16[2,48,1024]{2,1,0:T(8,128)(2,1)S(1)}, u32[]{:S(2)}, u32[]{:S(2)}) collective-permute-start(bf16[2,48,1024]{2,1,0:T(8,128)(2,1)S(1)} %get-tuple-element.13), channel_id=1, source_target_pairs={{0,8},{2,10},{4,12},{6,14},{8,0},{10,2},{12,4},{14,6},{1,9},{3,11}... | collective-permute-start | bytes 589832 | tf_op jit(solution)/shard_map/ppermute | solution.py:147
  64.1 13.9 %collective-permute-start.17 = (bf16[2,48,1024]{2,1,0:T(8,128)(2,1)S(1)}, bf16[2,48,1024]{2,1,0:T(8,128)(2,1)S(1)}, u32[]{:S(2)}, u32[]{:S(2)}) collective-permute-start(bf16[2,48,1024]{2,1,0:T(8,128)(2,1)S(1)} %get-tuple-element.12), channel_id=1, source_target_pairs={{0,12},{2,14},{4,0},{6,2},{8,4},{10,6},{12,8},{14,10},{1,13},{3,15... | collective-permute-start | bytes 589832 | tf_op jit(solution)/shard_map/ppermute | solution.py:147
  70.2 9.3 %collective-permute-start.10 = (bf16[96,1024]{1,0:T(8,128)(2,1)S(1)}, bf16[96,1024]{1,0:T(8,128)(2,1)S(1)}, u32[]{:S(2)}, u32[]{:S(2)}) collective-permute-start(bf16[96,1024]{1,0:T(8,128)(2,1)S(1)} %bitcast.239), channel_id=1, source_target_pairs={{0,1},{1,0},{2,3},{3,2},{4,5},{5,4},{6,7},{7,6},{8,9},{9,8},{10,11... | collective-permute-start | bytes 589832 | tf_op jit(solution)/shard_map/ppermute | solution.py:49
  77.5 7.8 %collective-permute-start.14 = (bf16[96,1024]{1,0:T(8,128)(2,1)S(1)}, bf16[96,1024]{1,0:T(8,128)(2,1)S(1)}, u32[]{:S(2)}, u32[]{:S(2)}) collective-permute-start(bf16[96,1024]{1,0:T(8,128)(2,1)S(1)} %bitcast.236), channel_id=1, source_target_pairs={{0,1},{1,0},{2,3},{3,2},{4,5},{5,4},{6,7},{7,6},{8,9},{9,8},{10,11... | collective-permute-start | bytes 589832 | tf_op jit(solution)/shard_map/ppermute | solution.py:49
  78.0 11.5 %collective-permute-start.18 = (bf16[96,1024]{1,0:T(8,128)(2,1)S(1)}, bf16[96,1024]{1,0:T(8,128)(2,1)S(1)}, u32[]{:S(2)}, u32[]{:S(2)}) collective-permute-start(bf16[96,1024]{1,0:T(8,128)(2,1)S(1)} %bitcast.233), channel_id=1, source_target_pairs={{0,1},{1,0},{2,3},{3,2},{4,5},{5,4},{6,7},{7,6},{8,9},{9,8},{10,11... | collective-permute-start | bytes 589832 | tf_op jit(solution)/shard_map/ppermute | solution.py:49
  81.3 12.4 %collective-permute-start.11 = (bf16[96,1024]{1,0:T(8,128)(2,1)S(1)}, bf16[96,1024]{1,0:T(8,128)(2,1)S(1)}, u32[]{:S(2)}, u32[]{:S(2)}) collective-permute-start(bf16[96,1024]{1,0:T(8,128)(2,1)S(1)} %convolution_convert_fusion.4), channel_id=1, source_target_pairs={{0,1},{1,0},{2,3},{3,2},{4,5},{5,4},{6,7},{7,6},{8,9},{9,8},{10,11... | collective-permute-start | bytes 589832 | tf_op jit(solution)/shard_map/ppermute | solution.py:49
  87.0 11.4 %collective-permute-start.15 = (bf16[96,1024]{1,0:T(8,128)(2,1)S(1)}, bf16[96,1024]{1,0:T(8,128)(2,1)S(1)}, u32[]{:S(2)}, u32[]{:S(2)}) collective-permute-start(bf16[96,1024]{1,0:T(8,128)(2,1)S(1)} %convolution_convert_fusion.3), channel_id=1, source_target_pairs={{0,1},{1,0},{2,3},{3,2},{4,5},{5,4},{6,7},{7,6},{8,9},{9,8},{10,11... | collective-permute-start | bytes 589832 | tf_op jit(solution)/shard_map/ppermute | solution.py:49
  91.3 9.8 %collective-permute-start.19 = (bf16[96,1024]{1,0:T(8,128)(2,1)S(1)}, bf16[96,1024]{1,0:T(8,128)(2,1)S(1)}, u32[]{:S(2)}, u32[]{:S(2)}) collective-permute-start(bf16[96,1024]{1,0:T(8,128)(2,1)S(1)} %convolution_convert_fusion.2), channel_id=1, source_target_pairs={{0,1},{1,0},{2,3},{3,2},{4,5},{5,4},{6,7},{7,6},{8,9},{9,8},{10,11... | collective-permute-start | bytes 589832 | tf_op jit(solution)/shard_map/ppermute | solution.py:49
  94.0 11.8 %collective-permute-start.12 = (bf16[48,1024]{1,0:T(8,128)(2,1)S(1)}, bf16[48,1024]{1,0:T(8,128)(2,1)S(1)}, u32[]{:S(2)}, u32[]{:S(2)}) collective-permute-start(bf16[48,1024]{1,0:T(8,128)(2,1)S(1)} %get-tuple-element.20), channel_id=1, source_target_pairs={{0,12},{2,14},{4,0},{6,2},{8,4},{10,6},{12,8},{14,10},{1,13},{3,15... | collective-permute-start | bytes 294920 | tf_op jit(solution)/shard_map/ppermute | solution.py:187
  98.7 7.7 %collective-permute-start.16 = (bf16[48,1024]{1,0:T(8,128)(2,1)S(1)}, bf16[48,1024]{1,0:T(8,128)(2,1)S(1)}, u32[]{:S(2)}, u32[]{:S(2)}) collective-permute-start(bf16[48,1024]{1,0:T(8,128)(2,1)S(1)} %get-tuple-element.22), channel_id=1, source_target_pairs={{0,8},{2,10},{4,12},{6,14},{8,0},{10,2},{12,4},{14,6},{1,9},{3,11}... | collective-permute-start | bytes 294920 | tf_op jit(solution)/shard_map/ppermute | solution.py:187
  101.4 6.9 %collective-permute-start.20 = (bf16[48,1024]{1,0:T(8,128)(2,1)S(1)}, bf16[48,1024]{1,0:T(8,128)(2,1)S(1)}, u32[]{:S(2)}, u32[]{:S(2)}) collective-permute-start(bf16[48,1024]{1,0:T(8,128)(2,1)S(1)} %get-tuple-element.24), channel_id=1, source_target_pairs={{0,4},{2,6},{4,8},{6,10},{8,12},{10,14},{12,0},{14,2},{1,5},{3,7},... | collective-permute-start | bytes 294920 | tf_op jit(solution)/shard_map/ppermute | solution.py:187
  103.6 4.8 %collective-permute-start.21 = (bf16[48,1024]{1,0:T(8,128)(2,1)S(1)}, bf16[48,1024]{1,0:T(8,128)(2,1)S(1)}, u32[]{:S(2)}, u32[]{:S(2)}) collective-permute-start(bf16[48,1024]{1,0:T(8,128)(2,1)S(1)} %get-tuple-element.19), channel_id=1, source_target_pairs={{0,2},{2,0},{4,6},{6,4},{8,10},{10,8},{12,14},{14,12},{1,3},{3,1},... | collective-permute-start | bytes 294920 | tf_op jit(solution)/shard_map/ppermute | solution.py:184
  103.7 5.7 %collective-permute-start.22 = (bf16[48,1024]{1,0:T(8,128)(2,1)S(1)}, bf16[48,1024]{1,0:T(8,128)(2,1)S(1)}, u32[]{:S(2)}, u32[]{:S(2)}) collective-permute-start(bf16[48,1024]{1,0:T(8,128)(2,1)S(1)} %get-tuple-element.21), channel_id=1, source_target_pairs={{0,14},{2,12},{4,2},{6,0},{8,6},{10,4},{12,10},{14,8},{1,15},{3,13... | collective-permute-start | bytes 294920 | tf_op jit(solution)/shard_map/ppermute | solution.py:189
  105.8 10.8 %collective-permute-start.23 = (bf16[48,1024]{1,0:T(8,128)(2,1)S(1)}, bf16[48,1024]{1,0:T(8,128)(2,1)S(1)}, u32[]{:S(2)}, u32[]{:S(2)}) collective-permute-start(bf16[48,1024]{1,0:T(8,128)(2,1)S(1)} %get-tuple-element.23), channel_id=1, source_target_pairs={{0,10},{2,8},{4,14},{6,12},{8,2},{10,0},{12,6},{14,4},{1,11},{3,9}... | collective-permute-start | bytes 294920 | tf_op jit(solution)/shard_map/ppermute | solution.py:189
  106.4 10.2 %collective-permute-start.24 = (bf16[48,1024]{1,0:T(8,128)(2,1)S(1)}, bf16[48,1024]{1,0:T(8,128)(2,1)S(1)}, u32[]{:S(2)}, u32[]{:S(2)}) collective-permute-start(bf16[48,1024]{1,0:T(8,128)(2,1)S(1)} %get-tuple-element.25), channel_id=1, source_target_pairs={{0,6},{2,4},{4,10},{6,8},{8,14},{10,12},{12,2},{14,0},{1,7},{3,5},... | collective-permute-start | bytes 294920 | tf_op jit(solution)/shard_map/ppermute | solution.py:189
  117.3 4.3 %collective-permute-start.25 = (bf16[32,1024]{1,0:T(8,128)(2,1)S(1)}, bf16[32,1024]{1,0:T(8,128)(2,1)S(1)}, u32[]{:S(2)}, u32[]{:S(2)}) collective-permute-start(bf16[32,1024]{1,0:T(8,128)(2,1)S(1)} %select_convert_fusion), channel_id=1, source_target_pairs={{0,1},{1,0},{2,3},{3,2},{4,5},{5,4},{6,7},{7,6},{8,9},{9,8},{10,11... | collective-permute-start | bytes 196616 | tf_op jit(solution)/shard_map/ppermute | solution.py:49
  (3 other events, 4.3 us)
Sparse Core Ops, SparseCore 0:
  9.6 34.5 all-gather.1

commit v22 on v21

--- a/solution.py
+++ b/solution.py
@@ -283,8 +283,10 @@
     )
     if lax.axis_size("exp") == 2:
         first_exp = lax.axis_index("exp") == 0
-        residual_all = join(residual[0], exp_swap(residual[0]), first_exp, 0)
-        head_all = out_parts + exp_swap(out_parts.astype(jnp.bfloat16)).astype(jnp.float32)
+        sent = jnp.concatenate([out_parts.astype(jnp.bfloat16), residual[0]], axis=0)
+        got = exp_swap(sent)
+        residual_all = join(residual[0], got[out_parts.shape[0]:], first_exp, 0)
+        head_all = out_parts + got[: out_parts.shape[0]].astype(jnp.float32)
         stream_all = (residual_all.astype(jnp.float32) + head_all).astype(jnp.bfloat16)
         stream = halves(stream_all, first_exp, 0)[0]
         stream_f = stream_all.astype(jnp.float32)

time: 130 us -> 132 us (1.015)
  waiting for transfers between devices: 59 us -> 64.1 us
  starting transfers between devices: 32.1 us -> 29.4 us
    ppermute x10 -> x9, waiting for transfers between devices: 19.5 us -> 22.4 us  [exp_swap(): return lax.ppermute(x, 'exp', perm=[(0, 1), (1, 0)])]
    ppermute x3, waiting for transfers between devices: 0.9 us -> 2.34 us  [ctx_gather_blocks(): stack.append(lax.ppermute(rows, 'ctx', perm=perm))]
    ppermute x10 -> x9, starting transfers between devices: 9.21 us -> 7.94 us  [exp_swap(): return lax.ppermute(x, 'exp', perm=[(0, 1), (1, 0)])]
  transfers between devices with their start and end apart: 27 -> 26, of which waited for: 15 -> 16; matrix products, arithmetic and copies ran while one was open for 15% -> 13% of each run, Pallas kernels for 0% -> 0%
where the time goes in v22:
time: 132 us
  waiting for transfers between devices  64.1 us (49%)
  starting transfers between devices  29.4 us (22%)
  between operations  15.3 us (12%)
  matrix products  13.6 us (10%)
  other arithmetic  4.76 us (4%)
  local copies, waits for them, and re-layouts  4.47 us (3%)
    ppermute x9, waiting for transfers between devices, exp_swap(): return lax.ppermute(x, 'exp', perm=[(0, 1), (1, 0)])  22.4 us
    all_gather x1, waiting for transfers between devices, local(): lax.all_gather(out_weight, 'ctx', axis=0, tiled=True)  16.7 us
    ppermute x3, waiting for transfers between devices, moe_column_halves(): arrived.append(lax.ppermute(far_pairs[shift - 1], 'ctx', perm=perm))  10.6 us
    ppermute x3, waiting for transfers between devices, moe_column_halves(): returned_partner[shift] = lax.ppermute(summed[idx][1], 'ctx', perm=perm)  8.2 us
    ppermute x9, starting transfers between devices, exp_swap(): return lax.ppermute(x, 'exp', perm=[(0, 1), (1, 0)])  7.94 us
    ppermute x3, starting transfers between devices, ctx_gather_blocks(): stack.append(lax.ppermute(rows, 'ctx', perm=perm))  7.03 us
    ppermute x3, starting transfers between devices, moe_column_halves(): returned[shift] = lax.ppermute(summed[idx][0], 'ctx', perm=perm)  5.98 us
    ppermute x3, starting transfers between devices, moe_column_halves(): arrived.append(lax.ppermute(far_pairs[shift - 1], 'ctx', perm=perm))  3.86 us
  transfers between devices with their start and end apart: 26, of which 16 were waited for; matrix products, arithmetic and copies ran while one was open for 13% of the time, Pallas kernels for 0%

profile of v22, /device:TPU:0, one launch (start us, length us, event | category | flops | bytes accessed | tf_op | source)
XLA Modules:
  0.0 131.7 jit_solution(3652406276796059656)
XLA Ops:
  7.9 0.9 fusion.155
  8.8 3.1 %collective-permute-start = (bf16[64,1024]{1,0:T(8,128)(2,1)S(1)}, bf16[64,1024]{1,0:T(8,128)(2,1)S(1)}, u32[]{:S(2)}, u32[]{:S(2)}) collective-permute-start(bf16[64,1024]{1,0:T(8,128)(2,1)S(1)} %get-tuple-element.27), channel_id=1, source_target_pairs={{0,4},{2,6},{4,8},{6,10},{8,12},{10,14},{12,0},{14,2},{1,5},{3,7},... | collective-permute-start | bytes 393224 | tf_op jit(solution)/shard_map/ppermute | solution.py:209
  11.9 2.6 %collective-permute-start.1 = (bf16[64,1024]{1,0:T(8,128)(2,1)S(1)}, bf16[64,1024]{1,0:T(8,128)(2,1)S(1)}, u32[]{:S(2)}, u32[]{:S(2)}) collective-permute-start(bf16[64,1024]{1,0:T(8,128)(2,1)S(1)} %get-tuple-element.27), channel_id=1, source_target_pairs={{0,8},{2,10},{4,12},{6,14},{8,0},{10,2},{12,4},{14,6},{1,9},{3,11}... | collective-permute-start | bytes 393224 | tf_op jit(solution)/shard_map/ppermute | solution.py:209
  14.5 1.4 %collective-permute-start.2 = (bf16[64,1024]{1,0:T(8,128)(2,1)S(1)}, bf16[64,1024]{1,0:T(8,128)(2,1)S(1)}, u32[]{:S(2)}, u32[]{:S(2)}) collective-permute-start(bf16[64,1024]{1,0:T(8,128)(2,1)S(1)} %get-tuple-element.27), channel_id=1, source_target_pairs={{0,12},{2,14},{4,0},{6,2},{8,4},{10,6},{12,8},{14,10},{1,13},{3,15... | collective-permute-start | bytes 393224 | tf_op jit(solution)/shard_map/ppermute | solution.py:209
  18.9 0.9 reshape_squeeze.7
  19.8 0.9 constant_dynamic-update-slice_fusion.4
  20.8 2.3 %collective-permute-done.1 = bf16[64,1024]{1,0:T(8,128)(2,1)S(1)} collective-permute-done((bf16[64,1024]{1,0:T(8,128)(2,1)S(1)}, bf16[64,1024]{1,0:T(8,128)(2,1)S(1)}, u32[]{:S(2)}, u32[]{:S(2)}) %collective-permute-start.1) | collective-permute-done | bytes 131104 | tf_op jit(solution)/shard_map/ppermute | solution.py:209
  23.3 1.8 %collective-permute-done.3 = bf16[4,64,1024]{2,1,0:T(8,128)(2,1)S(1)} collective-permute-done((bf16[4,64,1024]{2,1,0:T(8,128)(2,1)S(1)}, bf16[4,64,1024]{2,1,0:T(8,128)(2,1)S(1)}, u32[]{:S(2)}, u32[]{:S(2)}) %collective-permute-start.3) | collective-permute-done | bytes 524320 | tf_op jit(solution)/shard_map/ppermute | solution.py:211
  25.3 0.9 copy-done.3
  27.6 16.7 %all-gather.2.cloned.1.call-done = bf16[2048,512]{1,0:T(8,128)(2,1)} async-done(((bf16[256,512]{1,0:T(8,128)(2,1)}), bf16[2048,512]{1,0:T(8,128)(2,1)}) %all-gather.2.cloned.1.call-update) | async-done | bytes 2097168 | tf_op jit(solution)/shard_map/all_gather | solution.py:281
  44.2 2.3 %fusion.165 = (bf16[64,2048]{1,0:T(8,128)(2,1)S(1)}, f32[64,2048]{1,0:T(8,128)S(1)}) fusion(bf16[2048,512]{1,0:T(8,128)(2,1)} %all-gather.2.cloned.1.call-done, bf16[4,8,8,128]{3,2,1,0:T(8,128)(2,1)S(1)} %fusion.8), kind=kOutput, calls=%fused_computation.253 | convolution fusion | flops 134348800 | bytes 2949120 | tf_op jit(solution)/shard_map/tc,oc->to/dot_general | solution.py:278
  46.6 1.6 %collective-permute-start.4 = (bf16[96,2048]{1,0:T(8,128)(2,1)S(1)}, bf16[96,2048]{1,0:T(8,128)(2,1)S(1)}, u32[]{:S(2)}, u32[]{:S(2)}) collective-permute-start(bf16[96,2048]{1,0:T(8,128)(2,1)S(1)} %pad_maximum_fusion.2), channel_id=1, source_target_pairs={{0,1},{1,0},{2,3},{3,2},{4,5},{5,4},{6,7},{7,6},{8,9},{9,8},{10,11... | collective-permute-start | bytes 1179656 | tf_op jit(solution)/shard_map/ppermute | solution.py:49
  49.0 8.9 %collective-permute-done.4 = bf16[96,2048]{1,0:T(8,128)(2,1)S(1)} collective-permute-done((bf16[96,2048]{1,0:T(8,128)(2,1)S(1)}, bf16[96,2048]{1,0:T(8,128)(2,1)S(1)}, u32[]{:S(2)}, u32[]{:S(2)}) %collective-permute-start.4) | collective-permute-done | bytes 393248 | tf_op jit(solution)/shard_map/ppermute | solution.py:49
  61.7 1.6 %collective-permute-start.6 = (bf16[96,1024]{1,0:T(8,128)(2,1)S(1)}, bf16[96,1024]{1,0:T(8,128)(2,1)S(1)}, u32[]{:S(2)}, u32[]{:S(2)}) collective-permute-start(bf16[96,1024]{1,0:T(8,128)(2,1)S(1)} %convolution_convert_fusion.5), channel_id=1, source_target_pairs={{0,1},{1,0},{2,3},{3,2},{4,5},{5,4},{6,7},{7,6},{8,9},{9,8},{10,11... | collective-permute-start | bytes 589832 | tf_op jit(solution)/shard_map/ppermute | solution.py:49
  63.4 0.9 fusion.10
  64.3 0.9 fusion.9
  65.1 2.2 %collective-permute-start.12 = (bf16[2,48,1024]{2,1,0:T(8,128)(2,1)S(1)}, bf16[2,48,1024]{2,1,0:T(8,128)(2,1)S(1)}, u32[]{:S(2)}, u32[]{:S(2)}) collective-permute-start(bf16[2,48,1024]{2,1,0:T(8,128)(2,1)S(1)} %get-tuple-element.13), channel_id=1, source_target_pairs={{0,8},{2,10},{4,12},{6,14},{8,0},{10,2},{12,4},{14,6},{1,9},{3,11}... | collective-permute-start | bytes 589832 | tf_op jit(solution)/shard_map/ppermute | solution.py:147
  67.3 1.6 %collective-permute-start.16 = (bf16[2,48,1024]{2,1,0:T(8,128)(2,1)S(1)}, bf16[2,48,1024]{2,1,0:T(8,128)(2,1)S(1)}, u32[]{:S(2)}, u32[]{:S(2)}) collective-permute-start(bf16[2,48,1024]{2,1,0:T(8,128)(2,1)S(1)} %get-tuple-element.12), channel_id=1, source_target_pairs={{0,12},{2,14},{4,0},{6,2},{8,4},{10,6},{12,8},{14,10},{1,13},{3,15... | collective-permute-start | bytes 589832 | tf_op jit(solution)/shard_map/ppermute | solution.py:147
  68.9 4.1 %collective-permute-done.8 = bf16[2,48,1024]{2,1,0:T(8,128)(2,1)S(1)} collective-permute-done((bf16[2,48,1024]{2,1,0:T(8,128)(2,1)S(1)}, bf16[2,48,1024]{2,1,0:T(8,128)(2,1)S(1)}, u32[]{:S(2)}, u32[]{:S(2)}) %collective-permute-start.8) | collective-permute-done | bytes 196640 | tf_op jit(solution)/shard_map/ppermute | solution.py:147
  73.8 6.5 %collective-permute-done.12 = bf16[2,48,1024]{2,1,0:T(8,128)(2,1)S(1)} collective-permute-done((bf16[2,48,1024]{2,1,0:T(8,128)(2,1)S(1)}, bf16[2,48,1024]{2,1,0:T(8,128)(2,1)S(1)}, u32[]{:S(2)}, u32[]{:S(2)}) %collective-permute-start.12) | collective-permute-done | bytes 196640 | tf_op jit(solution)/shard_map/ppermute | solution.py:147
  80.8 1.5 %collective-permute-start.17 = (bf16[96,1024]{1,0:T(8,128)(2,1)S(1)}, bf16[96,1024]{1,0:T(8,128)(2,1)S(1)}, u32[]{:S(2)}, u32[]{:S(2)}) collective-permute-start(bf16[96,1024]{1,0:T(8,128)(2,1)S(1)} %bitcast.235), channel_id=1, source_target_pairs={{0,1},{1,0},{2,3},{3,2},{4,5},{5,4},{6,7},{7,6},{8,9},{9,8},{10,11... | collective-permute-start | bytes 589832 | tf_op jit(solution)/shard_map/ppermute | solution.py:49
  84.7 3.4 %collective-permute-done.13 = bf16[96,1024]{1,0:T(8,128)(2,1)S(1)} collective-permute-done((bf16[96,1024]{1,0:T(8,128)(2,1)S(1)}, bf16[96,1024]{1,0:T(8,128)(2,1)S(1)}, u32[]{:S(2)}, u32[]{:S(2)}) %collective-permute-start.13) | collective-permute-done | bytes 196640 | tf_op jit(solution)/shard_map/ppermute | solution.py:49
  90.5 1.9 %collective-permute-done.17 = bf16[96,1024]{1,0:T(8,128)(2,1)S(1)} collective-permute-done((bf16[96,1024]{1,0:T(8,128)(2,1)S(1)}, bf16[96,1024]{1,0:T(8,128)(2,1)S(1)}, u32[]{:S(2)}, u32[]{:S(2)}) %collective-permute-start.17) | collective-permute-done | bytes 196640 | tf_op jit(solution)/shard_map/ppermute | solution.py:49
  94.7 1.9 %collective-permute-done.10 = bf16[96,1024]{1,0:T(8,128)(2,1)S(1)} collective-permute-done((bf16[96,1024]{1,0:T(8,128)(2,1)S(1)}, bf16[96,1024]{1,0:T(8,128)(2,1)S(1)}, u32[]{:S(2)}, u32[]{:S(2)}) %collective-permute-start.10) | collective-permute-done | bytes 196640 | tf_op jit(solution)/shard_map/ppermute | solution.py:49
  96.9 4.1 %collective-permute-start.11 = (bf16[48,1024]{1,0:T(8,128)(2,1)S(1)}, bf16[48,1024]{1,0:T(8,128)(2,1)S(1)}, u32[]{:S(2)}, u32[]{:S(2)}) collective-permute-start(bf16[48,1024]{1,0:T(8,128)(2,1)S(1)} %get-tuple-element.20), channel_id=1, source_target_pairs={{0,12},{2,14},{4,0},{6,2},{8,4},{10,6},{12,8},{14,10},{1,13},{3,15... | collective-permute-start | bytes 294920 | tf_op jit(solution)/shard_map/ppermute | solution.py:187
  101.3 2.6 %collective-permute-done.18 = bf16[96,1024]{1,0:T(8,128)(2,1)S(1)} collective-permute-done((bf16[96,1024]{1,0:T(8,128)(2,1)S(1)}, bf16[96,1024]{1,0:T(8,128)(2,1)S(1)}, u32[]{:S(2)}, u32[]{:S(2)}) %collective-permute-start.18) | collective-permute-done | bytes 196640 | tf_op jit(solution)/shard_map/ppermute | solution.py:49
  104.2 1.8 %collective-permute-start.19 = (bf16[48,1024]{1,0:T(8,128)(2,1)S(1)}, bf16[48,1024]{1,0:T(8,128)(2,1)S(1)}, u32[]{:S(2)}, u32[]{:S(2)}) collective-permute-start(bf16[48,1024]{1,0:T(8,128)(2,1)S(1)} %get-tuple-element.24), channel_id=1, source_target_pairs={{0,4},{2,6},{4,8},{6,10},{8,12},{10,14},{12,0},{14,2},{1,5},{3,7},... | collective-permute-start | bytes 294920 | tf_op jit(solution)/shard_map/ppermute | solution.py:187
  106.2 2.1 %collective-permute-start.21 = (bf16[48,1024]{1,0:T(8,128)(2,1)S(1)}, bf16[48,1024]{1,0:T(8,128)(2,1)S(1)}, u32[]{:S(2)}, u32[]{:S(2)}) collective-permute-start(bf16[48,1024]{1,0:T(8,128)(2,1)S(1)} %get-tuple-element.21), channel_id=1, source_target_pairs={{0,14},{2,12},{4,2},{6,0},{8,6},{10,4},{12,10},{14,8},{1,15},{3,13... | collective-permute-start | bytes 294920 | tf_op jit(solution)/shard_map/ppermute | solution.py:189
  108.9 1.4 %collective-permute-start.23 = (bf16[48,1024]{1,0:T(8,128)(2,1)S(1)}, bf16[48,1024]{1,0:T(8,128)(2,1)S(1)}, u32[]{:S(2)}, u32[]{:S(2)}) collective-permute-start(bf16[48,1024]{1,0:T(8,128)(2,1)S(1)} %get-tuple-element.25), channel_id=1, source_target_pairs={{0,6},{2,4},{4,10},{6,8},{8,14},{10,12},{12,2},{14,0},{1,7},{3,5},... | collective-permute-start | bytes 294920 | tf_op jit(solution)/shard_map/ppermute | solution.py:189
  110.9 1.0 collective-permute-done.21
  111.9 7.2 %collective-permute-done.22 = bf16[48,1024]{1,0:T(8,128)(2,1)S(1)} collective-permute-done((bf16[48,1024]{1,0:T(8,128)(2,1)S(1)}, bf16[48,1024]{1,0:T(8,128)(2,1)S(1)}, u32[]{:S(2)}, u32[]{:S(2)}) %collective-permute-start.22) | collective-permute-done | bytes 98336 | tf_op jit(solution)/shard_map/ppermute | solution.py:189
  120.4 3.7 %collective-permute-done.24 = bf16[32,1024]{1,0:T(8,128)(2,1)S(1)} collective-permute-done((bf16[32,1024]{1,0:T(8,128)(2,1)S(1)}, bf16[32,1024]{1,0:T(8,128)(2,1)S(1)}, u32[]{:S(2)}, u32[]{:S(2)}) %collective-permute-start.24) | collective-permute-done | bytes 65568 | tf_op jit(solution)/shard_map/ppermute | solution.py:49
  (126 shorter events, 21.7 us)
Async XLA Ops:
  7.2 54.2 %copy-start = (bf16[1,352,2048]{2,1,0:T(8,128)(2,1)S(1)}, bf16[1,352,2048]{2,1,0:T(8,128)(2,1)}, u32[]{:S(2)}) copy-start(bf16[1,352,2048]{2,1,0:T(8,128)(2,1)} %param.20) | copy-start | bytes 4325380
  7.2 37.1 %all-gather.2.cloned.1.call-start = ((), (), s32[]{:S(2)}) async-start(), calls=%async_computation | async-start | bytes 2359296 | tf_op jit(solution)/shard_map/all_gather | solution.py:281
  8.8 12.0 %collective-permute-start = (bf16[64,1024]{1,0:T(8,128)(2,1)S(1)}, bf16[64,1024]{1,0:T(8,128)(2,1)S(1)}, u32[]{:S(2)}, u32[]{:S(2)}) collective-permute-start(bf16[64,1024]{1,0:T(8,128)(2,1)S(1)} %get-tuple-element.27), channel_id=1, source_target_pairs={{0,4},{2,6},{4,8},{6,10},{8,12},{10,14},{12,0},{14,2},{1,5},{3,7},... | collective-permute-start | bytes 393224 | tf_op jit(solution)/shard_map/ppermute | solution.py:209
  11.9 11.2 %collective-permute-start.1 = (bf16[64,1024]{1,0:T(8,128)(2,1)S(1)}, bf16[64,1024]{1,0:T(8,128)(2,1)S(1)}, u32[]{:S(2)}, u32[]{:S(2)}) collective-permute-start(bf16[64,1024]{1,0:T(8,128)(2,1)S(1)} %get-tuple-element.27), channel_id=1, source_target_pairs={{0,8},{2,10},{4,12},{6,14},{8,0},{10,2},{12,4},{14,6},{1,9},{3,11}... | collective-permute-start | bytes 393224 | tf_op jit(solution)/shard_map/ppermute | solution.py:209
  14.5 8.6 %collective-permute-start.2 = (bf16[64,1024]{1,0:T(8,128)(2,1)S(1)}, bf16[64,1024]{1,0:T(8,128)(2,1)S(1)}, u32[]{:S(2)}, u32[]{:S(2)}) collective-permute-start(bf16[64,1024]{1,0:T(8,128)(2,1)S(1)} %get-tuple-element.27), channel_id=1, source_target_pairs={{0,12},{2,14},{4,0},{6,2},{8,4},{10,6},{12,8},{14,10},{1,13},{3,15... | collective-permute-start | bytes 393224 | tf_op jit(solution)/shard_map/ppermute | solution.py:209
  23.2 2.0 %collective-permute-start.3 = (bf16[4,64,1024]{2,1,0:T(8,128)(2,1)S(1)}, bf16[4,64,1024]{2,1,0:T(8,128)(2,1)S(1)}, u32[]{:S(2)}, u32[]{:S(2)}) collective-permute-start(bf16[4,64,1024]{2,1,0:T(8,128)(2,1)S(1)} %pad_maximum_fusion.1), channel_id=1, source_target_pairs={{0,2},{2,0},{4,6},{6,4},{8,10},{10,8},{12,14},{14,12},{1,3},{3,1},... | collective-permute-start | bytes 1572872 | tf_op jit(solution)/shard_map/ppermute | solution.py:211
  27.5 19.0 %copy-start.5 = (bf16[1,32,2048]{2,1,0:T(8,128)(2,1)S(1)}, bf16[1,32,2048]{2,1,0:T(8,128)(2,1)}, u32[]{:S(2)}) copy-start(bf16[1,32,2048]{2,1,0:T(8,128)(2,1)} %param.15) | copy-start | bytes 393220
  27.6 20.8 %copy-start.7 = (f32[1,64,4]{1,2,0:T(4,128)S(1)}, f32[1,64,4]{1,2,0:T(4,128)}, u32[]{:S(2)}) copy-start(f32[1,64,4]{1,2,0:T(4,128)} %param.22) | copy-start | bytes 3076
  46.6 11.6 %copy-start.6 = (f32[2048]{0:T(1024)S(1)}, f32[2048]{0:T(1024)}, u32[]{:S(2)}) copy-start(f32[2048]{0:T(1024)} %param.17) | copy-start | bytes 24580
  46.6 11.3 %collective-permute-start.4 = (bf16[96,2048]{1,0:T(8,128)(2,1)S(1)}, bf16[96,2048]{1,0:T(8,128)(2,1)S(1)}, u32[]{:S(2)}, u32[]{:S(2)}) collective-permute-start(bf16[96,2048]{1,0:T(8,128)(2,1)S(1)} %pad_maximum_fusion.2), channel_id=1, source_target_pairs={{0,1},{1,0},{2,3},{3,2},{4,5},{5,4},{6,7},{7,6},{8,9},{9,8},{10,11... | collective-permute-start | bytes 1179656 | tf_op jit(solution)/shard_map/ppermute | solution.py:49
  58.7 1.5 %collective-permute-start.5 = (bf16[48,2048]{1,0:T(8,128)(2,1)S(1)}, bf16[48,2048]{1,0:T(8,128)(2,1)S(1)}, u32[]{:S(2)}, u32[]{:S(2)}) collective-permute-start(bf16[48,2048]{1,0:T(8,128)(2,1)S(1)} %get-tuple-element.17), channel_id=1, source_target_pairs={{0,2},{2,0},{4,6},{6,4},{8,10},{10,8},{12,14},{14,12},{1,3},{3,1},... | collective-permute-start | bytes 589832 | tf_op jit(solution)/shard_map/ppermute | solution.py:141
  59.0 1.7 %copy-start.2 = (bf16[1,2048,352]{1,2,0:T(8,128)(2,1)S(1)}, bf16[1,2048,352]{1,2,0:T(8,128)(2,1)}, u32[]{:S(2)}) copy-start(bf16[1,2048,352]{1,2,0:T(8,128)(2,1)} %param.19) | copy-start | bytes 4325380
  59.1 4.2 %collective-permute-start.7 = (bf16[3,48,1024]{2,1,0:T(8,128)(2,1)S(1)}, bf16[3,48,1024]{2,1,0:T(8,128)(2,1)S(1)}, u32[]{:S(2)}, u32[]{:S(2)}) collective-permute-start(bf16[3,48,1024]{2,1,0:T(8,128)(2,1)S(1)} %bitcast.230), channel_id=1, source_target_pairs={{0,2},{2,0},{4,6},{6,4},{8,10},{10,8},{12,14},{14,12},{1,3},{3,1},... | collective-permute-start | bytes 884744 | tf_op jit(solution)/shard_map/ppermute | solution.py:143
  61.4 2.0 %copy-start.4 = (bf16[8,64,1024]{2,1,0:T(8,128)(2,1)S(1)}, bf16[8,64,1024]{2,1,0:T(8,128)(2,1)}, u32[]{:S(2)}) copy-start(bf16[8,64,1024]{2,1,0:T(8,128)(2,1)} %copy-done.3) | copy-start | bytes 3145732
  61.7 11.9 %collective-permute-start.6 = (bf16[96,1024]{1,0:T(8,128)(2,1)S(1)}, bf16[96,1024]{1,0:T(8,128)(2,1)S(1)}, u32[]{:S(2)}, u32[]{:S(2)}) collective-permute-start(bf16[96,1024]{1,0:T(8,128)(2,1)S(1)} %convolution_convert_fusion.5), channel_id=1, source_target_pairs={{0,1},{1,0},{2,3},{3,2},{4,5},{5,4},{6,7},{7,6},{8,9},{9,8},{10,11... | collective-permute-start | bytes 589832 | tf_op jit(solution)/shard_map/ppermute | solution.py:49
  63.3 9.7 %collective-permute-start.8 = (bf16[2,48,1024]{2,1,0:T(8,128)(2,1)S(1)}, bf16[2,48,1024]{2,1,0:T(8,128)(2,1)S(1)}, u32[]{:S(2)}, u32[]{:S(2)}) collective-permute-start(bf16[2,48,1024]{2,1,0:T(8,128)(2,1)S(1)} %get-tuple-element.11), channel_id=1, source_target_pairs={{0,4},{2,6},{4,8},{6,10},{8,12},{10,14},{12,0},{14,2},{1,5},{3,7},... | collective-permute-start | bytes 589832 | tf_op jit(solution)/shard_map/ppermute | solution.py:147
  65.1 15.2 %collective-permute-start.12 = (bf16[2,48,1024]{2,1,0:T(8,128)(2,1)S(1)}, bf16[2,48,1024]{2,1,0:T(8,128)(2,1)S(1)}, u32[]{:S(2)}, u32[]{:S(2)}) collective-permute-start(bf16[2,48,1024]{2,1,0:T(8,128)(2,1)S(1)} %get-tuple-element.13), channel_id=1, source_target_pairs={{0,8},{2,10},{4,12},{6,14},{8,0},{10,2},{12,4},{14,6},{1,9},{3,11}... | collective-permute-start | bytes 589832 | tf_op jit(solution)/shard_map/ppermute | solution.py:147
  67.3 13.5 %collective-permute-start.16 = (bf16[2,48,1024]{2,1,0:T(8,128)(2,1)S(1)}, bf16[2,48,1024]{2,1,0:T(8,128)(2,1)S(1)}, u32[]{:S(2)}, u32[]{:S(2)}) collective-permute-start(bf16[2,48,1024]{2,1,0:T(8,128)(2,1)S(1)} %get-tuple-element.12), channel_id=1, source_target_pairs={{0,12},{2,14},{4,0},{6,2},{8,4},{10,6},{12,8},{14,10},{1,13},{3,15... | collective-permute-start | bytes 589832 | tf_op jit(solution)/shard_map/ppermute | solution.py:147
  73.0 9.3 %collective-permute-start.9 = (bf16[96,1024]{1,0:T(8,128)(2,1)S(1)}, bf16[96,1024]{1,0:T(8,128)(2,1)S(1)}, u32[]{:S(2)}, u32[]{:S(2)}) collective-permute-start(bf16[96,1024]{1,0:T(8,128)(2,1)S(1)} %bitcast.241), channel_id=1, source_target_pairs={{0,1},{1,0},{2,3},{3,2},{4,5},{5,4},{6,7},{7,6},{8,9},{9,8},{10,11... | collective-permute-start | bytes 589832 | tf_op jit(solution)/shard_map/ppermute | solution.py:49
  80.3 7.8 %collective-permute-start.13 = (bf16[96,1024]{1,0:T(8,128)(2,1)S(1)}, bf16[96,1024]{1,0:T(8,128)(2,1)S(1)}, u32[]{:S(2)}, u32[]{:S(2)}) collective-permute-start(bf16[96,1024]{1,0:T(8,128)(2,1)S(1)} %bitcast.238), channel_id=1, source_target_pairs={{0,1},{1,0},{2,3},{3,2},{4,5},{5,4},{6,7},{7,6},{8,9},{9,8},{10,11... | collective-permute-start | bytes 589832 | tf_op jit(solution)/shard_map/ppermute | solution.py:49
  80.8 11.5 %collective-permute-start.17 = (bf16[96,1024]{1,0:T(8,128)(2,1)S(1)}, bf16[96,1024]{1,0:T(8,128)(2,1)S(1)}, u32[]{:S(2)}, u32[]{:S(2)}) collective-permute-start(bf16[96,1024]{1,0:T(8,128)(2,1)S(1)} %bitcast.235), channel_id=1, source_target_pairs={{0,1},{1,0},{2,3},{3,2},{4,5},{5,4},{6,7},{7,6},{8,9},{9,8},{10,11... | collective-permute-start | bytes 589832 | tf_op jit(solution)/shard_map/ppermute | solution.py:49
  84.2 12.4 %collective-permute-start.10 = (bf16[96,1024]{1,0:T(8,128)(2,1)S(1)}, bf16[96,1024]{1,0:T(8,128)(2,1)S(1)}, u32[]{:S(2)}, u32[]{:S(2)}) collective-permute-start(bf16[96,1024]{1,0:T(8,128)(2,1)S(1)} %convolution_convert_fusion.4), channel_id=1, source_target_pairs={{0,1},{1,0},{2,3},{3,2},{4,5},{5,4},{6,7},{7,6},{8,9},{9,8},{10,11... | collective-permute-start | bytes 589832 | tf_op jit(solution)/shard_map/ppermute | solution.py:49
  89.9 11.0 %collective-permute-start.14 = (bf16[96,1024]{1,0:T(8,128)(2,1)S(1)}, bf16[96,1024]{1,0:T(8,128)(2,1)S(1)}, u32[]{:S(2)}, u32[]{:S(2)}) collective-permute-start(bf16[96,1024]{1,0:T(8,128)(2,1)S(1)} %convolution_convert_fusion.3), channel_id=1, source_target_pairs={{0,1},{1,0},{2,3},{3,2},{4,5},{5,4},{6,7},{7,6},{8,9},{9,8},{10,11... | collective-permute-start | bytes 589832 | tf_op jit(solution)/shard_map/ppermute | solution.py:49
  94.1 9.8 %collective-permute-start.18 = (bf16[96,1024]{1,0:T(8,128)(2,1)S(1)}, bf16[96,1024]{1,0:T(8,128)(2,1)S(1)}, u32[]{:S(2)}, u32[]{:S(2)}) collective-permute-start(bf16[96,1024]{1,0:T(8,128)(2,1)S(1)} %convolution_convert_fusion.2), channel_id=1, source_target_pairs={{0,1},{1,0},{2,3},{3,2},{4,5},{5,4},{6,7},{7,6},{8,9},{9,8},{10,11... | collective-permute-start | bytes 589832 | tf_op jit(solution)/shard_map/ppermute | solution.py:49
  96.9 11.5 %collective-permute-start.11 = (bf16[48,1024]{1,0:T(8,128)(2,1)S(1)}, bf16[48,1024]{1,0:T(8,128)(2,1)S(1)}, u32[]{:S(2)}, u32[]{:S(2)}) collective-permute-start(bf16[48,1024]{1,0:T(8,128)(2,1)S(1)} %get-tuple-element.20), channel_id=1, source_target_pairs={{0,12},{2,14},{4,0},{6,2},{8,4},{10,6},{12,8},{14,10},{1,13},{3,15... | collective-permute-start | bytes 294920 | tf_op jit(solution)/shard_map/ppermute | solution.py:187
  101.3 7.7 %collective-permute-start.15 = (bf16[48,1024]{1,0:T(8,128)(2,1)S(1)}, bf16[48,1024]{1,0:T(8,128)(2,1)S(1)}, u32[]{:S(2)}, u32[]{:S(2)}) collective-permute-start(bf16[48,1024]{1,0:T(8,128)(2,1)S(1)} %get-tuple-element.22), channel_id=1, source_target_pairs={{0,8},{2,10},{4,12},{6,14},{8,0},{10,2},{12,4},{14,6},{1,9},{3,11}... | collective-permute-start | bytes 294920 | tf_op jit(solution)/shard_map/ppermute | solution.py:187
  104.2 6.6 %collective-permute-start.19 = (bf16[48,1024]{1,0:T(8,128)(2,1)S(1)}, bf16[48,1024]{1,0:T(8,128)(2,1)S(1)}, u32[]{:S(2)}, u32[]{:S(2)}) collective-permute-start(bf16[48,1024]{1,0:T(8,128)(2,1)S(1)} %get-tuple-element.24), channel_id=1, source_target_pairs={{0,4},{2,6},{4,8},{6,10},{8,12},{10,14},{12,0},{14,2},{1,5},{3,7},... | collective-permute-start | bytes 294920 | tf_op jit(solution)/shard_map/ppermute | solution.py:187
  106.1 4.8 %collective-permute-start.20 = (bf16[48,1024]{1,0:T(8,128)(2,1)S(1)}, bf16[48,1024]{1,0:T(8,128)(2,1)S(1)}, u32[]{:S(2)}, u32[]{:S(2)}) collective-permute-start(bf16[48,1024]{1,0:T(8,128)(2,1)S(1)} %get-tuple-element.19), channel_id=1, source_target_pairs={{0,2},{2,0},{4,6},{6,4},{8,10},{10,8},{12,14},{14,12},{1,3},{3,1},... | collective-permute-start | bytes 294920 | tf_op jit(solution)/shard_map/ppermute | solution.py:184
  106.2 5.7 %collective-permute-start.21 = (bf16[48,1024]{1,0:T(8,128)(2,1)S(1)}, bf16[48,1024]{1,0:T(8,128)(2,1)S(1)}, u32[]{:S(2)}, u32[]{:S(2)}) collective-permute-start(bf16[48,1024]{1,0:T(8,128)(2,1)S(1)} %get-tuple-element.21), channel_id=1, source_target_pairs={{0,14},{2,12},{4,2},{6,0},{8,6},{10,4},{12,10},{14,8},{1,15},{3,13... | collective-permute-start | bytes 294920 | tf_op jit(solution)/shard_map/ppermute | solution.py:189
  108.3 10.8 %collective-permute-start.22 = (bf16[48,1024]{1,0:T(8,128)(2,1)S(1)}, bf16[48,1024]{1,0:T(8,128)(2,1)S(1)}, u32[]{:S(2)}, u32[]{:S(2)}) collective-permute-start(bf16[48,1024]{1,0:T(8,128)(2,1)S(1)} %get-tuple-element.23), channel_id=1, source_target_pairs={{0,10},{2,8},{4,14},{6,12},{8,2},{10,0},{12,6},{14,4},{1,11},{3,9}... | collective-permute-start | bytes 294920 | tf_op jit(solution)/shard_map/ppermute | solution.py:189
  108.9 10.2 %collective-permute-start.23 = (bf16[48,1024]{1,0:T(8,128)(2,1)S(1)}, bf16[48,1024]{1,0:T(8,128)(2,1)S(1)}, u32[]{:S(2)}, u32[]{:S(2)}) collective-permute-start(bf16[48,1024]{1,0:T(8,128)(2,1)S(1)} %get-tuple-element.25), channel_id=1, source_target_pairs={{0,6},{2,4},{4,10},{6,8},{8,14},{10,12},{12,2},{14,0},{1,7},{3,5},... | collective-permute-start | bytes 294920 | tf_op jit(solution)/shard_map/ppermute | solution.py:189
  119.8 4.3 %collective-permute-start.24 = (bf16[32,1024]{1,0:T(8,128)(2,1)S(1)}, bf16[32,1024]{1,0:T(8,128)(2,1)S(1)}, u32[]{:S(2)}, u32[]{:S(2)}) collective-permute-start(bf16[32,1024]{1,0:T(8,128)(2,1)S(1)} %select_convert_fusion), channel_id=1, source_target_pairs={{0,1},{1,0},{2,3},{3,2},{4,5},{5,4},{6,7},{7,6},{8,9},{9,8},{10,11... | collective-permute-start | bytes 196616 | tf_op jit(solution)/shard_map/ppermute | solution.py:49
  (2 other events, 2.5 us)
Sparse Core Ops, SparseCore 0:
  9.6 34.5 all-gather.1

commit v23 on v21

--- a/solution.py
+++ b/solution.py
@@ -284,7 +284,11 @@
     if lax.axis_size("exp") == 2:
         first_exp = lax.axis_index("exp") == 0
         residual_all = join(residual[0], exp_swap(residual[0]), first_exp, 0)
-        head_all = out_parts + exp_swap(out_parts.astype(jnp.bfloat16)).astype(jnp.float32)
+        split = out_parts.shape[0] // 2
+        head_parts = []
+        for part in (out_parts[:split], out_parts[split:]):
+            head_parts.append(part + exp_swap(part.astype(jnp.bfloat16)).astype(jnp.float32))
+        head_all = jnp.concatenate(head_parts, axis=0)
         stream_all = (residual_all.astype(jnp.float32) + head_all).astype(jnp.bfloat16)
         stream = halves(stream_all, first_exp, 0)[0]
         stream_f = stream_all.astype(jnp.float32)

time: 130 us -> 129 us (level)
  waiting for transfers between devices: 59 us -> 57.6 us
    ppermute x10 -> x11, starting transfers between devices: 9.21 us -> 9.94 us  [exp_swap(): return lax.ppermute(x, 'exp', perm=[(0, 1), (1, 0)])]
    ppermute x10 -> x11, waiting for transfers between devices: 19.5 us -> 19 us  [exp_swap(): return lax.ppermute(x, 'exp', perm=[(0, 1), (1, 0)])]
  transfers between devices with their start and end apart: 27 -> 28, of which waited for: 15 -> 17; matrix products, arithmetic and copies ran while one was open for 15% -> 15% of each run, Pallas kernels for 0% -> 0%
where the time goes in v23:
time: 129 us
  waiting for transfers between devices  57.6 us (45%)
  starting transfers between devices  32.7 us (25%)
  between operations  15.3 us (12%)
  matrix products  13.6 us (11%)
  other arithmetic  4.8 us (4%)
  local copies, waits for them, and re-layouts  4.5 us (3%)
    ppermute x11, waiting for transfers between devices, exp_swap(): return lax.ppermute(x, 'exp', perm=[(0, 1), (1, 0)])  19 us
    all_gather x1, waiting for transfers between devices, local(): lax.all_gather(out_weight, 'ctx', axis=0, tiled=True)  16.6 us
    ppermute x3, waiting for transfers between devices, moe_column_halves(): arrived.append(lax.ppermute(far_pairs[shift - 1], 'ctx', perm=perm))  10.4 us
    ppermute x11, starting transfers between devices, exp_swap(): return lax.ppermute(x, 'exp', perm=[(0, 1), (1, 0)])  9.94 us
    ppermute x3, waiting for transfers between devices, moe_column_halves(): returned_partner[shift] = lax.ppermute(summed[idx][1], 'ctx', perm=perm)  8.23 us
    ppermute x3, starting transfers between devices, ctx_gather_blocks(): stack.append(lax.ppermute(rows, 'ctx', perm=perm))  7.01 us
    ppermute x3, starting transfers between devices, moe_column_halves(): returned[shift] = lax.ppermute(summed[idx][0], 'ctx', perm=perm)  6.67 us
    ppermute x3, starting transfers between devices, moe_column_halves(): returned_partner[shift] = lax.ppermute(summed[idx][1], 'ctx', perm=perm)  4.24 us
  transfers between devices with their start and end apart: 28, of which 17 were waited for; matrix products, arithmetic and copies ran while one was open for 15% of the time, Pallas kernels for 0%

profile of v23, /device:TPU:0, one launch (start us, length us, event | category | flops | bytes accessed | tf_op | source)
XLA Modules:
  0.0 128.6 jit_solution(11143273615946846940)
XLA Ops:
  7.2 1.0 fusion.156
  8.2 3.1 %collective-permute-start.1 = (bf16[64,1024]{1,0:T(8,128)(2,1)S(1)}, bf16[64,1024]{1,0:T(8,128)(2,1)S(1)}, u32[]{:S(2)}, u32[]{:S(2)}) collective-permute-start(bf16[64,1024]{1,0:T(8,128)(2,1)S(1)} %get-tuple-element.31), channel_id=1, source_target_pairs={{0,4},{2,6},{4,8},{6,10},{8,12},{10,14},{12,0},{14,2},{1,5},{3,7},... | collective-permute-start | bytes 393224 | tf_op jit(solution)/shard_map/ppermute | solution.py:209
  11.3 2.6 %collective-permute-start.2 = (bf16[64,1024]{1,0:T(8,128)(2,1)S(1)}, bf16[64,1024]{1,0:T(8,128)(2,1)S(1)}, u32[]{:S(2)}, u32[]{:S(2)}) collective-permute-start(bf16[64,1024]{1,0:T(8,128)(2,1)S(1)} %get-tuple-element.31), channel_id=1, source_target_pairs={{0,8},{2,10},{4,12},{6,14},{8,0},{10,2},{12,4},{14,6},{1,9},{3,11}... | collective-permute-start | bytes 393224 | tf_op jit(solution)/shard_map/ppermute | solution.py:209
  13.9 1.3 %collective-permute-start.3 = (bf16[64,1024]{1,0:T(8,128)(2,1)S(1)}, bf16[64,1024]{1,0:T(8,128)(2,1)S(1)}, u32[]{:S(2)}, u32[]{:S(2)}) collective-permute-start(bf16[64,1024]{1,0:T(8,128)(2,1)S(1)} %get-tuple-element.31), channel_id=1, source_target_pairs={{0,12},{2,14},{4,0},{6,2},{8,4},{10,6},{12,8},{14,10},{1,13},{3,15... | collective-permute-start | bytes 393224 | tf_op jit(solution)/shard_map/ppermute | solution.py:209
  15.3 1.6 %collective-permute-start = (bf16[32,2048]{1,0:T(8,128)(2,1)}, bf16[32,2048]{1,0:T(8,128)(2,1)S(1)}, u32[]{:S(2)}, u32[]{:S(2)}) collective-permute-start(bf16[32,2048]{1,0:T(8,128)(2,1)} %bitcast.240), channel_id=1, source_target_pairs={{0,1},{1,0},{2,3},{3,2},{4,5},{5,4},{6,7},{7,6},{8,9},{9,8},{10,11... | collective-permute-start | bytes 393224 | tf_op jit(solution)/shard_map/ppermute | solution.py:49
  21.0 0.9 constant_dynamic-update-slice_fusion.4
  22.7 1.8 %collective-permute-done.4 = bf16[4,64,1024]{2,1,0:T(8,128)(2,1)S(1)} collective-permute-done((bf16[4,64,1024]{2,1,0:T(8,128)(2,1)S(1)}, bf16[4,64,1024]{2,1,0:T(8,128)(2,1)S(1)}, u32[]{:S(2)}, u32[]{:S(2)}) %collective-permute-start.4) | collective-permute-done | bytes 524320 | tf_op jit(solution)/shard_map/ppermute | solution.py:211
  24.7 0.9 copy-done.3
  27.0 16.6 %all-gather.2.cloned.1.call-done = bf16[2048,512]{1,0:T(8,128)(2,1)} async-done(((bf16[256,512]{1,0:T(8,128)(2,1)}), bf16[2048,512]{1,0:T(8,128)(2,1)}) %all-gather.2.cloned.1.call-update) | async-done | bytes 2097168 | tf_op jit(solution)/shard_map/all_gather | solution.py:281
  43.6 2.3 %fusion.84 = f32[64,2048]{1,0:T(8,128)S(1)} fusion(bf16[2048,512]{1,0:T(8,128)(2,1)} %all-gather.2.cloned.1.call-done, bf16[4,8,8,128]{3,2,1,0:T(8,128)(2,1)S(1)} %fusion.8), kind=kOutput, calls=%fused_computation.140 | convolution fusion | flops 134217728 | bytes 2686976 | tf_op jit(solution)/shard_map/tc,oc->to/dot_general | solution.py:278
  46.0 1.6 %collective-permute-start.5 = (bf16[32,2048]{1,0:T(8,128)(2,1)S(1)}, bf16[32,2048]{1,0:T(8,128)(2,1)S(1)}, u32[]{:S(2)}, u32[]{:S(2)}) collective-permute-start(bf16[32,2048]{1,0:T(8,128)(2,1)S(1)} %get-tuple-element.18), channel_id=1, source_target_pairs={{0,1},{1,0},{2,3},{3,2},{4,5},{5,4},{6,7},{7,6},{8,9},{9,8},{10,11... | collective-permute-start | bytes 393224 | tf_op jit(solution)/shard_map/ppermute | solution.py:49
  48.8 3.6 %collective-permute-done.5 = bf16[32,2048]{1,0:T(8,128)(2,1)S(1)} collective-permute-done((bf16[32,2048]{1,0:T(8,128)(2,1)S(1)}, bf16[32,2048]{1,0:T(8,128)(2,1)S(1)}, u32[]{:S(2)}, u32[]{:S(2)}) %collective-permute-start.5) | collective-permute-done | bytes 131104 | tf_op jit(solution)/shard_map/ppermute | solution.py:49
  52.4 2.1 %collective-permute-done.6 = bf16[32,2048]{1,0:T(8,128)(2,1)S(1)} collective-permute-done((bf16[32,2048]{1,0:T(8,128)(2,1)S(1)}, bf16[32,2048]{1,0:T(8,128)(2,1)S(1)}, u32[]{:S(2)}, u32[]{:S(2)}) %collective-permute-start.6) | collective-permute-done | bytes 131104 | tf_op jit(solution)/shard_map/ppermute | solution.py:49
  58.2 1.6 %collective-permute-start.8 = (bf16[96,1024]{1,0:T(8,128)(2,1)S(1)}, bf16[96,1024]{1,0:T(8,128)(2,1)S(1)}, u32[]{:S(2)}, u32[]{:S(2)}) collective-permute-start(bf16[96,1024]{1,0:T(8,128)(2,1)S(1)} %convolution_convert_fusion.5), channel_id=1, source_target_pairs={{0,1},{1,0},{2,3},{3,2},{4,5},{5,4},{6,7},{7,6},{8,9},{9,8},{10,11... | collective-permute-start | bytes 589832 | tf_op jit(solution)/shard_map/ppermute | solution.py:49
  60.6 0.9 fusion.10
  61.5 0.9 fusion.9
  62.4 1.5 %collective-permute-start.14 = (bf16[2,48,1024]{2,1,0:T(8,128)(2,1)S(1)}, bf16[2,48,1024]{2,1,0:T(8,128)(2,1)S(1)}, u32[]{:S(2)}, u32[]{:S(2)}) collective-permute-start(bf16[2,48,1024]{2,1,0:T(8,128)(2,1)S(1)} %get-tuple-element.13), channel_id=1, source_target_pairs={{0,8},{2,10},{4,12},{6,14},{8,0},{10,2},{12,4},{14,6},{1,9},{3,11}... | collective-permute-start | bytes 589832 | tf_op jit(solution)/shard_map/ppermute | solution.py:147
  63.9 1.8 %collective-permute-start.18 = (bf16[2,48,1024]{2,1,0:T(8,128)(2,1)S(1)}, bf16[2,48,1024]{2,1,0:T(8,128)(2,1)S(1)}, u32[]{:S(2)}, u32[]{:S(2)}) collective-permute-start(bf16[2,48,1024]{2,1,0:T(8,128)(2,1)S(1)} %get-tuple-element.12), channel_id=1, source_target_pairs={{0,12},{2,14},{4,0},{6,2},{8,4},{10,6},{12,8},{14,10},{1,13},{3,15... | collective-permute-start | bytes 589832 | tf_op jit(solution)/shard_map/ppermute | solution.py:147
  65.7 3.9 %collective-permute-done.10 = bf16[2,48,1024]{2,1,0:T(8,128)(2,1)S(1)} collective-permute-done((bf16[2,48,1024]{2,1,0:T(8,128)(2,1)S(1)}, bf16[2,48,1024]{2,1,0:T(8,128)(2,1)S(1)}, u32[]{:S(2)}, u32[]{:S(2)}) %collective-permute-start.10) | collective-permute-done | bytes 196640 | tf_op jit(solution)/shard_map/ppermute | solution.py:147
  70.4 6.5 %collective-permute-done.14 = bf16[2,48,1024]{2,1,0:T(8,128)(2,1)S(1)} collective-permute-done((bf16[2,48,1024]{2,1,0:T(8,128)(2,1)S(1)}, bf16[2,48,1024]{2,1,0:T(8,128)(2,1)S(1)}, u32[]{:S(2)}, u32[]{:S(2)}) %collective-permute-start.14) | collective-permute-done | bytes 196640 | tf_op jit(solution)/shard_map/ppermute | solution.py:147
  77.4 1.6 %collective-permute-start.19 = (bf16[96,1024]{1,0:T(8,128)(2,1)S(1)}, bf16[96,1024]{1,0:T(8,128)(2,1)S(1)}, u32[]{:S(2)}, u32[]{:S(2)}) collective-permute-start(bf16[96,1024]{1,0:T(8,128)(2,1)S(1)} %bitcast.231), channel_id=1, source_target_pairs={{0,1},{1,0},{2,3},{3,2},{4,5},{5,4},{6,7},{7,6},{8,9},{9,8},{10,11... | collective-permute-start | bytes 589832 | tf_op jit(solution)/shard_map/ppermute | solution.py:49
  81.3 3.4 %collective-permute-done.15 = bf16[96,1024]{1,0:T(8,128)(2,1)S(1)} collective-permute-done((bf16[96,1024]{1,0:T(8,128)(2,1)S(1)}, bf16[96,1024]{1,0:T(8,128)(2,1)S(1)}, u32[]{:S(2)}, u32[]{:S(2)}) %collective-permute-start.15) | collective-permute-done | bytes 196640 | tf_op jit(solution)/shard_map/ppermute | solution.py:49
  87.0 1.9 %collective-permute-done.19 = bf16[96,1024]{1,0:T(8,128)(2,1)S(1)} collective-permute-done((bf16[96,1024]{1,0:T(8,128)(2,1)S(1)}, bf16[96,1024]{1,0:T(8,128)(2,1)S(1)}, u32[]{:S(2)}, u32[]{:S(2)}) %collective-permute-start.19) | collective-permute-done | bytes 196640 | tf_op jit(solution)/shard_map/ppermute | solution.py:49
  91.2 1.9 %collective-permute-done.12 = bf16[96,1024]{1,0:T(8,128)(2,1)S(1)} collective-permute-done((bf16[96,1024]{1,0:T(8,128)(2,1)S(1)}, bf16[96,1024]{1,0:T(8,128)(2,1)S(1)}, u32[]{:S(2)}, u32[]{:S(2)}) %collective-permute-start.12) | collective-permute-done | bytes 196640 | tf_op jit(solution)/shard_map/ppermute | solution.py:49
  93.5 4.4 %collective-permute-start.13 = (bf16[48,1024]{1,0:T(8,128)(2,1)S(1)}, bf16[48,1024]{1,0:T(8,128)(2,1)S(1)}, u32[]{:S(2)}, u32[]{:S(2)}) collective-permute-start(bf16[48,1024]{1,0:T(8,128)(2,1)S(1)} %get-tuple-element.24), channel_id=1, source_target_pairs={{0,12},{2,14},{4,0},{6,2},{8,4},{10,6},{12,8},{14,10},{1,13},{3,15... | collective-permute-start | bytes 294920 | tf_op jit(solution)/shard_map/ppermute | solution.py:187
  98.3 2.2 %collective-permute-done.20 = bf16[96,1024]{1,0:T(8,128)(2,1)S(1)} collective-permute-done((bf16[96,1024]{1,0:T(8,128)(2,1)S(1)}, bf16[96,1024]{1,0:T(8,128)(2,1)S(1)}, u32[]{:S(2)}, u32[]{:S(2)}) %collective-permute-start.20) | collective-permute-done | bytes 196640 | tf_op jit(solution)/shard_map/ppermute | solution.py:49
  100.8 2.2 %collective-permute-start.21 = (bf16[48,1024]{1,0:T(8,128)(2,1)S(1)}, bf16[48,1024]{1,0:T(8,128)(2,1)S(1)}, u32[]{:S(2)}, u32[]{:S(2)}) collective-permute-start(bf16[48,1024]{1,0:T(8,128)(2,1)S(1)} %get-tuple-element.28), channel_id=1, source_target_pairs={{0,4},{2,6},{4,8},{6,10},{8,12},{10,14},{12,0},{14,2},{1,5},{3,7},... | collective-permute-start | bytes 294920 | tf_op jit(solution)/shard_map/ppermute | solution.py:187
  103.1 2.1 %collective-permute-start.23 = (bf16[48,1024]{1,0:T(8,128)(2,1)S(1)}, bf16[48,1024]{1,0:T(8,128)(2,1)S(1)}, u32[]{:S(2)}, u32[]{:S(2)}) collective-permute-start(bf16[48,1024]{1,0:T(8,128)(2,1)S(1)} %get-tuple-element.25), channel_id=1, source_target_pairs={{0,14},{2,12},{4,2},{6,0},{8,6},{10,4},{12,10},{14,8},{1,15},{3,13... | collective-permute-start | bytes 294920 | tf_op jit(solution)/shard_map/ppermute | solution.py:189
  105.9 1.6 %collective-permute-start.25 = (bf16[48,1024]{1,0:T(8,128)(2,1)S(1)}, bf16[48,1024]{1,0:T(8,128)(2,1)S(1)}, u32[]{:S(2)}, u32[]{:S(2)}) collective-permute-start(bf16[48,1024]{1,0:T(8,128)(2,1)S(1)} %get-tuple-element.29), channel_id=1, source_target_pairs={{0,6},{2,4},{4,10},{6,8},{8,14},{10,12},{12,2},{14,0},{1,7},{3,5},... | collective-permute-start | bytes 294920 | tf_op jit(solution)/shard_map/ppermute | solution.py:189
  107.8 1.2 collective-permute-done.23
  108.9 7.1 %collective-permute-done.24 = bf16[48,1024]{1,0:T(8,128)(2,1)S(1)} collective-permute-done((bf16[48,1024]{1,0:T(8,128)(2,1)S(1)}, bf16[48,1024]{1,0:T(8,128)(2,1)S(1)}, u32[]{:S(2)}, u32[]{:S(2)}) %collective-permute-start.24) | collective-permute-done | bytes 98336 | tf_op jit(solution)/shard_map/ppermute | solution.py:189
  117.3 3.8 %collective-permute-done.26 = bf16[32,1024]{1,0:T(8,128)(2,1)S(1)} collective-permute-done((bf16[32,1024]{1,0:T(8,128)(2,1)S(1)}, bf16[32,1024]{1,0:T(8,128)(2,1)S(1)}, u32[]{:S(2)}, u32[]{:S(2)}) %collective-permute-start.26) | collective-permute-done | bytes 65568 | tf_op jit(solution)/shard_map/ppermute | solution.py:49
  (130 shorter events, 23.3 us)
Async XLA Ops:
  7.2 50.7 %copy-start = (bf16[1,352,2048]{2,1,0:T(8,128)(2,1)S(1)}, bf16[1,352,2048]{2,1,0:T(8,128)(2,1)}, u32[]{:S(2)}) copy-start(bf16[1,352,2048]{2,1,0:T(8,128)(2,1)} %param.20) | copy-start | bytes 4325380
  7.2 36.4 %all-gather.2.cloned.1.call-start = ((), (), s32[]{:S(2)}) async-start(), calls=%async_computation | async-start | bytes 2359296 | tf_op jit(solution)/shard_map/all_gather | solution.py:281
  8.2 13.7 %collective-permute-start.1 = (bf16[64,1024]{1,0:T(8,128)(2,1)S(1)}, bf16[64,1024]{1,0:T(8,128)(2,1)S(1)}, u32[]{:S(2)}, u32[]{:S(2)}) collective-permute-start(bf16[64,1024]{1,0:T(8,128)(2,1)S(1)} %get-tuple-element.31), channel_id=1, source_target_pairs={{0,4},{2,6},{4,8},{6,10},{8,12},{10,14},{12,0},{14,2},{1,5},{3,7},... | collective-permute-start | bytes 393224 | tf_op jit(solution)/shard_map/ppermute | solution.py:209
  11.3 11.2 %collective-permute-start.2 = (bf16[64,1024]{1,0:T(8,128)(2,1)S(1)}, bf16[64,1024]{1,0:T(8,128)(2,1)S(1)}, u32[]{:S(2)}, u32[]{:S(2)}) collective-permute-start(bf16[64,1024]{1,0:T(8,128)(2,1)S(1)} %get-tuple-element.31), channel_id=1, source_target_pairs={{0,8},{2,10},{4,12},{6,14},{8,0},{10,2},{12,4},{14,6},{1,9},{3,11}... | collective-permute-start | bytes 393224 | tf_op jit(solution)/shard_map/ppermute | solution.py:209
  13.9 8.6 %collective-permute-start.3 = (bf16[64,1024]{1,0:T(8,128)(2,1)S(1)}, bf16[64,1024]{1,0:T(8,128)(2,1)S(1)}, u32[]{:S(2)}, u32[]{:S(2)}) collective-permute-start(bf16[64,1024]{1,0:T(8,128)(2,1)S(1)} %get-tuple-element.31), channel_id=1, source_target_pairs={{0,12},{2,14},{4,0},{6,2},{8,4},{10,6},{12,8},{14,10},{1,13},{3,15... | collective-permute-start | bytes 393224 | tf_op jit(solution)/shard_map/ppermute | solution.py:209
  15.3 39.3 %collective-permute-start = (bf16[32,2048]{1,0:T(8,128)(2,1)}, bf16[32,2048]{1,0:T(8,128)(2,1)S(1)}, u32[]{:S(2)}, u32[]{:S(2)}) collective-permute-start(bf16[32,2048]{1,0:T(8,128)(2,1)} %bitcast.240), channel_id=1, source_target_pairs={{0,1},{1,0},{2,3},{3,2},{4,5},{5,4},{6,7},{7,6},{8,9},{9,8},{10,11... | collective-permute-start | bytes 393224 | tf_op jit(solution)/shard_map/ppermute | solution.py:49
  22.6 2.0 %collective-permute-start.4 = (bf16[4,64,1024]{2,1,0:T(8,128)(2,1)S(1)}, bf16[4,64,1024]{2,1,0:T(8,128)(2,1)S(1)}, u32[]{:S(2)}, u32[]{:S(2)}) collective-permute-start(bf16[4,64,1024]{2,1,0:T(8,128)(2,1)S(1)} %pad_maximum_fusion.1), channel_id=1, source_target_pairs={{0,2},{2,0},{4,6},{6,4},{8,10},{10,8},{12,14},{14,12},{1,3},{3,1},... | collective-permute-start | bytes 1572872 | tf_op jit(solution)/shard_map/ppermute | solution.py:211
  27.0 21.1 %copy-start.7 = (f32[1,64,4]{1,2,0:T(4,128)S(1)}, f32[1,64,4]{1,2,0:T(4,128)}, u32[]{:S(2)}) copy-start(f32[1,64,4]{1,2,0:T(4,128)} %param.22) | copy-start | bytes 3076
  45.9 8.6 %copy-start.5 = (bf16[1,32,2048]{2,1,0:T(8,128)(2,1)S(1)}, bf16[1,32,2048]{2,1,0:T(8,128)(2,1)}, u32[]{:S(2)}) copy-start(bf16[1,32,2048]{2,1,0:T(8,128)(2,1)} %param.15) | copy-start | bytes 393220
  46.0 6.4 %collective-permute-start.5 = (bf16[32,2048]{1,0:T(8,128)(2,1)S(1)}, bf16[32,2048]{1,0:T(8,128)(2,1)S(1)}, u32[]{:S(2)}, u32[]{:S(2)}) collective-permute-start(bf16[32,2048]{1,0:T(8,128)(2,1)S(1)} %get-tuple-element.18), channel_id=1, source_target_pairs={{0,1},{1,0},{2,3},{3,2},{4,5},{5,4},{6,7},{7,6},{8,9},{9,8},{10,11... | collective-permute-start | bytes 393224 | tf_op jit(solution)/shard_map/ppermute | solution.py:49
  47.6 6.9 %collective-permute-start.6 = (bf16[32,2048]{1,0:T(8,128)(2,1)S(1)}, bf16[32,2048]{1,0:T(8,128)(2,1)S(1)}, u32[]{:S(2)}, u32[]{:S(2)}) collective-permute-start(bf16[32,2048]{1,0:T(8,128)(2,1)S(1)} %get-tuple-element.19), channel_id=1, source_target_pairs={{0,1},{1,0},{2,3},{3,2},{4,5},{5,4},{6,7},{7,6},{8,9},{9,8},{10,11... | collective-permute-start | bytes 393224 | tf_op jit(solution)/shard_map/ppermute | solution.py:49
  48.4 6.4 %copy-start.6 = (f32[2048]{0:T(1024)S(1)}, f32[2048]{0:T(1024)}, u32[]{:S(2)}) copy-start(f32[2048]{0:T(1024)} %param.17) | copy-start | bytes 24580
  55.2 1.5 %collective-permute-start.7 = (bf16[48,2048]{1,0:T(8,128)(2,1)S(1)}, bf16[48,2048]{1,0:T(8,128)(2,1)S(1)}, u32[]{:S(2)}, u32[]{:S(2)}) collective-permute-start(bf16[48,2048]{1,0:T(8,128)(2,1)S(1)} %get-tuple-element.21), channel_id=1, source_target_pairs={{0,2},{2,0},{4,6},{6,4},{8,10},{10,8},{12,14},{14,12},{1,3},{3,1},... | collective-permute-start | bytes 589832 | tf_op jit(solution)/shard_map/ppermute | solution.py:141
  55.7 4.2 %collective-permute-start.9 = (bf16[3,48,1024]{2,1,0:T(8,128)(2,1)S(1)}, bf16[3,48,1024]{2,1,0:T(8,128)(2,1)S(1)}, u32[]{:S(2)}, u32[]{:S(2)}) collective-permute-start(bf16[3,48,1024]{2,1,0:T(8,128)(2,1)S(1)} %bitcast.226), channel_id=1, source_target_pairs={{0,2},{2,0},{4,6},{6,4},{8,10},{10,8},{12,14},{14,12},{1,3},{3,1},... | collective-permute-start | bytes 884744 | tf_op jit(solution)/shard_map/ppermute | solution.py:143
  58.2 11.9 %collective-permute-start.8 = (bf16[96,1024]{1,0:T(8,128)(2,1)S(1)}, bf16[96,1024]{1,0:T(8,128)(2,1)S(1)}, u32[]{:S(2)}, u32[]{:S(2)}) collective-permute-start(bf16[96,1024]{1,0:T(8,128)(2,1)S(1)} %convolution_convert_fusion.5), channel_id=1, source_target_pairs={{0,1},{1,0},{2,3},{3,2},{4,5},{5,4},{6,7},{7,6},{8,9},{9,8},{10,11... | collective-permute-start | bytes 589832 | tf_op jit(solution)/shard_map/ppermute | solution.py:49
  59.9 9.7 %collective-permute-start.10 = (bf16[2,48,1024]{2,1,0:T(8,128)(2,1)S(1)}, bf16[2,48,1024]{2,1,0:T(8,128)(2,1)S(1)}, u32[]{:S(2)}, u32[]{:S(2)}) collective-permute-start(bf16[2,48,1024]{2,1,0:T(8,128)(2,1)S(1)} %get-tuple-element.11), channel_id=1, source_target_pairs={{0,4},{2,6},{4,8},{6,10},{8,12},{10,14},{12,0},{14,2},{1,5},{3,7},... | collective-permute-start | bytes 589832 | tf_op jit(solution)/shard_map/ppermute | solution.py:147
  62.4 14.6 %collective-permute-start.14 = (bf16[2,48,1024]{2,1,0:T(8,128)(2,1)S(1)}, bf16[2,48,1024]{2,1,0:T(8,128)(2,1)S(1)}, u32[]{:S(2)}, u32[]{:S(2)}) collective-permute-start(bf16[2,48,1024]{2,1,0:T(8,128)(2,1)S(1)} %get-tuple-element.13), channel_id=1, source_target_pairs={{0,8},{2,10},{4,12},{6,14},{8,0},{10,2},{12,4},{14,6},{1,9},{3,11}... | collective-permute-start | bytes 589832 | tf_op jit(solution)/shard_map/ppermute | solution.py:147
  63.9 13.5 %collective-permute-start.18 = (bf16[2,48,1024]{2,1,0:T(8,128)(2,1)S(1)}, bf16[2,48,1024]{2,1,0:T(8,128)(2,1)S(1)}, u32[]{:S(2)}, u32[]{:S(2)}) collective-permute-start(bf16[2,48,1024]{2,1,0:T(8,128)(2,1)S(1)} %get-tuple-element.12), channel_id=1, source_target_pairs={{0,12},{2,14},{4,0},{6,2},{8,4},{10,6},{12,8},{14,10},{1,13},{3,15... | collective-permute-start | bytes 589832 | tf_op jit(solution)/shard_map/ppermute | solution.py:147
  69.6 9.3 %collective-permute-start.11 = (bf16[96,1024]{1,0:T(8,128)(2,1)S(1)}, bf16[96,1024]{1,0:T(8,128)(2,1)S(1)}, u32[]{:S(2)}, u32[]{:S(2)}) collective-permute-start(bf16[96,1024]{1,0:T(8,128)(2,1)S(1)} %bitcast.237), channel_id=1, source_target_pairs={{0,1},{1,0},{2,3},{3,2},{4,5},{5,4},{6,7},{7,6},{8,9},{9,8},{10,11... | collective-permute-start | bytes 589832 | tf_op jit(solution)/shard_map/ppermute | solution.py:49
  76.9 7.8 %collective-permute-start.15 = (bf16[96,1024]{1,0:T(8,128)(2,1)S(1)}, bf16[96,1024]{1,0:T(8,128)(2,1)S(1)}, u32[]{:S(2)}, u32[]{:S(2)}) collective-permute-start(bf16[96,1024]{1,0:T(8,128)(2,1)S(1)} %bitcast.234), channel_id=1, source_target_pairs={{0,1},{1,0},{2,3},{3,2},{4,5},{5,4},{6,7},{7,6},{8,9},{9,8},{10,11... | collective-permute-start | bytes 589832 | tf_op jit(solution)/shard_map/ppermute | solution.py:49
  77.4 11.5 %collective-permute-start.19 = (bf16[96,1024]{1,0:T(8,128)(2,1)S(1)}, bf16[96,1024]{1,0:T(8,128)(2,1)S(1)}, u32[]{:S(2)}, u32[]{:S(2)}) collective-permute-start(bf16[96,1024]{1,0:T(8,128)(2,1)S(1)} %bitcast.231), channel_id=1, source_target_pairs={{0,1},{1,0},{2,3},{3,2},{4,5},{5,4},{6,7},{7,6},{8,9},{9,8},{10,11... | collective-permute-start | bytes 589832 | tf_op jit(solution)/shard_map/ppermute | solution.py:49
  80.8 12.4 %collective-permute-start.12 = (bf16[96,1024]{1,0:T(8,128)(2,1)S(1)}, bf16[96,1024]{1,0:T(8,128)(2,1)S(1)}, u32[]{:S(2)}, u32[]{:S(2)}) collective-permute-start(bf16[96,1024]{1,0:T(8,128)(2,1)S(1)} %convolution_convert_fusion.4), channel_id=1, source_target_pairs={{0,1},{1,0},{2,3},{3,2},{4,5},{5,4},{6,7},{7,6},{8,9},{9,8},{10,11... | collective-permute-start | bytes 589832 | tf_op jit(solution)/shard_map/ppermute | solution.py:49
  86.5 11.4 %collective-permute-start.16 = (bf16[96,1024]{1,0:T(8,128)(2,1)S(1)}, bf16[96,1024]{1,0:T(8,128)(2,1)S(1)}, u32[]{:S(2)}, u32[]{:S(2)}) collective-permute-start(bf16[96,1024]{1,0:T(8,128)(2,1)S(1)} %convolution_convert_fusion.3), channel_id=1, source_target_pairs={{0,1},{1,0},{2,3},{3,2},{4,5},{5,4},{6,7},{7,6},{8,9},{9,8},{10,11... | collective-permute-start | bytes 589832 | tf_op jit(solution)/shard_map/ppermute | solution.py:49
  90.7 9.8 %collective-permute-start.20 = (bf16[96,1024]{1,0:T(8,128)(2,1)S(1)}, bf16[96,1024]{1,0:T(8,128)(2,1)S(1)}, u32[]{:S(2)}, u32[]{:S(2)}) collective-permute-start(bf16[96,1024]{1,0:T(8,128)(2,1)S(1)} %convolution_convert_fusion.2), channel_id=1, source_target_pairs={{0,1},{1,0},{2,3},{3,2},{4,5},{5,4},{6,7},{7,6},{8,9},{9,8},{10,11... | collective-permute-start | bytes 589832 | tf_op jit(solution)/shard_map/ppermute | solution.py:49
  93.5 11.7 %collective-permute-start.13 = (bf16[48,1024]{1,0:T(8,128)(2,1)S(1)}, bf16[48,1024]{1,0:T(8,128)(2,1)S(1)}, u32[]{:S(2)}, u32[]{:S(2)}) collective-permute-start(bf16[48,1024]{1,0:T(8,128)(2,1)S(1)} %get-tuple-element.24), channel_id=1, source_target_pairs={{0,12},{2,14},{4,0},{6,2},{8,4},{10,6},{12,8},{14,10},{1,13},{3,15... | collective-permute-start | bytes 294920 | tf_op jit(solution)/shard_map/ppermute | solution.py:187
  98.2 7.7 %collective-permute-start.17 = (bf16[48,1024]{1,0:T(8,128)(2,1)S(1)}, bf16[48,1024]{1,0:T(8,128)(2,1)S(1)}, u32[]{:S(2)}, u32[]{:S(2)}) collective-permute-start(bf16[48,1024]{1,0:T(8,128)(2,1)S(1)} %get-tuple-element.26), channel_id=1, source_target_pairs={{0,8},{2,10},{4,12},{6,14},{8,0},{10,2},{12,4},{14,6},{1,9},{3,11}... | collective-permute-start | bytes 294920 | tf_op jit(solution)/shard_map/ppermute | solution.py:187
  100.8 6.9 %collective-permute-start.21 = (bf16[48,1024]{1,0:T(8,128)(2,1)S(1)}, bf16[48,1024]{1,0:T(8,128)(2,1)S(1)}, u32[]{:S(2)}, u32[]{:S(2)}) collective-permute-start(bf16[48,1024]{1,0:T(8,128)(2,1)S(1)} %get-tuple-element.28), channel_id=1, source_target_pairs={{0,4},{2,6},{4,8},{6,10},{8,12},{10,14},{12,0},{14,2},{1,5},{3,7},... | collective-permute-start | bytes 294920 | tf_op jit(solution)/shard_map/ppermute | solution.py:187
  103.1 4.7 %collective-permute-start.22 = (bf16[48,1024]{1,0:T(8,128)(2,1)S(1)}, bf16[48,1024]{1,0:T(8,128)(2,1)S(1)}, u32[]{:S(2)}, u32[]{:S(2)}) collective-permute-start(bf16[48,1024]{1,0:T(8,128)(2,1)S(1)} %get-tuple-element.23), channel_id=1, source_target_pairs={{0,2},{2,0},{4,6},{6,4},{8,10},{10,8},{12,14},{14,12},{1,3},{3,1},... | collective-permute-start | bytes 294920 | tf_op jit(solution)/shard_map/ppermute | solution.py:184
  103.1 5.8 %collective-permute-start.23 = (bf16[48,1024]{1,0:T(8,128)(2,1)S(1)}, bf16[48,1024]{1,0:T(8,128)(2,1)S(1)}, u32[]{:S(2)}, u32[]{:S(2)}) collective-permute-start(bf16[48,1024]{1,0:T(8,128)(2,1)S(1)} %get-tuple-element.25), channel_id=1, source_target_pairs={{0,14},{2,12},{4,2},{6,0},{8,6},{10,4},{12,10},{14,8},{1,15},{3,13... | collective-permute-start | bytes 294920 | tf_op jit(solution)/shard_map/ppermute | solution.py:189
  105.2 10.8 %collective-permute-start.24 = (bf16[48,1024]{1,0:T(8,128)(2,1)S(1)}, bf16[48,1024]{1,0:T(8,128)(2,1)S(1)}, u32[]{:S(2)}, u32[]{:S(2)}) collective-permute-start(bf16[48,1024]{1,0:T(8,128)(2,1)S(1)} %get-tuple-element.27), channel_id=1, source_target_pairs={{0,10},{2,8},{4,14},{6,12},{8,2},{10,0},{12,6},{14,4},{1,11},{3,9}... | collective-permute-start | bytes 294920 | tf_op jit(solution)/shard_map/ppermute | solution.py:189
  105.9 10.1 %collective-permute-start.25 = (bf16[48,1024]{1,0:T(8,128)(2,1)S(1)}, bf16[48,1024]{1,0:T(8,128)(2,1)S(1)}, u32[]{:S(2)}, u32[]{:S(2)}) collective-permute-start(bf16[48,1024]{1,0:T(8,128)(2,1)S(1)} %get-tuple-element.29), channel_id=1, source_target_pairs={{0,6},{2,4},{4,10},{6,8},{8,14},{10,12},{12,2},{14,0},{1,7},{3,5},... | collective-permute-start | bytes 294920 | tf_op jit(solution)/shard_map/ppermute | solution.py:189
  116.7 4.3 %collective-permute-start.26 = (bf16[32,1024]{1,0:T(8,128)(2,1)S(1)}, bf16[32,1024]{1,0:T(8,128)(2,1)S(1)}, u32[]{:S(2)}, u32[]{:S(2)}) collective-permute-start(bf16[32,1024]{1,0:T(8,128)(2,1)S(1)} %select_convert_fusion), channel_id=1, source_target_pairs={{0,1},{1,0},{2,3},{3,2},{4,5},{5,4},{6,7},{7,6},{8,9},{9,8},{10,11... | collective-permute-start | bytes 196616 | tf_op jit(solution)/shard_map/ppermute | solution.py:49
  (4 other events, 7.0 us)
Sparse Core Ops, SparseCore 0:
  15.4 28.1 all-gather.1

commit v24 on v23

--- a/solution.py
+++ b/solution.py
@@ -191,11 +191,18 @@
     served = served.reshape(n_ctx * capacity, half_d)
     weight_hi = combine.astype(jnp.bfloat16)
     weight_lo = (combine - weight_hi.astype(jnp.float32)).astype(jnp.bfloat16)
-    moe_half = jnp.dot(weight_hi, served, preferred_element_type=jnp.float32) + jnp.dot(
-        weight_lo, served, preferred_element_type=jnp.float32
-    )
-    my_tok, other_tok = halves(moe_half, first, 0)
-    got_tok = exp_swap(other_tok.astype(jnp.bfloat16)).astype(jnp.float32)
+    quarter = half_d // 2
+    mine_parts = []
+    got_parts = []
+    for cols in (served[:, :quarter], served[:, quarter:]):
+        moe_part = jnp.dot(weight_hi, cols, preferred_element_type=jnp.float32) + jnp.dot(
+            weight_lo, cols, preferred_element_type=jnp.float32
+        )
+        my_tok, other_tok = halves(moe_part, first, 0)
+        mine_parts.append(my_tok)
+        got_parts.append(exp_swap(other_tok.astype(jnp.bfloat16)).astype(jnp.float32))
+    my_tok = jnp.concatenate(mine_parts, axis=1)
+    got_tok = jnp.concatenate(got_parts, axis=1)
     return join(my_tok, got_tok, first, 1)
 
 

time: 129 us -> 129 us (level)
  starting transfers between devices: 32.7 us -> 34.3 us
  waiting for transfers between devices: 57.6 us -> 56.2 us
    ppermute x11 -> x12, starting transfers between devices: 9.94 us -> 11.5 us  [exp_swap(): return lax.ppermute(x, 'exp', perm=[(0, 1), (1, 0)])]
    ppermute x11 -> x12, waiting for transfers between devices: 19 us -> 17.6 us  [exp_swap(): return lax.ppermute(x, 'exp', perm=[(0, 1), (1, 0)])]
  transfers between devices with their start and end apart: 28 -> 29, of which waited for: 17 -> 18; matrix products, arithmetic and copies ran while one was open for 15% -> 15% of each run, Pallas kernels for 0% -> 0%
where the time goes in v24:
time: 129 us
  waiting for transfers between devices  56.2 us (44%)
  starting transfers between devices  34.3 us (27%)
  between operations  15.4 us (12%)
  matrix products  13.9 us (11%)
  other arithmetic  4.81 us (4%)
  local copies, waits for them, and re-layouts  4.5 us (3%)
    ppermute x12, waiting for transfers between devices, exp_swap(): return lax.ppermute(x, 'exp', perm=[(0, 1), (1, 0)])  17.6 us
    all_gather x1, waiting for transfers between devices, local(): lax.all_gather(out_weight, 'ctx', axis=0, tiled=True)  16.6 us
    ppermute x12, starting transfers between devices, exp_swap(): return lax.ppermute(x, 'exp', perm=[(0, 1), (1, 0)])  11.5 us
    ppermute x3, waiting for transfers between devices, moe_column_halves(): arrived.append(lax.ppermute(far_pairs[shift - 1], 'ctx', perm=perm))  10.4 us
    ppermute x3, waiting for transfers between devices, moe_column_halves(): returned_partner[shift] = lax.ppermute(summed[idx][1], 'ctx', perm=perm)  8.23 us
    ppermute x3, starting transfers between devices, ctx_gather_blocks(): stack.append(lax.ppermute(rows, 'ctx', perm=perm))  7.01 us
    ppermute x3, starting transfers between devices, moe_column_halves(): returned[shift] = lax.ppermute(summed[idx][0], 'ctx', perm=perm)  6.67 us
    ppermute x3, starting transfers between devices, moe_column_halves(): returned_partner[shift] = lax.ppermute(summed[idx][1], 'ctx', perm=perm)  4.24 us
  transfers between devices with their start and end apart: 29, of which 18 were waited for; matrix products, arithmetic and copies ran while one was open for 15% of the time, Pallas kernels for 0%

profile of v24, /device:TPU:0, one launch (start us, length us, event | category | flops | bytes accessed | tf_op | source)
XLA Modules:
  0.0 129.1 jit_solution(13609396237321299576)
XLA Ops:
  7.2 1.0 fusion.162
  8.2 3.1 %collective-permute-start.1 = (bf16[64,1024]{1,0:T(8,128)(2,1)S(1)}, bf16[64,1024]{1,0:T(8,128)(2,1)S(1)}, u32[]{:S(2)}, u32[]{:S(2)}) collective-permute-start(bf16[64,1024]{1,0:T(8,128)(2,1)S(1)} %get-tuple-element.31), channel_id=1, source_target_pairs={{0,4},{2,6},{4,8},{6,10},{8,12},{10,14},{12,0},{14,2},{1,5},{3,7},... | collective-permute-start | bytes 393224 | tf_op jit(solution)/shard_map/ppermute | solution.py:216
  11.3 2.6 %collective-permute-start.2 = (bf16[64,1024]{1,0:T(8,128)(2,1)S(1)}, bf16[64,1024]{1,0:T(8,128)(2,1)S(1)}, u32[]{:S(2)}, u32[]{:S(2)}) collective-permute-start(bf16[64,1024]{1,0:T(8,128)(2,1)S(1)} %get-tuple-element.31), channel_id=1, source_target_pairs={{0,8},{2,10},{4,12},{6,14},{8,0},{10,2},{12,4},{14,6},{1,9},{3,11}... | collective-permute-start | bytes 393224 | tf_op jit(solution)/shard_map/ppermute | solution.py:216
  13.9 1.3 %collective-permute-start.3 = (bf16[64,1024]{1,0:T(8,128)(2,1)S(1)}, bf16[64,1024]{1,0:T(8,128)(2,1)S(1)}, u32[]{:S(2)}, u32[]{:S(2)}) collective-permute-start(bf16[64,1024]{1,0:T(8,128)(2,1)S(1)} %get-tuple-element.31), channel_id=1, source_target_pairs={{0,12},{2,14},{4,0},{6,2},{8,4},{10,6},{12,8},{14,10},{1,13},{3,15... | collective-permute-start | bytes 393224 | tf_op jit(solution)/shard_map/ppermute | solution.py:216
  15.3 1.6 %collective-permute-start = (bf16[32,2048]{1,0:T(8,128)(2,1)}, bf16[32,2048]{1,0:T(8,128)(2,1)S(1)}, u32[]{:S(2)}, u32[]{:S(2)}) collective-permute-start(bf16[32,2048]{1,0:T(8,128)(2,1)} %bitcast.250), channel_id=1, source_target_pairs={{0,1},{1,0},{2,3},{3,2},{4,5},{5,4},{6,7},{7,6},{8,9},{9,8},{10,11... | collective-permute-start | bytes 393224 | tf_op jit(solution)/shard_map/ppermute | solution.py:49
  21.0 0.9 constant_dynamic-update-slice_fusion.4
  22.7 1.8 %collective-permute-done.4 = bf16[4,64,1024]{2,1,0:T(8,128)(2,1)S(1)} collective-permute-done((bf16[4,64,1024]{2,1,0:T(8,128)(2,1)S(1)}, bf16[4,64,1024]{2,1,0:T(8,128)(2,1)S(1)}, u32[]{:S(2)}, u32[]{:S(2)}) %collective-permute-start.4) | collective-permute-done | bytes 524320 | tf_op jit(solution)/shard_map/ppermute | solution.py:218
  24.7 0.9 copy-done.3
  27.0 16.6 %all-gather.2.cloned.1.call-done = bf16[2048,512]{1,0:T(8,128)(2,1)} async-done(((bf16[256,512]{1,0:T(8,128)(2,1)}), bf16[2048,512]{1,0:T(8,128)(2,1)}) %all-gather.2.cloned.1.call-update) | async-done | bytes 2097168 | tf_op jit(solution)/shard_map/all_gather | solution.py:288
  43.6 2.3 %fusion.90 = f32[64,2048]{1,0:T(8,128)S(1)} fusion(bf16[2048,512]{1,0:T(8,128)(2,1)} %all-gather.2.cloned.1.call-done, bf16[4,8,8,128]{3,2,1,0:T(8,128)(2,1)S(1)} %fusion.8), kind=kOutput, calls=%fused_computation.145 | convolution fusion | flops 134217728 | bytes 2686976 | tf_op jit(solution)/shard_map/tc,oc->to/dot_general | solution.py:285
  46.0 1.6 %collective-permute-start.5 = (bf16[32,2048]{1,0:T(8,128)(2,1)S(1)}, bf16[32,2048]{1,0:T(8,128)(2,1)S(1)}, u32[]{:S(2)}, u32[]{:S(2)}) collective-permute-start(bf16[32,2048]{1,0:T(8,128)(2,1)S(1)} %get-tuple-element.18), channel_id=1, source_target_pairs={{0,1},{1,0},{2,3},{3,2},{4,5},{5,4},{6,7},{7,6},{8,9},{9,8},{10,11... | collective-permute-start | bytes 393224 | tf_op jit(solution)/shard_map/ppermute | solution.py:49
  48.8 3.6 %collective-permute-done.5 = bf16[32,2048]{1,0:T(8,128)(2,1)S(1)} collective-permute-done((bf16[32,2048]{1,0:T(8,128)(2,1)S(1)}, bf16[32,2048]{1,0:T(8,128)(2,1)S(1)}, u32[]{:S(2)}, u32[]{:S(2)}) %collective-permute-start.5) | collective-permute-done | bytes 131104 | tf_op jit(solution)/shard_map/ppermute | solution.py:49
  52.4 2.1 %collective-permute-done.6 = bf16[32,2048]{1,0:T(8,128)(2,1)S(1)} collective-permute-done((bf16[32,2048]{1,0:T(8,128)(2,1)S(1)}, bf16[32,2048]{1,0:T(8,128)(2,1)S(1)}, u32[]{:S(2)}, u32[]{:S(2)}) %collective-permute-start.6) | collective-permute-done | bytes 131104 | tf_op jit(solution)/shard_map/ppermute | solution.py:49
  58.2 1.6 %collective-permute-start.8 = (bf16[96,1024]{1,0:T(8,128)(2,1)S(1)}, bf16[96,1024]{1,0:T(8,128)(2,1)S(1)}, u32[]{:S(2)}, u32[]{:S(2)}) collective-permute-start(bf16[96,1024]{1,0:T(8,128)(2,1)S(1)} %convolution_convert_fusion.5), channel_id=1, source_target_pairs={{0,1},{1,0},{2,3},{3,2},{4,5},{5,4},{6,7},{7,6},{8,9},{9,8},{10,11... | collective-permute-start | bytes 589832 | tf_op jit(solution)/shard_map/ppermute | solution.py:49
  60.6 0.9 fusion.10
  62.4 1.5 %collective-permute-start.14 = (bf16[2,48,1024]{2,1,0:T(8,128)(2,1)S(1)}, bf16[2,48,1024]{2,1,0:T(8,128)(2,1)S(1)}, u32[]{:S(2)}, u32[]{:S(2)}) collective-permute-start(bf16[2,48,1024]{2,1,0:T(8,128)(2,1)S(1)} %get-tuple-element.13), channel_id=1, source_target_pairs={{0,8},{2,10},{4,12},{6,14},{8,0},{10,2},{12,4},{14,6},{1,9},{3,11}... | collective-permute-start | bytes 589832 | tf_op jit(solution)/shard_map/ppermute | solution.py:147
  63.9 1.8 %collective-permute-start.18 = (bf16[2,48,1024]{2,1,0:T(8,128)(2,1)S(1)}, bf16[2,48,1024]{2,1,0:T(8,128)(2,1)S(1)}, u32[]{:S(2)}, u32[]{:S(2)}) collective-permute-start(bf16[2,48,1024]{2,1,0:T(8,128)(2,1)S(1)} %get-tuple-element.12), channel_id=1, source_target_pairs={{0,12},{2,14},{4,0},{6,2},{8,4},{10,6},{12,8},{14,10},{1,13},{3,15... | collective-permute-start | bytes 589832 | tf_op jit(solution)/shard_map/ppermute | solution.py:147
  65.7 3.9 %collective-permute-done.10 = bf16[2,48,1024]{2,1,0:T(8,128)(2,1)S(1)} collective-permute-done((bf16[2,48,1024]{2,1,0:T(8,128)(2,1)S(1)}, bf16[2,48,1024]{2,1,0:T(8,128)(2,1)S(1)}, u32[]{:S(2)}, u32[]{:S(2)}) %collective-permute-start.10) | collective-permute-done | bytes 196640 | tf_op jit(solution)/shard_map/ppermute | solution.py:147
  70.4 6.5 %collective-permute-done.14 = bf16[2,48,1024]{2,1,0:T(8,128)(2,1)S(1)} collective-permute-done((bf16[2,48,1024]{2,1,0:T(8,128)(2,1)S(1)}, bf16[2,48,1024]{2,1,0:T(8,128)(2,1)S(1)}, u32[]{:S(2)}, u32[]{:S(2)}) %collective-permute-start.14) | collective-permute-done | bytes 196640 | tf_op jit(solution)/shard_map/ppermute | solution.py:147
  77.4 1.6 %collective-permute-start.19 = (bf16[96,1024]{1,0:T(8,128)(2,1)S(1)}, bf16[96,1024]{1,0:T(8,128)(2,1)S(1)}, u32[]{:S(2)}, u32[]{:S(2)}) collective-permute-start(bf16[96,1024]{1,0:T(8,128)(2,1)S(1)} %bitcast.241), channel_id=1, source_target_pairs={{0,1},{1,0},{2,3},{3,2},{4,5},{5,4},{6,7},{7,6},{8,9},{9,8},{10,11... | collective-permute-start | bytes 589832 | tf_op jit(solution)/shard_map/ppermute | solution.py:49
  81.3 3.4 %collective-permute-done.15 = bf16[96,1024]{1,0:T(8,128)(2,1)S(1)} collective-permute-done((bf16[96,1024]{1,0:T(8,128)(2,1)S(1)}, bf16[96,1024]{1,0:T(8,128)(2,1)S(1)}, u32[]{:S(2)}, u32[]{:S(2)}) %collective-permute-start.15) | collective-permute-done | bytes 196640 | tf_op jit(solution)/shard_map/ppermute | solution.py:49
  87.0 1.9 %collective-permute-done.19 = bf16[96,1024]{1,0:T(8,128)(2,1)S(1)} collective-permute-done((bf16[96,1024]{1,0:T(8,128)(2,1)S(1)}, bf16[96,1024]{1,0:T(8,128)(2,1)S(1)}, u32[]{:S(2)}, u32[]{:S(2)}) %collective-permute-start.19) | collective-permute-done | bytes 196640 | tf_op jit(solution)/shard_map/ppermute | solution.py:49
  91.2 1.9 %collective-permute-done.12 = bf16[96,1024]{1,0:T(8,128)(2,1)S(1)} collective-permute-done((bf16[96,1024]{1,0:T(8,128)(2,1)S(1)}, bf16[96,1024]{1,0:T(8,128)(2,1)S(1)}, u32[]{:S(2)}, u32[]{:S(2)}) %collective-permute-start.12) | collective-permute-done | bytes 196640 | tf_op jit(solution)/shard_map/ppermute | solution.py:49
  93.5 4.4 %collective-permute-start.13 = (bf16[48,1024]{1,0:T(8,128)(2,1)S(1)}, bf16[48,1024]{1,0:T(8,128)(2,1)S(1)}, u32[]{:S(2)}, u32[]{:S(2)}) collective-permute-start(bf16[48,1024]{1,0:T(8,128)(2,1)S(1)} %get-tuple-element.24), channel_id=1, source_target_pairs={{0,12},{2,14},{4,0},{6,2},{8,4},{10,6},{12,8},{14,10},{1,13},{3,15... | collective-permute-start | bytes 294920 | tf_op jit(solution)/shard_map/ppermute | solution.py:187
  98.3 2.2 %collective-permute-done.20 = bf16[96,1024]{1,0:T(8,128)(2,1)S(1)} collective-permute-done((bf16[96,1024]{1,0:T(8,128)(2,1)S(1)}, bf16[96,1024]{1,0:T(8,128)(2,1)S(1)}, u32[]{:S(2)}, u32[]{:S(2)}) %collective-permute-start.20) | collective-permute-done | bytes 196640 | tf_op jit(solution)/shard_map/ppermute | solution.py:49
  100.8 2.2 %collective-permute-start.21 = (bf16[48,1024]{1,0:T(8,128)(2,1)S(1)}, bf16[48,1024]{1,0:T(8,128)(2,1)S(1)}, u32[]{:S(2)}, u32[]{:S(2)}) collective-permute-start(bf16[48,1024]{1,0:T(8,128)(2,1)S(1)} %get-tuple-element.28), channel_id=1, source_target_pairs={{0,4},{2,6},{4,8},{6,10},{8,12},{10,14},{12,0},{14,2},{1,5},{3,7},... | collective-permute-start | bytes 294920 | tf_op jit(solution)/shard_map/ppermute | solution.py:187
  103.1 2.1 %collective-permute-start.23 = (bf16[48,1024]{1,0:T(8,128)(2,1)S(1)}, bf16[48,1024]{1,0:T(8,128)(2,1)S(1)}, u32[]{:S(2)}, u32[]{:S(2)}) collective-permute-start(bf16[48,1024]{1,0:T(8,128)(2,1)S(1)} %get-tuple-element.25), channel_id=1, source_target_pairs={{0,14},{2,12},{4,2},{6,0},{8,6},{10,4},{12,10},{14,8},{1,15},{3,13... | collective-permute-start | bytes 294920 | tf_op jit(solution)/shard_map/ppermute | solution.py:189
  105.9 1.6 %collective-permute-start.25 = (bf16[48,1024]{1,0:T(8,128)(2,1)S(1)}, bf16[48,1024]{1,0:T(8,128)(2,1)S(1)}, u32[]{:S(2)}, u32[]{:S(2)}) collective-permute-start(bf16[48,1024]{1,0:T(8,128)(2,1)S(1)} %get-tuple-element.29), channel_id=1, source_target_pairs={{0,6},{2,4},{4,10},{6,8},{8,14},{10,12},{12,2},{14,0},{1,7},{3,5},... | collective-permute-start | bytes 294920 | tf_op jit(solution)/shard_map/ppermute | solution.py:189
  107.8 1.2 collective-permute-done.23
  108.9 7.1 %collective-permute-done.24 = bf16[48,1024]{1,0:T(8,128)(2,1)S(1)} collective-permute-done((bf16[48,1024]{1,0:T(8,128)(2,1)S(1)}, bf16[48,1024]{1,0:T(8,128)(2,1)S(1)}, u32[]{:S(2)}, u32[]{:S(2)}) %collective-permute-start.24) | collective-permute-done | bytes 98336 | tf_op jit(solution)/shard_map/ppermute | solution.py:189
  117.5 1.6 %collective-permute-start.27 = (bf16[32,512]{1,0:T(8,128)(2,1)S(1)}, bf16[32,512]{1,0:T(8,128)(2,1)S(1)}, u32[]{:S(2)}, u32[]{:S(2)}) collective-permute-start(bf16[32,512]{1,0:T(8,128)(2,1)S(1)} %select_convert_fusion), channel_id=1, source_target_pairs={{0,1},{1,0},{2,3},{3,2},{4,5},{5,4},{6,7},{7,6},{8,9},{9,8},{10,11... | collective-permute-start | bytes 98312 | tf_op jit(solution)/shard_map/ppermute | solution.py:49
  119.2 1.6 %collective-permute-done.26 = bf16[32,512]{1,0:T(8,128)(2,1)S(1)} collective-permute-done((bf16[32,512]{1,0:T(8,128)(2,1)S(1)}, bf16[32,512]{1,0:T(8,128)(2,1)S(1)}, u32[]{:S(2)}, u32[]{:S(2)}) %collective-permute-start.26) | collective-permute-done | bytes 32800 | tf_op jit(solution)/shard_map/ppermute | solution.py:49
  (137 shorter events, 25.2 us)
Async XLA Ops:
  7.2 50.7 %copy-start = (bf16[1,352,2048]{2,1,0:T(8,128)(2,1)S(1)}, bf16[1,352,2048]{2,1,0:T(8,128)(2,1)}, u32[]{:S(2)}) copy-start(bf16[1,352,2048]{2,1,0:T(8,128)(2,1)} %param.20) | copy-start | bytes 4325380
  7.2 36.4 %all-gather.2.cloned.1.call-start = ((), (), s32[]{:S(2)}) async-start(), calls=%async_computation | async-start | bytes 2359296 | tf_op jit(solution)/shard_map/all_gather | solution.py:288
  8.2 13.7 %collective-permute-start.1 = (bf16[64,1024]{1,0:T(8,128)(2,1)S(1)}, bf16[64,1024]{1,0:T(8,128)(2,1)S(1)}, u32[]{:S(2)}, u32[]{:S(2)}) collective-permute-start(bf16[64,1024]{1,0:T(8,128)(2,1)S(1)} %get-tuple-element.31), channel_id=1, source_target_pairs={{0,4},{2,6},{4,8},{6,10},{8,12},{10,14},{12,0},{14,2},{1,5},{3,7},... | collective-permute-start | bytes 393224 | tf_op jit(solution)/shard_map/ppermute | solution.py:216
  11.3 11.2 %collective-permute-start.2 = (bf16[64,1024]{1,0:T(8,128)(2,1)S(1)}, bf16[64,1024]{1,0:T(8,128)(2,1)S(1)}, u32[]{:S(2)}, u32[]{:S(2)}) collective-permute-start(bf16[64,1024]{1,0:T(8,128)(2,1)S(1)} %get-tuple-element.31), channel_id=1, source_target_pairs={{0,8},{2,10},{4,12},{6,14},{8,0},{10,2},{12,4},{14,6},{1,9},{3,11}... | collective-permute-start | bytes 393224 | tf_op jit(solution)/shard_map/ppermute | solution.py:216
  13.9 8.6 %collective-permute-start.3 = (bf16[64,1024]{1,0:T(8,128)(2,1)S(1)}, bf16[64,1024]{1,0:T(8,128)(2,1)S(1)}, u32[]{:S(2)}, u32[]{:S(2)}) collective-permute-start(bf16[64,1024]{1,0:T(8,128)(2,1)S(1)} %get-tuple-element.31), channel_id=1, source_target_pairs={{0,12},{2,14},{4,0},{6,2},{8,4},{10,6},{12,8},{14,10},{1,13},{3,15... | collective-permute-start | bytes 393224 | tf_op jit(solution)/shard_map/ppermute | solution.py:216
  15.3 39.3 %collective-permute-start = (bf16[32,2048]{1,0:T(8,128)(2,1)}, bf16[32,2048]{1,0:T(8,128)(2,1)S(1)}, u32[]{:S(2)}, u32[]{:S(2)}) collective-permute-start(bf16[32,2048]{1,0:T(8,128)(2,1)} %bitcast.250), channel_id=1, source_target_pairs={{0,1},{1,0},{2,3},{3,2},{4,5},{5,4},{6,7},{7,6},{8,9},{9,8},{10,11... | collective-permute-start | bytes 393224 | tf_op jit(solution)/shard_map/ppermute | solution.py:49
  22.6 2.0 %collective-permute-start.4 = (bf16[4,64,1024]{2,1,0:T(8,128)(2,1)S(1)}, bf16[4,64,1024]{2,1,0:T(8,128)(2,1)S(1)}, u32[]{:S(2)}, u32[]{:S(2)}) collective-permute-start(bf16[4,64,1024]{2,1,0:T(8,128)(2,1)S(1)} %pad_maximum_fusion.1), channel_id=1, source_target_pairs={{0,2},{2,0},{4,6},{6,4},{8,10},{10,8},{12,14},{14,12},{1,3},{3,1},... | collective-permute-start | bytes 1572872 | tf_op jit(solution)/shard_map/ppermute | solution.py:218
  27.0 21.1 %copy-start.7 = (f32[1,64,4]{1,2,0:T(4,128)S(1)}, f32[1,64,4]{1,2,0:T(4,128)}, u32[]{:S(2)}) copy-start(f32[1,64,4]{1,2,0:T(4,128)} %param.22) | copy-start | bytes 3076
  45.9 8.6 %copy-start.5 = (bf16[1,32,2048]{2,1,0:T(8,128)(2,1)S(1)}, bf16[1,32,2048]{2,1,0:T(8,128)(2,1)}, u32[]{:S(2)}) copy-start(bf16[1,32,2048]{2,1,0:T(8,128)(2,1)} %param.15) | copy-start | bytes 393220
  46.0 6.4 %collective-permute-start.5 = (bf16[32,2048]{1,0:T(8,128)(2,1)S(1)}, bf16[32,2048]{1,0:T(8,128)(2,1)S(1)}, u32[]{:S(2)}, u32[]{:S(2)}) collective-permute-start(bf16[32,2048]{1,0:T(8,128)(2,1)S(1)} %get-tuple-element.18), channel_id=1, source_target_pairs={{0,1},{1,0},{2,3},{3,2},{4,5},{5,4},{6,7},{7,6},{8,9},{9,8},{10,11... | collective-permute-start | bytes 393224 | tf_op jit(solution)/shard_map/ppermute | solution.py:49
  47.6 6.9 %collective-permute-start.6 = (bf16[32,2048]{1,0:T(8,128)(2,1)S(1)}, bf16[32,2048]{1,0:T(8,128)(2,1)S(1)}, u32[]{:S(2)}, u32[]{:S(2)}) collective-permute-start(bf16[32,2048]{1,0:T(8,128)(2,1)S(1)} %get-tuple-element.19), channel_id=1, source_target_pairs={{0,1},{1,0},{2,3},{3,2},{4,5},{5,4},{6,7},{7,6},{8,9},{9,8},{10,11... | collective-permute-start | bytes 393224 | tf_op jit(solution)/shard_map/ppermute | solution.py:49
  55.2 1.5 %collective-permute-start.7 = (bf16[48,2048]{1,0:T(8,128)(2,1)S(1)}, bf16[48,2048]{1,0:T(8,128)(2,1)S(1)}, u32[]{:S(2)}, u32[]{:S(2)}) collective-permute-start(bf16[48,2048]{1,0:T(8,128)(2,1)S(1)} %get-tuple-element.21), channel_id=1, source_target_pairs={{0,2},{2,0},{4,6},{6,4},{8,10},{10,8},{12,14},{14,12},{1,3},{3,1},... | collective-permute-start | bytes 589832 | tf_op jit(solution)/shard_map/ppermute | solution.py:141
  55.7 4.2 %collective-permute-start.9 = (bf16[3,48,1024]{2,1,0:T(8,128)(2,1)S(1)}, bf16[3,48,1024]{2,1,0:T(8,128)(2,1)S(1)}, u32[]{:S(2)}, u32[]{:S(2)}) collective-permute-start(bf16[3,48,1024]{2,1,0:T(8,128)(2,1)S(1)} %bitcast.236), channel_id=1, source_target_pairs={{0,2},{2,0},{4,6},{6,4},{8,10},{10,8},{12,14},{14,12},{1,3},{3,1},... | collective-permute-start | bytes 884744 | tf_op jit(solution)/shard_map/ppermute | solution.py:143
  58.2 11.9 %collective-permute-start.8 = (bf16[96,1024]{1,0:T(8,128)(2,1)S(1)}, bf16[96,1024]{1,0:T(8,128)(2,1)S(1)}, u32[]{:S(2)}, u32[]{:S(2)}) collective-permute-start(bf16[96,1024]{1,0:T(8,128)(2,1)S(1)} %convolution_convert_fusion.5), channel_id=1, source_target_pairs={{0,1},{1,0},{2,3},{3,2},{4,5},{5,4},{6,7},{7,6},{8,9},{9,8},{10,11... | collective-permute-start | bytes 589832 | tf_op jit(solution)/shard_map/ppermute | solution.py:49
  59.9 9.7 %collective-permute-start.10 = (bf16[2,48,1024]{2,1,0:T(8,128)(2,1)S(1)}, bf16[2,48,1024]{2,1,0:T(8,128)(2,1)S(1)}, u32[]{:S(2)}, u32[]{:S(2)}) collective-permute-start(bf16[2,48,1024]{2,1,0:T(8,128)(2,1)S(1)} %get-tuple-element.11), channel_id=1, source_target_pairs={{0,4},{2,6},{4,8},{6,10},{8,12},{10,14},{12,0},{14,2},{1,5},{3,7},... | collective-permute-start | bytes 589832 | tf_op jit(solution)/shard_map/ppermute | solution.py:147
  62.4 14.6 %collective-permute-start.14 = (bf16[2,48,1024]{2,1,0:T(8,128)(2,1)S(1)}, bf16[2,48,1024]{2,1,0:T(8,128)(2,1)S(1)}, u32[]{:S(2)}, u32[]{:S(2)}) collective-permute-start(bf16[2,48,1024]{2,1,0:T(8,128)(2,1)S(1)} %get-tuple-element.13), channel_id=1, source_target_pairs={{0,8},{2,10},{4,12},{6,14},{8,0},{10,2},{12,4},{14,6},{1,9},{3,11}... | collective-permute-start | bytes 589832 | tf_op jit(solution)/shard_map/ppermute | solution.py:147
  63.9 13.5 %collective-permute-start.18 = (bf16[2,48,1024]{2,1,0:T(8,128)(2,1)S(1)}, bf16[2,48,1024]{2,1,0:T(8,128)(2,1)S(1)}, u32[]{:S(2)}, u32[]{:S(2)}) collective-permute-start(bf16[2,48,1024]{2,1,0:T(8,128)(2,1)S(1)} %get-tuple-element.12), channel_id=1, source_target_pairs={{0,12},{2,14},{4,0},{6,2},{8,4},{10,6},{12,8},{14,10},{1,13},{3,15... | collective-permute-start | bytes 589832 | tf_op jit(solution)/shard_map/ppermute | solution.py:147
  69.6 9.3 %collective-permute-start.11 = (bf16[96,1024]{1,0:T(8,128)(2,1)S(1)}, bf16[96,1024]{1,0:T(8,128)(2,1)S(1)}, u32[]{:S(2)}, u32[]{:S(2)}) collective-permute-start(bf16[96,1024]{1,0:T(8,128)(2,1)S(1)} %bitcast.247), channel_id=1, source_target_pairs={{0,1},{1,0},{2,3},{3,2},{4,5},{5,4},{6,7},{7,6},{8,9},{9,8},{10,11... | collective-permute-start | bytes 589832 | tf_op jit(solution)/shard_map/ppermute | solution.py:49
  76.9 7.8 %collective-permute-start.15 = (bf16[96,1024]{1,0:T(8,128)(2,1)S(1)}, bf16[96,1024]{1,0:T(8,128)(2,1)S(1)}, u32[]{:S(2)}, u32[]{:S(2)}) collective-permute-start(bf16[96,1024]{1,0:T(8,128)(2,1)S(1)} %bitcast.244), channel_id=1, source_target_pairs={{0,1},{1,0},{2,3},{3,2},{4,5},{5,4},{6,7},{7,6},{8,9},{9,8},{10,11... | collective-permute-start | bytes 589832 | tf_op jit(solution)/shard_map/ppermute | solution.py:49
  77.4 11.5 %collective-permute-start.19 = (bf16[96,1024]{1,0:T(8,128)(2,1)S(1)}, bf16[96,1024]{1,0:T(8,128)(2,1)S(1)}, u32[]{:S(2)}, u32[]{:S(2)}) collective-permute-start(bf16[96,1024]{1,0:T(8,128)(2,1)S(1)} %bitcast.241), channel_id=1, source_target_pairs={{0,1},{1,0},{2,3},{3,2},{4,5},{5,4},{6,7},{7,6},{8,9},{9,8},{10,11... | collective-permute-start | bytes 589832 | tf_op jit(solution)/shard_map/ppermute | solution.py:49
  80.8 12.4 %collective-permute-start.12 = (bf16[96,1024]{1,0:T(8,128)(2,1)S(1)}, bf16[96,1024]{1,0:T(8,128)(2,1)S(1)}, u32[]{:S(2)}, u32[]{:S(2)}) collective-permute-start(bf16[96,1024]{1,0:T(8,128)(2,1)S(1)} %convolution_convert_fusion.4), channel_id=1, source_target_pairs={{0,1},{1,0},{2,3},{3,2},{4,5},{5,4},{6,7},{7,6},{8,9},{9,8},{10,11... | collective-permute-start | bytes 589832 | tf_op jit(solution)/shard_map/ppermute | solution.py:49
  86.5 11.4 %collective-permute-start.16 = (bf16[96,1024]{1,0:T(8,128)(2,1)S(1)}, bf16[96,1024]{1,0:T(8,128)(2,1)S(1)}, u32[]{:S(2)}, u32[]{:S(2)}) collective-permute-start(bf16[96,1024]{1,0:T(8,128)(2,1)S(1)} %convolution_convert_fusion.3), channel_id=1, source_target_pairs={{0,1},{1,0},{2,3},{3,2},{4,5},{5,4},{6,7},{7,6},{8,9},{9,8},{10,11... | collective-permute-start | bytes 589832 | tf_op jit(solution)/shard_map/ppermute | solution.py:49
  90.7 9.8 %collective-permute-start.20 = (bf16[96,1024]{1,0:T(8,128)(2,1)S(1)}, bf16[96,1024]{1,0:T(8,128)(2,1)S(1)}, u32[]{:S(2)}, u32[]{:S(2)}) collective-permute-start(bf16[96,1024]{1,0:T(8,128)(2,1)S(1)} %convolution_convert_fusion.2), channel_id=1, source_target_pairs={{0,1},{1,0},{2,3},{3,2},{4,5},{5,4},{6,7},{7,6},{8,9},{9,8},{10,11... | collective-permute-start | bytes 589832 | tf_op jit(solution)/shard_map/ppermute | solution.py:49
  93.5 11.7 %collective-permute-start.13 = (bf16[48,1024]{1,0:T(8,128)(2,1)S(1)}, bf16[48,1024]{1,0:T(8,128)(2,1)S(1)}, u32[]{:S(2)}, u32[]{:S(2)}) collective-permute-start(bf16[48,1024]{1,0:T(8,128)(2,1)S(1)} %get-tuple-element.24), channel_id=1, source_target_pairs={{0,12},{2,14},{4,0},{6,2},{8,4},{10,6},{12,8},{14,10},{1,13},{3,15... | collective-permute-start | bytes 294920 | tf_op jit(solution)/shard_map/ppermute | solution.py:187
  98.2 7.7 %collective-permute-start.17 = (bf16[48,1024]{1,0:T(8,128)(2,1)S(1)}, bf16[48,1024]{1,0:T(8,128)(2,1)S(1)}, u32[]{:S(2)}, u32[]{:S(2)}) collective-permute-start(bf16[48,1024]{1,0:T(8,128)(2,1)S(1)} %get-tuple-element.26), channel_id=1, source_target_pairs={{0,8},{2,10},{4,12},{6,14},{8,0},{10,2},{12,4},{14,6},{1,9},{3,11}... | collective-permute-start | bytes 294920 | tf_op jit(solution)/shard_map/ppermute | solution.py:187
  100.8 6.9 %collective-permute-start.21 = (bf16[48,1024]{1,0:T(8,128)(2,1)S(1)}, bf16[48,1024]{1,0:T(8,128)(2,1)S(1)}, u32[]{:S(2)}, u32[]{:S(2)}) collective-permute-start(bf16[48,1024]{1,0:T(8,128)(2,1)S(1)} %get-tuple-element.28), channel_id=1, source_target_pairs={{0,4},{2,6},{4,8},{6,10},{8,12},{10,14},{12,0},{14,2},{1,5},{3,7},... | collective-permute-start | bytes 294920 | tf_op jit(solution)/shard_map/ppermute | solution.py:187
  103.1 4.7 %collective-permute-start.22 = (bf16[48,1024]{1,0:T(8,128)(2,1)S(1)}, bf16[48,1024]{1,0:T(8,128)(2,1)S(1)}, u32[]{:S(2)}, u32[]{:S(2)}) collective-permute-start(bf16[48,1024]{1,0:T(8,128)(2,1)S(1)} %get-tuple-element.23), channel_id=1, source_target_pairs={{0,2},{2,0},{4,6},{6,4},{8,10},{10,8},{12,14},{14,12},{1,3},{3,1},... | collective-permute-start | bytes 294920 | tf_op jit(solution)/shard_map/ppermute | solution.py:184
  103.1 5.8 %collective-permute-start.23 = (bf16[48,1024]{1,0:T(8,128)(2,1)S(1)}, bf16[48,1024]{1,0:T(8,128)(2,1)S(1)}, u32[]{:S(2)}, u32[]{:S(2)}) collective-permute-start(bf16[48,1024]{1,0:T(8,128)(2,1)S(1)} %get-tuple-element.25), channel_id=1, source_target_pairs={{0,14},{2,12},{4,2},{6,0},{8,6},{10,4},{12,10},{14,8},{1,15},{3,13... | collective-permute-start | bytes 294920 | tf_op jit(solution)/shard_map/ppermute | solution.py:189
  105.2 10.8 %collective-permute-start.24 = (bf16[48,1024]{1,0:T(8,128)(2,1)S(1)}, bf16[48,1024]{1,0:T(8,128)(2,1)S(1)}, u32[]{:S(2)}, u32[]{:S(2)}) collective-permute-start(bf16[48,1024]{1,0:T(8,128)(2,1)S(1)} %get-tuple-element.27), channel_id=1, source_target_pairs={{0,10},{2,8},{4,14},{6,12},{8,2},{10,0},{12,6},{14,4},{1,11},{3,9}... | collective-permute-start | bytes 294920 | tf_op jit(solution)/shard_map/ppermute | solution.py:189
  105.9 10.1 %collective-permute-start.25 = (bf16[48,1024]{1,0:T(8,128)(2,1)S(1)}, bf16[48,1024]{1,0:T(8,128)(2,1)S(1)}, u32[]{:S(2)}, u32[]{:S(2)}) collective-permute-start(bf16[48,1024]{1,0:T(8,128)(2,1)S(1)} %get-tuple-element.29), channel_id=1, source_target_pairs={{0,6},{2,4},{4,10},{6,8},{8,14},{10,12},{12,2},{14,0},{1,7},{3,5},... | collective-permute-start | bytes 294920 | tf_op jit(solution)/shard_map/ppermute | solution.py:189
  116.8 4.0 %collective-permute-start.26 = (bf16[32,512]{1,0:T(8,128)(2,1)S(1)}, bf16[32,512]{1,0:T(8,128)(2,1)S(1)}, u32[]{:S(2)}, u32[]{:S(2)}) collective-permute-start(bf16[32,512]{1,0:T(8,128)(2,1)S(1)} %select_convert_fusion.1), channel_id=1, source_target_pairs={{0,1},{1,0},{2,3},{3,2},{4,5},{5,4},{6,7},{7,6},{8,9},{9,8},{10,11... | collective-permute-start | bytes 98312 | tf_op jit(solution)/shard_map/ppermute | solution.py:49
  117.5 4.0 %collective-permute-start.27 = (bf16[32,512]{1,0:T(8,128)(2,1)S(1)}, bf16[32,512]{1,0:T(8,128)(2,1)S(1)}, u32[]{:S(2)}, u32[]{:S(2)}) collective-permute-start(bf16[32,512]{1,0:T(8,128)(2,1)S(1)} %select_convert_fusion), channel_id=1, source_target_pairs={{0,1},{1,0},{2,3},{3,2},{4,5},{5,4},{6,7},{7,6},{8,9},{9,8},{10,11... | collective-permute-start | bytes 98312 | tf_op jit(solution)/shard_map/ppermute | solution.py:49
  (5 other events, 13.3 us)
Sparse Core Ops, SparseCore 0:
  15.4 28.1 all-gather.1
